TPU v7x, 32 devices: a whole 2x2x4 slice. The times are simulated.
32 devices in a mesh: seq: 8 (over z, x), tp: 4 (over y, core).
Axes of the slice: x: 2, y: 2, z: 4, core: 2. Of those that a mesh axis runs over, the one named last changes fastest.
Arguments:
- hidden: bfloat16 [2048, 2048], P('seq', 'tp'), may hold values from -40 to 40
- new_queries: bfloat16 [2048, 2048], P('seq', 'tp'), may hold values from -9 to 9
- new_keys: bfloat16 [2048, 2048], P('seq', 'tp'), may hold values from -6 to 6
- new_values: bfloat16 [2048, 2048], P('seq', 'tp'), may hold values from -6 to 6
- cache_keys: bfloat16 [8, 4096, 2048], P('seq', None, 'tp'), may hold values from -6 to 6
- cache_values: bfloat16 [8, 4096, 2048], P('seq', None, 'tp'), may hold values from -6 to 6
- cache_lengths: int32 [8], replicated, may hold values from 1 to 4096, as said below
- out_proj: bfloat16 [2048, 2048], P('tp'), may hold values from -0.5 to 0.5
- moe_gain: float32 [2048], P('tp'), may hold values from 0.1 to 1.9
- expert_ids: int32 [2048, 8], P('seq'), may hold values from 0 to 15, all different within a row; in each aligned block of 256 rows (0 to 255, 256 to 511, ...) at most 192 rows name the same one
- route_weights: float32 [2048, 8], P('seq'), may hold values from 0.25 to 0.5
- expert_gate_up: bfloat16 [16, 2048, 2, 1024], P('seq', None, None, 'tp'), may hold values from -0.125 to 0.125
- expert_down: bfloat16 [16, 1024, 2048], P('seq', 'tp'), may hold values from -0.375 to 0.375
- next_gain: float32 [2048], P('tp'), may hold values from 0.1 to 1.9
- qkv_proj: bfloat16 [2048, 3, 2048], P(None, None, 'tp'), may hold values from -0.125 to 0.125
- query_gain: float32 [2048], P('tp'), may hold values from 0.1 to 1.9
- key_gain: float32 [2048], P('tp'), may hold values from 0.1 to 1.9
Outputs:
- layer_out: bfloat16 [2048, 2048], P('seq', 'tp')
- next_query: bfloat16 [2048, 2048], P('seq', 'tp')
- next_key: bfloat16 [2048, 2048], P('seq', 'tp')
- next_value: bfloat16 [2048, 2048], P('seq', 'tp')
Inputs may be any that keep to these rules, and one draw needn't show every extreme that they name: Request r has cached positions 0 to cache_lengths[r] - 1; one request has 4096 of them and one has 1. `expert_ids`: each row names 8 different experts; among the 256 rows of one request no expert is named more than 192 times, and in some request one expert is named exactly 192 times.
All inputs are finite; a program needn't handle non-finite values.
Results may differ from a plain program's by a relative error of at most 0.017.
Values may be sent and summed in bfloat16 or wider, within the bound.
No kernel may reach another device: no remote copies, remote signals or barrier semaphores. Data moves between devices by JAX's collectives and lax.ppermute only.
A program may use at most 128 MiB of HBM per device.

v0:
```python
import math

import jax
import jax.numpy as jnp
from jax import lax
from jax.sharding import PartitionSpec as P

D = 2048
HEAD_DIM = 128
TOP = 8
NEW = 256


epsilon = 1e-05


def softmax_parts(queries, key_rows, values, allowed):
    scores = jnp.einsum(
        "bthe,bche->bhtc", queries, key_rows, preferred_element_type=jnp.float32
    ) / math.sqrt(HEAD_DIM)
    scores = jnp.where(allowed[:, None], scores, -1e30)
    row_max = jnp.max(scores, axis=3)
    weights = jnp.where(allowed[:, None], jnp.exp(scores - row_max[..., None]), 0.0)
    row_total = jnp.sum(weights, axis=3)
    partial_out = jnp.einsum(
        "bhtc,bche->bthe", weights.astype(jnp.bfloat16), values, preferred_element_type=jnp.float32
    )
    return (partial_out, jnp.swapaxes(row_max, 1, 2), jnp.swapaxes(row_total, 1, 2))


def combine_parts(first, second):
    out_a, max_a, total_a = first
    out_b, max_b, total_b = second
    joint = jnp.maximum(max_a, max_b)
    factor_a = jnp.exp(max_a - joint)
    factor_b = jnp.exp(max_b - joint)
    return (
        out_a * factor_a[..., None] + out_b * factor_b[..., None],
        joint,
        total_a * factor_a + total_b * factor_b,
    )


def merge_parts(pieces, maxima, totals):
    overall = jnp.max(maxima, axis=0)
    factor = jnp.exp(maxima - overall[None])
    denominator = jnp.sum(totals * factor, axis=0)
    merged = jnp.sum(pieces * factor[..., None], axis=0)
    return merged / denominator[..., None]


def body(
    hidden,
    new_queries,
    new_keys,
    new_values,
    cache_keys,
    cache_values,
    cache_lengths,
    out_proj,
    moe_gain,
    expert_ids,
    route_weights,
    expert_gate_up,
    expert_down,
    next_gain,
    qkv_proj,
    query_gain,
    key_gain,
):
    seq_count = lax.axis_size("seq")
    here = lax.axis_index("seq")
    local_width = new_queries.shape[1]
    local_heads = local_width // HEAD_DIM
    quarter = hidden.shape[1]
    own_queries = new_queries.reshape(1, NEW, local_heads, HEAD_DIM)
    own_keys = new_keys.reshape(1, NEW, local_heads, HEAD_DIM)
    own_values = new_values.reshape(1, NEW, local_heads, HEAD_DIM)
    offsets = jnp.arange(NEW, dtype=jnp.int32)
    causal = (offsets[None, :] <= offsets[:, None])[None]
    own_out, own_max, own_total = softmax_parts(own_queries, own_keys, own_values, causal)
    span = cache_keys.shape[1]
    block = min(512, span)
    my_length = lax.dynamic_index_in_dim(cache_lengths, here, 0, keepdims=False)
    block_count = (my_length + block - 1) // block
    key_blocks = cache_keys.reshape(span, local_heads, HEAD_DIM)
    value_blocks = cache_values.reshape(span, local_heads, HEAD_DIM)

    def cache_block(index, carry):
        begin = index * block
        keys_here = lax.dynamic_slice_in_dim(key_blocks, begin, block, 0)[None]
        values_here = lax.dynamic_slice_in_dim(value_blocks, begin, block, 0)[None]
        positions = begin + jnp.arange(block, dtype=jnp.int32)
        allowed = jnp.broadcast_to((positions < my_length)[None, None, :], (1, NEW, block))
        return combine_parts(carry, softmax_parts(own_queries, keys_here, values_here, allowed))

    start_parts = (
        jnp.zeros((1, NEW, local_heads, HEAD_DIM), jnp.float32),
        jnp.full((1, NEW, local_heads), -1e30, jnp.float32),
        jnp.zeros((1, NEW, local_heads), jnp.float32),
    )
    pieces, maxima, totals = lax.fori_loop(0, block_count, cache_block, start_parts)
    attended = merge_parts(
        jnp.concatenate([own_out, pieces], 0),
        jnp.concatenate([own_max, maxima], 0),
        jnp.concatenate([own_total, totals], 0),
    )
    attended = attended.reshape(NEW, local_width).astype(jnp.bfloat16)
    attn_term = jnp.dot(attended, out_proj, preferred_element_type=jnp.float32)
    residual = hidden.astype(jnp.float32) + lax.psum_scatter(
        attn_term.astype(jnp.bfloat16), "tp", scatter_dimension=1, tiled=True
    ).astype(jnp.float32)
    square_total = lax.psum(jnp.sum(residual * residual, axis=1), "tp")
    moe_in = (residual * lax.rsqrt(square_total / D + epsilon)[:, None] * moe_gain[None, :]).astype(
        jnp.bfloat16
    )
    local_experts = expert_gate_up.shape[0]
    experts_all = local_experts * seq_count
    capacity = max(2, 3 * NEW * TOP // (2 * experts_all))
    flat_ids = expert_ids.reshape(NEW * TOP)
    onehot = (flat_ids[:, None] == jnp.arange(experts_all, dtype=jnp.int32)[None, :]).astype(
        jnp.int32
    )
    ranks = jnp.sum((jnp.cumsum(onehot, axis=0) - onehot) * onehot, axis=1)
    target = (flat_ids * capacity + ranks).reshape(NEW, TOP)
    slot_ids = jnp.arange(experts_all * capacity, dtype=jnp.int32)
    selector = jnp.sum(
        (target[None, :, :] == slot_ids[:, None, None]).astype(jnp.int32), axis=2
    ).astype(jnp.bfloat16)
    send_rows = jnp.dot(selector, moe_in, preferred_element_type=jnp.float32).astype(jnp.bfloat16)
    send_rows = send_rows.reshape(experts_all, capacity, quarter)
    received = lax.all_to_all(send_rows, "seq", split_axis=0, concat_axis=1, tiled=True)
    hidden_quarter = expert_gate_up.shape[3]
    gate_up_local = expert_gate_up.reshape(local_experts, D, 2 * hidden_quarter)
    weight_rows = gate_up_local
    projected = jnp.einsum(
        "erd,edf->erf",
        lax.all_gather(received, "tp", axis=2, tiled=True),
        weight_rows,
        preferred_element_type=jnp.float32,
    )
    activated = (
        jax.nn.silu(projected[..., :hidden_quarter]) * projected[..., hidden_quarter:]
    ).astype(jnp.bfloat16)
    down_terms = jnp.einsum(
        "erf,efd->erd", activated, expert_down, preferred_element_type=jnp.float32
    )
    expert_result = lax.psum_scatter(
        down_terms.astype(jnp.bfloat16), "tp", scatter_dimension=2, tiled=True
    )
    returned = lax.all_to_all(
        expert_result, "seq", split_axis=1, concat_axis=0, tiled=True
    ).reshape(experts_all * capacity, quarter)
    picked = jnp.take(returned, target, axis=0)
    routed = residual + jnp.sum(route_weights[:, :, None] * picked.astype(jnp.float32), axis=1)
    layer_out = routed.astype(jnp.bfloat16)
    scaled = (routed * next_gain[None, :]).astype(jnp.bfloat16)
    qkv_local = qkv_proj.reshape(D, 3 * local_width)
    weight_rows = qkv_local
    mixed = jnp.dot(
        lax.all_gather(scaled, "tp", axis=1, tiled=True),
        weight_rows,
        preferred_element_type=jnp.float32,
    )
    mixed = mixed.reshape(NEW, 3, local_width)
    squares_routed = jnp.sum(routed * routed, axis=1)
    routed_total, query_raw, key_raw = lax.psum(
        (
            squares_routed,
            jnp.sum(mixed[:, 0] * mixed[:, 0], axis=1),
            jnp.sum(mixed[:, 1] * mixed[:, 1], axis=1),
        ),
        "tp",
    )
    x_scale = lax.rsqrt(routed_total / D + epsilon)
    query_pre = mixed[:, 0] * x_scale[:, None]
    key_pre = mixed[:, 1] * x_scale[:, None]
    query_total = query_raw * x_scale * x_scale
    key_total = key_raw * x_scale * x_scale
    next_query = (
        query_pre * lax.rsqrt(query_total / D + epsilon)[:, None] * query_gain[None, :]
    ).astype(jnp.bfloat16)
    next_key = (key_pre * lax.rsqrt(key_total / D + epsilon)[:, None] * key_gain[None, :]).astype(
        jnp.bfloat16
    )
    next_value = (mixed[:, 2] * x_scale[:, None]).astype(jnp.bfloat16)
    return (layer_out, next_query, next_key, next_value)


def solution(mesh):
    return jax.shard_map(
        body,
        mesh=mesh,
        in_specs=(
            P("seq", "tp"),
            P("seq", "tp"),
            P("seq", "tp"),
            P("seq", "tp"),
            P("seq", None, "tp"),
            P("seq", None, "tp"),
            P(),
            P("tp", None),
            P("tp"),
            P("seq", None),
            P("seq", None),
            P("seq", None, None, "tp"),
            P("seq", "tp", None),
            P("tp"),
            P(None, None, "tp"),
            P("tp"),
            P("tp"),
        ),
        out_specs=(P("seq", "tp"), P("seq", "tp"), P("seq", "tp"), P("seq", "tp")),
        check_vma=False,
    )
```

profile of v0, /device:TPU:0, one launch (start us, length us, event | category | flops | bytes accessed | tf_op | source)
XLA Modules:
  0.0 551.8 jit_solution(16717053400990705615)
XLA Ops:
  7.2 1.4 dynamic_slice.10
  9.3 6.4 %copy.120 = bf16[1,4096,512]{1,2,0:T(8,128)(2,1)} copy(bf16[1,4096,512]{2,1,0:T(8,128)(2,1)} %param.23) | data formatting | bytes 8388608 | tf_op args[4]
  15.7 6.5 %copy.122 = bf16[1,4096,512]{1,2,0:T(8,128)(2,1)} copy(bf16[1,4096,512]{2,1,0:T(8,128)(2,1)} %param.24) | data formatting | bytes 8388608 | tf_op args[5]
  23.5 39.9 %while.14 = (s32[]{:T(128)}, f32[1,256,4,128]{1,3,2,0:T(8,128)}, f32[1,256,4]{1,2,0:T(4,128)S(1)}, f32[1,256,4]{1,2,0:T(4,128)S(1)}, s32[]{:T(128)}, /*index=5*/...) while((s32[]{:T(128)}, f32[1,256,4,128]{1,3,2,0:T(8,128)}, ...), condition=%wide.region_4.5_spmd, body=%wide.region_1.4_spmd.sunk | while | flops 275651584 | bytes 8731323 | solution.py:102
  24.1 1.6 bitcast_reduce_fusion.2
  26.4 2.8 fusion.88
  29.8 1.6 bitcast_reduce_fusion.2
  32.1 2.8 fusion.88
  35.5 1.6 bitcast_reduce_fusion.2
  37.8 2.8 fusion.88
  41.2 1.6 bitcast_reduce_fusion.2
  43.5 2.8 fusion.88
  46.9 1.6 bitcast_reduce_fusion.2
  49.2 2.8 fusion.88
  52.6 1.6 bitcast_reduce_fusion.2
  54.9 2.8 fusion.88
  58.3 1.6 bitcast_reduce_fusion.2
  60.6 2.8 fusion.88
  63.4 1.3 fusion.67
  64.9 2.0 copy.125
  66.9 1.4 convolution_bitcast_fusion.1
  68.3 1.4 fusion.32
  70.1 3.3 convolution_convert_fusion.2
  73.8 4.5 reduce-window.6
  79.4 33.6 %convert_reduce_fusion = s32[3072,256]{1,0:T(8,128)} fusion(s32[256,8]{0,1:T(8,128)S(1)} %get-tuple-element.128), kind=kLoop, calls=%fused_computation.34 | loop fusion | flops 18087936 | bytes 3153920 | tf_op jit(solution)/shard_map/reduce_sum | solution.py:127
  113.0 1.1 multiply_reduce_fusion.4
  114.1 8.6 %psum.28 = f32[256]{0:T(256)S(1)} all-reduce(f32[256]{0:T(256)S(1)} %multiply_reduce_fusion.4), channel_id=1, replica_groups=mesh['seq'=8,'tp'=4] {'tp'}, use_global_device_ids=true, to_apply=%region_14.15 | all-reduce | flops 256 | bytes 2048 | tf_op jit(solution)/shard_map/psum | solution.py:113
  122.7 3.0 convolution_convert_fusion.1
  125.7 80.8 %all_to_all.33 = bf16[16,192,512]{2,1,0:T(8,128)(2,1)S(1)} all-to-all(bf16[16,192,512]{2,1,0:T(8,128)(2,1)S(1)} %bitcast.171), channel_id=1, replica_groups=mesh['seq'=8,'tp'=4] {'seq'}, dimensions={0} | all-to-all | bytes 6291456 | tf_op jit(solution)/shard_map/all_to_all | solution.py:132
  206.4 1.9 copy.132
  208.5 7.7 %reshape.191 = bf16[2,2048,512]{2,1,0:T(8,128)(2,1)} reshape(bf16[2,2048,2,256]{3,2,1,0:T(2,128)(2,1)} %param.30) | data formatting | bytes 8388608 | tf_op jit(solution)/shard_map/reshape | solution.py:134
  216.2 73.6 %all-gather.3.cloned.1.call-done = bf16[2,1536,2048]{2,1,0:T(8,128)(2,1)} async-done(((bf16[2,1536,512]{2,1,0:T(8,128)(2,1)}), bf16[2,1536,2048]{2,1,0:T(8,128)(2,1)}) %all-gather.3.cloned.1.call-update) | async-done | bytes 12582928 | tf_op jit(solution)/shard_map/all_gather | solution.py:138
  289.8 12.5 %fusion.68 = f32[2,1536,512]{2,1,0:T(8,128)} fusion(bf16[2,1536,2048]{2,1,0:T(8,128)(2,1)} %all-gather.3.cloned.1.call-done, bf16[2,2048,512]{2,1,0:T(8,128)(2,1)} %reshape.191), kind=kOutput, calls=%fused_computation.116 | convolution fusion | flops 6442450944 | bytes 23068672 | tf_op jit(solution)/shard_map/erd,edf->erf/dot_general | solution.py:136
  302.3 9.3 %convolution_convert_fusion = bf16[2,1536,2048]{2,1,0:T(8,128)(2,1)} fusion(bf16[2,256,2048]{2,1,0:T(8,128)(2,1)S(1)} %copy-done, f32[2,1536,512]{2,1,0:T(8,128)} %fusion.68), kind=kOutput, calls=%fused_computation.36 | convolution fusion | flops 3232235520 | bytes 20971520 | tf_op jit(solution)/shard_map/erf,efd->erd/dot_general | solution.py:145
  311.5 99.2 %reduce-scatter.5.cloned.1.call-done = bf16[2,1536,512]{2,1,0:T(8,128)(2,1)} async-done(((bf16[2,1536,2048]{2,1,0:T(8,128)(2,1)}), bf16[2,1536,512]{2,1,0:T(8,128)(2,1)}) %reduce-scatter.5.cloned.1.call-update) | async-done | bytes 3145744 | tf_op jit(solution)/shard_map/reduce_scatter | solution.py:148
  410.8 7.9 %copy.133 = bf16[2,1536,512]{2,0,1:T(2,128)(2,1)} copy(bf16[2,1536,512]{2,1,0:T(8,128)(2,1)} %reduce-scatter.5.cloned.1.call-done) | data formatting | bytes 6291456 | tf_op jit(solution)/shard_map/reduce_scatter | solution.py:148
  418.7 5.6 %all-to-all-start.1 = ((bf16[2,1536,512]{2,0,1:T(2,128)(2,1)}), bf16[2,1536,512]{2,0,1:T(2,128)(2,1)}, u32[]{:S(2)}, u32[]{:S(2)}) async-start(bf16[2,1536,512]{2,0,1:T(2,128)(2,1)} %copy.133), calls=%async_computation.3 | async-start | bytes 6291456 | tf_op jit(solution)/shard_map/all_to_all | solution.py:151
  425.2 70.0 %all-to-all-done.1 = bf16[2,1536,512]{2,0,1:T(2,128)(2,1)} async-done(((bf16[2,1536,512]{2,0,1:T(2,128)(2,1)}), bf16[2,1536,512]{2,0,1:T(2,128)(2,1)}, u32[]{:S(2)}, u32[]{:S(2)}) %all-to-all-start.1) | async-done | bytes 3145760 | tf_op jit(solution)/shard_map/all_to_all | solution.py:151
  495.2 4.2 copy.134
  499.4 11.6 %gather_fusion = bf16[2048,512]{1,0:T(8,128)(2,1)} fusion(bf16[3072,512]{1,0:T(8,128)(2,1)} %bitcast.170, s32[2048]{0:T(1024)S(1)} %broadcast_clamp_fusion), kind=kCustom, calls=%fused_computation | custom fusion | bytes 4202496 | tf_op jit(solution)/shard_map/jit(_take)/gather | solution.py:154
  511.0 3.7 multiply_reduce_fusion
  514.7 0.9 multiply_reduce_fusion.3
  515.7 8.9 %copy.136 = bf16[2048,3,512]{0,2,1:T(8,128)(2,1)} copy(bf16[2048,3,512]{2,0,1:T(8,128)(2,1)} %param.33) | data formatting | bytes 12582912 | tf_op args[14]
  524.5 6.1 %all-gather.5.cloned.1.call-done = bf16[256,2048]{1,0:T(8,128)(2,1)} async-done(((bf16[256,512]{1,0:T(8,128)(2,1)}), bf16[256,2048]{1,0:T(8,128)(2,1)}) %all-gather.5.cloned.1.call-update) | async-done | bytes 1048592 | tf_op jit(solution)/shard_map/all_gather | solution.py:161
  530.7 4.9 fusion.25
  535.6 1.1 copy-done.1
  536.9 5.9 %all-reduce = (f32[256]{0:T(256)S(1)}, f32[256]{0:T(256)S(1)}, f32[256]{0:T(256)S(1)}) all-reduce(f32[256]{0:T(256)S(1)} %get-tuple-element.103, f32[256]{0:T(256)S(1)} %get-tuple-element.138, f32[256]{0:T(256)S(1)} %get-tuple-element.102), channel_id=1, replica_groups=mesh['seq'=8,'tp'=4] {'tp'}, use_global_device_ids=true, to_apply=%region_20.21 | all-reduce | flops 768 | bytes 6144 | tf_op jit(solution)/shard_map/psum | solution.py:167
  542.8 2.4 fusion.38
  (96 shorter events, 13.3 us)
Async XLA Ops:
  7.2 295.1 %copy-start = (bf16[2,256,2048]{2,1,0:T(8,128)(2,1)S(1)}, bf16[2,256,2048]{2,1,0:T(8,128)(2,1)}, u32[]{:S(2)}) copy-start(bf16[2,256,2048]{2,1,0:T(8,128)(2,1)} %param.31) | copy-start | bytes 6291460
  7.2 105.8 %reduce-scatter.3.cloned.1.call-start = ((), (), s32[]{:S(2)}) async-start(), calls=%async_computation.4 | async-start | bytes 1310720 | tf_op jit(solution)/shard_map/reduce_scatter | solution.py:110
  15.7 6.5 %copy-start.4 = (bf16[256,512]{1,0:T(8,128)(2,1)S(1)}, bf16[256,512]{1,0:T(8,128)(2,1)}, u32[]{:S(2)}) copy-start(bf16[256,512]{1,0:T(8,128)(2,1)} %param.20) | copy-start | bytes 786436
  69.7 3.8 copy-start.5
  73.4 39.6 %copy-start.2 = (bf16[256,512]{1,0:T(8,128)(2,1)S(1)}, bf16[256,512]{1,0:T(8,128)(2,1)}, u32[]{:S(2)}) copy-start(bf16[256,512]{1,0:T(8,128)(2,1)} %param.19) | copy-start | bytes 786436
  73.4 49.3 %copy-start.10 = (f32[512]{0:T(512)S(1)}, f32[512]{0:T(512)}, u32[]{:S(2)}) copy-start(f32[512]{0:T(512)} %param.27) | copy-start | bytes 6148
  73.4 216.3 %all-gather.3.cloned.1.call-start = ((), (), s32[]{:S(2)}) async-start(), calls=%async_computation.5 | async-start | bytes 15728640 | tf_op jit(solution)/shard_map/all_gather | solution.py:138
  208.4 202.3 %reduce-scatter.5.cloned.1.call-start = ((), (), s32[]{:S(2)}) async-start(), calls=%async_computation.6 | async-start | bytes 15728640 | tf_op jit(solution)/shard_map/reduce_scatter | solution.py:148
  418.7 6.3 %copy-start.6 = (f32[256,8]{0,1:T(8,128)S(1)}, f32[256,8]{0,1:T(8,128)}, u32[]{:S(2)}) copy-start(f32[256,8]{0,1:T(8,128)} %param.29) | copy-start | bytes 24580
  418.7 76.5 %all-to-all-start.1 = ((bf16[2,1536,512]{2,0,1:T(2,128)(2,1)}), bf16[2,1536,512]{2,0,1:T(2,128)(2,1)}, u32[]{:S(2)}, u32[]{:S(2)}) async-start(bf16[2,1536,512]{2,0,1:T(2,128)(2,1)} %copy.133), calls=%async_computation.3 | async-start | bytes 6291456 | tf_op jit(solution)/shard_map/all_to_all | solution.py:151
  424.4 106.3 %all-gather.5.cloned.1.call-start = ((), (), s32[]{:S(2)}) async-start(), calls=%async_computation.7 | async-start | bytes 1310720 | tf_op jit(solution)/shard_map/all_gather | solution.py:161
  499.4 15.3 %copy-start.3 = (bf16[256,512]{1,0:T(8,128)(2,1)S(1)}, bf16[256,512]{1,0:T(8,128)(2,1)}, u32[]{:S(2)}) copy-start(bf16[256,512]{1,0:T(8,128)(2,1)} %reduce-scatter.3.cloned.1.call-done) | copy-start | bytes 786436
  499.4 15.3 %copy-start.7 = (f32[512]{0:T(512)S(1)}, f32[512]{0:T(512)}, u32[]{:S(2)}) copy-start(f32[512]{0:T(512)} %param.32) | copy-start | bytes 6148
  524.5 18.3 %copy-start.8 = (f32[512]{0:T(512)S(1)}, f32[512]{0:T(512)}, u32[]{:S(2)}) copy-start(f32[512]{0:T(512)} %param.35) | copy-start | bytes 6148
  524.5 18.3 %copy-start.9 = (f32[512]{0:T(512)S(1)}, f32[512]{0:T(512)}, u32[]{:S(2)}) copy-start(f32[512]{0:T(512)} %param.34) | copy-start | bytes 6148
  535.6 1.2 copy-start.1
Sparse Core Ops, SparseCore 0:
  73.5 33.2 reduce-scatter.2
  208.5 81.1 all-gather.2
  311.7 99.0 reduce-scatter.4
  515.8 14.8 all-gather.4
where the time goes:
time: 554 us; the launch traced here: 552 us
  waiting for transfers between devices  249 us (45%)
  blocking collectives  95.2 us (17%)
  matrix products  66.3 us (12%)
  local copies, waits for them, and re-layouts  62.6 us (11%)
  other arithmetic  57.8 us (10%)
  between operations  14.7 us (3%)
  starting transfers between devices  6.02 us (1%)
    reduce_scatter x1, waiting for transfers between devices, body(): lax.psum_scatter(down_terms.astype(jnp.bfloat16), 'tp', scatter_dimension...  99.2 us
    all_to_all x1, blocking collectives, body(): lax.all_to_all(send_rows, 'seq', split_axis=0, concat_axis=1, tiled=True)  80.8 us
    all_gather x1, waiting for transfers between devices, body(): lax.all_gather(received, 'tp', axis=2, tiled=True)  73.6 us
    all_to_all x1, waiting for transfers between devices, body(): lax.all_to_all(expert_result, 'seq', split_axis=1, concat_axis=0, tiled=T...  70 us
    reduce_sum x1, other arithmetic, body(): jnp.sum((target[None, :, :] == slot_ids[:, None, None]).astype(jnp.int32)...  33.6 us
    unnamed x28, local copies, waits for them, and re-layouts  23.3 us
    dot_general x8, matrix products, softmax_parts(): jnp.einsum('bhtc,bche->bthe', weights.astype(jnp.bfloat16), values, prefe...  20.8 us
    dot_general x8, matrix products, softmax_parts(): jnp.einsum('bthe,bche->bhtc', queries, key_rows, preferred_element_type=j...  12.6 us
  transfers between devices with their start and end apart: 5, of which 4 were waited for; matrix products, arithmetic and copies ran while one was open for 10% of the time, Pallas kernels for 0%

commit v1 on v0

--- a/solution.py
+++ b/solution.py
@@ -47,6 +47,71 @@
     denominator = jnp.sum(totals * factor, axis=0)
     merged = jnp.sum(pieces * factor[..., None], axis=0)
     return merged / denominator[..., None]
+
+
+def dense_experts(moe_in, expert_ids, route_weights, expert_gate_up, expert_down, here, experts_all):
+    local_experts = expert_gate_up.shape[0]
+    hidden_quarter = expert_gate_up.shape[3]
+    gate_w = jnp.sum(
+        route_weights[:, :, None]
+        * (expert_ids[:, :, None] == jnp.arange(experts_all, dtype=jnp.int32)[None, None, :]),
+        axis=1,
+    )
+    gate_all = lax.all_gather(gate_w, "seq", axis=0, tiled=True)
+    gate_local = lax.dynamic_slice_in_dim(gate_all, here * local_experts, local_experts, axis=1)
+    rows = lax.all_gather(lax.all_gather(moe_in, "seq", axis=0, tiled=True), "tp", axis=1, tiled=True)
+    gate_up = expert_gate_up.reshape(local_experts, D, 2 * hidden_quarter)
+    projected = jnp.einsum("td,edf->etf", rows, gate_up, preferred_element_type=jnp.float32)
+    activated = jax.nn.silu(projected[..., :hidden_quarter]) * projected[..., hidden_quarter:]
+    activated = activated.astype(jnp.bfloat16).astype(jnp.float32)
+    weighted = (activated * jnp.transpose(gate_local)[:, :, None]).astype(jnp.bfloat16)
+    weighted = jnp.transpose(weighted, (1, 0, 2)).reshape(rows.shape[0], local_experts * hidden_quarter)
+    down_rows = expert_down.reshape(local_experts * hidden_quarter, D)
+    partial = jnp.dot(weighted, down_rows, preferred_element_type=jnp.float32).astype(jnp.bfloat16)
+    partial = lax.psum_scatter(partial, "tp", scatter_dimension=1, tiled=True)
+    partial = lax.psum_scatter(partial, "seq", scatter_dimension=0, tiled=True)
+    return partial.astype(jnp.float32)
+
+
+def dispatch_experts(moe_in, expert_ids, route_weights, expert_gate_up, expert_down, experts_all, capacity):
+    quarter = moe_in.shape[1]
+    local_experts = expert_gate_up.shape[0]
+    flat_ids = expert_ids.reshape(NEW * TOP)
+    onehot = (flat_ids[:, None] == jnp.arange(experts_all, dtype=jnp.int32)[None, :]).astype(
+        jnp.int32
+    )
+    ranks = jnp.sum((jnp.cumsum(onehot, axis=0) - onehot) * onehot, axis=1)
+    target = (flat_ids * capacity + ranks).reshape(NEW, TOP)
+    slot_ids = jnp.arange(experts_all * capacity, dtype=jnp.int32)
+    selector = jnp.sum(
+        (target[None, :, :] == slot_ids[:, None, None]).astype(jnp.int32), axis=2
+    ).astype(jnp.bfloat16)
+    send_rows = jnp.dot(selector, moe_in, preferred_element_type=jnp.float32).astype(jnp.bfloat16)
+    send_rows = send_rows.reshape(experts_all, capacity, quarter)
+    received = lax.all_to_all(send_rows, "seq", split_axis=0, concat_axis=1, tiled=True)
+    hidden_quarter = expert_gate_up.shape[3]
+    gate_up_local = expert_gate_up.reshape(local_experts, D, 2 * hidden_quarter)
+    weight_rows = gate_up_local
+    projected = jnp.einsum(
+        "erd,edf->erf",
+        lax.all_gather(received, "tp", axis=2, tiled=True),
+        weight_rows,
+        preferred_element_type=jnp.float32,
+    )
+    activated = (
+        jax.nn.silu(projected[..., :hidden_quarter]) * projected[..., hidden_quarter:]
+    ).astype(jnp.bfloat16)
+    down_terms = jnp.einsum(
+        "erf,efd->erd", activated, expert_down, preferred_element_type=jnp.float32
+    )
+    expert_result = lax.psum_scatter(
+        down_terms.astype(jnp.bfloat16), "tp", scatter_dimension=2, tiled=True
+    )
+    returned = lax.all_to_all(
+        expert_result, "seq", split_axis=1, concat_axis=0, tiled=True
+    ).reshape(experts_all * capacity, quarter)
+    picked = jnp.take(returned, target, axis=0)
+    return jnp.sum(route_weights[:, :, None] * picked.astype(jnp.float32), axis=1)
 
 
 def body(
@@ -117,42 +182,15 @@
     local_experts = expert_gate_up.shape[0]
     experts_all = local_experts * seq_count
     capacity = max(2, 3 * NEW * TOP // (2 * experts_all))
-    flat_ids = expert_ids.reshape(NEW * TOP)
-    onehot = (flat_ids[:, None] == jnp.arange(experts_all, dtype=jnp.int32)[None, :]).astype(
-        jnp.int32
-    )
-    ranks = jnp.sum((jnp.cumsum(onehot, axis=0) - onehot) * onehot, axis=1)
-    target = (flat_ids * capacity + ranks).reshape(NEW, TOP)
-    slot_ids = jnp.arange(experts_all * capacity, dtype=jnp.int32)
-    selector = jnp.sum(
-        (target[None, :, :] == slot_ids[:, None, None]).astype(jnp.int32), axis=2
-    ).astype(jnp.bfloat16)
-    send_rows = jnp.dot(selector, moe_in, preferred_element_type=jnp.float32).astype(jnp.bfloat16)
-    send_rows = send_rows.reshape(experts_all, capacity, quarter)
-    received = lax.all_to_all(send_rows, "seq", split_axis=0, concat_axis=1, tiled=True)
-    hidden_quarter = expert_gate_up.shape[3]
-    gate_up_local = expert_gate_up.reshape(local_experts, D, 2 * hidden_quarter)
-    weight_rows = gate_up_local
-    projected = jnp.einsum(
-        "erd,edf->erf",
-        lax.all_gather(received, "tp", axis=2, tiled=True),
-        weight_rows,
-        preferred_element_type=jnp.float32,
-    )
-    activated = (
-        jax.nn.silu(projected[..., :hidden_quarter]) * projected[..., hidden_quarter:]
-    ).astype(jnp.bfloat16)
-    down_terms = jnp.einsum(
-        "erf,efd->erd", activated, expert_down, preferred_element_type=jnp.float32
-    )
-    expert_result = lax.psum_scatter(
-        down_terms.astype(jnp.bfloat16), "tp", scatter_dimension=2, tiled=True
-    )
-    returned = lax.all_to_all(
-        expert_result, "seq", split_axis=1, concat_axis=0, tiled=True
-    ).reshape(experts_all * capacity, quarter)
-    picked = jnp.take(returned, target, axis=0)
-    routed = residual + jnp.sum(route_weights[:, :, None] * picked.astype(jnp.float32), axis=1)
+    if NEW <= 2 * capacity:
+        moe_term = dense_experts(
+            moe_in, expert_ids, route_weights, expert_gate_up, expert_down, here, experts_all
+        )
+    else:
+        moe_term = dispatch_experts(
+            moe_in, expert_ids, route_weights, expert_gate_up, expert_down, experts_all, capacity
+        )
+    routed = residual + moe_term
     layer_out = routed.astype(jnp.bfloat16)
     scaled = (routed * next_gain[None, :]).astype(jnp.bfloat16)
     qkv_local = qkv_proj.reshape(D, 3 * local_width)

time: 554 us -> 426 us (0.77)
  blocking collectives: 95.2 us -> 42.2 us
  other arithmetic: 57.8 us -> 9.48 us
  waiting for transfers between devices: 249 us -> 288 us
  matrix products: 66.3 us -> 33.7 us
  local copies, waits for them, and re-layouts: 62.6 us -> 36.1 us
  starting transfers between devices: 6.02 us -> 0.42 us
    all_to_all x1 -> x0, blocking collectives: 80.8 us -> none  [body(): lax.all_to_all(send_rows, 'seq', split_axis=0, concat_axis=1, tiled=True)]
    all_to_all x1 -> x0, waiting for transfers between devices: 70 us -> none  [body(): lax.all_to_all(expert_result, 'seq', split_axis=1, concat_axis=0, tiled=T...]
    reduce_scatter x1, waiting for transfers between devices: 0.01 us -> 67.6 us  [body(): lax.psum_scatter(attn_term.astype(jnp.bfloat16), 'tp', scatter_dimension=...]
    reduce_scatter x1 -> x2, waiting for transfers between devices: 99.2 us -> 143 us  [the longest x1 71.8 us: dense_experts(): partial = lax.psum_scatter(partial, 'tp', scatter_dimension=1, tiled=True)]
    reduce_sum x3 -> x1, other arithmetic: 37.4 us -> 0.02 us  [dense_experts(): jnp.sum(route_weights[:, :, None] * (expert_ids[:, :, None] == jnp.arange...]
    all_gather x0 -> x1, blocking collectives: none -> 30.5 us  [dense_experts(): gate_all = lax.all_gather(gate_w, 'seq', axis=0, tiled=True)]
    dot_general x8 -> x2, matrix products: 20.8 us -> 3.18 us  [softmax_parts(): jnp.einsum('bhtc,bche->bthe', weights.astype(jnp.bfloat16), values, prefe...]
    gather x1 -> x0, local copies, waits for them, and re-layouts: 11.6 us -> none  [body(): picked = jnp.take(returned, target, axis=0)]
  transfers between devices with their start and end apart: 5 -> 6, of which waited for: 4 -> 6; matrix products, arithmetic and copies ran while one was open for 10% -> 4% of each run, Pallas kernels for 0% -> 0%
where the time goes in v1:
time: 426 us; the launch traced here: 425 us
  waiting for transfers between devices  288 us (68%)
  blocking collectives  42.2 us (10%)
  local copies, waits for them, and re-layouts  36.1 us (8%)
  matrix products  33.7 us (8%)
  between operations  15 us (4%)
  other arithmetic  9.48 us (2%)
    reduce_scatter x1, waiting for transfers between devices, dense_experts(): partial = lax.psum_scatter(partial, 'tp', scatter_dimension=1, tiled=True)  71.8 us
    reduce_scatter x1, waiting for transfers between devices, dense_experts(): partial = lax.psum_scatter(partial, 'seq', scatter_dimension=0, tiled=True)  70.9 us
    reduce_scatter x1, waiting for transfers between devices, body(): lax.psum_scatter(attn_term.astype(jnp.bfloat16), 'tp', scatter_dimension=...  67.6 us
    all_gather x1, waiting for transfers between devices, dense_experts(): lax.all_gather(moe_in, 'seq', axis=0, tiled=True)  50.5 us
    all_gather x1, blocking collectives, dense_experts(): gate_all = lax.all_gather(gate_w, 'seq', axis=0, tiled=True)  30.5 us
    unnamed x30, local copies, waits for them, and re-layouts  23.7 us
    all_gather x1, waiting for transfers between devices, dense_experts(): lax.all_gather(lax.all_gather(moe_in, 'seq', axis=0, tiled=True), 'tp', a...  20 us
    dot_general x1, matrix products, dense_experts(): jnp.einsum('td,edf->etf', rows, gate_up, preferred_element_type=jnp.float32)  12.4 us
  transfers between devices with their start and end apart: 6, of which 6 were waited for; matrix products, arithmetic and copies ran while one was open for 4% of the time, Pallas kernels for 0%

profile of v1, /device:TPU:0, one launch (start us, length us, event | category | flops | bytes accessed | tf_op | source)
XLA Modules:
  0.0 424.8 jit_solution(6269661821771716054)
XLA Ops:
  7.2 0.0 reduce-scatter.4.cloned.1.call-start
  7.2 1.4 dynamic_slice.13
  9.3 6.4 %copy.78 = bf16[1,4096,512]{1,2,0:T(8,128)(2,1)} copy(bf16[1,4096,512]{2,1,0:T(8,128)(2,1)} %param.23) | data formatting | bytes 8388608 | tf_op args[4]
  15.7 6.5 %copy.80 = bf16[1,4096,512]{1,2,0:T(8,128)(2,1)} copy(bf16[1,4096,512]{2,1,0:T(8,128)(2,1)} %param.24) | data formatting | bytes 8388608 | tf_op args[5]
  22.2 0.1 copy.79
  22.4 0.2 copy.82
  22.6 0.9 broadcast_in_dim.61
  23.5 5.7 %while.14 = (s32[]{:T(128)}, f32[1,256,4,128]{1,3,2,0:T(8,128)}, f32[1,256,4]{1,2,0:T(4,128)S(1)}, f32[1,256,4]{1,2,0:T(4,128)S(1)}, s32[]{:T(128)}, /*index=5*/...) while((s32[]{:T(128)}, f32[1,256,4,128]{1,3,2,0:T(8,128)}, ...), condition=%wide.region_4.5_spmd, body=%wide.region_1.4_spmd.sunk | while | flops 275651584 | bytes 8731323 | solution.py:167
  23.5 0.7 add_compare_fusion.2
  24.1 1.6 bitcast_reduce_fusion.2
  25.7 0.6 fusion.82
  26.4 2.8 fusion.85
  29.2 1.3 fusion.66
  30.5 0.2 fusion.40
  30.7 2.0 copy.83
  32.7 0.4 convolution_bitcast_fusion.1
  33.2 0.6 copy-done.4
  33.8 0.3 fusion.38
  34.1 0.2 divide_convert_fusion
  34.3 0.1 copy.84
  34.5 3.4 convolution_convert_fusion
  37.9 0.0 all-gather.4.cloned.1.call-start
  37.9 67.6 %reduce-scatter.4.cloned.1.call-done = bf16[256,512]{1,0:T(8,128)(2,1)} async-done(((bf16[256,2048]{1,0:T(8,128)(2,1)}), bf16[256,512]{1,0:T(8,128)(2,1)}) %reduce-scatter.4.cloned.1.call-update) | async-done | bytes 262160 | tf_op jit(solution)/shard_map/reduce_scatter | solution.py:175
  105.5 1.1 multiply_reduce_fusion.3
  106.6 5.8 %psum.28 = f32[256]{0:T(256)S(1)} all-reduce(f32[256]{0:T(256)S(1)} %multiply_reduce_fusion.3), channel_id=1, replica_groups=mesh['seq'=8,'tp'=4] {'tp'}, use_global_device_ids=true, to_apply=%region_10.11 | all-reduce | flops 256 | bytes 2048 | tf_op jit(solution)/shard_map/psum | solution.py:178
  112.4 1.8 multiply_convert_fusion.4
  114.2 0.0 all-gather.4.cloned.1.call-update
  114.2 0.0 all-gather.6.cloned.1.call-start
  114.2 50.5 %all-gather.4.cloned.1.call-done = bf16[2048,512]{1,0:T(8,128)(2,1)} async-done(((bf16[256,512]{1,0:T(8,128)(2,1)}), bf16[2048,512]{1,0:T(8,128)(2,1)}) %all-gather.4.cloned.1.call-update) | async-done | bytes 2097168 | tf_op jit(solution)/shard_map/all_gather | solution.py:62
  164.8 0.0 reduce-scatter.6.cloned.1.call-start
  164.8 7.8 %reshape.155 = bf16[2,2048,512]{2,1,0:T(8,128)(2,1)} reshape(bf16[2,2048,2,256]{3,2,1,0:T(2,128)(2,1)} %param.30) | data formatting | bytes 8388608 | tf_op jit(solution)/shard_map/reshape | solution.py:63
  172.6 30.5 %all_gather.14 = f32[2048,16]{0,1:T(8,128)S(1)} all-gather(f32[256,16]{0,1:T(8,128)S(1)} %select_reduce_fusion), channel_id=1, replica_groups=mesh['seq'=8,'tp'=4] {'seq'}, dimensions={0}, use_global_device_ids=true | all-gather | bytes 147456 | tf_op jit(solution)/shard_map/all_gather | solution.py:60
  203.1 20.0 %all-gather.6.cloned.1.call-done = bf16[2048,2048]{1,0:T(8,128)(2,1)} async-done(((bf16[2048,512]{1,0:T(8,128)(2,1)}), bf16[2048,2048]{1,0:T(8,128)(2,1)}) %all-gather.6.cloned.1.call-update) | async-done | bytes 8388624 | tf_op jit(solution)/shard_map/all_gather | solution.py:62
  223.2 12.4 %fusion.29 = f32[2,2048,512]{2,1,0:T(8,128)S(1)} fusion(bf16[2,2048,512]{2,1,0:T(8,128)(2,1)} %reshape.155, bf16[2048,2048]{1,0:T(8,128)(2,1)} %all-gather.6.cloned.1.call-done), kind=kOutput, calls=%fused_computation.38 | convolution fusion | flops 8589934592 | bytes 20971520 | tf_op jit(solution)/shard_map/td,edf->etf/dot_general | solution.py:64
  235.6 6.8 %bitcast_convert_fusion = bf16[2048,2048]{1,0:T(8,128)(2,1)} fusion(bf16[2,256,2048]{2,1,0:T(8,128)(2,1)S(1)} %copy-done, f32[2,2048]{1,0:T(2,128)S(1)} %dynamic-slice_bitcast_fusion, f32[2,2048,512]{2,1,0:T(8,128)S(1)} %fusion.29), kind=kOutput, calls=%fused_computation.33 | convolution fusion | flops 4308598784 | bytes 18890752 | tf_op jit(solution)/shard_map/dot_general | solution.py:70
  242.5 0.0 reduce-scatter.8.cloned.1.call-start
  242.6 71.8 %reduce-scatter.6.cloned.1.call-done = bf16[2048,512]{1,0:T(8,128)(2,1)} async-done(((bf16[2048,2048]{1,0:T(8,128)(2,1)}), bf16[2048,512]{1,0:T(8,128)(2,1)}) %reduce-scatter.6.cloned.1.call-update) | async-done | bytes 2097168 | tf_op jit(solution)/shard_map/reduce_scatter | solution.py:71
  314.4 0.2 all-gather.8.cloned.1.call-start
  314.6 70.9 %reduce-scatter.8.cloned.1.call-done = bf16[256,512]{1,0:T(8,128)(2,1)} async-done(((bf16[2048,512]{1,0:T(8,128)(2,1)}), bf16[256,512]{1,0:T(8,128)(2,1)}) %reduce-scatter.8.cloned.1.call-update) | async-done | bytes 262160 | tf_op jit(solution)/shard_map/reduce_scatter | solution.py:72
  385.6 1.9 multiply_reduce_fusion.2
  387.5 0.0 all-gather.8.cloned.1.call-update
  387.5 8.9 %copy.85 = bf16[2048,3,512]{0,2,1:T(8,128)(2,1)} copy(bf16[2048,3,512]{2,0,1:T(8,128)(2,1)} %param.33) | data formatting | bytes 12582912 | tf_op args[14]
  396.3 7.0 %all-gather.8.cloned.1.call-done = bf16[256,2048]{1,0:T(8,128)(2,1)} async-done(((bf16[256,512]{1,0:T(8,128)(2,1)}), bf16[256,2048]{1,0:T(8,128)(2,1)}) %all-gather.8.cloned.1.call-update) | async-done | bytes 1048592 | tf_op jit(solution)/shard_map/all_gather | solution.py:199
  403.3 4.9 %fusion.27 = f32[256,3,512]{2,0,1:T(8,128)S(1)} fusion(bf16[2048,3,512]{0,2,1:T(8,128)(2,1)} %copy.85, bf16[256,2048]{1,0:T(8,128)(2,1)} %all-gather.8.cloned.1.call-done), kind=kOutput, calls=%fused_computation.36 | convolution fusion | flops 1610612736 | bytes 8912896 | tf_op jit(solution)/shard_map/dot_general | solution.py:198
  408.3 1.1 copy-done.1
  409.4 0.1 multiply_reduce_fusion
  409.6 5.9 %all-reduce = (f32[256]{0:T(256)S(1)}, f32[256]{0:T(256)S(1)}, f32[256]{0:T(256)S(1)}) all-reduce(f32[256]{0:T(256)S(1)} %get-tuple-element.94, f32[256]{0:T(256)S(1)} %get-tuple-element.127, f32[256]{0:T(256)S(1)} %get-tuple-element.93), channel_id=1, replica_groups=mesh['seq'=8,'tp'=4] {'tp'}, use_global_device_ids=true, to_apply=%region_17.18 | all-reduce | flops 768 | bytes 6144 | tf_op jit(solution)/shard_map/psum | solution.py:205
  415.5 2.4 fusion.44
  (40 shorter events, 0.3 us)
Async XLA Ops:
  7.2 228.5 %copy-start = (bf16[2,256,2048]{2,1,0:T(8,128)(2,1)S(1)}, bf16[2,256,2048]{2,1,0:T(8,128)(2,1)}, u32[]{:S(2)}) copy-start(bf16[2,256,2048]{2,1,0:T(8,128)(2,1)} %param.31) | copy-start | bytes 6291460
  7.2 98.3 %reduce-scatter.4.cloned.1.call-start = ((), (), s32[]{:S(2)}) async-start(), calls=%async_computation.3 | async-start | bytes 1310720 | tf_op jit(solution)/shard_map/reduce_scatter | solution.py:175
  15.7 6.5 %copy-start.5 = (bf16[256,512]{1,0:T(8,128)(2,1)S(1)}, bf16[256,512]{1,0:T(8,128)(2,1)}, u32[]{:S(2)}) copy-start(bf16[256,512]{1,0:T(8,128)(2,1)} %param.20) | copy-start | bytes 786436
  30.4 2.3 copy-start.6
  32.7 1.0 copy-start.4
  34.5 71.0 %copy-start.2 = (bf16[256,512]{1,0:T(8,128)(2,1)S(1)}, bf16[256,512]{1,0:T(8,128)(2,1)}, u32[]{:S(2)}) copy-start(bf16[256,512]{1,0:T(8,128)(2,1)} %param.19) | copy-start | bytes 786436
  34.5 77.9 %copy-start.9 = (f32[512]{0:T(512)S(1)}, f32[512]{0:T(512)}, u32[]{:S(2)}) copy-start(f32[512]{0:T(512)} %param.27) | copy-start | bytes 6148
  37.9 126.9 %all-gather.4.cloned.1.call-start = ((), (), s32[]{:S(2)}) async-start(), calls=%async_computation.4 | async-start | bytes 2359296 | tf_op jit(solution)/shard_map/all_gather | solution.py:62
  114.2 109.0 %all-gather.6.cloned.1.call-start = ((), (), s32[]{:S(2)}) async-start(), calls=%async_computation.5 | async-start | bytes 10485760 | tf_op jit(solution)/shard_map/all_gather | solution.py:62
  164.7 7.8 %copy-start.7 = (f32[256,8]{0,1:T(8,128)S(1)}, f32[256,8]{0,1:T(8,128)}, u32[]{:S(2)}) copy-start(f32[256,8]{0,1:T(8,128)} %param.29) | copy-start | bytes 24580
  164.8 7.8 %copy-start.8 = (s32[256,8]{0,1:T(8,128)S(1)}, s32[256,8]{0,1:T(8,128)}, u32[]{:S(2)}) copy-start(s32[256,8]{0,1:T(8,128)} %param.28) | copy-start | bytes 24580
  164.8 149.6 %reduce-scatter.6.cloned.1.call-start = ((), (), s32[]{:S(2)}) async-start(), calls=%async_computation.6 | async-start | bytes 10485760 | tf_op jit(solution)/shard_map/reduce_scatter | solution.py:71
  242.5 143.0 %copy-start.3 = (bf16[256,512]{1,0:T(8,128)(2,1)S(1)}, bf16[256,512]{1,0:T(8,128)(2,1)}, u32[]{:S(2)}) copy-start(bf16[256,512]{1,0:T(8,128)(2,1)} %reduce-scatter.4.cloned.1.call-done) | copy-start | bytes 786436
  242.5 143.0 %copy-start.10 = (f32[512]{0:T(512)S(1)}, f32[512]{0:T(512)}, u32[]{:S(2)}) copy-start(f32[512]{0:T(512)} %param.32) | copy-start | bytes 6148
  242.5 143.0 %reduce-scatter.8.cloned.1.call-start = ((), (), s32[]{:S(2)}) async-start(), calls=%async_computation.7 | async-start | bytes 2359296 | tf_op jit(solution)/shard_map/reduce_scatter | solution.py:72
  314.4 88.9 %all-gather.8.cloned.1.call-start = ((), (), s32[]{:S(2)}) async-start(), calls=%async_computation.8 | async-start | bytes 1310720 | tf_op jit(solution)/shard_map/all_gather | solution.py:199
  396.3 19.1 %copy-start.11 = (f32[512]{0:T(512)S(1)}, f32[512]{0:T(512)}, u32[]{:S(2)}) copy-start(f32[512]{0:T(512)} %param.35) | copy-start | bytes 6148
  396.3 19.2 %copy-start.12 = (f32[512]{0:T(512)S(1)}, f32[512]{0:T(512)}, u32[]{:S(2)}) copy-start(f32[512]{0:T(512)} %param.34) | copy-start | bytes 6148
  408.3 1.2 copy-start.1
Sparse Core Ops, SparseCore 0:
  38.0 67.4 reduce-scatter.3
  114.3 50.3 all-gather.3
  166.4 56.7 all-gather.5
  242.6 71.6 reduce-scatter.5
  317.8 67.7 reduce-scatter.7
  387.6 15.6 all-gather.7

commit v2 on v1

--- a/solution.py
+++ b/solution.py
@@ -49,26 +49,35 @@
     return merged / denominator[..., None]
 
 
-def dense_experts(moe_in, expert_ids, route_weights, expert_gate_up, expert_down, here, experts_all):
+def dense_experts(moe_in, expert_ids, route_weights, expert_gate_up, down_full, here, experts_all):
     local_experts = expert_gate_up.shape[0]
     hidden_quarter = expert_gate_up.shape[3]
+    tokens, quarter = moe_in.shape
+    seq_count = experts_all // local_experts
     gate_w = jnp.sum(
         route_weights[:, :, None]
         * (expert_ids[:, :, None] == jnp.arange(experts_all, dtype=jnp.int32)[None, None, :]),
         axis=1,
     )
-    gate_all = lax.all_gather(gate_w, "seq", axis=0, tiled=True)
+    gate_hi = gate_w.astype(jnp.bfloat16)
+    gate_lo = (gate_w - gate_hi.astype(jnp.float32)).astype(jnp.bfloat16)
+    info = jnp.concatenate([gate_hi, gate_lo], axis=1).reshape(-1, quarter)
+    info_rows = info.shape[0]
+    packed = jnp.concatenate([moe_in, info], axis=0)
+    gathered = lax.all_gather(packed, "seq", axis=0, tiled=False)
+    rows_q = gathered[:, :tokens].reshape(seq_count * tokens, quarter)
+    info_all = gathered[:, tokens:].reshape(seq_count * tokens, 2, experts_all).astype(jnp.float32)
+    gate_all = info_all[:, 0] + info_all[:, 1]
     gate_local = lax.dynamic_slice_in_dim(gate_all, here * local_experts, local_experts, axis=1)
-    rows = lax.all_gather(lax.all_gather(moe_in, "seq", axis=0, tiled=True), "tp", axis=1, tiled=True)
+    rows = lax.all_gather(rows_q, "tp", axis=1, tiled=True)
     gate_up = expert_gate_up.reshape(local_experts, D, 2 * hidden_quarter)
     projected = jnp.einsum("td,edf->etf", rows, gate_up, preferred_element_type=jnp.float32)
     activated = jax.nn.silu(projected[..., :hidden_quarter]) * projected[..., hidden_quarter:]
     activated = activated.astype(jnp.bfloat16).astype(jnp.float32)
     weighted = (activated * jnp.transpose(gate_local)[:, :, None]).astype(jnp.bfloat16)
-    weighted = jnp.transpose(weighted, (1, 0, 2)).reshape(rows.shape[0], local_experts * hidden_quarter)
-    down_rows = expert_down.reshape(local_experts * hidden_quarter, D)
-    partial = jnp.dot(weighted, down_rows, preferred_element_type=jnp.float32).astype(jnp.bfloat16)
-    partial = lax.psum_scatter(partial, "tp", scatter_dimension=1, tiled=True)
+    weighted = lax.all_gather(weighted, "tp", axis=2, tiled=True)
+    weighted = jnp.transpose(weighted, (1, 0, 2)).reshape(rows.shape[0], -1)
+    partial = jnp.dot(weighted, down_full, preferred_element_type=jnp.float32).astype(jnp.bfloat16)
     partial = lax.psum_scatter(partial, "seq", scatter_dimension=0, tiled=True)
     return partial.astype(jnp.float32)
 
@@ -135,6 +144,16 @@
 ):
     seq_count = lax.axis_size("seq")
     here = lax.axis_index("seq")
+    local_experts = expert_gate_up.shape[0]
+    experts_all = local_experts * seq_count
+    capacity = max(2, 3 * NEW * TOP // (2 * experts_all))
+    dense = NEW <= 2 * capacity
+    if dense:
+        tp_here = lax.axis_index("tp")
+        quarter_width = hidden.shape[1]
+        down_full = lax.all_gather(expert_down, "tp", axis=1, tiled=True)
+        down_full = lax.dynamic_slice_in_dim(down_full, tp_here * quarter_width, quarter_width, axis=2)
+        down_full = down_full.reshape(-1, quarter_width)
     local_width = new_queries.shape[1]
     local_heads = local_width // HEAD_DIM
     quarter = hidden.shape[1]
@@ -179,12 +198,9 @@
     moe_in = (residual * lax.rsqrt(square_total / D + epsilon)[:, None] * moe_gain[None, :]).astype(
         jnp.bfloat16
     )
-    local_experts = expert_gate_up.shape[0]
-    experts_all = local_experts * seq_count
-    capacity = max(2, 3 * NEW * TOP // (2 * experts_all))
-    if NEW <= 2 * capacity:
+    if dense:
         moe_term = dense_experts(
-            moe_in, expert_ids, route_weights, expert_gate_up, expert_down, here, experts_all
+            moe_in, expert_ids, route_weights, expert_gate_up, down_full, here, experts_all
         )
     else:
         moe_term = dispatch_experts(

time: 426 us -> 454 us (1.066)
  blocking collectives: 42.2 us -> 11.7 us
  matrix products: 33.7 us -> 54.9 us
  other arithmetic: 9.48 us -> 24.9 us
  waiting for transfers between devices: 288 us -> 303 us
  local copies, waits for them, and re-layouts: 36.1 us -> 41.3 us
    all_gather x2 -> x4, waiting for transfers between devices: 70.5 us -> 195 us  [the longest x1 60.9 us: dense_experts(): weighted = lax.all_gather(weighted, 'tp', axis=2, tiled=True)]
    reduce_scatter x1 -> x0, waiting for transfers between devices: 71.8 us -> none  [dense_experts(): partial = lax.psum_scatter(partial, 'tp', scatter_dimension=1, tiled=True)]
    reduce_scatter x1, waiting for transfers between devices: 67.6 us -> 32.2 us  [body(): lax.psum_scatter(attn_term.astype(jnp.bfloat16), 'tp', scatter_dimension=...]
    all_gather x1 -> x0, blocking collectives: 30.5 us -> none  [dense_experts(): gate_all = lax.all_gather(gate_w, 'seq', axis=0, tiled=True)]
    dot_general x2 -> x8, matrix products: 3.18 us -> 13.3 us  [softmax_parts(): jnp.einsum('bhtc,bche->bthe', weights.astype(jnp.bfloat16), values, prefe...]
    dot_general x2 -> x8, matrix products: 2.88 us -> 12.6 us  [softmax_parts(): jnp.einsum('bthe,bche->bhtc', queries, key_rows, preferred_element_type=j...]
    slice x0 -> x2, local copies, waits for them, and re-layouts: none -> 4.74 us  [the longest x1 3.07 us: dense_experts(): rows_q = gathered[:, :tokens].reshape(seq_count * tokens, quarter)]
  transfers between devices with their start and end apart: 6 -> 7, of which waited for: 6 -> 7; matrix products, arithmetic and copies ran while one was open for 4% -> 9% of each run, Pallas kernels for 0% -> 0%
where the time goes in v2:
time: 454 us; the launch traced here: 452 us
  waiting for transfers between devices  303 us (67%)
  matrix products  54.9 us (12%)
  local copies, waits for them, and re-layouts  41.3 us (9%)
  other arithmetic  24.9 us (5%)
  between operations  15.1 us (3%)
  blocking collectives  11.7 us (3%)
    reduce_scatter x1, waiting for transfers between devices, dense_experts(): partial = lax.psum_scatter(partial, 'seq', scatter_dimension=0, tiled=True)  67.9 us
    all_gather x1, waiting for transfers between devices, dense_experts(): weighted = lax.all_gather(weighted, 'tp', axis=2, tiled=True)  60.9 us
    all_gather x1, waiting for transfers between devices, dense_experts(): gathered = lax.all_gather(packed, 'seq', axis=0, tiled=False)  51.8 us
    all_gather x1, waiting for transfers between devices, body(): down_full = lax.all_gather(expert_down, 'tp', axis=1, tiled=True)  44.9 us
    all_gather x1, waiting for transfers between devices, dense_experts(): rows = lax.all_gather(rows_q, 'tp', axis=1, tiled=True)  37.8 us
    reduce_scatter x1, waiting for transfers between devices, body(): lax.psum_scatter(attn_term.astype(jnp.bfloat16), 'tp', scatter_dimension=...  32.2 us
    unnamed x30, local copies, waits for them, and re-layouts  23.3 us
    dot_general x8, matrix products, softmax_parts(): jnp.einsum('bhtc,bche->bthe', weights.astype(jnp.bfloat16), values, prefe...  13.3 us
  transfers between devices with their start and end apart: 7, of which 7 were waited for; matrix products, arithmetic and copies ran while one was open for 9% of the time, Pallas kernels for 0%

profile of v2, /device:TPU:0, one launch (start us, length us, event | category | flops | bytes accessed | tf_op | source)
XLA Modules:
  0.0 452.3 jit_solution(3500501600721248029)
XLA Ops:
  7.2 1.4 dynamic_slice.18
  9.3 6.5 %copy.98 = bf16[1,4096,512]{1,2,0:T(8,128)(2,1)} copy(bf16[1,4096,512]{2,1,0:T(8,128)(2,1)} %param.23) | data formatting | bytes 8388608 | tf_op args[4]
  16.1 6.5 %copy.100 = bf16[1,4096,512]{1,2,0:T(8,128)(2,1)} copy(bf16[1,4096,512]{2,1,0:T(8,128)(2,1)} %param.24) | data formatting | bytes 8388608 | tf_op args[5]
  22.7 33.6 %while.14 = (s32[]{:T(128)}, f32[1,256,4,128]{1,3,2,0:T(8,128)S(1)}, f32[1,256,4]{1,2,0:T(4,128)S(1)}, f32[1,256,4]{1,2,0:T(4,128)S(1)}, s32[]{:T(128)}, /*index...) while((s32[]{:T(128)}, ...), condition=%wide.region_4.5_spmd, body=%wide.region_1.4_spmd.sunk | while | flops 275651584 | bytes 8731331 | solution.py:186
  22.7 0.7 add_compare_fusion.2
  23.4 1.6 bitcast_reduce_fusion.2
  25.6 1.8 fusion.86
  27.5 0.7 add_compare_fusion.2
  28.2 1.6 bitcast_reduce_fusion.2
  30.5 1.8 fusion.86
  33.0 1.6 bitcast_reduce_fusion.2
  35.3 1.8 fusion.86
  37.8 1.6 bitcast_reduce_fusion.2
  40.1 1.8 fusion.86
  42.6 1.6 bitcast_reduce_fusion.2
  44.9 1.8 fusion.86
  47.4 1.6 bitcast_reduce_fusion.2
  49.7 1.8 fusion.86
  52.2 1.6 bitcast_reduce_fusion.2
  54.5 1.8 fusion.86
  56.5 1.3 fusion.68
  59.3 1.7 convolution_convert_fusion
  61.4 32.2 %reduce-scatter.3.cloned.1.call-done = bf16[256,512]{1,0:T(8,128)(2,1)} async-done(((bf16[256,2048]{1,0:T(8,128)(2,1)}), bf16[256,512]{1,0:T(8,128)(2,1)}) %reduce-scatter.3.cloned.1.call-update) | async-done | bytes 262160 | tf_op jit(solution)/shard_map/reduce_scatter | solution.py:194
  93.6 1.1 multiply_reduce_fusion.3
  94.7 5.8 %psum.28 = f32[256]{0:T(256)S(1)} all-reduce(f32[256]{0:T(256)S(1)} %multiply_reduce_fusion.3), channel_id=1, replica_groups=mesh['seq'=8,'tp'=4] {'tp'}, use_global_device_ids=true, to_apply=%region_10.11 | all-reduce | flops 256 | bytes 2048 | tf_op jit(solution)/shard_map/psum | solution.py:197
  100.5 1.1 multiply_convert_fusion.4
  101.5 0.7 pad_maximum_fusion
  102.3 51.8 %all-gather.15.cloned.1.call-done = bf16[2176,512]{1,0:T(8,128)(2,1)} async-done(((bf16[272,512]{1,0:T(8,128)(2,1)}), bf16[2176,512]{1,0:T(8,128)(2,1)}) %all-gather.15.cloned.1.call-update) | async-done | bytes 2228240 | tf_op jit(solution)/shard_map/all_gather | solution.py:67
  154.2 3.1 slice.40
  158.1 7.8 %reshape.168 = bf16[2,2048,512]{2,1,0:T(8,128)(2,1)} reshape(bf16[2,2048,2,256]{3,2,1,0:T(2,128)(2,1)} %param.30) | data formatting | bytes 8388608 | tf_op jit(solution)/shard_map/reshape | solution.py:73
  165.9 1.0 slice_convert_fusion
  166.9 2.8 reshape.170
  169.7 1.7 fusion.67
  171.3 4.5 dynamic-slice_add_fusion
  176.4 37.8 %all-gather.7.cloned.1.call-done = bf16[2048,2048]{1,0:T(8,128)(2,1)} async-done(((bf16[2048,512]{1,0:T(8,128)(2,1)}), bf16[2048,2048]{1,0:T(8,128)(2,1)}) %all-gather.7.cloned.1.call-update) | async-done | bytes 8388624 | tf_op jit(solution)/shard_map/all_gather | solution.py:72
  214.2 12.5 %fusion.31 = f32[2,2048,512]{2,1,0:T(8,128)S(1)} fusion(bf16[2,2048,512]{2,1,0:T(8,128)(2,1)} %reshape.168, bf16[2048,2048]{1,0:T(8,128)(2,1)} %all-gather.7.cloned.1.call-done), kind=kOutput, calls=%fused_computation.39 | convolution fusion | flops 8589934592 | bytes 20971520 | tf_op jit(solution)/shard_map/td,edf->etf/dot_general | solution.py:74
  226.7 2.2 multiply_convert_fusion
  229.2 44.9 %all-gather.11.cloned.1.call-done = bf16[2,1024,2048]{2,1,0:T(8,128)(2,1)} async-done(((bf16[2,256,2048]{2,1,0:T(8,128)(2,1)}), bf16[2,1024,2048]{2,1,0:T(8,128)(2,1)}) %all-gather.11.cloned.1.call-update) | async-done | bytes 8388624 | tf_op jit(solution)/shard_map/all_gather | solution.py:154
  274.1 60.9 %all-gather.9.cloned.1.call-done = bf16[2,2048,1024]{2,1,0:T(8,128)(2,1)} async-done(((bf16[2,2048,256]{2,1,0:T(8,128)(2,1)}), bf16[2,2048,1024]{2,1,0:T(8,128)(2,1)}) %all-gather.9.cloned.1.call-update) | async-done | bytes 8388624 | tf_op jit(solution)/shard_map/all_gather | solution.py:78
  335.0 9.8 %bitcast_convert_fusion = bf16[2048,512]{1,0:T(8,128)(2,1)} fusion(bf16[2,2048,1024]{2,1,0:T(8,128)(2,1)} %all-gather.9.cloned.1.call-done, bf16[2,1024,2048]{2,1,0:T(8,128)(2,1)} %all-gather.11.cloned.1.call-done, s32[]{:T(128)S(6)} %select_n.45), kind=kOutput, calls=%fused_computation.42 | convolution fusion | flops 4296015872 | bytes 12582916 | tf_op jit(solution)/shard_map/dot_general | solution.py:80
  344.9 67.9 %reduce-scatter.5.cloned.1.call-done = bf16[256,512]{1,0:T(8,128)(2,1)} async-done(((bf16[2048,512]{1,0:T(8,128)(2,1)}), bf16[256,512]{1,0:T(8,128)(2,1)}) %reduce-scatter.5.cloned.1.call-update) | async-done | bytes 262160 | tf_op jit(solution)/shard_map/reduce_scatter | solution.py:81
  412.8 1.9 multiply_reduce_fusion.2
  414.7 8.9 %copy.107 = bf16[2048,3,512]{0,2,1:T(8,128)(2,1)} copy(bf16[2048,3,512]{2,0,1:T(8,128)(2,1)} %param.33) | data formatting | bytes 12582912 | tf_op args[14]
  423.6 7.1 %all-gather.13.cloned.1.call-done = bf16[256,2048]{1,0:T(8,128)(2,1)} async-done(((bf16[256,512]{1,0:T(8,128)(2,1)}), bf16[256,2048]{1,0:T(8,128)(2,1)}) %all-gather.13.cloned.1.call-update) | async-done | bytes 1048592 | tf_op jit(solution)/shard_map/all_gather | solution.py:215
  430.7 5.1 %fusion.29 = f32[256,3,512]{2,0,1:T(8,128)S(1)} fusion(bf16[2048,3,512]{0,2,1:T(8,128)(2,1)} %copy.107, bf16[256,2048]{1,0:T(8,128)(2,1)} %all-gather.13.cloned.1.call-done), kind=kOutput, calls=%fused_computation.37 | convolution fusion | flops 1610612736 | bytes 8912896 | tf_op jit(solution)/shard_map/dot_general | solution.py:214
  435.8 1.2 copy-done.2
  437.1 5.9 %all-reduce = (f32[256]{0:T(256)S(1)}, f32[256]{0:T(256)S(1)}, f32[256]{0:T(256)S(1)}) all-reduce(f32[256]{0:T(256)S(1)} %get-tuple-element.103, f32[256]{0:T(256)S(1)} %get-tuple-element.140, f32[256]{0:T(256)S(1)} %get-tuple-element.102), channel_id=1, replica_groups=mesh['seq'=8,'tp'=4] {'tp'}, use_global_device_ids=true, to_apply=%region_16.17 | all-reduce | flops 768 | bytes 6144 | tf_op jit(solution)/shard_map/psum | solution.py:221
  443.0 2.4 fusion.45
  (95 shorter events, 12.0 us)
Async XLA Ops:
  7.2 52.1 %copy-start = (bf16[512,2048]{1,0:T(8,128)(2,1)S(1)}, bf16[512,2048]{1,0:T(8,128)(2,1)}, u32[]{:S(2)}) copy-start(bf16[512,2048]{1,0:T(8,128)(2,1)} %param.26) | copy-start | bytes 6291460
  7.2 86.4 %reduce-scatter.3.cloned.1.call-start = ((), (), s32[]{:S(2)}) async-start(), calls=%async_computation.2 | async-start | bytes 1310720 | tf_op jit(solution)/shard_map/reduce_scatter | solution.py:194
  9.3 6.5 %copy-start.5 = (bf16[256,512]{1,0:T(8,128)(2,1)S(1)}, bf16[256,512]{1,0:T(8,128)(2,1)}, u32[]{:S(2)}) copy-start(bf16[256,512]{1,0:T(8,128)(2,1)} %param.20) | copy-start | bytes 786436
  56.5 1.6 copy-start.6
  59.3 1.8 copy-start.7
  59.3 1.8 copy-start.8
  59.3 34.3 %copy-start.3 = (bf16[256,512]{1,0:T(8,128)(2,1)S(1)}, bf16[256,512]{1,0:T(8,128)(2,1)}, u32[]{:S(2)}) copy-start(bf16[256,512]{1,0:T(8,128)(2,1)} %param.19) | copy-start | bytes 786436
  59.3 41.2 %copy-start.9 = (f32[512]{0:T(512)S(1)}, f32[512]{0:T(512)}, u32[]{:S(2)}) copy-start(f32[512]{0:T(512)} %param.27) | copy-start | bytes 6148
  61.0 93.1 %all-gather.15.cloned.1.call-start = ((), (), s32[]{:S(2)}) async-start(), calls=%async_computation.8 | async-start | bytes 2506752 | tf_op jit(solution)/shard_map/all_gather | solution.py:67
  102.3 112.0 %all-gather.7.cloned.1.call-start = ((), (), s32[]{:S(2)}) async-start(), calls=%async_computation.3 | async-start | bytes 10485760 | tf_op jit(solution)/shard_map/all_gather | solution.py:72
  157.3 116.8 %all-gather.11.cloned.1.call-start = ((), (), s32[]{:S(2)}) async-start(), calls=%async_computation.5 | async-start | bytes 10485760 | tf_op jit(solution)/shard_map/all_gather | solution.py:154
  157.9 177.1 %all-gather.9.cloned.1.call-start = ((), (), s32[]{:S(2)}) async-start(), calls=%async_computation.4 | async-start | bytes 10485760 | tf_op jit(solution)/shard_map/all_gather | solution.py:78
  228.9 183.9 %reduce-scatter.5.cloned.1.call-start = ((), (), s32[]{:S(2)}) async-start(), calls=%async_computation.6 | async-start | bytes 2359296 | tf_op jit(solution)/shard_map/reduce_scatter | solution.py:81
  229.2 183.6 %copy-start.10 = (f32[512]{0:T(512)S(1)}, f32[512]{0:T(512)}, u32[]{:S(2)}) copy-start(f32[512]{0:T(512)} %param.32) | copy-start | bytes 6148
  344.8 67.9 %copy-start.4 = (bf16[256,512]{1,0:T(8,128)(2,1)S(1)}, bf16[256,512]{1,0:T(8,128)(2,1)}, u32[]{:S(2)}) copy-start(bf16[256,512]{1,0:T(8,128)(2,1)} %reduce-scatter.3.cloned.1.call-done) | copy-start | bytes 786436
  344.8 85.8 %all-gather.13.cloned.1.call-start = ((), (), s32[]{:S(2)}) async-start(), calls=%async_computation.7 | async-start | bytes 1310720 | tf_op jit(solution)/shard_map/all_gather | solution.py:215
  423.6 19.4 %copy-start.11 = (f32[512]{0:T(512)S(1)}, f32[512]{0:T(512)}, u32[]{:S(2)}) copy-start(f32[512]{0:T(512)} %param.35) | copy-start | bytes 6148
  423.6 19.4 %copy-start.12 = (f32[512]{0:T(512)S(1)}, f32[512]{0:T(512)}, u32[]{:S(2)}) copy-start(f32[512]{0:T(512)} %param.34) | copy-start | bytes 6148
  430.7 14.7 %copy-start.1 = (bf16[512,2048]{1,0:T(8,128)(2,1)S(1)}, bf16[512,2048]{1,0:T(8,128)(2,1)}, u32[]{:S(2)}) copy-start(bf16[512,2048]{1,0:T(8,128)(2,1)} %param.26) | copy-start | bytes 6291460
  435.8 1.2 copy-start.2
Sparse Core Ops, SparseCore 0:
  61.2 32.3 reduce-scatter.2
  102.4 51.7 all-gather.14
  157.4 56.7 all-gather.6
  215.7 58.2 all-gather.10
  275.5 59.3 all-gather.8
  345.0 67.7 reduce-scatter.4
  415.0 15.6 all-gather.12

commit v3 on v2

--- a/solution.py
+++ b/solution.py
@@ -190,6 +190,8 @@
         jnp.concatenate([own_total, totals], 0),
     )
     attended = attended.reshape(NEW, local_width).astype(jnp.bfloat16)
+    if dense:
+        attended, down_full = lax.optimization_barrier((attended, down_full))
     attn_term = jnp.dot(attended, out_proj, preferred_element_type=jnp.float32)
     residual = hidden.astype(jnp.float32) + lax.psum_scatter(
         attn_term.astype(jnp.bfloat16), "tp", scatter_dimension=1, tiled=True

time: 454 us -> 426 us (0.938)
  waiting for transfers between devices: 303 us -> 285 us
  matrix products: 54.9 us -> 37.3 us
  local copies, waits for them, and re-layouts: 41.3 us -> 55.5 us
  other arithmetic: 24.9 us -> 18.4 us
    transpose x0 -> x1, local copies, waits for them, and re-layouts: none -> 11.8 us  [dense_experts(): weighted = jnp.transpose(weighted, (1, 0, 2)).reshape(rows.shape[0], -1)]
    all_gather x1, waiting for transfers between devices: 44.9 us -> 35.3 us  [body(): down_full = lax.all_gather(expert_down, 'tp', axis=1, tiled=True)]
    dot_general x8 -> x3, matrix products: 13.3 us -> 4.07 us  [softmax_parts(): jnp.einsum('bhtc,bche->bthe', weights.astype(jnp.bfloat16), values, prefe...]
    dot_general x8 -> x3, matrix products: 12.6 us -> 4.58 us  [softmax_parts(): jnp.einsum('bthe,bche->bhtc', queries, key_rows, preferred_element_type=j...]
    reduce_scatter x1, waiting for transfers between devices: 32.2 us -> 24.7 us  [body(): lax.psum_scatter(attn_term.astype(jnp.bfloat16), 'tp', scatter_dimension=...]
    unnamed x30 -> x34, local copies, waits for them, and re-layouts: 23.3 us -> 23.4 us
  transfers between devices with their start and end apart: 7 -> 7, of which waited for: 7 -> 7; matrix products, arithmetic and copies ran while one was open for 9% -> 13% of each run, Pallas kernels for 0% -> 0%
where the time goes in v3:
time: 426 us; the launch traced here: 424 us
  waiting for transfers between devices  285 us (67%)
  local copies, waits for them, and re-layouts  55.5 us (13%)
  matrix products  37.3 us (9%)
  other arithmetic  18.4 us (4%)
  between operations  15.1 us (4%)
  blocking collectives  11.7 us (3%)
    reduce_scatter x1, waiting for transfers between devices, dense_experts(): partial = lax.psum_scatter(partial, 'seq', scatter_dimension=0, tiled=True)  67.7 us
    all_gather x1, waiting for transfers between devices, dense_experts(): weighted = lax.all_gather(weighted, 'tp', axis=2, tiled=True)  59.5 us
    all_gather x1, waiting for transfers between devices, dense_experts(): gathered = lax.all_gather(packed, 'seq', axis=0, tiled=False)  51.9 us
    all_gather x1, waiting for transfers between devices, dense_experts(): rows = lax.all_gather(rows_q, 'tp', axis=1, tiled=True)  38.4 us
    all_gather x1, waiting for transfers between devices, body(): down_full = lax.all_gather(expert_down, 'tp', axis=1, tiled=True)  35.3 us
    reduce_scatter x1, waiting for transfers between devices, body(): lax.psum_scatter(attn_term.astype(jnp.bfloat16), 'tp', scatter_dimension=...  24.7 us
    unnamed x34, local copies, waits for them, and re-layouts  23.4 us
    dot_general x1, matrix products, dense_experts(): jnp.einsum('td,edf->etf', rows, gate_up, preferred_element_type=jnp.float32)  12.4 us
  transfers between devices with their start and end apart: 7, of which 7 were waited for; matrix products, arithmetic and copies ran while one was open for 13% of the time, Pallas kernels for 0%

profile of v3, /device:TPU:0, one launch (start us, length us, event | category | flops | bytes accessed | tf_op | source)
XLA Modules:
  0.0 424.2 jit_solution(4387394247393528178)
XLA Ops:
  7.2 0.7 all-gather.7.cloned.1.call-update
  8.0 0.6 dynamic_slice.18
  9.6 6.5 %copy.102 = bf16[1,4096,512]{1,2,0:T(8,128)(2,1)} copy(bf16[1,4096,512]{2,1,0:T(8,128)(2,1)} %param.23) | data formatting | bytes 8388608 | tf_op args[4]
  16.1 6.6 %copy.104 = bf16[1,4096,512]{1,2,0:T(8,128)(2,1)} copy(bf16[1,4096,512]{2,1,0:T(8,128)(2,1)} %param.24) | data formatting | bytes 8388608 | tf_op args[5]
  22.7 9.7 %while.14 = (s32[]{:T(128)}, f32[1,256,4,128]{1,3,2,0:T(8,128)S(1)}, f32[1,256,4]{1,2,0:T(4,128)S(1)}, f32[1,256,4]{1,2,0:T(4,128)S(1)}, s32[]{:T(128)}, /*index...) while((s32[]{:T(128)}, ...), condition=%wide.region_4.5_spmd, body=%wide.region_1.4_spmd.sunk | while | flops 275651584 | bytes 8731323 | solution.py:186
  22.8 0.7 add_compare_fusion.2
  23.4 1.7 bitcast_reduce_fusion.2
  25.1 0.6 fusion.79
  25.8 1.8 fusion.82
  27.6 0.7 add_compare_fusion.2
  28.3 1.6 bitcast_reduce_fusion.2
  29.9 0.6 fusion.79
  30.6 1.8 fusion.82
  32.7 1.3 fusion.62
  34.2 0.4 convolution_bitcast_fusion.1
  34.6 0.3 fusion.34
  35.3 35.3 %all-gather.7.cloned.1.call-done = bf16[2,1024,2048]{2,1,0:T(8,128)(2,1)} async-done(((bf16[2,256,2048]{2,1,0:T(8,128)(2,1)}), bf16[2,1024,2048]{2,1,0:T(8,128)(2,1)}) %all-gather.7.cloned.1.call-update) | async-done | bytes 8388624 | tf_op jit(solution)/shard_map/all_gather | solution.py:154
  70.6 3.1 constant_dynamic-slice_fusion
  73.7 1.7 convolution_convert_fusion.1
  75.8 24.7 %reduce-scatter.3.cloned.1.call-done = bf16[256,512]{1,0:T(8,128)(2,1)} async-done(((bf16[256,2048]{1,0:T(8,128)(2,1)}), bf16[256,512]{1,0:T(8,128)(2,1)}) %reduce-scatter.3.cloned.1.call-update) | async-done | bytes 262160 | tf_op jit(solution)/shard_map/reduce_scatter | solution.py:196
  100.5 1.1 multiply_reduce_fusion.3
  101.6 5.8 %psum.28 = f32[256]{0:T(256)S(1)} all-reduce(f32[256]{0:T(256)S(1)} %multiply_reduce_fusion.3), channel_id=1, replica_groups=mesh['seq'=8,'tp'=4] {'tp'}, use_global_device_ids=true, to_apply=%region_10.11 | all-reduce | flops 256 | bytes 2048 | tf_op jit(solution)/shard_map/psum | solution.py:199
  107.4 1.1 multiply_convert_fusion.4
  108.5 0.7 pad_maximum_fusion
  109.3 51.9 %all-gather.15.cloned.1.call-done = bf16[2176,512]{1,0:T(8,128)(2,1)} async-done(((bf16[272,512]{1,0:T(8,128)(2,1)}), bf16[2176,512]{1,0:T(8,128)(2,1)}) %all-gather.15.cloned.1.call-update) | async-done | bytes 2228240 | tf_op jit(solution)/shard_map/all_gather | solution.py:67
  161.1 3.1 slice.40
  164.2 0.2 all-gather.11.cloned.1.call-start
  164.4 7.8 %reshape.173 = bf16[2,2048,512]{2,1,0:T(8,128)(2,1)} reshape(bf16[2,2048,2,256]{3,2,1,0:T(2,128)(2,1)} %param.30) | data formatting | bytes 8388608 | tf_op jit(solution)/shard_map/reshape | solution.py:73
  172.3 0.9 slice_convert_fusion
  173.2 2.8 reshape.176
  176.0 1.7 fusion.61
  177.7 4.5 %dynamic-slice_add_fusion = f32[2048,1,2]{2,1,0:T(1,128)S(1)} fusion(f32[2048,1,16]{2,1,0:T(1,128)S(1)} %get-tuple-element.140, s32[]{:T(128)S(6)} %select_n.45, f32[2048,1,16]{2,1,0:T(1,128)S(1)} %get-tuple-element.139), kind=kLoop, calls=%fused_computation.46 | loop fusion | flops 4096 | bytes 49156 | tf_op jit(solution)/shard_map/add | solution.py:70
  182.2 0.6 copy.110
  182.7 38.4 %all-gather.9.cloned.1.call-done = bf16[2048,2048]{1,0:T(8,128)(2,1)} async-done(((bf16[2048,512]{1,0:T(8,128)(2,1)}), bf16[2048,2048]{1,0:T(8,128)(2,1)}) %all-gather.9.cloned.1.call-update) | async-done | bytes 8388624 | tf_op jit(solution)/shard_map/all_gather | solution.py:72
  221.2 12.4 %fusion.29 = f32[2,2048,512]{2,1,0:T(8,128)S(1)} fusion(bf16[2,2048,512]{2,1,0:T(8,128)(2,1)} %reshape.173, bf16[2048,2048]{1,0:T(8,128)(2,1)} %all-gather.9.cloned.1.call-done), kind=kOutput, calls=%fused_computation.37 | convolution fusion | flops 8589934592 | bytes 20971520 | tf_op jit(solution)/shard_map/td,edf->etf/dot_general | solution.py:74
  233.6 2.2 multiply_convert_fusion
  235.9 59.5 %all-gather.11.cloned.1.call-done = bf16[2,2048,1024]{2,1,0:T(8,128)(2,1)} async-done(((bf16[2,2048,256]{2,1,0:T(8,128)(2,1)}), bf16[2,2048,1024]{2,1,0:T(8,128)(2,1)}) %all-gather.11.cloned.1.call-update) | async-done | bytes 8388624 | tf_op jit(solution)/shard_map/all_gather | solution.py:78
  295.4 11.8 %copy.111 = bf16[2048,2,1024]{0,2,1:T(8,128)(2,1)} copy(bf16[2048,2,1024]{2,0,1:T(8,128)(2,1)} %bitcast.155) | data formatting | bytes 16777216 | tf_op jit(solution)/shard_map/transpose | solution.py:79
  307.2 9.5 %convolution_convert_fusion = bf16[2048,512]{1,0:T(8,128)(2,1)} fusion(bf16[2048,2048]{0,1:T(8,128)(2,1)} %bitcast.156, bf16[2048,512]{1,0:T(8,128)(2,1)S(1)} %bitcast.161), kind=kOutput, calls=%fused_computation.41 | convolution fusion | flops 4296015872 | bytes 12582912 | tf_op jit(solution)/shard_map/dot_general | solution.py:80
  316.7 0.3 all-gather.13.cloned.1.call-start
  317.0 67.7 %reduce-scatter.5.cloned.1.call-done = bf16[256,512]{1,0:T(8,128)(2,1)} async-done(((bf16[2048,512]{1,0:T(8,128)(2,1)}), bf16[256,512]{1,0:T(8,128)(2,1)}) %reduce-scatter.5.cloned.1.call-update) | async-done | bytes 262160 | tf_op jit(solution)/shard_map/reduce_scatter | solution.py:81
  384.7 1.9 multiply_reduce_fusion.2
  386.6 8.9 %copy.112 = bf16[2048,3,512]{0,2,1:T(8,128)(2,1)} copy(bf16[2048,3,512]{2,0,1:T(8,128)(2,1)} %param.33) | data formatting | bytes 12582912 | tf_op args[14]
  395.5 7.1 %all-gather.13.cloned.1.call-done = bf16[256,2048]{1,0:T(8,128)(2,1)} async-done(((bf16[256,512]{1,0:T(8,128)(2,1)}), bf16[256,2048]{1,0:T(8,128)(2,1)}) %all-gather.13.cloned.1.call-update) | async-done | bytes 1048592 | tf_op jit(solution)/shard_map/all_gather | solution.py:217
  402.7 5.1 %fusion.27 = f32[256,3,512]{2,0,1:T(8,128)S(1)} fusion(bf16[2048,3,512]{0,2,1:T(8,128)(2,1)} %copy.112, bf16[256,2048]{1,0:T(8,128)(2,1)} %all-gather.13.cloned.1.call-done), kind=kOutput, calls=%fused_computation.35 | convolution fusion | flops 1610612736 | bytes 8912896 | tf_op jit(solution)/shard_map/dot_general | solution.py:216
  407.7 1.2 copy-done.2
  409.1 5.9 %all-reduce = (f32[256]{0:T(256)S(1)}, f32[256]{0:T(256)S(1)}, f32[256]{0:T(256)S(1)}) all-reduce(f32[256]{0:T(256)S(1)} %get-tuple-element.107, f32[256]{0:T(256)S(1)} %get-tuple-element.144, f32[256]{0:T(256)S(1)} %get-tuple-element.106), channel_id=1, replica_groups=mesh['seq'=8,'tp'=4] {'tp'}, use_global_device_ids=true, to_apply=%region_16.17 | all-reduce | flops 768 | bytes 6144 | tf_op jit(solution)/shard_map/psum | solution.py:223
  415.0 2.4 fusion.40
  (66 shorter events, 2.0 us)
Async XLA Ops:
  7.2 66.5 %copy-start = (bf16[512,2048]{1,0:T(8,128)(2,1)S(1)}, bf16[512,2048]{1,0:T(8,128)(2,1)}, u32[]{:S(2)}) copy-start(bf16[512,2048]{1,0:T(8,128)(2,1)} %param.26) | copy-start | bytes 6291460
  7.2 0.8 copy-start.14
  7.2 2.1 copy-start.6
  7.2 63.4 %all-gather.7.cloned.1.call-start = ((), (), s32[]{:S(2)}) async-start(), calls=%async_computation.2 | async-start | bytes 10485760 | tf_op jit(solution)/shard_map/all_gather | solution.py:154
  7.9 92.6 %reduce-scatter.3.cloned.1.call-start = ((), (), s32[]{:S(2)}) async-start(), calls=%async_computation.3 | async-start | bytes 1310720 | tf_op jit(solution)/shard_map/reduce_scatter | solution.py:196
  32.6 1.6 copy-start.7
  73.7 1.8 copy-start.8
  73.7 1.8 copy-start.9
  73.7 26.8 %copy-start.3 = (bf16[256,512]{1,0:T(8,128)(2,1)S(1)}, bf16[256,512]{1,0:T(8,128)(2,1)}, u32[]{:S(2)}) copy-start(bf16[256,512]{1,0:T(8,128)(2,1)} %param.19) | copy-start | bytes 786436
  73.7 33.7 %copy-start.10 = (f32[512]{0:T(512)S(1)}, f32[512]{0:T(512)}, u32[]{:S(2)}) copy-start(f32[512]{0:T(512)} %param.27) | copy-start | bytes 6148
  75.4 85.7 %all-gather.15.cloned.1.call-start = ((), (), s32[]{:S(2)}) async-start(), calls=%async_computation.8 | async-start | bytes 2506752 | tf_op jit(solution)/shard_map/all_gather | solution.py:67
  109.2 112.0 %all-gather.9.cloned.1.call-start = ((), (), s32[]{:S(2)}) async-start(), calls=%async_computation.4 | async-start | bytes 10485760 | tf_op jit(solution)/shard_map/all_gather | solution.py:72
  164.2 131.2 %all-gather.11.cloned.1.call-start = ((), (), s32[]{:S(2)}) async-start(), calls=%async_computation.5 | async-start | bytes 10485760 | tf_op jit(solution)/shard_map/all_gather | solution.py:78
  235.8 148.9 %reduce-scatter.5.cloned.1.call-start = ((), (), s32[]{:S(2)}) async-start(), calls=%async_computation.6 | async-start | bytes 2359296 | tf_op jit(solution)/shard_map/reduce_scatter | solution.py:81
  295.4 11.8 %copy-start.5 = (bf16[2,1024,512]{2,1,0:T(8,128)(2,1)S(1)}, bf16[2,1024,512]{2,1,0:T(8,128)(2,1)}, u32[]{:S(2)}) copy-start(bf16[2,1024,512]{2,1,0:T(8,128)(2,1)} %constant_dynamic-slice_fusion) | copy-start | bytes 6291460
  316.7 68.0 %copy-start.4 = (bf16[256,512]{1,0:T(8,128)(2,1)S(1)}, bf16[256,512]{1,0:T(8,128)(2,1)}, u32[]{:S(2)}) copy-start(bf16[256,512]{1,0:T(8,128)(2,1)} %reduce-scatter.3.cloned.1.call-done) | copy-start | bytes 786436
  316.7 68.0 %copy-start.11 = (f32[512]{0:T(512)S(1)}, f32[512]{0:T(512)}, u32[]{:S(2)}) copy-start(f32[512]{0:T(512)} %param.32) | copy-start | bytes 6148
  316.7 86.0 %all-gather.13.cloned.1.call-start = ((), (), s32[]{:S(2)}) async-start(), calls=%async_computation.7 | async-start | bytes 1310720 | tf_op jit(solution)/shard_map/all_gather | solution.py:217
  395.5 19.4 %copy-start.12 = (f32[512]{0:T(512)S(1)}, f32[512]{0:T(512)}, u32[]{:S(2)}) copy-start(f32[512]{0:T(512)} %param.35) | copy-start | bytes 6148
  395.5 19.4 %copy-start.13 = (f32[512]{0:T(512)S(1)}, f32[512]{0:T(512)}, u32[]{:S(2)}) copy-start(f32[512]{0:T(512)} %param.34) | copy-start | bytes 6148
  402.7 14.7 %copy-start.1 = (bf16[512,2048]{1,0:T(8,128)(2,1)S(1)}, bf16[512,2048]{1,0:T(8,128)(2,1)}, u32[]{:S(2)}) copy-start(bf16[512,2048]{1,0:T(8,128)(2,1)} %param.26) | copy-start | bytes 6291460
  407.7 1.2 copy-start.2
Sparse Core Ops, SparseCore 0:
  9.6 60.9 all-gather.6
  75.6 24.8 reduce-scatter.2
  109.3 51.7 all-gather.14
  164.3 56.7 all-gather.8
  235.9 59.3 all-gather.10
  316.8 67.8 reduce-scatter.4
  386.9 15.6 all-gather.12

commit v4 on v3

--- a/solution.py
+++ b/solution.py
@@ -59,25 +59,27 @@
         * (expert_ids[:, :, None] == jnp.arange(experts_all, dtype=jnp.int32)[None, None, :]),
         axis=1,
     )
-    gate_hi = gate_w.astype(jnp.bfloat16)
-    gate_lo = (gate_w - gate_hi.astype(jnp.float32)).astype(jnp.bfloat16)
-    info = jnp.concatenate([gate_hi, gate_lo], axis=1).reshape(-1, quarter)
-    info_rows = info.shape[0]
+    gate_t = jnp.transpose(gate_w)
+    gate_hi = gate_t.astype(jnp.bfloat16)
+    gate_lo = (gate_t - gate_hi.astype(jnp.float32)).astype(jnp.bfloat16)
+    info = jnp.concatenate([gate_hi, gate_lo], axis=0).reshape(-1, quarter)
     packed = jnp.concatenate([moe_in, info], axis=0)
     gathered = lax.all_gather(packed, "seq", axis=0, tiled=False)
     rows_q = gathered[:, :tokens].reshape(seq_count * tokens, quarter)
-    info_all = gathered[:, tokens:].reshape(seq_count * tokens, 2, experts_all).astype(jnp.float32)
+    info_all = gathered[:, tokens:].reshape(seq_count, 2, experts_all, tokens).astype(jnp.float32)
     gate_all = info_all[:, 0] + info_all[:, 1]
     gate_local = lax.dynamic_slice_in_dim(gate_all, here * local_experts, local_experts, axis=1)
+    gate_local = jnp.transpose(gate_local, (1, 0, 2)).reshape(local_experts, seq_count * tokens)
     rows = lax.all_gather(rows_q, "tp", axis=1, tiled=True)
     gate_up = expert_gate_up.reshape(local_experts, D, 2 * hidden_quarter)
     projected = jnp.einsum("td,edf->etf", rows, gate_up, preferred_element_type=jnp.float32)
     activated = jax.nn.silu(projected[..., :hidden_quarter]) * projected[..., hidden_quarter:]
     activated = activated.astype(jnp.bfloat16).astype(jnp.float32)
-    weighted = (activated * jnp.transpose(gate_local)[:, :, None]).astype(jnp.bfloat16)
+    weighted = (activated * gate_local[:, :, None]).astype(jnp.bfloat16)
     weighted = lax.all_gather(weighted, "tp", axis=2, tiled=True)
-    weighted = jnp.transpose(weighted, (1, 0, 2)).reshape(rows.shape[0], -1)
-    partial = jnp.dot(weighted, down_full, preferred_element_type=jnp.float32).astype(jnp.bfloat16)
+    partial = jnp.einsum(
+        "etf,efd->td", weighted, down_full, preferred_element_type=jnp.float32
+    ).astype(jnp.bfloat16)
     partial = lax.psum_scatter(partial, "seq", scatter_dimension=0, tiled=True)
     return partial.astype(jnp.float32)
 
@@ -153,7 +155,6 @@
         quarter_width = hidden.shape[1]
         down_full = lax.all_gather(expert_down, "tp", axis=1, tiled=True)
         down_full = lax.dynamic_slice_in_dim(down_full, tp_here * quarter_width, quarter_width, axis=2)
-        down_full = down_full.reshape(-1, quarter_width)
     local_width = new_queries.shape[1]
     local_heads = local_width // HEAD_DIM
     quarter = hidden.shape[1]

time: 426 us -> 414 us (0.972)
  local copies, waits for them, and re-layouts: 55.5 us -> 38.4 us
  waiting for transfers between devices: 285 us -> 300 us
  other arithmetic: 18.4 us -> 12.7 us
    transpose x1 -> x0, local copies, waits for them, and re-layouts: 11.8 us -> none  [dense_experts(): weighted = jnp.transpose(weighted, (1, 0, 2)).reshape(rows.shape[0], -1)]
    all_gather x1, waiting for transfers between devices: 38.4 us -> 48 us  [dense_experts(): rows = lax.all_gather(rows_q, 'tp', axis=1, tiled=True)]
    all_gather x1, waiting for transfers between devices: 35.3 us -> 40.1 us  [body(): down_full = lax.all_gather(expert_down, 'tp', axis=1, tiled=True)]
    add x1, other arithmetic: 4.49 us -> 0.02 us  [dense_experts(): gate_all = info_all[:, 0] + info_all[:, 1]]
    unnamed x34 -> x35, local copies, waits for them, and re-layouts: 23.4 us -> 23.3 us
  transfers between devices with their start and end apart: 7 -> 7, of which waited for: 7 -> 7; matrix products, arithmetic and copies ran while one was open for 13% -> 10% of each run, Pallas kernels for 0% -> 0%
where the time goes in v4:
time: 414 us; the launch traced here: 412 us
  waiting for transfers between devices  300 us (72%)
  local copies, waits for them, and re-layouts  38.4 us (9%)
  matrix products  33.6 us (8%)
  between operations  15.1 us (4%)
  other arithmetic  12.7 us (3%)
  blocking collectives  11.7 us (3%)
    reduce_scatter x1, waiting for transfers between devices, dense_experts(): partial = lax.psum_scatter(partial, 'seq', scatter_dimension=0, tiled=True)  68 us
    all_gather x1, waiting for transfers between devices, dense_experts(): weighted = lax.all_gather(weighted, 'tp', axis=2, tiled=True)  59.3 us
    all_gather x1, waiting for transfers between devices, dense_experts(): gathered = lax.all_gather(packed, 'seq', axis=0, tiled=False)  51.9 us
    all_gather x1, waiting for transfers between devices, dense_experts(): rows = lax.all_gather(rows_q, 'tp', axis=1, tiled=True)  48 us
    all_gather x1, waiting for transfers between devices, body(): down_full = lax.all_gather(expert_down, 'tp', axis=1, tiled=True)  40.1 us
    reduce_scatter x1, waiting for transfers between devices, body(): lax.psum_scatter(attn_term.astype(jnp.bfloat16), 'tp', scatter_dimension=...  24.9 us
    unnamed x35, local copies, waits for them, and re-layouts  23.3 us
    dot_general x1, matrix products, dense_experts(): jnp.einsum('td,edf->etf', rows, gate_up, preferred_element_type=jnp.float32)  12.4 us
  transfers between devices with their start and end apart: 7, of which 7 were waited for; matrix products, arithmetic and copies ran while one was open for 10% of the time, Pallas kernels for 0%

profile of v4, /device:TPU:0, one launch (start us, length us, event | category | flops | bytes accessed | tf_op | source)
XLA Modules:
  0.0 412.0 jit_solution(3361592434585957795)
XLA Ops:
  7.2 0.7 all-gather.7.cloned.1.call-update
  8.0 0.6 dynamic_slice.18
  9.3 0.1 copy.96
  9.4 0.2 copy.99
  9.6 6.4 %copy.95 = bf16[1,4096,512]{1,2,0:T(8,128)(2,1)} copy(bf16[1,4096,512]{2,1,0:T(8,128)(2,1)} %param.23) | data formatting | bytes 8388608 | tf_op args[4]
  16.0 6.6 %copy.97 = bf16[1,4096,512]{1,2,0:T(8,128)(2,1)} copy(bf16[1,4096,512]{2,1,0:T(8,128)(2,1)} %param.24) | data formatting | bytes 8388608 | tf_op args[5]
  22.7 4.9 %while.14 = (s32[]{:T(128)}, f32[1,256,4,128]{1,3,2,0:T(8,128)S(1)}, f32[1,256,4]{1,2,0:T(4,128)S(1)}, f32[1,256,4]{1,2,0:T(4,128)S(1)}, s32[]{:T(128)}, /*index...) while((s32[]{:T(128)}, ...), condition=%wide.region_4.5_spmd, body=%wide.region_1.4_spmd.sunk | while | flops 275651584 | bytes 8731323 | solution.py:187
  22.7 0.7 add_compare_fusion.2
  23.4 1.7 bitcast_reduce_fusion.2
  25.0 0.6 fusion.80
  25.7 1.8 fusion.83
  27.6 0.2 copy.100
  27.8 1.3 fusion.63
  29.1 0.2 fusion.36
  29.3 0.4 convolution_bitcast_fusion.1
  29.8 0.3 fusion.34
  30.1 0.2 divide_convert_fusion
  30.3 0.1 copy.101
  30.5 40.1 %all-gather.7.cloned.1.call-done = bf16[2,1024,2048]{2,1,0:T(8,128)(2,1)} async-done(((bf16[2,256,2048]{2,1,0:T(8,128)(2,1)}), bf16[2,1024,2048]{2,1,0:T(8,128)(2,1)}) %all-gather.7.cloned.1.call-update) | async-done | bytes 8388624 | tf_op jit(solution)/shard_map/all_gather | solution.py:156
  70.6 3.0 constant_dynamic-slice_fusion
  73.7 1.7 convolution_convert_fusion
  75.4 0.0 all-gather.15.cloned.1.call-start
  75.5 24.9 %reduce-scatter.3.cloned.1.call-done = bf16[256,512]{1,0:T(8,128)(2,1)} async-done(((bf16[256,2048]{1,0:T(8,128)(2,1)}), bf16[256,512]{1,0:T(8,128)(2,1)}) %reduce-scatter.3.cloned.1.call-update) | async-done | bytes 262160 | tf_op jit(solution)/shard_map/reduce_scatter | solution.py:197
  100.4 1.1 multiply_reduce_fusion.3
  101.6 5.8 %psum.28 = f32[256]{0:T(256)S(1)} all-reduce(f32[256]{0:T(256)S(1)} %multiply_reduce_fusion.3), channel_id=1, replica_groups=mesh['seq'=8,'tp'=4] {'tp'}, use_global_device_ids=true, to_apply=%region_10.11 | all-reduce | flops 256 | bytes 2048 | tf_op jit(solution)/shard_map/psum | solution.py:200
  107.3 1.1 multiply_convert_fusion.4
  108.4 0.7 pad_maximum_fusion
  109.1 0.0 all-gather.9.cloned.1.call-start
  109.2 51.9 %all-gather.15.cloned.1.call-done = bf16[2176,512]{1,0:T(8,128)(2,1)} async-done(((bf16[272,512]{1,0:T(8,128)(2,1)}), bf16[2176,512]{1,0:T(8,128)(2,1)}) %all-gather.15.cloned.1.call-update) | async-done | bytes 2228240 | tf_op jit(solution)/shard_map/all_gather | solution.py:67
  161.1 3.1 slice.40
  164.1 0.0 all-gather.11.cloned.1.call-start
  164.2 7.8 %reshape.166 = bf16[2,2048,512]{2,1,0:T(8,128)(2,1)} reshape(bf16[2,2048,2,256]{3,2,1,0:T(2,128)(2,1)} %param.30) | data formatting | bytes 8388608 | tf_op jit(solution)/shard_map/reshape | solution.py:74
  172.0 1.0 slice_convert_fusion
  173.1 48.0 %all-gather.9.cloned.1.call-done = bf16[2048,2048]{1,0:T(8,128)(2,1)} async-done(((bf16[2048,512]{1,0:T(8,128)(2,1)}), bf16[2048,2048]{1,0:T(8,128)(2,1)}) %all-gather.9.cloned.1.call-update) | async-done | bytes 8388624 | tf_op jit(solution)/shard_map/all_gather | solution.py:73
  221.1 12.4 %fusion.29 = f32[2,2048,512]{2,1,0:T(8,128)S(1)} fusion(bf16[2,2048,512]{2,1,0:T(8,128)(2,1)} %reshape.166, bf16[2048,2048]{1,0:T(8,128)(2,1)} %all-gather.9.cloned.1.call-done), kind=kOutput, calls=%fused_computation.37 | convolution fusion | flops 8589934592 | bytes 20971520 | tf_op jit(solution)/shard_map/td,edf->etf/dot_general | solution.py:75
  233.6 2.2 multiply_convert_fusion
  235.8 0.2 reduce-scatter.5.cloned.1.call-start
  236.0 59.3 %all-gather.11.cloned.1.call-done = bf16[2,2048,1024]{2,1,0:T(8,128)(2,1)} async-done(((bf16[2,2048,256]{2,1,0:T(8,128)(2,1)}), bf16[2,2048,1024]{2,1,0:T(8,128)(2,1)}) %all-gather.11.cloned.1.call-update) | async-done | bytes 8388624 | tf_op jit(solution)/shard_map/all_gather | solution.py:79
  295.3 9.1 %bitcast_convert_fusion = bf16[2048,512]{1,0:T(8,128)(2,1)} fusion(bf16[2,2048,1024]{2,1,0:T(8,128)(2,1)} %all-gather.11.cloned.1.call-done, bf16[2,1024,512]{2,1,0:T(8,128)(2,1)S(1)} %copy-done.5), kind=kOutput, calls=%fused_computation.40 | convolution fusion | flops 4296015872 | bytes 12582912 | tf_op jit(solution)/shard_map/etf,efd->td/dot_general | solution.py:80
  304.5 68.0 %reduce-scatter.5.cloned.1.call-done = bf16[256,512]{1,0:T(8,128)(2,1)} async-done(((bf16[2048,512]{1,0:T(8,128)(2,1)}), bf16[256,512]{1,0:T(8,128)(2,1)}) %reduce-scatter.5.cloned.1.call-update) | async-done | bytes 262160 | tf_op jit(solution)/shard_map/reduce_scatter | solution.py:83
  372.5 1.9 multiply_reduce_fusion.2
  374.4 8.9 %copy.103 = bf16[2048,3,512]{0,2,1:T(8,128)(2,1)} copy(bf16[2048,3,512]{2,0,1:T(8,128)(2,1)} %param.33) | data formatting | bytes 12582912 | tf_op args[14]
  383.3 7.1 %all-gather.13.cloned.1.call-done = bf16[256,2048]{1,0:T(8,128)(2,1)} async-done(((bf16[256,512]{1,0:T(8,128)(2,1)}), bf16[256,2048]{1,0:T(8,128)(2,1)}) %all-gather.13.cloned.1.call-update) | async-done | bytes 1048592 | tf_op jit(solution)/shard_map/all_gather | solution.py:218
  390.4 5.1 %fusion.27 = f32[256,3,512]{2,0,1:T(8,128)S(1)} fusion(bf16[2048,3,512]{0,2,1:T(8,128)(2,1)} %copy.103, bf16[256,2048]{1,0:T(8,128)(2,1)} %all-gather.13.cloned.1.call-done), kind=kOutput, calls=%fused_computation.35 | convolution fusion | flops 1610612736 | bytes 8912896 | tf_op jit(solution)/shard_map/dot_general | solution.py:217
  395.5 1.2 copy-done.2
  396.7 0.1 multiply_reduce_fusion
  396.8 5.9 %all-reduce = (f32[256]{0:T(256)S(1)}, f32[256]{0:T(256)S(1)}, f32[256]{0:T(256)S(1)}) all-reduce(f32[256]{0:T(256)S(1)} %get-tuple-element.107, f32[256]{0:T(256)S(1)} %get-tuple-element.142, f32[256]{0:T(256)S(1)} %get-tuple-element.106), channel_id=1, replica_groups=mesh['seq'=8,'tp'=4] {'tp'}, use_global_device_ids=true, to_apply=%region_16.17 | all-reduce | flops 768 | bytes 6144 | tf_op jit(solution)/shard_map/psum | solution.py:224
  402.7 2.4 fusion.40
  (58 shorter events, 0.6 us)
Async XLA Ops:
  7.2 66.5 %copy-start = (bf16[512,2048]{1,0:T(8,128)(2,1)S(1)}, bf16[512,2048]{1,0:T(8,128)(2,1)}, u32[]{:S(2)}) copy-start(bf16[512,2048]{1,0:T(8,128)(2,1)} %param.26) | copy-start | bytes 6291460
  7.2 0.8 copy-start.14
  7.2 2.1 copy-start.6
  7.2 63.4 %all-gather.7.cloned.1.call-start = ((), (), s32[]{:S(2)}) async-start(), calls=%async_computation.2 | async-start | bytes 10485760 | tf_op jit(solution)/shard_map/all_gather | solution.py:156
  7.9 92.5 %reduce-scatter.3.cloned.1.call-start = ((), (), s32[]{:S(2)}) async-start(), calls=%async_computation.3 | async-start | bytes 1310720 | tf_op jit(solution)/shard_map/reduce_scatter | solution.py:197
  27.8 1.6 copy-start.7
  73.6 1.8 copy-start.8
  73.6 1.8 copy-start.9
  73.6 26.8 %copy-start.3 = (bf16[256,512]{1,0:T(8,128)(2,1)S(1)}, bf16[256,512]{1,0:T(8,128)(2,1)}, u32[]{:S(2)}) copy-start(bf16[256,512]{1,0:T(8,128)(2,1)} %param.19) | copy-start | bytes 786436
  73.7 33.7 %copy-start.10 = (f32[512]{0:T(512)S(1)}, f32[512]{0:T(512)}, u32[]{:S(2)}) copy-start(f32[512]{0:T(512)} %param.27) | copy-start | bytes 6148
  75.4 85.7 %all-gather.15.cloned.1.call-start = ((), (), s32[]{:S(2)}) async-start(), calls=%async_computation.8 | async-start | bytes 2506752 | tf_op jit(solution)/shard_map/all_gather | solution.py:67
  109.1 111.9 %all-gather.9.cloned.1.call-start = ((), (), s32[]{:S(2)}) async-start(), calls=%async_computation.4 | async-start | bytes 10485760 | tf_op jit(solution)/shard_map/all_gather | solution.py:73
  164.1 131.2 %all-gather.11.cloned.1.call-start = ((), (), s32[]{:S(2)}) async-start(), calls=%async_computation.5 | async-start | bytes 10485760 | tf_op jit(solution)/shard_map/all_gather | solution.py:79
  235.7 59.6 %copy-start.5 = (bf16[2,1024,512]{2,1,0:T(8,128)(2,1)S(1)}, bf16[2,1024,512]{2,1,0:T(8,128)(2,1)}, u32[]{:S(2)}) copy-start(bf16[2,1024,512]{2,1,0:T(8,128)(2,1)} %constant_dynamic-slice_fusion) | copy-start | bytes 6291460
  235.8 136.7 %reduce-scatter.5.cloned.1.call-start = ((), (), s32[]{:S(2)}) async-start(), calls=%async_computation.6 | async-start | bytes 2359296 | tf_op jit(solution)/shard_map/reduce_scatter | solution.py:83
  304.4 68.0 %copy-start.4 = (bf16[256,512]{1,0:T(8,128)(2,1)S(1)}, bf16[256,512]{1,0:T(8,128)(2,1)}, u32[]{:S(2)}) copy-start(bf16[256,512]{1,0:T(8,128)(2,1)} %reduce-scatter.3.cloned.1.call-done) | copy-start | bytes 786436
  304.4 68.0 %copy-start.11 = (f32[512]{0:T(512)S(1)}, f32[512]{0:T(512)}, u32[]{:S(2)}) copy-start(f32[512]{0:T(512)} %param.32) | copy-start | bytes 6148
  304.5 86.0 %all-gather.13.cloned.1.call-start = ((), (), s32[]{:S(2)}) async-start(), calls=%async_computation.7 | async-start | bytes 1310720 | tf_op jit(solution)/shard_map/all_gather | solution.py:218
  383.3 19.4 %copy-start.12 = (f32[512]{0:T(512)S(1)}, f32[512]{0:T(512)}, u32[]{:S(2)}) copy-start(f32[512]{0:T(512)} %param.35) | copy-start | bytes 6148
  383.3 19.4 %copy-start.13 = (f32[512]{0:T(512)S(1)}, f32[512]{0:T(512)}, u32[]{:S(2)}) copy-start(f32[512]{0:T(512)} %param.34) | copy-start | bytes 6148
  390.4 14.7 %copy-start.1 = (bf16[512,2048]{1,0:T(8,128)(2,1)S(1)}, bf16[512,2048]{1,0:T(8,128)(2,1)}, u32[]{:S(2)}) copy-start(bf16[512,2048]{1,0:T(8,128)(2,1)} %param.26) | copy-start | bytes 6291460
  395.5 1.2 copy-start.2
Sparse Core Ops, SparseCore 0:
  9.6 60.9 all-gather.6
  75.5 24.8 reduce-scatter.2
  109.3 51.7 all-gather.14
  164.3 56.7 all-gather.8
  235.9 59.3 all-gather.10
  304.6 67.8 reduce-scatter.4
  374.7 15.6 all-gather.12

commit v5 on v4

--- a/solution.py
+++ b/solution.py
@@ -1,8 +1,11 @@
+import functools
 import math
 
 import jax
 import jax.numpy as jnp
 from jax import lax
+from jax.experimental import pallas as pl
+from jax.experimental.pallas import tpu as pltpu
 from jax.sharding import PartitionSpec as P
 
 D = 2048
@@ -14,39 +17,86 @@
 epsilon = 1e-05
 
 
-def softmax_parts(queries, key_rows, values, allowed):
-    scores = jnp.einsum(
-        "bthe,bche->bhtc", queries, key_rows, preferred_element_type=jnp.float32
-    ) / math.sqrt(HEAD_DIM)
-    scores = jnp.where(allowed[:, None], scores, -1e30)
-    row_max = jnp.max(scores, axis=3)
-    weights = jnp.where(allowed[:, None], jnp.exp(scores - row_max[..., None]), 0.0)
-    row_total = jnp.sum(weights, axis=3)
-    partial_out = jnp.einsum(
-        "bhtc,bche->bthe", weights.astype(jnp.bfloat16), values, preferred_element_type=jnp.float32
-    )
-    return (partial_out, jnp.swapaxes(row_max, 1, 2), jnp.swapaxes(row_total, 1, 2))
-
-
-def combine_parts(first, second):
-    out_a, max_a, total_a = first
-    out_b, max_b, total_b = second
-    joint = jnp.maximum(max_a, max_b)
-    factor_a = jnp.exp(max_a - joint)
-    factor_b = jnp.exp(max_b - joint)
-    return (
-        out_a * factor_a[..., None] + out_b * factor_b[..., None],
-        joint,
-        total_a * factor_a + total_b * factor_b,
-    )
-
-
-def merge_parts(pieces, maxima, totals):
-    overall = jnp.max(maxima, axis=0)
-    factor = jnp.exp(maxima - overall[None])
-    denominator = jnp.sum(totals * factor, axis=0)
-    merged = jnp.sum(pieces * factor[..., None], axis=0)
-    return merged / denominator[..., None]
+def flash_kernel(len_ref, q_ref, k_ref, v_ref, nk_ref, nv_ref, o_ref, m_sc, l_sc, acc_sc, *, block, heads, steps):
+    j = pl.program_id(0)
+    length = len_ref[0]
+    valid = (length + block - 1) // block
+    tokens = q_ref.shape[0]
+    scale = 1.0 / math.sqrt(HEAD_DIM)
+
+    @pl.when(j == 0)
+    def _():
+        m_sc[...] = jnp.full(m_sc.shape, -1e30, jnp.float32)
+        l_sc[...] = jnp.zeros(l_sc.shape, jnp.float32)
+        acc_sc[...] = jnp.zeros(acc_sc.shape, jnp.float32)
+
+    def update(keys_ref, values_ref, allowed):
+        for h in range(heads):
+            cols = slice(h * HEAD_DIM, (h + 1) * HEAD_DIM)
+            q = q_ref[:, cols]
+            k = keys_ref[:, cols]
+            s = lax.dot_general(q, k, (((1,), (1,)), ((), ())), preferred_element_type=jnp.float32) * scale
+            s = jnp.where(allowed, s, -1e30)
+            m_old = m_sc[h]
+            m_new = jnp.maximum(m_old, jnp.max(s, axis=1, keepdims=True))
+            alpha = jnp.exp(m_old - m_new)
+            p = jnp.where(allowed, jnp.exp(s - m_new), 0.0)
+            l_sc[h] = alpha * l_sc[h] + jnp.sum(p, axis=1, keepdims=True)
+            pv = jnp.dot(p.astype(jnp.bfloat16), values_ref[:, cols], preferred_element_type=jnp.float32)
+            acc_sc[:, cols] = alpha * acc_sc[:, cols] + pv
+            m_sc[h] = m_new
+
+    @pl.when(j < valid)
+    def _():
+        pos = j * block + lax.broadcasted_iota(jnp.int32, (tokens, block), 1)
+        update(k_ref, v_ref, pos < length)
+
+    @pl.when(j == steps - 1)
+    def _():
+        row = lax.broadcasted_iota(jnp.int32, (tokens, tokens), 0)
+        col = lax.broadcasted_iota(jnp.int32, (tokens, tokens), 1)
+        update(nk_ref, nv_ref, col <= row)
+        for h in range(heads):
+            cols = slice(h * HEAD_DIM, (h + 1) * HEAD_DIM)
+            o_ref[:, cols] = (acc_sc[:, cols] / l_sc[h]).astype(o_ref.dtype)
+
+
+def flash_attention(length, queries, cache_k, cache_v, new_k, new_v, block=1024):
+    tokens, width = queries.shape
+    span = cache_k.shape[0]
+    block = min(block, span)
+    heads = width // HEAD_DIM
+    steps = span // block + 1
+    last = span // block - 1
+
+    def cache_map(j, len_ref):
+        valid = (len_ref[0] + block - 1) // block
+        return (jnp.minimum(j, jnp.maximum(valid - 1, 0)), 0)
+
+    grid_spec = pltpu.PrefetchScalarGridSpec(
+        num_scalar_prefetch=1,
+        grid=(steps,),
+        in_specs=[
+            pl.BlockSpec((tokens, width), lambda j, l: (0, 0)),
+            pl.BlockSpec((block, width), cache_map),
+            pl.BlockSpec((block, width), cache_map),
+            pl.BlockSpec((tokens, width), lambda j, l: (0, 0)),
+            pl.BlockSpec((tokens, width), lambda j, l: (0, 0)),
+        ],
+        out_specs=pl.BlockSpec((tokens, width), lambda j, l: (0, 0)),
+        scratch_shapes=[
+            pltpu.VMEM((heads, tokens, 1), jnp.float32),
+            pltpu.VMEM((heads, tokens, 1), jnp.float32),
+            pltpu.VMEM((tokens, width), jnp.float32),
+        ],
+    )
+    kernel = functools.partial(flash_kernel, block=block, heads=heads, steps=steps)
+    return pl.pallas_call(
+        kernel,
+        grid_spec=grid_spec,
+        out_shape=jax.ShapeDtypeStruct((tokens, width), jnp.bfloat16),
+        compiler_params=pltpu.CompilerParams(dimension_semantics=("arbitrary",)),
+    )(length.reshape(1), queries, cache_k, cache_v, new_k, new_v)
 
 
 def dense_experts(moe_in, expert_ids, route_weights, expert_gate_up, down_full, here, experts_all):
@@ -158,39 +208,16 @@
     local_width = new_queries.shape[1]
     local_heads = local_width // HEAD_DIM
     quarter = hidden.shape[1]
-    own_queries = new_queries.reshape(1, NEW, local_heads, HEAD_DIM)
-    own_keys = new_keys.reshape(1, NEW, local_heads, HEAD_DIM)
-    own_values = new_values.reshape(1, NEW, local_heads, HEAD_DIM)
-    offsets = jnp.arange(NEW, dtype=jnp.int32)
-    causal = (offsets[None, :] <= offsets[:, None])[None]
-    own_out, own_max, own_total = softmax_parts(own_queries, own_keys, own_values, causal)
     span = cache_keys.shape[1]
-    block = min(512, span)
     my_length = lax.dynamic_index_in_dim(cache_lengths, here, 0, keepdims=False)
-    block_count = (my_length + block - 1) // block
-    key_blocks = cache_keys.reshape(span, local_heads, HEAD_DIM)
-    value_blocks = cache_values.reshape(span, local_heads, HEAD_DIM)
-
-    def cache_block(index, carry):
-        begin = index * block
-        keys_here = lax.dynamic_slice_in_dim(key_blocks, begin, block, 0)[None]
-        values_here = lax.dynamic_slice_in_dim(value_blocks, begin, block, 0)[None]
-        positions = begin + jnp.arange(block, dtype=jnp.int32)
-        allowed = jnp.broadcast_to((positions < my_length)[None, None, :], (1, NEW, block))
-        return combine_parts(carry, softmax_parts(own_queries, keys_here, values_here, allowed))
-
-    start_parts = (
-        jnp.zeros((1, NEW, local_heads, HEAD_DIM), jnp.float32),
-        jnp.full((1, NEW, local_heads), -1e30, jnp.float32),
-        jnp.zeros((1, NEW, local_heads), jnp.float32),
-    )
-    pieces, maxima, totals = lax.fori_loop(0, block_count, cache_block, start_parts)
-    attended = merge_parts(
-        jnp.concatenate([own_out, pieces], 0),
-        jnp.concatenate([own_max, maxima], 0),
-        jnp.concatenate([own_total, totals], 0),
-    )
-    attended = attended.reshape(NEW, local_width).astype(jnp.bfloat16)
+    attended = flash_attention(
+        my_length,
+        new_queries,
+        cache_keys.reshape(span, local_width),
+        cache_values.reshape(span, local_width),
+        new_keys,
+        new_values,
+    )
     if dense:
         attended, down_full = lax.optimization_barrier((attended, down_full))
     attn_term = jnp.dot(attended, out_proj, preferred_element_type=jnp.float32)

time: 414 us -> 413 us (level)
  local copies, waits for them, and re-layouts: 38.4 us -> 25.3 us
  Pallas kernels: 0 us -> 11.6 us
  waiting for transfers between devices: 300 us -> 310 us
  matrix products: 33.6 us -> 29.1 us
    unnamed x35 -> x26, local copies, waits for them, and re-layouts: 23.3 us -> 10.1 us
    pallas_call x0 -> x1, Pallas kernels: none -> 11.6 us  [flash_attention(): pl.pallas_call(kernel, grid_spec=grid_spec, out_shape=jax.ShapeDtypeStruc...]
    all_gather x1, waiting for transfers between devices: 40.1 us -> 49.8 us  [body(): down_full = lax.all_gather(expert_down, 'tp', axis=1, tiled=True)]
    dot_general x4 -> x0, matrix products: 5.22 us -> none  [the longest x2 2.98 us: softmax_parts(): jnp.einsum('bthe,bche->bhtc', queries, key_rows, preferred_element_type=j...]
  transfers between devices with their start and end apart: 7 -> 7, of which waited for: 7 -> 7; matrix products, arithmetic and copies ran while one was open for 10% -> 5% of each run, Pallas kernels for 0% -> 3%
where the time goes in v5:
time: 413 us
  waiting for transfers between devices  310 us (75%)
  matrix products  29.1 us (7%)
  local copies, waits for them, and re-layouts  25.3 us (6%)
  between operations  14.3 us (3%)
  blocking collectives  11.7 us (3%)
  Pallas kernels  11.6 us (3%)
  other arithmetic  10.6 us (3%)
    reduce_scatter x1, waiting for transfers between devices, dense_experts(): partial = lax.psum_scatter(partial, 'seq', scatter_dimension=0, tiled=True)  67.9 us
    all_gather x1, waiting for transfers between devices, dense_experts(): weighted = lax.all_gather(weighted, 'tp', axis=2, tiled=True)  59.3 us
    all_gather x1, waiting for transfers between devices, dense_experts(): gathered = lax.all_gather(packed, 'seq', axis=0, tiled=False)  51.9 us
    all_gather x1, waiting for transfers between devices, body(): down_full = lax.all_gather(expert_down, 'tp', axis=1, tiled=True)  49.8 us
    all_gather x1, waiting for transfers between devices, dense_experts(): rows = lax.all_gather(rows_q, 'tp', axis=1, tiled=True)  48 us
    reduce_scatter x1, waiting for transfers between devices, body(): lax.psum_scatter(attn_term.astype(jnp.bfloat16), 'tp', scatter_dimension=...  24.9 us
    dot_general x1, matrix products, dense_experts(): jnp.einsum('td,edf->etf', rows, gate_up, preferred_element_type=jnp.float32)  12.4 us
    pallas_call x1, Pallas kernels, flash_attention(): pl.pallas_call(kernel, grid_spec=grid_spec, out_shape=jax.ShapeDtypeStruc...  11.6 us
  transfers between devices with their start and end apart: 7, of which 7 were waited for; matrix products, arithmetic and copies ran while one was open for 5% of the time, Pallas kernels for 3%

profile of v5, /device:TPU:0, one launch (start us, length us, event | category | flops | bytes accessed | tf_op | source)
XLA Modules:
  0.0 412.7 jit_solution(12560529255269238337)
XLA Ops:
  7.2 0.0 copy-start
  7.2 0.0 all-gather.7.cloned.1.call-start
  7.2 0.7 all-gather.7.cloned.1.call-update
  7.9 0.0 reduce-scatter.3.cloned.1.call-start
  8.0 1.2 dynamic_slice.12.len_ref
  9.2 11.6 %shard_map.192 = bf16[256,512]{1,0:T(8,128)(2,1)} custom-call(s32[1]{0:T(128)} %dynamic_slice.12.len_ref, bf16[256,512]{1,0:T(8,128)(2,1)} %q_ref.1, bf16[4096,512]{1,0:T(8,128)(2,1)} %bitcast.60, bf16[4096,512]{1,0:T(8,128)(2,1)} %bitcast.61, bf16[256,512]{1,0:T(8,128)(2,1)} %nk_ref.1, bf16[256,512]{1,0:T(8,128)(2,1)} %nv_ref.1), custom_call_target="tpu_custom_call" | custom-call | tf_op jit(solution)/shard_map/pallas_call | solution.py:94
  20.8 0.0 copy-start.3
  20.8 0.0 copy-start.8
  20.8 49.8 %all-gather.7.cloned.1.call-done = bf16[2,1024,2048]{2,1,0:T(8,128)(2,1)} async-done(((bf16[2,256,2048]{2,1,0:T(8,128)(2,1)}), bf16[2,1024,2048]{2,1,0:T(8,128)(2,1)}) %all-gather.7.cloned.1.call-update) | async-done | bytes 8388624 | tf_op jit(solution)/shard_map/all_gather | solution.py:206
  70.6 3.0 constant_dynamic-slice_fusion
  73.7 1.7 convolution_convert_fusion
  75.3 0.0 reduce-scatter.3.cloned.1.call-update
  75.4 0.0 all-gather.15.cloned.1.call-start
  75.4 0.0 copy-done.6
  75.4 0.0 copy-done.7
  75.5 24.9 %reduce-scatter.3.cloned.1.call-done = bf16[256,512]{1,0:T(8,128)(2,1)} async-done(((bf16[256,2048]{1,0:T(8,128)(2,1)}), bf16[256,512]{1,0:T(8,128)(2,1)}) %reduce-scatter.3.cloned.1.call-update) | async-done | bytes 262160 | tf_op jit(solution)/shard_map/reduce_scatter | solution.py:224
  100.4 1.1 multiply_reduce_fusion.3
  101.5 5.8 %psum.28 = f32[256]{0:T(256)S(1)} all-reduce(f32[256]{0:T(256)S(1)} %multiply_reduce_fusion.3), channel_id=1, replica_groups=mesh['seq'=8,'tp'=4] {'tp'}, use_global_device_ids=true, to_apply=%region_2.3 | all-reduce | flops 256 | bytes 2048 | tf_op jit(solution)/shard_map/psum | solution.py:227
  107.3 1.1 multiply_convert_fusion.4
  108.4 0.7 pad_maximum_fusion
  109.1 0.0 all-gather.15.cloned.1.call-update
  109.1 0.0 all-gather.9.cloned.1.call-start
  109.2 51.9 %all-gather.15.cloned.1.call-done = bf16[2176,512]{1,0:T(8,128)(2,1)} async-done(((bf16[272,512]{1,0:T(8,128)(2,1)}), bf16[2176,512]{1,0:T(8,128)(2,1)}) %all-gather.15.cloned.1.call-update) | async-done | bytes 2228240 | tf_op jit(solution)/shard_map/all_gather | solution.py:117
  161.0 3.1 slice.40
  164.1 0.0 all-gather.9.cloned.1.call-update
  164.1 0.0 all-gather.11.cloned.1.call-start
  164.2 7.8 %reshape.49 = bf16[2,2048,512]{2,1,0:T(8,128)(2,1)} reshape(bf16[2,2048,2,256]{3,2,1,0:T(2,128)(2,1)} %param.28) | data formatting | bytes 8388608 | tf_op jit(solution)/shard_map/reshape | solution.py:124
  172.0 1.0 slice_convert_fusion
  173.1 48.0 %all-gather.9.cloned.1.call-done = bf16[2048,2048]{1,0:T(8,128)(2,1)} async-done(((bf16[2048,512]{1,0:T(8,128)(2,1)}), bf16[2048,2048]{1,0:T(8,128)(2,1)}) %all-gather.9.cloned.1.call-update) | async-done | bytes 8388624 | tf_op jit(solution)/shard_map/all_gather | solution.py:123
  221.1 12.4 %fusion.4 = f32[2,2048,512]{2,1,0:T(8,128)S(1)} fusion(bf16[2,2048,512]{2,1,0:T(8,128)(2,1)} %reshape.49, bf16[2048,2048]{1,0:T(8,128)(2,1)} %all-gather.9.cloned.1.call-done), kind=kOutput, calls=%fused_computation.4 | convolution fusion | flops 8589934592 | bytes 20971520 | tf_op jit(solution)/shard_map/td,edf->etf/dot_general | solution.py:125
  233.5 2.2 multiply_convert_fusion
  235.7 0.0 all-gather.11.cloned.1.call-update
  235.8 0.0 copy-start.9
  235.8 0.2 reduce-scatter.5.cloned.1.call-start
  236.0 59.3 %all-gather.11.cloned.1.call-done = bf16[2,2048,1024]{2,1,0:T(8,128)(2,1)} async-done(((bf16[2,2048,256]{2,1,0:T(8,128)(2,1)}), bf16[2,2048,1024]{2,1,0:T(8,128)(2,1)}) %all-gather.11.cloned.1.call-update) | async-done | bytes 8388624 | tf_op jit(solution)/shard_map/all_gather | solution.py:129
  295.3 9.9 %bitcast_convert_fusion = bf16[2048,512]{1,0:T(8,128)(2,1)} fusion(bf16[2,2048,1024]{2,1,0:T(8,128)(2,1)} %all-gather.11.cloned.1.call-done, bf16[2,1024,512]{2,1,0:T(8,128)(2,1)} %constant_dynamic-slice_fusion), kind=kOutput, calls=%fused_computation.7 | convolution fusion | flops 4296015872 | bytes 12582912 | tf_op jit(solution)/shard_map/etf,efd->td/dot_general | solution.py:130
  305.2 0.0 reduce-scatter.5.cloned.1.call-update
  305.2 0.0 all-gather.13.cloned.1.call-start
  305.2 67.9 %reduce-scatter.5.cloned.1.call-done = bf16[256,512]{1,0:T(8,128)(2,1)} async-done(((bf16[2048,512]{1,0:T(8,128)(2,1)}), bf16[256,512]{1,0:T(8,128)(2,1)}) %reduce-scatter.5.cloned.1.call-update) | async-done | bytes 262160 | tf_op jit(solution)/shard_map/reduce_scatter | solution.py:133
  373.2 1.9 multiply_reduce_fusion.2
  375.1 0.0 all-gather.13.cloned.1.call-update
  375.1 8.9 %copy.31 = bf16[2048,3,512]{0,2,1:T(8,128)(2,1)} copy(bf16[2048,3,512]{2,0,1:T(8,128)(2,1)} %param.31) | data formatting | bytes 12582912 | tf_op args[14]
  383.9 7.2 %all-gather.13.cloned.1.call-done = bf16[256,2048]{1,0:T(8,128)(2,1)} async-done(((bf16[256,512]{1,0:T(8,128)(2,1)}), bf16[256,2048]{1,0:T(8,128)(2,1)}) %all-gather.13.cloned.1.call-update) | async-done | bytes 1048592 | tf_op jit(solution)/shard_map/all_gather | solution.py:245
  391.1 5.1 %fusion.2 = f32[256,3,512]{2,0,1:T(8,128)S(1)} fusion(bf16[2048,3,512]{0,2,1:T(8,128)(2,1)} %copy.31, bf16[256,2048]{1,0:T(8,128)(2,1)} %all-gather.13.cloned.1.call-done), kind=kOutput, calls=%fused_computation.2 | convolution fusion | flops 1610612736 | bytes 8912896 | tf_op jit(solution)/shard_map/dot_general | solution.py:244
  396.2 1.2 copy-done.2
  397.4 0.1 multiply_reduce_fusion
  397.5 5.9 %all-reduce = (f32[256]{0:T(256)S(1)}, f32[256]{0:T(256)S(1)}, f32[256]{0:T(256)S(1)}) all-reduce(f32[256]{0:T(256)S(1)} %get-tuple-element.9, f32[256]{0:T(256)S(1)} %get-tuple-element.18, f32[256]{0:T(256)S(1)} %get-tuple-element.8), channel_id=1, replica_groups=mesh['seq'=8,'tp'=4] {'tp'}, use_global_device_ids=true, to_apply=%region_8.9 | all-reduce | flops 768 | bytes 6144 | tf_op jit(solution)/shard_map/psum | solution.py:251
  403.4 2.4 fusion.10
  (28 shorter events, 0.2 us)
Async XLA Ops:
  7.2 66.5 %copy-start = (bf16[512,2048]{1,0:T(8,128)(2,1)S(1)}, bf16[512,2048]{1,0:T(8,128)(2,1)}, u32[]{:S(2)}) copy-start(bf16[512,2048]{1,0:T(8,128)(2,1)} %param.24) | copy-start | bytes 6291460
  7.2 63.4 %all-gather.7.cloned.1.call-start = ((), (), s32[]{:S(2)}) async-start(), calls=%async_computation.2 | async-start | bytes 10485760 | tf_op jit(solution)/shard_map/all_gather | solution.py:206
  7.9 92.5 %reduce-scatter.3.cloned.1.call-start = ((), (), s32[]{:S(2)}) async-start(), calls=%async_computation.3 | async-start | bytes 1310720 | tf_op jit(solution)/shard_map/reduce_scatter | solution.py:224
  20.8 52.9 %copy-start.5 = (bf16[256,512]{1,0:T(8,128)(2,1)S(1)}, bf16[256,512]{1,0:T(8,128)(2,1)}, u32[]{:S(2)}) copy-start(bf16[256,512]{1,0:T(8,128)(2,1)} %shard_map.192) | copy-start | bytes 786436
  20.8 54.6 %copy-start.6 = (f32[256,8]{0,1:T(8,128)S(1)}, f32[256,8]{0,1:T(8,128)}, u32[]{:S(2)}) copy-start(f32[256,8]{0,1:T(8,128)} %param.27) | copy-start | bytes 24580
  20.8 54.6 %copy-start.7 = (s32[256,8]{0,1:T(8,128)S(1)}, s32[256,8]{0,1:T(8,128)}, u32[]{:S(2)}) copy-start(s32[256,8]{0,1:T(8,128)} %param.26) | copy-start | bytes 24580
  20.8 79.6 %copy-start.3 = (bf16[256,512]{1,0:T(8,128)(2,1)S(1)}, bf16[256,512]{1,0:T(8,128)(2,1)}, u32[]{:S(2)}) copy-start(bf16[256,512]{1,0:T(8,128)(2,1)} %param.17) | copy-start | bytes 786436
  20.8 86.5 %copy-start.8 = (f32[512]{0:T(512)S(1)}, f32[512]{0:T(512)}, u32[]{:S(2)}) copy-start(f32[512]{0:T(512)} %param.25) | copy-start | bytes 6148
  75.4 85.7 %all-gather.15.cloned.1.call-start = ((), (), s32[]{:S(2)}) async-start(), calls=%async_computation.8 | async-start | bytes 2506752 | tf_op jit(solution)/shard_map/all_gather | solution.py:117
  109.1 112.0 %all-gather.9.cloned.1.call-start = ((), (), s32[]{:S(2)}) async-start(), calls=%async_computation.4 | async-start | bytes 10485760 | tf_op jit(solution)/shard_map/all_gather | solution.py:123
  164.1 131.2 %all-gather.11.cloned.1.call-start = ((), (), s32[]{:S(2)}) async-start(), calls=%async_computation.5 | async-start | bytes 10485760 | tf_op jit(solution)/shard_map/all_gather | solution.py:129
  235.7 137.4 %copy-start.4 = (bf16[256,512]{1,0:T(8,128)(2,1)S(1)}, bf16[256,512]{1,0:T(8,128)(2,1)}, u32[]{:S(2)}) copy-start(bf16[256,512]{1,0:T(8,128)(2,1)} %reduce-scatter.3.cloned.1.call-done) | copy-start | bytes 786436
  235.8 137.4 %copy-start.9 = (f32[512]{0:T(512)S(1)}, f32[512]{0:T(512)}, u32[]{:S(2)}) copy-start(f32[512]{0:T(512)} %param.30) | copy-start | bytes 6148
  235.8 137.4 %reduce-scatter.5.cloned.1.call-start = ((), (), s32[]{:S(2)}) async-start(), calls=%async_computation.6 | async-start | bytes 2359296 | tf_op jit(solution)/shard_map/reduce_scatter | solution.py:133
  305.2 85.9 %all-gather.13.cloned.1.call-start = ((), (), s32[]{:S(2)}) async-start(), calls=%async_computation.7 | async-start | bytes 1310720 | tf_op jit(solution)/shard_map/all_gather | solution.py:245
  383.9 19.5 %copy-start.10 = (f32[512]{0:T(512)S(1)}, f32[512]{0:T(512)}, u32[]{:S(2)}) copy-start(f32[512]{0:T(512)} %param.33) | copy-start | bytes 6148
  383.9 19.5 %copy-start.11 = (f32[512]{0:T(512)S(1)}, f32[512]{0:T(512)}, u32[]{:S(2)}) copy-start(f32[512]{0:T(512)} %param.32) | copy-start | bytes 6148
  391.1 14.7 %copy-start.1 = (bf16[512,2048]{1,0:T(8,128)(2,1)S(1)}, bf16[512,2048]{1,0:T(8,128)(2,1)}, u32[]{:S(2)}) copy-start(bf16[512,2048]{1,0:T(8,128)(2,1)} %param.24) | copy-start | bytes 6291460
  396.2 1.2 copy-start.2
Sparse Core Ops, SparseCore 0:
  9.6 60.9 all-gather.6
  75.5 24.8 reduce-scatter.2
  109.2 51.7 all-gather.14
  164.2 56.7 all-gather.8
  235.9 59.3 all-gather.10
  305.3 67.8 reduce-scatter.4
  375.4 15.6 all-gather.12

commit v6 on v5

--- a/solution.py
+++ b/solution.py
@@ -101,7 +101,7 @@
 
 def dense_experts(moe_in, expert_ids, route_weights, expert_gate_up, down_full, here, experts_all):
     local_experts = expert_gate_up.shape[0]
-    hidden_quarter = expert_gate_up.shape[3]
+    hidden_quarter = expert_gate_up.shape[2] // 2
     tokens, quarter = moe_in.shape
     seq_count = experts_all // local_experts
     gate_w = jnp.sum(
@@ -121,8 +121,7 @@
     gate_local = lax.dynamic_slice_in_dim(gate_all, here * local_experts, local_experts, axis=1)
     gate_local = jnp.transpose(gate_local, (1, 0, 2)).reshape(local_experts, seq_count * tokens)
     rows = lax.all_gather(rows_q, "tp", axis=1, tiled=True)
-    gate_up = expert_gate_up.reshape(local_experts, D, 2 * hidden_quarter)
-    projected = jnp.einsum("td,edf->etf", rows, gate_up, preferred_element_type=jnp.float32)
+    projected = jnp.einsum("td,edf->etf", rows, expert_gate_up, preferred_element_type=jnp.float32)
     activated = jax.nn.silu(projected[..., :hidden_quarter]) * projected[..., hidden_quarter:]
     activated = activated.astype(jnp.bfloat16).astype(jnp.float32)
     weighted = (activated * gate_local[:, :, None]).astype(jnp.bfloat16)
@@ -203,8 +202,18 @@
     if dense:
         tp_here = lax.axis_index("tp")
         quarter_width = hidden.shape[1]
-        down_full = lax.all_gather(expert_down, "tp", axis=1, tiled=True)
-        down_full = lax.dynamic_slice_in_dim(down_full, tp_here * quarter_width, quarter_width, axis=2)
+        tp_count = lax.axis_size("tp")
+        pieces = [lax.dynamic_slice_in_dim(expert_down, tp_here * quarter_width, quarter_width, axis=2)]
+        for shift in range(1, tp_count):
+            target = (tp_here + shift) % tp_count
+            piece = lax.dynamic_slice_in_dim(expert_down, target * quarter_width, quarter_width, axis=2)
+            pairs = [(i, (i + shift) % tp_count) for i in range(tp_count)]
+            pieces.append(lax.ppermute(piece, "tp", pairs))
+        order = (tp_here - jnp.arange(tp_count, dtype=jnp.int32)) % tp_count
+        down_full = jnp.take(jnp.stack(pieces), order, axis=0)
+        down_full = jnp.transpose(down_full, (1, 0, 2, 3)).reshape(local_experts, -1, quarter_width)
+        gate_up_flat = expert_gate_up.reshape(local_experts, D, -1)
+        qkv_flat = qkv_proj.reshape(D, -1)
     local_width = new_queries.shape[1]
     local_heads = local_width // HEAD_DIM
     quarter = hidden.shape[1]
@@ -219,7 +228,12 @@
         new_values,
     )
     if dense:
-        attended, down_full = lax.optimization_barrier((attended, down_full))
+        attended, down_full, gate_up_flat, qkv_flat = lax.optimization_barrier(
+            (attended, down_full, gate_up_flat, qkv_flat)
+        )
+    else:
+        gate_up_flat = expert_gate_up
+        qkv_flat = qkv_proj.reshape(D, -1)
     attn_term = jnp.dot(attended, out_proj, preferred_element_type=jnp.float32)
     residual = hidden.astype(jnp.float32) + lax.psum_scatter(
         attn_term.astype(jnp.bfloat16), "tp", scatter_dimension=1, tiled=True
@@ -230,7 +244,7 @@
     )
     if dense:
         moe_term = dense_experts(
-            moe_in, expert_ids, route_weights, expert_gate_up, down_full, here, experts_all
+            moe_in, expert_ids, route_weights, gate_up_flat, down_full, here, experts_all
         )
     else:
         moe_term = dispatch_experts(
@@ -239,8 +253,7 @@
     routed = residual + moe_term
     layer_out = routed.astype(jnp.bfloat16)
     scaled = (routed * next_gain[None, :]).astype(jnp.bfloat16)
-    qkv_local = qkv_proj.reshape(D, 3 * local_width)
-    weight_rows = qkv_local
+    weight_rows = qkv_flat
     mixed = jnp.dot(
         lax.all_gather(scaled, "tp", axis=1, tiled=True),
         weight_rows,

time: 413 us -> 399 us (0.966)
  waiting for transfers between devices: 310 us -> 277 us
  local copies, waits for them, and re-layouts: 25.3 us -> 32 us
  starting transfers between devices: 0.47 us -> 5.14 us
  other arithmetic: 10.6 us -> 14.9 us
    all_gather x1 -> x0, waiting for transfers between devices: 49.8 us -> none  [body(): down_full = lax.all_gather(expert_down, 'tp', axis=1, tiled=True)]
    all_gather x1, waiting for transfers between devices: 7.17 us -> 15.9 us  [body(): lax.all_gather(scaled, 'tp', axis=1, tiled=True)]
    all_gather x1, waiting for transfers between devices: 48 us -> 55.7 us  [dense_experts(): rows = lax.all_gather(rows_q, 'tp', axis=1, tiled=True)]
    ppermute x0 -> x3, starting transfers between devices: none -> 4.71 us  [body(): pieces.append(lax.ppermute(piece, 'tp', pairs))]
    unnamed x26 -> x33, local copies, waits for them, and re-layouts: 10.1 us -> 12.6 us
  transfers between devices with their start and end apart: 7 -> 9, of which waited for: 7 -> 6; matrix products, arithmetic and copies ran while one was open for 5% -> 5% of each run, Pallas kernels for 3% -> 4%
where the time goes in v6:
time: 399 us; the launch traced here: 398 us
  waiting for transfers between devices  277 us (69%)
  local copies, waits for them, and re-layouts  32 us (8%)
  matrix products  28.7 us (7%)
  other arithmetic  14.9 us (4%)
  between operations  14.4 us (4%)
  Pallas kernels  14.2 us (4%)
  blocking collectives  11.8 us (3%)
  starting transfers between devices  5.14 us (1%)
    reduce_scatter x1, waiting for transfers between devices, dense_experts(): partial = lax.psum_scatter(partial, 'seq', scatter_dimension=0, tiled=True)  68 us
    all_gather x1, waiting for transfers between devices, dense_experts(): weighted = lax.all_gather(weighted, 'tp', axis=2, tiled=True)  58.4 us
    all_gather x1, waiting for transfers between devices, dense_experts(): rows = lax.all_gather(rows_q, 'tp', axis=1, tiled=True)  55.7 us
    all_gather x1, waiting for transfers between devices, dense_experts(): gathered = lax.all_gather(packed, 'seq', axis=0, tiled=False)  51.9 us
    reduce_scatter x1, waiting for transfers between devices, body(): lax.psum_scatter(attn_term.astype(jnp.bfloat16), 'tp', scatter_dimension=...  26.9 us
    all_gather x1, waiting for transfers between devices, body(): lax.all_gather(scaled, 'tp', axis=1, tiled=True)  15.9 us
    pallas_call x1, Pallas kernels, flash_attention(): pl.pallas_call(kernel, grid_spec=grid_spec, out_shape=jax.ShapeDtypeStruc...  14.2 us
    unnamed x33, local copies, waits for them, and re-layouts  12.6 us
  transfers between devices with their start and end apart: 9, of which 6 were waited for; matrix products, arithmetic and copies ran while one was open for 5% of the time, Pallas kernels for 4%

profile of v6, /device:TPU:0, one launch (start us, length us, event | category | flops | bytes accessed | tf_op | source)
XLA Modules:
  0.0 397.9 jit_solution(11459714358495147510)
XLA Ops:
  7.2 0.0 reduce-scatter.3.cloned.1.call-start
  7.3 2.8 dynamic-slice_bitcast_fusion
  10.1 0.5 collective-permute-start
  10.6 2.0 collective-permute-start.2
  12.5 2.3 collective-permute-start.1
  14.8 7.6 %reshape.106 = bf16[2,2048,512]{2,1,0:T(8,128)(2,1)} reshape(bf16[2,2048,2,256]{3,2,1,0:T(2,128)(2,1)} %param.28) | data formatting | bytes 8388608 | tf_op jit(solution)/shard_map/reshape | solution.py:215
  22.4 8.9 %copy.49 = bf16[2048,3,512]{0,2,1:T(8,128)(2,1)} copy(bf16[2048,3,512]{2,0,1:T(8,128)(2,1)} %param.31) | data formatting | bytes 12582912 | tf_op args[14]
  31.3 0.6 dynamic_slice.21.len_ref
  31.9 14.2 %shard_map.192 = bf16[256,512]{1,0:T(8,128)(2,1)} custom-call(s32[1]{0:T(128)} %dynamic_slice.21.len_ref, bf16[256,512]{1,0:T(8,128)(2,1)} %q_ref.1, bf16[4096,512]{1,0:T(8,128)(2,1)} %bitcast.67, bf16[4096,512]{1,0:T(8,128)(2,1)} %bitcast.68, bf16[256,512]{1,0:T(8,128)(2,1)} %nk_ref.1, bf16[256,512]{1,0:T(8,128)(2,1)} %nv_ref.1), custom_call_target="tpu_custom_call" | custom-call | tf_op jit(solution)/shard_map/pallas_call | solution.py:94
  46.1 3.0 pad_maximum_fusion
  49.1 3.6 gather_fusion
  52.7 1.9 select_bitcast_fusion
  54.5 1.6 copy.48
  56.1 1.7 convolution_convert_fusion
  57.8 0.0 reduce-scatter.3.cloned.1.call-update
  57.9 0.0 all-gather.12.cloned.1.call-start
  58.0 26.9 %reduce-scatter.3.cloned.1.call-done = bf16[256,512]{1,0:T(8,128)(2,1)} async-done(((bf16[256,2048]{1,0:T(8,128)(2,1)}), bf16[256,512]{1,0:T(8,128)(2,1)}) %reduce-scatter.3.cloned.1.call-update) | async-done | bytes 262160 | tf_op jit(solution)/shard_map/reduce_scatter | solution.py:238
  84.9 1.1 multiply_reduce_fusion.3
  86.0 5.8 %psum.28 = f32[256]{0:T(256)S(1)} all-reduce(f32[256]{0:T(256)S(1)} %multiply_reduce_fusion.3), channel_id=1, replica_groups=mesh['seq'=8,'tp'=4] {'tp'}, use_global_device_ids=true, to_apply=%region_2.3 | all-reduce | flops 256 | bytes 2048 | tf_op jit(solution)/shard_map/psum | solution.py:241
  91.8 1.1 multiply_convert_fusion.4
  92.8 0.7 pad_maximum_fusion.1
  93.5 0.0 all-gather.12.cloned.1.call-update
  93.6 0.0 all-gather.6.cloned.1.call-start
  93.6 51.9 %all-gather.12.cloned.1.call-done = bf16[2176,512]{1,0:T(8,128)(2,1)} async-done(((bf16[272,512]{1,0:T(8,128)(2,1)}), bf16[2176,512]{1,0:T(8,128)(2,1)}) %all-gather.12.cloned.1.call-update) | async-done | bytes 2228240 | tf_op jit(solution)/shard_map/all_gather | solution.py:117
  145.5 3.1 slice.42
  148.6 0.0 all-gather.6.cloned.1.call-update
  148.6 0.2 all-gather.8.cloned.1.call-start
  148.8 0.9 slice_convert_fusion
  149.9 55.7 %all-gather.6.cloned.1.call-done = bf16[2048,2048]{1,0:T(8,128)(2,1)} async-done(((bf16[2048,512]{1,0:T(8,128)(2,1)}), bf16[2048,2048]{1,0:T(8,128)(2,1)}) %all-gather.6.cloned.1.call-update) | async-done | bytes 8388624 | tf_op jit(solution)/shard_map/all_gather | solution.py:123
  205.6 12.6 %fusion.2 = f32[2,2048,512]{1,2,0:T(8,128)S(1)} fusion(bf16[2,2048,512]{2,1,0:T(8,128)(2,1)} %reshape.106, bf16[2048,2048]{1,0:T(8,128)(2,1)} %all-gather.6.cloned.1.call-done), kind=kOutput, calls=%fused_computation.3 | convolution fusion | flops 8589934592 | bytes 20971520 | tf_op jit(solution)/shard_map/td,edf->etf/dot_general | solution.py:124
  218.2 2.6 multiply_convert_fusion
  220.8 0.0 all-gather.8.cloned.1.call-update
  220.8 0.0 reduce-scatter.5.cloned.1.call-start
  220.9 58.4 %all-gather.8.cloned.1.call-done = bf16[2,2048,1024]{1,2,0:T(8,128)(2,1)} async-done(((bf16[2,2048,256]{1,2,0:T(8,128)(2,1)}), bf16[2,2048,1024]{1,2,0:T(8,128)(2,1)}) %all-gather.8.cloned.1.call-update) | async-done | bytes 8388624 | tf_op jit(solution)/shard_map/all_gather | solution.py:128
  279.2 9.5 %bitcast_convert_fusion = bf16[2048,512]{1,0:T(8,128)(2,1)} fusion(bf16[2,2048,1024]{1,2,0:T(8,128)(2,1)} %all-gather.8.cloned.1.call-done, bf16[2,1024,512]{2,1,0:T(8,128)(2,1)S(1)} %bitcast.71), kind=kOutput, calls=%fused_computation.6 | convolution fusion | flops 4296015872 | bytes 12582912 | tf_op jit(solution)/shard_map/etf,efd->td/dot_general | solution.py:129
  288.7 0.0 all-gather.10.cloned.1.call-start
  288.8 68.0 %reduce-scatter.5.cloned.1.call-done = bf16[256,512]{1,0:T(8,128)(2,1)} async-done(((bf16[2048,512]{1,0:T(8,128)(2,1)}), bf16[256,512]{1,0:T(8,128)(2,1)}) %reduce-scatter.5.cloned.1.call-update) | async-done | bytes 262160 | tf_op jit(solution)/shard_map/reduce_scatter | solution.py:132
  356.7 1.9 multiply_reduce_fusion.2
  358.6 0.0 all-gather.10.cloned.1.call-update
  358.7 15.9 %all-gather.10.cloned.1.call-done = bf16[256,2048]{1,0:T(8,128)(2,1)} async-done(((bf16[256,512]{1,0:T(8,128)(2,1)}), bf16[256,2048]{1,0:T(8,128)(2,1)}) %all-gather.10.cloned.1.call-update) | async-done | bytes 1048592 | tf_op jit(solution)/shard_map/all_gather | solution.py:258
  374.5 5.0 %fusion.20 = f32[256,1536]{0,1:T(8,128)S(1)} fusion(bf16[256,2048]{1,0:T(8,128)(2,1)} %all-gather.10.cloned.1.call-done, bf16[2048,1536]{0,1:T(8,128)(2,1)} %bitcast.64), kind=kOutput, calls=%fused_computation.65 | convolution fusion | flops 1610612736 | bytes 8912896 | tf_op jit(solution)/shard_map/dot_general | solution.py:257
  379.6 1.2 copy-done.2
  380.7 0.1 multiply_reduce_fusion
  380.8 6.0 %all-reduce = (f32[256]{0:T(256)S(1)}, f32[256]{0:T(256)S(1)}, f32[256]{0:T(256)S(1)}) all-reduce(f32[256]{0:T(256)S(1)} %get-tuple-element.25, f32[256]{0:T(256)S(1)} %get-tuple-element.38, f32[256]{0:T(256)S(1)} %get-tuple-element.24), channel_id=1, replica_groups=mesh['seq'=8,'tp'=4] {'tp'}, use_global_device_ids=true, to_apply=%region_8.9 | all-reduce | flops 768 | bytes 6144 | tf_op jit(solution)/shard_map/psum | solution.py:264
  386.9 1.6 fusion.7
  388.5 0.8 copy.56
  389.3 0.8 copy.55
  390.2 0.8 copy.54
  (45 shorter events, 0.3 us)
Async XLA Ops:
  7.2 48.9 %copy-start = (bf16[512,2048]{1,0:T(8,128)(2,1)S(1)}, bf16[512,2048]{1,0:T(8,128)(2,1)}, u32[]{:S(2)}) copy-start(bf16[512,2048]{1,0:T(8,128)(2,1)} %param.24) | copy-start | bytes 6291460
  7.2 77.7 %reduce-scatter.3.cloned.1.call-start = ((), (), s32[]{:S(2)}) async-start(), calls=%async_computation.2 | async-start | bytes 1310720 | tf_op jit(solution)/shard_map/reduce_scatter | solution.py:238
  10.1 36.0 %collective-permute-start = (bf16[2,256,512]{2,1,0:T(8,128)(2,1)}, bf16[2,256,512]{2,1,0:T(8,128)(2,1)}, u32[]{:S(2)}, u32[]{:S(2)}) collective-permute-start(bf16[2,256,512]{2,1,0:T(8,128)(2,1)} %get-tuple-element.32), channel_id=1, source_target_pairs={{0,1},{1,2},{2,3},{3,0},{4,5},{5,6},{6,7},{7,4},{8,9},{9,10},{10,1... | collective-permute-start | bytes 1572872 | tf_op jit(solution)/shard_map/ppermute | solution.py:211
  10.6 35.5 %collective-permute-start.2 = (bf16[2,256,512]{2,1,0:T(8,128)(2,1)}, bf16[2,256,512]{2,1,0:T(8,128)(2,1)}, u32[]{:S(2)}, u32[]{:S(2)}) collective-permute-start(bf16[2,256,512]{2,1,0:T(8,128)(2,1)} %get-tuple-element.33), channel_id=1, source_target_pairs={{0,3},{1,0},{2,1},{3,2},{4,7},{5,4},{6,5},{7,6},{8,11},{9,8},{10,9... | collective-permute-start | bytes 1572872 | tf_op jit(solution)/shard_map/ppermute | solution.py:211
  12.5 33.6 %collective-permute-start.1 = (bf16[2,256,512]{2,1,0:T(8,128)(2,1)S(1)}, bf16[2,256,512]{2,1,0:T(8,128)(2,1)}, u32[]{:S(2)}, u32[]{:S(2)}) collective-permute-start(bf16[2,256,512]{2,1,0:T(8,128)(2,1)S(1)} %get-tuple-element.34), channel_id=1, source_target_pairs={{0,2},{1,3},{2,0},{3,1},{4,6},{5,7},{6,4},{7,5},{8,10},{9,11},{10,... | collective-permute-start | bytes 1572872 | tf_op jit(solution)/shard_map/ppermute | solution.py:211
  22.4 8.9 %copy-start.13 = (s32[8]{0:T(128)S(1)}, s32[8]{0:T(128)}, u32[]{:S(2)}) copy-start(s32[8]{0:T(128)} %param.23) | copy-start | bytes 100
  54.5 1.6 copy-start.6
  56.1 1.8 copy-start.7
  56.1 1.8 copy-start.8
  56.1 28.7 %copy-start.3 = (bf16[256,512]{1,0:T(8,128)(2,1)S(1)}, bf16[256,512]{1,0:T(8,128)(2,1)}, u32[]{:S(2)}) copy-start(bf16[256,512]{1,0:T(8,128)(2,1)} %param.17) | copy-start | bytes 786436
  56.1 35.6 %copy-start.9 = (f32[512]{0:T(512)S(1)}, f32[512]{0:T(512)}, u32[]{:S(2)}) copy-start(f32[512]{0:T(512)} %param.25) | copy-start | bytes 6148
  57.9 87.6 %all-gather.12.cloned.1.call-start = ((), (), s32[]{:S(2)}) async-start(), calls=%async_computation.7 | async-start | bytes 2506752 | tf_op jit(solution)/shard_map/all_gather | solution.py:117
  93.6 112.0 %all-gather.6.cloned.1.call-start = ((), (), s32[]{:S(2)}) async-start(), calls=%async_computation.3 | async-start | bytes 10485760 | tf_op jit(solution)/shard_map/all_gather | solution.py:123
  148.6 130.6 %all-gather.8.cloned.1.call-start = ((), (), s32[]{:S(2)}) async-start(), calls=%async_computation.4 | async-start | bytes 10485760 | tf_op jit(solution)/shard_map/all_gather | solution.py:128
  218.2 61.1 %copy-start.5 = (bf16[2,4,256,512]{3,2,1,0:T(8,128)(2,1)S(1)}, bf16[2,4,256,512]{3,2,1,0:T(8,128)(2,1)}, u32[]{:S(2)}) copy-start(bf16[2,4,256,512]{3,2,1,0:T(8,128)(2,1)} %copy.48) | copy-start | bytes 6291460
  220.8 135.9 %copy-start.10 = (f32[512]{0:T(512)S(1)}, f32[512]{0:T(512)}, u32[]{:S(2)}) copy-start(f32[512]{0:T(512)} %param.30) | copy-start | bytes 6148
  220.8 135.9 %reduce-scatter.5.cloned.1.call-start = ((), (), s32[]{:S(2)}) async-start(), calls=%async_computation.5 | async-start | bytes 2359296 | tf_op jit(solution)/shard_map/reduce_scatter | solution.py:132
  288.7 68.0 %copy-start.4 = (bf16[256,512]{1,0:T(8,128)(2,1)S(1)}, bf16[256,512]{1,0:T(8,128)(2,1)}, u32[]{:S(2)}) copy-start(bf16[256,512]{1,0:T(8,128)(2,1)} %reduce-scatter.3.cloned.1.call-done) | copy-start | bytes 786436
  288.7 85.8 %all-gather.10.cloned.1.call-start = ((), (), s32[]{:S(2)}) async-start(), calls=%async_computation.6 | async-start | bytes 1310720 | tf_op jit(solution)/shard_map/all_gather | solution.py:258
  358.7 28.2 %copy-start.11 = (f32[512]{0:T(512)S(1)}, f32[512]{0:T(512)}, u32[]{:S(2)}) copy-start(f32[512]{0:T(512)} %param.33) | copy-start | bytes 6148
  358.7 28.2 %copy-start.12 = (f32[512]{0:T(512)S(1)}, f32[512]{0:T(512)}, u32[]{:S(2)}) copy-start(f32[512]{0:T(512)} %param.32) | copy-start | bytes 6148
  379.6 1.2 copy-start.2
  380.7 10.3 %copy-start.1 = (bf16[512,2048]{1,0:T(8,128)(2,1)S(1)}, bf16[512,2048]{1,0:T(8,128)(2,1)}, u32[]{:S(2)}) copy-start(bf16[512,2048]{1,0:T(8,128)(2,1)} %param.24) | copy-start | bytes 6291460
Sparse Core Ops, SparseCore 0:
  58.0 26.8 reduce-scatter.2
  93.7 51.7 all-gather.11
  148.7 56.7 all-gather.5
  220.9 58.2 all-gather.7
  288.9 67.8 reduce-scatter.4
  358.8 15.6 all-gather.9

commit v7 on v6

--- a/solution.py
+++ b/solution.py
@@ -129,8 +129,37 @@
     partial = jnp.einsum(
         "etf,efd->td", weighted, down_full, preferred_element_type=jnp.float32
     ).astype(jnp.bfloat16)
-    partial = lax.psum_scatter(partial, "seq", scatter_dimension=0, tiled=True)
-    return partial.astype(jnp.float32)
+    return ring_reduce_scatter(partial, here, seq_count)
+
+
+def ring_reduce_scatter(partial, here, count):
+    half = count // 2
+    cycle = [2 * i for i in range(half)] + [2 * i + 1 for i in reversed(range(half))]
+    if count % 2 or count < 4:
+        cycle = list(range(count))
+    place = [0] * count
+    for p, device in enumerate(cycle):
+        place[device] = p
+    cycle_arr = jnp.array(cycle, jnp.int32)
+    pos = jnp.array(place, jnp.int32)[here]
+    tokens = partial.shape[0] // count
+    width = partial.shape[1]
+    blocks = partial.reshape(count, tokens, width)
+    halves = []
+    for direction in (1, -1):
+        cols = slice(0, width // 2) if direction == 1 else slice(width // 2, width)
+        pairs = [(cycle[p], cycle[(p + direction) % count]) for p in range(count)]
+
+        def block_for(q, cols=cols):
+            device = cycle_arr[q % count]
+            return lax.dynamic_index_in_dim(blocks, device, 0, keepdims=False)[:, cols].astype(jnp.float32)
+
+        acc = block_for(pos - direction)
+        for step in range(count - 1):
+            received = lax.ppermute(acc.astype(jnp.bfloat16), "seq", pairs)
+            acc = received.astype(jnp.float32) + block_for(pos - direction * (step + 2))
+        halves.append(acc)
+    return jnp.concatenate(halves, axis=1)
 
 
 def dispatch_experts(moe_in, expert_ids, route_weights, expert_gate_up, expert_down, experts_all, capacity):

time: 399 us -> 369 us (0.925)
  waiting for transfers between devices: 277 us -> 189 us
  between operations: 14.4 us -> 55.5 us
  starting transfers between devices: 5.14 us -> 19.2 us
    reduce_scatter x1 -> x0, waiting for transfers between devices: 68 us -> none  [dense_experts(): partial = lax.psum_scatter(partial, 'seq', scatter_dimension=0, tiled=True)]
    all_gather x1, waiting for transfers between devices: 58.4 us -> 15.1 us  [dense_experts(): weighted = lax.all_gather(weighted, 'tp', axis=2, tiled=True)]
    ppermute x0 -> x14, waiting for transfers between devices: none -> 23.7 us  [ring_reduce_scatter(): received = lax.ppermute(acc.astype(jnp.bfloat16), 'seq', pairs)]
    ppermute x0 -> x14, starting transfers between devices: none -> 15.6 us  [ring_reduce_scatter(): received = lax.ppermute(acc.astype(jnp.bfloat16), 'seq', pairs)]
    unnamed x33 -> x35, local copies, waits for them, and re-layouts: 12.6 us -> 13.2 us
  transfers between devices with their start and end apart: 9 -> 22, of which waited for: 6 -> 16; matrix products, arithmetic and copies ran while one was open for 5% -> 5% of each run, Pallas kernels for 4% -> 5%
where the time goes in v7:
time: 369 us
  waiting for transfers between devices  189 us (51%)
  between operations  55.5 us (15%)
  local copies, waits for them, and re-layouts  34.5 us (9%)
  matrix products  27.8 us (8%)
  starting transfers between devices  19.2 us (5%)
  Pallas kernels  16.8 us (5%)
  other arithmetic  14.4 us (4%)
  blocking collectives  11.8 us (3%)
    all_gather x1, waiting for transfers between devices, dense_experts(): rows = lax.all_gather(rows_q, 'tp', axis=1, tiled=True)  55.7 us
    all_gather x1, waiting for transfers between devices, dense_experts(): gathered = lax.all_gather(packed, 'seq', axis=0, tiled=False)  51.9 us
    reduce_scatter x1, waiting for transfers between devices, body(): lax.psum_scatter(attn_term.astype(jnp.bfloat16), 'tp', scatter_dimension=...  26.2 us
    ppermute x14, waiting for transfers between devices, ring_reduce_scatter(): received = lax.ppermute(acc.astype(jnp.bfloat16), 'seq', pairs)  23.7 us
    pallas_call x1, Pallas kernels, flash_attention(): pl.pallas_call(kernel, grid_spec=grid_spec, out_shape=jax.ShapeDtypeStruc...  16.8 us
    all_gather x1, waiting for transfers between devices, body(): lax.all_gather(scaled, 'tp', axis=1, tiled=True)  15.9 us
    ppermute x14, starting transfers between devices, ring_reduce_scatter(): received = lax.ppermute(acc.astype(jnp.bfloat16), 'seq', pairs)  15.6 us
    all_gather x1, waiting for transfers between devices, dense_experts(): weighted = lax.all_gather(weighted, 'tp', axis=2, tiled=True)  15.1 us
  transfers between devices with their start and end apart: 22, of which 16 were waited for; matrix products, arithmetic and copies ran while one was open for 5% of the time, Pallas kernels for 5%

profile of v7, /device:TPU:0, one launch (start us, length us, event | category | flops | bytes accessed | tf_op | source)
XLA Modules:
  0.0 368.6 jit_solution(7591835156740910073)
XLA Ops:
  7.3 2.8 dynamic-slice_bitcast_fusion
  10.1 2.4 collective-permute-start.2
  13.3 7.6 %reshape.141 = bf16[2,2048,512]{2,1,0:T(8,128)(2,1)} reshape(bf16[2,2048,2,256]{3,2,1,0:T(2,128)(2,1)} %param.30) | data formatting | bytes 8388608 | tf_op jit(solution)/shard_map/reshape | solution.py:244
  20.9 8.8 %copy.51 = bf16[2048,3,512]{0,2,1:T(8,128)(2,1)} copy(bf16[2048,3,512]{2,0,1:T(8,128)(2,1)} %param.33) | data formatting | bytes 12582912 | tf_op args[14]
  30.3 16.8 %shard_map.210 = bf16[256,512]{1,0:T(8,128)(2,1)} custom-call(s32[1]{0:T(128)} %dynamic_slice.121.len_ref, bf16[256,512]{1,0:T(8,128)(2,1)} %q_ref.1, bf16[4096,512]{1,0:T(8,128)(2,1)} %bitcast.133, bf16[4096,512]{1,0:T(8,128)(2,1)} %bitcast.134, bf16[256,512]{1,0:T(8,128)(2,1)} %nk_ref.1, bf16[256,512]{1,0:T(8,128)(2,1)} %nv_ref.1), custom_call_target="tpu_custom_call" | custom-call | tf_op jit(solution)/shard_map/pallas_call | solution.py:94
  47.2 3.0 pad_maximum_fusion
  50.2 3.6 gather_fusion
  53.8 1.9 select_bitcast_fusion
  55.6 1.6 copy.50
  57.3 1.7 convolution_convert_fusion
  59.1 26.2 %reduce-scatter.2.cloned.1.call-done = bf16[256,512]{1,0:T(8,128)(2,1)} async-done(((bf16[256,2048]{1,0:T(8,128)(2,1)}), bf16[256,512]{1,0:T(8,128)(2,1)}) %reduce-scatter.2.cloned.1.call-update) | async-done | bytes 262160 | tf_op jit(solution)/shard_map/reduce_scatter | solution.py:267
  85.3 1.1 multiply_reduce_fusion.3
  86.5 5.8 %psum.28 = f32[256]{0:T(256)S(1)} all-reduce(f32[256]{0:T(256)S(1)} %multiply_reduce_fusion.3), channel_id=1, replica_groups=mesh['seq'=8,'tp'=4] {'tp'}, use_global_device_ids=true, to_apply=%region_2.3 | all-reduce | flops 256 | bytes 2048 | tf_op jit(solution)/shard_map/psum | solution.py:270
  92.2 1.1 multiply_convert_fusion.4
  94.1 51.9 %all-gather.12.cloned.1.call-done = bf16[2176,512]{1,0:T(8,128)(2,1)} async-done(((bf16[272,512]{1,0:T(8,128)(2,1)}), bf16[2176,512]{1,0:T(8,128)(2,1)}) %all-gather.12.cloned.1.call-update) | async-done | bytes 2228240 | tf_op jit(solution)/shard_map/all_gather | solution.py:117
  146.0 3.1 slice.106
  149.4 0.9 slice_convert_fusion
  150.4 55.7 %all-gather.6.cloned.1.call-done = bf16[2048,2048]{1,0:T(8,128)(2,1)} async-done(((bf16[2048,512]{1,0:T(8,128)(2,1)}), bf16[2048,2048]{1,0:T(8,128)(2,1)}) %all-gather.6.cloned.1.call-update) | async-done | bytes 8388624 | tf_op jit(solution)/shard_map/all_gather | solution.py:123
  206.1 12.6 %fusion.2 = f32[2,2048,512]{1,2,0:T(8,128)S(1)} fusion(bf16[2,2048,512]{2,1,0:T(8,128)(2,1)} %reshape.141, bf16[2048,2048]{1,0:T(8,128)(2,1)} %all-gather.6.cloned.1.call-done), kind=kOutput, calls=%fused_computation.3 | convolution fusion | flops 8589934592 | bytes 20971520 | tf_op jit(solution)/shard_map/td,edf->etf/dot_general | solution.py:124
  218.7 2.6 multiply_convert_fusion
  264.6 15.1 %all-gather.8.cloned.1.call-done = bf16[2,2048,1024]{1,2,0:T(8,128)(2,1)} async-done(((bf16[2,2048,256]{1,2,0:T(8,128)(2,1)}), bf16[2,2048,1024]{1,2,0:T(8,128)(2,1)}) %all-gather.8.cloned.1.call-update) | async-done | bytes 8388624 | tf_op jit(solution)/shard_map/all_gather | solution.py:128
  279.8 8.5 %bitcast_convert_fusion = bf16[2048,512]{1,0:T(8,128)(2,1)S(1)} fusion(bf16[2,2048,1024]{1,2,0:T(8,128)(2,1)} %all-gather.8.cloned.1.call-done, bf16[2,1024,512]{2,1,0:T(8,128)(2,1)} %bitcast.137), kind=kOutput, calls=%fused_computation.6 | convolution fusion | flops 4296015872 | bytes 12582912 | tf_op jit(solution)/shard_map/etf,efd->td/dot_general | solution.py:129
  288.8 1.5 collective-permute-start.10
  291.0 3.6 collective-permute-done.10
  294.6 1.5 collective-permute-start.11
  296.1 0.8 collective-permute-start.4
  297.0 2.6 collective-permute-done.11
  299.6 1.5 collective-permute-start.12
  302.0 2.8 collective-permute-done.12
  304.8 1.5 collective-permute-start.13
  307.2 3.7 %collective-permute-done.13 = bf16[256,256]{1,0:T(8,128)(2,1)S(1)} collective-permute-done((bf16[256,256]{1,0:T(8,128)(2,1)S(1)}, bf16[256,256]{1,0:T(8,128)(2,1)S(1)}, u32[]{:S(2)}, u32[]{:S(2)}) %collective-permute-start.13) | collective-permute-done | bytes 131104 | tf_op jit(solution)/shard_map/ppermute | solution.py:159
  310.9 1.5 collective-permute-start.14
  312.6 0.9 collective-permute-start.7
  313.5 3.3 collective-permute-done.14
  316.9 1.5 collective-permute-start.15
  319.1 2.9 collective-permute-done.15
  322.0 1.5 collective-permute-start.16
  324.2 2.8 collective-permute-done.16
  327.1 1.5 collective-permute-done.9
  328.7 0.9 multiply_reduce_fusion.2
  329.6 15.9 %all-gather.10.cloned.1.call-done = bf16[256,2048]{1,0:T(8,128)(2,1)} async-done(((bf16[256,512]{1,0:T(8,128)(2,1)}), bf16[256,2048]{1,0:T(8,128)(2,1)}) %all-gather.10.cloned.1.call-update) | async-done | bytes 1048592 | tf_op jit(solution)/shard_map/all_gather | solution.py:287
  345.6 5.0 %fusion.21 = f32[256,1536]{0,1:T(8,128)S(1)} fusion(bf16[256,2048]{1,0:T(8,128)(2,1)} %all-gather.10.cloned.1.call-done, bf16[2048,1536]{0,1:T(8,128)(2,1)} %bitcast.130), kind=kOutput, calls=%fused_computation.96 | convolution fusion | flops 1610612736 | bytes 8912896 | tf_op jit(solution)/shard_map/dot_general | solution.py:286
  350.6 1.2 copy-done.2
  351.9 6.0 %all-reduce = (f32[256]{0:T(256)S(1)}, f32[256]{0:T(256)S(1)}, f32[256]{0:T(256)S(1)}) all-reduce(f32[256]{0:T(256)S(1)} %get-tuple-element.25, f32[256]{0:T(256)S(1)} %get-tuple-element.54, f32[256]{0:T(256)S(1)} %get-tuple-element.24), channel_id=1, replica_groups=mesh['seq'=8,'tp'=4] {'tp'}, use_global_device_ids=true, to_apply=%region_7.8 | all-reduce | flops 768 | bytes 6144 | tf_op jit(solution)/shard_map/psum | solution.py:293
  357.9 1.6 fusion.7
  359.5 0.8 copy.56
  360.4 0.8 copy.57
  361.2 0.8 copy.58
  (91 shorter events, 9.5 us)
Async XLA Ops:
  7.2 50.1 %copy-start = (bf16[512,2048]{1,0:T(8,128)(2,1)S(1)}, bf16[512,2048]{1,0:T(8,128)(2,1)}, u32[]{:S(2)}) copy-start(bf16[512,2048]{1,0:T(8,128)(2,1)} %param.26) | copy-start | bytes 6291460
  7.2 78.2 %reduce-scatter.2.cloned.1.call-start = ((), (), s32[]{:S(2)}) async-start(), calls=%async_computation.1 | async-start | bytes 1310720 | tf_op jit(solution)/shard_map/reduce_scatter | solution.py:267
  10.1 37.0 %collective-permute-start.2 = (bf16[2,256,512]{2,1,0:T(8,128)(2,1)}, bf16[2,256,512]{2,1,0:T(8,128)(2,1)}, u32[]{:S(2)}, u32[]{:S(2)}) collective-permute-start(bf16[2,256,512]{2,1,0:T(8,128)(2,1)} %get-tuple-element.49), channel_id=1, source_target_pairs={{0,3},{1,0},{2,1},{3,2},{4,7},{5,4},{6,5},{7,6},{8,11},{9,8},{10,9... | collective-permute-start | bytes 1572872 | tf_op jit(solution)/shard_map/ppermute | solution.py:240
  12.5 34.7 %collective-permute-start.1 = (bf16[2,256,512]{2,1,0:T(8,128)(2,1)}, bf16[2,256,512]{2,1,0:T(8,128)(2,1)}, u32[]{:S(2)}, u32[]{:S(2)}) collective-permute-start(bf16[2,256,512]{2,1,0:T(8,128)(2,1)} %get-tuple-element.50), channel_id=1, source_target_pairs={{0,2},{1,3},{2,0},{3,1},{4,6},{5,7},{6,4},{7,5},{8,10},{9,11},{10,... | collective-permute-start | bytes 1572872 | tf_op jit(solution)/shard_map/ppermute | solution.py:240
  13.1 34.1 %collective-permute-start = (bf16[2,256,512]{2,1,0:T(8,128)(2,1)S(1)}, bf16[2,256,512]{2,1,0:T(8,128)(2,1)}, u32[]{:S(2)}, u32[]{:S(2)}) collective-permute-start(bf16[2,256,512]{2,1,0:T(8,128)(2,1)S(1)} %get-tuple-element.48), channel_id=1, source_target_pairs={{0,1},{1,2},{2,3},{3,0},{4,5},{5,6},{6,7},{7,4},{8,9},{9,10},{10,1... | collective-permute-start | bytes 1572872 | tf_op jit(solution)/shard_map/ppermute | solution.py:240
  20.9 8.8 %copy-start.13 = (s32[8]{0:T(128)S(1)}, s32[8]{0:T(128)}, u32[]{:S(2)}) copy-start(s32[8]{0:T(128)} %param.25) | copy-start | bytes 100
  55.6 1.6 copy-start.5
  57.2 1.8 copy-start.7
  57.2 1.8 copy-start.8
  57.2 28.1 %copy-start.3 = (bf16[256,512]{1,0:T(8,128)(2,1)S(1)}, bf16[256,512]{1,0:T(8,128)(2,1)}, u32[]{:S(2)}) copy-start(bf16[256,512]{1,0:T(8,128)(2,1)} %param.19) | copy-start | bytes 786436
  57.3 35.0 %copy-start.9 = (f32[512]{0:T(512)S(1)}, f32[512]{0:T(512)}, u32[]{:S(2)}) copy-start(f32[512]{0:T(512)} %param.27) | copy-start | bytes 6148
  59.0 87.0 %all-gather.12.cloned.1.call-start = ((), (), s32[]{:S(2)}) async-start(), calls=%async_computation.5 | async-start | bytes 2506752 | tf_op jit(solution)/shard_map/all_gather | solution.py:117
  94.0 112.1 %all-gather.6.cloned.1.call-start = ((), (), s32[]{:S(2)}) async-start(), calls=%async_computation.2 | async-start | bytes 10485760 | tf_op jit(solution)/shard_map/all_gather | solution.py:123
  149.1 130.6 %all-gather.8.cloned.1.call-start = ((), (), s32[]{:S(2)}) async-start(), calls=%async_computation.3 | async-start | bytes 10485760 | tf_op jit(solution)/shard_map/all_gather | solution.py:128
  221.3 0.7 copy-start.14
  221.3 12.0 %copy-start.6 = (s32[8]{0:T(128)S(1)}, s32[8]{0:T(128)}, u32[]{:S(2)}) copy-start(s32[8]{0:T(128)} %constant.251.clone) | copy-start | bytes 100
  221.3 124.2 %all-gather.10.cloned.1.call-start = ((), (), s32[]{:S(2)}) async-start(), calls=%async_computation.4 | async-start | bytes 1310720 | tf_op jit(solution)/shard_map/all_gather | solution.py:287
  288.8 5.7 %collective-permute-start.10 = (bf16[256,256]{1,0:T(8,128)(2,1)S(1)}, bf16[256,256]{1,0:T(8,128)(2,1)S(1)}, u32[]{:S(2)}, u32[]{:S(2)}) collective-permute-start(bf16[256,256]{1,0:T(8,128)(2,1)S(1)} %slice.120), channel_id=1, source_target_pairs={{0,4},{8,0},{16,8},{24,16},{28,24},{20,28},{12,20},{4,12},{1,5},{9... | collective-permute-start | bytes 393224 | tf_op jit(solution)/shard_map/ppermute | solution.py:159
  290.4 5.7 %collective-permute-start.3 = (bf16[256,256]{1,0:T(8,128)(2,1)S(1)}, bf16[256,256]{1,0:T(8,128)(2,1)S(1)}, u32[]{:S(2)}, u32[]{:S(2)}) collective-permute-start(bf16[256,256]{1,0:T(8,128)(2,1)S(1)} %slice.112), channel_id=1, source_target_pairs={{0,8},{8,16},{16,24},{24,28},{28,20},{20,12},{12,4},{4,0},{1,9},{9... | collective-permute-start | bytes 393224 | tf_op jit(solution)/shard_map/ppermute | solution.py:159
  294.6 5.0 %collective-permute-start.11 = (bf16[256,256]{1,0:T(8,128)(2,1)S(1)}, bf16[256,256]{1,0:T(8,128)(2,1)S(1)}, u32[]{:S(2)}, u32[]{:S(2)}) collective-permute-start(bf16[256,256]{1,0:T(8,128)(2,1)S(1)} %add_convert_fusion.5), channel_id=1, source_target_pairs={{0,4},{8,0},{16,8},{24,16},{28,24},{20,28},{12,20},{4,12},{1,5},{9... | collective-permute-start | bytes 393224 | tf_op jit(solution)/shard_map/ppermute | solution.py:159
  296.1 5.2 %collective-permute-start.4 = (bf16[256,256]{1,0:T(8,128)(2,1)S(1)}, bf16[256,256]{1,0:T(8,128)(2,1)S(1)}, u32[]{:S(2)}, u32[]{:S(2)}) collective-permute-start(bf16[256,256]{1,0:T(8,128)(2,1)S(1)} %add_convert_fusion.11), channel_id=1, source_target_pairs={{0,8},{8,16},{16,24},{24,28},{28,20},{20,12},{12,4},{4,0},{1,9},{9... | collective-permute-start | bytes 393224 | tf_op jit(solution)/shard_map/ppermute | solution.py:159
  299.6 5.1 %collective-permute-start.12 = (bf16[256,256]{1,0:T(8,128)(2,1)S(1)}, bf16[256,256]{1,0:T(8,128)(2,1)S(1)}, u32[]{:S(2)}, u32[]{:S(2)}) collective-permute-start(bf16[256,256]{1,0:T(8,128)(2,1)S(1)} %add_convert_fusion.4), channel_id=1, source_target_pairs={{0,4},{8,0},{16,8},{24,16},{28,24},{20,28},{12,20},{4,12},{1,5},{9... | collective-permute-start | bytes 393224 | tf_op jit(solution)/shard_map/ppermute | solution.py:159
  301.4 5.0 %collective-permute-start.5 = (bf16[256,256]{1,0:T(8,128)(2,1)S(1)}, bf16[256,256]{1,0:T(8,128)(2,1)S(1)}, u32[]{:S(2)}, u32[]{:S(2)}) collective-permute-start(bf16[256,256]{1,0:T(8,128)(2,1)S(1)} %add_convert_fusion.10), channel_id=1, source_target_pairs={{0,8},{8,16},{16,24},{24,28},{28,20},{20,12},{12,4},{4,0},{1,9},{9... | collective-permute-start | bytes 393224 | tf_op jit(solution)/shard_map/ppermute | solution.py:159
  304.8 23.9 %copy-start.4 = (bf16[256,512]{1,0:T(8,128)(2,1)S(1)}, bf16[256,512]{1,0:T(8,128)(2,1)}, u32[]{:S(2)}) copy-start(bf16[256,512]{1,0:T(8,128)(2,1)} %reduce-scatter.2.cloned.1.call-done) | copy-start | bytes 786436
  304.8 23.9 %copy-start.10 = (f32[512]{0:T(512)S(1)}, f32[512]{0:T(512)}, u32[]{:S(2)}) copy-start(f32[512]{0:T(512)} %param.32) | copy-start | bytes 6148
  304.8 6.1 %collective-permute-start.13 = (bf16[256,256]{1,0:T(8,128)(2,1)S(1)}, bf16[256,256]{1,0:T(8,128)(2,1)S(1)}, u32[]{:S(2)}, u32[]{:S(2)}) collective-permute-start(bf16[256,256]{1,0:T(8,128)(2,1)S(1)} %add_convert_fusion.3), channel_id=1, source_target_pairs={{0,4},{8,0},{16,8},{24,16},{28,24},{20,28},{12,20},{4,12},{1,5},{9... | collective-permute-start | bytes 393224 | tf_op jit(solution)/shard_map/ppermute | solution.py:159
  306.5 6.1 %collective-permute-start.6 = (bf16[256,256]{1,0:T(8,128)(2,1)S(1)}, bf16[256,256]{1,0:T(8,128)(2,1)S(1)}, u32[]{:S(2)}, u32[]{:S(2)}) collective-permute-start(bf16[256,256]{1,0:T(8,128)(2,1)S(1)} %add_convert_fusion.9), channel_id=1, source_target_pairs={{0,8},{8,16},{16,24},{24,28},{28,20},{20,12},{12,4},{4,0},{1,9},{9... | collective-permute-start | bytes 393224 | tf_op jit(solution)/shard_map/ppermute | solution.py:159
  310.9 5.9 %collective-permute-start.14 = (bf16[256,256]{1,0:T(8,128)(2,1)S(1)}, bf16[256,256]{1,0:T(8,128)(2,1)S(1)}, u32[]{:S(2)}, u32[]{:S(2)}) collective-permute-start(bf16[256,256]{1,0:T(8,128)(2,1)S(1)} %add_convert_fusion.2), channel_id=1, source_target_pairs={{0,4},{8,0},{16,8},{24,16},{28,24},{20,28},{12,20},{4,12},{1,5},{9... | collective-permute-start | bytes 393224 | tf_op jit(solution)/shard_map/ppermute | solution.py:159
  312.6 5.8 %collective-permute-start.7 = (bf16[256,256]{1,0:T(8,128)(2,1)S(1)}, bf16[256,256]{1,0:T(8,128)(2,1)S(1)}, u32[]{:S(2)}, u32[]{:S(2)}) collective-permute-start(bf16[256,256]{1,0:T(8,128)(2,1)S(1)} %add_convert_fusion.8), channel_id=1, source_target_pairs={{0,8},{8,16},{16,24},{24,28},{28,20},{20,12},{12,4},{4,0},{1,9},{9... | collective-permute-start | bytes 393224 | tf_op jit(solution)/shard_map/ppermute | solution.py:159
  316.9 5.1 %collective-permute-start.15 = (bf16[256,256]{1,0:T(8,128)(2,1)S(1)}, bf16[256,256]{1,0:T(8,128)(2,1)S(1)}, u32[]{:S(2)}, u32[]{:S(2)}) collective-permute-start(bf16[256,256]{1,0:T(8,128)(2,1)S(1)} %add_convert_fusion.1), channel_id=1, source_target_pairs={{0,4},{8,0},{16,8},{24,16},{28,24},{20,28},{12,20},{4,12},{1,5},{9... | collective-permute-start | bytes 393224 | tf_op jit(solution)/shard_map/ppermute | solution.py:159
  318.4 5.1 %collective-permute-start.8 = (bf16[256,256]{1,0:T(8,128)(2,1)S(1)}, bf16[256,256]{1,0:T(8,128)(2,1)S(1)}, u32[]{:S(2)}, u32[]{:S(2)}) collective-permute-start(bf16[256,256]{1,0:T(8,128)(2,1)S(1)} %add_convert_fusion.7), channel_id=1, source_target_pairs={{0,8},{8,16},{16,24},{24,28},{28,20},{20,12},{12,4},{4,0},{1,9},{9... | collective-permute-start | bytes 393224 | tf_op jit(solution)/shard_map/ppermute | solution.py:159
  322.0 5.0 %collective-permute-start.16 = (bf16[256,256]{1,0:T(8,128)(2,1)S(1)}, bf16[256,256]{1,0:T(8,128)(2,1)S(1)}, u32[]{:S(2)}, u32[]{:S(2)}) collective-permute-start(bf16[256,256]{1,0:T(8,128)(2,1)S(1)} %add_convert_fusion), channel_id=1, source_target_pairs={{0,4},{8,0},{16,8},{24,16},{28,24},{20,28},{12,20},{4,12},{1,5},{9... | collective-permute-start | bytes 393224 | tf_op jit(solution)/shard_map/ppermute | solution.py:159
  323.6 5.0 %collective-permute-start.9 = (bf16[256,256]{1,0:T(8,128)(2,1)S(1)}, bf16[256,256]{1,0:T(8,128)(2,1)S(1)}, u32[]{:S(2)}, u32[]{:S(2)}) collective-permute-start(bf16[256,256]{1,0:T(8,128)(2,1)S(1)} %add_convert_fusion.6), channel_id=1, source_target_pairs={{0,8},{8,16},{16,24},{24,28},{28,20},{20,12},{12,4},{4,0},{1,9},{9... | collective-permute-start | bytes 393224 | tf_op jit(solution)/shard_map/ppermute | solution.py:159
  329.6 28.3 %copy-start.11 = (f32[512]{0:T(512)S(1)}, f32[512]{0:T(512)}, u32[]{:S(2)}) copy-start(f32[512]{0:T(512)} %param.35) | copy-start | bytes 6148
  329.6 28.3 %copy-start.12 = (f32[512]{0:T(512)S(1)}, f32[512]{0:T(512)}, u32[]{:S(2)}) copy-start(f32[512]{0:T(512)} %param.34) | copy-start | bytes 6148
  350.6 1.2 copy-start.2
  351.8 10.3 %copy-start.1 = (bf16[512,2048]{1,0:T(8,128)(2,1)S(1)}, bf16[512,2048]{1,0:T(8,128)(2,1)}, u32[]{:S(2)}) copy-start(bf16[512,2048]{1,0:T(8,128)(2,1)} %param.26) | copy-start | bytes 6291460
Sparse Core Ops, SparseCore 0:
  59.1 26.1 reduce-scatter.1
  94.2 51.7 all-gather.11
  149.3 56.7 all-gather.5
  221.5 58.2 all-gather.7
  329.7 15.7 all-gather.9

commit v8 on v7

--- a/solution.py
+++ b/solution.py
@@ -114,7 +114,8 @@
     gate_lo = (gate_t - gate_hi.astype(jnp.float32)).astype(jnp.bfloat16)
     info = jnp.concatenate([gate_hi, gate_lo], axis=0).reshape(-1, quarter)
     packed = jnp.concatenate([moe_in, info], axis=0)
-    gathered = lax.all_gather(packed, "seq", axis=0, tiled=False)
+    ring = ring_order(seq_count)
+    gathered = ring_all_gather(packed, here, ring)
     rows_q = gathered[:, :tokens].reshape(seq_count * tokens, quarter)
     info_all = gathered[:, tokens:].reshape(seq_count, 2, experts_all, tokens).astype(jnp.float32)
     gate_all = info_all[:, 0] + info_all[:, 1]
@@ -129,19 +130,34 @@
     partial = jnp.einsum(
         "etf,efd->td", weighted, down_full, preferred_element_type=jnp.float32
     ).astype(jnp.bfloat16)
-    return ring_reduce_scatter(partial, here, seq_count)
-
-
-def ring_reduce_scatter(partial, here, count):
+    return ring_reduce_scatter(partial, ring)
+
+
+def ring_order(count):
     half = count // 2
-    cycle = [2 * i for i in range(half)] + [2 * i + 1 for i in reversed(range(half))]
     if count % 2 or count < 4:
-        cycle = list(range(count))
-    place = [0] * count
-    for p, device in enumerate(cycle):
-        place[device] = p
-    cycle_arr = jnp.array(cycle, jnp.int32)
-    pos = jnp.array(place, jnp.int32)[here]
+        return list(range(count))
+    return [2 * i for i in range(half)] + [2 * i + 1 for i in reversed(range(half))]
+
+
+def ring_all_gather(block, here, cycle):
+    count = len(cycle)
+    forward = [(cycle[p], cycle[(p + 1) % count]) for p in range(count)]
+    backward = [(cycle[p], cycle[(p - 1) % count]) for p in range(count)]
+    by_offset = [block] * count
+    ahead = block
+    for step in range(1, count // 2 + 1):
+        ahead = lax.ppermute(ahead, "seq", forward)
+        by_offset[(-step) % count] = ahead
+    behind = block
+    for step in range(1, count - count // 2):
+        behind = lax.ppermute(behind, "seq", backward)
+        by_offset[step] = behind
+    return jnp.stack(by_offset)
+
+
+def ring_reduce_scatter(partial, cycle):
+    count = len(cycle)
     tokens = partial.shape[0] // count
     width = partial.shape[1]
     blocks = partial.reshape(count, tokens, width)
@@ -149,15 +165,11 @@
     for direction in (1, -1):
         cols = slice(0, width // 2) if direction == 1 else slice(width // 2, width)
         pairs = [(cycle[p], cycle[(p + direction) % count]) for p in range(count)]
-
-        def block_for(q, cols=cols):
-            device = cycle_arr[q % count]
-            return lax.dynamic_index_in_dim(blocks, device, 0, keepdims=False)[:, cols].astype(jnp.float32)
-
-        acc = block_for(pos - direction)
+        acc = blocks[(-direction) % count, :, cols].astype(jnp.float32)
         for step in range(count - 1):
             received = lax.ppermute(acc.astype(jnp.bfloat16), "seq", pairs)
-            acc = received.astype(jnp.float32) + block_for(pos - direction * (step + 2))
+            offset = (-direction * (step + 2)) % count
+            acc = received.astype(jnp.float32) + blocks[offset, :, cols].astype(jnp.float32)
         halves.append(acc)
     return jnp.concatenate(halves, axis=1)
 

time: 369 us -> 360 us (0.976)
  between operations: 55.5 us -> 14.2 us
  waiting for transfers between devices: 189 us -> 210 us
  starting transfers between devices: 19.2 us -> 27.2 us
  other arithmetic: 14.4 us -> 20.5 us
    all_gather x1 -> x0, waiting for transfers between devices: 51.9 us -> none  [dense_experts(): gathered = lax.all_gather(packed, 'seq', axis=0, tiled=False)]
    all_gather x1, waiting for transfers between devices: 15.1 us -> 58.4 us  [dense_experts(): weighted = lax.all_gather(weighted, 'tp', axis=2, tiled=True)]
    ppermute x0 -> x7, waiting for transfers between devices: none -> 21.7 us  [the longest x4 21.7 us: ring_all_gather(): ahead = lax.ppermute(ahead, 'seq', forward)]
    ppermute x0 -> x7, starting transfers between devices: none -> 7.62 us  [the longest x4 5.79 us: ring_all_gather(): ahead = lax.ppermute(ahead, 'seq', forward)]
    ppermute x14, waiting for transfers between devices: 23.7 us -> 30 us  [ring_reduce_scatter(): received = lax.ppermute(acc.astype(jnp.bfloat16), 'seq', pairs)]
    convert_element_type x12 -> x6, other arithmetic: 0.4 us -> 6.19 us  [ring_reduce_scatter(): received = lax.ppermute(acc.astype(jnp.bfloat16), 'seq', pairs)]
    unnamed x35 -> x43, local copies, waits for them, and re-layouts: 13.2 us -> 14.1 us
  transfers between devices with their start and end apart: 22 -> 28, of which waited for: 16 -> 22; matrix products, arithmetic and copies ran while one was open for 5% -> 5% of each run, Pallas kernels for 5% -> 5%
where the time goes in v8:
time: 360 us
  waiting for transfers between devices  210 us (58%)
  local copies, waits for them, and re-layouts  32.1 us (9%)
  matrix products  27.7 us (8%)
  starting transfers between devices  27.2 us (8%)
  other arithmetic  20.5 us (6%)
  Pallas kernels  16.8 us (5%)
  between operations  14.2 us (4%)
  blocking collectives  11.8 us (3%)
    all_gather x1, waiting for transfers between devices, dense_experts(): weighted = lax.all_gather(weighted, 'tp', axis=2, tiled=True)  58.4 us
    all_gather x1, waiting for transfers between devices, dense_experts(): rows = lax.all_gather(rows_q, 'tp', axis=1, tiled=True)  58.3 us
    ppermute x14, waiting for transfers between devices, ring_reduce_scatter(): received = lax.ppermute(acc.astype(jnp.bfloat16), 'seq', pairs)  30 us
    reduce_scatter x1, waiting for transfers between devices, body(): lax.psum_scatter(attn_term.astype(jnp.bfloat16), 'tp', scatter_dimension=...  25.2 us
    ppermute x4, waiting for transfers between devices, ring_all_gather(): ahead = lax.ppermute(ahead, 'seq', forward)  21.7 us
    pallas_call x1, Pallas kernels, flash_attention(): pl.pallas_call(kernel, grid_spec=grid_spec, out_shape=jax.ShapeDtypeStruc...  16.8 us
    all_gather x1, waiting for transfers between devices, body(): lax.all_gather(scaled, 'tp', axis=1, tiled=True)  15.9 us
    ppermute x14, starting transfers between devices, ring_reduce_scatter(): received = lax.ppermute(acc.astype(jnp.bfloat16), 'seq', pairs)  14.5 us
  transfers between devices with their start and end apart: 28, of which 22 were waited for; matrix products, arithmetic and copies ran while one was open for 5% of the time, Pallas kernels for 5%

profile of v8, /device:TPU:0, one launch (start us, length us, event | category | flops | bytes accessed | tf_op | source)
XLA Modules:
  0.0 359.9 jit_solution(1670479779411876217)
XLA Ops:
  7.3 2.9 dynamic-slice_bitcast_fusion
  10.6 2.0 collective-permute-start.2
  12.5 2.3 collective-permute-start.1
  14.8 7.6 %reshape.137 = bf16[2,2048,512]{2,1,0:T(8,128)(2,1)} reshape(bf16[2,2048,2,256]{3,2,1,0:T(2,128)(2,1)} %param.28) | data formatting | bytes 8388608 | tf_op jit(solution)/shard_map/reshape | solution.py:256
  22.5 8.8 %copy.52 = bf16[2048,3,512]{0,2,1:T(8,128)(2,1)} copy(bf16[2048,3,512]{2,0,1:T(8,128)(2,1)} %param.31) | data formatting | bytes 12582912 | tf_op args[14]
  31.9 16.8 %shard_map.192 = bf16[256,512]{1,0:T(8,128)(2,1)} custom-call(s32[1]{0:T(128)} %dynamic_slice.21.len_ref, bf16[256,512]{1,0:T(8,128)(2,1)} %q_ref.1, bf16[4096,512]{1,0:T(8,128)(2,1)} %bitcast.156, bf16[4096,512]{1,0:T(8,128)(2,1)} %bitcast.157, bf16[256,512]{1,0:T(8,128)(2,1)} %nk_ref.1, bf16[256,512]{1,0:T(8,128)(2,1)} %nv_ref.1), custom_call_target="tpu_custom_call" | custom-call | tf_op jit(solution)/shard_map/pallas_call | solution.py:94
  48.7 3.0 pad_maximum_fusion
  51.7 3.6 %gather_fusion = bf16[4,2,256,512]{3,2,1,0:T(8,128)(2,1)} fusion(bf16[4,2,256,512]{3,2,1,0:T(8,128)(2,1)} %pad_maximum_fusion, s32[1024]{0:T(1024)S(1)} %pad_clamp_fusion), kind=kCustom, calls=%fused_computation | custom fusion | bytes 4194320 | tf_op jit(solution)/shard_map/jit(_take)/gather | solution.py:254
  55.3 1.9 select_bitcast_fusion
  57.2 1.6 copy.51
  58.8 1.7 convolution_convert_fusion
  60.7 25.2 %reduce-scatter.2.cloned.1.call-done = bf16[256,512]{1,0:T(8,128)(2,1)} async-done(((bf16[256,2048]{1,0:T(8,128)(2,1)}), bf16[256,512]{1,0:T(8,128)(2,1)}) %reduce-scatter.2.cloned.1.call-update) | async-done | bytes 262160 | tf_op jit(solution)/shard_map/reduce_scatter | solution.py:279
  87.0 5.8 %psum.28 = f32[256]{0:T(256)S(1)} all-reduce(f32[256]{0:T(256)S(1)} %multiply_reduce_fusion.3), channel_id=1, replica_groups=mesh['seq'=8,'tp'=4] {'tp'}, use_global_device_ids=true, to_apply=%region_2.3 | all-reduce | flops 256 | bytes 2048 | tf_op jit(solution)/shard_map/psum | solution.py:282
  93.9 1.7 collective-permute-start.6
  96.0 6.3 %collective-permute-done.6 = bf16[272,512]{1,0:T(8,128)(2,1)S(1)} collective-permute-done((bf16[272,512]{1,0:T(8,128)(2,1)S(1)}, bf16[272,512]{1,0:T(8,128)(2,1)S(1)}, u32[]{:S(2)}, u32[]{:S(2)}) %collective-permute-start.6) | collective-permute-done | bytes 278560 | tf_op jit(solution)/shard_map/ppermute | solution.py:150
  102.3 1.4 collective-permute-start.7
  104.3 5.4 %collective-permute-done.7 = bf16[272,512]{1,0:T(8,128)(2,1)S(1)} collective-permute-done((bf16[272,512]{1,0:T(8,128)(2,1)S(1)}, bf16[272,512]{1,0:T(8,128)(2,1)S(1)}, u32[]{:S(2)}, u32[]{:S(2)}) %collective-permute-start.7) | collective-permute-done | bytes 278560 | tf_op jit(solution)/shard_map/ppermute | solution.py:150
  111.9 4.9 %collective-permute-done.8 = bf16[272,512]{1,0:T(8,128)(2,1)S(1)} collective-permute-done((bf16[272,512]{1,0:T(8,128)(2,1)S(1)}, bf16[272,512]{1,0:T(8,128)(2,1)S(1)}, u32[]{:S(2)}, u32[]{:S(2)}) %collective-permute-start.8) | collective-permute-done | bytes 278560 | tf_op jit(solution)/shard_map/ppermute | solution.py:150
  116.8 1.4 collective-permute-start.9
  118.3 5.0 %collective-permute-done.9 = bf16[272,512]{1,0:T(8,128)(2,1)S(1)} collective-permute-done((bf16[272,512]{1,0:T(8,128)(2,1)S(1)}, bf16[272,512]{1,0:T(8,128)(2,1)S(1)}, u32[]{:S(2)}, u32[]{:S(2)}) %collective-permute-start.9) | collective-permute-done | bytes 278560 | tf_op jit(solution)/shard_map/ppermute | solution.py:150
  123.5 1.4 copy-done.3
  124.8 1.6 slice.106
  127.8 58.3 %all-gather.4.cloned.1.call-done = bf16[2048,2048]{1,0:T(8,128)(2,1)} async-done(((bf16[2048,512]{1,0:T(8,128)(2,1)}), bf16[2048,2048]{1,0:T(8,128)(2,1)}) %all-gather.4.cloned.1.call-update) | async-done | bytes 8388624 | tf_op jit(solution)/shard_map/all_gather | solution.py:124
  186.1 12.6 %fusion.2 = f32[2,2048,512]{1,2,0:T(8,128)S(1)} fusion(bf16[2,2048,512]{2,1,0:T(8,128)(2,1)} %reshape.137, bf16[2048,2048]{1,0:T(8,128)(2,1)} %all-gather.4.cloned.1.call-done), kind=kOutput, calls=%fused_computation.3 | convolution fusion | flops 8589934592 | bytes 20971520 | tf_op jit(solution)/shard_map/td,edf->etf/dot_general | solution.py:125
  198.7 2.6 multiply_convert_fusion
  201.3 58.4 %all-gather.6.cloned.1.call-done = bf16[2,2048,1024]{1,2,0:T(8,128)(2,1)} async-done(((bf16[2,2048,256]{1,2,0:T(8,128)(2,1)}), bf16[2,2048,1024]{1,2,0:T(8,128)(2,1)}) %all-gather.6.cloned.1.call-update) | async-done | bytes 8388624 | tf_op jit(solution)/shard_map/all_gather | solution.py:129
  259.7 8.4 %bitcast_convert_fusion = bf16[2048,512]{1,0:T(8,128)(2,1)S(1)} fusion(bf16[2,2048,1024]{1,2,0:T(8,128)(2,1)} %all-gather.6.cloned.1.call-done, bf16[2,1024,512]{2,1,0:T(8,128)(2,1)S(1)} %bitcast.166), kind=kOutput, calls=%fused_computation.6 | convolution fusion | flops 4296015872 | bytes 12582912 | tf_op jit(solution)/shard_map/etf,efd->td/dot_general | solution.py:130
  268.2 1.5 collective-permute-start.10
  270.3 3.6 %collective-permute-done.10 = bf16[256,256]{1,0:T(8,128)(2,1)S(1)} collective-permute-done((bf16[256,256]{1,0:T(8,128)(2,1)S(1)}, bf16[256,256]{1,0:T(8,128)(2,1)S(1)}, u32[]{:S(2)}, u32[]{:S(2)}) %collective-permute-start.10) | collective-permute-done | bytes 131104 | tf_op jit(solution)/shard_map/ppermute | solution.py:170
  276.2 1.5 collective-permute-start.11
  278.3 2.9 collective-permute-done.11
  281.2 1.5 collective-permute-done.18
  283.7 1.5 collective-permute-start.12
  285.8 2.9 collective-permute-done.12
  288.8 1.5 collective-permute-done.19
  291.3 1.5 collective-permute-start.13
  293.4 2.9 collective-permute-done.13
  296.3 2.6 collective-permute-done.20
  300.6 1.4 collective-permute-start.21
  302.0 3.5 collective-permute-done.14
  307.4 1.5 collective-permute-start.22
  308.9 2.9 collective-permute-done.15
  314.0 1.5 collective-permute-start.23
  315.5 2.9 collective-permute-done.16
  321.0 15.9 %all-gather.8.cloned.1.call-done = bf16[256,2048]{1,0:T(8,128)(2,1)} async-done(((bf16[256,512]{1,0:T(8,128)(2,1)}), bf16[256,2048]{1,0:T(8,128)(2,1)}) %all-gather.8.cloned.1.call-update) | async-done | bytes 1048592 | tf_op jit(solution)/shard_map/all_gather | solution.py:299
  336.9 5.0 %fusion.33 = f32[256,1536]{0,1:T(8,128)S(1)} fusion(bf16[256,2048]{1,0:T(8,128)(2,1)} %all-gather.8.cloned.1.call-done, bf16[2048,1536]{0,1:T(8,128)(2,1)} %bitcast.153), kind=kOutput, calls=%fused_computation.117 | convolution fusion | flops 1610612736 | bytes 8912896 | tf_op jit(solution)/shard_map/dot_general | solution.py:298
  343.2 6.0 %all-reduce = (f32[256]{0:T(256)S(1)}, f32[256]{0:T(256)S(1)}, f32[256]{0:T(256)S(1)}) all-reduce(f32[256]{0:T(256)S(1)} %get-tuple-element.25, f32[256]{0:T(256)S(1)} %get-tuple-element.54, f32[256]{0:T(256)S(1)} %get-tuple-element.24), channel_id=1, replica_groups=mesh['seq'=8,'tp'=4] {'tp'}, use_global_device_ids=true, to_apply=%region_7.8 | all-reduce | flops 768 | bytes 6144 | tf_op jit(solution)/shard_map/psum | solution.py:305
  349.3 1.6 fusion.7
  (101 shorter events, 26.6 us)
Async XLA Ops:
  7.2 51.6 %copy-start = (bf16[512,2048]{1,0:T(8,128)(2,1)S(1)}, bf16[512,2048]{1,0:T(8,128)(2,1)}, u32[]{:S(2)}) copy-start(bf16[512,2048]{1,0:T(8,128)(2,1)} %param.24) | copy-start | bytes 6291460
  7.2 78.7 %reduce-scatter.2.cloned.1.call-start = ((), (), s32[]{:S(2)}) async-start(), calls=%async_computation.1 | async-start | bytes 1310720 | tf_op jit(solution)/shard_map/reduce_scatter | solution.py:279
  10.1 38.6 %collective-permute-start = (bf16[2,256,512]{2,1,0:T(8,128)(2,1)}, bf16[2,256,512]{2,1,0:T(8,128)(2,1)}, u32[]{:S(2)}, u32[]{:S(2)}) collective-permute-start(bf16[2,256,512]{2,1,0:T(8,128)(2,1)} %get-tuple-element.48), channel_id=1, source_target_pairs={{0,1},{1,2},{2,3},{3,0},{4,5},{5,6},{6,7},{7,4},{8,9},{9,10},{10,1... | collective-permute-start | bytes 1572872 | tf_op jit(solution)/shard_map/ppermute | solution.py:252
  10.6 38.1 %collective-permute-start.2 = (bf16[2,256,512]{2,1,0:T(8,128)(2,1)}, bf16[2,256,512]{2,1,0:T(8,128)(2,1)}, u32[]{:S(2)}, u32[]{:S(2)}) collective-permute-start(bf16[2,256,512]{2,1,0:T(8,128)(2,1)} %get-tuple-element.49), channel_id=1, source_target_pairs={{0,3},{1,0},{2,1},{3,2},{4,7},{5,4},{6,5},{7,6},{8,11},{9,8},{10,9... | collective-permute-start | bytes 1572872 | tf_op jit(solution)/shard_map/ppermute | solution.py:252
  12.5 36.2 %collective-permute-start.1 = (bf16[2,256,512]{2,1,0:T(8,128)(2,1)S(1)}, bf16[2,256,512]{2,1,0:T(8,128)(2,1)}, u32[]{:S(2)}, u32[]{:S(2)}) collective-permute-start(bf16[2,256,512]{2,1,0:T(8,128)(2,1)S(1)} %get-tuple-element.50), channel_id=1, source_target_pairs={{0,2},{1,3},{2,0},{3,1},{4,6},{5,7},{6,4},{7,5},{8,10},{9,11},{10,... | collective-permute-start | bytes 1572872 | tf_op jit(solution)/shard_map/ppermute | solution.py:252
  22.5 8.9 %copy-start.15 = (s32[8]{0:T(128)S(1)}, s32[8]{0:T(128)}, u32[]{:S(2)}) copy-start(s32[8]{0:T(128)} %param.23) | copy-start | bytes 100
  57.2 1.6 copy-start.8
  58.8 1.8 copy-start.9
  58.8 1.8 copy-start.10
  58.8 27.1 %copy-start.4 = (bf16[256,512]{1,0:T(8,128)(2,1)S(1)}, bf16[256,512]{1,0:T(8,128)(2,1)}, u32[]{:S(2)}) copy-start(bf16[256,512]{1,0:T(8,128)(2,1)} %param.17) | copy-start | bytes 786436
  58.8 34.0 %copy-start.11 = (f32[512]{0:T(512)S(1)}, f32[512]{0:T(512)}, u32[]{:S(2)}) copy-start(f32[512]{0:T(512)} %param.25) | copy-start | bytes 6148
  60.5 125.6 %all-gather.4.cloned.1.call-start = ((), (), s32[]{:S(2)}) async-start(), calls=%async_computation.2 | async-start | bytes 10485760 | tf_op jit(solution)/shard_map/all_gather | solution.py:124
  93.9 8.4 %collective-permute-start.6 = (bf16[272,512]{1,0:T(8,128)(2,1)S(1)}, bf16[272,512]{1,0:T(8,128)(2,1)S(1)}, u32[]{:S(2)}, u32[]{:S(2)}) collective-permute-start(bf16[272,512]{1,0:T(8,128)(2,1)S(1)} %pad_maximum_fusion.1), channel_id=1, source_target_pairs={{0,8},{8,16},{16,24},{24,28},{28,20},{20,12},{12,4},{4,0},{1,9},{9... | collective-permute-start | bytes 835592 | tf_op jit(solution)/shard_map/ppermute | solution.py:150
  95.6 8.1 %collective-permute-start.3 = (bf16[272,512]{1,0:T(8,128)(2,1)S(1)}, bf16[272,512]{1,0:T(8,128)(2,1)S(1)}, u32[]{:S(2)}, u32[]{:S(2)}) collective-permute-start(bf16[272,512]{1,0:T(8,128)(2,1)S(1)} %pad_maximum_fusion.1), channel_id=1, source_target_pairs={{0,4},{8,0},{16,8},{24,16},{28,24},{20,28},{12,20},{4,12},{1,5},{9... | collective-permute-start | bytes 835592 | tf_op jit(solution)/shard_map/ppermute | solution.py:154
  102.3 7.5 %collective-permute-start.7 = (bf16[272,512]{1,0:T(8,128)(2,1)S(1)}, bf16[272,512]{1,0:T(8,128)(2,1)S(1)}, u32[]{:S(2)}, u32[]{:S(2)}) collective-permute-start(bf16[272,512]{1,0:T(8,128)(2,1)S(1)} %collective-permute-done.6), channel_id=1, source_target_pairs={{0,8},{8,16},{16,24},{24,28},{28,20},{20,12},{12,4},{4,0},{1,9},{9... | collective-permute-start | bytes 835592 | tf_op jit(solution)/shard_map/ppermute | solution.py:150
  103.7 7.2 %collective-permute-start.4 = (bf16[272,512]{1,0:T(8,128)(2,1)S(1)}, bf16[272,512]{1,0:T(8,128)(2,1)S(1)}, u32[]{:S(2)}, u32[]{:S(2)}) collective-permute-start(bf16[272,512]{1,0:T(8,128)(2,1)S(1)} %collective-permute-done.3), channel_id=1, source_target_pairs={{0,4},{8,0},{16,8},{24,16},{28,24},{20,28},{12,20},{4,12},{1,5},{9... | collective-permute-start | bytes 835592 | tf_op jit(solution)/shard_map/ppermute | solution.py:154
  109.7 7.0 %collective-permute-start.8 = (bf16[272,512]{1,0:T(8,128)(2,1)S(1)}, bf16[272,512]{1,0:T(8,128)(2,1)S(1)}, u32[]{:S(2)}, u32[]{:S(2)}) collective-permute-start(bf16[272,512]{1,0:T(8,128)(2,1)S(1)} %collective-permute-done.7), channel_id=1, source_target_pairs={{0,8},{8,16},{16,24},{24,28},{28,20},{20,12},{12,4},{4,0},{1,9},{9... | collective-permute-start | bytes 835592 | tf_op jit(solution)/shard_map/ppermute | solution.py:150
  111.0 7.3 %collective-permute-start.5 = (bf16[272,512]{1,0:T(8,128)(2,1)S(1)}, bf16[272,512]{1,0:T(8,128)(2,1)S(1)}, u32[]{:S(2)}, u32[]{:S(2)}) collective-permute-start(bf16[272,512]{1,0:T(8,128)(2,1)S(1)} %collective-permute-done.4), channel_id=1, source_target_pairs={{0,4},{8,0},{16,8},{24,16},{28,24},{20,28},{12,20},{4,12},{1,5},{9... | collective-permute-start | bytes 835592 | tf_op jit(solution)/shard_map/ppermute | solution.py:154
  116.8 6.5 %collective-permute-start.9 = (bf16[272,512]{1,0:T(8,128)(2,1)S(1)}, bf16[272,512]{1,0:T(8,128)(2,1)S(1)}, u32[]{:S(2)}, u32[]{:S(2)}) collective-permute-start(bf16[272,512]{1,0:T(8,128)(2,1)S(1)} %collective-permute-done.8), channel_id=1, source_target_pairs={{0,8},{8,16},{16,24},{24,28},{28,20},{20,12},{12,4},{4,0},{1,9},{9... | collective-permute-start | bytes 835592 | tf_op jit(solution)/shard_map/ppermute | solution.py:150
  123.5 1.4 copy-start.3
  126.5 133.3 %all-gather.6.cloned.1.call-start = ((), (), s32[]{:S(2)}) async-start(), calls=%async_computation.3 | async-start | bytes 10485760 | tf_op jit(solution)/shard_map/all_gather | solution.py:129
  198.7 61.1 %copy-start.7 = (bf16[2,4,256,512]{3,2,1,0:T(8,128)(2,1)S(1)}, bf16[2,4,256,512]{3,2,1,0:T(8,128)(2,1)}, u32[]{:S(2)}) copy-start(bf16[2,4,256,512]{3,2,1,0:T(8,128)(2,1)} %copy.51) | copy-start | bytes 6291460
  201.3 135.6 %all-gather.8.cloned.1.call-start = ((), (), s32[]{:S(2)}) async-start(), calls=%async_computation.4 | async-start | bytes 1310720 | tf_op jit(solution)/shard_map/all_gather | solution.py:299
  268.2 7.0 %copy-start.6 = (bf16[2048,512]{1,0:T(8,128)(2,1)}, bf16[2048,512]{1,0:T(8,128)(2,1)S(1)}, u32[]{:S(2)}) copy-start(bf16[2048,512]{1,0:T(8,128)(2,1)S(1)} %bitcast_convert_fusion) | copy-start | bytes 6291460
  268.2 5.7 %collective-permute-start.10 = (bf16[256,256]{1,0:T(8,128)(2,1)S(1)}, bf16[256,256]{1,0:T(8,128)(2,1)S(1)}, u32[]{:S(2)}, u32[]{:S(2)}) collective-permute-start(bf16[256,256]{1,0:T(8,128)(2,1)S(1)} %get-tuple-element.45), channel_id=1, source_target_pairs={{0,8},{8,16},{16,24},{24,28},{28,20},{20,12},{12,4},{4,0},{1,9},{9... | collective-permute-start | bytes 393224 | tf_op jit(solution)/shard_map/ppermute | solution.py:170
  269.8 5.4 %collective-permute-start.17 = (bf16[256,256]{1,0:T(8,128)(2,1)S(1)}, bf16[256,256]{1,0:T(8,128)(2,1)S(1)}, u32[]{:S(2)}, u32[]{:S(2)}) collective-permute-start(bf16[256,256]{1,0:T(8,128)(2,1)S(1)} %get-tuple-element.46), channel_id=1, source_target_pairs={{0,4},{8,0},{16,8},{24,16},{28,24},{20,28},{12,20},{4,12},{1,5},{9... | collective-permute-start | bytes 393224 | tf_op jit(solution)/shard_map/ppermute | solution.py:170
  276.2 5.0 %collective-permute-start.11 = (bf16[256,256]{1,0:T(8,128)(2,1)S(1)}, bf16[256,256]{1,0:T(8,128)(2,1)S(1)}, u32[]{:S(2)}, u32[]{:S(2)}) collective-permute-start(bf16[256,256]{1,0:T(8,128)(2,1)S(1)} %get-tuple-element.43), channel_id=1, source_target_pairs={{0,8},{8,16},{16,24},{24,28},{28,20},{20,12},{12,4},{4,0},{1,9},{9... | collective-permute-start | bytes 393224 | tf_op jit(solution)/shard_map/ppermute | solution.py:170
  277.7 5.0 %collective-permute-start.18 = (bf16[256,256]{1,0:T(8,128)(2,1)S(1)}, bf16[256,256]{1,0:T(8,128)(2,1)S(1)}, u32[]{:S(2)}, u32[]{:S(2)}) collective-permute-start(bf16[256,256]{1,0:T(8,128)(2,1)S(1)} %get-tuple-element.44), channel_id=1, source_target_pairs={{0,4},{8,0},{16,8},{24,16},{28,24},{20,28},{12,20},{4,12},{1,5},{9... | collective-permute-start | bytes 393224 | tf_op jit(solution)/shard_map/ppermute | solution.py:170
  283.7 36.3 %copy-start.5 = (bf16[256,512]{1,0:T(8,128)(2,1)S(1)}, bf16[256,512]{1,0:T(8,128)(2,1)}, u32[]{:S(2)}) copy-start(bf16[256,512]{1,0:T(8,128)(2,1)} %reduce-scatter.2.cloned.1.call-done) | copy-start | bytes 786436
  283.7 36.3 %copy-start.12 = (f32[512]{0:T(512)S(1)}, f32[512]{0:T(512)}, u32[]{:S(2)}) copy-start(f32[512]{0:T(512)} %param.30) | copy-start | bytes 6148
  283.7 5.0 %collective-permute-start.12 = (bf16[256,256]{1,0:T(8,128)(2,1)S(1)}, bf16[256,256]{1,0:T(8,128)(2,1)S(1)}, u32[]{:S(2)}, u32[]{:S(2)}) collective-permute-start(bf16[256,256]{1,0:T(8,128)(2,1)S(1)} %get-tuple-element.41), channel_id=1, source_target_pairs={{0,8},{8,16},{16,24},{24,28},{28,20},{20,12},{12,4},{4,0},{1,9},{9... | collective-permute-start | bytes 393224 | tf_op jit(solution)/shard_map/ppermute | solution.py:170
  285.3 5.0 %collective-permute-start.19 = (bf16[256,256]{1,0:T(8,128)(2,1)S(1)}, bf16[256,256]{1,0:T(8,128)(2,1)S(1)}, u32[]{:S(2)}, u32[]{:S(2)}) collective-permute-start(bf16[256,256]{1,0:T(8,128)(2,1)S(1)} %get-tuple-element.42), channel_id=1, source_target_pairs={{0,4},{8,0},{16,8},{24,16},{28,24},{20,28},{12,20},{4,12},{1,5},{9... | collective-permute-start | bytes 393224 | tf_op jit(solution)/shard_map/ppermute | solution.py:170
  291.3 5.0 %collective-permute-start.13 = (bf16[256,256]{1,0:T(8,128)(2,1)S(1)}, bf16[256,256]{1,0:T(8,128)(2,1)S(1)}, u32[]{:S(2)}, u32[]{:S(2)}) collective-permute-start(bf16[256,256]{1,0:T(8,128)(2,1)S(1)} %get-tuple-element.39), channel_id=1, source_target_pairs={{0,8},{8,16},{16,24},{24,28},{28,20},{20,12},{12,4},{4,0},{1,9},{9... | collective-permute-start | bytes 393224 | tf_op jit(solution)/shard_map/ppermute | solution.py:170
  292.8 6.1 %collective-permute-start.20 = (bf16[256,256]{1,0:T(8,128)(2,1)S(1)}, bf16[256,256]{1,0:T(8,128)(2,1)S(1)}, u32[]{:S(2)}, u32[]{:S(2)}) collective-permute-start(bf16[256,256]{1,0:T(8,128)(2,1)S(1)} %get-tuple-element.40), channel_id=1, source_target_pairs={{0,4},{8,0},{16,8},{24,16},{28,24},{20,28},{12,20},{4,12},{1,5},{9... | collective-permute-start | bytes 393224 | tf_op jit(solution)/shard_map/ppermute | solution.py:170
  299.9 5.6 %collective-permute-start.14 = (bf16[256,256]{1,0:T(8,128)(2,1)S(1)}, bf16[256,256]{1,0:T(8,128)(2,1)S(1)}, u32[]{:S(2)}, u32[]{:S(2)}) collective-permute-start(bf16[256,256]{1,0:T(8,128)(2,1)S(1)} %get-tuple-element.37), channel_id=1, source_target_pairs={{0,8},{8,16},{16,24},{24,28},{28,20},{20,12},{12,4},{4,0},{1,9},{9... | collective-permute-start | bytes 393224 | tf_op jit(solution)/shard_map/ppermute | solution.py:170
  300.6 5.2 %collective-permute-start.21 = (bf16[256,256]{1,0:T(8,128)(2,1)S(1)}, bf16[256,256]{1,0:T(8,128)(2,1)S(1)}, u32[]{:S(2)}, u32[]{:S(2)}) collective-permute-start(bf16[256,256]{1,0:T(8,128)(2,1)S(1)} %get-tuple-element.38), channel_id=1, source_target_pairs={{0,4},{8,0},{16,8},{24,16},{28,24},{20,28},{12,20},{4,12},{1,5},{9... | collective-permute-start | bytes 393224 | tf_op jit(solution)/shard_map/ppermute | solution.py:170
  306.8 5.0 %collective-permute-start.15 = (bf16[256,256]{1,0:T(8,128)(2,1)S(1)}, bf16[256,256]{1,0:T(8,128)(2,1)S(1)}, u32[]{:S(2)}, u32[]{:S(2)}) collective-permute-start(bf16[256,256]{1,0:T(8,128)(2,1)S(1)} %get-tuple-element.35), channel_id=1, source_target_pairs={{0,8},{8,16},{16,24},{24,28},{28,20},{20,12},{12,4},{4,0},{1,9},{9... | collective-permute-start | bytes 393224 | tf_op jit(solution)/shard_map/ppermute | solution.py:170
  307.4 5.0 %collective-permute-start.22 = (bf16[256,256]{1,0:T(8,128)(2,1)S(1)}, bf16[256,256]{1,0:T(8,128)(2,1)S(1)}, u32[]{:S(2)}, u32[]{:S(2)}) collective-permute-start(bf16[256,256]{1,0:T(8,128)(2,1)S(1)} %get-tuple-element.36), channel_id=1, source_target_pairs={{0,4},{8,0},{16,8},{24,16},{28,24},{20,28},{12,20},{4,12},{1,5},{9... | collective-permute-start | bytes 393224 | tf_op jit(solution)/shard_map/ppermute | solution.py:170
  313.4 5.0 %collective-permute-start.16 = (bf16[256,256]{1,0:T(8,128)(2,1)S(1)}, bf16[256,256]{1,0:T(8,128)(2,1)S(1)}, u32[]{:S(2)}, u32[]{:S(2)}) collective-permute-start(bf16[256,256]{1,0:T(8,128)(2,1)S(1)} %get-tuple-element.33), channel_id=1, source_target_pairs={{0,8},{8,16},{16,24},{24,28},{28,20},{20,12},{12,4},{4,0},{1,9},{9... | collective-permute-start | bytes 393224 | tf_op jit(solution)/shard_map/ppermute | solution.py:170
  314.0 5.0 %collective-permute-start.23 = (bf16[256,256]{1,0:T(8,128)(2,1)S(1)}, bf16[256,256]{1,0:T(8,128)(2,1)S(1)}, u32[]{:S(2)}, u32[]{:S(2)}) collective-permute-start(bf16[256,256]{1,0:T(8,128)(2,1)S(1)} %get-tuple-element.34), channel_id=1, source_target_pairs={{0,4},{8,0},{16,8},{24,16},{28,24},{20,28},{12,20},{4,12},{1,5},{9... | collective-permute-start | bytes 393224 | tf_op jit(solution)/shard_map/ppermute | solution.py:170
  321.0 28.3 %copy-start.13 = (f32[512]{0:T(512)S(1)}, f32[512]{0:T(512)}, u32[]{:S(2)}) copy-start(f32[512]{0:T(512)} %param.33) | copy-start | bytes 6148
  321.0 28.3 %copy-start.14 = (f32[512]{0:T(512)S(1)}, f32[512]{0:T(512)}, u32[]{:S(2)}) copy-start(f32[512]{0:T(512)} %param.32) | copy-start | bytes 6148
  341.9 1.2 copy-start.2
  343.1 10.3 %copy-start.1 = (bf16[512,2048]{1,0:T(8,128)(2,1)S(1)}, bf16[512,2048]{1,0:T(8,128)(2,1)}, u32[]{:S(2)}) copy-start(bf16[512,2048]{1,0:T(8,128)(2,1)} %param.24) | copy-start | bytes 6291460
Sparse Core Ops, SparseCore 0:
  60.6 25.1 reduce-scatter.1
  126.6 59.4 all-gather.3
  201.4 58.2 all-gather.5
  321.1 15.7 all-gather.7

commit v9 on v8

--- a/solution.py
+++ b/solution.py
@@ -115,22 +115,35 @@
     info = jnp.concatenate([gate_hi, gate_lo], axis=0).reshape(-1, quarter)
     packed = jnp.concatenate([moe_in, info], axis=0)
     ring = ring_order(seq_count)
-    gathered = ring_all_gather(packed, here, ring)
-    rows_q = gathered[:, :tokens].reshape(seq_count * tokens, quarter)
-    info_all = gathered[:, tokens:].reshape(seq_count, 2, experts_all, tokens).astype(jnp.float32)
-    gate_all = info_all[:, 0] + info_all[:, 1]
-    gate_local = lax.dynamic_slice_in_dim(gate_all, here * local_experts, local_experts, axis=1)
-    gate_local = jnp.transpose(gate_local, (1, 0, 2)).reshape(local_experts, seq_count * tokens)
-    rows = lax.all_gather(rows_q, "tp", axis=1, tiled=True)
-    projected = jnp.einsum("td,edf->etf", rows, expert_gate_up, preferred_element_type=jnp.float32)
-    activated = jax.nn.silu(projected[..., :hidden_quarter]) * projected[..., hidden_quarter:]
-    activated = activated.astype(jnp.bfloat16).astype(jnp.float32)
-    weighted = (activated * gate_local[:, :, None]).astype(jnp.bfloat16)
-    weighted = lax.all_gather(weighted, "tp", axis=2, tiled=True)
-    partial = jnp.einsum(
-        "etf,efd->td", weighted, down_full, preferred_element_type=jnp.float32
-    ).astype(jnp.bfloat16)
-    return ring_reduce_scatter(partial, ring)
+    offsets, blocks = ring_all_gather(packed, ring)
+    first = min(len(blocks), 5)
+    chunks = [(0, first), (first, len(blocks))] if first < len(blocks) else [(0, first)]
+    outputs = []
+    for begin, end in chunks:
+        gathered = jnp.stack(blocks[begin:end])
+        count = end - begin
+        rows_q = gathered[:, :tokens].reshape(count * tokens, quarter)
+        info_all = gathered[:, tokens:].reshape(count, 2, experts_all, tokens).astype(jnp.float32)
+        gate_all = info_all[:, 0] + info_all[:, 1]
+        gate_local = lax.dynamic_slice_in_dim(gate_all, here * local_experts, local_experts, axis=1)
+        gate_local = jnp.transpose(gate_local, (1, 0, 2)).reshape(local_experts, count * tokens)
+        rows = lax.all_gather(rows_q, "tp", axis=1, tiled=True)
+        projected = jnp.einsum("td,edf->etf", rows, expert_gate_up, preferred_element_type=jnp.float32)
+        activated = jax.nn.silu(projected[..., :hidden_quarter]) * projected[..., hidden_quarter:]
+        activated = activated.astype(jnp.bfloat16).astype(jnp.float32)
+        weighted = (activated * gate_local[:, :, None]).astype(jnp.bfloat16)
+        weighted = lax.all_gather(weighted, "tp", axis=2, tiled=True)
+        partial = jnp.einsum(
+            "etf,efd->td", weighted, down_full, preferred_element_type=jnp.float32
+        ).astype(jnp.bfloat16)
+        outputs.append(partial.reshape(count, tokens, -1))
+    by_offset = {}
+    index = 0
+    for part in outputs:
+        for i in range(part.shape[0]):
+            by_offset[offsets[index]] = part[i]
+            index += 1
+    return ring_reduce_scatter(by_offset, ring)
 
 
 def ring_order(count):
@@ -140,36 +153,35 @@
     return [2 * i for i in range(half)] + [2 * i + 1 for i in reversed(range(half))]
 
 
-def ring_all_gather(block, here, cycle):
+def ring_all_gather(block, cycle):
     count = len(cycle)
     forward = [(cycle[p], cycle[(p + 1) % count]) for p in range(count)]
     backward = [(cycle[p], cycle[(p - 1) % count]) for p in range(count)]
-    by_offset = [block] * count
-    ahead = block
+    offsets, blocks = [0], [block]
+    ahead, behind = block, block
     for step in range(1, count // 2 + 1):
         ahead = lax.ppermute(ahead, "seq", forward)
-        by_offset[(-step) % count] = ahead
-    behind = block
-    for step in range(1, count - count // 2):
-        behind = lax.ppermute(behind, "seq", backward)
-        by_offset[step] = behind
-    return jnp.stack(by_offset)
-
-
-def ring_reduce_scatter(partial, cycle):
+        offsets.append((-step) % count)
+        blocks.append(ahead)
+        if step < count - count // 2:
+            behind = lax.ppermute(behind, "seq", backward)
+            offsets.append(step)
+            blocks.append(behind)
+    return offsets, blocks
+
+
+def ring_reduce_scatter(by_offset, cycle):
     count = len(cycle)
-    tokens = partial.shape[0] // count
-    width = partial.shape[1]
-    blocks = partial.reshape(count, tokens, width)
+    width = by_offset[0].shape[1]
     halves = []
     for direction in (1, -1):
         cols = slice(0, width // 2) if direction == 1 else slice(width // 2, width)
         pairs = [(cycle[p], cycle[(p + direction) % count]) for p in range(count)]
-        acc = blocks[(-direction) % count, :, cols].astype(jnp.float32)
+        acc = by_offset[(-direction) % count][:, cols].astype(jnp.float32)
         for step in range(count - 1):
             received = lax.ppermute(acc.astype(jnp.bfloat16), "seq", pairs)
             offset = (-direction * (step + 2)) % count
-            acc = received.astype(jnp.float32) + blocks[offset, :, cols].astype(jnp.float32)
+            acc = received.astype(jnp.float32) + by_offset[offset][:, cols].astype(jnp.float32)
         halves.append(acc)
     return jnp.concatenate(halves, axis=1)
 

time: 360 us -> 330 us (0.917)
  waiting for transfers between devices: 210 us -> 183 us
  other arithmetic: 20.5 us -> 14.6 us
    all_gather x1 -> x2, waiting for transfers between devices: 58.3 us -> 42.3 us  [dense_experts(): rows = lax.all_gather(rows_q, 'tp', axis=1, tiled=True)]
    all_gather x1 -> x2, waiting for transfers between devices: 58.4 us -> 49.8 us  [dense_experts(): weighted = lax.all_gather(weighted, 'tp', axis=2, tiled=True)]
    convert_element_type x6, other arithmetic: 6.19 us -> 0.42 us  [ring_reduce_scatter(): received = lax.ppermute(acc.astype(jnp.bfloat16), 'seq', pairs)]
    dot_general x1 -> x2, matrix products: 12.6 us -> 15.2 us  [dense_experts(): jnp.einsum('td,edf->etf', rows, expert_gate_up, preferred_element_type=jn...]
    dot_general x1 -> x2, matrix products: 8.44 us -> 9.09 us  [dense_experts(): jnp.einsum('etf,efd->td', weighted, down_full, preferred_element_type=jnp...]
  transfers between devices with their start and end apart: 28 -> 30, of which waited for: 22 -> 23; matrix products, arithmetic and copies ran while one was open for 5% -> 14% of each run, Pallas kernels for 5% -> 5%
where the time goes in v9:
time: 330 us
  waiting for transfers between devices  183 us (55%)
  local copies, waits for them, and re-layouts  31.3 us (9%)
  matrix products  31 us (9%)
  starting transfers between devices  26.1 us (8%)
  Pallas kernels  16.8 us (5%)
  other arithmetic  14.6 us (4%)
  between operations  14.6 us (4%)
  blocking collectives  11.8 us (4%)
    all_gather x2, waiting for transfers between devices, dense_experts(): weighted = lax.all_gather(weighted, 'tp', axis=2, tiled=True)  49.8 us
    all_gather x2, waiting for transfers between devices, dense_experts(): rows = lax.all_gather(rows_q, 'tp', axis=1, tiled=True)  42.3 us
    ppermute x14, waiting for transfers between devices, ring_reduce_scatter(): received = lax.ppermute(acc.astype(jnp.bfloat16), 'seq', pairs)  27.6 us
    reduce_scatter x1, waiting for transfers between devices, body(): lax.psum_scatter(attn_term.astype(jnp.bfloat16), 'tp', scatter_dimension=...  26.2 us
    ppermute x4, waiting for transfers between devices, ring_all_gather(): ahead = lax.ppermute(ahead, 'seq', forward)  22.3 us
    pallas_call x1, Pallas kernels, flash_attention(): pl.pallas_call(kernel, grid_spec=grid_spec, out_shape=jax.ShapeDtypeStruc...  16.8 us
    dot_general x2, matrix products, dense_experts(): jnp.einsum('td,edf->etf', rows, expert_gate_up, preferred_element_type=jn...  15.2 us
    ppermute x14, starting transfers between devices, ring_reduce_scatter(): received = lax.ppermute(acc.astype(jnp.bfloat16), 'seq', pairs)  14.7 us
  transfers between devices with their start and end apart: 30, of which 23 were waited for; matrix products, arithmetic and copies ran while one was open for 14% of the time, Pallas kernels for 5%

profile of v9, /device:TPU:0, one launch (start us, length us, event | category | flops | bytes accessed | tf_op | source)
XLA Modules:
  0.0 329.5 jit_solution(11916643331837701559)
XLA Ops:
  7.3 2.8 dynamic-slice_bitcast_fusion
  10.1 2.4 collective-permute-start.2
  13.3 7.6 %reshape.133 = bf16[2,2048,512]{2,1,0:T(8,128)(2,1)} reshape(bf16[2,2048,2,256]{3,2,1,0:T(2,128)(2,1)} %param.28) | data formatting | bytes 8388608 | tf_op jit(solution)/shard_map/reshape | solution.py:268
  20.9 8.9 %copy.68 = bf16[2048,3,512]{0,2,1:T(8,128)(2,1)} copy(bf16[2048,3,512]{2,0,1:T(8,128)(2,1)} %param.31) | data formatting | bytes 12582912 | tf_op args[14]
  30.4 16.8 %shard_map.192 = bf16[256,512]{1,0:T(8,128)(2,1)} custom-call(s32[1]{0:T(128)} %dynamic_slice.26.len_ref, bf16[256,512]{1,0:T(8,128)(2,1)} %q_ref.1, bf16[4096,512]{1,0:T(8,128)(2,1)} %bitcast.107, bf16[4096,512]{1,0:T(8,128)(2,1)} %bitcast.108, bf16[256,512]{1,0:T(8,128)(2,1)} %nk_ref.1, bf16[256,512]{1,0:T(8,128)(2,1)} %nv_ref.1), custom_call_target="tpu_custom_call" | custom-call | tf_op jit(solution)/shard_map/pallas_call | solution.py:94
  47.2 3.0 pad_maximum_fusion
  50.2 3.6 %gather_fusion = bf16[4,2,256,512]{3,2,1,0:T(8,128)(2,1)} fusion(bf16[4,2,256,512]{3,2,1,0:T(8,128)(2,1)} %pad_maximum_fusion, s32[1024]{0:T(1024)S(1)} %pad_clamp_fusion), kind=kCustom, calls=%fused_computation | custom fusion | bytes 4194320 | tf_op jit(solution)/shard_map/jit(_take)/gather | solution.py:266
  53.8 1.9 select_bitcast_fusion
  55.7 1.6 copy.67
  57.3 1.7 convolution_convert_fusion
  59.2 26.2 %reduce-scatter.2.cloned.1.call-done = bf16[256,512]{1,0:T(8,128)(2,1)} async-done(((bf16[256,2048]{1,0:T(8,128)(2,1)}), bf16[256,512]{1,0:T(8,128)(2,1)}) %reduce-scatter.2.cloned.1.call-update) | async-done | bytes 262160 | tf_op jit(solution)/shard_map/reduce_scatter | solution.py:291
  86.5 5.8 %psum.28 = f32[256]{0:T(256)S(1)} all-reduce(f32[256]{0:T(256)S(1)} %multiply_reduce_fusion.3), channel_id=1, replica_groups=mesh['seq'=8,'tp'=4] {'tp'}, use_global_device_ids=true, to_apply=%region_2.3 | all-reduce | flops 256 | bytes 2048 | tf_op jit(solution)/shard_map/psum | solution.py:294
  93.3 1.7 collective-permute-start.3
  95.5 6.3 %collective-permute-done.3 = bf16[272,512]{1,0:T(8,128)(2,1)S(1)} collective-permute-done((bf16[272,512]{1,0:T(8,128)(2,1)S(1)}, bf16[272,512]{1,0:T(8,128)(2,1)S(1)}, u32[]{:S(2)}, u32[]{:S(2)}) %collective-permute-start.3) | collective-permute-done | bytes 278560 | tf_op jit(solution)/shard_map/ppermute | solution.py:163
  103.9 5.4 %collective-permute-done.5 = bf16[272,512]{1,0:T(8,128)(2,1)S(1)} collective-permute-done((bf16[272,512]{1,0:T(8,128)(2,1)S(1)}, bf16[272,512]{1,0:T(8,128)(2,1)S(1)}, u32[]{:S(2)}, u32[]{:S(2)}) %collective-permute-start.5) | collective-permute-done | bytes 278560 | tf_op jit(solution)/shard_map/ppermute | solution.py:163
  111.6 1.6 collective-permute-start.9
  113.7 5.6 %collective-permute-done.9 = bf16[272,512]{1,0:T(8,128)(2,1)S(1)} collective-permute-done((bf16[272,512]{1,0:T(8,128)(2,1)S(1)}, bf16[272,512]{1,0:T(8,128)(2,1)S(1)}, u32[]{:S(2)}, u32[]{:S(2)}) %collective-permute-start.9) | collective-permute-done | bytes 278560 | tf_op jit(solution)/shard_map/ppermute | solution.py:163
  119.3 1.5 collective-permute-start.11
  120.8 5.0 %collective-permute-done.11 = bf16[272,512]{1,0:T(8,128)(2,1)S(1)} collective-permute-done((bf16[272,512]{1,0:T(8,128)(2,1)S(1)}, bf16[272,512]{1,0:T(8,128)(2,1)S(1)}, u32[]{:S(2)}, u32[]{:S(2)}) %collective-permute-start.11) | collective-permute-done | bytes 278560 | tf_op jit(solution)/shard_map/ppermute | solution.py:163
  128.2 23.2 %all-gather.6.cloned.1.call-done = bf16[1280,2048]{1,0:T(8,128)(2,1)} async-done(((bf16[1280,512]{1,0:T(8,128)(2,1)}), bf16[1280,2048]{1,0:T(8,128)(2,1)}) %all-gather.6.cloned.1.call-update) | async-done | bytes 5242896 | tf_op jit(solution)/shard_map/all_gather | solution.py:130
  151.3 9.0 %fusion.2 = f32[2,1280,512]{1,2,0:T(8,128)S(1)} fusion(bf16[2,2048,512]{2,1,0:T(8,128)(2,1)} %reshape.133, bf16[1280,2048]{1,0:T(8,128)(2,1)} %all-gather.6.cloned.1.call-done), kind=kOutput, calls=%fused_computation.3 | convolution fusion | flops 5368709120 | bytes 14680064 | tf_op jit(solution)/shard_map/td,edf->etf/dot_general | solution.py:131
  160.3 1.9 multiply_convert_fusion
  162.4 19.1 %all-gather.10.cloned.1.call-done = bf16[768,2048]{1,0:T(8,128)(2,1)} async-done(((bf16[768,512]{1,0:T(8,128)(2,1)}), bf16[768,2048]{1,0:T(8,128)(2,1)}) %all-gather.10.cloned.1.call-update) | async-done | bytes 3145744 | tf_op jit(solution)/shard_map/all_gather | solution.py:130
  181.6 6.2 %fusion.9 = f32[2,768,512]{1,2,0:T(8,128)S(1)} fusion(bf16[2,2048,512]{2,1,0:T(8,128)(2,1)} %reshape.133, bf16[768,2048]{1,0:T(8,128)(2,1)} %all-gather.10.cloned.1.call-done), kind=kOutput, calls=%fused_computation.14 | convolution fusion | flops 3221225472 | bytes 10485760 | tf_op jit(solution)/shard_map/td,edf->etf/dot_general | solution.py:131
  189.2 34.3 %all-gather.8.cloned.1.call-done = bf16[2,1280,1024]{1,2,0:T(8,128)(2,1)} async-done(((bf16[2,1280,256]{1,2,0:T(8,128)(2,1)}), bf16[2,1280,1024]{1,2,0:T(8,128)(2,1)}) %all-gather.8.cloned.1.call-update) | async-done | bytes 5242896 | tf_op jit(solution)/shard_map/all_gather | solution.py:135
  223.5 5.4 %fusion.7 = bf16[1280,512]{1,0:T(8,128)(2,1)S(1)} fusion(bf16[2,1280,1024]{1,2,0:T(8,128)(2,1)} %all-gather.8.cloned.1.call-done, bf16[2,1024,512]{2,1,0:T(8,128)(2,1)S(1)} %bitcast.101), kind=kOutput, calls=%fused_computation.7 | convolution fusion | flops 2685009920 | bytes 8650752 | tf_op jit(solution)/shard_map/etf,efd->td/dot_general | solution.py:136
  229.0 1.5 collective-permute-start.7
  231.0 3.6 %collective-permute-done.7 = bf16[256,256]{1,0:T(8,128)(2,1)S(1)} collective-permute-done((bf16[256,256]{1,0:T(8,128)(2,1)S(1)}, bf16[256,256]{1,0:T(8,128)(2,1)S(1)}, u32[]{:S(2)}, u32[]{:S(2)}) %collective-permute-start.7) | collective-permute-done | bytes 131104 | tf_op jit(solution)/shard_map/ppermute | solution.py:182
  235.9 1.5 collective-permute-start.8
  238.0 15.5 %all-gather.12.cloned.1.call-done = bf16[2,768,1024]{1,2,0:T(8,128)(2,1)} async-done(((bf16[2,768,256]{1,2,0:T(8,128)(2,1)}), bf16[2,768,1024]{1,2,0:T(8,128)(2,1)}) %all-gather.12.cloned.1.call-update) | async-done | bytes 3145744 | tf_op jit(solution)/shard_map/all_gather | solution.py:135
  253.6 3.7 %bitcast_convert_fusion = bf16[768,512]{1,0:T(8,128)(2,1)S(1)} fusion(bf16[2,768,1024]{1,2,0:T(8,128)(2,1)} %all-gather.12.cloned.1.call-done, bf16[2,1024,512]{2,1,0:T(8,128)(2,1)S(1)} %bitcast.102), kind=kOutput, calls=%fused_computation.17 | convolution fusion | flops 1611005952 | bytes 6029312 | tf_op jit(solution)/shard_map/etf,efd->td/dot_general | solution.py:136
  257.4 1.5 collective-permute-start.12
  259.5 3.6 %collective-permute-done.12 = bf16[256,256]{1,0:T(8,128)(2,1)S(1)} collective-permute-done((bf16[256,256]{1,0:T(8,128)(2,1)S(1)}, bf16[256,256]{1,0:T(8,128)(2,1)S(1)}, u32[]{:S(2)}, u32[]{:S(2)}) %collective-permute-start.12) | collective-permute-done | bytes 131104 | tf_op jit(solution)/shard_map/ppermute | solution.py:182
  264.4 1.5 collective-permute-start.13
  266.5 2.9 collective-permute-done.13
  269.4 1.5 collective-permute-done.20
  271.0 1.5 collective-permute-start.14
  273.0 2.9 collective-permute-done.14
  276.0 1.5 collective-permute-done.21
  277.5 2.2 collective-permute-start.15
  279.8 3.5 %collective-permute-done.15 = bf16[256,256]{1,0:T(8,128)(2,1)S(1)} collective-permute-done((bf16[256,256]{1,0:T(8,128)(2,1)S(1)}, bf16[256,256]{1,0:T(8,128)(2,1)S(1)}, u32[]{:S(2)}, u32[]{:S(2)}) %collective-permute-start.15) | collective-permute-done | bytes 131104 | tf_op jit(solution)/shard_map/ppermute | solution.py:182
  283.3 2.1 collective-permute-done.22
  286.1 1.5 collective-permute-start.23
  287.5 2.9 collective-permute-done.16
  292.1 14.1 %all-gather.14.cloned.1.call-done = bf16[256,2048]{1,0:T(8,128)(2,1)} async-done(((bf16[256,512]{1,0:T(8,128)(2,1)}), bf16[256,2048]{1,0:T(8,128)(2,1)}) %all-gather.14.cloned.1.call-update) | async-done | bytes 1048592 | tf_op jit(solution)/shard_map/all_gather | solution.py:311
  306.2 5.0 %fusion.27 = f32[256,1536]{0,1:T(8,128)S(1)} fusion(bf16[256,2048]{1,0:T(8,128)(2,1)} %all-gather.14.cloned.1.call-done, bf16[2048,1536]{0,1:T(8,128)(2,1)} %bitcast.103), kind=kOutput, calls=%fused_computation.98 | convolution fusion | flops 1610612736 | bytes 8912896 | tf_op jit(solution)/shard_map/dot_general | solution.py:310
  312.5 6.0 %all-reduce = (f32[256]{0:T(256)S(1)}, f32[256]{0:T(256)S(1)}, f32[256]{0:T(256)S(1)}) all-reduce(f32[256]{0:T(256)S(1)} %get-tuple-element.25, f32[256]{0:T(256)S(1)} %get-tuple-element.48, f32[256]{0:T(256)S(1)} %get-tuple-element.24), channel_id=1, replica_groups=mesh['seq'=8,'tp'=4] {'tp'}, use_global_device_ids=true, to_apply=%region_7.8 | all-reduce | flops 768 | bytes 6144 | tf_op jit(solution)/shard_map/psum | solution.py:317
  318.6 1.6 fusion.14
  (113 shorter events, 24.6 us)
Async XLA Ops:
  7.2 50.1 %copy-start = (bf16[512,2048]{1,0:T(8,128)(2,1)S(1)}, bf16[512,2048]{1,0:T(8,128)(2,1)}, u32[]{:S(2)}) copy-start(bf16[512,2048]{1,0:T(8,128)(2,1)} %param.24) | copy-start | bytes 6291460
  7.2 78.2 %reduce-scatter.2.cloned.1.call-start = ((), (), s32[]{:S(2)}) async-start(), calls=%async_computation.1 | async-start | bytes 1310720 | tf_op jit(solution)/shard_map/reduce_scatter | solution.py:291
  10.1 37.1 %collective-permute-start.2 = (bf16[2,256,512]{2,1,0:T(8,128)(2,1)}, bf16[2,256,512]{2,1,0:T(8,128)(2,1)}, u32[]{:S(2)}, u32[]{:S(2)}) collective-permute-start(bf16[2,256,512]{2,1,0:T(8,128)(2,1)} %get-tuple-element.33), channel_id=1, source_target_pairs={{0,3},{1,0},{2,1},{3,2},{4,7},{5,4},{6,5},{7,6},{8,11},{9,8},{10,9... | collective-permute-start | bytes 1572872 | tf_op jit(solution)/shard_map/ppermute | solution.py:264
  12.5 34.7 %collective-permute-start.1 = (bf16[2,256,512]{2,1,0:T(8,128)(2,1)}, bf16[2,256,512]{2,1,0:T(8,128)(2,1)}, u32[]{:S(2)}, u32[]{:S(2)}) collective-permute-start(bf16[2,256,512]{2,1,0:T(8,128)(2,1)} %get-tuple-element.34), channel_id=1, source_target_pairs={{0,2},{1,3},{2,0},{3,1},{4,6},{5,7},{6,4},{7,5},{8,10},{9,11},{10,... | collective-permute-start | bytes 1572872 | tf_op jit(solution)/shard_map/ppermute | solution.py:264
  13.1 34.1 %collective-permute-start = (bf16[2,256,512]{2,1,0:T(8,128)(2,1)S(1)}, bf16[2,256,512]{2,1,0:T(8,128)(2,1)}, u32[]{:S(2)}, u32[]{:S(2)}) collective-permute-start(bf16[2,256,512]{2,1,0:T(8,128)(2,1)S(1)} %get-tuple-element.32), channel_id=1, source_target_pairs={{0,1},{1,2},{2,3},{3,0},{4,5},{5,6},{6,7},{7,4},{8,9},{9,10},{10,1... | collective-permute-start | bytes 1572872 | tf_op jit(solution)/shard_map/ppermute | solution.py:264
  20.9 8.9 %copy-start.16 = (s32[8]{0:T(128)S(1)}, s32[8]{0:T(128)}, u32[]{:S(2)}) copy-start(s32[8]{0:T(128)} %param.23) | copy-start | bytes 100
  55.7 1.6 copy-start.9
  57.3 1.8 copy-start.10
  57.3 1.8 copy-start.11
  57.3 28.1 %copy-start.4 = (bf16[256,512]{1,0:T(8,128)(2,1)S(1)}, bf16[256,512]{1,0:T(8,128)(2,1)}, u32[]{:S(2)}) copy-start(bf16[256,512]{1,0:T(8,128)(2,1)} %param.17) | copy-start | bytes 786436
  57.3 35.0 %copy-start.12 = (f32[512]{0:T(512)S(1)}, f32[512]{0:T(512)}, u32[]{:S(2)}) copy-start(f32[512]{0:T(512)} %param.25) | copy-start | bytes 6148
  59.0 92.3 %all-gather.6.cloned.1.call-start = ((), (), s32[]{:S(2)}) async-start(), calls=%async_computation.2 | async-start | bytes 6553600 | tf_op jit(solution)/shard_map/all_gather | solution.py:130
  93.3 8.4 %collective-permute-start.3 = (bf16[272,512]{1,0:T(8,128)(2,1)S(1)}, bf16[272,512]{1,0:T(8,128)(2,1)S(1)}, u32[]{:S(2)}, u32[]{:S(2)}) collective-permute-start(bf16[272,512]{1,0:T(8,128)(2,1)S(1)} %pad_maximum_fusion.2), channel_id=1, source_target_pairs={{0,8},{8,16},{16,24},{24,28},{28,20},{20,12},{12,4},{4,0},{1,9},{9... | collective-permute-start | bytes 835592 | tf_op jit(solution)/shard_map/ppermute | solution.py:163
  95.1 8.2 %collective-permute-start.4 = (bf16[272,512]{1,0:T(8,128)(2,1)S(1)}, bf16[272,512]{1,0:T(8,128)(2,1)S(1)}, u32[]{:S(2)}, u32[]{:S(2)}) collective-permute-start(bf16[272,512]{1,0:T(8,128)(2,1)S(1)} %pad_maximum_fusion.2), channel_id=1, source_target_pairs={{0,4},{8,0},{16,8},{24,16},{28,24},{20,28},{12,20},{4,12},{1,5},{9... | collective-permute-start | bytes 835592 | tf_op jit(solution)/shard_map/ppermute | solution.py:167
  101.8 7.5 %collective-permute-start.5 = (bf16[272,512]{1,0:T(8,128)(2,1)S(1)}, bf16[272,512]{1,0:T(8,128)(2,1)S(1)}, u32[]{:S(2)}, u32[]{:S(2)}) collective-permute-start(bf16[272,512]{1,0:T(8,128)(2,1)S(1)} %collective-permute-done.3), channel_id=1, source_target_pairs={{0,8},{8,16},{16,24},{24,28},{28,20},{20,12},{12,4},{4,0},{1,9},{9... | collective-permute-start | bytes 835592 | tf_op jit(solution)/shard_map/ppermute | solution.py:163
  103.2 7.0 %collective-permute-start.6 = (bf16[272,512]{1,0:T(8,128)(2,1)S(1)}, bf16[272,512]{1,0:T(8,128)(2,1)S(1)}, u32[]{:S(2)}, u32[]{:S(2)}) collective-permute-start(bf16[272,512]{1,0:T(8,128)(2,1)S(1)} %collective-permute-done.4), channel_id=1, source_target_pairs={{0,4},{8,0},{16,8},{24,16},{28,24},{20,28},{12,20},{4,12},{1,5},{9... | collective-permute-start | bytes 835592 | tf_op jit(solution)/shard_map/ppermute | solution.py:167
  110.3 15.6 %copy-start.6 = (bf16[5,272,512]{2,1,0:T(8,128)(2,1)}, bf16[5,272,512]{2,1,0:T(8,128)(2,1)S(1)}, u32[]{:S(2)}) copy-start(bf16[5,272,512]{2,1,0:T(8,128)(2,1)S(1)} %bitcast_dynamic-update-slice_fusion) | copy-start | bytes 4177924
  111.6 70.0 %all-gather.10.cloned.1.call-start = ((), (), s32[]{:S(2)}) async-start(), calls=%async_computation.4 | async-start | bytes 3932160 | tf_op jit(solution)/shard_map/all_gather | solution.py:130
  111.6 7.6 %collective-permute-start.9 = (bf16[272,512]{1,0:T(8,128)(2,1)S(1)}, bf16[272,512]{1,0:T(8,128)(2,1)S(1)}, u32[]{:S(2)}, u32[]{:S(2)}) collective-permute-start(bf16[272,512]{1,0:T(8,128)(2,1)S(1)} %collective-permute-done.5), channel_id=1, source_target_pairs={{0,8},{8,16},{16,24},{24,28},{28,20},{20,12},{12,4},{4,0},{1,9},{9... | collective-permute-start | bytes 835592 | tf_op jit(solution)/shard_map/ppermute | solution.py:163
  113.2 7.6 %collective-permute-start.10 = (bf16[272,512]{1,0:T(8,128)(2,1)S(1)}, bf16[272,512]{1,0:T(8,128)(2,1)S(1)}, u32[]{:S(2)}, u32[]{:S(2)}) collective-permute-start(bf16[272,512]{1,0:T(8,128)(2,1)S(1)} %collective-permute-done.6), channel_id=1, source_target_pairs={{0,4},{8,0},{16,8},{24,16},{28,24},{20,28},{12,20},{4,12},{1,5},{9... | collective-permute-start | bytes 835592 | tf_op jit(solution)/shard_map/ppermute | solution.py:167
  119.3 6.5 %collective-permute-start.11 = (bf16[272,512]{1,0:T(8,128)(2,1)S(1)}, bf16[272,512]{1,0:T(8,128)(2,1)S(1)}, u32[]{:S(2)}, u32[]{:S(2)}) collective-permute-start(bf16[272,512]{1,0:T(8,128)(2,1)S(1)} %collective-permute-done.9), channel_id=1, source_target_pairs={{0,8},{8,16},{16,24},{24,28},{28,20},{20,12},{12,4},{4,0},{1,9},{9... | collective-permute-start | bytes 835592 | tf_op jit(solution)/shard_map/ppermute | solution.py:163
  126.9 96.6 %all-gather.8.cloned.1.call-start = ((), (), s32[]{:S(2)}) async-start(), calls=%async_computation.3 | async-start | bytes 6553600 | tf_op jit(solution)/shard_map/all_gather | solution.py:135
  162.3 91.3 %all-gather.12.cloned.1.call-start = ((), (), s32[]{:S(2)}) async-start(), calls=%async_computation.5 | async-start | bytes 3932160 | tf_op jit(solution)/shard_map/all_gather | solution.py:135
  187.8 35.7 %copy-start.2 = (bf16[2,4,256,512]{3,2,1,0:T(8,128)(2,1)S(1)}, bf16[2,4,256,512]{3,2,1,0:T(8,128)(2,1)}, u32[]{:S(2)}) copy-start(bf16[2,4,256,512]{3,2,1,0:T(8,128)(2,1)} %copy.67) | copy-start | bytes 6291460
  189.2 117.0 %all-gather.14.cloned.1.call-start = ((), (), s32[]{:S(2)}) async-start(), calls=%async_computation.6 | async-start | bytes 1310720 | tf_op jit(solution)/shard_map/all_gather | solution.py:311
  228.9 7.0 %copy-start.7 = (bf16[1280,512]{1,0:T(8,128)(2,1)}, bf16[1280,512]{1,0:T(8,128)(2,1)S(1)}, u32[]{:S(2)}) copy-start(bf16[1280,512]{1,0:T(8,128)(2,1)S(1)} %fusion.7) | copy-start | bytes 3932164
  229.0 5.7 %collective-permute-start.7 = (bf16[256,256]{1,0:T(8,128)(2,1)S(1)}, bf16[256,256]{1,0:T(8,128)(2,1)S(1)}, u32[]{:S(2)}, u32[]{:S(2)}) collective-permute-start(bf16[256,256]{1,0:T(8,128)(2,1)S(1)} %get-tuple-element.46), channel_id=1, source_target_pairs={{0,8},{8,16},{16,24},{24,28},{28,20},{20,12},{12,4},{4,0},{1,9},{9... | collective-permute-start | bytes 393224 | tf_op jit(solution)/shard_map/ppermute | solution.py:182
  230.5 5.4 %collective-permute-start.17 = (bf16[256,256]{1,0:T(8,128)(2,1)S(1)}, bf16[256,256]{1,0:T(8,128)(2,1)S(1)}, u32[]{:S(2)}, u32[]{:S(2)}) collective-permute-start(bf16[256,256]{1,0:T(8,128)(2,1)S(1)} %get-tuple-element.47), channel_id=1, source_target_pairs={{0,4},{8,0},{16,8},{24,16},{28,24},{20,28},{12,20},{4,12},{1,5},{9... | collective-permute-start | bytes 393224 | tf_op jit(solution)/shard_map/ppermute | solution.py:182
  235.9 21.3 %collective-permute-start.8 = (bf16[256,256]{1,0:T(8,128)(2,1)S(1)}, bf16[256,256]{1,0:T(8,128)(2,1)S(1)}, u32[]{:S(2)}, u32[]{:S(2)}) collective-permute-start(bf16[256,256]{1,0:T(8,128)(2,1)S(1)} %get-tuple-element.44), channel_id=1, source_target_pairs={{0,8},{8,16},{16,24},{24,28},{28,20},{20,12},{12,4},{4,0},{1,9},{9... | collective-permute-start | bytes 393224 | tf_op jit(solution)/shard_map/ppermute | solution.py:182
  237.5 19.8 %collective-permute-start.18 = (bf16[256,256]{1,0:T(8,128)(2,1)S(1)}, bf16[256,256]{1,0:T(8,128)(2,1)S(1)}, u32[]{:S(2)}, u32[]{:S(2)}) collective-permute-start(bf16[256,256]{1,0:T(8,128)(2,1)S(1)} %get-tuple-element.45), channel_id=1, source_target_pairs={{0,4},{8,0},{16,8},{24,16},{28,24},{20,28},{12,20},{4,12},{1,5},{9... | collective-permute-start | bytes 393224 | tf_op jit(solution)/shard_map/ppermute | solution.py:182
  257.3 20.2 %copy-start.8 = (bf16[1280,512]{1,0:T(8,128)(2,1)S(1)}, bf16[1280,512]{1,0:T(8,128)(2,1)}, u32[]{:S(2)}) copy-start(bf16[1280,512]{1,0:T(8,128)(2,1)} %copy-done.7) | copy-start | bytes 3932164
  257.4 5.7 %collective-permute-start.12 = (bf16[256,256]{1,0:T(8,128)(2,1)S(1)}, bf16[256,256]{1,0:T(8,128)(2,1)S(1)}, u32[]{:S(2)}, u32[]{:S(2)}) collective-permute-start(bf16[256,256]{1,0:T(8,128)(2,1)S(1)} %get-tuple-element.55), channel_id=1, source_target_pairs={{0,8},{8,16},{16,24},{24,28},{28,20},{20,12},{12,4},{4,0},{1,9},{9... | collective-permute-start | bytes 393224 | tf_op jit(solution)/shard_map/ppermute | solution.py:182
  258.9 32.2 %copy-start.5 = (bf16[256,512]{1,0:T(8,128)(2,1)S(1)}, bf16[256,512]{1,0:T(8,128)(2,1)}, u32[]{:S(2)}) copy-start(bf16[256,512]{1,0:T(8,128)(2,1)} %reduce-scatter.2.cloned.1.call-done) | copy-start | bytes 786436
  258.9 32.2 %copy-start.13 = (f32[512]{0:T(512)S(1)}, f32[512]{0:T(512)}, u32[]{:S(2)}) copy-start(f32[512]{0:T(512)} %param.30) | copy-start | bytes 6148
  258.9 5.4 %collective-permute-start.19 = (bf16[256,256]{1,0:T(8,128)(2,1)S(1)}, bf16[256,256]{1,0:T(8,128)(2,1)S(1)}, u32[]{:S(2)}, u32[]{:S(2)}) collective-permute-start(bf16[256,256]{1,0:T(8,128)(2,1)S(1)} %get-tuple-element.56), channel_id=1, source_target_pairs={{0,4},{8,0},{16,8},{24,16},{28,24},{20,28},{12,20},{4,12},{1,5},{9... | collective-permute-start | bytes 393224 | tf_op jit(solution)/shard_map/ppermute | solution.py:182
  264.4 5.0 %collective-permute-start.13 = (bf16[256,256]{1,0:T(8,128)(2,1)S(1)}, bf16[256,256]{1,0:T(8,128)(2,1)S(1)}, u32[]{:S(2)}, u32[]{:S(2)}) collective-permute-start(bf16[256,256]{1,0:T(8,128)(2,1)S(1)} %get-tuple-element.53), channel_id=1, source_target_pairs={{0,8},{8,16},{16,24},{24,28},{28,20},{20,12},{12,4},{4,0},{1,9},{9... | collective-permute-start | bytes 393224 | tf_op jit(solution)/shard_map/ppermute | solution.py:182
  265.9 5.0 %collective-permute-start.20 = (bf16[256,256]{1,0:T(8,128)(2,1)S(1)}, bf16[256,256]{1,0:T(8,128)(2,1)S(1)}, u32[]{:S(2)}, u32[]{:S(2)}) collective-permute-start(bf16[256,256]{1,0:T(8,128)(2,1)S(1)} %get-tuple-element.54), channel_id=1, source_target_pairs={{0,4},{8,0},{16,8},{24,16},{28,24},{20,28},{12,20},{4,12},{1,5},{9... | collective-permute-start | bytes 393224 | tf_op jit(solution)/shard_map/ppermute | solution.py:182
  271.0 5.0 %collective-permute-start.14 = (bf16[256,256]{1,0:T(8,128)(2,1)S(1)}, bf16[256,256]{1,0:T(8,128)(2,1)S(1)}, u32[]{:S(2)}, u32[]{:S(2)}) collective-permute-start(bf16[256,256]{1,0:T(8,128)(2,1)S(1)} %get-tuple-element.51), channel_id=1, source_target_pairs={{0,8},{8,16},{16,24},{24,28},{28,20},{20,12},{12,4},{4,0},{1,9},{9... | collective-permute-start | bytes 393224 | tf_op jit(solution)/shard_map/ppermute | solution.py:182
  272.5 5.0 %collective-permute-start.21 = (bf16[256,256]{1,0:T(8,128)(2,1)S(1)}, bf16[256,256]{1,0:T(8,128)(2,1)S(1)}, u32[]{:S(2)}, u32[]{:S(2)}) collective-permute-start(bf16[256,256]{1,0:T(8,128)(2,1)S(1)} %get-tuple-element.52), channel_id=1, source_target_pairs={{0,4},{8,0},{16,8},{24,16},{28,24},{20,28},{12,20},{4,12},{1,5},{9... | collective-permute-start | bytes 393224 | tf_op jit(solution)/shard_map/ppermute | solution.py:182
  277.5 5.8 %collective-permute-start.15 = (bf16[256,256]{1,0:T(8,128)(2,1)S(1)}, bf16[256,256]{1,0:T(8,128)(2,1)S(1)}, u32[]{:S(2)}, u32[]{:S(2)}) collective-permute-start(bf16[256,256]{1,0:T(8,128)(2,1)S(1)} %get-tuple-element.42), channel_id=1, source_target_pairs={{0,8},{8,16},{16,24},{24,28},{28,20},{20,12},{12,4},{4,0},{1,9},{9... | collective-permute-start | bytes 393224 | tf_op jit(solution)/shard_map/ppermute | solution.py:182
  279.8 5.6 %collective-permute-start.22 = (bf16[256,256]{1,0:T(8,128)(2,1)S(1)}, bf16[256,256]{1,0:T(8,128)(2,1)S(1)}, u32[]{:S(2)}, u32[]{:S(2)}) collective-permute-start(bf16[256,256]{1,0:T(8,128)(2,1)S(1)} %get-tuple-element.43), channel_id=1, source_target_pairs={{0,4},{8,0},{16,8},{24,16},{28,24},{20,28},{12,20},{4,12},{1,5},{9... | collective-permute-start | bytes 393224 | tf_op jit(solution)/shard_map/ppermute | solution.py:182
  285.5 5.0 %collective-permute-start.16 = (bf16[256,256]{1,0:T(8,128)(2,1)S(1)}, bf16[256,256]{1,0:T(8,128)(2,1)S(1)}, u32[]{:S(2)}, u32[]{:S(2)}) collective-permute-start(bf16[256,256]{1,0:T(8,128)(2,1)S(1)} %get-tuple-element.40), channel_id=1, source_target_pairs={{0,8},{8,16},{16,24},{24,28},{28,20},{20,12},{12,4},{4,0},{1,9},{9... | collective-permute-start | bytes 393224 | tf_op jit(solution)/shard_map/ppermute | solution.py:182
  286.1 5.0 %collective-permute-start.23 = (bf16[256,256]{1,0:T(8,128)(2,1)S(1)}, bf16[256,256]{1,0:T(8,128)(2,1)S(1)}, u32[]{:S(2)}, u32[]{:S(2)}) collective-permute-start(bf16[256,256]{1,0:T(8,128)(2,1)S(1)} %get-tuple-element.41), channel_id=1, source_target_pairs={{0,4},{8,0},{16,8},{24,16},{28,24},{20,28},{12,20},{4,12},{1,5},{9... | collective-permute-start | bytes 393224 | tf_op jit(solution)/shard_map/ppermute | solution.py:182
  292.1 26.4 %copy-start.14 = (f32[512]{0:T(512)S(1)}, f32[512]{0:T(512)}, u32[]{:S(2)}) copy-start(f32[512]{0:T(512)} %param.33) | copy-start | bytes 6148
  292.1 26.4 %copy-start.15 = (f32[512]{0:T(512)S(1)}, f32[512]{0:T(512)}, u32[]{:S(2)}) copy-start(f32[512]{0:T(512)} %param.32) | copy-start | bytes 6148
  311.2 1.2 copy-start.3
  312.4 10.3 %copy-start.1 = (bf16[512,2048]{1,0:T(8,128)(2,1)S(1)}, bf16[512,2048]{1,0:T(8,128)(2,1)}, u32[]{:S(2)}) copy-start(bf16[512,2048]{1,0:T(8,128)(2,1)} %param.24) | copy-start | bytes 6291460
Sparse Core Ops, SparseCore 0:
  59.1 26.1 reduce-scatter.1
  111.7 39.5 all-gather.5
  153.0 28.5 all-gather.9
  183.0 40.4 all-gather.7
  225.0 28.5 all-gather.11
  292.2 13.9 all-gather.13

commit v10 on v9

--- a/solution.py
+++ b/solution.py
@@ -144,6 +144,39 @@
             by_offset[offsets[index]] = part[i]
             index += 1
     return ring_reduce_scatter(by_offset, ring)
+
+
+def permute_reduce_scatter(term, width):
+    tp_count = lax.axis_size("tp")
+    tp_here = lax.axis_index("tp")
+    total = lax.dynamic_slice_in_dim(term, tp_here * width, width, axis=1)
+    for shift in range(1, tp_count):
+        target = (tp_here + shift) % tp_count
+        piece = lax.dynamic_slice_in_dim(term, target * width, width, axis=1).astype(jnp.bfloat16)
+        pairs = [(i, (i + shift) % tp_count) for i in range(tp_count)]
+        total = total + lax.ppermute(piece, "tp", pairs).astype(jnp.float32)
+    return total
+
+
+def permute_gather_dot(rows, weight):
+    tp_count = lax.axis_size("tp")
+    tp_here = lax.axis_index("tp")
+    width = rows.shape[1]
+    total = jnp.dot(
+        rows,
+        lax.dynamic_slice_in_dim(weight, tp_here * width, width, axis=0),
+        preferred_element_type=jnp.float32,
+    )
+    for shift in range(1, tp_count):
+        source = (tp_here - shift) % tp_count
+        pairs = [(i, (i + shift) % tp_count) for i in range(tp_count)]
+        piece = lax.ppermute(rows, "tp", pairs)
+        total = total + jnp.dot(
+            piece,
+            lax.dynamic_slice_in_dim(weight, source * width, width, axis=0),
+            preferred_element_type=jnp.float32,
+        )
+    return total
 
 
 def ring_order(count):
@@ -288,9 +321,12 @@
         gate_up_flat = expert_gate_up
         qkv_flat = qkv_proj.reshape(D, -1)
     attn_term = jnp.dot(attended, out_proj, preferred_element_type=jnp.float32)
-    residual = hidden.astype(jnp.float32) + lax.psum_scatter(
-        attn_term.astype(jnp.bfloat16), "tp", scatter_dimension=1, tiled=True
-    ).astype(jnp.float32)
+    if dense:
+        residual = hidden.astype(jnp.float32) + permute_reduce_scatter(attn_term, local_width)
+    else:
+        residual = hidden.astype(jnp.float32) + lax.psum_scatter(
+            attn_term.astype(jnp.bfloat16), "tp", scatter_dimension=1, tiled=True
+        ).astype(jnp.float32)
     square_total = lax.psum(jnp.sum(residual * residual, axis=1), "tp")
     moe_in = (residual * lax.rsqrt(square_total / D + epsilon)[:, None] * moe_gain[None, :]).astype(
         jnp.bfloat16
@@ -307,11 +343,14 @@
     layer_out = routed.astype(jnp.bfloat16)
     scaled = (routed * next_gain[None, :]).astype(jnp.bfloat16)
     weight_rows = qkv_flat
-    mixed = jnp.dot(
-        lax.all_gather(scaled, "tp", axis=1, tiled=True),
-        weight_rows,
-        preferred_element_type=jnp.float32,
-    )
+    if dense:
+        mixed = permute_gather_dot(scaled, weight_rows)
+    else:
+        mixed = jnp.dot(
+            lax.all_gather(scaled, "tp", axis=1, tiled=True),
+            weight_rows,
+            preferred_element_type=jnp.float32,
+        )
     mixed = mixed.reshape(NEW, 3, local_width)
     squares_routed = jnp.sum(routed * routed, axis=1)
     routed_total, query_raw, key_raw = lax.psum(

time: 330 us -> 321 us (0.973)
  waiting for transfers between devices: 183 us -> 162 us
  starting transfers between devices: 26.1 us -> 34.7 us
  Pallas kernels: 16.8 us -> 11.6 us
  local copies, waits for them, and re-layouts: 31.3 us -> 34.7 us
  matrix products: 31 us -> 34.4 us
    reduce_scatter x1 -> x0, waiting for transfers between devices: 26.2 us -> none  [body(): lax.psum_scatter(attn_term.astype(jnp.bfloat16), 'tp', scatter_dimension=...]
    ppermute x0 -> x6, waiting for transfers between devices: none -> 17.8 us  [the longest x3 12.2 us: permute_reduce_scatter(): total = total + lax.ppermute(piece, 'tp', pairs).astype(jnp.float32)]
    all_gather x1 -> x0, waiting for transfers between devices: 14.1 us -> none  [body(): lax.all_gather(scaled, 'tp', axis=1, tiled=True)]
    pallas_call x1, Pallas kernels: 16.8 us -> 11.6 us  [flash_attention(): pl.pallas_call(kernel, grid_spec=grid_spec, out_shape=jax.ShapeDtypeStruc...]
    dot_general x1 -> x4, matrix products: 5 us -> 9.33 us  [the longest x3 7.33 us: permute_gather_dot(): jnp.dot(piece, lax.dynamic_slice_in_dim(weight, source * width, width, ax...]
    ppermute x0 -> x6, starting transfers between devices: none -> 4.09 us  [the longest x3 3.03 us: permute_reduce_scatter(): total = total + lax.ppermute(piece, 'tp', pairs).astype(jnp.float32)]
    ppermute x4, starting transfers between devices: 6.26 us -> 9.74 us  [ring_all_gather(): ahead = lax.ppermute(ahead, 'seq', forward)]
    unnamed x43 -> x41, local copies, waits for them, and re-layouts: 12.7 us -> 12.9 us
  transfers between devices with their start and end apart: 30 -> 34, of which waited for: 23 -> 25; matrix products, arithmetic and copies ran while one was open for 14% -> 17% of each run, Pallas kernels for 5% -> 4%
where the time goes in v10:
time: 321 us; the launch traced here: 320 us
  waiting for transfers between devices  162 us (50%)
  local copies, waits for them, and re-layouts  34.7 us (11%)
  starting transfers between devices  34.7 us (11%)
  matrix products  34.4 us (11%)
  other arithmetic  14.9 us (5%)
  between operations  14.2 us (4%)
  blocking collectives  13.4 us (4%)
  Pallas kernels  11.6 us (4%)
    all_gather x2, waiting for transfers between devices, dense_experts(): weighted = lax.all_gather(weighted, 'tp', axis=2, tiled=True)  49.9 us
    all_gather x2, waiting for transfers between devices, dense_experts(): rows = lax.all_gather(rows_q, 'tp', axis=1, tiled=True)  43.2 us
    ppermute x14, waiting for transfers between devices, ring_reduce_scatter(): received = lax.ppermute(acc.astype(jnp.bfloat16), 'seq', pairs)  27.7 us
    ppermute x4, waiting for transfers between devices, ring_all_gather(): ahead = lax.ppermute(ahead, 'seq', forward)  21.5 us
    dot_general x2, matrix products, dense_experts(): jnp.einsum('td,edf->etf', rows, expert_gate_up, preferred_element_type=jn...  15.2 us
    ppermute x14, starting transfers between devices, ring_reduce_scatter(): received = lax.ppermute(acc.astype(jnp.bfloat16), 'seq', pairs)  14.7 us
    unnamed x41, local copies, waits for them, and re-layouts  12.9 us
    ppermute x3, waiting for transfers between devices, permute_reduce_scatter(): total = total + lax.ppermute(piece, 'tp', pairs).astype(jnp.float32)  12.2 us
  transfers between devices with their start and end apart: 34, of which 25 were waited for; matrix products, arithmetic and copies ran while one was open for 17% of the time, Pallas kernels for 4%

profile of v10, /device:TPU:0, one launch (start us, length us, event | category | flops | bytes accessed | tf_op | source)
XLA Modules:
  0.0 319.7 jit_solution(14406229239777973152)
XLA Ops:
  7.3 2.9 dynamic-slice_bitcast_fusion
  10.1 2.4 collective-permute-start.2
  13.3 7.6 %reshape.133 = bf16[2,2048,512]{2,1,0:T(8,128)(2,1)} reshape(bf16[2,2048,2,256]{3,2,1,0:T(2,128)(2,1)} %param.28) | data formatting | bytes 8388608 | tf_op jit(solution)/shard_map/reshape | solution.py:301
  20.9 8.9 %copy.68 = bf16[2048,3,512]{0,2,1:T(8,128)(2,1)} copy(bf16[2048,3,512]{2,0,1:T(8,128)(2,1)} %param.31) | data formatting | bytes 12582912 | tf_op args[14]
  30.4 11.6 %shard_map.192 = bf16[256,512]{1,0:T(8,128)(2,1)} custom-call(s32[1]{0:T(128)} %dynamic_slice.50.len_ref, bf16[256,512]{1,0:T(8,128)(2,1)} %q_ref.1, bf16[4096,512]{1,0:T(8,128)(2,1)} %bitcast.112, bf16[4096,512]{1,0:T(8,128)(2,1)} %bitcast.113, bf16[256,512]{1,0:T(8,128)(2,1)} %nk_ref.1, bf16[256,512]{1,0:T(8,128)(2,1)} %nv_ref.1), custom_call_target="tpu_custom_call" | custom-call | tf_op jit(solution)/shard_map/pallas_call | solution.py:94
  42.1 2.8 pad_maximum_fusion
  45.0 3.6 %gather_fusion = bf16[4,2,256,512]{3,2,1,0:T(8,128)(2,1)} fusion(bf16[4,2,256,512]{3,2,1,0:T(8,128)(2,1)} %pad_maximum_fusion, s32[1024]{0:T(1024)S(1)} %pad_clamp_fusion), kind=kCustom, calls=%fused_computation | custom fusion | bytes 4194320 | tf_op jit(solution)/shard_map/jit(_take)/gather | solution.py:299
  48.6 1.9 select_bitcast_fusion
  50.4 1.6 copy.67
  54.2 1.6 collective-permute-start.5
  57.2 5.1 %collective-permute-done.5 = bf16[256,512]{1,0:T(8,128)(2,1)S(1)} collective-permute-done((bf16[256,512]{1,0:T(8,128)(2,1)S(1)}, bf16[256,512]{1,0:T(8,128)(2,1)S(1)}, u32[]{:S(2)}, u32[]{:S(2)}) %collective-permute-start.5) | collective-permute-done | bytes 262176 | tf_op jit(solution)/shard_map/ppermute | solution.py:157
  62.3 7.1 %collective-permute-done.4 = bf16[256,512]{1,0:T(8,128)(2,1)S(1)} collective-permute-done((bf16[256,512]{1,0:T(8,128)(2,1)S(1)}, bf16[256,512]{1,0:T(8,128)(2,1)S(1)}, u32[]{:S(2)}, u32[]{:S(2)}) %collective-permute-start.4) | collective-permute-done | bytes 262176 | tf_op jit(solution)/shard_map/ppermute | solution.py:157
  70.8 6.0 %psum.28 = f32[256]{0:T(256)S(1)} all-reduce(f32[256]{0:T(256)S(1)} %get-tuple-element.29), channel_id=1, replica_groups=mesh['seq'=8,'tp'=4] {'tp'}, use_global_device_ids=true, to_apply=%region_1.2 | all-reduce | flops 256 | bytes 2048 | tf_op jit(solution)/shard_map/psum | solution.py:330
  76.9 2.0 collective-permute-start.7
  79.0 6.1 %collective-permute-done.6 = bf16[272,512]{1,0:T(8,128)(2,1)S(1)} collective-permute-done((bf16[272,512]{1,0:T(8,128)(2,1)S(1)}, bf16[272,512]{1,0:T(8,128)(2,1)S(1)}, u32[]{:S(2)}, u32[]{:S(2)}) %collective-permute-start.6) | collective-permute-done | bytes 278560 | tf_op jit(solution)/shard_map/ppermute | solution.py:196
  85.1 5.9 %collective-permute-start.8 = (bf16[272,512]{1,0:T(8,128)(2,1)S(1)}, bf16[272,512]{1,0:T(8,128)(2,1)S(1)}, u32[]{:S(2)}, u32[]{:S(2)}) collective-permute-start(bf16[272,512]{1,0:T(8,128)(2,1)S(1)} %collective-permute-done.6), channel_id=1, source_target_pairs={{0,8},{8,16},{16,24},{24,28},{28,20},{20,12},{12,4},{4,0},{1,9},{9... | collective-permute-start | bytes 835592 | tf_op jit(solution)/shard_map/ppermute | solution.py:196
  91.7 5.7 %collective-permute-done.8 = bf16[272,512]{1,0:T(8,128)(2,1)S(1)} collective-permute-done((bf16[272,512]{1,0:T(8,128)(2,1)S(1)}, bf16[272,512]{1,0:T(8,128)(2,1)S(1)}, u32[]{:S(2)}, u32[]{:S(2)}) %collective-permute-start.8) | collective-permute-done | bytes 278560 | tf_op jit(solution)/shard_map/ppermute | solution.py:196
  100.1 1.8 collective-permute-start.12
  102.2 5.3 %collective-permute-done.12 = bf16[272,512]{1,0:T(8,128)(2,1)S(1)} collective-permute-done((bf16[272,512]{1,0:T(8,128)(2,1)S(1)}, bf16[272,512]{1,0:T(8,128)(2,1)S(1)}, u32[]{:S(2)}, u32[]{:S(2)}) %collective-permute-start.12) | collective-permute-done | bytes 278560 | tf_op jit(solution)/shard_map/ppermute | solution.py:196
  107.4 2.0 collective-permute-start.14
  109.5 4.5 %collective-permute-done.14 = bf16[272,512]{1,0:T(8,128)(2,1)S(1)} collective-permute-done((bf16[272,512]{1,0:T(8,128)(2,1)S(1)}, bf16[272,512]{1,0:T(8,128)(2,1)S(1)}, u32[]{:S(2)}, u32[]{:S(2)}) %collective-permute-start.14) | collective-permute-done | bytes 278560 | tf_op jit(solution)/shard_map/ppermute | solution.py:196
  116.3 24.2 %all-gather.5.cloned.1.call-done = bf16[1280,2048]{1,0:T(8,128)(2,1)} async-done(((bf16[1280,512]{1,0:T(8,128)(2,1)}), bf16[1280,2048]{1,0:T(8,128)(2,1)}) %all-gather.5.cloned.1.call-update) | async-done | bytes 5242896 | tf_op jit(solution)/shard_map/all_gather | solution.py:130
  140.5 9.0 %fusion.2 = f32[2,1280,512]{1,2,0:T(8,128)S(1)} fusion(bf16[2,2048,512]{2,1,0:T(8,128)(2,1)} %reshape.133, bf16[1280,2048]{1,0:T(8,128)(2,1)} %all-gather.5.cloned.1.call-done), kind=kOutput, calls=%fused_computation.3 | convolution fusion | flops 5368709120 | bytes 14680064 | tf_op jit(solution)/shard_map/td,edf->etf/dot_general | solution.py:131
  149.5 1.9 multiply_convert_fusion
  151.6 19.0 %all-gather.9.cloned.1.call-done = bf16[768,2048]{1,0:T(8,128)(2,1)} async-done(((bf16[768,512]{1,0:T(8,128)(2,1)}), bf16[768,2048]{1,0:T(8,128)(2,1)}) %all-gather.9.cloned.1.call-update) | async-done | bytes 3145744 | tf_op jit(solution)/shard_map/all_gather | solution.py:130
  170.7 6.2 %fusion.10 = f32[2,768,512]{1,2,0:T(8,128)S(1)} fusion(bf16[2,2048,512]{2,1,0:T(8,128)(2,1)} %reshape.133, bf16[768,2048]{1,0:T(8,128)(2,1)} %all-gather.9.cloned.1.call-done), kind=kOutput, calls=%fused_computation.16 | convolution fusion | flops 3221225472 | bytes 10485760 | tf_op jit(solution)/shard_map/td,edf->etf/dot_general | solution.py:131
  178.3 34.4 %all-gather.7.cloned.1.call-done = bf16[2,1280,1024]{1,2,0:T(8,128)(2,1)} async-done(((bf16[2,1280,256]{1,2,0:T(8,128)(2,1)}), bf16[2,1280,1024]{1,2,0:T(8,128)(2,1)}) %all-gather.7.cloned.1.call-update) | async-done | bytes 5242896 | tf_op jit(solution)/shard_map/all_gather | solution.py:135
  212.7 5.4 %fusion.7 = bf16[1280,512]{1,0:T(8,128)(2,1)S(1)} fusion(bf16[2,1280,1024]{1,2,0:T(8,128)(2,1)} %all-gather.7.cloned.1.call-done, bf16[2,1024,512]{2,1,0:T(8,128)(2,1)S(1)} %bitcast.109), kind=kOutput, calls=%fused_computation.7 | convolution fusion | flops 2685009920 | bytes 8650752 | tf_op jit(solution)/shard_map/etf,efd->td/dot_general | solution.py:136
  220.2 3.6 %collective-permute-done.10 = bf16[256,256]{1,0:T(8,128)(2,1)S(1)} collective-permute-done((bf16[256,256]{1,0:T(8,128)(2,1)S(1)}, bf16[256,256]{1,0:T(8,128)(2,1)S(1)}, u32[]{:S(2)}, u32[]{:S(2)}) %collective-permute-start.10) | collective-permute-done | bytes 131104 | tf_op jit(solution)/shard_map/ppermute | solution.py:215
  225.1 1.5 collective-permute-start.11
  227.2 15.5 %all-gather.11.cloned.1.call-done = bf16[2,768,1024]{1,2,0:T(8,128)(2,1)} async-done(((bf16[2,768,256]{1,2,0:T(8,128)(2,1)}), bf16[2,768,1024]{1,2,0:T(8,128)(2,1)}) %all-gather.11.cloned.1.call-update) | async-done | bytes 3145744 | tf_op jit(solution)/shard_map/all_gather | solution.py:135
  242.7 3.7 %bitcast_convert_fusion = bf16[768,512]{1,0:T(8,128)(2,1)S(1)} fusion(bf16[2,768,1024]{1,2,0:T(8,128)(2,1)} %all-gather.11.cloned.1.call-done, bf16[2,1024,512]{2,1,0:T(8,128)(2,1)S(1)} %bitcast.110), kind=kOutput, calls=%fused_computation.19 | convolution fusion | flops 1611005952 | bytes 6029312 | tf_op jit(solution)/shard_map/etf,efd->td/dot_general | solution.py:136
  248.6 3.6 %collective-permute-done.15 = bf16[256,256]{1,0:T(8,128)(2,1)S(1)} collective-permute-done((bf16[256,256]{1,0:T(8,128)(2,1)S(1)}, bf16[256,256]{1,0:T(8,128)(2,1)S(1)}, u32[]{:S(2)}, u32[]{:S(2)}) %collective-permute-start.15) | collective-permute-done | bytes 131104 | tf_op jit(solution)/shard_map/ppermute | solution.py:215
  253.5 1.5 collective-permute-start.16
  255.6 2.9 collective-permute-done.16
  262.2 2.9 collective-permute-done.17
  266.7 2.2 collective-permute-start.18
  268.9 3.5 %collective-permute-done.18 = bf16[256,256]{1,0:T(8,128)(2,1)S(1)} collective-permute-done((bf16[256,256]{1,0:T(8,128)(2,1)S(1)}, bf16[256,256]{1,0:T(8,128)(2,1)S(1)}, u32[]{:S(2)}, u32[]{:S(2)}) %collective-permute-start.18) | collective-permute-done | bytes 131104 | tf_op jit(solution)/shard_map/ppermute | solution.py:215
  272.4 2.1 collective-permute-done.25
  276.7 2.9 collective-permute-done.19
  282.1 2.0 fusion.18
  284.1 5.5 %collective-permute-done.27 = bf16[256,512]{1,0:T(8,128)(2,1)S(1)} collective-permute-done((bf16[256,512]{1,0:T(8,128)(2,1)S(1)}, bf16[256,512]{1,0:T(8,128)(2,1)S(1)}, u32[]{:S(2)}, u32[]{:S(2)}) %collective-permute-start.27) | collective-permute-done | bytes 262176 | tf_op jit(solution)/shard_map/ppermute | solution.py:173
  289.6 2.0 convolution_add_fusion.1
  291.7 2.0 fusion.14
  293.7 3.3 %fusion.8 = f32[256,1536]{1,0:T(8,128)} fusion(f32[256,1536]{1,0:T(8,128)S(1)} %fusion.14, f32[256,1536]{1,0:T(8,128)S(1)} %convolution_add_fusion.1, bf16[256,512]{1,0:T(8,128)(2,1)S(1)} %collective-permute-done.28, bf16[2048,1536]{0,1:T(8,128)(2,1)} %bitcast.106, s32[]{:T(128)S(6)} %select_n.126), kind=kOutput, calls=%fused_computation.9 | convolution fusion | flops 403439616 | bytes 6553604 | tf_op jit(solution)/shard_map/dot_general | solution.py:174
  297.0 3.1 copy.79
  301.5 7.5 %all-reduce = (f32[256]{0:T(256)S(1)}, f32[256]{0:T(256)S(1)}, f32[256]{0:T(256)S(1)}) all-reduce(f32[256]{0:T(256)S(1)} %get-tuple-element.25, f32[256]{0:T(256)S(1)} %get-tuple-element.53, f32[256]{0:T(256)S(1)} %get-tuple-element.24), channel_id=1, replica_groups=mesh['seq'=8,'tp'=4] {'tp'}, use_global_device_ids=true, to_apply=%region_6.7 | all-reduce | flops 768 | bytes 6144 | tf_op jit(solution)/shard_map/psum | solution.py:356
  309.0 1.6 fusion.21
  (122 shorter events, 35.9 us)
Async XLA Ops:
  7.2 44.8 %copy-start = (bf16[512,2048]{1,0:T(8,128)(2,1)S(1)}, bf16[512,2048]{1,0:T(8,128)(2,1)}, u32[]{:S(2)}) copy-start(bf16[512,2048]{1,0:T(8,128)(2,1)} %param.24) | copy-start | bytes 6291460
  7.2 133.4 %all-gather.5.cloned.1.call-start = ((), (), s32[]{:S(2)}) async-start(), calls=%async_computation | async-start | bytes 6553600 | tf_op jit(solution)/shard_map/all_gather | solution.py:130
  10.1 31.9 %collective-permute-start.2 = (bf16[2,256,512]{2,1,0:T(8,128)(2,1)}, bf16[2,256,512]{2,1,0:T(8,128)(2,1)S(1)}, u32[]{:S(2)}, u32[]{:S(2)}) collective-permute-start(bf16[2,256,512]{2,1,0:T(8,128)(2,1)} %get-tuple-element.38), channel_id=1, source_target_pairs={{0,3},{1,0},{2,1},{3,2},{4,7},{5,4},{6,5},{7,6},{8,11},{9,8},{10,9... | collective-permute-start | bytes 1572872 | tf_op jit(solution)/shard_map/ppermute | solution.py:297
  12.5 29.5 %collective-permute-start.1 = (bf16[2,256,512]{2,1,0:T(8,128)(2,1)}, bf16[2,256,512]{2,1,0:T(8,128)(2,1)}, u32[]{:S(2)}, u32[]{:S(2)}) collective-permute-start(bf16[2,256,512]{2,1,0:T(8,128)(2,1)} %get-tuple-element.39), channel_id=1, source_target_pairs={{0,2},{1,3},{2,0},{3,1},{4,6},{5,7},{6,4},{7,5},{8,10},{9,11},{10,... | collective-permute-start | bytes 1572872 | tf_op jit(solution)/shard_map/ppermute | solution.py:297
  13.1 29.0 %collective-permute-start = (bf16[2,256,512]{2,1,0:T(8,128)(2,1)}, bf16[2,256,512]{2,1,0:T(8,128)(2,1)}, u32[]{:S(2)}, u32[]{:S(2)}) collective-permute-start(bf16[2,256,512]{2,1,0:T(8,128)(2,1)} %get-tuple-element.37), channel_id=1, source_target_pairs={{0,1},{1,2},{2,3},{3,0},{4,5},{5,6},{6,7},{7,4},{8,9},{9,10},{10,1... | collective-permute-start | bytes 1572872 | tf_op jit(solution)/shard_map/ppermute | solution.py:297
  20.9 8.9 %copy-start.15 = (s32[8]{0:T(128)S(1)}, s32[8]{0:T(128)}, u32[]{:S(2)}) copy-start(s32[8]{0:T(128)} %param.23) | copy-start | bytes 100
  30.4 11.6 %copy-start.9 = (f32[256,8]{0,1:T(8,128)S(1)}, f32[256,8]{0,1:T(8,128)}, u32[]{:S(2)}) copy-start(f32[256,8]{0,1:T(8,128)} %param.27) | copy-start | bytes 24580
  30.4 11.7 %copy-start.10 = (s32[256,8]{0,1:T(8,128)S(1)}, s32[256,8]{0,1:T(8,128)}, u32[]{:S(2)}) copy-start(s32[256,8]{0,1:T(8,128)} %param.26) | copy-start | bytes 24580
  52.0 17.5 %copy-start.8 = (bf16[256,512]{1,0:T(8,128)(2,1)S(1)}, bf16[256,512]{1,0:T(8,128)(2,1)}, u32[]{:S(2)}) copy-start(bf16[256,512]{1,0:T(8,128)(2,1)} %param.17) | copy-start | bytes 786436
  54.0 22.7 %copy-start.11 = (f32[512]{0:T(512)S(1)}, f32[512]{0:T(512)}, u32[]{:S(2)}) copy-start(f32[512]{0:T(512)} %param.25) | copy-start | bytes 6148
  54.2 8.2 %collective-permute-start.5 = (bf16[256,512]{1,0:T(8,128)(2,1)S(1)}, bf16[256,512]{1,0:T(8,128)(2,1)S(1)}, u32[]{:S(2)}, u32[]{:S(2)}) collective-permute-start(bf16[256,512]{1,0:T(8,128)(2,1)S(1)} %get-tuple-element.34), channel_id=1, source_target_pairs={{0,3},{1,0},{2,1},{3,2},{4,7},{5,4},{6,5},{7,6},{8,11},{9,8},{10,9... | collective-permute-start | bytes 786440 | tf_op jit(solution)/shard_map/ppermute | solution.py:157
  55.7 13.7 %collective-permute-start.4 = (bf16[256,512]{1,0:T(8,128)(2,1)S(1)}, bf16[256,512]{1,0:T(8,128)(2,1)S(1)}, u32[]{:S(2)}, u32[]{:S(2)}) collective-permute-start(bf16[256,512]{1,0:T(8,128)(2,1)S(1)} %get-tuple-element.35), channel_id=1, source_target_pairs={{0,2},{1,3},{2,0},{3,1},{4,6},{5,7},{6,4},{7,5},{8,10},{9,11},{10,... | collective-permute-start | bytes 786440 | tf_op jit(solution)/shard_map/ppermute | solution.py:157
  57.2 12.3 %collective-permute-start.3 = (bf16[256,512]{1,0:T(8,128)(2,1)S(1)}, bf16[256,512]{1,0:T(8,128)(2,1)S(1)}, u32[]{:S(2)}, u32[]{:S(2)}) collective-permute-start(bf16[256,512]{1,0:T(8,128)(2,1)S(1)} %get-tuple-element.33), channel_id=1, source_target_pairs={{0,1},{1,2},{2,3},{3,0},{4,5},{5,6},{6,7},{7,4},{8,9},{9,10},{10,1... | collective-permute-start | bytes 786440 | tf_op jit(solution)/shard_map/ppermute | solution.py:157
  76.9 8.2 %collective-permute-start.6 = (bf16[272,512]{1,0:T(8,128)(2,1)S(1)}, bf16[272,512]{1,0:T(8,128)(2,1)S(1)}, u32[]{:S(2)}, u32[]{:S(2)}) collective-permute-start(bf16[272,512]{1,0:T(8,128)(2,1)S(1)} %pad_maximum_fusion.2), channel_id=1, source_target_pairs={{0,8},{8,16},{16,24},{24,28},{28,20},{20,12},{12,4},{4,0},{1,9},{9... | collective-permute-start | bytes 835592 | tf_op jit(solution)/shard_map/ppermute | solution.py:196
  76.9 14.4 %collective-permute-start.7 = (bf16[272,512]{1,0:T(8,128)(2,1)S(1)}, bf16[272,512]{1,0:T(8,128)(2,1)S(1)}, u32[]{:S(2)}, u32[]{:S(2)}) collective-permute-start(bf16[272,512]{1,0:T(8,128)(2,1)S(1)} %pad_maximum_fusion.2), channel_id=1, source_target_pairs={{0,4},{8,0},{16,8},{24,16},{28,24},{20,28},{12,20},{4,12},{1,5},{9... | collective-permute-start | bytes 835592 | tf_op jit(solution)/shard_map/ppermute | solution.py:200
  85.1 12.3 %collective-permute-start.8 = (bf16[272,512]{1,0:T(8,128)(2,1)S(1)}, bf16[272,512]{1,0:T(8,128)(2,1)S(1)}, u32[]{:S(2)}, u32[]{:S(2)}) collective-permute-start(bf16[272,512]{1,0:T(8,128)(2,1)S(1)} %collective-permute-done.6), channel_id=1, source_target_pairs={{0,8},{8,16},{16,24},{24,28},{28,20},{20,12},{12,4},{4,0},{1,9},{9... | collective-permute-start | bytes 835592 | tf_op jit(solution)/shard_map/ppermute | solution.py:196
  91.4 7.3 %collective-permute-start.9 = (bf16[272,512]{1,0:T(8,128)(2,1)S(1)}, bf16[272,512]{1,0:T(8,128)(2,1)S(1)}, u32[]{:S(2)}, u32[]{:S(2)}) collective-permute-start(bf16[272,512]{1,0:T(8,128)(2,1)S(1)} %collective-permute-done.7), channel_id=1, source_target_pairs={{0,4},{8,0},{16,8},{24,16},{28,24},{20,28},{12,20},{4,12},{1,5},{9... | collective-permute-start | bytes 835592 | tf_op jit(solution)/shard_map/ppermute | solution.py:200
  98.7 15.3 %copy-start.4 = (bf16[5,272,512]{2,1,0:T(8,128)(2,1)}, bf16[5,272,512]{2,1,0:T(8,128)(2,1)S(1)}, u32[]{:S(2)}) copy-start(bf16[5,272,512]{2,1,0:T(8,128)(2,1)S(1)} %bitcast_dynamic-update-slice_fusion) | copy-start | bytes 4177924
  100.0 70.6 %all-gather.9.cloned.1.call-start = ((), (), s32[]{:S(2)}) async-start(), calls=%async_computation.2 | async-start | bytes 3932160 | tf_op jit(solution)/shard_map/all_gather | solution.py:130
  100.1 7.4 %collective-permute-start.12 = (bf16[272,512]{1,0:T(8,128)(2,1)S(1)}, bf16[272,512]{1,0:T(8,128)(2,1)S(1)}, u32[]{:S(2)}, u32[]{:S(2)}) collective-permute-start(bf16[272,512]{1,0:T(8,128)(2,1)S(1)} %collective-permute-done.8), channel_id=1, source_target_pairs={{0,8},{8,16},{16,24},{24,28},{28,20},{20,12},{12,4},{4,0},{1,9},{9... | collective-permute-start | bytes 835592 | tf_op jit(solution)/shard_map/ppermute | solution.py:196
  101.9 7.6 %collective-permute-start.13 = (bf16[272,512]{1,0:T(8,128)(2,1)S(1)}, bf16[272,512]{1,0:T(8,128)(2,1)S(1)}, u32[]{:S(2)}, u32[]{:S(2)}) collective-permute-start(bf16[272,512]{1,0:T(8,128)(2,1)S(1)} %collective-permute-done.9), channel_id=1, source_target_pairs={{0,4},{8,0},{16,8},{24,16},{28,24},{20,28},{12,20},{4,12},{1,5},{9... | collective-permute-start | bytes 835592 | tf_op jit(solution)/shard_map/ppermute | solution.py:200
  107.4 6.5 %collective-permute-start.14 = (bf16[272,512]{1,0:T(8,128)(2,1)S(1)}, bf16[272,512]{1,0:T(8,128)(2,1)S(1)}, u32[]{:S(2)}, u32[]{:S(2)}) collective-permute-start(bf16[272,512]{1,0:T(8,128)(2,1)S(1)} %collective-permute-done.12), channel_id=1, source_target_pairs={{0,8},{8,16},{16,24},{24,28},{28,20},{20,12},{12,4},{4,0},{1,9},{9... | collective-permute-start | bytes 835592 | tf_op jit(solution)/shard_map/ppermute | solution.py:196
  115.1 97.6 %all-gather.7.cloned.1.call-start = ((), (), s32[]{:S(2)}) async-start(), calls=%async_computation.1 | async-start | bytes 6553600 | tf_op jit(solution)/shard_map/all_gather | solution.py:135
  151.5 91.2 %all-gather.11.cloned.1.call-start = ((), (), s32[]{:S(2)}) async-start(), calls=%async_computation.3 | async-start | bytes 3932160 | tf_op jit(solution)/shard_map/all_gather | solution.py:135
  176.9 35.8 %copy-start.2 = (bf16[2,4,256,512]{3,2,1,0:T(8,128)(2,1)S(1)}, bf16[2,4,256,512]{3,2,1,0:T(8,128)(2,1)}, u32[]{:S(2)}) copy-start(bf16[2,4,256,512]{3,2,1,0:T(8,128)(2,1)} %copy.67) | copy-start | bytes 6291460
  218.1 7.0 %copy-start.5 = (bf16[1280,512]{1,0:T(8,128)(2,1)}, bf16[1280,512]{1,0:T(8,128)(2,1)S(1)}, u32[]{:S(2)}) copy-start(bf16[1280,512]{1,0:T(8,128)(2,1)S(1)} %fusion.7) | copy-start | bytes 3932164
  218.1 5.7 %collective-permute-start.10 = (bf16[256,256]{1,0:T(8,128)(2,1)S(1)}, bf16[256,256]{1,0:T(8,128)(2,1)S(1)}, u32[]{:S(2)}, u32[]{:S(2)}) collective-permute-start(bf16[256,256]{1,0:T(8,128)(2,1)S(1)} %get-tuple-element.51), channel_id=1, source_target_pairs={{0,8},{8,16},{16,24},{24,28},{28,20},{20,12},{12,4},{4,0},{1,9},{9... | collective-permute-start | bytes 393224 | tf_op jit(solution)/shard_map/ppermute | solution.py:215
  219.7 5.4 %collective-permute-start.20 = (bf16[256,256]{1,0:T(8,128)(2,1)S(1)}, bf16[256,256]{1,0:T(8,128)(2,1)S(1)}, u32[]{:S(2)}, u32[]{:S(2)}) collective-permute-start(bf16[256,256]{1,0:T(8,128)(2,1)S(1)} %get-tuple-element.52), channel_id=1, source_target_pairs={{0,4},{8,0},{16,8},{24,16},{28,24},{20,28},{12,20},{4,12},{1,5},{9... | collective-permute-start | bytes 393224 | tf_op jit(solution)/shard_map/ppermute | solution.py:215
  225.1 21.3 %collective-permute-start.11 = (bf16[256,256]{1,0:T(8,128)(2,1)S(1)}, bf16[256,256]{1,0:T(8,128)(2,1)S(1)}, u32[]{:S(2)}, u32[]{:S(2)}) collective-permute-start(bf16[256,256]{1,0:T(8,128)(2,1)S(1)} %get-tuple-element.49), channel_id=1, source_target_pairs={{0,8},{8,16},{16,24},{24,28},{28,20},{20,12},{12,4},{4,0},{1,9},{9... | collective-permute-start | bytes 393224 | tf_op jit(solution)/shard_map/ppermute | solution.py:215
  226.7 19.7 %collective-permute-start.21 = (bf16[256,256]{1,0:T(8,128)(2,1)S(1)}, bf16[256,256]{1,0:T(8,128)(2,1)S(1)}, u32[]{:S(2)}, u32[]{:S(2)}) collective-permute-start(bf16[256,256]{1,0:T(8,128)(2,1)S(1)} %get-tuple-element.50), channel_id=1, source_target_pairs={{0,4},{8,0},{16,8},{24,16},{28,24},{20,28},{12,20},{4,12},{1,5},{9... | collective-permute-start | bytes 393224 | tf_op jit(solution)/shard_map/ppermute | solution.py:215
  246.4 20.2 %copy-start.6 = (bf16[1280,512]{1,0:T(8,128)(2,1)S(1)}, bf16[1280,512]{1,0:T(8,128)(2,1)}, u32[]{:S(2)}) copy-start(bf16[1280,512]{1,0:T(8,128)(2,1)} %copy-done.5) | copy-start | bytes 3932164
  246.5 5.7 %collective-permute-start.15 = (bf16[256,256]{1,0:T(8,128)(2,1)S(1)}, bf16[256,256]{1,0:T(8,128)(2,1)S(1)}, u32[]{:S(2)}, u32[]{:S(2)}) collective-permute-start(bf16[256,256]{1,0:T(8,128)(2,1)S(1)} %get-tuple-element.60), channel_id=1, source_target_pairs={{0,8},{8,16},{16,24},{24,28},{28,20},{20,12},{12,4},{4,0},{1,9},{9... | collective-permute-start | bytes 393224 | tf_op jit(solution)/shard_map/ppermute | solution.py:215
  248.0 32.2 %copy-start.12 = (f32[512]{0:T(512)S(1)}, f32[512]{0:T(512)}, u32[]{:S(2)}) copy-start(f32[512]{0:T(512)} %param.30) | copy-start | bytes 6148
  248.1 5.4 %collective-permute-start.22 = (bf16[256,256]{1,0:T(8,128)(2,1)S(1)}, bf16[256,256]{1,0:T(8,128)(2,1)S(1)}, u32[]{:S(2)}, u32[]{:S(2)}) collective-permute-start(bf16[256,256]{1,0:T(8,128)(2,1)S(1)} %get-tuple-element.61), channel_id=1, source_target_pairs={{0,4},{8,0},{16,8},{24,16},{28,24},{20,28},{12,20},{4,12},{1,5},{9... | collective-permute-start | bytes 393224 | tf_op jit(solution)/shard_map/ppermute | solution.py:215
  253.5 5.0 %collective-permute-start.16 = (bf16[256,256]{1,0:T(8,128)(2,1)S(1)}, bf16[256,256]{1,0:T(8,128)(2,1)S(1)}, u32[]{:S(2)}, u32[]{:S(2)}) collective-permute-start(bf16[256,256]{1,0:T(8,128)(2,1)S(1)} %get-tuple-element.58), channel_id=1, source_target_pairs={{0,8},{8,16},{16,24},{24,28},{28,20},{20,12},{12,4},{4,0},{1,9},{9... | collective-permute-start | bytes 393224 | tf_op jit(solution)/shard_map/ppermute | solution.py:215
  255.0 5.0 %collective-permute-start.23 = (bf16[256,256]{1,0:T(8,128)(2,1)S(1)}, bf16[256,256]{1,0:T(8,128)(2,1)S(1)}, u32[]{:S(2)}, u32[]{:S(2)}) collective-permute-start(bf16[256,256]{1,0:T(8,128)(2,1)S(1)} %get-tuple-element.59), channel_id=1, source_target_pairs={{0,4},{8,0},{16,8},{24,16},{28,24},{20,28},{12,20},{4,12},{1,5},{9... | collective-permute-start | bytes 393224 | tf_op jit(solution)/shard_map/ppermute | solution.py:215
  260.1 5.0 %collective-permute-start.17 = (bf16[256,256]{1,0:T(8,128)(2,1)S(1)}, bf16[256,256]{1,0:T(8,128)(2,1)S(1)}, u32[]{:S(2)}, u32[]{:S(2)}) collective-permute-start(bf16[256,256]{1,0:T(8,128)(2,1)S(1)} %get-tuple-element.56), channel_id=1, source_target_pairs={{0,8},{8,16},{16,24},{24,28},{28,20},{20,12},{12,4},{4,0},{1,9},{9... | collective-permute-start | bytes 393224 | tf_op jit(solution)/shard_map/ppermute | solution.py:215
  261.6 5.0 %collective-permute-start.24 = (bf16[256,256]{1,0:T(8,128)(2,1)S(1)}, bf16[256,256]{1,0:T(8,128)(2,1)S(1)}, u32[]{:S(2)}, u32[]{:S(2)}) collective-permute-start(bf16[256,256]{1,0:T(8,128)(2,1)S(1)} %get-tuple-element.57), channel_id=1, source_target_pairs={{0,4},{8,0},{16,8},{24,16},{28,24},{20,28},{12,20},{4,12},{1,5},{9... | collective-permute-start | bytes 393224 | tf_op jit(solution)/shard_map/ppermute | solution.py:215
  266.7 5.8 %collective-permute-start.18 = (bf16[256,256]{1,0:T(8,128)(2,1)S(1)}, bf16[256,256]{1,0:T(8,128)(2,1)S(1)}, u32[]{:S(2)}, u32[]{:S(2)}) collective-permute-start(bf16[256,256]{1,0:T(8,128)(2,1)S(1)} %get-tuple-element.47), channel_id=1, source_target_pairs={{0,8},{8,16},{16,24},{24,28},{28,20},{20,12},{12,4},{4,0},{1,9},{9... | collective-permute-start | bytes 393224 | tf_op jit(solution)/shard_map/ppermute | solution.py:215
  268.9 5.6 %collective-permute-start.25 = (bf16[256,256]{1,0:T(8,128)(2,1)S(1)}, bf16[256,256]{1,0:T(8,128)(2,1)S(1)}, u32[]{:S(2)}, u32[]{:S(2)}) collective-permute-start(bf16[256,256]{1,0:T(8,128)(2,1)S(1)} %get-tuple-element.48), channel_id=1, source_target_pairs={{0,4},{8,0},{16,8},{24,16},{28,24},{20,28},{12,20},{4,12},{1,5},{9... | collective-permute-start | bytes 393224 | tf_op jit(solution)/shard_map/ppermute | solution.py:215
  274.6 5.0 %collective-permute-start.19 = (bf16[256,256]{1,0:T(8,128)(2,1)S(1)}, bf16[256,256]{1,0:T(8,128)(2,1)S(1)}, u32[]{:S(2)}, u32[]{:S(2)}) collective-permute-start(bf16[256,256]{1,0:T(8,128)(2,1)S(1)} %get-tuple-element.45), channel_id=1, source_target_pairs={{0,8},{8,16},{16,24},{24,28},{28,20},{20,12},{12,4},{4,0},{1,9},{9... | collective-permute-start | bytes 393224 | tf_op jit(solution)/shard_map/ppermute | solution.py:215
  275.2 5.0 %collective-permute-start.26 = (bf16[256,256]{1,0:T(8,128)(2,1)S(1)}, bf16[256,256]{1,0:T(8,128)(2,1)S(1)}, u32[]{:S(2)}, u32[]{:S(2)}) collective-permute-start(bf16[256,256]{1,0:T(8,128)(2,1)S(1)} %get-tuple-element.46), channel_id=1, source_target_pairs={{0,4},{8,0},{16,8},{24,16},{28,24},{20,28},{12,20},{4,12},{1,5},{9... | collective-permute-start | bytes 393224 | tf_op jit(solution)/shard_map/ppermute | solution.py:215
  281.0 10.6 %collective-permute-start.29 = (bf16[256,512]{1,0:T(8,128)(2,1)S(1)}, bf16[256,512]{1,0:T(8,128)(2,1)S(1)}, u32[]{:S(2)}, u32[]{:S(2)}) collective-permute-start(bf16[256,512]{1,0:T(8,128)(2,1)S(1)} %get-tuple-element.55), channel_id=1, source_target_pairs={{0,3},{1,0},{2,1},{3,2},{4,7},{5,4},{6,5},{7,6},{8,11},{9,8},{10,9... | collective-permute-start | bytes 786440 | tf_op jit(solution)/shard_map/ppermute | solution.py:173
  281.0 8.6 %collective-permute-start.27 = (bf16[256,512]{1,0:T(8,128)(2,1)S(1)}, bf16[256,512]{1,0:T(8,128)(2,1)S(1)}, u32[]{:S(2)}, u32[]{:S(2)}) collective-permute-start(bf16[256,512]{1,0:T(8,128)(2,1)S(1)} %get-tuple-element.55), channel_id=1, source_target_pairs={{0,1},{1,2},{2,3},{3,0},{4,5},{5,6},{6,7},{7,4},{8,9},{9,10},{10,1... | collective-permute-start | bytes 786440 | tf_op jit(solution)/shard_map/ppermute | solution.py:173
  281.5 12.2 %collective-permute-start.28 = (bf16[256,512]{1,0:T(8,128)(2,1)S(1)}, bf16[256,512]{1,0:T(8,128)(2,1)S(1)}, u32[]{:S(2)}, u32[]{:S(2)}) collective-permute-start(bf16[256,512]{1,0:T(8,128)(2,1)S(1)} %get-tuple-element.55), channel_id=1, source_target_pairs={{0,2},{1,3},{2,0},{3,1},{4,6},{5,7},{6,4},{7,5},{8,10},{9,11},{10,... | collective-permute-start | bytes 786440 | tf_op jit(solution)/shard_map/ppermute | solution.py:173
  297.0 12.0 %copy-start.13 = (f32[512]{0:T(512)S(1)}, f32[512]{0:T(512)}, u32[]{:S(2)}) copy-start(f32[512]{0:T(512)} %param.33) | copy-start | bytes 6148
  297.0 12.0 %copy-start.14 = (f32[512]{0:T(512)S(1)}, f32[512]{0:T(512)}, u32[]{:S(2)}) copy-start(f32[512]{0:T(512)} %param.32) | copy-start | bytes 6148
  300.1 13.1 %copy-start.1 = (bf16[512,2048]{1,0:T(8,128)(2,1)S(1)}, bf16[512,2048]{1,0:T(8,128)(2,1)}, u32[]{:S(2)}) copy-start(bf16[512,2048]{1,0:T(8,128)(2,1)} %param.24) | copy-start | bytes 6291460
  (2 other events, 2.9 us)
Sparse Core Ops, SparseCore 0:
  100.2 40.3 all-gather.4
  142.1 28.5 all-gather.8
  172.2 40.4 all-gather.6
  214.1 28.5 all-gather.10

commit v11 on v10

--- a/solution.py
+++ b/solution.py
@@ -99,7 +99,7 @@
     )(length.reshape(1), queries, cache_k, cache_v, new_k, new_v)
 
 
-def dense_experts(moe_in, expert_ids, route_weights, expert_gate_up, down_full, here, experts_all):
+def dense_experts(moe_in, expert_ids, route_weights, expert_gate_up, down_full, qkv_flat, here, experts_all):
     local_experts = expert_gate_up.shape[0]
     hidden_quarter = expert_gate_up.shape[2] // 2
     tokens, quarter = moe_in.shape
@@ -115,7 +115,7 @@
     info = jnp.concatenate([gate_hi, gate_lo], axis=0).reshape(-1, quarter)
     packed = jnp.concatenate([moe_in, info], axis=0)
     ring = ring_order(seq_count)
-    offsets, blocks = ring_all_gather(packed, ring)
+    offsets, blocks, (expert_gate_up, qkv_flat) = ring_all_gather(packed, ring, (expert_gate_up, qkv_flat))
     first = min(len(blocks), 5)
     chunks = [(0, first), (first, len(blocks))] if first < len(blocks) else [(0, first)]
     outputs = []
@@ -143,7 +143,7 @@
         for i in range(part.shape[0]):
             by_offset[offsets[index]] = part[i]
             index += 1
-    return ring_reduce_scatter(by_offset, ring)
+    return ring_reduce_scatter(by_offset, ring), qkv_flat
 
 
 def permute_reduce_scatter(term, width):
@@ -186,7 +186,7 @@
     return [2 * i for i in range(half)] + [2 * i + 1 for i in reversed(range(half))]
 
 
-def ring_all_gather(block, cycle):
+def ring_all_gather(block, cycle, riders):
     count = len(cycle)
     forward = [(cycle[p], cycle[(p + 1) % count]) for p in range(count)]
     backward = [(cycle[p], cycle[(p - 1) % count]) for p in range(count)]
@@ -200,7 +200,10 @@
             behind = lax.ppermute(behind, "seq", backward)
             offsets.append(step)
             blocks.append(behind)
-    return offsets, blocks
+        if step == 1:
+            ahead, behind, riders = lax.optimization_barrier((ahead, behind, riders))
+            blocks[1:] = [ahead, behind][: len(blocks) - 1]
+    return offsets, blocks, riders
 
 
 def ring_reduce_scatter(by_offset, cycle):
@@ -314,9 +317,7 @@
         new_values,
     )
     if dense:
-        attended, down_full, gate_up_flat, qkv_flat = lax.optimization_barrier(
-            (attended, down_full, gate_up_flat, qkv_flat)
-        )
+        attended, down_full = lax.optimization_barrier((attended, down_full))
     else:
         gate_up_flat = expert_gate_up
         qkv_flat = qkv_proj.reshape(D, -1)
@@ -332,8 +333,8 @@
         jnp.bfloat16
     )
     if dense:
-        moe_term = dense_experts(
-            moe_in, expert_ids, route_weights, gate_up_flat, down_full, here, experts_all
+        moe_term, qkv_flat = dense_experts(
+            moe_in, expert_ids, route_weights, gate_up_flat, down_full, qkv_flat, here, experts_all
         )
     else:
         moe_term = dispatch_experts(

time: 321 us -> 320 us (level)
  starting transfers between devices: 34.7 us -> 30.3 us
    ppermute x3, waiting for transfers between devices: 0.01 us -> 9.03 us  [body(): pieces.append(lax.ppermute(piece, 'tp', pairs))]
    ppermute x4, waiting for transfers between devices: 21.5 us -> 15.8 us  [ring_all_gather(): ahead = lax.ppermute(ahead, 'seq', forward)]
where the time goes in v11:
time: 320 us; the launch traced here: 319 us
  waiting for transfers between devices  165 us (52%)
  local copies, waits for them, and re-layouts  34.7 us (11%)
  matrix products  34.3 us (11%)
  starting transfers between devices  30.3 us (9%)
  other arithmetic  14.8 us (5%)
  Pallas kernels  14.2 us (4%)
  between operations  14.2 us (4%)
  blocking collectives  11.8 us (4%)
    all_gather x2, waiting for transfers between devices, dense_experts(): weighted = lax.all_gather(weighted, 'tp', axis=2, tiled=True)  49.9 us
    all_gather x2, waiting for transfers between devices, dense_experts(): rows = lax.all_gather(rows_q, 'tp', axis=1, tiled=True)  42.7 us
    ppermute x14, waiting for transfers between devices, ring_reduce_scatter(): received = lax.ppermute(acc.astype(jnp.bfloat16), 'seq', pairs)  27.6 us
    ppermute x4, waiting for transfers between devices, ring_all_gather(): ahead = lax.ppermute(ahead, 'seq', forward)  15.8 us
    dot_general x2, matrix products, dense_experts(): jnp.einsum('td,edf->etf', rows, expert_gate_up, preferred_element_type=jn...  15.2 us
    ppermute x14, starting transfers between devices, ring_reduce_scatter(): received = lax.ppermute(acc.astype(jnp.bfloat16), 'seq', pairs)  14.7 us
    pallas_call x1, Pallas kernels, flash_attention(): pl.pallas_call(kernel, grid_spec=grid_spec, out_shape=jax.ShapeDtypeStruc...  14.2 us
    unnamed x41, local copies, waits for them, and re-layouts  12.9 us
  transfers between devices with their start and end apart: 34, of which 25 were waited for; matrix products, arithmetic and copies ran while one was open for 17% of the time, Pallas kernels for 4%

profile of v11, /device:TPU:0, one launch (start us, length us, event | category | flops | bytes accessed | tf_op | source)
XLA Modules:
  0.0 319.2 jit_solution(13474959187093504050)
XLA Ops:
  7.3 2.9 dynamic-slice_bitcast_fusion
  10.2 2.4 collective-permute-start.2
  13.9 14.2 %shard_map.192 = bf16[256,512]{1,0:T(8,128)(2,1)} custom-call(s32[1]{0:T(128)} %dynamic_slice.50.len_ref, bf16[256,512]{1,0:T(8,128)(2,1)} %q_ref.1, bf16[4096,512]{1,0:T(8,128)(2,1)} %bitcast.112, bf16[4096,512]{1,0:T(8,128)(2,1)} %bitcast.113, bf16[256,512]{1,0:T(8,128)(2,1)} %nk_ref.1, bf16[256,512]{1,0:T(8,128)(2,1)} %nv_ref.1), custom_call_target="tpu_custom_call" | custom-call | tf_op jit(solution)/shard_map/pallas_call | solution.py:94
  28.2 9.0 %collective-permute-done.1 = bf16[2,256,512]{2,1,0:T(8,128)(2,1)} collective-permute-done((bf16[2,256,512]{2,1,0:T(8,128)(2,1)}, bf16[2,256,512]{2,1,0:T(8,128)(2,1)}, u32[]{:S(2)}, u32[]{:S(2)}) %collective-permute-start.1) | collective-permute-done | bytes 524320 | tf_op jit(solution)/shard_map/ppermute | solution.py:300
  37.3 2.8 pad_maximum_fusion
  40.1 3.6 %gather_fusion = bf16[4,2,256,512]{3,2,1,0:T(8,128)(2,1)} fusion(bf16[4,2,256,512]{3,2,1,0:T(8,128)(2,1)} %pad_maximum_fusion, s32[1024]{0:T(1024)S(1)} %pad_clamp_fusion), kind=kCustom, calls=%fused_computation | custom fusion | bytes 4194320 | tf_op jit(solution)/shard_map/jit(_take)/gather | solution.py:302
  43.7 1.9 select_bitcast_fusion
  45.6 1.6 copy.67
  49.4 1.7 collective-permute-start.4
  51.3 3.6 %collective-permute-done.5 = bf16[256,512]{1,0:T(8,128)(2,1)S(1)} collective-permute-done((bf16[256,512]{1,0:T(8,128)(2,1)S(1)}, bf16[256,512]{1,0:T(8,128)(2,1)S(1)}, u32[]{:S(2)}, u32[]{:S(2)}) %collective-permute-start.5) | collective-permute-done | bytes 262176 | tf_op jit(solution)/shard_map/ppermute | solution.py:157
  54.9 8.9 %collective-permute-done.4 = bf16[256,512]{1,0:T(8,128)(2,1)S(1)} collective-permute-done((bf16[256,512]{1,0:T(8,128)(2,1)S(1)}, bf16[256,512]{1,0:T(8,128)(2,1)S(1)}, u32[]{:S(2)}, u32[]{:S(2)}) %collective-permute-start.4) | collective-permute-done | bytes 262176 | tf_op jit(solution)/shard_map/ppermute | solution.py:157
  65.0 5.8 %psum.28 = f32[256]{0:T(256)S(1)} all-reduce(f32[256]{0:T(256)S(1)} %get-tuple-element.33), channel_id=1, replica_groups=mesh['seq'=8,'tp'=4] {'tp'}, use_global_device_ids=true, to_apply=%region_1.2 | all-reduce | flops 256 | bytes 2048 | tf_op jit(solution)/shard_map/psum | solution.py:331
  71.0 1.8 collective-permute-start.6
  73.1 7.6 %reshape.134 = bf16[2,2048,512]{2,1,0:T(8,128)(2,1)} reshape(bf16[2,2048,2,256]{3,2,1,0:T(2,128)(2,1)} %param.28) | data formatting | bytes 8388608 | tf_op jit(solution)/shard_map/reshape | solution.py:304
  80.7 8.8 %copy.68 = bf16[2048,3,512]{0,2,1:T(8,128)(2,1)} copy(bf16[2048,3,512]{2,0,1:T(8,128)(2,1)} %param.31) | data formatting | bytes 12582912 | tf_op args[14]
  89.6 1.8 collective-permute-start.8
  91.8 5.6 %collective-permute-done.8 = bf16[272,512]{1,0:T(8,128)(2,1)S(1)} collective-permute-done((bf16[272,512]{1,0:T(8,128)(2,1)S(1)}, bf16[272,512]{1,0:T(8,128)(2,1)S(1)}, u32[]{:S(2)}, u32[]{:S(2)}) %collective-permute-start.8) | collective-permute-done | bytes 278560 | tf_op jit(solution)/shard_map/ppermute | solution.py:196
  100.2 1.6 collective-permute-start.12
  102.3 5.2 %collective-permute-done.12 = bf16[272,512]{1,0:T(8,128)(2,1)S(1)} collective-permute-done((bf16[272,512]{1,0:T(8,128)(2,1)S(1)}, bf16[272,512]{1,0:T(8,128)(2,1)S(1)}, u32[]{:S(2)}, u32[]{:S(2)}) %collective-permute-start.12) | collective-permute-done | bytes 278560 | tf_op jit(solution)/shard_map/ppermute | solution.py:196
  107.5 1.6 collective-permute-start.14
  109.1 5.0 %collective-permute-done.14 = bf16[272,512]{1,0:T(8,128)(2,1)S(1)} collective-permute-done((bf16[272,512]{1,0:T(8,128)(2,1)S(1)}, bf16[272,512]{1,0:T(8,128)(2,1)S(1)}, u32[]{:S(2)}, u32[]{:S(2)}) %collective-permute-start.14) | collective-permute-done | bytes 278560 | tf_op jit(solution)/shard_map/ppermute | solution.py:196
  116.4 23.7 %all-gather.5.cloned.1.call-done = bf16[1280,2048]{1,0:T(8,128)(2,1)} async-done(((bf16[1280,512]{1,0:T(8,128)(2,1)}), bf16[1280,2048]{1,0:T(8,128)(2,1)}) %all-gather.5.cloned.1.call-update) | async-done | bytes 5242896 | tf_op jit(solution)/shard_map/all_gather | solution.py:130
  140.0 9.0 %fusion.2 = f32[2,1280,512]{1,2,0:T(8,128)S(1)} fusion(bf16[2,2048,512]{2,1,0:T(8,128)(2,1)} %reshape.134, bf16[1280,2048]{1,0:T(8,128)(2,1)} %all-gather.5.cloned.1.call-done), kind=kOutput, calls=%fused_computation.3 | convolution fusion | flops 5368709120 | bytes 14680064 | tf_op jit(solution)/shard_map/td,edf->etf/dot_general | solution.py:131
  149.1 1.9 multiply_convert_fusion
  151.1 19.0 %all-gather.9.cloned.1.call-done = bf16[768,2048]{1,0:T(8,128)(2,1)} async-done(((bf16[768,512]{1,0:T(8,128)(2,1)}), bf16[768,2048]{1,0:T(8,128)(2,1)}) %all-gather.9.cloned.1.call-update) | async-done | bytes 3145744 | tf_op jit(solution)/shard_map/all_gather | solution.py:130
  170.2 6.2 %fusion.10 = f32[2,768,512]{1,2,0:T(8,128)S(1)} fusion(bf16[2,2048,512]{2,1,0:T(8,128)(2,1)} %reshape.134, bf16[768,2048]{1,0:T(8,128)(2,1)} %all-gather.9.cloned.1.call-done), kind=kOutput, calls=%fused_computation.16 | convolution fusion | flops 3221225472 | bytes 10485760 | tf_op jit(solution)/shard_map/td,edf->etf/dot_general | solution.py:131
  177.8 34.4 %all-gather.7.cloned.1.call-done = bf16[2,1280,1024]{1,2,0:T(8,128)(2,1)} async-done(((bf16[2,1280,256]{1,2,0:T(8,128)(2,1)}), bf16[2,1280,1024]{1,2,0:T(8,128)(2,1)}) %all-gather.7.cloned.1.call-update) | async-done | bytes 5242896 | tf_op jit(solution)/shard_map/all_gather | solution.py:135
  212.2 5.4 %fusion.7 = bf16[1280,512]{1,0:T(8,128)(2,1)S(1)} fusion(bf16[2,1280,1024]{1,2,0:T(8,128)(2,1)} %all-gather.7.cloned.1.call-done, bf16[2,1024,512]{2,1,0:T(8,128)(2,1)S(1)} %bitcast.109), kind=kOutput, calls=%fused_computation.7 | convolution fusion | flops 2685009920 | bytes 8650752 | tf_op jit(solution)/shard_map/etf,efd->td/dot_general | solution.py:136
  217.7 1.5 collective-permute-start.10
  219.7 3.6 %collective-permute-done.10 = bf16[256,256]{1,0:T(8,128)(2,1)S(1)} collective-permute-done((bf16[256,256]{1,0:T(8,128)(2,1)S(1)}, bf16[256,256]{1,0:T(8,128)(2,1)S(1)}, u32[]{:S(2)}, u32[]{:S(2)}) %collective-permute-start.10) | collective-permute-done | bytes 131104 | tf_op jit(solution)/shard_map/ppermute | solution.py:218
  226.7 15.5 %all-gather.11.cloned.1.call-done = bf16[2,768,1024]{1,2,0:T(8,128)(2,1)} async-done(((bf16[2,768,256]{1,2,0:T(8,128)(2,1)}), bf16[2,768,1024]{1,2,0:T(8,128)(2,1)}) %all-gather.11.cloned.1.call-update) | async-done | bytes 3145744 | tf_op jit(solution)/shard_map/all_gather | solution.py:135
  242.2 3.7 %bitcast_convert_fusion = bf16[768,512]{1,0:T(8,128)(2,1)S(1)} fusion(bf16[2,768,1024]{1,2,0:T(8,128)(2,1)} %all-gather.11.cloned.1.call-done, bf16[2,1024,512]{2,1,0:T(8,128)(2,1)S(1)} %bitcast.110), kind=kOutput, calls=%fused_computation.19 | convolution fusion | flops 1611005952 | bytes 6029312 | tf_op jit(solution)/shard_map/etf,efd->td/dot_general | solution.py:136
  248.1 3.6 %collective-permute-done.15 = bf16[256,256]{1,0:T(8,128)(2,1)S(1)} collective-permute-done((bf16[256,256]{1,0:T(8,128)(2,1)S(1)}, bf16[256,256]{1,0:T(8,128)(2,1)S(1)}, u32[]{:S(2)}, u32[]{:S(2)}) %collective-permute-start.15) | collective-permute-done | bytes 131104 | tf_op jit(solution)/shard_map/ppermute | solution.py:218
  255.1 2.9 collective-permute-done.16
  261.7 2.9 collective-permute-done.17
  266.2 2.2 collective-permute-start.18
  268.4 3.5 %collective-permute-done.18 = bf16[256,256]{1,0:T(8,128)(2,1)S(1)} collective-permute-done((bf16[256,256]{1,0:T(8,128)(2,1)S(1)}, bf16[256,256]{1,0:T(8,128)(2,1)S(1)}, u32[]{:S(2)}, u32[]{:S(2)}) %collective-permute-start.18) | collective-permute-done | bytes 131104 | tf_op jit(solution)/shard_map/ppermute | solution.py:218
  271.9 2.1 collective-permute-done.25
  276.2 2.9 collective-permute-done.19
  280.5 1.7 collective-permute-start.29
  282.8 5.5 %collective-permute-done.27 = bf16[256,512]{1,0:T(8,128)(2,1)S(1)} collective-permute-done((bf16[256,512]{1,0:T(8,128)(2,1)S(1)}, bf16[256,512]{1,0:T(8,128)(2,1)S(1)}, u32[]{:S(2)}, u32[]{:S(2)}) %collective-permute-start.27) | collective-permute-done | bytes 262176 | tf_op jit(solution)/shard_map/ppermute | solution.py:173
  288.3 2.0 fusion.17
  290.3 2.0 convolution_add_fusion.1
  292.4 2.0 fusion.14
  294.8 3.3 %fusion.8 = f32[256,1536]{1,0:T(8,128)} fusion(f32[256,1536]{1,0:T(8,128)S(1)} %fusion.14, f32[256,1536]{1,0:T(8,128)S(1)} %convolution_add_fusion.1, bf16[256,512]{1,0:T(8,128)(2,1)S(1)} %collective-permute-done.28, bf16[2048,1536]{0,1:T(8,128)(2,1)} %bitcast.106, s32[]{:T(128)S(6)} %select_n.126), kind=kOutput, calls=%fused_computation.9 | convolution fusion | flops 403439616 | bytes 6553604 | tf_op jit(solution)/shard_map/dot_general | solution.py:174
  298.0 3.1 copy.79
  302.6 5.9 %all-reduce = (f32[256]{0:T(256)S(1)}, f32[256]{0:T(256)S(1)}, f32[256]{0:T(256)S(1)}) all-reduce(f32[256]{0:T(256)S(1)} %get-tuple-element.29, f32[256]{0:T(256)S(1)} %get-tuple-element.57, f32[256]{0:T(256)S(1)} %get-tuple-element.28), channel_id=1, replica_groups=mesh['seq'=8,'tp'=4] {'tp'}, use_global_device_ids=true, to_apply=%region_6.7 | all-reduce | flops 768 | bytes 6144 | tf_op jit(solution)/shard_map/psum | solution.py:357
  308.5 1.6 fusion.21
  (122 shorter events, 36.1 us)
Async XLA Ops:
  7.2 40.0 %copy-start = (bf16[512,2048]{1,0:T(8,128)(2,1)S(1)}, bf16[512,2048]{1,0:T(8,128)(2,1)}, u32[]{:S(2)}) copy-start(bf16[512,2048]{1,0:T(8,128)(2,1)} %param.24) | copy-start | bytes 6291460
  7.2 132.9 %all-gather.5.cloned.1.call-start = ((), (), s32[]{:S(2)}) async-start(), calls=%async_computation | async-start | bytes 6553600 | tf_op jit(solution)/shard_map/all_gather | solution.py:130
  7.3 6.1 %copy-start.15 = (s32[8]{0:T(128)S(1)}, s32[8]{0:T(128)}, u32[]{:S(2)}) copy-start(s32[8]{0:T(128)} %param.23) | copy-start | bytes 100
  10.2 18.1 %collective-permute-start.2 = (bf16[2,256,512]{2,1,0:T(8,128)(2,1)}, bf16[2,256,512]{2,1,0:T(8,128)(2,1)S(1)}, u32[]{:S(2)}, u32[]{:S(2)}) collective-permute-start(bf16[2,256,512]{2,1,0:T(8,128)(2,1)} %get-tuple-element.42), channel_id=1, source_target_pairs={{0,3},{1,0},{2,1},{3,2},{4,7},{5,4},{6,5},{7,6},{8,11},{9,8},{10,9... | collective-permute-start | bytes 1572872 | tf_op jit(solution)/shard_map/ppermute | solution.py:300
  12.6 24.7 %collective-permute-start.1 = (bf16[2,256,512]{2,1,0:T(8,128)(2,1)}, bf16[2,256,512]{2,1,0:T(8,128)(2,1)}, u32[]{:S(2)}, u32[]{:S(2)}) collective-permute-start(bf16[2,256,512]{2,1,0:T(8,128)(2,1)} %get-tuple-element.43), channel_id=1, source_target_pairs={{0,2},{1,3},{2,0},{3,1},{4,6},{5,7},{6,4},{7,5},{8,10},{9,11},{10,... | collective-permute-start | bytes 1572872 | tf_op jit(solution)/shard_map/ppermute | solution.py:300
  13.1 24.1 %collective-permute-start = (bf16[2,256,512]{2,1,0:T(8,128)(2,1)}, bf16[2,256,512]{2,1,0:T(8,128)(2,1)}, u32[]{:S(2)}, u32[]{:S(2)}) collective-permute-start(bf16[2,256,512]{2,1,0:T(8,128)(2,1)} %get-tuple-element.41), channel_id=1, source_target_pairs={{0,1},{1,2},{2,3},{3,0},{4,5},{5,6},{6,7},{7,4},{8,9},{9,10},{10,1... | collective-permute-start | bytes 1572872 | tf_op jit(solution)/shard_map/ppermute | solution.py:300
  13.9 14.2 %copy-start.9 = (f32[256,8]{0,1:T(8,128)S(1)}, f32[256,8]{0,1:T(8,128)}, u32[]{:S(2)}) copy-start(f32[256,8]{0,1:T(8,128)} %param.27) | copy-start | bytes 24580
  13.9 14.3 %copy-start.10 = (s32[256,8]{0,1:T(8,128)S(1)}, s32[256,8]{0,1:T(8,128)}, u32[]{:S(2)}) copy-start(s32[256,8]{0,1:T(8,128)} %param.26) | copy-start | bytes 24580
  47.2 16.6 %copy-start.8 = (bf16[256,512]{1,0:T(8,128)(2,1)S(1)}, bf16[256,512]{1,0:T(8,128)(2,1)}, u32[]{:S(2)}) copy-start(bf16[256,512]{1,0:T(8,128)(2,1)} %param.17) | copy-start | bytes 786436
  49.2 21.6 %copy-start.11 = (f32[512]{0:T(512)S(1)}, f32[512]{0:T(512)}, u32[]{:S(2)}) copy-start(f32[512]{0:T(512)} %param.25) | copy-start | bytes 6148
  49.3 5.5 %collective-permute-start.5 = (bf16[256,512]{1,0:T(8,128)(2,1)S(1)}, bf16[256,512]{1,0:T(8,128)(2,1)S(1)}, u32[]{:S(2)}, u32[]{:S(2)}) collective-permute-start(bf16[256,512]{1,0:T(8,128)(2,1)S(1)} %get-tuple-element.38), channel_id=1, source_target_pairs={{0,3},{1,0},{2,1},{3,2},{4,7},{5,4},{6,5},{7,6},{8,11},{9,8},{10,9... | collective-permute-start | bytes 786440 | tf_op jit(solution)/shard_map/ppermute | solution.py:157
  49.4 14.3 %collective-permute-start.4 = (bf16[256,512]{1,0:T(8,128)(2,1)S(1)}, bf16[256,512]{1,0:T(8,128)(2,1)S(1)}, u32[]{:S(2)}, u32[]{:S(2)}) collective-permute-start(bf16[256,512]{1,0:T(8,128)(2,1)S(1)} %get-tuple-element.39), channel_id=1, source_target_pairs={{0,2},{1,3},{2,0},{3,1},{4,6},{5,7},{6,4},{7,5},{8,10},{9,11},{10,... | collective-permute-start | bytes 786440 | tf_op jit(solution)/shard_map/ppermute | solution.py:157
  51.1 12.6 %collective-permute-start.3 = (bf16[256,512]{1,0:T(8,128)(2,1)S(1)}, bf16[256,512]{1,0:T(8,128)(2,1)S(1)}, u32[]{:S(2)}, u32[]{:S(2)}) collective-permute-start(bf16[256,512]{1,0:T(8,128)(2,1)S(1)} %get-tuple-element.37), channel_id=1, source_target_pairs={{0,1},{1,2},{2,3},{3,0},{4,5},{5,6},{6,7},{7,4},{8,9},{9,10},{10,1... | collective-permute-start | bytes 786440 | tf_op jit(solution)/shard_map/ppermute | solution.py:157
  71.0 18.6 %collective-permute-start.6 = (bf16[272,512]{1,0:T(8,128)(2,1)S(1)}, bf16[272,512]{1,0:T(8,128)(2,1)S(1)}, u32[]{:S(2)}, u32[]{:S(2)}) collective-permute-start(bf16[272,512]{1,0:T(8,128)(2,1)S(1)} %pad_maximum_fusion.2), channel_id=1, source_target_pairs={{0,8},{8,16},{16,24},{24,28},{28,20},{20,12},{12,4},{4,0},{1,9},{9... | collective-permute-start | bytes 835592 | tf_op jit(solution)/shard_map/ppermute | solution.py:196
  72.9 16.7 %collective-permute-start.7 = (bf16[272,512]{1,0:T(8,128)(2,1)S(1)}, bf16[272,512]{1,0:T(8,128)(2,1)S(1)}, u32[]{:S(2)}, u32[]{:S(2)}) collective-permute-start(bf16[272,512]{1,0:T(8,128)(2,1)S(1)} %pad_maximum_fusion.2), channel_id=1, source_target_pairs={{0,4},{8,0},{16,8},{24,16},{28,24},{20,28},{12,20},{4,12},{1,5},{9... | collective-permute-start | bytes 835592 | tf_op jit(solution)/shard_map/ppermute | solution.py:200
  89.6 7.8 %collective-permute-start.8 = (bf16[272,512]{1,0:T(8,128)(2,1)S(1)}, bf16[272,512]{1,0:T(8,128)(2,1)S(1)}, u32[]{:S(2)}, u32[]{:S(2)}) collective-permute-start(bf16[272,512]{1,0:T(8,128)(2,1)S(1)} %collective-permute-done.6), channel_id=1, source_target_pairs={{0,8},{8,16},{16,24},{24,28},{28,20},{20,12},{12,4},{4,0},{1,9},{9... | collective-permute-start | bytes 835592 | tf_op jit(solution)/shard_map/ppermute | solution.py:196
  91.4 7.3 %collective-permute-start.9 = (bf16[272,512]{1,0:T(8,128)(2,1)S(1)}, bf16[272,512]{1,0:T(8,128)(2,1)S(1)}, u32[]{:S(2)}, u32[]{:S(2)}) collective-permute-start(bf16[272,512]{1,0:T(8,128)(2,1)S(1)} %collective-permute-done.7), channel_id=1, source_target_pairs={{0,4},{8,0},{16,8},{24,16},{28,24},{20,28},{12,20},{4,12},{1,5},{9... | collective-permute-start | bytes 835592 | tf_op jit(solution)/shard_map/ppermute | solution.py:200
  98.8 15.2 %copy-start.4 = (bf16[5,272,512]{2,1,0:T(8,128)(2,1)}, bf16[5,272,512]{2,1,0:T(8,128)(2,1)S(1)}, u32[]{:S(2)}) copy-start(bf16[5,272,512]{2,1,0:T(8,128)(2,1)S(1)} %bitcast_dynamic-update-slice_fusion) | copy-start | bytes 4177924
  100.1 70.0 %all-gather.9.cloned.1.call-start = ((), (), s32[]{:S(2)}) async-start(), calls=%async_computation.2 | async-start | bytes 3932160 | tf_op jit(solution)/shard_map/all_gather | solution.py:130
  100.2 7.3 %collective-permute-start.12 = (bf16[272,512]{1,0:T(8,128)(2,1)S(1)}, bf16[272,512]{1,0:T(8,128)(2,1)S(1)}, u32[]{:S(2)}, u32[]{:S(2)}) collective-permute-start(bf16[272,512]{1,0:T(8,128)(2,1)S(1)} %collective-permute-done.8), channel_id=1, source_target_pairs={{0,8},{8,16},{16,24},{24,28},{28,20},{20,12},{12,4},{4,0},{1,9},{9... | collective-permute-start | bytes 835592 | tf_op jit(solution)/shard_map/ppermute | solution.py:196
  101.8 7.2 %collective-permute-start.13 = (bf16[272,512]{1,0:T(8,128)(2,1)S(1)}, bf16[272,512]{1,0:T(8,128)(2,1)S(1)}, u32[]{:S(2)}, u32[]{:S(2)}) collective-permute-start(bf16[272,512]{1,0:T(8,128)(2,1)S(1)} %collective-permute-done.9), channel_id=1, source_target_pairs={{0,4},{8,0},{16,8},{24,16},{28,24},{20,28},{12,20},{4,12},{1,5},{9... | collective-permute-start | bytes 835592 | tf_op jit(solution)/shard_map/ppermute | solution.py:200
  107.5 6.5 %collective-permute-start.14 = (bf16[272,512]{1,0:T(8,128)(2,1)S(1)}, bf16[272,512]{1,0:T(8,128)(2,1)S(1)}, u32[]{:S(2)}, u32[]{:S(2)}) collective-permute-start(bf16[272,512]{1,0:T(8,128)(2,1)S(1)} %collective-permute-done.12), channel_id=1, source_target_pairs={{0,8},{8,16},{16,24},{24,28},{28,20},{20,12},{12,4},{4,0},{1,9},{9... | collective-permute-start | bytes 835592 | tf_op jit(solution)/shard_map/ppermute | solution.py:196
  115.1 97.1 %all-gather.7.cloned.1.call-start = ((), (), s32[]{:S(2)}) async-start(), calls=%async_computation.1 | async-start | bytes 6553600 | tf_op jit(solution)/shard_map/all_gather | solution.py:135
  151.0 91.2 %all-gather.11.cloned.1.call-start = ((), (), s32[]{:S(2)}) async-start(), calls=%async_computation.3 | async-start | bytes 3932160 | tf_op jit(solution)/shard_map/all_gather | solution.py:135
  176.4 35.8 %copy-start.2 = (bf16[2,4,256,512]{3,2,1,0:T(8,128)(2,1)S(1)}, bf16[2,4,256,512]{3,2,1,0:T(8,128)(2,1)}, u32[]{:S(2)}) copy-start(bf16[2,4,256,512]{3,2,1,0:T(8,128)(2,1)} %copy.67) | copy-start | bytes 6291460
  217.6 7.0 %copy-start.5 = (bf16[1280,512]{1,0:T(8,128)(2,1)}, bf16[1280,512]{1,0:T(8,128)(2,1)S(1)}, u32[]{:S(2)}) copy-start(bf16[1280,512]{1,0:T(8,128)(2,1)S(1)} %fusion.7) | copy-start | bytes 3932164
  217.7 5.7 %collective-permute-start.10 = (bf16[256,256]{1,0:T(8,128)(2,1)S(1)}, bf16[256,256]{1,0:T(8,128)(2,1)S(1)}, u32[]{:S(2)}, u32[]{:S(2)}) collective-permute-start(bf16[256,256]{1,0:T(8,128)(2,1)S(1)} %get-tuple-element.55), channel_id=1, source_target_pairs={{0,8},{8,16},{16,24},{24,28},{28,20},{20,12},{12,4},{4,0},{1,9},{9... | collective-permute-start | bytes 393224 | tf_op jit(solution)/shard_map/ppermute | solution.py:218
  219.2 5.4 %collective-permute-start.20 = (bf16[256,256]{1,0:T(8,128)(2,1)S(1)}, bf16[256,256]{1,0:T(8,128)(2,1)S(1)}, u32[]{:S(2)}, u32[]{:S(2)}) collective-permute-start(bf16[256,256]{1,0:T(8,128)(2,1)S(1)} %get-tuple-element.56), channel_id=1, source_target_pairs={{0,4},{8,0},{16,8},{24,16},{28,24},{20,28},{12,20},{4,12},{1,5},{9... | collective-permute-start | bytes 393224 | tf_op jit(solution)/shard_map/ppermute | solution.py:218
  224.7 21.3 %collective-permute-start.11 = (bf16[256,256]{1,0:T(8,128)(2,1)S(1)}, bf16[256,256]{1,0:T(8,128)(2,1)S(1)}, u32[]{:S(2)}, u32[]{:S(2)}) collective-permute-start(bf16[256,256]{1,0:T(8,128)(2,1)S(1)} %get-tuple-element.53), channel_id=1, source_target_pairs={{0,8},{8,16},{16,24},{24,28},{28,20},{20,12},{12,4},{4,0},{1,9},{9... | collective-permute-start | bytes 393224 | tf_op jit(solution)/shard_map/ppermute | solution.py:218
  226.2 19.7 %collective-permute-start.21 = (bf16[256,256]{1,0:T(8,128)(2,1)S(1)}, bf16[256,256]{1,0:T(8,128)(2,1)S(1)}, u32[]{:S(2)}, u32[]{:S(2)}) collective-permute-start(bf16[256,256]{1,0:T(8,128)(2,1)S(1)} %get-tuple-element.54), channel_id=1, source_target_pairs={{0,4},{8,0},{16,8},{24,16},{28,24},{20,28},{12,20},{4,12},{1,5},{9... | collective-permute-start | bytes 393224 | tf_op jit(solution)/shard_map/ppermute | solution.py:218
  245.9 20.2 %copy-start.6 = (bf16[1280,512]{1,0:T(8,128)(2,1)S(1)}, bf16[1280,512]{1,0:T(8,128)(2,1)}, u32[]{:S(2)}) copy-start(bf16[1280,512]{1,0:T(8,128)(2,1)} %copy-done.5) | copy-start | bytes 3932164
  246.0 5.7 %collective-permute-start.15 = (bf16[256,256]{1,0:T(8,128)(2,1)S(1)}, bf16[256,256]{1,0:T(8,128)(2,1)S(1)}, u32[]{:S(2)}, u32[]{:S(2)}) collective-permute-start(bf16[256,256]{1,0:T(8,128)(2,1)S(1)} %get-tuple-element.64), channel_id=1, source_target_pairs={{0,8},{8,16},{16,24},{24,28},{28,20},{20,12},{12,4},{4,0},{1,9},{9... | collective-permute-start | bytes 393224 | tf_op jit(solution)/shard_map/ppermute | solution.py:218
  247.6 32.2 %copy-start.12 = (f32[512]{0:T(512)S(1)}, f32[512]{0:T(512)}, u32[]{:S(2)}) copy-start(f32[512]{0:T(512)} %param.30) | copy-start | bytes 6148
  247.6 5.4 %collective-permute-start.22 = (bf16[256,256]{1,0:T(8,128)(2,1)S(1)}, bf16[256,256]{1,0:T(8,128)(2,1)S(1)}, u32[]{:S(2)}, u32[]{:S(2)}) collective-permute-start(bf16[256,256]{1,0:T(8,128)(2,1)S(1)} %get-tuple-element.65), channel_id=1, source_target_pairs={{0,4},{8,0},{16,8},{24,16},{28,24},{20,28},{12,20},{4,12},{1,5},{9... | collective-permute-start | bytes 393224 | tf_op jit(solution)/shard_map/ppermute | solution.py:218
  253.0 5.0 %collective-permute-start.16 = (bf16[256,256]{1,0:T(8,128)(2,1)S(1)}, bf16[256,256]{1,0:T(8,128)(2,1)S(1)}, u32[]{:S(2)}, u32[]{:S(2)}) collective-permute-start(bf16[256,256]{1,0:T(8,128)(2,1)S(1)} %get-tuple-element.62), channel_id=1, source_target_pairs={{0,8},{8,16},{16,24},{24,28},{28,20},{20,12},{12,4},{4,0},{1,9},{9... | collective-permute-start | bytes 393224 | tf_op jit(solution)/shard_map/ppermute | solution.py:218
  254.5 5.0 %collective-permute-start.23 = (bf16[256,256]{1,0:T(8,128)(2,1)S(1)}, bf16[256,256]{1,0:T(8,128)(2,1)S(1)}, u32[]{:S(2)}, u32[]{:S(2)}) collective-permute-start(bf16[256,256]{1,0:T(8,128)(2,1)S(1)} %get-tuple-element.63), channel_id=1, source_target_pairs={{0,4},{8,0},{16,8},{24,16},{28,24},{20,28},{12,20},{4,12},{1,5},{9... | collective-permute-start | bytes 393224 | tf_op jit(solution)/shard_map/ppermute | solution.py:218
  259.6 5.0 %collective-permute-start.17 = (bf16[256,256]{1,0:T(8,128)(2,1)S(1)}, bf16[256,256]{1,0:T(8,128)(2,1)S(1)}, u32[]{:S(2)}, u32[]{:S(2)}) collective-permute-start(bf16[256,256]{1,0:T(8,128)(2,1)S(1)} %get-tuple-element.60), channel_id=1, source_target_pairs={{0,8},{8,16},{16,24},{24,28},{28,20},{20,12},{12,4},{4,0},{1,9},{9... | collective-permute-start | bytes 393224 | tf_op jit(solution)/shard_map/ppermute | solution.py:218
  261.1 5.0 %collective-permute-start.24 = (bf16[256,256]{1,0:T(8,128)(2,1)S(1)}, bf16[256,256]{1,0:T(8,128)(2,1)S(1)}, u32[]{:S(2)}, u32[]{:S(2)}) collective-permute-start(bf16[256,256]{1,0:T(8,128)(2,1)S(1)} %get-tuple-element.61), channel_id=1, source_target_pairs={{0,4},{8,0},{16,8},{24,16},{28,24},{20,28},{12,20},{4,12},{1,5},{9... | collective-permute-start | bytes 393224 | tf_op jit(solution)/shard_map/ppermute | solution.py:218
  266.2 5.8 %collective-permute-start.18 = (bf16[256,256]{1,0:T(8,128)(2,1)S(1)}, bf16[256,256]{1,0:T(8,128)(2,1)S(1)}, u32[]{:S(2)}, u32[]{:S(2)}) collective-permute-start(bf16[256,256]{1,0:T(8,128)(2,1)S(1)} %get-tuple-element.51), channel_id=1, source_target_pairs={{0,8},{8,16},{16,24},{24,28},{28,20},{20,12},{12,4},{4,0},{1,9},{9... | collective-permute-start | bytes 393224 | tf_op jit(solution)/shard_map/ppermute | solution.py:218
  268.4 5.6 %collective-permute-start.25 = (bf16[256,256]{1,0:T(8,128)(2,1)S(1)}, bf16[256,256]{1,0:T(8,128)(2,1)S(1)}, u32[]{:S(2)}, u32[]{:S(2)}) collective-permute-start(bf16[256,256]{1,0:T(8,128)(2,1)S(1)} %get-tuple-element.52), channel_id=1, source_target_pairs={{0,4},{8,0},{16,8},{24,16},{28,24},{20,28},{12,20},{4,12},{1,5},{9... | collective-permute-start | bytes 393224 | tf_op jit(solution)/shard_map/ppermute | solution.py:218
  274.1 5.0 %collective-permute-start.19 = (bf16[256,256]{1,0:T(8,128)(2,1)S(1)}, bf16[256,256]{1,0:T(8,128)(2,1)S(1)}, u32[]{:S(2)}, u32[]{:S(2)}) collective-permute-start(bf16[256,256]{1,0:T(8,128)(2,1)S(1)} %get-tuple-element.49), channel_id=1, source_target_pairs={{0,8},{8,16},{16,24},{24,28},{28,20},{20,12},{12,4},{4,0},{1,9},{9... | collective-permute-start | bytes 393224 | tf_op jit(solution)/shard_map/ppermute | solution.py:218
  274.7 5.0 %collective-permute-start.26 = (bf16[256,256]{1,0:T(8,128)(2,1)S(1)}, bf16[256,256]{1,0:T(8,128)(2,1)S(1)}, u32[]{:S(2)}, u32[]{:S(2)}) collective-permute-start(bf16[256,256]{1,0:T(8,128)(2,1)S(1)} %get-tuple-element.50), channel_id=1, source_target_pairs={{0,4},{8,0},{16,8},{24,16},{28,24},{20,28},{12,20},{4,12},{1,5},{9... | collective-permute-start | bytes 393224 | tf_op jit(solution)/shard_map/ppermute | solution.py:218
  280.5 7.8 %collective-permute-start.27 = (bf16[256,512]{1,0:T(8,128)(2,1)S(1)}, bf16[256,512]{1,0:T(8,128)(2,1)S(1)}, u32[]{:S(2)}, u32[]{:S(2)}) collective-permute-start(bf16[256,512]{1,0:T(8,128)(2,1)S(1)} %get-tuple-element.59), channel_id=1, source_target_pairs={{0,1},{1,2},{2,3},{3,0},{4,5},{5,6},{6,7},{7,4},{8,9},{9,10},{10,1... | collective-permute-start | bytes 786440 | tf_op jit(solution)/shard_map/ppermute | solution.py:173
  280.5 11.8 %collective-permute-start.29 = (bf16[256,512]{1,0:T(8,128)(2,1)S(1)}, bf16[256,512]{1,0:T(8,128)(2,1)S(1)}, u32[]{:S(2)}, u32[]{:S(2)}) collective-permute-start(bf16[256,512]{1,0:T(8,128)(2,1)S(1)} %get-tuple-element.59), channel_id=1, source_target_pairs={{0,3},{1,0},{2,1},{3,2},{4,7},{5,4},{6,5},{7,6},{8,11},{9,8},{10,9... | collective-permute-start | bytes 786440 | tf_op jit(solution)/shard_map/ppermute | solution.py:173
  282.3 12.5 %collective-permute-start.28 = (bf16[256,512]{1,0:T(8,128)(2,1)S(1)}, bf16[256,512]{1,0:T(8,128)(2,1)S(1)}, u32[]{:S(2)}, u32[]{:S(2)}) collective-permute-start(bf16[256,512]{1,0:T(8,128)(2,1)S(1)} %get-tuple-element.59), channel_id=1, source_target_pairs={{0,2},{1,3},{2,0},{3,1},{4,6},{5,7},{6,4},{7,5},{8,10},{9,11},{10,... | collective-permute-start | bytes 786440 | tf_op jit(solution)/shard_map/ppermute | solution.py:173
  298.0 10.5 %copy-start.13 = (f32[512]{0:T(512)S(1)}, f32[512]{0:T(512)}, u32[]{:S(2)}) copy-start(f32[512]{0:T(512)} %param.33) | copy-start | bytes 6148
  298.0 10.5 %copy-start.14 = (f32[512]{0:T(512)S(1)}, f32[512]{0:T(512)}, u32[]{:S(2)}) copy-start(f32[512]{0:T(512)} %param.32) | copy-start | bytes 6148
  301.1 11.5 %copy-start.1 = (bf16[512,2048]{1,0:T(8,128)(2,1)S(1)}, bf16[512,2048]{1,0:T(8,128)(2,1)}, u32[]{:S(2)}) copy-start(bf16[512,2048]{1,0:T(8,128)(2,1)} %param.24) | copy-start | bytes 6291460
  (2 other events, 3.0 us)
Sparse Core Ops, SparseCore 0:
  100.3 39.7 all-gather.4
  141.6 28.5 all-gather.8
  171.7 40.4 all-gather.6
  213.6 28.5 all-gather.10

commit v12 on v11

--- a/solution.py
+++ b/solution.py
@@ -115,7 +115,7 @@
     info = jnp.concatenate([gate_hi, gate_lo], axis=0).reshape(-1, quarter)
     packed = jnp.concatenate([moe_in, info], axis=0)
     ring = ring_order(seq_count)
-    offsets, blocks, (expert_gate_up, qkv_flat) = ring_all_gather(packed, ring, (expert_gate_up, qkv_flat))
+    offsets, blocks = ring_all_gather(packed, ring)
     first = min(len(blocks), 5)
     chunks = [(0, first), (first, len(blocks))] if first < len(blocks) else [(0, first)]
     outputs = []
@@ -128,6 +128,10 @@
         gate_local = lax.dynamic_slice_in_dim(gate_all, here * local_experts, local_experts, axis=1)
         gate_local = jnp.transpose(gate_local, (1, 0, 2)).reshape(local_experts, count * tokens)
         rows = lax.all_gather(rows_q, "tp", axis=1, tiled=True)
+        if begin == 0:
+            rows, expert_gate_up, qkv_flat, down_full = lax.optimization_barrier(
+                (rows, expert_gate_up, qkv_flat, down_full)
+            )
         projected = jnp.einsum("td,edf->etf", rows, expert_gate_up, preferred_element_type=jnp.float32)
         activated = jax.nn.silu(projected[..., :hidden_quarter]) * projected[..., hidden_quarter:]
         activated = activated.astype(jnp.bfloat16).astype(jnp.float32)
@@ -186,7 +190,7 @@
     return [2 * i for i in range(half)] + [2 * i + 1 for i in reversed(range(half))]
 
 
-def ring_all_gather(block, cycle, riders):
+def ring_all_gather(block, cycle):
     count = len(cycle)
     forward = [(cycle[p], cycle[(p + 1) % count]) for p in range(count)]
     backward = [(cycle[p], cycle[(p - 1) % count]) for p in range(count)]
@@ -200,10 +204,7 @@
             behind = lax.ppermute(behind, "seq", backward)
             offsets.append(step)
             blocks.append(behind)
-        if step == 1:
-            ahead, behind, riders = lax.optimization_barrier((ahead, behind, riders))
-            blocks[1:] = [ahead, behind][: len(blocks) - 1]
-    return offsets, blocks, riders
+    return offsets, blocks
 
 
 def ring_reduce_scatter(by_offset, cycle):
@@ -316,9 +317,7 @@
         new_keys,
         new_values,
     )
-    if dense:
-        attended, down_full = lax.optimization_barrier((attended, down_full))
-    else:
+    if not dense:
         gate_up_flat = expert_gate_up
         qkv_flat = qkv_proj.reshape(D, -1)
     attn_term = jnp.dot(attended, out_proj, preferred_element_type=jnp.float32)

time: 320 us -> 311 us (0.972)
  waiting for transfers between devices: 165 us -> 156 us
    all_gather x2, waiting for transfers between devices: 42.7 us -> 8.55 us  [dense_experts(): rows = lax.all_gather(rows_q, 'tp', axis=1, tiled=True)]
    ppermute x3, waiting for transfers between devices: 9.03 us -> 26.3 us  [body(): pieces.append(lax.ppermute(piece, 'tp', pairs))]
    ppermute x4, waiting for transfers between devices: 15.8 us -> 22.1 us  [ring_all_gather(): ahead = lax.ppermute(ahead, 'seq', forward)]
    ppermute x3, starting transfers between devices: 1 us -> 6.6 us  [ring_all_gather(): behind = lax.ppermute(behind, 'seq', backward)]
    unnamed x41 -> x45, local copies, waits for them, and re-layouts: 12.9 us -> 12.2 us
  transfers between devices with their start and end apart: 34 -> 34, of which waited for: 25 -> 26; matrix products, arithmetic and copies ran while one was open for 17% -> 20% of each run, Pallas kernels for 4% -> 0%
where the time goes in v12:
time: 311 us; the launch traced here: 310 us
  waiting for transfers between devices  156 us (50%)
  matrix products  37 us (12%)
  local copies, waits for them, and re-layouts  33 us (11%)
  starting transfers between devices  31.2 us (10%)
  other arithmetic  14.5 us (5%)
  between operations  14.2 us (5%)
  blocking collectives  13.1 us (4%)
  Pallas kernels  11.6 us (4%)
    all_gather x2, waiting for transfers between devices, dense_experts(): weighted = lax.all_gather(weighted, 'tp', axis=2, tiled=True)  49.9 us
    ppermute x14, waiting for transfers between devices, ring_reduce_scatter(): received = lax.ppermute(acc.astype(jnp.bfloat16), 'seq', pairs)  27.6 us
    ppermute x3, waiting for transfers between devices, body(): pieces.append(lax.ppermute(piece, 'tp', pairs))  26.3 us
    ppermute x4, waiting for transfers between devices, ring_all_gather(): ahead = lax.ppermute(ahead, 'seq', forward)  22.1 us
    dot_general x2, matrix products, dense_experts(): jnp.einsum('td,edf->etf', rows, expert_gate_up, preferred_element_type=jn...  15.5 us
    ppermute x14, starting transfers between devices, ring_reduce_scatter(): received = lax.ppermute(acc.astype(jnp.bfloat16), 'seq', pairs)  14.9 us
    ppermute x3, waiting for transfers between devices, permute_reduce_scatter(): total = total + lax.ppermute(piece, 'tp', pairs).astype(jnp.float32)  12.3 us
    unnamed x45, local copies, waits for them, and re-layouts  12.2 us
  transfers between devices with their start and end apart: 34, of which 26 were waited for; matrix products, arithmetic and copies ran while one was open for 20% of the time, Pallas kernels for 0%

profile of v12, /device:TPU:0, one launch (start us, length us, event | category | flops | bytes accessed | tf_op | source)
XLA Modules:
  0.0 310.3 jit_solution(265768305776364585)
XLA Ops:
  8.6 11.6 %shard_map.192 = bf16[256,512]{1,0:T(8,128)(2,1)} custom-call(s32[1]{0:T(128)} %dynamic_slice.50.len_ref, bf16[256,512]{1,0:T(8,128)(2,1)} %q_ref.1, bf16[4096,512]{1,0:T(8,128)(2,1)} %bitcast.112, bf16[4096,512]{1,0:T(8,128)(2,1)} %bitcast.113, bf16[256,512]{1,0:T(8,128)(2,1)} %nk_ref.1, bf16[256,512]{1,0:T(8,128)(2,1)} %nv_ref.1), custom_call_target="tpu_custom_call" | custom-call | tf_op jit(solution)/shard_map/pallas_call | solution.py:94
  20.2 3.0 fusion.38
  24.8 2.5 collective-permute-start.2
  28.1 5.7 %collective-permute-done.2 = bf16[256,512]{1,0:T(8,128)(2,1)S(1)} collective-permute-done((bf16[256,512]{1,0:T(8,128)(2,1)S(1)}, bf16[256,512]{1,0:T(8,128)(2,1)S(1)}, u32[]{:S(2)}, u32[]{:S(2)}) %collective-permute-start.2) | collective-permute-done | bytes 262176 | tf_op jit(solution)/shard_map/ppermute | solution.py:161
  33.8 6.6 %collective-permute-done.1 = bf16[256,512]{1,0:T(8,128)(2,1)S(1)} collective-permute-done((bf16[256,512]{1,0:T(8,128)(2,1)S(1)}, bf16[256,512]{1,0:T(8,128)(2,1)S(1)}, u32[]{:S(2)}, u32[]{:S(2)}) %collective-permute-start.1) | collective-permute-done | bytes 262176 | tf_op jit(solution)/shard_map/ppermute | solution.py:161
  41.7 5.7 %psum.28 = f32[256]{0:T(256)S(1)} all-reduce(f32[256]{0:T(256)S(1)} %get-tuple-element.29), channel_id=1, replica_groups=mesh['seq'=8,'tp'=4] {'tp'}, use_global_device_ids=true, to_apply=%region_1.2 | all-reduce | flops 256 | bytes 2048 | tf_op jit(solution)/shard_map/psum | solution.py:330
  47.6 4.3 %collective-permute-start.4 = (bf16[272,512]{1,0:T(8,128)(2,1)S(1)}, bf16[272,512]{1,0:T(8,128)(2,1)S(1)}, u32[]{:S(2)}, u32[]{:S(2)}) collective-permute-start(bf16[272,512]{1,0:T(8,128)(2,1)S(1)} %pad_maximum_fusion.2), channel_id=1, source_target_pairs={{0,4},{8,0},{16,8},{24,16},{28,24},{20,28},{12,20},{4,12},{1,5},{9... | collective-permute-start | bytes 835592 | tf_op jit(solution)/shard_map/ppermute | solution.py:204
  51.9 6.6 %collective-permute-done.3 = bf16[272,512]{1,0:T(8,128)(2,1)S(1)} collective-permute-done((bf16[272,512]{1,0:T(8,128)(2,1)S(1)}, bf16[272,512]{1,0:T(8,128)(2,1)S(1)}, u32[]{:S(2)}, u32[]{:S(2)}) %collective-permute-start.3) | collective-permute-done | bytes 278560 | tf_op jit(solution)/shard_map/ppermute | solution.py:200
  58.6 2.1 collective-permute-start.6
  60.7 5.7 %collective-permute-done.5 = bf16[272,512]{1,0:T(8,128)(2,1)S(1)} collective-permute-done((bf16[272,512]{1,0:T(8,128)(2,1)S(1)}, bf16[272,512]{1,0:T(8,128)(2,1)S(1)}, u32[]{:S(2)}, u32[]{:S(2)}) %collective-permute-start.5) | collective-permute-done | bytes 278560 | tf_op jit(solution)/shard_map/ppermute | solution.py:200
  66.4 3.5 %collective-permute-done.6 = bf16[272,512]{1,0:T(8,128)(2,1)S(1)} collective-permute-done((bf16[272,512]{1,0:T(8,128)(2,1)S(1)}, bf16[272,512]{1,0:T(8,128)(2,1)S(1)}, u32[]{:S(2)}, u32[]{:S(2)}) %collective-permute-start.6) | collective-permute-done | bytes 278560 | tf_op jit(solution)/shard_map/ppermute | solution.py:204
  71.3 1.9 collective-permute-start.12
  73.4 4.9 %collective-permute-done.12 = bf16[272,512]{1,0:T(8,128)(2,1)S(1)} collective-permute-done((bf16[272,512]{1,0:T(8,128)(2,1)S(1)}, bf16[272,512]{1,0:T(8,128)(2,1)S(1)}, u32[]{:S(2)}, u32[]{:S(2)}) %collective-permute-start.12) | collective-permute-done | bytes 278560 | tf_op jit(solution)/shard_map/ppermute | solution.py:200
  78.3 1.7 collective-permute-start.14
  80.0 4.8 %collective-permute-done.14 = bf16[272,512]{1,0:T(8,128)(2,1)S(1)} collective-permute-done((bf16[272,512]{1,0:T(8,128)(2,1)S(1)}, bf16[272,512]{1,0:T(8,128)(2,1)S(1)}, u32[]{:S(2)}, u32[]{:S(2)}) %collective-permute-start.14) | collective-permute-done | bytes 278560 | tf_op jit(solution)/shard_map/ppermute | solution.py:200
  86.0 2.6 dynamic-slice_bitcast_fusion
  90.1 7.6 %reshape.134 = bf16[2,2048,512]{2,1,0:T(8,128)(2,1)} reshape(bf16[2,2048,2,256]{3,2,1,0:T(2,128)(2,1)} %param.28) | data formatting | bytes 8388608 | tf_op jit(solution)/shard_map/reshape | solution.py:305
  97.7 8.8 %copy.67 = bf16[2048,3,512]{0,2,1:T(8,128)(2,1)} copy(bf16[2048,3,512]{2,0,1:T(8,128)(2,1)} %param.31) | data formatting | bytes 12582912 | tf_op args[14]
  106.6 5.6 %collective-permute-done.9 = bf16[2,256,512]{2,1,0:T(8,128)(2,1)S(1)} collective-permute-done((bf16[2,256,512]{2,1,0:T(8,128)(2,1)}, bf16[2,256,512]{2,1,0:T(8,128)(2,1)S(1)}, u32[]{:S(2)}, u32[]{:S(2)}) %collective-permute-start.9) | collective-permute-done | bytes 524320 | tf_op jit(solution)/shard_map/ppermute | solution.py:301
  112.2 20.6 %collective-permute-done.8 = bf16[2,256,512]{2,1,0:T(8,128)(2,1)S(1)} collective-permute-done((bf16[2,256,512]{2,1,0:T(8,128)(2,1)S(1)}, bf16[2,256,512]{2,1,0:T(8,128)(2,1)S(1)}, u32[]{:S(2)}, u32[]{:S(2)}) %collective-permute-start.8) | collective-permute-done | bytes 524320 | tf_op jit(solution)/shard_map/ppermute | solution.py:301
  133.6 1.6 pad_maximum_fusion
  135.2 2.0 gather_fusion
  137.2 2.0 select_bitcast_fusion
  140.5 9.3 %fusion.2 = f32[2,1280,512]{1,2,0:T(8,128)S(1)} fusion(bf16[2,2048,512]{2,1,0:T(8,128)(2,1)} %reshape.134, bf16[1280,2048]{1,0:T(8,128)(2,1)} %all-gather.5.cloned.1.call-done), kind=kOutput, calls=%fused_computation.3 | convolution fusion | flops 5368709120 | bytes 14680064 | tf_op jit(solution)/shard_map/td,edf->etf/dot_general | solution.py:135
  149.8 1.9 multiply_convert_fusion
  152.6 8.5 %all-gather.9.cloned.1.call-done = bf16[768,2048]{1,0:T(8,128)(2,1)} async-done(((bf16[768,512]{1,0:T(8,128)(2,1)}), bf16[768,2048]{1,0:T(8,128)(2,1)}) %all-gather.9.cloned.1.call-update) | async-done | bytes 3145744 | tf_op jit(solution)/shard_map/all_gather | solution.py:130
  161.1 6.2 %fusion.10 = f32[2,768,512]{1,2,0:T(8,128)S(1)} fusion(bf16[2,2048,512]{2,1,0:T(8,128)(2,1)} %reshape.134, bf16[768,2048]{1,0:T(8,128)(2,1)} %all-gather.9.cloned.1.call-done), kind=kOutput, calls=%fused_computation.16 | convolution fusion | flops 3221225472 | bytes 10485760 | tf_op jit(solution)/shard_map/td,edf->etf/dot_general | solution.py:135
  168.8 34.4 %all-gather.7.cloned.1.call-done = bf16[2,1280,1024]{1,2,0:T(8,128)(2,1)} async-done(((bf16[2,1280,256]{1,2,0:T(8,128)(2,1)}), bf16[2,1280,1024]{1,2,0:T(8,128)(2,1)}) %all-gather.7.cloned.1.call-update) | async-done | bytes 5242896 | tf_op jit(solution)/shard_map/all_gather | solution.py:139
  203.1 5.4 %fusion.7 = bf16[1280,512]{1,0:T(8,128)(2,1)S(1)} fusion(bf16[2,1280,1024]{1,2,0:T(8,128)(2,1)} %all-gather.7.cloned.1.call-done, bf16[2,1024,512]{2,1,0:T(8,128)(2,1)S(1)} %bitcast.109), kind=kOutput, calls=%fused_computation.7 | convolution fusion | flops 2685009920 | bytes 8650752 | tf_op jit(solution)/shard_map/etf,efd->td/dot_general | solution.py:140
  210.6 3.6 %collective-permute-done.10 = bf16[256,256]{1,0:T(8,128)(2,1)S(1)} collective-permute-done((bf16[256,256]{1,0:T(8,128)(2,1)S(1)}, bf16[256,256]{1,0:T(8,128)(2,1)S(1)}, u32[]{:S(2)}, u32[]{:S(2)}) %collective-permute-start.10) | collective-permute-done | bytes 131104 | tf_op jit(solution)/shard_map/ppermute | solution.py:219
  217.6 15.5 %all-gather.11.cloned.1.call-done = bf16[2,768,1024]{1,2,0:T(8,128)(2,1)} async-done(((bf16[2,768,256]{1,2,0:T(8,128)(2,1)}), bf16[2,768,1024]{1,2,0:T(8,128)(2,1)}) %all-gather.11.cloned.1.call-update) | async-done | bytes 3145744 | tf_op jit(solution)/shard_map/all_gather | solution.py:139
  233.1 3.7 %bitcast_convert_fusion = bf16[768,512]{1,0:T(8,128)(2,1)S(1)} fusion(bf16[2,768,1024]{1,2,0:T(8,128)(2,1)} %all-gather.11.cloned.1.call-done, bf16[2,1024,512]{2,1,0:T(8,128)(2,1)S(1)} %bitcast.110), kind=kOutput, calls=%fused_computation.19 | convolution fusion | flops 1611005952 | bytes 6029312 | tf_op jit(solution)/shard_map/etf,efd->td/dot_general | solution.py:140
  236.9 1.8 collective-permute-start.15
  239.2 3.6 %collective-permute-done.15 = bf16[256,256]{1,0:T(8,128)(2,1)S(1)} collective-permute-done((bf16[256,256]{1,0:T(8,128)(2,1)S(1)}, bf16[256,256]{1,0:T(8,128)(2,1)S(1)}, u32[]{:S(2)}, u32[]{:S(2)}) %collective-permute-start.15) | collective-permute-done | bytes 131104 | tf_op jit(solution)/shard_map/ppermute | solution.py:219
  246.2 2.9 collective-permute-done.16
  252.8 2.9 collective-permute-done.17
  257.3 2.2 collective-permute-start.18
  259.5 3.5 %collective-permute-done.18 = bf16[256,256]{1,0:T(8,128)(2,1)S(1)} collective-permute-done((bf16[256,256]{1,0:T(8,128)(2,1)S(1)}, bf16[256,256]{1,0:T(8,128)(2,1)S(1)}, u32[]{:S(2)}, u32[]{:S(2)}) %collective-permute-start.18) | collective-permute-done | bytes 131104 | tf_op jit(solution)/shard_map/ppermute | solution.py:219
  263.1 2.1 collective-permute-done.25
  267.3 2.9 collective-permute-done.19
  272.7 2.0 fusion.18
  274.7 5.5 %collective-permute-done.27 = bf16[256,512]{1,0:T(8,128)(2,1)S(1)} collective-permute-done((bf16[256,512]{1,0:T(8,128)(2,1)S(1)}, bf16[256,512]{1,0:T(8,128)(2,1)S(1)}, u32[]{:S(2)}, u32[]{:S(2)}) %collective-permute-start.27) | collective-permute-done | bytes 262176 | tf_op jit(solution)/shard_map/ppermute | solution.py:177
  280.2 2.0 convolution_add_fusion.1
  282.3 2.0 fusion.14
  284.3 3.3 %fusion.8 = f32[256,1536]{1,0:T(8,128)} fusion(f32[256,1536]{1,0:T(8,128)S(1)} %fusion.14, f32[256,1536]{1,0:T(8,128)S(1)} %convolution_add_fusion.1, bf16[256,512]{1,0:T(8,128)(2,1)S(1)} %collective-permute-done.28, bf16[2048,1536]{0,1:T(8,128)(2,1)} %bitcast.106, s32[]{:T(128)S(6)} %select_n.126), kind=kOutput, calls=%fused_computation.9 | convolution fusion | flops 403439616 | bytes 6553604 | tf_op jit(solution)/shard_map/dot_general | solution.py:178
  287.6 3.1 copy.79
  292.2 7.5 %all-reduce = (f32[256]{0:T(256)S(1)}, f32[256]{0:T(256)S(1)}, f32[256]{0:T(256)S(1)}) all-reduce(f32[256]{0:T(256)S(1)} %get-tuple-element.25, f32[256]{0:T(256)S(1)} %get-tuple-element.53, f32[256]{0:T(256)S(1)} %get-tuple-element.24), channel_id=1, replica_groups=mesh['seq'=8,'tp'=4] {'tp'}, use_global_device_ids=true, to_apply=%region_6.7 | all-reduce | flops 768 | bytes 6144 | tf_op jit(solution)/shard_map/psum | solution.py:356
  299.7 1.6 fusion.21
  (126 shorter events, 37.1 us)
Async XLA Ops:
  7.2 13.0 %copy-start = (bf16[512,2048]{1,0:T(8,128)(2,1)S(1)}, bf16[512,2048]{1,0:T(8,128)(2,1)}, u32[]{:S(2)}) copy-start(bf16[512,2048]{1,0:T(8,128)(2,1)} %param.24) | copy-start | bytes 6291460
  7.2 133.3 %all-gather.5.cloned.1.call-start = ((), (), s32[]{:S(2)}) async-start(), calls=%async_computation | async-start | bytes 6553600 | tf_op jit(solution)/shard_map/all_gather | solution.py:130
  20.2 7.8 %copy-start.12 = (f32[256,8]{0,1:T(8,128)S(1)}, f32[256,8]{0,1:T(8,128)}, u32[]{:S(2)}) copy-start(f32[256,8]{0,1:T(8,128)} %param.27) | copy-start | bytes 24580
  20.2 7.8 %copy-start.13 = (s32[256,8]{0,1:T(8,128)S(1)}, s32[256,8]{0,1:T(8,128)}, u32[]{:S(2)}) copy-start(s32[256,8]{0,1:T(8,128)} %param.26) | copy-start | bytes 24580
  20.2 20.2 %copy-start.11 = (bf16[256,512]{1,0:T(8,128)(2,1)S(1)}, bf16[256,512]{1,0:T(8,128)(2,1)}, u32[]{:S(2)}) copy-start(bf16[256,512]{1,0:T(8,128)(2,1)} %param.17) | copy-start | bytes 786436
  23.3 24.1 %copy-start.14 = (f32[512]{0:T(512)S(1)}, f32[512]{0:T(512)}, u32[]{:S(2)}) copy-start(f32[512]{0:T(512)} %param.25) | copy-start | bytes 6148
  24.8 9.0 %collective-permute-start.2 = (bf16[256,512]{1,0:T(8,128)(2,1)S(1)}, bf16[256,512]{1,0:T(8,128)(2,1)S(1)}, u32[]{:S(2)}, u32[]{:S(2)}) collective-permute-start(bf16[256,512]{1,0:T(8,128)(2,1)S(1)} %get-tuple-element.38), channel_id=1, source_target_pairs={{0,3},{1,0},{2,1},{3,2},{4,7},{5,4},{6,5},{7,6},{8,11},{9,8},{10,9... | collective-permute-start | bytes 786440 | tf_op jit(solution)/shard_map/ppermute | solution.py:161
  27.2 13.2 %collective-permute-start.1 = (bf16[256,512]{1,0:T(8,128)(2,1)S(1)}, bf16[256,512]{1,0:T(8,128)(2,1)S(1)}, u32[]{:S(2)}, u32[]{:S(2)}) collective-permute-start(bf16[256,512]{1,0:T(8,128)(2,1)S(1)} %get-tuple-element.39), channel_id=1, source_target_pairs={{0,2},{1,3},{2,0},{3,1},{4,6},{5,7},{6,4},{7,5},{8,10},{9,11},{10,... | collective-permute-start | bytes 786440 | tf_op jit(solution)/shard_map/ppermute | solution.py:161
  27.9 12.5 %collective-permute-start = (bf16[256,512]{1,0:T(8,128)(2,1)S(1)}, bf16[256,512]{1,0:T(8,128)(2,1)S(1)}, u32[]{:S(2)}, u32[]{:S(2)}) collective-permute-start(bf16[256,512]{1,0:T(8,128)(2,1)S(1)} %get-tuple-element.37), channel_id=1, source_target_pairs={{0,1},{1,2},{2,3},{3,0},{4,5},{5,6},{6,7},{7,4},{8,9},{9,10},{10,1... | collective-permute-start | bytes 786440 | tf_op jit(solution)/shard_map/ppermute | solution.py:161
  47.5 11.0 %collective-permute-start.3 = (bf16[272,512]{1,0:T(8,128)(2,1)S(1)}, bf16[272,512]{1,0:T(8,128)(2,1)S(1)}, u32[]{:S(2)}, u32[]{:S(2)}) collective-permute-start(bf16[272,512]{1,0:T(8,128)(2,1)S(1)} %pad_maximum_fusion.2), channel_id=1, source_target_pairs={{0,8},{8,16},{16,24},{24,28},{28,20},{20,12},{12,4},{4,0},{1,9},{9... | collective-permute-start | bytes 835592 | tf_op jit(solution)/shard_map/ppermute | solution.py:200
  47.6 11.0 %collective-permute-start.4 = (bf16[272,512]{1,0:T(8,128)(2,1)S(1)}, bf16[272,512]{1,0:T(8,128)(2,1)S(1)}, u32[]{:S(2)}, u32[]{:S(2)}) collective-permute-start(bf16[272,512]{1,0:T(8,128)(2,1)S(1)} %pad_maximum_fusion.2), channel_id=1, source_target_pairs={{0,4},{8,0},{16,8},{24,16},{28,24},{20,28},{12,20},{4,12},{1,5},{9... | collective-permute-start | bytes 835592 | tf_op jit(solution)/shard_map/ppermute | solution.py:204
  58.5 7.9 %collective-permute-start.5 = (bf16[272,512]{1,0:T(8,128)(2,1)S(1)}, bf16[272,512]{1,0:T(8,128)(2,1)S(1)}, u32[]{:S(2)}, u32[]{:S(2)}) collective-permute-start(bf16[272,512]{1,0:T(8,128)(2,1)S(1)} %collective-permute-done.3), channel_id=1, source_target_pairs={{0,8},{8,16},{16,24},{24,28},{28,20},{20,12},{12,4},{4,0},{1,9},{9... | collective-permute-start | bytes 835592 | tf_op jit(solution)/shard_map/ppermute | solution.py:200
  58.6 11.3 %collective-permute-start.6 = (bf16[272,512]{1,0:T(8,128)(2,1)S(1)}, bf16[272,512]{1,0:T(8,128)(2,1)S(1)}, u32[]{:S(2)}, u32[]{:S(2)}) collective-permute-start(bf16[272,512]{1,0:T(8,128)(2,1)S(1)} %collective-permute-done.4), channel_id=1, source_target_pairs={{0,4},{8,0},{16,8},{24,16},{28,24},{20,28},{12,20},{4,12},{1,5},{9... | collective-permute-start | bytes 835592 | tf_op jit(solution)/shard_map/ppermute | solution.py:204
  69.9 14.9 %copy-start.2 = (bf16[5,272,512]{2,1,0:T(8,128)(2,1)}, bf16[5,272,512]{2,1,0:T(8,128)(2,1)S(1)}, u32[]{:S(2)}) copy-start(bf16[5,272,512]{2,1,0:T(8,128)(2,1)S(1)} %bitcast_dynamic-update-slice_fusion) | copy-start | bytes 4177924
  71.2 89.8 %all-gather.9.cloned.1.call-start = ((), (), s32[]{:S(2)}) async-start(), calls=%async_computation.2 | async-start | bytes 3932160 | tf_op jit(solution)/shard_map/all_gather | solution.py:130
  71.3 7.0 %collective-permute-start.12 = (bf16[272,512]{1,0:T(8,128)(2,1)S(1)}, bf16[272,512]{1,0:T(8,128)(2,1)S(1)}, u32[]{:S(2)}, u32[]{:S(2)}) collective-permute-start(bf16[272,512]{1,0:T(8,128)(2,1)S(1)} %collective-permute-done.5), channel_id=1, source_target_pairs={{0,8},{8,16},{16,24},{24,28},{28,20},{20,12},{12,4},{4,0},{1,9},{9... | collective-permute-start | bytes 835592 | tf_op jit(solution)/shard_map/ppermute | solution.py:200
  73.2 6.8 %collective-permute-start.13 = (bf16[272,512]{1,0:T(8,128)(2,1)}, bf16[272,512]{1,0:T(8,128)(2,1)S(1)}, u32[]{:S(2)}, u32[]{:S(2)}) collective-permute-start(bf16[272,512]{1,0:T(8,128)(2,1)} %copy-done.10), channel_id=1, source_target_pairs={{0,4},{8,0},{16,8},{24,16},{28,24},{20,28},{12,20},{4,12},{1,5},{9... | collective-permute-start | bytes 835592 | tf_op jit(solution)/shard_map/ppermute | solution.py:204
  78.3 6.5 %collective-permute-start.14 = (bf16[272,512]{1,0:T(8,128)(2,1)S(1)}, bf16[272,512]{1,0:T(8,128)(2,1)S(1)}, u32[]{:S(2)}, u32[]{:S(2)}) collective-permute-start(bf16[272,512]{1,0:T(8,128)(2,1)S(1)} %collective-permute-done.12), channel_id=1, source_target_pairs={{0,8},{8,16},{16,24},{24,28},{28,20},{20,12},{12,4},{4,0},{1,9},{9... | collective-permute-start | bytes 835592 | tf_op jit(solution)/shard_map/ppermute | solution.py:200
  80.0 8.6 %copy-start.5 = (bf16[272,512]{1,0:T(8,128)(2,1)}, bf16[272,512]{1,0:T(8,128)(2,1)S(1)}, u32[]{:S(2)}) copy-start(bf16[272,512]{1,0:T(8,128)(2,1)S(1)} %collective-permute-done.13) | copy-start | bytes 835588
  86.0 117.2 %all-gather.7.cloned.1.call-start = ((), (), s32[]{:S(2)}) async-start(), calls=%async_computation.1 | async-start | bytes 6553600 | tf_op jit(solution)/shard_map/all_gather | solution.py:139
  88.6 23.6 %collective-permute-start.9 = (bf16[2,256,512]{2,1,0:T(8,128)(2,1)}, bf16[2,256,512]{2,1,0:T(8,128)(2,1)S(1)}, u32[]{:S(2)}, u32[]{:S(2)}) collective-permute-start(bf16[2,256,512]{2,1,0:T(8,128)(2,1)} %get-tuple-element.35), channel_id=1, source_target_pairs={{0,3},{1,0},{2,1},{3,2},{4,7},{5,4},{6,5},{7,6},{8,11},{9,8},{10,9... | collective-permute-start | bytes 1572872 | tf_op jit(solution)/shard_map/ppermute | solution.py:301
  88.6 44.2 %collective-permute-start.8 = (bf16[2,256,512]{2,1,0:T(8,128)(2,1)S(1)}, bf16[2,256,512]{2,1,0:T(8,128)(2,1)S(1)}, u32[]{:S(2)}, u32[]{:S(2)}) collective-permute-start(bf16[2,256,512]{2,1,0:T(8,128)(2,1)S(1)} %get-tuple-element.36), channel_id=1, source_target_pairs={{0,2},{1,3},{2,0},{3,1},{4,6},{5,7},{6,4},{7,5},{8,10},{9,11},{10,... | collective-permute-start | bytes 1572872 | tf_op jit(solution)/shard_map/ppermute | solution.py:301
  89.9 43.0 %collective-permute-start.7 = (bf16[2,256,512]{2,1,0:T(8,128)(2,1)S(1)}, bf16[2,256,512]{2,1,0:T(8,128)(2,1)}, u32[]{:S(2)}, u32[]{:S(2)}) collective-permute-start(bf16[2,256,512]{2,1,0:T(8,128)(2,1)S(1)} %get-tuple-element.34), channel_id=1, source_target_pairs={{0,1},{1,2},{2,3},{3,0},{4,5},{5,6},{6,7},{7,4},{8,9},{9,10},{10,1... | collective-permute-start | bytes 1572872 | tf_op jit(solution)/shard_map/ppermute | solution.py:301
  112.2 20.7 %copy-start.8 = (bf16[2,256,512]{2,1,0:T(8,128)(2,1)}, bf16[2,256,512]{2,1,0:T(8,128)(2,1)S(1)}, u32[]{:S(2)}) copy-start(bf16[2,256,512]{2,1,0:T(8,128)(2,1)S(1)} %collective-permute-done.9) | copy-start | bytes 1572868
  151.7 81.4 %all-gather.11.cloned.1.call-start = ((), (), s32[]{:S(2)}) async-start(), calls=%async_computation.3 | async-start | bytes 3932160 | tf_op jit(solution)/shard_map/all_gather | solution.py:139
  208.5 7.0 %copy-start.3 = (bf16[1280,512]{1,0:T(8,128)(2,1)}, bf16[1280,512]{1,0:T(8,128)(2,1)S(1)}, u32[]{:S(2)}) copy-start(bf16[1280,512]{1,0:T(8,128)(2,1)S(1)} %fusion.7) | copy-start | bytes 3932164
  208.6 5.7 %collective-permute-start.10 = (bf16[256,256]{1,0:T(8,128)(2,1)S(1)}, bf16[256,256]{1,0:T(8,128)(2,1)S(1)}, u32[]{:S(2)}, u32[]{:S(2)}) collective-permute-start(bf16[256,256]{1,0:T(8,128)(2,1)S(1)} %get-tuple-element.51), channel_id=1, source_target_pairs={{0,8},{8,16},{16,24},{24,28},{28,20},{20,12},{12,4},{4,0},{1,9},{9... | collective-permute-start | bytes 393224 | tf_op jit(solution)/shard_map/ppermute | solution.py:219
  210.1 5.4 %collective-permute-start.20 = (bf16[256,256]{1,0:T(8,128)(2,1)S(1)}, bf16[256,256]{1,0:T(8,128)(2,1)S(1)}, u32[]{:S(2)}, u32[]{:S(2)}) collective-permute-start(bf16[256,256]{1,0:T(8,128)(2,1)S(1)} %get-tuple-element.52), channel_id=1, source_target_pairs={{0,4},{8,0},{16,8},{24,16},{28,24},{20,28},{12,20},{4,12},{1,5},{9... | collective-permute-start | bytes 393224 | tf_op jit(solution)/shard_map/ppermute | solution.py:219
  215.6 21.3 %collective-permute-start.11 = (bf16[256,256]{1,0:T(8,128)(2,1)S(1)}, bf16[256,256]{1,0:T(8,128)(2,1)S(1)}, u32[]{:S(2)}, u32[]{:S(2)}) collective-permute-start(bf16[256,256]{1,0:T(8,128)(2,1)S(1)} %get-tuple-element.49), channel_id=1, source_target_pairs={{0,8},{8,16},{16,24},{24,28},{28,20},{20,12},{12,4},{4,0},{1,9},{9... | collective-permute-start | bytes 393224 | tf_op jit(solution)/shard_map/ppermute | solution.py:219
  217.1 19.7 %collective-permute-start.21 = (bf16[256,256]{1,0:T(8,128)(2,1)S(1)}, bf16[256,256]{1,0:T(8,128)(2,1)S(1)}, u32[]{:S(2)}, u32[]{:S(2)}) collective-permute-start(bf16[256,256]{1,0:T(8,128)(2,1)S(1)} %get-tuple-element.50), channel_id=1, source_target_pairs={{0,4},{8,0},{16,8},{24,16},{28,24},{20,28},{12,20},{4,12},{1,5},{9... | collective-permute-start | bytes 393224 | tf_op jit(solution)/shard_map/ppermute | solution.py:219
  236.8 20.4 %copy-start.4 = (bf16[1280,512]{1,0:T(8,128)(2,1)S(1)}, bf16[1280,512]{1,0:T(8,128)(2,1)}, u32[]{:S(2)}) copy-start(bf16[1280,512]{1,0:T(8,128)(2,1)} %copy-done.3) | copy-start | bytes 3932164
  236.9 5.9 %collective-permute-start.15 = (bf16[256,256]{1,0:T(8,128)(2,1)S(1)}, bf16[256,256]{1,0:T(8,128)(2,1)S(1)}, u32[]{:S(2)}, u32[]{:S(2)}) collective-permute-start(bf16[256,256]{1,0:T(8,128)(2,1)S(1)} %get-tuple-element.60), channel_id=1, source_target_pairs={{0,8},{8,16},{16,24},{24,28},{28,20},{20,12},{12,4},{4,0},{1,9},{9... | collective-permute-start | bytes 393224 | tf_op jit(solution)/shard_map/ppermute | solution.py:219
  238.7 32.2 %copy-start.15 = (f32[512]{0:T(512)S(1)}, f32[512]{0:T(512)}, u32[]{:S(2)}) copy-start(f32[512]{0:T(512)} %param.30) | copy-start | bytes 6148
  238.7 5.4 %collective-permute-start.22 = (bf16[256,256]{1,0:T(8,128)(2,1)S(1)}, bf16[256,256]{1,0:T(8,128)(2,1)S(1)}, u32[]{:S(2)}, u32[]{:S(2)}) collective-permute-start(bf16[256,256]{1,0:T(8,128)(2,1)S(1)} %get-tuple-element.61), channel_id=1, source_target_pairs={{0,4},{8,0},{16,8},{24,16},{28,24},{20,28},{12,20},{4,12},{1,5},{9... | collective-permute-start | bytes 393224 | tf_op jit(solution)/shard_map/ppermute | solution.py:219
  244.1 5.0 %collective-permute-start.16 = (bf16[256,256]{1,0:T(8,128)(2,1)S(1)}, bf16[256,256]{1,0:T(8,128)(2,1)S(1)}, u32[]{:S(2)}, u32[]{:S(2)}) collective-permute-start(bf16[256,256]{1,0:T(8,128)(2,1)S(1)} %get-tuple-element.58), channel_id=1, source_target_pairs={{0,8},{8,16},{16,24},{24,28},{28,20},{20,12},{12,4},{4,0},{1,9},{9... | collective-permute-start | bytes 393224 | tf_op jit(solution)/shard_map/ppermute | solution.py:219
  245.7 5.0 %collective-permute-start.23 = (bf16[256,256]{1,0:T(8,128)(2,1)S(1)}, bf16[256,256]{1,0:T(8,128)(2,1)S(1)}, u32[]{:S(2)}, u32[]{:S(2)}) collective-permute-start(bf16[256,256]{1,0:T(8,128)(2,1)S(1)} %get-tuple-element.59), channel_id=1, source_target_pairs={{0,4},{8,0},{16,8},{24,16},{28,24},{20,28},{12,20},{4,12},{1,5},{9... | collective-permute-start | bytes 393224 | tf_op jit(solution)/shard_map/ppermute | solution.py:219
  250.7 5.0 %collective-permute-start.17 = (bf16[256,256]{1,0:T(8,128)(2,1)S(1)}, bf16[256,256]{1,0:T(8,128)(2,1)S(1)}, u32[]{:S(2)}, u32[]{:S(2)}) collective-permute-start(bf16[256,256]{1,0:T(8,128)(2,1)S(1)} %get-tuple-element.56), channel_id=1, source_target_pairs={{0,8},{8,16},{16,24},{24,28},{28,20},{20,12},{12,4},{4,0},{1,9},{9... | collective-permute-start | bytes 393224 | tf_op jit(solution)/shard_map/ppermute | solution.py:219
  252.3 5.0 %collective-permute-start.24 = (bf16[256,256]{1,0:T(8,128)(2,1)S(1)}, bf16[256,256]{1,0:T(8,128)(2,1)S(1)}, u32[]{:S(2)}, u32[]{:S(2)}) collective-permute-start(bf16[256,256]{1,0:T(8,128)(2,1)S(1)} %get-tuple-element.57), channel_id=1, source_target_pairs={{0,4},{8,0},{16,8},{24,16},{28,24},{20,28},{12,20},{4,12},{1,5},{9... | collective-permute-start | bytes 393224 | tf_op jit(solution)/shard_map/ppermute | solution.py:219
  257.3 5.8 %collective-permute-start.18 = (bf16[256,256]{1,0:T(8,128)(2,1)S(1)}, bf16[256,256]{1,0:T(8,128)(2,1)S(1)}, u32[]{:S(2)}, u32[]{:S(2)}) collective-permute-start(bf16[256,256]{1,0:T(8,128)(2,1)S(1)} %get-tuple-element.47), channel_id=1, source_target_pairs={{0,8},{8,16},{16,24},{24,28},{28,20},{20,12},{12,4},{4,0},{1,9},{9... | collective-permute-start | bytes 393224 | tf_op jit(solution)/shard_map/ppermute | solution.py:219
  259.5 5.6 %collective-permute-start.25 = (bf16[256,256]{1,0:T(8,128)(2,1)S(1)}, bf16[256,256]{1,0:T(8,128)(2,1)S(1)}, u32[]{:S(2)}, u32[]{:S(2)}) collective-permute-start(bf16[256,256]{1,0:T(8,128)(2,1)S(1)} %get-tuple-element.48), channel_id=1, source_target_pairs={{0,4},{8,0},{16,8},{24,16},{28,24},{20,28},{12,20},{4,12},{1,5},{9... | collective-permute-start | bytes 393224 | tf_op jit(solution)/shard_map/ppermute | solution.py:219
  265.2 5.0 %collective-permute-start.19 = (bf16[256,256]{1,0:T(8,128)(2,1)S(1)}, bf16[256,256]{1,0:T(8,128)(2,1)S(1)}, u32[]{:S(2)}, u32[]{:S(2)}) collective-permute-start(bf16[256,256]{1,0:T(8,128)(2,1)S(1)} %get-tuple-element.45), channel_id=1, source_target_pairs={{0,8},{8,16},{16,24},{24,28},{28,20},{20,12},{12,4},{4,0},{1,9},{9... | collective-permute-start | bytes 393224 | tf_op jit(solution)/shard_map/ppermute | solution.py:219
  265.8 5.0 %collective-permute-start.26 = (bf16[256,256]{1,0:T(8,128)(2,1)S(1)}, bf16[256,256]{1,0:T(8,128)(2,1)S(1)}, u32[]{:S(2)}, u32[]{:S(2)}) collective-permute-start(bf16[256,256]{1,0:T(8,128)(2,1)S(1)} %get-tuple-element.46), channel_id=1, source_target_pairs={{0,4},{8,0},{16,8},{24,16},{28,24},{20,28},{12,20},{4,12},{1,5},{9... | collective-permute-start | bytes 393224 | tf_op jit(solution)/shard_map/ppermute | solution.py:219
  271.7 10.6 %collective-permute-start.29 = (bf16[256,512]{1,0:T(8,128)(2,1)S(1)}, bf16[256,512]{1,0:T(8,128)(2,1)S(1)}, u32[]{:S(2)}, u32[]{:S(2)}) collective-permute-start(bf16[256,512]{1,0:T(8,128)(2,1)S(1)} %get-tuple-element.55), channel_id=1, source_target_pairs={{0,3},{1,0},{2,1},{3,2},{4,7},{5,4},{6,5},{7,6},{8,11},{9,8},{10,9... | collective-permute-start | bytes 786440 | tf_op jit(solution)/shard_map/ppermute | solution.py:177
  271.7 8.6 %collective-permute-start.27 = (bf16[256,512]{1,0:T(8,128)(2,1)S(1)}, bf16[256,512]{1,0:T(8,128)(2,1)S(1)}, u32[]{:S(2)}, u32[]{:S(2)}) collective-permute-start(bf16[256,512]{1,0:T(8,128)(2,1)S(1)} %get-tuple-element.55), channel_id=1, source_target_pairs={{0,1},{1,2},{2,3},{3,0},{4,5},{5,6},{6,7},{7,4},{8,9},{9,10},{10,1... | collective-permute-start | bytes 786440 | tf_op jit(solution)/shard_map/ppermute | solution.py:177
  272.2 12.2 %collective-permute-start.28 = (bf16[256,512]{1,0:T(8,128)(2,1)S(1)}, bf16[256,512]{1,0:T(8,128)(2,1)S(1)}, u32[]{:S(2)}, u32[]{:S(2)}) collective-permute-start(bf16[256,512]{1,0:T(8,128)(2,1)S(1)} %get-tuple-element.55), channel_id=1, source_target_pairs={{0,2},{1,3},{2,0},{3,1},{4,6},{5,7},{6,4},{7,5},{8,10},{9,11},{10,... | collective-permute-start | bytes 786440 | tf_op jit(solution)/shard_map/ppermute | solution.py:177
  287.6 12.0 %copy-start.16 = (f32[512]{0:T(512)S(1)}, f32[512]{0:T(512)}, u32[]{:S(2)}) copy-start(f32[512]{0:T(512)} %param.33) | copy-start | bytes 6148
  287.6 12.0 %copy-start.17 = (f32[512]{0:T(512)S(1)}, f32[512]{0:T(512)}, u32[]{:S(2)}) copy-start(f32[512]{0:T(512)} %param.32) | copy-start | bytes 6148
  290.7 13.1 %copy-start.1 = (bf16[512,2048]{1,0:T(8,128)(2,1)S(1)}, bf16[512,2048]{1,0:T(8,128)(2,1)}, u32[]{:S(2)}) copy-start(bf16[512,2048]{1,0:T(8,128)(2,1)} %param.24) | copy-start | bytes 6291460
  (4 other events, 5.3 us)
Sparse Core Ops, SparseCore 0:
  71.4 59.5 all-gather.4
  132.5 28.5 all-gather.8
  162.7 40.4 all-gather.6
  204.6 28.5 all-gather.10

commit v13 on v12

--- a/solution.py
+++ b/solution.py
@@ -127,18 +127,19 @@
         gate_all = info_all[:, 0] + info_all[:, 1]
         gate_local = lax.dynamic_slice_in_dim(gate_all, here * local_experts, local_experts, axis=1)
         gate_local = jnp.transpose(gate_local, (1, 0, 2)).reshape(local_experts, count * tokens)
-        rows = lax.all_gather(rows_q, "tp", axis=1, tiled=True)
+        rows = lax.all_gather(rows_q, "tp", axis=0, tiled=False)
         if begin == 0:
             rows, expert_gate_up, qkv_flat, down_full = lax.optimization_barrier(
                 (rows, expert_gate_up, qkv_flat, down_full)
             )
-        projected = jnp.einsum("td,edf->etf", rows, expert_gate_up, preferred_element_type=jnp.float32)
+        gate_up_split = expert_gate_up.reshape(local_experts, rows.shape[0], quarter, -1)
+        projected = jnp.einsum("qtd,eqdf->etf", rows, gate_up_split, preferred_element_type=jnp.float32)
         activated = jax.nn.silu(projected[..., :hidden_quarter]) * projected[..., hidden_quarter:]
         activated = activated.astype(jnp.bfloat16).astype(jnp.float32)
         weighted = (activated * gate_local[:, :, None]).astype(jnp.bfloat16)
-        weighted = lax.all_gather(weighted, "tp", axis=2, tiled=True)
+        weighted = lax.all_gather(weighted, "tp", axis=0, tiled=False)
         partial = jnp.einsum(
-            "etf,efd->td", weighted, down_full, preferred_element_type=jnp.float32
+            "qetf,qefd->td", weighted, down_full, preferred_element_type=jnp.float32
         ).astype(jnp.bfloat16)
         outputs.append(partial.reshape(count, tokens, -1))
     by_offset = {}
@@ -301,7 +302,6 @@
             pieces.append(lax.ppermute(piece, "tp", pairs))
         order = (tp_here - jnp.arange(tp_count, dtype=jnp.int32)) % tp_count
         down_full = jnp.take(jnp.stack(pieces), order, axis=0)
-        down_full = jnp.transpose(down_full, (1, 0, 2, 3)).reshape(local_experts, -1, quarter_width)
         gate_up_flat = expert_gate_up.reshape(local_experts, D, -1)
         qkv_flat = qkv_proj.reshape(D, -1)
     local_width = new_queries.shape[1]

time: 311 us -> 311 us (level)
  waiting for transfers between devices: 156 us -> 150 us
  Pallas kernels: 11.6 us -> 16.8 us
    pallas_call x1, Pallas kernels: 11.6 us -> 16.8 us  [flash_attention(): pl.pallas_call(kernel, grid_spec=grid_spec, out_shape=jax.ShapeDtypeStruc...]
    ppermute x3, starting transfers between devices: 6.6 us -> 3.11 us  [ring_all_gather(): behind = lax.ppermute(behind, 'seq', backward)]
    unnamed x45 -> x49, local copies, waits for them, and re-layouts: 12.2 us -> 12.3 us
  transfers between devices with their start and end apart: 34 -> 34, of which waited for: 26 -> 26; matrix products, arithmetic and copies ran while one was open for 20% -> 21% of each run, Pallas kernels for 0% -> 0%
where the time goes in v13:
time: 311 us; the launch traced here: 310 us
  waiting for transfers between devices  150 us (48%)
  matrix products  37.8 us (12%)
  local copies, waits for them, and re-layouts  35.5 us (11%)
  starting transfers between devices  29.2 us (9%)
  Pallas kernels  16.8 us (5%)
  between operations  14.3 us (5%)
  blocking collectives  13.1 us (4%)
  other arithmetic  13 us (4%)
    all_gather x2, waiting for transfers between devices, dense_experts(): weighted = lax.all_gather(weighted, 'tp', axis=0, tiled=False)  48.8 us
    ppermute x14, waiting for transfers between devices, ring_reduce_scatter(): received = lax.ppermute(acc.astype(jnp.bfloat16), 'seq', pairs)  27.6 us
    ppermute x3, waiting for transfers between devices, body(): pieces.append(lax.ppermute(piece, 'tp', pairs))  23.9 us
    ppermute x4, waiting for transfers between devices, ring_all_gather(): ahead = lax.ppermute(ahead, 'seq', forward)  21 us
    pallas_call x1, Pallas kernels, flash_attention(): pl.pallas_call(kernel, grid_spec=grid_spec, out_shape=jax.ShapeDtypeStruc...  16.8 us
    dot_general x2, matrix products, dense_experts(): jnp.einsum('qtd,eqdf->etf', rows, gate_up_split, preferred_element_type=j...  15.5 us
    ppermute x14, starting transfers between devices, ring_reduce_scatter(): received = lax.ppermute(acc.astype(jnp.bfloat16), 'seq', pairs)  14.9 us
    unnamed x49, local copies, waits for them, and re-layouts  12.3 us
  transfers between devices with their start and end apart: 34, of which 26 were waited for; matrix products, arithmetic and copies ran while one was open for 21% of the time, Pallas kernels for 0%

profile of v13, /device:TPU:0, one launch (start us, length us, event | category | flops | bytes accessed | tf_op | source)
XLA Modules:
  0.0 309.6 jit_solution(7779108459714137575)
XLA Ops:
  8.6 16.8 %shard_map.192 = bf16[256,512]{1,0:T(8,128)(2,1)} custom-call(s32[1]{0:T(128)} %dynamic_slice.50.len_ref, bf16[256,512]{1,0:T(8,128)(2,1)} %q_ref.1, bf16[4096,512]{1,0:T(8,128)(2,1)} %bitcast.114, bf16[4096,512]{1,0:T(8,128)(2,1)} %bitcast.115, bf16[256,512]{1,0:T(8,128)(2,1)} %nk_ref.1, bf16[256,512]{1,0:T(8,128)(2,1)} %nv_ref.1), custom_call_target="tpu_custom_call" | custom-call | tf_op jit(solution)/shard_map/pallas_call | solution.py:94
  25.4 3.1 fusion.53
  30.0 2.5 collective-permute-start.2
  33.3 5.7 %collective-permute-done.2 = bf16[256,512]{1,0:T(8,128)(2,1)S(1)} collective-permute-done((bf16[256,512]{1,0:T(8,128)(2,1)S(1)}, bf16[256,512]{1,0:T(8,128)(2,1)S(1)}, u32[]{:S(2)}, u32[]{:S(2)}) %collective-permute-start.2) | collective-permute-done | bytes 262176 | tf_op jit(solution)/shard_map/ppermute | solution.py:162
  39.0 6.6 %collective-permute-done.1 = bf16[256,512]{1,0:T(8,128)(2,1)S(1)} collective-permute-done((bf16[256,512]{1,0:T(8,128)(2,1)S(1)}, bf16[256,512]{1,0:T(8,128)(2,1)S(1)}, u32[]{:S(2)}, u32[]{:S(2)}) %collective-permute-start.1) | collective-permute-done | bytes 262176 | tf_op jit(solution)/shard_map/ppermute | solution.py:162
  46.9 5.7 %psum.28 = f32[256]{0:T(256)S(1)} all-reduce(f32[256]{0:T(256)S(1)} %get-tuple-element.33), channel_id=1, replica_groups=mesh['seq'=8,'tp'=4] {'tp'}, use_global_device_ids=true, to_apply=%region_1.2 | all-reduce | flops 256 | bytes 2048 | tf_op jit(solution)/shard_map/psum | solution.py:330
  52.8 2.0 collective-permute-start.4
  54.8 6.4 %collective-permute-done.3 = bf16[272,512]{1,0:T(8,128)(2,1)S(1)} collective-permute-done((bf16[272,512]{1,0:T(8,128)(2,1)S(1)}, bf16[272,512]{1,0:T(8,128)(2,1)S(1)}, u32[]{:S(2)}, u32[]{:S(2)}) %collective-permute-start.3) | collective-permute-done | bytes 278560 | tf_op jit(solution)/shard_map/ppermute | solution.py:201
  63.3 5.4 %collective-permute-done.5 = bf16[272,512]{1,0:T(8,128)(2,1)S(1)} collective-permute-done((bf16[272,512]{1,0:T(8,128)(2,1)S(1)}, bf16[272,512]{1,0:T(8,128)(2,1)S(1)}, u32[]{:S(2)}, u32[]{:S(2)}) %collective-permute-start.5) | collective-permute-done | bytes 278560 | tf_op jit(solution)/shard_map/ppermute | solution.py:201
  71.6 1.8 collective-permute-start.12
  73.7 4.8 %collective-permute-done.12 = bf16[272,512]{1,0:T(8,128)(2,1)S(1)} collective-permute-done((bf16[272,512]{1,0:T(8,128)(2,1)S(1)}, bf16[272,512]{1,0:T(8,128)(2,1)S(1)}, u32[]{:S(2)}, u32[]{:S(2)}) %collective-permute-start.12) | collective-permute-done | bytes 278560 | tf_op jit(solution)/shard_map/ppermute | solution.py:201
  78.5 2.2 collective-permute-start.14
  80.6 4.4 %collective-permute-done.14 = bf16[272,512]{1,0:T(8,128)(2,1)S(1)} collective-permute-done((bf16[272,512]{1,0:T(8,128)(2,1)S(1)}, bf16[272,512]{1,0:T(8,128)(2,1)S(1)}, u32[]{:S(2)}, u32[]{:S(2)}) %collective-permute-start.14) | collective-permute-done | bytes 278560 | tf_op jit(solution)/shard_map/ppermute | solution.py:201
  86.2 2.5 dynamic-slice_bitcast_fusion
  88.8 1.6 collective-permute-start.8
  90.6 7.6 %reshape.128 = bf16[2,2048,512]{2,1,0:T(8,128)(2,1)} reshape(bf16[2,2048,2,256]{3,2,1,0:T(2,128)(2,1)} %param.28) | data formatting | bytes 8388608 | tf_op jit(solution)/shard_map/reshape | solution.py:305
  98.3 8.8 %copy.87 = bf16[2048,3,512]{0,2,1:T(8,128)(2,1)} copy(bf16[2048,3,512]{2,0,1:T(8,128)(2,1)} %param.31) | data formatting | bytes 12582912 | tf_op args[14]
  107.2 5.1 %collective-permute-done.9 = bf16[2,256,512]{2,1,0:T(8,128)(2,1)S(1)} collective-permute-done((bf16[2,256,512]{2,1,0:T(8,128)(2,1)}, bf16[2,256,512]{2,1,0:T(8,128)(2,1)S(1)}, u32[]{:S(2)}, u32[]{:S(2)}) %collective-permute-start.9) | collective-permute-done | bytes 524320 | tf_op jit(solution)/shard_map/ppermute | solution.py:302
  112.3 18.8 %collective-permute-done.8 = bf16[2,256,512]{2,1,0:T(8,128)(2,1)S(1)} collective-permute-done((bf16[2,256,512]{2,1,0:T(8,128)(2,1)S(1)}, bf16[2,256,512]{2,1,0:T(8,128)(2,1)S(1)}, u32[]{:S(2)}, u32[]{:S(2)}) %collective-permute-start.8) | collective-permute-done | bytes 524320 | tf_op jit(solution)/shard_map/ppermute | solution.py:302
  131.9 1.6 pad_maximum_fusion
  133.5 2.1 gather_fusion
  135.5 3.2 %broadcast_select_fusion = bf16[4,2,256,512]{3,2,1,0:T(8,128)(2,1)} fusion(bf16[4,2,256,512]{3,2,1,0:T(8,128)(2,1)} %gather_fusion, pred[4]{0:T(512)(128)(4,1)S(1)} %compare_and_fusion), kind=kLoop, calls=%fused_computation.19 | loop fusion | flops 1048576 | bytes 4194308 | tf_op jit(solution)/shard_map/jit(_take)/select_n | solution.py:304
  139.8 9.3 %fusion.4 = f32[2,1280,512]{1,2,0:T(8,128)S(1)} fusion(bf16[2,4,512,512]{3,2,1,0:T(8,128)(2,1)} %bitcast.116, bf16[4,1280,512]{2,1,0:T(8,128)(2,1)} %all-gather.7.cloned.1.call-done), kind=kOutput, calls=%fused_computation.5 | convolution fusion | flops 5368709120 | bytes 14680064 | tf_op jit(solution)/shard_map/qtd,eqdf->etf/dot_general | solution.py:136
  151.6 8.9 %all-gather.9.cloned.1.call-done = bf16[4,768,512]{2,1,0:T(8,128)(2,1)} async-done(((bf16[1,768,512]{2,1,0:T(8,128)(2,1)}), bf16[4,768,512]{2,1,0:T(8,128)(2,1)}) %all-gather.9.cloned.1.call-update) | async-done | bytes 3145744 | tf_op jit(solution)/shard_map/all_gather | solution.py:130
  160.4 6.2 %fusion.19 = f32[2,768,512]{1,2,0:T(8,128)S(1)} fusion(bf16[2,4,512,512]{3,2,1,0:T(8,128)(2,1)} %bitcast.117, bf16[4,768,512]{2,1,0:T(8,128)(2,1)} %all-gather.9.cloned.1.call-done), kind=kOutput, calls=%fused_computation.20 | convolution fusion | flops 3221225472 | bytes 10485760 | tf_op jit(solution)/shard_map/qtd,eqdf->etf/dot_general | solution.py:136
  168.3 34.1 %all-gather.11.cloned.1.call-done = bf16[8,1280,256]{2,1,0:T(8,128)(2,1)} async-done(((bf16[2,1280,256]{2,1,0:T(8,128)(2,1)}), bf16[8,1280,256]{2,1,0:T(8,128)(2,1)}) %all-gather.11.cloned.1.call-update) | async-done | bytes 5242896 | tf_op jit(solution)/shard_map/all_gather | solution.py:140
  202.5 6.2 %fusion.14 = bf16[1280,512]{1,0:T(8,128)(2,1)S(1)} fusion(bf16[4,2,1280,256]{3,2,1,0:T(8,128)(2,1)} %bitcast.129, bf16[4,2,256,512]{3,2,1,0:T(8,128)(2,1)} %broadcast_select_fusion), kind=kOutput, calls=%fused_computation.11 | convolution fusion | flops 2685009920 | bytes 8650752 | tf_op jit(solution)/shard_map/qetf,qefd->td/dot_general | solution.py:141
  208.7 1.5 collective-permute-start.10
  210.8 3.6 %collective-permute-done.10 = bf16[256,256]{1,0:T(8,128)(2,1)S(1)} collective-permute-done((bf16[256,256]{1,0:T(8,128)(2,1)S(1)}, bf16[256,256]{1,0:T(8,128)(2,1)S(1)}, u32[]{:S(2)}, u32[]{:S(2)}) %collective-permute-start.10) | collective-permute-done | bytes 131104 | tf_op jit(solution)/shard_map/ppermute | solution.py:220
  217.8 14.7 %all-gather.13.cloned.1.call-done = bf16[8,768,256]{2,1,0:T(8,128)(2,1)} async-done(((bf16[2,768,256]{2,1,0:T(8,128)(2,1)}), bf16[8,768,256]{2,1,0:T(8,128)(2,1)}) %all-gather.13.cloned.1.call-update) | async-done | bytes 3145744 | tf_op jit(solution)/shard_map/all_gather | solution.py:140
  232.5 3.7 %bitcast_convert_fusion = bf16[768,512]{1,0:T(8,128)(2,1)S(1)} fusion(bf16[4,2,256,512]{3,2,1,0:T(8,128)(2,1)S(1)} %copy-done.2, bf16[4,2,768,256]{3,2,1,0:T(8,128)(2,1)} %bitcast.130), kind=kOutput, calls=%fused_computation.25 | convolution fusion | flops 1611005952 | bytes 6029312 | tf_op jit(solution)/shard_map/qetf,qefd->td/dot_general | solution.py:141
  238.3 3.6 %collective-permute-done.15 = bf16[256,256]{1,0:T(8,128)(2,1)S(1)} collective-permute-done((bf16[256,256]{1,0:T(8,128)(2,1)S(1)}, bf16[256,256]{1,0:T(8,128)(2,1)S(1)}, u32[]{:S(2)}, u32[]{:S(2)}) %collective-permute-start.15) | collective-permute-done | bytes 131104 | tf_op jit(solution)/shard_map/ppermute | solution.py:220
  243.2 1.5 collective-permute-start.16
  245.3 2.9 collective-permute-done.16
  249.8 1.8 collective-permute-start.17
  252.1 2.9 collective-permute-done.17
  256.6 2.2 collective-permute-start.18
  258.8 3.5 %collective-permute-done.18 = bf16[256,256]{1,0:T(8,128)(2,1)S(1)} collective-permute-done((bf16[256,256]{1,0:T(8,128)(2,1)S(1)}, bf16[256,256]{1,0:T(8,128)(2,1)S(1)}, u32[]{:S(2)}, u32[]{:S(2)}) %collective-permute-start.18) | collective-permute-done | bytes 131104 | tf_op jit(solution)/shard_map/ppermute | solution.py:220
  262.4 2.1 collective-permute-done.25
  266.6 2.9 collective-permute-done.19
  272.0 2.0 fusion.29
  274.0 5.5 %collective-permute-done.27 = bf16[256,512]{1,0:T(8,128)(2,1)S(1)} collective-permute-done((bf16[256,512]{1,0:T(8,128)(2,1)S(1)}, bf16[256,512]{1,0:T(8,128)(2,1)S(1)}, u32[]{:S(2)}, u32[]{:S(2)}) %collective-permute-start.27) | collective-permute-done | bytes 262176 | tf_op jit(solution)/shard_map/ppermute | solution.py:178
  279.6 2.0 convolution_add_fusion.1
  281.6 2.0 fusion.25
  283.7 3.3 %fusion.17 = f32[256,1536]{1,0:T(8,128)} fusion(f32[256,1536]{1,0:T(8,128)S(1)} %fusion.25, f32[256,1536]{1,0:T(8,128)S(1)} %convolution_add_fusion.1, bf16[256,512]{1,0:T(8,128)(2,1)S(1)} %collective-permute-done.28, bf16[2048,1536]{0,1:T(8,128)(2,1)} %bitcast.110, s32[]{:T(128)S(6)} %select_n.121), kind=kOutput, calls=%fused_computation.13 | convolution fusion | flops 403439616 | bytes 6553604 | tf_op jit(solution)/shard_map/dot_general | solution.py:179
  287.0 3.1 copy.101
  291.5 7.5 %all-reduce = (f32[256]{0:T(256)S(1)}, f32[256]{0:T(256)S(1)}, f32[256]{0:T(256)S(1)}) all-reduce(f32[256]{0:T(256)S(1)} %get-tuple-element.29, f32[256]{0:T(256)S(1)} %get-tuple-element.57, f32[256]{0:T(256)S(1)} %get-tuple-element.28), channel_id=1, replica_groups=mesh['seq'=8,'tp'=4] {'tp'}, use_global_device_ids=true, to_apply=%region_6.7 | all-reduce | flops 768 | bytes 6144 | tf_op jit(solution)/shard_map/psum | solution.py:356
  299.0 1.6 fusion.36
  (131 shorter events, 37.9 us)
Async XLA Ops:
  7.2 18.2 %copy-start = (bf16[512,2048]{1,0:T(8,128)(2,1)S(1)}, bf16[512,2048]{1,0:T(8,128)(2,1)}, u32[]{:S(2)}) copy-start(bf16[512,2048]{1,0:T(8,128)(2,1)} %param.24) | copy-start | bytes 6291460
  7.2 132.6 %all-gather.7.cloned.1.call-start = ((), (), s32[]{:S(2)}) async-start(), calls=%async_computation | async-start | bytes 6553600 | tf_op jit(solution)/shard_map/all_gather | solution.py:130
  25.4 7.8 %copy-start.14 = (f32[256,8]{0,1:T(8,128)S(1)}, f32[256,8]{0,1:T(8,128)}, u32[]{:S(2)}) copy-start(f32[256,8]{0,1:T(8,128)} %param.27) | copy-start | bytes 24580
  25.4 7.8 %copy-start.15 = (s32[256,8]{0,1:T(8,128)S(1)}, s32[256,8]{0,1:T(8,128)}, u32[]{:S(2)}) copy-start(s32[256,8]{0,1:T(8,128)} %param.26) | copy-start | bytes 24580
  25.4 20.2 %copy-start.13 = (bf16[256,512]{1,0:T(8,128)(2,1)S(1)}, bf16[256,512]{1,0:T(8,128)(2,1)}, u32[]{:S(2)}) copy-start(bf16[256,512]{1,0:T(8,128)(2,1)} %param.17) | copy-start | bytes 786436
  28.5 24.1 %copy-start.16 = (f32[512]{0:T(512)S(1)}, f32[512]{0:T(512)}, u32[]{:S(2)}) copy-start(f32[512]{0:T(512)} %param.25) | copy-start | bytes 6148
  30.0 9.0 %collective-permute-start.2 = (bf16[256,512]{1,0:T(8,128)(2,1)S(1)}, bf16[256,512]{1,0:T(8,128)(2,1)S(1)}, u32[]{:S(2)}, u32[]{:S(2)}) collective-permute-start(bf16[256,512]{1,0:T(8,128)(2,1)S(1)} %get-tuple-element.42), channel_id=1, source_target_pairs={{0,3},{1,0},{2,1},{3,2},{4,7},{5,4},{6,5},{7,6},{8,11},{9,8},{10,9... | collective-permute-start | bytes 786440 | tf_op jit(solution)/shard_map/ppermute | solution.py:162
  32.4 13.2 %collective-permute-start.1 = (bf16[256,512]{1,0:T(8,128)(2,1)S(1)}, bf16[256,512]{1,0:T(8,128)(2,1)S(1)}, u32[]{:S(2)}, u32[]{:S(2)}) collective-permute-start(bf16[256,512]{1,0:T(8,128)(2,1)S(1)} %get-tuple-element.43), channel_id=1, source_target_pairs={{0,2},{1,3},{2,0},{3,1},{4,6},{5,7},{6,4},{7,5},{8,10},{9,11},{10,... | collective-permute-start | bytes 786440 | tf_op jit(solution)/shard_map/ppermute | solution.py:162
  33.1 12.5 %collective-permute-start = (bf16[256,512]{1,0:T(8,128)(2,1)S(1)}, bf16[256,512]{1,0:T(8,128)(2,1)S(1)}, u32[]{:S(2)}, u32[]{:S(2)}) collective-permute-start(bf16[256,512]{1,0:T(8,128)(2,1)S(1)} %get-tuple-element.41), channel_id=1, source_target_pairs={{0,1},{1,2},{2,3},{3,0},{4,5},{5,6},{6,7},{7,4},{8,9},{9,10},{10,1... | collective-permute-start | bytes 786440 | tf_op jit(solution)/shard_map/ppermute | solution.py:162
  52.7 8.5 %collective-permute-start.3 = (bf16[272,512]{1,0:T(8,128)(2,1)S(1)}, bf16[272,512]{1,0:T(8,128)(2,1)S(1)}, u32[]{:S(2)}, u32[]{:S(2)}) collective-permute-start(bf16[272,512]{1,0:T(8,128)(2,1)S(1)} %pad_maximum_fusion.2), channel_id=1, source_target_pairs={{0,8},{8,16},{16,24},{24,28},{28,20},{20,12},{12,4},{4,0},{1,9},{9... | collective-permute-start | bytes 835592 | tf_op jit(solution)/shard_map/ppermute | solution.py:201
  52.8 9.7 %collective-permute-start.4 = (bf16[272,512]{1,0:T(8,128)(2,1)S(1)}, bf16[272,512]{1,0:T(8,128)(2,1)S(1)}, u32[]{:S(2)}, u32[]{:S(2)}) collective-permute-start(bf16[272,512]{1,0:T(8,128)(2,1)S(1)} %pad_maximum_fusion.2), channel_id=1, source_target_pairs={{0,4},{8,0},{16,8},{24,16},{28,24},{20,28},{12,20},{4,12},{1,5},{9... | collective-permute-start | bytes 835592 | tf_op jit(solution)/shard_map/ppermute | solution.py:205
  61.2 7.6 %collective-permute-start.5 = (bf16[272,512]{1,0:T(8,128)(2,1)S(1)}, bf16[272,512]{1,0:T(8,128)(2,1)S(1)}, u32[]{:S(2)}, u32[]{:S(2)}) collective-permute-start(bf16[272,512]{1,0:T(8,128)(2,1)S(1)} %collective-permute-done.3), channel_id=1, source_target_pairs={{0,8},{8,16},{16,24},{24,28},{28,20},{20,12},{12,4},{4,0},{1,9},{9... | collective-permute-start | bytes 835592 | tf_op jit(solution)/shard_map/ppermute | solution.py:201
  62.5 7.7 %collective-permute-start.6 = (bf16[272,512]{1,0:T(8,128)(2,1)S(1)}, bf16[272,512]{1,0:T(8,128)(2,1)S(1)}, u32[]{:S(2)}, u32[]{:S(2)}) collective-permute-start(bf16[272,512]{1,0:T(8,128)(2,1)S(1)} %collective-permute-done.4), channel_id=1, source_target_pairs={{0,4},{8,0},{16,8},{24,16},{28,24},{20,28},{12,20},{4,12},{1,5},{9... | collective-permute-start | bytes 835592 | tf_op jit(solution)/shard_map/ppermute | solution.py:205
  70.2 14.8 %copy-start.3 = (bf16[5,272,512]{2,1,0:T(8,128)(2,1)}, bf16[5,272,512]{2,1,0:T(8,128)(2,1)S(1)}, u32[]{:S(2)}) copy-start(bf16[5,272,512]{2,1,0:T(8,128)(2,1)S(1)} %bitcast_dynamic-update-slice_fusion) | copy-start | bytes 4177924
  71.5 88.9 %all-gather.9.cloned.1.call-start = ((), (), s32[]{:S(2)}) async-start(), calls=%async_computation.1 | async-start | bytes 3932160 | tf_op jit(solution)/shard_map/all_gather | solution.py:130
  71.6 6.9 %collective-permute-start.12 = (bf16[272,512]{1,0:T(8,128)(2,1)S(1)}, bf16[272,512]{1,0:T(8,128)(2,1)S(1)}, u32[]{:S(2)}, u32[]{:S(2)}) collective-permute-start(bf16[272,512]{1,0:T(8,128)(2,1)S(1)} %collective-permute-done.5), channel_id=1, source_target_pairs={{0,8},{8,16},{16,24},{24,28},{28,20},{20,12},{12,4},{4,0},{1,9},{9... | collective-permute-start | bytes 835592 | tf_op jit(solution)/shard_map/ppermute | solution.py:201
  73.4 7.2 %collective-permute-start.13 = (bf16[272,512]{1,0:T(8,128)(2,1)}, bf16[272,512]{1,0:T(8,128)(2,1)S(1)}, u32[]{:S(2)}, u32[]{:S(2)}) collective-permute-start(bf16[272,512]{1,0:T(8,128)(2,1)} %copy-done.12), channel_id=1, source_target_pairs={{0,4},{8,0},{16,8},{24,16},{28,24},{20,28},{12,20},{4,12},{1,5},{9... | collective-permute-start | bytes 835592 | tf_op jit(solution)/shard_map/ppermute | solution.py:205
  78.5 6.5 %collective-permute-start.14 = (bf16[272,512]{1,0:T(8,128)(2,1)S(1)}, bf16[272,512]{1,0:T(8,128)(2,1)S(1)}, u32[]{:S(2)}, u32[]{:S(2)}) collective-permute-start(bf16[272,512]{1,0:T(8,128)(2,1)S(1)} %collective-permute-done.12), channel_id=1, source_target_pairs={{0,8},{8,16},{16,24},{24,28},{28,20},{20,12},{12,4},{4,0},{1,9},{9... | collective-permute-start | bytes 835592 | tf_op jit(solution)/shard_map/ppermute | solution.py:201
  80.6 8.1 %copy-start.6 = (bf16[272,512]{1,0:T(8,128)(2,1)}, bf16[272,512]{1,0:T(8,128)(2,1)S(1)}, u32[]{:S(2)}) copy-start(bf16[272,512]{1,0:T(8,128)(2,1)S(1)} %collective-permute-done.13) | copy-start | bytes 835588
  86.2 116.3 %all-gather.11.cloned.1.call-start = ((), (), s32[]{:S(2)}) async-start(), calls=%async_computation.2 | async-start | bytes 6553600 | tf_op jit(solution)/shard_map/all_gather | solution.py:140
  88.8 23.5 %collective-permute-start.9 = (bf16[2,256,512]{2,1,0:T(8,128)(2,1)}, bf16[2,256,512]{2,1,0:T(8,128)(2,1)S(1)}, u32[]{:S(2)}, u32[]{:S(2)}) collective-permute-start(bf16[2,256,512]{2,1,0:T(8,128)(2,1)} %get-tuple-element.39), channel_id=1, source_target_pairs={{0,3},{1,0},{2,1},{3,2},{4,7},{5,4},{6,5},{7,6},{8,11},{9,8},{10,9... | collective-permute-start | bytes 1572872 | tf_op jit(solution)/shard_map/ppermute | solution.py:302
  88.8 42.3 %collective-permute-start.8 = (bf16[2,256,512]{2,1,0:T(8,128)(2,1)S(1)}, bf16[2,256,512]{2,1,0:T(8,128)(2,1)S(1)}, u32[]{:S(2)}, u32[]{:S(2)}) collective-permute-start(bf16[2,256,512]{2,1,0:T(8,128)(2,1)S(1)} %get-tuple-element.40), channel_id=1, source_target_pairs={{0,2},{1,3},{2,0},{3,1},{4,6},{5,7},{6,4},{7,5},{8,10},{9,11},{10,... | collective-permute-start | bytes 1572872 | tf_op jit(solution)/shard_map/ppermute | solution.py:302
  90.4 40.7 %collective-permute-start.7 = (bf16[2,256,512]{2,1,0:T(8,128)(2,1)S(1)}, bf16[2,256,512]{2,1,0:T(8,128)(2,1)}, u32[]{:S(2)}, u32[]{:S(2)}) collective-permute-start(bf16[2,256,512]{2,1,0:T(8,128)(2,1)S(1)} %get-tuple-element.38), channel_id=1, source_target_pairs={{0,1},{1,2},{2,3},{3,0},{4,5},{5,6},{6,7},{7,4},{8,9},{9,10},{10,1... | collective-permute-start | bytes 1572872 | tf_op jit(solution)/shard_map/ppermute | solution.py:302
  112.3 18.8 %copy-start.10 = (bf16[2,256,512]{2,1,0:T(8,128)(2,1)}, bf16[2,256,512]{2,1,0:T(8,128)(2,1)S(1)}, u32[]{:S(2)}) copy-start(bf16[2,256,512]{2,1,0:T(8,128)(2,1)S(1)} %collective-permute-done.9) | copy-start | bytes 1572868
  151.4 81.0 %all-gather.13.cloned.1.call-start = ((), (), s32[]{:S(2)}) async-start(), calls=%async_computation.3 | async-start | bytes 3932160 | tf_op jit(solution)/shard_map/all_gather | solution.py:140
  202.5 30.0 %copy-start.2 = (bf16[4,2,256,512]{3,2,1,0:T(8,128)(2,1)S(1)}, bf16[4,2,256,512]{3,2,1,0:T(8,128)(2,1)}, u32[]{:S(2)}) copy-start(bf16[4,2,256,512]{3,2,1,0:T(8,128)(2,1)} %broadcast_select_fusion) | copy-start | bytes 6291460
  208.7 5.7 %collective-permute-start.10 = (bf16[256,256]{1,0:T(8,128)(2,1)S(1)}, bf16[256,256]{1,0:T(8,128)(2,1)S(1)}, u32[]{:S(2)}, u32[]{:S(2)}) collective-permute-start(bf16[256,256]{1,0:T(8,128)(2,1)S(1)} %get-tuple-element.55), channel_id=1, source_target_pairs={{0,8},{8,16},{16,24},{24,28},{28,20},{20,12},{12,4},{4,0},{1,9},{9... | collective-permute-start | bytes 393224 | tf_op jit(solution)/shard_map/ppermute | solution.py:220
  210.2 5.4 %collective-permute-start.20 = (bf16[256,256]{1,0:T(8,128)(2,1)S(1)}, bf16[256,256]{1,0:T(8,128)(2,1)S(1)}, u32[]{:S(2)}, u32[]{:S(2)}) collective-permute-start(bf16[256,256]{1,0:T(8,128)(2,1)S(1)} %get-tuple-element.56), channel_id=1, source_target_pairs={{0,4},{8,0},{16,8},{24,16},{28,24},{20,28},{12,20},{4,12},{1,5},{9... | collective-permute-start | bytes 393224 | tf_op jit(solution)/shard_map/ppermute | solution.py:220
  215.7 20.5 %collective-permute-start.11 = (bf16[256,256]{1,0:T(8,128)(2,1)S(1)}, bf16[256,256]{1,0:T(8,128)(2,1)S(1)}, u32[]{:S(2)}, u32[]{:S(2)}) collective-permute-start(bf16[256,256]{1,0:T(8,128)(2,1)S(1)} %get-tuple-element.53), channel_id=1, source_target_pairs={{0,8},{8,16},{16,24},{24,28},{28,20},{20,12},{12,4},{4,0},{1,9},{9... | collective-permute-start | bytes 393224 | tf_op jit(solution)/shard_map/ppermute | solution.py:220
  217.2 18.9 %collective-permute-start.21 = (bf16[256,256]{1,0:T(8,128)(2,1)S(1)}, bf16[256,256]{1,0:T(8,128)(2,1)S(1)}, u32[]{:S(2)}, u32[]{:S(2)}) collective-permute-start(bf16[256,256]{1,0:T(8,128)(2,1)S(1)} %get-tuple-element.54), channel_id=1, source_target_pairs={{0,4},{8,0},{16,8},{24,16},{28,24},{20,28},{12,20},{4,12},{1,5},{9... | collective-permute-start | bytes 393224 | tf_op jit(solution)/shard_map/ppermute | solution.py:220
  236.1 20.4 %copy-start.5 = (bf16[1280,512]{1,0:T(8,128)(2,1)S(1)}, bf16[1280,512]{1,0:T(8,128)(2,1)}, u32[]{:S(2)}) copy-start(bf16[1280,512]{1,0:T(8,128)(2,1)} %copy-done.4) | copy-start | bytes 3932164
  236.2 5.7 %collective-permute-start.15 = (bf16[256,256]{1,0:T(8,128)(2,1)S(1)}, bf16[256,256]{1,0:T(8,128)(2,1)S(1)}, u32[]{:S(2)}, u32[]{:S(2)}) collective-permute-start(bf16[256,256]{1,0:T(8,128)(2,1)S(1)} %get-tuple-element.64), channel_id=1, source_target_pairs={{0,8},{8,16},{16,24},{24,28},{28,20},{20,12},{12,4},{4,0},{1,9},{9... | collective-permute-start | bytes 393224 | tf_op jit(solution)/shard_map/ppermute | solution.py:220
  237.8 32.4 %copy-start.17 = (f32[512]{0:T(512)S(1)}, f32[512]{0:T(512)}, u32[]{:S(2)}) copy-start(f32[512]{0:T(512)} %param.30) | copy-start | bytes 6148
  237.8 5.4 %collective-permute-start.22 = (bf16[256,256]{1,0:T(8,128)(2,1)S(1)}, bf16[256,256]{1,0:T(8,128)(2,1)S(1)}, u32[]{:S(2)}, u32[]{:S(2)}) collective-permute-start(bf16[256,256]{1,0:T(8,128)(2,1)S(1)} %get-tuple-element.65), channel_id=1, source_target_pairs={{0,4},{8,0},{16,8},{24,16},{28,24},{20,28},{12,20},{4,12},{1,5},{9... | collective-permute-start | bytes 393224 | tf_op jit(solution)/shard_map/ppermute | solution.py:220
  243.2 5.0 %collective-permute-start.16 = (bf16[256,256]{1,0:T(8,128)(2,1)S(1)}, bf16[256,256]{1,0:T(8,128)(2,1)S(1)}, u32[]{:S(2)}, u32[]{:S(2)}) collective-permute-start(bf16[256,256]{1,0:T(8,128)(2,1)S(1)} %get-tuple-element.62), channel_id=1, source_target_pairs={{0,8},{8,16},{16,24},{24,28},{28,20},{20,12},{12,4},{4,0},{1,9},{9... | collective-permute-start | bytes 393224 | tf_op jit(solution)/shard_map/ppermute | solution.py:220
  244.8 5.0 %collective-permute-start.23 = (bf16[256,256]{1,0:T(8,128)(2,1)S(1)}, bf16[256,256]{1,0:T(8,128)(2,1)S(1)}, u32[]{:S(2)}, u32[]{:S(2)}) collective-permute-start(bf16[256,256]{1,0:T(8,128)(2,1)S(1)} %get-tuple-element.63), channel_id=1, source_target_pairs={{0,4},{8,0},{16,8},{24,16},{28,24},{20,28},{12,20},{4,12},{1,5},{9... | collective-permute-start | bytes 393224 | tf_op jit(solution)/shard_map/ppermute | solution.py:220
  249.8 5.2 %collective-permute-start.17 = (bf16[256,256]{1,0:T(8,128)(2,1)S(1)}, bf16[256,256]{1,0:T(8,128)(2,1)S(1)}, u32[]{:S(2)}, u32[]{:S(2)}) collective-permute-start(bf16[256,256]{1,0:T(8,128)(2,1)S(1)} %get-tuple-element.60), channel_id=1, source_target_pairs={{0,8},{8,16},{16,24},{24,28},{28,20},{20,12},{12,4},{4,0},{1,9},{9... | collective-permute-start | bytes 393224 | tf_op jit(solution)/shard_map/ppermute | solution.py:220
  251.6 5.0 %collective-permute-start.24 = (bf16[256,256]{1,0:T(8,128)(2,1)S(1)}, bf16[256,256]{1,0:T(8,128)(2,1)S(1)}, u32[]{:S(2)}, u32[]{:S(2)}) collective-permute-start(bf16[256,256]{1,0:T(8,128)(2,1)S(1)} %get-tuple-element.61), channel_id=1, source_target_pairs={{0,4},{8,0},{16,8},{24,16},{28,24},{20,28},{12,20},{4,12},{1,5},{9... | collective-permute-start | bytes 393224 | tf_op jit(solution)/shard_map/ppermute | solution.py:220
  256.6 5.8 %collective-permute-start.18 = (bf16[256,256]{1,0:T(8,128)(2,1)S(1)}, bf16[256,256]{1,0:T(8,128)(2,1)S(1)}, u32[]{:S(2)}, u32[]{:S(2)}) collective-permute-start(bf16[256,256]{1,0:T(8,128)(2,1)S(1)} %get-tuple-element.51), channel_id=1, source_target_pairs={{0,8},{8,16},{16,24},{24,28},{28,20},{20,12},{12,4},{4,0},{1,9},{9... | collective-permute-start | bytes 393224 | tf_op jit(solution)/shard_map/ppermute | solution.py:220
  258.8 5.6 %collective-permute-start.25 = (bf16[256,256]{1,0:T(8,128)(2,1)S(1)}, bf16[256,256]{1,0:T(8,128)(2,1)S(1)}, u32[]{:S(2)}, u32[]{:S(2)}) collective-permute-start(bf16[256,256]{1,0:T(8,128)(2,1)S(1)} %get-tuple-element.52), channel_id=1, source_target_pairs={{0,4},{8,0},{16,8},{24,16},{28,24},{20,28},{12,20},{4,12},{1,5},{9... | collective-permute-start | bytes 393224 | tf_op jit(solution)/shard_map/ppermute | solution.py:220
  264.5 5.0 %collective-permute-start.19 = (bf16[256,256]{1,0:T(8,128)(2,1)S(1)}, bf16[256,256]{1,0:T(8,128)(2,1)S(1)}, u32[]{:S(2)}, u32[]{:S(2)}) collective-permute-start(bf16[256,256]{1,0:T(8,128)(2,1)S(1)} %get-tuple-element.49), channel_id=1, source_target_pairs={{0,8},{8,16},{16,24},{24,28},{28,20},{20,12},{12,4},{4,0},{1,9},{9... | collective-permute-start | bytes 393224 | tf_op jit(solution)/shard_map/ppermute | solution.py:220
  265.1 5.0 %collective-permute-start.26 = (bf16[256,256]{1,0:T(8,128)(2,1)S(1)}, bf16[256,256]{1,0:T(8,128)(2,1)S(1)}, u32[]{:S(2)}, u32[]{:S(2)}) collective-permute-start(bf16[256,256]{1,0:T(8,128)(2,1)S(1)} %get-tuple-element.50), channel_id=1, source_target_pairs={{0,4},{8,0},{16,8},{24,16},{28,24},{20,28},{12,20},{4,12},{1,5},{9... | collective-permute-start | bytes 393224 | tf_op jit(solution)/shard_map/ppermute | solution.py:220
  271.0 10.6 %collective-permute-start.29 = (bf16[256,512]{1,0:T(8,128)(2,1)S(1)}, bf16[256,512]{1,0:T(8,128)(2,1)S(1)}, u32[]{:S(2)}, u32[]{:S(2)}) collective-permute-start(bf16[256,512]{1,0:T(8,128)(2,1)S(1)} %get-tuple-element.59), channel_id=1, source_target_pairs={{0,3},{1,0},{2,1},{3,2},{4,7},{5,4},{6,5},{7,6},{8,11},{9,8},{10,9... | collective-permute-start | bytes 786440 | tf_op jit(solution)/shard_map/ppermute | solution.py:178
  271.0 8.6 %collective-permute-start.27 = (bf16[256,512]{1,0:T(8,128)(2,1)S(1)}, bf16[256,512]{1,0:T(8,128)(2,1)S(1)}, u32[]{:S(2)}, u32[]{:S(2)}) collective-permute-start(bf16[256,512]{1,0:T(8,128)(2,1)S(1)} %get-tuple-element.59), channel_id=1, source_target_pairs={{0,1},{1,2},{2,3},{3,0},{4,5},{5,6},{6,7},{7,4},{8,9},{9,10},{10,1... | collective-permute-start | bytes 786440 | tf_op jit(solution)/shard_map/ppermute | solution.py:178
  271.5 12.2 %collective-permute-start.28 = (bf16[256,512]{1,0:T(8,128)(2,1)S(1)}, bf16[256,512]{1,0:T(8,128)(2,1)S(1)}, u32[]{:S(2)}, u32[]{:S(2)}) collective-permute-start(bf16[256,512]{1,0:T(8,128)(2,1)S(1)} %get-tuple-element.59), channel_id=1, source_target_pairs={{0,2},{1,3},{2,0},{3,1},{4,6},{5,7},{6,4},{7,5},{8,10},{9,11},{10,... | collective-permute-start | bytes 786440 | tf_op jit(solution)/shard_map/ppermute | solution.py:178
  287.0 12.0 %copy-start.18 = (f32[512]{0:T(512)S(1)}, f32[512]{0:T(512)}, u32[]{:S(2)}) copy-start(f32[512]{0:T(512)} %param.33) | copy-start | bytes 6148
  287.0 12.0 %copy-start.19 = (f32[512]{0:T(512)S(1)}, f32[512]{0:T(512)}, u32[]{:S(2)}) copy-start(f32[512]{0:T(512)} %param.32) | copy-start | bytes 6148
  290.0 13.1 %copy-start.1 = (bf16[512,2048]{1,0:T(8,128)(2,1)S(1)}, bf16[512,2048]{1,0:T(8,128)(2,1)}, u32[]{:S(2)}) copy-start(bf16[512,2048]{1,0:T(8,128)(2,1)} %param.24) | copy-start | bytes 6291460
  (6 other events, 13.4 us)
Sparse Core Ops, SparseCore 0:
  71.7 55.4 all-gather.6
  128.7 31.6 all-gather.8
  162.0 40.4 all-gather.10
  203.9 28.5 all-gather.12

commit v14 on v13

--- a/solution.py
+++ b/solution.py
@@ -210,18 +210,24 @@
 
 def ring_reduce_scatter(by_offset, cycle):
     count = len(cycle)
-    width = by_offset[0].shape[1]
-    halves = []
-    for direction in (1, -1):
-        cols = slice(0, width // 2) if direction == 1 else slice(width // 2, width)
-        pairs = [(cycle[p], cycle[(p + direction) % count]) for p in range(count)]
-        acc = by_offset[(-direction) % count][:, cols].astype(jnp.float32)
-        for step in range(count - 1):
-            received = lax.ppermute(acc.astype(jnp.bfloat16), "seq", pairs)
-            offset = (-direction * (step + 2)) % count
-            acc = received.astype(jnp.float32) + by_offset[offset][:, cols].astype(jnp.float32)
-        halves.append(acc)
-    return jnp.concatenate(halves, axis=1)
+    forward = [(cycle[p], cycle[(p + 1) % count]) for p in range(count)]
+    backward = [(cycle[p], cycle[(p - 1) % count]) for p in range(count)]
+
+    def block(offset):
+        return by_offset[offset % count].astype(jnp.float32)
+
+    total = block(0)
+    for pairs, hops, sign in ((forward, count - 1 - count // 2, 1), (backward, count // 2, -1)):
+        if hops == 0:
+            continue
+        acc = block(sign * hops)
+        for step in range(1, hops + 1):
+            received = lax.ppermute(acc.astype(jnp.bfloat16), "seq", pairs).astype(jnp.float32)
+            if step < hops:
+                acc = received + block(sign * (hops - step))
+            else:
+                total = total + received
+    return total
 
 
 def dispatch_experts(moe_in, expert_ids, route_weights, expert_gate_up, expert_down, experts_all, capacity):

time: 311 us -> 306 us (0.984)
  Pallas kernels: 16.8 us -> 11.6 us
  starting transfers between devices: 29.2 us -> 24.4 us
    all_gather x2, waiting for transfers between devices: 8.87 us -> 21.3 us  [dense_experts(): rows = lax.all_gather(rows_q, 'tp', axis=0, tiled=False)]
    ppermute x14 -> x7, waiting for transfers between devices: 27.6 us -> 19.7 us  [ring_reduce_scatter(): lax.ppermute(acc.astype(jnp.bfloat16), 'seq', pairs).astype(jnp.float32)]
    ppermute x14 -> x7, starting transfers between devices: 14.9 us -> 7.76 us  [ring_reduce_scatter(): lax.ppermute(acc.astype(jnp.bfloat16), 'seq', pairs).astype(jnp.float32)]
    all_gather x2, waiting for transfers between devices: 48.8 us -> 43.5 us  [dense_experts(): weighted = lax.all_gather(weighted, 'tp', axis=0, tiled=False)]
    pallas_call x1, Pallas kernels: 16.8 us -> 11.6 us  [flash_attention(): pl.pallas_call(kernel, grid_spec=grid_spec, out_shape=jax.ShapeDtypeStruc...]
    ppermute x3, starting transfers between devices: 3.11 us -> 7.31 us  [ring_all_gather(): behind = lax.ppermute(behind, 'seq', backward)]
    unnamed x49 -> x47, local copies, waits for them, and re-layouts: 12.3 us -> 12 us
  transfers between devices with their start and end apart: 34 -> 27, of which waited for: 26 -> 18; matrix products, arithmetic and copies ran while one was open for 21% -> 18% of each run, Pallas kernels for 0% -> 0%
where the time goes in v14:
time: 306 us; the launch traced here: 304 us
  waiting for transfers between devices  153 us (50%)
  matrix products  37.4 us (12%)
  local copies, waits for them, and re-layouts  35.3 us (12%)
  starting transfers between devices  24.4 us (8%)
  other arithmetic  15.2 us (5%)
  between operations  14.2 us (5%)
  blocking collectives  13.1 us (4%)
  Pallas kernels  11.6 us (4%)
    all_gather x2, waiting for transfers between devices, dense_experts(): weighted = lax.all_gather(weighted, 'tp', axis=0, tiled=False)  43.5 us
    ppermute x3, waiting for transfers between devices, body(): pieces.append(lax.ppermute(piece, 'tp', pairs))  26.5 us
    ppermute x4, waiting for transfers between devices, ring_all_gather(): ahead = lax.ppermute(ahead, 'seq', forward)  23.9 us
    all_gather x2, waiting for transfers between devices, dense_experts(): rows = lax.all_gather(rows_q, 'tp', axis=0, tiled=False)  21.3 us
    ppermute x7, waiting for transfers between devices, ring_reduce_scatter(): lax.ppermute(acc.astype(jnp.bfloat16), 'seq', pairs).astype(jnp.float32)  19.7 us
    dot_general x2, matrix products, dense_experts(): jnp.einsum('qtd,eqdf->etf', rows, gate_up_split, preferred_element_type=j...  15.2 us
    ppermute x3, waiting for transfers between devices, permute_reduce_scatter(): total = total + lax.ppermute(piece, 'tp', pairs).astype(jnp.float32)  12.3 us
    unnamed x47, local copies, waits for them, and re-layouts  12 us
  transfers between devices with their start and end apart: 27, of which 18 were waited for; matrix products, arithmetic and copies ran while one was open for 18% of the time, Pallas kernels for 0%

profile of v14, /device:TPU:0, one launch (start us, length us, event | category | flops | bytes accessed | tf_op | source)
XLA Modules:
  0.0 304.0 jit_solution(17876953295520227572)
XLA Ops:
  7.3 1.4 dynamic_slice.50.len_ref
  8.6 11.6 %shard_map.192 = bf16[256,512]{1,0:T(8,128)(2,1)} custom-call(s32[1]{0:T(128)} %dynamic_slice.50.len_ref, bf16[256,512]{1,0:T(8,128)(2,1)} %q_ref.1, bf16[4096,512]{1,0:T(8,128)(2,1)} %bitcast.114, bf16[4096,512]{1,0:T(8,128)(2,1)} %bitcast.115, bf16[256,512]{1,0:T(8,128)(2,1)} %nk_ref.1, bf16[256,512]{1,0:T(8,128)(2,1)} %nv_ref.1), custom_call_target="tpu_custom_call" | custom-call | tf_op jit(solution)/shard_map/pallas_call | solution.py:94
  20.2 3.0 %fusion.52 = f32[256,2048]{1,0:T(8,128)} fusion(bf16[256,512]{1,0:T(8,128)(2,1)} %shard_map.192, bf16[512,2048]{1,0:T(8,128)(2,1)S(1)} %copy-done), kind=kOutput, calls=%fused_computation.109 | convolution fusion | flops 536870912 | bytes 4456448 | tf_op jit(solution)/shard_map/dot_general | solution.py:329
  23.3 1.5 dynamic-slice_convert_fusion.2
  24.8 2.5 collective-permute-start.2
  28.1 5.7 %collective-permute-done.2 = bf16[256,512]{1,0:T(8,128)(2,1)S(1)} collective-permute-done((bf16[256,512]{1,0:T(8,128)(2,1)S(1)}, bf16[256,512]{1,0:T(8,128)(2,1)S(1)}, u32[]{:S(2)}, u32[]{:S(2)}) %collective-permute-start.2) | collective-permute-done | bytes 262176 | tf_op jit(solution)/shard_map/ppermute | solution.py:162
  33.8 6.6 %collective-permute-done.1 = bf16[256,512]{1,0:T(8,128)(2,1)S(1)} collective-permute-done((bf16[256,512]{1,0:T(8,128)(2,1)S(1)}, bf16[256,512]{1,0:T(8,128)(2,1)S(1)}, u32[]{:S(2)}, u32[]{:S(2)}) %collective-permute-start.1) | collective-permute-done | bytes 262176 | tf_op jit(solution)/shard_map/ppermute | solution.py:162
  41.7 5.7 %psum.28 = f32[256]{0:T(256)S(1)} all-reduce(f32[256]{0:T(256)S(1)} %get-tuple-element.35), channel_id=1, replica_groups=mesh['seq'=8,'tp'=4] {'tp'}, use_global_device_ids=true, to_apply=%region_1.2 | all-reduce | flops 256 | bytes 2048 | tf_op jit(solution)/shard_map/psum | solution.py:336
  47.5 1.8 collective-permute-start.3
  49.6 6.4 %collective-permute-done.3 = bf16[272,512]{1,0:T(8,128)(2,1)S(1)} collective-permute-done((bf16[272,512]{1,0:T(8,128)(2,1)S(1)}, bf16[272,512]{1,0:T(8,128)(2,1)S(1)}, u32[]{:S(2)}, u32[]{:S(2)}) %collective-permute-start.3) | collective-permute-done | bytes 278560 | tf_op jit(solution)/shard_map/ppermute | solution.py:201
  56.0 1.7 collective-permute-start.5
  57.8 5.0 %collective-permute-start.6 = (bf16[272,512]{1,0:T(8,128)(2,1)S(1)}, bf16[272,512]{1,0:T(8,128)(2,1)S(1)}, u32[]{:S(2)}, u32[]{:S(2)}) collective-permute-start(bf16[272,512]{1,0:T(8,128)(2,1)S(1)} %collective-permute-done.4), channel_id=1, source_target_pairs={{0,4},{8,0},{16,8},{24,16},{28,24},{20,28},{12,20},{4,12},{1,5},{9... | collective-permute-start | bytes 835592 | tf_op jit(solution)/shard_map/ppermute | solution.py:205
  62.8 6.0 %collective-permute-done.5 = bf16[272,512]{1,0:T(8,128)(2,1)S(1)} collective-permute-done((bf16[272,512]{1,0:T(8,128)(2,1)S(1)}, bf16[272,512]{1,0:T(8,128)(2,1)S(1)}, u32[]{:S(2)}, u32[]{:S(2)}) %collective-permute-start.5) | collective-permute-done | bytes 278560 | tf_op jit(solution)/shard_map/ppermute | solution.py:201
  70.4 2.0 collective-permute-start.11
  72.4 5.2 %collective-permute-done.10 = bf16[272,512]{1,0:T(8,128)(2,1)S(1)} collective-permute-done((bf16[272,512]{1,0:T(8,128)(2,1)S(1)}, bf16[272,512]{1,0:T(8,128)(2,1)S(1)}, u32[]{:S(2)}, u32[]{:S(2)}) %collective-permute-start.10) | collective-permute-done | bytes 278560 | tf_op jit(solution)/shard_map/ppermute | solution.py:201
  77.9 6.3 %collective-permute-done.12 = bf16[272,512]{1,0:T(8,128)(2,1)S(1)} collective-permute-done((bf16[272,512]{1,0:T(8,128)(2,1)S(1)}, bf16[272,512]{1,0:T(8,128)(2,1)S(1)}, u32[]{:S(2)}, u32[]{:S(2)}) %collective-permute-start.12) | collective-permute-done | bytes 278560 | tf_op jit(solution)/shard_map/ppermute | solution.py:201
  85.4 2.6 dynamic-slice_bitcast_fusion
  88.9 7.7 %reshape.128 = bf16[2,2048,512]{2,1,0:T(8,128)(2,1)} reshape(bf16[2,2048,2,256]{3,2,1,0:T(2,128)(2,1)} %param.28) | data formatting | bytes 8388608 | tf_op jit(solution)/shard_map/reshape | solution.py:311
  96.5 8.8 %copy.87 = bf16[2048,3,512]{0,2,1:T(8,128)(2,1)} copy(bf16[2048,3,512]{2,0,1:T(8,128)(2,1)} %param.31) | data formatting | bytes 12582912 | tf_op args[14]
  105.4 6.4 %collective-permute-done.9 = bf16[2,256,512]{2,1,0:T(8,128)(2,1)S(1)} collective-permute-done((bf16[2,256,512]{2,1,0:T(8,128)(2,1)}, bf16[2,256,512]{2,1,0:T(8,128)(2,1)S(1)}, u32[]{:S(2)}, u32[]{:S(2)}) %collective-permute-start.9) | collective-permute-done | bytes 524320 | tf_op jit(solution)/shard_map/ppermute | solution.py:308
  111.8 19.8 %collective-permute-done.8 = bf16[2,256,512]{2,1,0:T(8,128)(2,1)S(1)} collective-permute-done((bf16[2,256,512]{2,1,0:T(8,128)(2,1)S(1)}, bf16[2,256,512]{2,1,0:T(8,128)(2,1)S(1)}, u32[]{:S(2)}, u32[]{:S(2)}) %collective-permute-start.8) | collective-permute-done | bytes 524320 | tf_op jit(solution)/shard_map/ppermute | solution.py:308
  132.4 1.6 pad_maximum_fusion
  134.0 2.0 gather_fusion
  136.0 3.2 %broadcast_select_fusion = bf16[4,2,256,512]{3,2,1,0:T(8,128)(2,1)} fusion(bf16[4,2,256,512]{3,2,1,0:T(8,128)(2,1)} %gather_fusion, pred[4]{0:T(512)(128)(4,1)S(1)} %compare_and_fusion), kind=kLoop, calls=%fused_computation.19 | loop fusion | flops 1048576 | bytes 4194308 | tf_op jit(solution)/shard_map/jit(_take)/select_n | solution.py:310
  139.4 21.3 %all-gather.9.cloned.1.call-done = bf16[4,768,512]{2,1,0:T(8,128)(2,1)} async-done(((bf16[1,768,512]{2,1,0:T(8,128)(2,1)}), bf16[4,768,512]{2,1,0:T(8,128)(2,1)}) %all-gather.9.cloned.1.call-update) | async-done | bytes 3145744 | tf_op jit(solution)/shard_map/all_gather | solution.py:130
  160.7 6.2 %fusion.19 = f32[2,768,512]{1,2,0:T(8,128)S(1)} fusion(bf16[2,4,512,512]{3,2,1,0:T(8,128)(2,1)} %bitcast.116, bf16[4,768,512]{2,1,0:T(8,128)(2,1)} %all-gather.9.cloned.1.call-done), kind=kOutput, calls=%fused_computation.20 | convolution fusion | flops 3221225472 | bytes 10485760 | tf_op jit(solution)/shard_map/qtd,eqdf->etf/dot_general | solution.py:136
  169.6 9.0 %fusion.4 = f32[2,1280,512]{1,2,0:T(8,128)S(1)} fusion(bf16[2,4,512,512]{3,2,1,0:T(8,128)(2,1)} %bitcast.117, bf16[4,1280,512]{2,1,0:T(8,128)(2,1)} %all-gather.7.cloned.1.call-done), kind=kOutput, calls=%fused_computation.5 | convolution fusion | flops 5368709120 | bytes 14680064 | tf_op jit(solution)/shard_map/qtd,eqdf->etf/dot_general | solution.py:136
  179.5 1.5 copy.91
  181.0 16.3 %all-gather.13.cloned.1.call-done = bf16[8,768,256]{2,1,0:T(8,128)(2,1)} async-done(((bf16[2,768,256]{2,1,0:T(8,128)(2,1)}), bf16[8,768,256]{2,1,0:T(8,128)(2,1)}) %all-gather.13.cloned.1.call-update) | async-done | bytes 3145744 | tf_op jit(solution)/shard_map/all_gather | solution.py:140
  197.3 4.5 %bitcast_convert_fusion = bf16[768,512]{1,0:T(8,128)(2,1)S(1)} fusion(bf16[4,2,256,512]{3,2,1,0:T(8,128)(2,1)} %broadcast_select_fusion, bf16[4,2,768,256]{3,2,1,0:T(8,128)(2,1)} %bitcast.130), kind=kOutput, calls=%fused_computation.25 | convolution fusion | flops 1611005952 | bytes 6029312 | tf_op jit(solution)/shard_map/qetf,qefd->td/dot_general | solution.py:141
  201.8 1.5 collective-permute-start.16
  203.9 6.4 %collective-permute-done.16 = bf16[256,512]{1,0:T(8,128)(2,1)S(1)} collective-permute-done((bf16[256,512]{1,0:T(8,128)(2,1)S(1)}, bf16[256,512]{1,0:T(8,128)(2,1)S(1)}, u32[]{:S(2)}, u32[]{:S(2)}) %collective-permute-start.16) | collective-permute-done | bytes 262176 | tf_op jit(solution)/shard_map/ppermute | solution.py:225
  210.4 1.5 collective-permute-start.17
  211.9 27.3 %all-gather.11.cloned.1.call-done = bf16[8,1280,256]{2,1,0:T(8,128)(2,1)} async-done(((bf16[2,1280,256]{2,1,0:T(8,128)(2,1)}), bf16[8,1280,256]{2,1,0:T(8,128)(2,1)}) %all-gather.11.cloned.1.call-update) | async-done | bytes 5242896 | tf_op jit(solution)/shard_map/all_gather | solution.py:140
  239.2 5.4 %fusion.14 = bf16[1280,512]{1,0:T(8,128)(2,1)S(1)} fusion(bf16[4,2,1280,256]{3,2,1,0:T(8,128)(2,1)} %bitcast.129, bf16[4,2,256,512]{3,2,1,0:T(8,128)(2,1)S(1)} %copy-done.2), kind=kOutput, calls=%fused_computation.11 | convolution fusion | flops 2685009920 | bytes 8650752 | tf_op jit(solution)/shard_map/qetf,qefd->td/dot_general | solution.py:141
  245.9 1.5 collective-permute-start.14
  247.9 6.4 %collective-permute-done.14 = bf16[256,512]{1,0:T(8,128)(2,1)S(1)} collective-permute-done((bf16[256,512]{1,0:T(8,128)(2,1)S(1)}, bf16[256,512]{1,0:T(8,128)(2,1)S(1)}, u32[]{:S(2)}, u32[]{:S(2)}) %collective-permute-start.14) | collective-permute-done | bytes 262176 | tf_op jit(solution)/shard_map/ppermute | solution.py:225
  256.3 1.5 collective-permute-start.15
  257.8 5.3 %collective-permute-done.19 = bf16[256,512]{1,0:T(8,128)(2,1)S(1)} collective-permute-done((bf16[256,512]{1,0:T(8,128)(2,1)S(1)}, bf16[256,512]{1,0:T(8,128)(2,1)S(1)}, u32[]{:S(2)}, u32[]{:S(2)}) %collective-permute-start.19) | collective-permute-done | bytes 262176 | tf_op jit(solution)/shard_map/ppermute | solution.py:225
  266.4 2.0 fusion.29
  268.4 5.5 %collective-permute-done.20 = bf16[256,512]{1,0:T(8,128)(2,1)S(1)} collective-permute-done((bf16[256,512]{1,0:T(8,128)(2,1)S(1)}, bf16[256,512]{1,0:T(8,128)(2,1)S(1)}, u32[]{:S(2)}, u32[]{:S(2)}) %collective-permute-start.20) | collective-permute-done | bytes 262176 | tf_op jit(solution)/shard_map/ppermute | solution.py:178
  273.9 2.0 convolution_add_fusion.1
  276.0 2.0 fusion.25
  278.0 3.3 %fusion.17 = f32[256,1536]{1,0:T(8,128)} fusion(f32[256,1536]{1,0:T(8,128)S(1)} %fusion.25, f32[256,1536]{1,0:T(8,128)S(1)} %convolution_add_fusion.1, bf16[256,512]{1,0:T(8,128)(2,1)S(1)} %collective-permute-done.21, bf16[2048,1536]{0,1:T(8,128)(2,1)} %bitcast.110, s32[]{:T(128)S(6)} %select_n.121), kind=kOutput, calls=%fused_computation.13 | convolution fusion | flops 403439616 | bytes 6553604 | tf_op jit(solution)/shard_map/dot_general | solution.py:179
  281.3 3.1 %copy.101 = f32[256,1536]{0,1:T(8,128)} copy(f32[256,1536]{1,0:T(8,128)} %fusion.17) | data formatting | bytes 3145728 | tf_op jit(solution)/shard_map/add | solution.py:179
  284.4 1.5 multiply_reduce_fusion
  285.8 7.5 %all-reduce = (f32[256]{0:T(256)S(1)}, f32[256]{0:T(256)S(1)}, f32[256]{0:T(256)S(1)}) all-reduce(f32[256]{0:T(256)S(1)} %get-tuple-element.29, f32[256]{0:T(256)S(1)} %get-tuple-element.33, f32[256]{0:T(256)S(1)} %get-tuple-element.28), channel_id=1, replica_groups=mesh['seq'=8,'tp'=4] {'tp'}, use_global_device_ids=true, to_apply=%region_6.7 | all-reduce | flops 768 | bytes 6144 | tf_op jit(solution)/shard_map/psum | solution.py:362
  293.3 1.6 fusion.36
  (112 shorter events, 21.2 us)
Async XLA Ops:
  7.2 13.0 %copy-start = (bf16[512,2048]{1,0:T(8,128)(2,1)S(1)}, bf16[512,2048]{1,0:T(8,128)(2,1)}, u32[]{:S(2)}) copy-start(bf16[512,2048]{1,0:T(8,128)(2,1)} %param.24) | copy-start | bytes 6291460
  7.2 132.2 %all-gather.7.cloned.1.call-start = ((), (), s32[]{:S(2)}) async-start(), calls=%async_computation | async-start | bytes 6553600 | tf_op jit(solution)/shard_map/all_gather | solution.py:130
  20.2 7.8 %copy-start.13 = (f32[256,8]{0,1:T(8,128)S(1)}, f32[256,8]{0,1:T(8,128)}, u32[]{:S(2)}) copy-start(f32[256,8]{0,1:T(8,128)} %param.27) | copy-start | bytes 24580
  20.2 7.8 %copy-start.14 = (s32[256,8]{0,1:T(8,128)S(1)}, s32[256,8]{0,1:T(8,128)}, u32[]{:S(2)}) copy-start(s32[256,8]{0,1:T(8,128)} %param.26) | copy-start | bytes 24580
  20.2 20.2 %copy-start.12 = (bf16[256,512]{1,0:T(8,128)(2,1)S(1)}, bf16[256,512]{1,0:T(8,128)(2,1)}, u32[]{:S(2)}) copy-start(bf16[256,512]{1,0:T(8,128)(2,1)} %param.17) | copy-start | bytes 786436
  23.3 24.1 %copy-start.15 = (f32[512]{0:T(512)S(1)}, f32[512]{0:T(512)}, u32[]{:S(2)}) copy-start(f32[512]{0:T(512)} %param.25) | copy-start | bytes 6148
  24.8 9.0 %collective-permute-start.2 = (bf16[256,512]{1,0:T(8,128)(2,1)S(1)}, bf16[256,512]{1,0:T(8,128)(2,1)S(1)}, u32[]{:S(2)}, u32[]{:S(2)}) collective-permute-start(bf16[256,512]{1,0:T(8,128)(2,1)S(1)} %get-tuple-element.44), channel_id=1, source_target_pairs={{0,3},{1,0},{2,1},{3,2},{4,7},{5,4},{6,5},{7,6},{8,11},{9,8},{10,9... | collective-permute-start | bytes 786440 | tf_op jit(solution)/shard_map/ppermute | solution.py:162
  27.2 13.2 %collective-permute-start.1 = (bf16[256,512]{1,0:T(8,128)(2,1)S(1)}, bf16[256,512]{1,0:T(8,128)(2,1)S(1)}, u32[]{:S(2)}, u32[]{:S(2)}) collective-permute-start(bf16[256,512]{1,0:T(8,128)(2,1)S(1)} %get-tuple-element.45), channel_id=1, source_target_pairs={{0,2},{1,3},{2,0},{3,1},{4,6},{5,7},{6,4},{7,5},{8,10},{9,11},{10,... | collective-permute-start | bytes 786440 | tf_op jit(solution)/shard_map/ppermute | solution.py:162
  27.9 12.5 %collective-permute-start = (bf16[256,512]{1,0:T(8,128)(2,1)S(1)}, bf16[256,512]{1,0:T(8,128)(2,1)S(1)}, u32[]{:S(2)}, u32[]{:S(2)}) collective-permute-start(bf16[256,512]{1,0:T(8,128)(2,1)S(1)} %get-tuple-element.43), channel_id=1, source_target_pairs={{0,1},{1,2},{2,3},{3,0},{4,5},{5,6},{6,7},{7,4},{8,9},{9,10},{10,1... | collective-permute-start | bytes 786440 | tf_op jit(solution)/shard_map/ppermute | solution.py:162
  47.5 8.5 %collective-permute-start.3 = (bf16[272,512]{1,0:T(8,128)(2,1)S(1)}, bf16[272,512]{1,0:T(8,128)(2,1)S(1)}, u32[]{:S(2)}, u32[]{:S(2)}) collective-permute-start(bf16[272,512]{1,0:T(8,128)(2,1)S(1)} %pad_maximum_fusion.2), channel_id=1, source_target_pairs={{0,8},{8,16},{16,24},{24,28},{28,20},{20,12},{12,4},{4,0},{1,9},{9... | collective-permute-start | bytes 835592 | tf_op jit(solution)/shard_map/ppermute | solution.py:201
  49.3 8.5 %collective-permute-start.4 = (bf16[272,512]{1,0:T(8,128)(2,1)S(1)}, bf16[272,512]{1,0:T(8,128)(2,1)S(1)}, u32[]{:S(2)}, u32[]{:S(2)}) collective-permute-start(bf16[272,512]{1,0:T(8,128)(2,1)S(1)} %pad_maximum_fusion.2), channel_id=1, source_target_pairs={{0,4},{8,0},{16,8},{24,16},{28,24},{20,28},{12,20},{4,12},{1,5},{9... | collective-permute-start | bytes 835592 | tf_op jit(solution)/shard_map/ppermute | solution.py:205
  56.0 12.9 %collective-permute-start.5 = (bf16[272,512]{1,0:T(8,128)(2,1)S(1)}, bf16[272,512]{1,0:T(8,128)(2,1)S(1)}, u32[]{:S(2)}, u32[]{:S(2)}) collective-permute-start(bf16[272,512]{1,0:T(8,128)(2,1)S(1)} %collective-permute-done.3), channel_id=1, source_target_pairs={{0,8},{8,16},{16,24},{24,28},{28,20},{20,12},{12,4},{4,0},{1,9},{9... | collective-permute-start | bytes 835592 | tf_op jit(solution)/shard_map/ppermute | solution.py:201
  57.8 11.1 %collective-permute-start.6 = (bf16[272,512]{1,0:T(8,128)(2,1)S(1)}, bf16[272,512]{1,0:T(8,128)(2,1)S(1)}, u32[]{:S(2)}, u32[]{:S(2)}) collective-permute-start(bf16[272,512]{1,0:T(8,128)(2,1)S(1)} %collective-permute-done.4), channel_id=1, source_target_pairs={{0,4},{8,0},{16,8},{24,16},{28,24},{20,28},{12,20},{4,12},{1,5},{9... | collective-permute-start | bytes 835592 | tf_op jit(solution)/shard_map/ppermute | solution.py:205
  68.9 1.4 copy-start.11
  68.9 15.3 %copy-start.3 = (bf16[5,272,512]{2,1,0:T(8,128)(2,1)}, bf16[5,272,512]{2,1,0:T(8,128)(2,1)S(1)}, u32[]{:S(2)}) copy-start(bf16[5,272,512]{2,1,0:T(8,128)(2,1)S(1)} %bitcast_dynamic-update-slice_fusion) | copy-start | bytes 4177924
  70.3 90.4 %all-gather.9.cloned.1.call-start = ((), (), s32[]{:S(2)}) async-start(), calls=%async_computation.1 | async-start | bytes 3932160 | tf_op jit(solution)/shard_map/all_gather | solution.py:130
  70.3 7.3 %collective-permute-start.10 = (bf16[272,512]{1,0:T(8,128)(2,1)S(1)}, bf16[272,512]{1,0:T(8,128)(2,1)S(1)}, u32[]{:S(2)}, u32[]{:S(2)}) collective-permute-start(bf16[272,512]{1,0:T(8,128)(2,1)S(1)} %collective-permute-done.5), channel_id=1, source_target_pairs={{0,8},{8,16},{16,24},{24,28},{28,20},{20,12},{12,4},{4,0},{1,9},{9... | collective-permute-start | bytes 835592 | tf_op jit(solution)/shard_map/ppermute | solution.py:201
  70.4 7.5 %collective-permute-start.11 = (bf16[272,512]{1,0:T(8,128)(2,1)}, bf16[272,512]{1,0:T(8,128)(2,1)S(1)}, u32[]{:S(2)}, u32[]{:S(2)}) collective-permute-start(bf16[272,512]{1,0:T(8,128)(2,1)} %copy-done.11), channel_id=1, source_target_pairs={{0,4},{8,0},{16,8},{24,16},{28,24},{20,28},{12,20},{4,12},{1,5},{9... | collective-permute-start | bytes 835592 | tf_op jit(solution)/shard_map/ppermute | solution.py:205
  77.6 6.5 %collective-permute-start.12 = (bf16[272,512]{1,0:T(8,128)(2,1)S(1)}, bf16[272,512]{1,0:T(8,128)(2,1)S(1)}, u32[]{:S(2)}, u32[]{:S(2)}) collective-permute-start(bf16[272,512]{1,0:T(8,128)(2,1)S(1)} %collective-permute-done.10), channel_id=1, source_target_pairs={{0,8},{8,16},{16,24},{24,28},{28,20},{20,12},{12,4},{4,0},{1,9},{9... | collective-permute-start | bytes 835592 | tf_op jit(solution)/shard_map/ppermute | solution.py:201
  77.9 10.0 %copy-start.5 = (bf16[272,512]{1,0:T(8,128)(2,1)}, bf16[272,512]{1,0:T(8,128)(2,1)S(1)}, u32[]{:S(2)}) copy-start(bf16[272,512]{1,0:T(8,128)(2,1)S(1)} %collective-permute-done.11) | copy-start | bytes 835588
  84.2 1.1 copy-start.7
  85.3 112.0 %all-gather.13.cloned.1.call-start = ((), (), s32[]{:S(2)}) async-start(), calls=%async_computation.3 | async-start | bytes 3932160 | tf_op jit(solution)/shard_map/all_gather | solution.py:140
  87.9 23.8 %collective-permute-start.9 = (bf16[2,256,512]{2,1,0:T(8,128)(2,1)}, bf16[2,256,512]{2,1,0:T(8,128)(2,1)S(1)}, u32[]{:S(2)}, u32[]{:S(2)}) collective-permute-start(bf16[2,256,512]{2,1,0:T(8,128)(2,1)} %get-tuple-element.41), channel_id=1, source_target_pairs={{0,3},{1,0},{2,1},{3,2},{4,7},{5,4},{6,5},{7,6},{8,11},{9,8},{10,9... | collective-permute-start | bytes 1572872 | tf_op jit(solution)/shard_map/ppermute | solution.py:308
  88.0 43.6 %collective-permute-start.8 = (bf16[2,256,512]{2,1,0:T(8,128)(2,1)S(1)}, bf16[2,256,512]{2,1,0:T(8,128)(2,1)S(1)}, u32[]{:S(2)}, u32[]{:S(2)}) collective-permute-start(bf16[2,256,512]{2,1,0:T(8,128)(2,1)S(1)} %get-tuple-element.42), channel_id=1, source_target_pairs={{0,2},{1,3},{2,0},{3,1},{4,6},{5,7},{6,4},{7,5},{8,10},{9,11},{10,... | collective-permute-start | bytes 1572872 | tf_op jit(solution)/shard_map/ppermute | solution.py:308
  88.6 43.2 %collective-permute-start.7 = (bf16[2,256,512]{2,1,0:T(8,128)(2,1)S(1)}, bf16[2,256,512]{2,1,0:T(8,128)(2,1)}, u32[]{:S(2)}, u32[]{:S(2)}) collective-permute-start(bf16[2,256,512]{2,1,0:T(8,128)(2,1)S(1)} %get-tuple-element.40), channel_id=1, source_target_pairs={{0,1},{1,2},{2,3},{3,0},{4,5},{5,6},{6,7},{7,4},{8,9},{9,10},{10,1... | collective-permute-start | bytes 1572872 | tf_op jit(solution)/shard_map/ppermute | solution.py:308
  111.8 20.1 %copy-start.9 = (bf16[2,256,512]{2,1,0:T(8,128)(2,1)}, bf16[2,256,512]{2,1,0:T(8,128)(2,1)S(1)}, u32[]{:S(2)}) copy-start(bf16[2,256,512]{2,1,0:T(8,128)(2,1)S(1)} %collective-permute-done.9) | copy-start | bytes 1572868
  131.6 0.8 copy-start.10
  136.0 3.3 %copy-start.6 = (bf16[272,512]{1,0:T(8,128)(2,1)S(1)}, bf16[272,512]{1,0:T(8,128)(2,1)}, u32[]{:S(2)}) copy-start(bf16[272,512]{1,0:T(8,128)(2,1)} %copy-done.5) | copy-start | bytes 835588
  136.0 3.3 %copy-start.8 = (bf16[272,512]{1,0:T(8,128)(2,1)S(1)}, bf16[272,512]{1,0:T(8,128)(2,1)}, u32[]{:S(2)}) copy-start(bf16[272,512]{1,0:T(8,128)(2,1)} %copy-done.7) | copy-start | bytes 835588
  168.6 70.6 %all-gather.11.cloned.1.call-start = ((), (), s32[]{:S(2)}) async-start(), calls=%async_computation.2 | async-start | bytes 6553600 | tf_op jit(solution)/shard_map/all_gather | solution.py:140
  197.3 41.9 %copy-start.2 = (bf16[4,2,256,512]{3,2,1,0:T(8,128)(2,1)S(1)}, bf16[4,2,256,512]{3,2,1,0:T(8,128)(2,1)}, u32[]{:S(2)}) copy-start(bf16[4,2,256,512]{3,2,1,0:T(8,128)(2,1)} %broadcast_select_fusion) | copy-start | bytes 6291460
  201.8 8.5 %collective-permute-start.16 = (bf16[256,512]{1,0:T(8,128)(2,1)S(1)}, bf16[256,512]{1,0:T(8,128)(2,1)S(1)}, u32[]{:S(2)}, u32[]{:S(2)}) collective-permute-start(bf16[256,512]{1,0:T(8,128)(2,1)S(1)} %get-tuple-element.54), channel_id=1, source_target_pairs={{0,4},{8,0},{16,8},{24,16},{28,24},{20,28},{12,20},{4,12},{1,5},{9... | collective-permute-start | bytes 786440 | tf_op jit(solution)/shard_map/ppermute | solution.py:225
  203.3 41.2 %collective-permute-start.13 = (bf16[256,512]{1,0:T(8,128)(2,1)S(1)}, bf16[256,512]{1,0:T(8,128)(2,1)S(1)}, u32[]{:S(2)}, u32[]{:S(2)}) collective-permute-start(bf16[256,512]{1,0:T(8,128)(2,1)S(1)} %get-tuple-element.53), channel_id=1, source_target_pairs={{0,8},{8,16},{16,24},{24,28},{28,20},{20,12},{12,4},{4,0},{1,9},{9... | collective-permute-start | bytes 786440 | tf_op jit(solution)/shard_map/ppermute | solution.py:225
  210.4 34.2 %collective-permute-start.17 = (bf16[256,512]{1,0:T(8,128)(2,1)S(1)}, bf16[256,512]{1,0:T(8,128)(2,1)}, u32[]{:S(2)}, u32[]{:S(2)}) collective-permute-start(bf16[256,512]{1,0:T(8,128)(2,1)S(1)} %add_convert_fusion.2), channel_id=1, source_target_pairs={{0,4},{8,0},{16,8},{24,16},{28,24},{20,28},{12,20},{4,12},{1,5},{9... | collective-permute-start | bytes 786440 | tf_op jit(solution)/shard_map/ppermute | solution.py:225
  244.5 11.1 %copy-start.4 = (bf16[1280,512]{1,0:T(8,128)(2,1)}, bf16[1280,512]{1,0:T(8,128)(2,1)S(1)}, u32[]{:S(2)}) copy-start(bf16[1280,512]{1,0:T(8,128)(2,1)S(1)} %fusion.14) | copy-start | bytes 3932164
  245.8 18.7 %copy-start.16 = (f32[512]{0:T(512)S(1)}, f32[512]{0:T(512)}, u32[]{:S(2)}) copy-start(f32[512]{0:T(512)} %param.30) | copy-start | bytes 6148
  245.9 8.5 %collective-permute-start.14 = (bf16[256,512]{1,0:T(8,128)(2,1)S(1)}, bf16[256,512]{1,0:T(8,128)(2,1)S(1)}, u32[]{:S(2)}, u32[]{:S(2)}) collective-permute-start(bf16[256,512]{1,0:T(8,128)(2,1)S(1)} %get-tuple-element.51), channel_id=1, source_target_pairs={{0,8},{8,16},{16,24},{24,28},{28,20},{20,12},{12,4},{4,0},{1,9},{9... | collective-permute-start | bytes 786440 | tf_op jit(solution)/shard_map/ppermute | solution.py:225
  247.4 8.2 %collective-permute-start.18 = (bf16[256,512]{1,0:T(8,128)(2,1)S(1)}, bf16[256,512]{1,0:T(8,128)(2,1)S(1)}, u32[]{:S(2)}, u32[]{:S(2)}) collective-permute-start(bf16[256,512]{1,0:T(8,128)(2,1)S(1)} %get-tuple-element.52), channel_id=1, source_target_pairs={{0,4},{8,0},{16,8},{24,16},{28,24},{20,28},{12,20},{4,12},{1,5},{9... | collective-permute-start | bytes 786440 | tf_op jit(solution)/shard_map/ppermute | solution.py:225
  255.7 7.4 %collective-permute-start.19 = (bf16[256,512]{1,0:T(8,128)(2,1)S(1)}, bf16[256,512]{1,0:T(8,128)(2,1)S(1)}, u32[]{:S(2)}, u32[]{:S(2)}) collective-permute-start(bf16[256,512]{1,0:T(8,128)(2,1)S(1)} %get-tuple-element.50), channel_id=1, source_target_pairs={{0,4},{8,0},{16,8},{24,16},{28,24},{20,28},{12,20},{4,12},{1,5},{9... | collective-permute-start | bytes 786440 | tf_op jit(solution)/shard_map/ppermute | solution.py:225
  256.3 7.1 %collective-permute-start.15 = (bf16[256,512]{1,0:T(8,128)(2,1)S(1)}, bf16[256,512]{1,0:T(8,128)(2,1)S(1)}, u32[]{:S(2)}, u32[]{:S(2)}) collective-permute-start(bf16[256,512]{1,0:T(8,128)(2,1)S(1)} %get-tuple-element.49), channel_id=1, source_target_pairs={{0,8},{8,16},{16,24},{24,28},{28,20},{20,12},{12,4},{4,0},{1,9},{9... | collective-permute-start | bytes 786440 | tf_op jit(solution)/shard_map/ppermute | solution.py:225
  265.4 10.6 %collective-permute-start.22 = (bf16[256,512]{1,0:T(8,128)(2,1)S(1)}, bf16[256,512]{1,0:T(8,128)(2,1)S(1)}, u32[]{:S(2)}, u32[]{:S(2)}) collective-permute-start(bf16[256,512]{1,0:T(8,128)(2,1)S(1)} %get-tuple-element.55), channel_id=1, source_target_pairs={{0,3},{1,0},{2,1},{3,2},{4,7},{5,4},{6,5},{7,6},{8,11},{9,8},{10,9... | collective-permute-start | bytes 786440 | tf_op jit(solution)/shard_map/ppermute | solution.py:178
  265.4 8.6 %collective-permute-start.20 = (bf16[256,512]{1,0:T(8,128)(2,1)S(1)}, bf16[256,512]{1,0:T(8,128)(2,1)S(1)}, u32[]{:S(2)}, u32[]{:S(2)}) collective-permute-start(bf16[256,512]{1,0:T(8,128)(2,1)S(1)} %get-tuple-element.55), channel_id=1, source_target_pairs={{0,1},{1,2},{2,3},{3,0},{4,5},{5,6},{6,7},{7,4},{8,9},{9,10},{10,1... | collective-permute-start | bytes 786440 | tf_op jit(solution)/shard_map/ppermute | solution.py:178
  265.9 12.2 %collective-permute-start.21 = (bf16[256,512]{1,0:T(8,128)(2,1)S(1)}, bf16[256,512]{1,0:T(8,128)(2,1)S(1)}, u32[]{:S(2)}, u32[]{:S(2)}) collective-permute-start(bf16[256,512]{1,0:T(8,128)(2,1)S(1)} %get-tuple-element.55), channel_id=1, source_target_pairs={{0,2},{1,3},{2,0},{3,1},{4,6},{5,7},{6,4},{7,5},{8,10},{9,11},{10,... | collective-permute-start | bytes 786440 | tf_op jit(solution)/shard_map/ppermute | solution.py:178
  281.3 12.0 %copy-start.17 = (f32[512]{0:T(512)S(1)}, f32[512]{0:T(512)}, u32[]{:S(2)}) copy-start(f32[512]{0:T(512)} %param.33) | copy-start | bytes 6148
  281.3 12.0 %copy-start.18 = (f32[512]{0:T(512)S(1)}, f32[512]{0:T(512)}, u32[]{:S(2)}) copy-start(f32[512]{0:T(512)} %param.32) | copy-start | bytes 6148
  284.4 13.1 %copy-start.1 = (bf16[512,2048]{1,0:T(8,128)(2,1)S(1)}, bf16[512,2048]{1,0:T(8,128)(2,1)}, u32[]{:S(2)}) copy-start(bf16[512,2048]{1,0:T(8,128)(2,1)} %param.24) | copy-start | bytes 6291460
Sparse Core Ops, SparseCore 0:
  70.4 59.4 all-gather.6
  131.4 29.1 all-gather.8
  168.7 28.5 all-gather.12
  198.7 40.4 all-gather.10

commit v15 on v14

--- a/solution.py
+++ b/solution.py
@@ -129,9 +129,7 @@
         gate_local = jnp.transpose(gate_local, (1, 0, 2)).reshape(local_experts, count * tokens)
         rows = lax.all_gather(rows_q, "tp", axis=0, tiled=False)
         if begin == 0:
-            rows, expert_gate_up, qkv_flat, down_full = lax.optimization_barrier(
-                (rows, expert_gate_up, qkv_flat, down_full)
-            )
+            rows, expert_gate_up, qkv_flat = lax.optimization_barrier((rows, expert_gate_up, qkv_flat))
         gate_up_split = expert_gate_up.reshape(local_experts, rows.shape[0], quarter, -1)
         projected = jnp.einsum("qtd,eqdf->etf", rows, gate_up_split, preferred_element_type=jnp.float32)
         activated = jax.nn.silu(projected[..., :hidden_quarter]) * projected[..., hidden_quarter:]
@@ -323,7 +321,9 @@
         new_keys,
         new_values,
     )
-    if not dense:
+    if dense:
+        attended, down_full = lax.optimization_barrier((attended, down_full))
+    else:
         gate_up_flat = expert_gate_up
         qkv_flat = qkv_proj.reshape(D, -1)
     attn_term = jnp.dot(attended, out_proj, preferred_element_type=jnp.float32)

time: 306 us -> 302 us (0.987)
  waiting for transfers between devices: 153 us -> 157 us
    all_gather x2, waiting for transfers between devices: 21.3 us -> 38.2 us  [dense_experts(): rows = lax.all_gather(rows_q, 'tp', axis=0, tiled=False)]
    ppermute x3, waiting for transfers between devices: 26.5 us -> 14.2 us  [body(): pieces.append(lax.ppermute(piece, 'tp', pairs))]
    ppermute x3, starting transfers between devices: 7.31 us -> 1.09 us  [ring_all_gather(): behind = lax.ppermute(behind, 'seq', backward)]
    unnamed x47 -> x41, local copies, waits for them, and re-layouts: 12 us -> 12.9 us
  transfers between devices with their start and end apart: 27 -> 27, of which waited for: 18 -> 19; matrix products, arithmetic and copies ran while one was open for 18% -> 16% of each run, Pallas kernels for 0% -> 3%
where the time goes in v15:
time: 302 us; the launch traced here: 301 us
  waiting for transfers between devices  157 us (52%)
  local copies, waits for them, and re-layouts  36.4 us (12%)
  matrix products  35.6 us (12%)
  starting transfers between devices  22 us (7%)
  between operations  14.2 us (5%)
  other arithmetic  13.4 us (4%)
  blocking collectives  13.3 us (4%)
  Pallas kernels  8.99 us (3%)
    all_gather x2, waiting for transfers between devices, dense_experts(): weighted = lax.all_gather(weighted, 'tp', axis=0, tiled=False)  43.9 us
    all_gather x2, waiting for transfers between devices, dense_experts(): rows = lax.all_gather(rows_q, 'tp', axis=0, tiled=False)  38.2 us
    ppermute x4, waiting for transfers between devices, ring_all_gather(): ahead = lax.ppermute(ahead, 'seq', forward)  22 us
    ppermute x7, waiting for transfers between devices, ring_reduce_scatter(): lax.ppermute(acc.astype(jnp.bfloat16), 'seq', pairs).astype(jnp.float32)  19.7 us
    dot_general x2, matrix products, dense_experts(): jnp.einsum('qtd,eqdf->etf', rows, gate_up_split, preferred_element_type=j...  15.2 us
    ppermute x3, waiting for transfers between devices, body(): pieces.append(lax.ppermute(piece, 'tp', pairs))  14.2 us
    unnamed x41, local copies, waits for them, and re-layouts  12.9 us
    ppermute x3, waiting for transfers between devices, permute_reduce_scatter(): total = total + lax.ppermute(piece, 'tp', pairs).astype(jnp.float32)  12.4 us
  transfers between devices with their start and end apart: 27, of which 19 were waited for; matrix products, arithmetic and copies ran while one was open for 16% of the time, Pallas kernels for 3%

profile of v15, /device:TPU:0, one launch (start us, length us, event | category | flops | bytes accessed | tf_op | source)
XLA Modules:
  0.0 301.2 jit_solution(2733067366744481690)
XLA Ops:
  7.3 2.8 dynamic-slice_bitcast_fusion
  10.1 2.4 collective-permute-start.2
  13.9 9.0 %shard_map.192 = bf16[256,512]{1,0:T(8,128)(2,1)} custom-call(s32[1]{0:T(128)} %dynamic_slice.50.len_ref, bf16[256,512]{1,0:T(8,128)(2,1)} %q_ref.1, bf16[4096,512]{1,0:T(8,128)(2,1)} %bitcast.114, bf16[4096,512]{1,0:T(8,128)(2,1)} %bitcast.115, bf16[256,512]{1,0:T(8,128)(2,1)} %nk_ref.1, bf16[256,512]{1,0:T(8,128)(2,1)} %nv_ref.1), custom_call_target="tpu_custom_call" | custom-call | tf_op jit(solution)/shard_map/pallas_call | solution.py:94
  23.0 2.1 collective-permute-done.2
  25.1 12.2 %collective-permute-done.1 = bf16[2,256,512]{2,1,0:T(8,128)(2,1)} collective-permute-done((bf16[2,256,512]{2,1,0:T(8,128)(2,1)}, bf16[2,256,512]{2,1,0:T(8,128)(2,1)}, u32[]{:S(2)}, u32[]{:S(2)}) %collective-permute-start.1) | collective-permute-done | bytes 524320 | tf_op jit(solution)/shard_map/ppermute | solution.py:306
  37.2 2.8 pad_maximum_fusion
  40.1 3.6 %gather_fusion = bf16[4,2,256,512]{3,2,1,0:T(8,128)(2,1)} fusion(bf16[4,2,256,512]{3,2,1,0:T(8,128)(2,1)} %pad_maximum_fusion, s32[1024]{0:T(1024)S(1)} %pad_clamp_fusion), kind=kCustom, calls=%fused_computation | custom fusion | bytes 4194320 | tf_op jit(solution)/shard_map/jit(_take)/gather | solution.py:308
  43.7 3.2 %broadcast_select_fusion = bf16[4,2,256,512]{3,2,1,0:T(8,128)(2,1)} fusion(bf16[4,2,256,512]{3,2,1,0:T(8,128)(2,1)} %gather_fusion, pred[4]{0:T(512)(128)(4,1)S(1)} %compare_and_fusion), kind=kLoop, calls=%fused_computation.19 | loop fusion | flops 1048576 | bytes 4194308 | tf_op jit(solution)/shard_map/jit(_take)/select_n | solution.py:308
  47.6 1.3 copy-done.2
  49.1 1.7 collective-permute-start.4
  51.0 3.6 %collective-permute-done.5 = bf16[256,512]{1,0:T(8,128)(2,1)S(1)} collective-permute-done((bf16[256,512]{1,0:T(8,128)(2,1)S(1)}, bf16[256,512]{1,0:T(8,128)(2,1)S(1)}, u32[]{:S(2)}, u32[]{:S(2)}) %collective-permute-start.5) | collective-permute-done | bytes 262176 | tf_op jit(solution)/shard_map/ppermute | solution.py:160
  54.6 8.9 %collective-permute-done.4 = bf16[256,512]{1,0:T(8,128)(2,1)S(1)} collective-permute-done((bf16[256,512]{1,0:T(8,128)(2,1)S(1)}, bf16[256,512]{1,0:T(8,128)(2,1)S(1)}, u32[]{:S(2)}, u32[]{:S(2)}) %collective-permute-start.4) | collective-permute-done | bytes 262176 | tf_op jit(solution)/shard_map/ppermute | solution.py:160
  64.8 5.8 %psum.28 = f32[256]{0:T(256)S(1)} all-reduce(f32[256]{0:T(256)S(1)} %get-tuple-element.37), channel_id=1, replica_groups=mesh['seq'=8,'tp'=4] {'tp'}, use_global_device_ids=true, to_apply=%region_1.2 | all-reduce | flops 256 | bytes 2048 | tf_op jit(solution)/shard_map/psum | solution.py:336
  70.8 1.8 collective-permute-start.6
  72.9 6.2 %collective-permute-done.6 = bf16[272,512]{1,0:T(8,128)(2,1)S(1)} collective-permute-done((bf16[272,512]{1,0:T(8,128)(2,1)S(1)}, bf16[272,512]{1,0:T(8,128)(2,1)S(1)}, u32[]{:S(2)}, u32[]{:S(2)}) %collective-permute-start.6) | collective-permute-done | bytes 278560 | tf_op jit(solution)/shard_map/ppermute | solution.py:199
  79.1 1.6 collective-permute-start.8
  81.2 5.3 %collective-permute-done.8 = bf16[272,512]{1,0:T(8,128)(2,1)S(1)} collective-permute-done((bf16[272,512]{1,0:T(8,128)(2,1)S(1)}, bf16[272,512]{1,0:T(8,128)(2,1)S(1)}, u32[]{:S(2)}, u32[]{:S(2)}) %collective-permute-start.8) | collective-permute-done | bytes 278560 | tf_op jit(solution)/shard_map/ppermute | solution.py:199
  89.0 1.6 collective-permute-start.10
  91.0 5.6 %collective-permute-done.10 = bf16[272,512]{1,0:T(8,128)(2,1)S(1)} collective-permute-done((bf16[272,512]{1,0:T(8,128)(2,1)S(1)}, bf16[272,512]{1,0:T(8,128)(2,1)S(1)}, u32[]{:S(2)}, u32[]{:S(2)}) %collective-permute-start.10) | collective-permute-done | bytes 278560 | tf_op jit(solution)/shard_map/ppermute | solution.py:199
  96.6 1.6 collective-permute-start.12
  98.2 5.0 %collective-permute-done.12 = bf16[272,512]{1,0:T(8,128)(2,1)S(1)} collective-permute-done((bf16[272,512]{1,0:T(8,128)(2,1)S(1)}, bf16[272,512]{1,0:T(8,128)(2,1)S(1)}, u32[]{:S(2)}, u32[]{:S(2)}) %collective-permute-start.12) | collective-permute-done | bytes 278560 | tf_op jit(solution)/shard_map/ppermute | solution.py:199
  104.4 7.6 %reshape.128 = bf16[2,2048,512]{2,1,0:T(8,128)(2,1)} reshape(bf16[2,2048,2,256]{3,2,1,0:T(2,128)(2,1)} %param.28) | data formatting | bytes 8388608 | tf_op jit(solution)/shard_map/reshape | solution.py:309
  112.1 8.9 %copy.87 = bf16[2048,3,512]{0,2,1:T(8,128)(2,1)} copy(bf16[2048,3,512]{2,0,1:T(8,128)(2,1)} %param.31) | data formatting | bytes 12582912 | tf_op args[14]
  121.1 8.1 %all-gather.7.cloned.1.call-done = bf16[4,1280,512]{2,1,0:T(8,128)(2,1)} async-done(((bf16[1,1280,512]{2,1,0:T(8,128)(2,1)}), bf16[4,1280,512]{2,1,0:T(8,128)(2,1)}) %all-gather.7.cloned.1.call-update) | async-done | bytes 5242896 | tf_op jit(solution)/shard_map/all_gather | solution.py:130
  129.2 30.1 %all-gather.9.cloned.1.call-done = bf16[4,768,512]{2,1,0:T(8,128)(2,1)} async-done(((bf16[1,768,512]{2,1,0:T(8,128)(2,1)}), bf16[4,768,512]{2,1,0:T(8,128)(2,1)}) %all-gather.9.cloned.1.call-update) | async-done | bytes 3145744 | tf_op jit(solution)/shard_map/all_gather | solution.py:130
  159.3 6.2 %fusion.19 = f32[2,768,512]{1,2,0:T(8,128)S(1)} fusion(bf16[2,4,512,512]{3,2,1,0:T(8,128)(2,1)} %bitcast.116, bf16[4,768,512]{2,1,0:T(8,128)(2,1)} %all-gather.9.cloned.1.call-done), kind=kOutput, calls=%fused_computation.20 | convolution fusion | flops 3221225472 | bytes 10485760 | tf_op jit(solution)/shard_map/qtd,eqdf->etf/dot_general | solution.py:134
  167.4 9.0 %fusion.4 = f32[2,1280,512]{1,2,0:T(8,128)S(1)} fusion(bf16[2,4,512,512]{3,2,1,0:T(8,128)(2,1)} %bitcast.117, bf16[4,1280,512]{2,1,0:T(8,128)(2,1)} %all-gather.7.cloned.1.call-done), kind=kOutput, calls=%fused_computation.5 | convolution fusion | flops 5368709120 | bytes 14680064 | tf_op jit(solution)/shard_map/qtd,eqdf->etf/dot_general | solution.py:134
  177.3 1.5 copy.91
  178.8 17.1 %all-gather.13.cloned.1.call-done = bf16[8,768,256]{2,1,0:T(8,128)(2,1)} async-done(((bf16[2,768,256]{2,1,0:T(8,128)(2,1)}), bf16[8,768,256]{2,1,0:T(8,128)(2,1)}) %all-gather.13.cloned.1.call-update) | async-done | bytes 3145744 | tf_op jit(solution)/shard_map/all_gather | solution.py:138
  195.9 4.3 %bitcast_convert_fusion = bf16[768,512]{1,0:T(8,128)(2,1)S(1)} fusion(bf16[4,2,256,512]{3,2,1,0:T(8,128)(2,1)} %broadcast_select_fusion, bf16[4,2,768,256]{3,2,1,0:T(8,128)(2,1)} %bitcast.129), kind=kOutput, calls=%fused_computation.25 | convolution fusion | flops 1611005952 | bytes 6029312 | tf_op jit(solution)/shard_map/qetf,qefd->td/dot_general | solution.py:139
  201.0 1.5 collective-permute-start.16
  203.0 6.4 %collective-permute-done.16 = bf16[256,512]{1,0:T(8,128)(2,1)S(1)} collective-permute-done((bf16[256,512]{1,0:T(8,128)(2,1)S(1)}, bf16[256,512]{1,0:T(8,128)(2,1)S(1)}, u32[]{:S(2)}, u32[]{:S(2)}) %collective-permute-start.16) | collective-permute-done | bytes 262176 | tf_op jit(solution)/shard_map/ppermute | solution.py:223
  209.5 1.5 collective-permute-start.17
  211.0 26.8 %all-gather.11.cloned.1.call-done = bf16[8,1280,256]{2,1,0:T(8,128)(2,1)} async-done(((bf16[2,1280,256]{2,1,0:T(8,128)(2,1)}), bf16[8,1280,256]{2,1,0:T(8,128)(2,1)}) %all-gather.11.cloned.1.call-update) | async-done | bytes 5242896 | tf_op jit(solution)/shard_map/all_gather | solution.py:138
  237.8 6.0 %fusion.14 = bf16[1280,512]{1,0:T(8,128)(2,1)S(1)} fusion(bf16[4,2,1280,256]{3,2,1,0:T(8,128)(2,1)} %bitcast.128, bf16[4,2,256,512]{3,2,1,0:T(8,128)(2,1)} %broadcast_select_fusion), kind=kOutput, calls=%fused_computation.11 | convolution fusion | flops 2685009920 | bytes 8650752 | tf_op jit(solution)/shard_map/qetf,qefd->td/dot_general | solution.py:139
  244.0 1.5 collective-permute-start.14
  246.1 6.4 %collective-permute-done.14 = bf16[256,512]{1,0:T(8,128)(2,1)S(1)} collective-permute-done((bf16[256,512]{1,0:T(8,128)(2,1)S(1)}, bf16[256,512]{1,0:T(8,128)(2,1)S(1)}, u32[]{:S(2)}, u32[]{:S(2)}) %collective-permute-start.14) | collective-permute-done | bytes 262176 | tf_op jit(solution)/shard_map/ppermute | solution.py:223
  254.5 1.5 collective-permute-start.15
  256.0 5.3 %collective-permute-done.19 = bf16[256,512]{1,0:T(8,128)(2,1)S(1)} collective-permute-done((bf16[256,512]{1,0:T(8,128)(2,1)S(1)}, bf16[256,512]{1,0:T(8,128)(2,1)S(1)}, u32[]{:S(2)}, u32[]{:S(2)}) %collective-permute-start.19) | collective-permute-done | bytes 262176 | tf_op jit(solution)/shard_map/ppermute | solution.py:223
  263.6 2.0 fusion.29
  265.7 5.5 %collective-permute-done.20 = bf16[256,512]{1,0:T(8,128)(2,1)S(1)} collective-permute-done((bf16[256,512]{1,0:T(8,128)(2,1)S(1)}, bf16[256,512]{1,0:T(8,128)(2,1)S(1)}, u32[]{:S(2)}, u32[]{:S(2)}) %collective-permute-start.20) | collective-permute-done | bytes 262176 | tf_op jit(solution)/shard_map/ppermute | solution.py:176
  271.2 2.0 convolution_add_fusion.1
  273.2 2.0 fusion.25
  275.2 3.2 %fusion.17 = f32[256,1536]{1,0:T(8,128)} fusion(f32[256,1536]{1,0:T(8,128)S(1)} %fusion.25, f32[256,1536]{1,0:T(8,128)S(1)} %convolution_add_fusion.1, bf16[256,512]{1,0:T(8,128)(2,1)S(1)} %collective-permute-done.21, bf16[2048,1536]{0,1:T(8,128)(2,1)} %bitcast.110, s32[]{:T(128)S(6)} %select_n.121), kind=kOutput, calls=%fused_computation.13 | convolution fusion | flops 403439616 | bytes 6553604 | tf_op jit(solution)/shard_map/dot_general | solution.py:177
  278.5 3.1 %copy.101 = f32[256,1536]{0,1:T(8,128)} copy(f32[256,1536]{1,0:T(8,128)} %fusion.17) | data formatting | bytes 3145728 | tf_op jit(solution)/shard_map/add | solution.py:177
  281.6 1.5 multiply_reduce_fusion
  283.0 7.5 %all-reduce = (f32[256]{0:T(256)S(1)}, f32[256]{0:T(256)S(1)}, f32[256]{0:T(256)S(1)}) all-reduce(f32[256]{0:T(256)S(1)} %get-tuple-element.31, f32[256]{0:T(256)S(1)} %get-tuple-element.35, f32[256]{0:T(256)S(1)} %get-tuple-element.30), channel_id=1, replica_groups=mesh['seq'=8,'tp'=4] {'tp'}, use_global_device_ids=true, to_apply=%region_6.7 | all-reduce | flops 768 | bytes 6144 | tf_op jit(solution)/shard_map/psum | solution.py:362
  290.5 1.6 fusion.36
  (106 shorter events, 20.5 us)
Async XLA Ops:
  7.2 39.7 %copy-start = (bf16[512,2048]{1,0:T(8,128)(2,1)S(1)}, bf16[512,2048]{1,0:T(8,128)(2,1)}, u32[]{:S(2)}) copy-start(bf16[512,2048]{1,0:T(8,128)(2,1)} %param.24) | copy-start | bytes 6291460
  7.2 122.0 %all-gather.7.cloned.1.call-start = ((), (), s32[]{:S(2)}) async-start(), calls=%async_computation | async-start | bytes 6553600 | tf_op jit(solution)/shard_map/all_gather | solution.py:130
  7.3 6.1 %copy-start.15 = (s32[8]{0:T(128)S(1)}, s32[8]{0:T(128)}, u32[]{:S(2)}) copy-start(s32[8]{0:T(128)} %param.23) | copy-start | bytes 100
  10.1 14.9 %collective-permute-start.2 = (bf16[2,256,512]{2,1,0:T(8,128)(2,1)}, bf16[2,256,512]{2,1,0:T(8,128)(2,1)S(1)}, u32[]{:S(2)}, u32[]{:S(2)}) collective-permute-start(bf16[2,256,512]{2,1,0:T(8,128)(2,1)} %get-tuple-element.46), channel_id=1, source_target_pairs={{0,3},{1,0},{2,1},{3,2},{4,7},{5,4},{6,5},{7,6},{8,11},{9,8},{10,9... | collective-permute-start | bytes 1572872 | tf_op jit(solution)/shard_map/ppermute | solution.py:306
  12.5 24.7 %collective-permute-start.1 = (bf16[2,256,512]{2,1,0:T(8,128)(2,1)}, bf16[2,256,512]{2,1,0:T(8,128)(2,1)}, u32[]{:S(2)}, u32[]{:S(2)}) collective-permute-start(bf16[2,256,512]{2,1,0:T(8,128)(2,1)} %get-tuple-element.47), channel_id=1, source_target_pairs={{0,2},{1,3},{2,0},{3,1},{4,6},{5,7},{6,4},{7,5},{8,10},{9,11},{10,... | collective-permute-start | bytes 1572872 | tf_op jit(solution)/shard_map/ppermute | solution.py:306
  13.1 24.1 %collective-permute-start = (bf16[2,256,512]{2,1,0:T(8,128)(2,1)}, bf16[2,256,512]{2,1,0:T(8,128)(2,1)}, u32[]{:S(2)}, u32[]{:S(2)}) collective-permute-start(bf16[2,256,512]{2,1,0:T(8,128)(2,1)} %get-tuple-element.45), channel_id=1, source_target_pairs={{0,1},{1,2},{2,3},{3,0},{4,5},{5,6},{6,7},{7,4},{8,9},{9,10},{10,1... | collective-permute-start | bytes 1572872 | tf_op jit(solution)/shard_map/ppermute | solution.py:306
  13.9 9.0 %copy-start.9 = (f32[256,8]{0,1:T(8,128)S(1)}, f32[256,8]{0,1:T(8,128)}, u32[]{:S(2)}) copy-start(f32[256,8]{0,1:T(8,128)} %param.27) | copy-start | bytes 24580
  13.9 9.0 %copy-start.10 = (s32[256,8]{0,1:T(8,128)S(1)}, s32[256,8]{0,1:T(8,128)}, u32[]{:S(2)}) copy-start(s32[256,8]{0,1:T(8,128)} %param.26) | copy-start | bytes 24580
  43.7 3.2 %copy-start.7 = (bf16[256,512]{1,0:T(8,128)(2,1)S(1)}, bf16[256,512]{1,0:T(8,128)(2,1)}, u32[]{:S(2)}) copy-start(bf16[256,512]{1,0:T(8,128)(2,1)} %shard_map.192) | copy-start | bytes 786436
  46.9 16.6 %copy-start.8 = (bf16[256,512]{1,0:T(8,128)(2,1)S(1)}, bf16[256,512]{1,0:T(8,128)(2,1)}, u32[]{:S(2)}) copy-start(bf16[256,512]{1,0:T(8,128)(2,1)} %param.17) | copy-start | bytes 786436
  47.6 1.4 copy-start.2
  49.0 21.6 %copy-start.11 = (f32[512]{0:T(512)S(1)}, f32[512]{0:T(512)}, u32[]{:S(2)}) copy-start(f32[512]{0:T(512)} %param.25) | copy-start | bytes 6148
  49.1 5.5 %collective-permute-start.5 = (bf16[256,512]{1,0:T(8,128)(2,1)S(1)}, bf16[256,512]{1,0:T(8,128)(2,1)S(1)}, u32[]{:S(2)}, u32[]{:S(2)}) collective-permute-start(bf16[256,512]{1,0:T(8,128)(2,1)S(1)} %get-tuple-element.42), channel_id=1, source_target_pairs={{0,3},{1,0},{2,1},{3,2},{4,7},{5,4},{6,5},{7,6},{8,11},{9,8},{10,9... | collective-permute-start | bytes 786440 | tf_op jit(solution)/shard_map/ppermute | solution.py:160
  49.1 14.3 %collective-permute-start.4 = (bf16[256,512]{1,0:T(8,128)(2,1)S(1)}, bf16[256,512]{1,0:T(8,128)(2,1)S(1)}, u32[]{:S(2)}, u32[]{:S(2)}) collective-permute-start(bf16[256,512]{1,0:T(8,128)(2,1)S(1)} %get-tuple-element.43), channel_id=1, source_target_pairs={{0,2},{1,3},{2,0},{3,1},{4,6},{5,7},{6,4},{7,5},{8,10},{9,11},{10,... | collective-permute-start | bytes 786440 | tf_op jit(solution)/shard_map/ppermute | solution.py:160
  50.8 12.6 %collective-permute-start.3 = (bf16[256,512]{1,0:T(8,128)(2,1)S(1)}, bf16[256,512]{1,0:T(8,128)(2,1)S(1)}, u32[]{:S(2)}, u32[]{:S(2)}) collective-permute-start(bf16[256,512]{1,0:T(8,128)(2,1)S(1)} %get-tuple-element.41), channel_id=1, source_target_pairs={{0,1},{1,2},{2,3},{3,0},{4,5},{5,6},{6,7},{7,4},{8,9},{9,10},{10,1... | collective-permute-start | bytes 786440 | tf_op jit(solution)/shard_map/ppermute | solution.py:160
  70.8 8.3 %collective-permute-start.6 = (bf16[272,512]{1,0:T(8,128)(2,1)S(1)}, bf16[272,512]{1,0:T(8,128)(2,1)S(1)}, u32[]{:S(2)}, u32[]{:S(2)}) collective-permute-start(bf16[272,512]{1,0:T(8,128)(2,1)S(1)} %pad_maximum_fusion.2), channel_id=1, source_target_pairs={{0,8},{8,16},{16,24},{24,28},{28,20},{20,12},{12,4},{4,0},{1,9},{9... | collective-permute-start | bytes 835592 | tf_op jit(solution)/shard_map/ppermute | solution.py:199
  72.6 8.1 %collective-permute-start.7 = (bf16[272,512]{1,0:T(8,128)(2,1)S(1)}, bf16[272,512]{1,0:T(8,128)(2,1)S(1)}, u32[]{:S(2)}, u32[]{:S(2)}) collective-permute-start(bf16[272,512]{1,0:T(8,128)(2,1)S(1)} %pad_maximum_fusion.2), channel_id=1, source_target_pairs={{0,4},{8,0},{16,8},{24,16},{28,24},{20,28},{12,20},{4,12},{1,5},{9... | collective-permute-start | bytes 835592 | tf_op jit(solution)/shard_map/ppermute | solution.py:203
  79.1 7.4 %collective-permute-start.8 = (bf16[272,512]{1,0:T(8,128)(2,1)S(1)}, bf16[272,512]{1,0:T(8,128)(2,1)S(1)}, u32[]{:S(2)}, u32[]{:S(2)}) collective-permute-start(bf16[272,512]{1,0:T(8,128)(2,1)S(1)} %collective-permute-done.6), channel_id=1, source_target_pairs={{0,8},{8,16},{16,24},{24,28},{28,20},{20,12},{12,4},{4,0},{1,9},{9... | collective-permute-start | bytes 835592 | tf_op jit(solution)/shard_map/ppermute | solution.py:199
  80.7 6.9 %collective-permute-start.9 = (bf16[272,512]{1,0:T(8,128)(2,1)S(1)}, bf16[272,512]{1,0:T(8,128)(2,1)S(1)}, u32[]{:S(2)}, u32[]{:S(2)}) collective-permute-start(bf16[272,512]{1,0:T(8,128)(2,1)S(1)} %collective-permute-done.7), channel_id=1, source_target_pairs={{0,4},{8,0},{16,8},{24,16},{28,24},{20,28},{12,20},{4,12},{1,5},{9... | collective-permute-start | bytes 835592 | tf_op jit(solution)/shard_map/ppermute | solution.py:203
  88.9 70.4 %all-gather.9.cloned.1.call-start = ((), (), s32[]{:S(2)}) async-start(), calls=%async_computation.1 | async-start | bytes 3932160 | tf_op jit(solution)/shard_map/all_gather | solution.py:130
  89.0 7.6 %collective-permute-start.10 = (bf16[272,512]{1,0:T(8,128)(2,1)S(1)}, bf16[272,512]{1,0:T(8,128)(2,1)S(1)}, u32[]{:S(2)}, u32[]{:S(2)}) collective-permute-start(bf16[272,512]{1,0:T(8,128)(2,1)S(1)} %collective-permute-done.8), channel_id=1, source_target_pairs={{0,8},{8,16},{16,24},{24,28},{28,20},{20,12},{12,4},{4,0},{1,9},{9... | collective-permute-start | bytes 835592 | tf_op jit(solution)/shard_map/ppermute | solution.py:199
  90.6 7.6 %collective-permute-start.11 = (bf16[272,512]{1,0:T(8,128)(2,1)S(1)}, bf16[272,512]{1,0:T(8,128)(2,1)S(1)}, u32[]{:S(2)}, u32[]{:S(2)}) collective-permute-start(bf16[272,512]{1,0:T(8,128)(2,1)S(1)} %collective-permute-done.9), channel_id=1, source_target_pairs={{0,4},{8,0},{16,8},{24,16},{28,24},{20,28},{12,20},{4,12},{1,5},{9... | collective-permute-start | bytes 835592 | tf_op jit(solution)/shard_map/ppermute | solution.py:203
  96.6 6.5 %collective-permute-start.12 = (bf16[272,512]{1,0:T(8,128)(2,1)S(1)}, bf16[272,512]{1,0:T(8,128)(2,1)S(1)}, u32[]{:S(2)}, u32[]{:S(2)}) collective-permute-start(bf16[272,512]{1,0:T(8,128)(2,1)S(1)} %collective-permute-done.10), channel_id=1, source_target_pairs={{0,8},{8,16},{16,24},{24,28},{28,20},{20,12},{12,4},{4,0},{1,9},{9... | collective-permute-start | bytes 835592 | tf_op jit(solution)/shard_map/ppermute | solution.py:199
  98.2 6.0 %copy-start.3 = (bf16[272,512]{1,0:T(8,128)(2,1)}, bf16[272,512]{1,0:T(8,128)(2,1)S(1)}, u32[]{:S(2)}) copy-start(bf16[272,512]{1,0:T(8,128)(2,1)S(1)} %collective-permute-done.11) | copy-start | bytes 835588
  103.1 1.1 copy-start.5
  104.2 91.7 %all-gather.13.cloned.1.call-start = ((), (), s32[]{:S(2)}) async-start(), calls=%async_computation.3 | async-start | bytes 3932160 | tf_op jit(solution)/shard_map/all_gather | solution.py:138
  112.1 8.9 %copy-start.4 = (bf16[272,512]{1,0:T(8,128)(2,1)S(1)}, bf16[272,512]{1,0:T(8,128)(2,1)}, u32[]{:S(2)}) copy-start(bf16[272,512]{1,0:T(8,128)(2,1)} %copy-done.3) | copy-start | bytes 835588
  112.1 8.9 %copy-start.6 = (bf16[272,512]{1,0:T(8,128)(2,1)S(1)}, bf16[272,512]{1,0:T(8,128)(2,1)}, u32[]{:S(2)}) copy-start(bf16[272,512]{1,0:T(8,128)(2,1)} %copy-done.5) | copy-start | bytes 835588
  167.2 70.6 %all-gather.11.cloned.1.call-start = ((), (), s32[]{:S(2)}) async-start(), calls=%async_computation.2 | async-start | bytes 6553600 | tf_op jit(solution)/shard_map/all_gather | solution.py:138
  201.0 8.5 %collective-permute-start.16 = (bf16[256,512]{1,0:T(8,128)(2,1)S(1)}, bf16[256,512]{1,0:T(8,128)(2,1)S(1)}, u32[]{:S(2)}, u32[]{:S(2)}) collective-permute-start(bf16[256,512]{1,0:T(8,128)(2,1)S(1)} %get-tuple-element.56), channel_id=1, source_target_pairs={{0,4},{8,0},{16,8},{24,16},{28,24},{20,28},{12,20},{4,12},{1,5},{9... | collective-permute-start | bytes 786440 | tf_op jit(solution)/shard_map/ppermute | solution.py:223
  202.5 41.4 %collective-permute-start.13 = (bf16[256,512]{1,0:T(8,128)(2,1)}, bf16[256,512]{1,0:T(8,128)(2,1)S(1)}, u32[]{:S(2)}, u32[]{:S(2)}) collective-permute-start(bf16[256,512]{1,0:T(8,128)(2,1)} %get-tuple-element.55), channel_id=1, source_target_pairs={{0,8},{8,16},{16,24},{24,28},{28,20},{20,12},{12,4},{4,0},{1,9},{9... | collective-permute-start | bytes 786440 | tf_op jit(solution)/shard_map/ppermute | solution.py:223
  209.5 34.3 %collective-permute-start.17 = (bf16[256,512]{1,0:T(8,128)(2,1)S(1)}, bf16[256,512]{1,0:T(8,128)(2,1)S(1)}, u32[]{:S(2)}, u32[]{:S(2)}) collective-permute-start(bf16[256,512]{1,0:T(8,128)(2,1)S(1)} %add_convert_fusion.2), channel_id=1, source_target_pairs={{0,4},{8,0},{16,8},{24,16},{28,24},{20,28},{12,20},{4,12},{1,5},{9... | collective-permute-start | bytes 786440 | tf_op jit(solution)/shard_map/ppermute | solution.py:223
  244.0 17.8 %copy-start.12 = (f32[512]{0:T(512)S(1)}, f32[512]{0:T(512)}, u32[]{:S(2)}) copy-start(f32[512]{0:T(512)} %param.30) | copy-start | bytes 6148
  244.0 8.5 %collective-permute-start.14 = (bf16[256,512]{1,0:T(8,128)(2,1)S(1)}, bf16[256,512]{1,0:T(8,128)(2,1)S(1)}, u32[]{:S(2)}, u32[]{:S(2)}) collective-permute-start(bf16[256,512]{1,0:T(8,128)(2,1)S(1)} %get-tuple-element.53), channel_id=1, source_target_pairs={{0,8},{8,16},{16,24},{24,28},{28,20},{20,12},{12,4},{4,0},{1,9},{9... | collective-permute-start | bytes 786440 | tf_op jit(solution)/shard_map/ppermute | solution.py:223
  245.6 8.2 %collective-permute-start.18 = (bf16[256,512]{1,0:T(8,128)(2,1)S(1)}, bf16[256,512]{1,0:T(8,128)(2,1)S(1)}, u32[]{:S(2)}, u32[]{:S(2)}) collective-permute-start(bf16[256,512]{1,0:T(8,128)(2,1)S(1)} %get-tuple-element.54), channel_id=1, source_target_pairs={{0,4},{8,0},{16,8},{24,16},{28,24},{20,28},{12,20},{4,12},{1,5},{9... | collective-permute-start | bytes 786440 | tf_op jit(solution)/shard_map/ppermute | solution.py:223
  253.9 7.4 %collective-permute-start.19 = (bf16[256,512]{1,0:T(8,128)(2,1)S(1)}, bf16[256,512]{1,0:T(8,128)(2,1)S(1)}, u32[]{:S(2)}, u32[]{:S(2)}) collective-permute-start(bf16[256,512]{1,0:T(8,128)(2,1)S(1)} %get-tuple-element.52), channel_id=1, source_target_pairs={{0,4},{8,0},{16,8},{24,16},{28,24},{20,28},{12,20},{4,12},{1,5},{9... | collective-permute-start | bytes 786440 | tf_op jit(solution)/shard_map/ppermute | solution.py:223
  254.5 7.1 %collective-permute-start.15 = (bf16[256,512]{1,0:T(8,128)(2,1)S(1)}, bf16[256,512]{1,0:T(8,128)(2,1)S(1)}, u32[]{:S(2)}, u32[]{:S(2)}) collective-permute-start(bf16[256,512]{1,0:T(8,128)(2,1)S(1)} %get-tuple-element.51), channel_id=1, source_target_pairs={{0,8},{8,16},{16,24},{24,28},{28,20},{20,12},{12,4},{4,0},{1,9},{9... | collective-permute-start | bytes 786440 | tf_op jit(solution)/shard_map/ppermute | solution.py:223
  262.6 10.6 %collective-permute-start.22 = (bf16[256,512]{1,0:T(8,128)(2,1)S(1)}, bf16[256,512]{1,0:T(8,128)(2,1)S(1)}, u32[]{:S(2)}, u32[]{:S(2)}) collective-permute-start(bf16[256,512]{1,0:T(8,128)(2,1)S(1)} %get-tuple-element.57), channel_id=1, source_target_pairs={{0,3},{1,0},{2,1},{3,2},{4,7},{5,4},{6,5},{7,6},{8,11},{9,8},{10,9... | collective-permute-start | bytes 786440 | tf_op jit(solution)/shard_map/ppermute | solution.py:176
  262.6 8.6 %collective-permute-start.20 = (bf16[256,512]{1,0:T(8,128)(2,1)S(1)}, bf16[256,512]{1,0:T(8,128)(2,1)S(1)}, u32[]{:S(2)}, u32[]{:S(2)}) collective-permute-start(bf16[256,512]{1,0:T(8,128)(2,1)S(1)} %get-tuple-element.57), channel_id=1, source_target_pairs={{0,1},{1,2},{2,3},{3,0},{4,5},{5,6},{6,7},{7,4},{8,9},{9,10},{10,1... | collective-permute-start | bytes 786440 | tf_op jit(solution)/shard_map/ppermute | solution.py:176
  263.1 12.2 %collective-permute-start.21 = (bf16[256,512]{1,0:T(8,128)(2,1)S(1)}, bf16[256,512]{1,0:T(8,128)(2,1)S(1)}, u32[]{:S(2)}, u32[]{:S(2)}) collective-permute-start(bf16[256,512]{1,0:T(8,128)(2,1)S(1)} %get-tuple-element.57), channel_id=1, source_target_pairs={{0,2},{1,3},{2,0},{3,1},{4,6},{5,7},{6,4},{7,5},{8,10},{9,11},{10,... | collective-permute-start | bytes 786440 | tf_op jit(solution)/shard_map/ppermute | solution.py:176
  278.5 12.0 %copy-start.13 = (f32[512]{0:T(512)S(1)}, f32[512]{0:T(512)}, u32[]{:S(2)}) copy-start(f32[512]{0:T(512)} %param.33) | copy-start | bytes 6148
  278.5 12.0 %copy-start.14 = (f32[512]{0:T(512)S(1)}, f32[512]{0:T(512)}, u32[]{:S(2)}) copy-start(f32[512]{0:T(512)} %param.32) | copy-start | bytes 6148
  281.6 13.1 %copy-start.1 = (bf16[512,2048]{1,0:T(8,128)(2,1)S(1)}, bf16[512,2048]{1,0:T(8,128)(2,1)}, u32[]{:S(2)}) copy-start(bf16[512,2048]{1,0:T(8,128)(2,1)} %param.24) | copy-start | bytes 6291460
Sparse Core Ops, SparseCore 0:
  89.0 40.0 all-gather.6
  130.7 28.5 all-gather.8
  167.4 28.5 all-gather.12
  197.3 40.4 all-gather.10

commit v16 on v15

--- a/solution.py
+++ b/solution.py
@@ -116,8 +116,8 @@
     packed = jnp.concatenate([moe_in, info], axis=0)
     ring = ring_order(seq_count)
     offsets, blocks = ring_all_gather(packed, ring)
-    first = min(len(blocks), 5)
-    chunks = [(0, first), (first, len(blocks))] if first < len(blocks) else [(0, first)]
+    cuts = sorted({0, min(3, len(blocks)), min(6, len(blocks)), len(blocks)})
+    chunks = list(zip(cuts[:-1], cuts[1:]))
     outputs = []
     for begin, end in chunks:
         gathered = jnp.stack(blocks[begin:end])

time: 302 us -> 301 us (level)
  waiting for transfers between devices: 157 us -> 140 us
  Pallas kernels: 8.99 us -> 16.8 us
  matrix products: 35.6 us -> 40.2 us
    ppermute x3, waiting for transfers between devices: 14.2 us -> 4.34 us  [body(): pieces.append(lax.ppermute(piece, 'tp', pairs))]
    pallas_call x1, Pallas kernels: 8.99 us -> 16.8 us  [flash_attention(): pl.pallas_call(kernel, grid_spec=grid_spec, out_shape=jax.ShapeDtypeStruc...]
    ppermute x7, waiting for transfers between devices: 19.7 us -> 14.6 us  [ring_reduce_scatter(): lax.ppermute(acc.astype(jnp.bfloat16), 'seq', pairs).astype(jnp.float32)]
    ppermute x3, waiting for transfers between devices: 1.18 us -> 6.01 us  [ring_all_gather(): behind = lax.ppermute(behind, 'seq', backward)]
    ppermute x4, starting transfers between devices: 6.67 us -> 1.99 us  [ring_all_gather(): ahead = lax.ppermute(ahead, 'seq', forward)]
    ppermute x4, waiting for transfers between devices: 22 us -> 17.8 us  [ring_all_gather(): ahead = lax.ppermute(ahead, 'seq', forward)]
    ppermute x3, starting transfers between devices: 1.09 us -> 4.63 us  [ring_all_gather(): behind = lax.ppermute(behind, 'seq', backward)]
    ppermute x3, waiting for transfers between devices: 12.4 us -> 9.29 us  [permute_reduce_scatter(): total = total + lax.ppermute(piece, 'tp', pairs).astype(jnp.float32)]
  transfers between devices with their start and end apart: 27 -> 29, of which waited for: 19 -> 19; matrix products, arithmetic and copies ran while one was open for 16% -> 20% of each run, Pallas kernels for 3% -> 6%
where the time goes in v16:
time: 301 us
  waiting for transfers between devices  140 us (47%)
  matrix products  40.2 us (13%)
  local copies, waits for them, and re-layouts  36.1 us (12%)
  starting transfers between devices  23.9 us (8%)
  Pallas kernels  16.8 us (6%)
  between operations  14.6 us (5%)
  other arithmetic  14.4 us (5%)
  blocking collectives  14.2 us (5%)
    all_gather x3, waiting for transfers between devices, dense_experts(): weighted = lax.all_gather(weighted, 'tp', axis=0, tiled=False)  46.9 us
    all_gather x3, waiting for transfers between devices, dense_experts(): rows = lax.all_gather(rows_q, 'tp', axis=0, tiled=False)  35.5 us
    dot_general x3, matrix products, dense_experts(): jnp.einsum('qtd,eqdf->etf', rows, gate_up_split, preferred_element_type=j...  18.1 us
    ppermute x4, waiting for transfers between devices, ring_all_gather(): ahead = lax.ppermute(ahead, 'seq', forward)  17.8 us
    pallas_call x1, Pallas kernels, flash_attention(): pl.pallas_call(kernel, grid_spec=grid_spec, out_shape=jax.ShapeDtypeStruc...  16.8 us
    ppermute x7, waiting for transfers between devices, ring_reduce_scatter(): lax.ppermute(acc.astype(jnp.bfloat16), 'seq', pairs).astype(jnp.float32)  14.6 us
    unnamed x35, local copies, waits for them, and re-layouts  12.7 us
    dot_general x3, matrix products, dense_experts(): jnp.einsum('qetf,qefd->td', weighted, down_full, preferred_element_type=j...  12.1 us
  transfers between devices with their start and end apart: 29, of which 19 were waited for; matrix products, arithmetic and copies ran while one was open for 20% of the time, Pallas kernels for 6%

profile of v16, /device:TPU:0, one launch (start us, length us, event | category | flops | bytes accessed | tf_op | source)
XLA Modules:
  0.0 300.5 jit_solution(5900775489719124151)
XLA Ops:
  7.3 2.8 dynamic-slice_bitcast_fusion
  10.6 2.5 collective-permute-start.1
  15.2 16.8 %shard_map.192 = bf16[256,512]{1,0:T(8,128)(2,1)} custom-call(s32[1]{0:T(128)} %dynamic_slice.55.len_ref, bf16[256,512]{1,0:T(8,128)(2,1)} %q_ref.1, bf16[4096,512]{1,0:T(8,128)(2,1)} %bitcast.135, bf16[4096,512]{1,0:T(8,128)(2,1)} %bitcast.136, bf16[256,512]{1,0:T(8,128)(2,1)} %nk_ref.1, bf16[256,512]{1,0:T(8,128)(2,1)} %nv_ref.1), custom_call_target="tpu_custom_call" | custom-call | tf_op jit(solution)/shard_map/pallas_call | solution.py:94
  32.1 4.3 %collective-permute-done.2 = bf16[2,256,512]{2,1,0:T(8,128)(2,1)} collective-permute-done((bf16[2,256,512]{2,1,0:T(8,128)(2,1)}, bf16[2,256,512]{2,1,0:T(8,128)(2,1)}, u32[]{:S(2)}, u32[]{:S(2)}) %collective-permute-start.2) | collective-permute-done | bytes 524320 | tf_op jit(solution)/shard_map/ppermute | solution.py:306
  36.4 2.8 pad_maximum_fusion
  39.2 3.6 %gather_fusion = bf16[4,2,256,512]{3,2,1,0:T(8,128)(2,1)} fusion(bf16[4,2,256,512]{3,2,1,0:T(8,128)(2,1)} %pad_maximum_fusion, s32[1024]{0:T(1024)S(1)} %pad_clamp_fusion), kind=kCustom, calls=%fused_computation | custom fusion | bytes 4194320 | tf_op jit(solution)/shard_map/jit(_take)/gather | solution.py:308
  42.8 3.2 %broadcast_select_fusion = bf16[4,2,256,512]{3,2,1,0:T(8,128)(2,1)} fusion(bf16[4,2,256,512]{3,2,1,0:T(8,128)(2,1)} %gather_fusion, pred[4]{0:T(512)(128)(4,1)S(1)} %compare_and_fusion), kind=kLoop, calls=%fused_computation.17 | loop fusion | flops 1048576 | bytes 4194308 | tf_op jit(solution)/shard_map/jit(_take)/select_n | solution.py:308
  48.3 2.3 collective-permute-start.4
  50.6 5.8 %collective-permute-done.3 = bf16[256,512]{1,0:T(8,128)(2,1)S(1)} collective-permute-done((bf16[256,512]{1,0:T(8,128)(2,1)S(1)}, bf16[256,512]{1,0:T(8,128)(2,1)S(1)}, u32[]{:S(2)}, u32[]{:S(2)}) %collective-permute-start.3) | collective-permute-done | bytes 262176 | tf_op jit(solution)/shard_map/ppermute | solution.py:160
  57.7 2.2 collective-permute-done.5
  61.2 8.2 %psum.28 = f32[256]{0:T(256)S(1)} all-reduce(f32[256]{0:T(256)S(1)} %get-tuple-element.37), channel_id=1, replica_groups=mesh['seq'=8,'tp'=4] {'tp'}, use_global_device_ids=true, to_apply=%region_1.2 | all-reduce | flops 256 | bytes 2048 | tf_op jit(solution)/shard_map/psum | solution.py:336
  69.6 1.7 collective-permute-start.7
  71.7 6.0 %collective-permute-done.7 = bf16[272,512]{1,0:T(8,128)(2,1)S(1)} collective-permute-done((bf16[272,512]{1,0:T(8,128)(2,1)S(1)}, bf16[272,512]{1,0:T(8,128)(2,1)S(1)}, u32[]{:S(2)}, u32[]{:S(2)}) %collective-permute-start.7) | collective-permute-done | bytes 278560 | tf_op jit(solution)/shard_map/ppermute | solution.py:203
  80.6 1.5 collective-permute-start.8
  82.1 4.8 %collective-permute-done.10 = bf16[272,512]{1,0:T(8,128)(2,1)S(1)} collective-permute-done((bf16[272,512]{1,0:T(8,128)(2,1)S(1)}, bf16[272,512]{1,0:T(8,128)(2,1)S(1)}, u32[]{:S(2)}, u32[]{:S(2)}) %collective-permute-start.10) | collective-permute-done | bytes 278560 | tf_op jit(solution)/shard_map/ppermute | solution.py:199
  87.4 1.5 collective-permute-start.9
  88.9 5.7 %collective-permute-done.11 = bf16[272,512]{1,0:T(8,128)(2,1)S(1)} collective-permute-done((bf16[272,512]{1,0:T(8,128)(2,1)S(1)}, bf16[272,512]{1,0:T(8,128)(2,1)S(1)}, u32[]{:S(2)}, u32[]{:S(2)}) %collective-permute-start.11) | collective-permute-done | bytes 278560 | tf_op jit(solution)/shard_map/ppermute | solution.py:199
  95.1 6.1 %collective-permute-done.12 = bf16[272,512]{1,0:T(8,128)(2,1)S(1)} collective-permute-done((bf16[272,512]{1,0:T(8,128)(2,1)S(1)}, bf16[272,512]{1,0:T(8,128)(2,1)S(1)}, u32[]{:S(2)}, u32[]{:S(2)}) %collective-permute-start.12) | collective-permute-done | bytes 278560 | tf_op jit(solution)/shard_map/ppermute | solution.py:199
  103.5 8.8 %copy.105 = bf16[2048,3,512]{0,2,1:T(8,128)(2,1)} copy(bf16[2048,3,512]{2,0,1:T(8,128)(2,1)} %param.31) | data formatting | bytes 12582912 | tf_op args[14]
  112.3 7.7 %reshape.136 = bf16[2,2048,512]{2,1,0:T(8,128)(2,1)} reshape(bf16[2,2048,2,256]{3,2,1,0:T(2,128)(2,1)} %param.28) | data formatting | bytes 8388608 | tf_op jit(solution)/shard_map/reshape | solution.py:309
  120.1 12.1 %all-gather.12.cloned.1.call-done = bf16[4,512,512]{2,1,0:T(8,128)(2,1)} async-done(((bf16[1,512,512]{2,1,0:T(8,128)(2,1)}), bf16[4,512,512]{2,1,0:T(8,128)(2,1)}) %all-gather.12.cloned.1.call-update) | async-done | bytes 2097168 | tf_op jit(solution)/shard_map/all_gather | solution.py:130
  132.2 5.2 %fusion.19 = f32[2,512,512]{1,2,0:T(8,128)S(1)} fusion(bf16[2,4,512,512]{3,2,1,0:T(8,128)(2,1)} %bitcast.137, bf16[4,512,512]{2,1,0:T(8,128)(2,1)} %all-gather.12.cloned.1.call-done), kind=kOutput, calls=%fused_computation.20 | convolution fusion | flops 2147483648 | bytes 8388608 | tf_op jit(solution)/shard_map/qtd,eqdf->etf/dot_general | solution.py:134
  139.0 23.4 %all-gather.14.cloned.1.call-done = bf16[4,768,512]{2,1,0:T(8,128)(2,1)} async-done(((bf16[1,768,512]{2,1,0:T(8,128)(2,1)}), bf16[4,768,512]{2,1,0:T(8,128)(2,1)}) %all-gather.14.cloned.1.call-update) | async-done | bytes 3145744 | tf_op jit(solution)/shard_map/all_gather | solution.py:130
  162.4 6.2 %fusion.16 = f32[2,768,512]{1,2,0:T(8,128)S(1)} fusion(bf16[2,4,512,512]{3,2,1,0:T(8,128)(2,1)} %bitcast.138, bf16[4,768,512]{2,1,0:T(8,128)(2,1)} %all-gather.14.cloned.1.call-done), kind=kOutput, calls=%fused_computation.19 | convolution fusion | flops 3221225472 | bytes 10485760 | tf_op jit(solution)/shard_map/qtd,eqdf->etf/dot_general | solution.py:134
  170.4 6.6 %fusion.13 = f32[2,768,512]{1,2,0:T(8,128)S(1)} fusion(bf16[2,4,512,512]{3,2,1,0:T(8,128)(2,1)} %bitcast.139, bf16[4,768,512]{2,1,0:T(8,128)(2,1)} %all-gather.10.cloned.1.call-done), kind=kOutput, calls=%fused_computation.18 | convolution fusion | flops 3221225472 | bytes 10485760 | tf_op jit(solution)/shard_map/qtd,eqdf->etf/dot_general | solution.py:134
  178.7 7.6 %all-gather.18.cloned.1.call-done = bf16[8,512,256]{2,1,0:T(8,128)(2,1)} async-done(((bf16[2,512,256]{2,1,0:T(8,128)(2,1)}), bf16[8,512,256]{2,1,0:T(8,128)(2,1)}) %all-gather.18.cloned.1.call-update) | async-done | bytes 2097168 | tf_op jit(solution)/shard_map/all_gather | solution.py:138
  186.4 3.5 %fusion.46 = bf16[512,512]{1,0:T(8,128)(2,1)S(1)} fusion(bf16[4,2,256,512]{3,2,1,0:T(8,128)(2,1)} %broadcast_select_fusion, bf16[4,2,512,256]{3,2,1,0:T(8,128)(2,1)} %bitcast.163), kind=kOutput, calls=%fused_computation.39 | convolution fusion | flops 1074003968 | bytes 4718592 | tf_op jit(solution)/shard_map/qetf,qefd->td/dot_general | solution.py:139
  189.9 1.5 collective-permute-start.16
  192.0 24.4 %all-gather.20.cloned.1.call-done = bf16[8,768,256]{2,1,0:T(8,128)(2,1)} async-done(((bf16[2,768,256]{2,1,0:T(8,128)(2,1)}), bf16[8,768,256]{2,1,0:T(8,128)(2,1)}) %all-gather.20.cloned.1.call-update) | async-done | bytes 3145744 | tf_op jit(solution)/shard_map/all_gather | solution.py:138
  216.4 4.3 %bitcast_convert_fusion = bf16[768,512]{1,0:T(8,128)(2,1)S(1)} fusion(bf16[4,2,256,512]{3,2,1,0:T(8,128)(2,1)} %broadcast_select_fusion, bf16[4,2,768,256]{3,2,1,0:T(8,128)(2,1)} %bitcast.162), kind=kOutput, calls=%fused_computation.28 | convolution fusion | flops 1611005952 | bytes 6029312 | tf_op jit(solution)/shard_map/qetf,qefd->td/dot_general | solution.py:139
  220.8 1.5 collective-permute-start.17
  222.3 7.0 %collective-permute-done.17 = bf16[256,512]{1,0:T(8,128)(2,1)S(1)} collective-permute-done((bf16[256,512]{1,0:T(8,128)(2,1)S(1)}, bf16[256,512]{1,0:T(8,128)(2,1)S(1)}, u32[]{:S(2)}, u32[]{:S(2)}) %collective-permute-start.17) | collective-permute-done | bytes 262176 | tf_op jit(solution)/shard_map/ppermute | solution.py:223
  229.4 1.5 collective-permute-start.14
  231.5 14.9 %all-gather.16.cloned.1.call-done = bf16[8,768,256]{2,1,0:T(8,128)(2,1)} async-done(((bf16[2,768,256]{2,1,0:T(8,128)(2,1)}), bf16[8,768,256]{2,1,0:T(8,128)(2,1)}) %all-gather.16.cloned.1.call-update) | async-done | bytes 3145744 | tf_op jit(solution)/shard_map/all_gather | solution.py:138
  246.4 4.3 %bitcast_convert_fusion.1 = bf16[768,512]{1,0:T(8,128)(2,1)S(1)} fusion(bf16[4,2,256,512]{3,2,1,0:T(8,128)(2,1)} %broadcast_select_fusion, bf16[4,2,768,256]{3,2,1,0:T(8,128)(2,1)} %bitcast.161), kind=kOutput, calls=%fused_computation.29 | convolution fusion | flops 1611005952 | bytes 6029312 | tf_op jit(solution)/shard_map/qetf,qefd->td/dot_general | solution.py:139
  250.9 1.5 collective-permute-start.15
  252.9 6.4 %collective-permute-done.15 = bf16[256,512]{1,0:T(8,128)(2,1)S(1)} collective-permute-done((bf16[256,512]{1,0:T(8,128)(2,1)S(1)}, bf16[256,512]{1,0:T(8,128)(2,1)S(1)}, u32[]{:S(2)}, u32[]{:S(2)}) %collective-permute-start.15) | collective-permute-done | bytes 262176 | tf_op jit(solution)/shard_map/ppermute | solution.py:223
  261.6 1.7 collective-permute-start.22
  263.9 2.0 fusion.31
  265.9 3.5 %collective-permute-done.20 = bf16[256,512]{1,0:T(8,128)(2,1)S(1)} collective-permute-done((bf16[256,512]{1,0:T(8,128)(2,1)S(1)}, bf16[256,512]{1,0:T(8,128)(2,1)S(1)}, u32[]{:S(2)}, u32[]{:S(2)}) %collective-permute-start.20) | collective-permute-done | bytes 262176 | tf_op jit(solution)/shard_map/ppermute | solution.py:176
  269.3 2.0 convolution_add_fusion.1
  271.4 2.0 fusion.27
  273.4 2.4 collective-permute-done.21
  275.8 3.2 %fusion.8 = f32[256,1536]{1,0:T(8,128)} fusion(f32[256,1536]{1,0:T(8,128)S(1)} %fusion.27, f32[256,1536]{1,0:T(8,128)S(1)} %convolution_add_fusion.1, bf16[256,512]{1,0:T(8,128)(2,1)S(1)} %collective-permute-done.21, bf16[2048,1536]{0,1:T(8,128)(2,1)} %bitcast.132, s32[]{:T(128)S(6)} %select_n.122), kind=kOutput, calls=%fused_computation.10 | convolution fusion | flops 403439616 | bytes 6553604 | tf_op jit(solution)/shard_map/dot_general | solution.py:177
  279.0 3.1 %copy.125 = f32[256,1536]{0,1:T(8,128)} copy(f32[256,1536]{1,0:T(8,128)} %fusion.8) | data formatting | bytes 3145728 | tf_op jit(solution)/shard_map/add | solution.py:177
  282.1 1.5 multiply_reduce_fusion
  283.6 6.0 %all-reduce = (f32[256]{0:T(256)S(1)}, f32[256]{0:T(256)S(1)}, f32[256]{0:T(256)S(1)}) all-reduce(f32[256]{0:T(256)S(1)} %get-tuple-element.31, f32[256]{0:T(256)S(1)} %get-tuple-element.35, f32[256]{0:T(256)S(1)} %get-tuple-element.30), channel_id=1, replica_groups=mesh['seq'=8,'tp'=4] {'tp'}, use_global_device_ids=true, to_apply=%region_6.7 | all-reduce | flops 768 | bytes 6144 | tf_op jit(solution)/shard_map/psum | solution.py:362
  289.6 1.6 fusion.54
  (113 shorter events, 26.5 us)
Async XLA Ops:
  7.2 38.9 %copy-start = (bf16[512,2048]{1,0:T(8,128)(2,1)S(1)}, bf16[512,2048]{1,0:T(8,128)(2,1)}, u32[]{:S(2)}) copy-start(bf16[512,2048]{1,0:T(8,128)(2,1)} %param.24) | copy-start | bytes 6291460
  7.2 112.9 %all-gather.10.cloned.1.call-start = ((), (), s32[]{:S(2)}) async-start(), calls=%async_computation | async-start | bytes 3932160 | tf_op jit(solution)/shard_map/all_gather | solution.py:130
  7.3 7.3 %copy-start.13 = (s32[8]{0:T(128)S(1)}, s32[8]{0:T(128)}, u32[]{:S(2)}) copy-start(s32[8]{0:T(128)} %param.23) | copy-start | bytes 100
  10.1 21.9 %collective-permute-start = (bf16[2,256,512]{2,1,0:T(8,128)(2,1)}, bf16[2,256,512]{2,1,0:T(8,128)(2,1)S(1)}, u32[]{:S(2)}, u32[]{:S(2)}) collective-permute-start(bf16[2,256,512]{2,1,0:T(8,128)(2,1)} %get-tuple-element.45), channel_id=1, source_target_pairs={{0,1},{1,2},{2,3},{3,0},{4,5},{5,6},{6,7},{7,4},{8,9},{9,10},{10,1... | collective-permute-start | bytes 1572872 | tf_op jit(solution)/shard_map/ppermute | solution.py:306
  10.6 21.5 %collective-permute-start.1 = (bf16[2,256,512]{2,1,0:T(8,128)(2,1)}, bf16[2,256,512]{2,1,0:T(8,128)(2,1)}, u32[]{:S(2)}, u32[]{:S(2)}) collective-permute-start(bf16[2,256,512]{2,1,0:T(8,128)(2,1)} %get-tuple-element.47), channel_id=1, source_target_pairs={{0,2},{1,3},{2,0},{3,1},{4,6},{5,7},{6,4},{7,5},{8,10},{9,11},{10,... | collective-permute-start | bytes 1572872 | tf_op jit(solution)/shard_map/ppermute | solution.py:306
  13.1 23.3 %collective-permute-start.2 = (bf16[2,256,512]{2,1,0:T(8,128)(2,1)}, bf16[2,256,512]{2,1,0:T(8,128)(2,1)}, u32[]{:S(2)}, u32[]{:S(2)}) collective-permute-start(bf16[2,256,512]{2,1,0:T(8,128)(2,1)} %get-tuple-element.46), channel_id=1, source_target_pairs={{0,3},{1,0},{2,1},{3,2},{4,7},{5,4},{6,5},{7,6},{8,11},{9,8},{10,9... | collective-permute-start | bytes 1572872 | tf_op jit(solution)/shard_map/ppermute | solution.py:306
  15.2 16.8 %copy-start.7 = (f32[256,8]{0,1:T(8,128)S(1)}, f32[256,8]{0,1:T(8,128)}, u32[]{:S(2)}) copy-start(f32[256,8]{0,1:T(8,128)} %param.27) | copy-start | bytes 24580
  15.2 16.8 %copy-start.8 = (s32[256,8]{0,1:T(8,128)S(1)}, s32[256,8]{0,1:T(8,128)}, u32[]{:S(2)}) copy-start(s32[256,8]{0,1:T(8,128)} %param.26) | copy-start | bytes 24580
  42.8 3.2 %copy-start.5 = (bf16[256,512]{1,0:T(8,128)(2,1)S(1)}, bf16[256,512]{1,0:T(8,128)(2,1)}, u32[]{:S(2)}) copy-start(bf16[256,512]{1,0:T(8,128)(2,1)} %shard_map.192) | copy-start | bytes 786436
  46.0 13.9 %copy-start.6 = (bf16[256,512]{1,0:T(8,128)(2,1)S(1)}, bf16[256,512]{1,0:T(8,128)(2,1)}, u32[]{:S(2)}) copy-start(bf16[256,512]{1,0:T(8,128)(2,1)} %param.17) | copy-start | bytes 786436
  46.8 1.3 copy-start.2
  48.1 21.3 %copy-start.9 = (f32[512]{0:T(512)S(1)}, f32[512]{0:T(512)}, u32[]{:S(2)}) copy-start(f32[512]{0:T(512)} %param.25) | copy-start | bytes 6148
  48.2 8.2 %collective-permute-start.3 = (bf16[256,512]{1,0:T(8,128)(2,1)S(1)}, bf16[256,512]{1,0:T(8,128)(2,1)S(1)}, u32[]{:S(2)}, u32[]{:S(2)}) collective-permute-start(bf16[256,512]{1,0:T(8,128)(2,1)S(1)} %get-tuple-element.41), channel_id=1, source_target_pairs={{0,1},{1,2},{2,3},{3,0},{4,5},{5,6},{6,7},{7,4},{8,9},{9,10},{10,1... | collective-permute-start | bytes 786440 | tf_op jit(solution)/shard_map/ppermute | solution.py:160
  48.3 9.4 %collective-permute-start.4 = (bf16[256,512]{1,0:T(8,128)(2,1)S(1)}, bf16[256,512]{1,0:T(8,128)(2,1)S(1)}, u32[]{:S(2)}, u32[]{:S(2)}) collective-permute-start(bf16[256,512]{1,0:T(8,128)(2,1)S(1)} %get-tuple-element.43), channel_id=1, source_target_pairs={{0,2},{1,3},{2,0},{3,1},{4,6},{5,7},{6,4},{7,5},{8,10},{9,11},{10,... | collective-permute-start | bytes 786440 | tf_op jit(solution)/shard_map/ppermute | solution.py:160
  50.6 9.3 %collective-permute-start.5 = (bf16[256,512]{1,0:T(8,128)(2,1)S(1)}, bf16[256,512]{1,0:T(8,128)(2,1)S(1)}, u32[]{:S(2)}, u32[]{:S(2)}) collective-permute-start(bf16[256,512]{1,0:T(8,128)(2,1)S(1)} %get-tuple-element.42), channel_id=1, source_target_pairs={{0,3},{1,0},{2,1},{3,2},{4,7},{5,4},{6,5},{7,6},{8,11},{9,8},{10,9... | collective-permute-start | bytes 786440 | tf_op jit(solution)/shard_map/ppermute | solution.py:160
  69.6 8.1 %collective-permute-start.7 = (bf16[272,512]{1,0:T(8,128)(2,1)S(1)}, bf16[272,512]{1,0:T(8,128)(2,1)S(1)}, u32[]{:S(2)}, u32[]{:S(2)}) collective-permute-start(bf16[272,512]{1,0:T(8,128)(2,1)S(1)} %get-tuple-element.60), channel_id=1, source_target_pairs={{0,4},{8,0},{16,8},{24,16},{28,24},{20,28},{12,20},{4,12},{1,5},{9... | collective-permute-start | bytes 835592 | tf_op jit(solution)/shard_map/ppermute | solution.py:203
  71.3 7.6 %collective-permute-start.6 = (bf16[272,512]{1,0:T(8,128)(2,1)S(1)}, bf16[272,512]{1,0:T(8,128)(2,1)S(1)}, u32[]{:S(2)}, u32[]{:S(2)}) collective-permute-start(bf16[272,512]{1,0:T(8,128)(2,1)S(1)} %get-tuple-element.60), channel_id=1, source_target_pairs={{0,8},{8,16},{16,24},{24,28},{28,20},{20,12},{12,4},{4,0},{1,9},{9... | collective-permute-start | bytes 835592 | tf_op jit(solution)/shard_map/ppermute | solution.py:199
  80.0 52.2 %all-gather.12.cloned.1.call-start = ((), (), s32[]{:S(2)}) async-start(), calls=%async_computation.1 | async-start | bytes 2621440 | tf_op jit(solution)/shard_map/all_gather | solution.py:130
  80.0 6.9 %collective-permute-start.10 = (bf16[272,512]{1,0:T(8,128)(2,1)S(1)}, bf16[272,512]{1,0:T(8,128)(2,1)S(1)}, u32[]{:S(2)}, u32[]{:S(2)}) collective-permute-start(bf16[272,512]{1,0:T(8,128)(2,1)S(1)} %collective-permute-done.6), channel_id=1, source_target_pairs={{0,8},{8,16},{16,24},{24,28},{28,20},{20,12},{12,4},{4,0},{1,9},{9... | collective-permute-start | bytes 835592 | tf_op jit(solution)/shard_map/ppermute | solution.py:199
  80.6 6.8 %collective-permute-start.8 = (bf16[272,512]{1,0:T(8,128)(2,1)S(1)}, bf16[272,512]{1,0:T(8,128)(2,1)S(1)}, u32[]{:S(2)}, u32[]{:S(2)}) collective-permute-start(bf16[272,512]{1,0:T(8,128)(2,1)S(1)} %collective-permute-done.7), channel_id=1, source_target_pairs={{0,4},{8,0},{16,8},{24,16},{28,24},{20,28},{12,20},{4,12},{1,5},{9... | collective-permute-start | bytes 835592 | tf_op jit(solution)/shard_map/ppermute | solution.py:203
  86.9 7.7 %collective-permute-start.11 = (bf16[272,512]{1,0:T(8,128)(2,1)S(1)}, bf16[272,512]{1,0:T(8,128)(2,1)S(1)}, u32[]{:S(2)}, u32[]{:S(2)}) collective-permute-start(bf16[272,512]{1,0:T(8,128)(2,1)S(1)} %collective-permute-done.10), channel_id=1, source_target_pairs={{0,8},{8,16},{16,24},{24,28},{28,20},{20,12},{12,4},{4,0},{1,9},{9... | collective-permute-start | bytes 835592 | tf_op jit(solution)/shard_map/ppermute | solution.py:199
  87.4 7.6 %collective-permute-start.9 = (bf16[272,512]{1,0:T(8,128)(2,1)S(1)}, bf16[272,512]{1,0:T(8,128)(2,1)S(1)}, u32[]{:S(2)}, u32[]{:S(2)}) collective-permute-start(bf16[272,512]{1,0:T(8,128)(2,1)S(1)} %collective-permute-done.8), channel_id=1, source_target_pairs={{0,4},{8,0},{16,8},{24,16},{28,24},{20,28},{12,20},{4,12},{1,5},{9... | collective-permute-start | bytes 835592 | tf_op jit(solution)/shard_map/ppermute | solution.py:203
  94.6 6.5 %collective-permute-start.12 = (bf16[272,512]{1,0:T(8,128)(2,1)S(1)}, bf16[272,512]{1,0:T(8,128)(2,1)S(1)}, u32[]{:S(2)}, u32[]{:S(2)}) collective-permute-start(bf16[272,512]{1,0:T(8,128)(2,1)S(1)} %collective-permute-done.11), channel_id=1, source_target_pairs={{0,8},{8,16},{16,24},{24,28},{28,20},{20,12},{12,4},{4,0},{1,9},{9... | collective-permute-start | bytes 835592 | tf_op jit(solution)/shard_map/ppermute | solution.py:199
  101.2 1.0 copy-start.3
  102.1 60.2 %all-gather.14.cloned.1.call-start = ((), (), s32[]{:S(2)}) async-start(), calls=%async_computation.2 | async-start | bytes 3932160 | tf_op jit(solution)/shard_map/all_gather | solution.py:130
  103.3 83.1 %all-gather.18.cloned.1.call-start = ((), (), s32[]{:S(2)}) async-start(), calls=%async_computation.4 | async-start | bytes 2621440 | tf_op jit(solution)/shard_map/all_gather | solution.py:138
  112.3 7.7 %copy-start.4 = (bf16[272,512]{1,0:T(8,128)(2,1)S(1)}, bf16[272,512]{1,0:T(8,128)(2,1)}, u32[]{:S(2)}) copy-start(bf16[272,512]{1,0:T(8,128)(2,1)} %copy-done.3) | copy-start | bytes 835588
  138.8 77.5 %all-gather.20.cloned.1.call-start = ((), (), s32[]{:S(2)}) async-start(), calls=%async_computation.5 | async-start | bytes 3932160 | tf_op jit(solution)/shard_map/all_gather | solution.py:138
  170.3 76.1 %all-gather.16.cloned.1.call-start = ((), (), s32[]{:S(2)}) async-start(), calls=%async_computation.3 | async-start | bytes 3932160 | tf_op jit(solution)/shard_map/all_gather | solution.py:138
  189.9 30.8 %collective-permute-start.16 = (bf16[256,512]{1,0:T(8,128)(2,1)S(1)}, bf16[256,512]{1,0:T(8,128)(2,1)S(1)}, u32[]{:S(2)}, u32[]{:S(2)}) collective-permute-start(bf16[256,512]{1,0:T(8,128)(2,1)S(1)} %get-tuple-element.58), channel_id=1, source_target_pairs={{0,4},{8,0},{16,8},{24,16},{28,24},{20,28},{12,20},{4,12},{1,5},{9... | collective-permute-start | bytes 786440 | tf_op jit(solution)/shard_map/ppermute | solution.py:223
  191.4 30.9 %collective-permute-start.13 = (bf16[256,512]{1,0:T(8,128)(2,1)S(1)}, bf16[256,512]{1,0:T(8,128)(2,1)S(1)}, u32[]{:S(2)}, u32[]{:S(2)}) collective-permute-start(bf16[256,512]{1,0:T(8,128)(2,1)S(1)} %get-tuple-element.57), channel_id=1, source_target_pairs={{0,8},{8,16},{16,24},{24,28},{28,20},{20,12},{12,4},{4,0},{1,9},{9... | collective-permute-start | bytes 786440 | tf_op jit(solution)/shard_map/ppermute | solution.py:223
  220.8 8.5 %collective-permute-start.17 = (bf16[256,512]{1,0:T(8,128)(2,1)S(1)}, bf16[256,512]{1,0:T(8,128)(2,1)S(1)}, u32[]{:S(2)}, u32[]{:S(2)}) collective-permute-start(bf16[256,512]{1,0:T(8,128)(2,1)S(1)} %add_convert_fusion.2), channel_id=1, source_target_pairs={{0,4},{8,0},{16,8},{24,16},{28,24},{20,28},{12,20},{4,12},{1,5},{9... | collective-permute-start | bytes 786440 | tf_op jit(solution)/shard_map/ppermute | solution.py:223
  229.4 21.3 %collective-permute-start.14 = (bf16[256,512]{1,0:T(8,128)(2,1)S(1)}, bf16[256,512]{1,0:T(8,128)(2,1)S(1)}, u32[]{:S(2)}, u32[]{:S(2)}) collective-permute-start(bf16[256,512]{1,0:T(8,128)(2,1)S(1)} %get-tuple-element.53), channel_id=1, source_target_pairs={{0,8},{8,16},{16,24},{24,28},{28,20},{20,12},{12,4},{4,0},{1,9},{9... | collective-permute-start | bytes 786440 | tf_op jit(solution)/shard_map/ppermute | solution.py:223
  231.0 19.7 %collective-permute-start.18 = (bf16[256,512]{1,0:T(8,128)(2,1)S(1)}, bf16[256,512]{1,0:T(8,128)(2,1)S(1)}, u32[]{:S(2)}, u32[]{:S(2)}) collective-permute-start(bf16[256,512]{1,0:T(8,128)(2,1)S(1)} %get-tuple-element.54), channel_id=1, source_target_pairs={{0,4},{8,0},{16,8},{24,16},{28,24},{20,28},{12,20},{4,12},{1,5},{9... | collective-permute-start | bytes 786440 | tf_op jit(solution)/shard_map/ppermute | solution.py:223
  250.7 10.1 %copy-start.10 = (f32[512]{0:T(512)S(1)}, f32[512]{0:T(512)}, u32[]{:S(2)}) copy-start(f32[512]{0:T(512)} %param.30) | copy-start | bytes 6148
  250.9 8.5 %collective-permute-start.15 = (bf16[256,512]{1,0:T(8,128)(2,1)S(1)}, bf16[256,512]{1,0:T(8,128)(2,1)S(1)}, u32[]{:S(2)}, u32[]{:S(2)}) collective-permute-start(bf16[256,512]{1,0:T(8,128)(2,1)S(1)} %get-tuple-element.51), channel_id=1, source_target_pairs={{0,8},{8,16},{16,24},{24,28},{28,20},{20,12},{12,4},{4,0},{1,9},{9... | collective-permute-start | bytes 786440 | tf_op jit(solution)/shard_map/ppermute | solution.py:223
  252.4 8.2 %collective-permute-start.19 = (bf16[256,512]{1,0:T(8,128)(2,1)S(1)}, bf16[256,512]{1,0:T(8,128)(2,1)S(1)}, u32[]{:S(2)}, u32[]{:S(2)}) collective-permute-start(bf16[256,512]{1,0:T(8,128)(2,1)S(1)} %get-tuple-element.52), channel_id=1, source_target_pairs={{0,4},{8,0},{16,8},{24,16},{28,24},{20,28},{12,20},{4,12},{1,5},{9... | collective-permute-start | bytes 786440 | tf_op jit(solution)/shard_map/ppermute | solution.py:223
  261.6 7.8 %collective-permute-start.20 = (bf16[256,512]{1,0:T(8,128)(2,1)S(1)}, bf16[256,512]{1,0:T(8,128)(2,1)S(1)}, u32[]{:S(2)}, u32[]{:S(2)}) collective-permute-start(bf16[256,512]{1,0:T(8,128)(2,1)S(1)} %get-tuple-element.55), channel_id=1, source_target_pairs={{0,1},{1,2},{2,3},{3,0},{4,5},{5,6},{6,7},{7,4},{8,9},{9,10},{10,1... | collective-permute-start | bytes 786440 | tf_op jit(solution)/shard_map/ppermute | solution.py:176
  261.6 9.8 %collective-permute-start.22 = (bf16[256,512]{1,0:T(8,128)(2,1)S(1)}, bf16[256,512]{1,0:T(8,128)(2,1)S(1)}, u32[]{:S(2)}, u32[]{:S(2)}) collective-permute-start(bf16[256,512]{1,0:T(8,128)(2,1)S(1)} %get-tuple-element.55), channel_id=1, source_target_pairs={{0,3},{1,0},{2,1},{3,2},{4,7},{5,4},{6,5},{7,6},{8,11},{9,8},{10,9... | collective-permute-start | bytes 786440 | tf_op jit(solution)/shard_map/ppermute | solution.py:176
  263.3 12.5 %collective-permute-start.21 = (bf16[256,512]{1,0:T(8,128)(2,1)S(1)}, bf16[256,512]{1,0:T(8,128)(2,1)S(1)}, u32[]{:S(2)}, u32[]{:S(2)}) collective-permute-start(bf16[256,512]{1,0:T(8,128)(2,1)S(1)} %get-tuple-element.55), channel_id=1, source_target_pairs={{0,2},{1,3},{2,0},{3,1},{4,6},{5,7},{6,4},{7,5},{8,10},{9,11},{10,... | collective-permute-start | bytes 786440 | tf_op jit(solution)/shard_map/ppermute | solution.py:176
  279.0 10.5 %copy-start.11 = (f32[512]{0:T(512)S(1)}, f32[512]{0:T(512)}, u32[]{:S(2)}) copy-start(f32[512]{0:T(512)} %param.33) | copy-start | bytes 6148
  279.0 10.5 %copy-start.12 = (f32[512]{0:T(512)S(1)}, f32[512]{0:T(512)}, u32[]{:S(2)}) copy-start(f32[512]{0:T(512)} %param.32) | copy-start | bytes 6148
  282.1 11.6 %copy-start.1 = (bf16[512,2048]{1,0:T(8,128)(2,1)S(1)}, bf16[512,2048]{1,0:T(8,128)(2,1)}, u32[]{:S(2)}) copy-start(bf16[512,2048]{1,0:T(8,128)(2,1)} %param.24) | copy-start | bytes 6291460
Sparse Core Ops, SparseCore 0:
  80.1 27.8 all-gather.9
  109.6 22.5 all-gather.11
  133.8 28.5 all-gather.13
  163.8 22.5 all-gather.17
  187.8 28.5 all-gather.19
  217.8 28.5 all-gather.15

commit v17 on v16

--- a/solution.py
+++ b/solution.py
@@ -135,7 +135,7 @@
         activated = jax.nn.silu(projected[..., :hidden_quarter]) * projected[..., hidden_quarter:]
         activated = activated.astype(jnp.bfloat16).astype(jnp.float32)
         weighted = (activated * gate_local[:, :, None]).astype(jnp.bfloat16)
-        weighted = lax.all_gather(weighted, "tp", axis=0, tiled=False)
+        weighted = pair_gather(weighted)
         partial = jnp.einsum(
             "qetf,qefd->td", weighted, down_full, preferred_element_type=jnp.float32
         ).astype(jnp.bfloat16)
@@ -180,6 +180,14 @@
             preferred_element_type=jnp.float32,
         )
     return total
+
+
+def pair_gather(block):
+    if lax.axis_size("tp") != 4:
+        return lax.all_gather(block, "tp", axis=0, tiled=False)
+    far = lax.ppermute(block, "tp", [(i, i ^ 2) for i in range(4)])
+    near = lax.ppermute(jnp.stack([block, far]), "tp", [(i, i ^ 1) for i in range(4)])
+    return jnp.stack([block, near[0], far, near[1]])
 
 
 def ring_order(count):
@@ -304,7 +312,10 @@
             piece = lax.dynamic_slice_in_dim(expert_down, target * quarter_width, quarter_width, axis=2)
             pairs = [(i, (i + shift) % tp_count) for i in range(tp_count)]
             pieces.append(lax.ppermute(piece, "tp", pairs))
-        order = (tp_here - jnp.arange(tp_count, dtype=jnp.int32)) % tp_count
+        if tp_count == 4:
+            order = (tp_here - (tp_here ^ jnp.arange(tp_count, dtype=jnp.int32))) % tp_count
+        else:
+            order = (tp_here - jnp.arange(tp_count, dtype=jnp.int32)) % tp_count
         down_full = jnp.take(jnp.stack(pieces), order, axis=0)
         gate_up_flat = expert_gate_up.reshape(local_experts, D, -1)
         qkv_flat = qkv_proj.reshape(D, -1)

time: 301 us -> 290 us (0.963)
  Pallas kernels: 16.8 us -> 9 us
  matrix products: 40.2 us -> 33 us
  other arithmetic: 14.4 us -> 18 us
    all_gather x3 -> x0, waiting for transfers between devices: 46.9 us -> none  [dense_experts(): weighted = lax.all_gather(weighted, 'tp', axis=0, tiled=False)]
    ppermute x0 -> x6, waiting for transfers between devices: none -> 31.5 us  [the longest x3 31.5 us: pair_gather(): far = lax.ppermute(block, 'tp', [(i, i ^ 2) for i in range(4)])]
    ppermute x3, waiting for transfers between devices: 4.34 us -> 12.1 us  [body(): pieces.append(lax.ppermute(piece, 'tp', pairs))]
    pallas_call x1, Pallas kernels: 16.8 us -> 9 us  [flash_attention(): pl.pallas_call(kernel, grid_spec=grid_spec, out_shape=jax.ShapeDtypeStruc...]
    dot_general x3, matrix products: 12.1 us -> 5.94 us  [dense_experts(): jnp.einsum('qetf,qefd->td', weighted, down_full, preferred_element_type=j...]
    ppermute x7, waiting for transfers between devices: 14.6 us -> 18.6 us  [ring_reduce_scatter(): lax.ppermute(acc.astype(jnp.bfloat16), 'seq', pairs).astype(jnp.float32)]
    convert_element_type x3 -> x0, local copies, waits for them, and re-layouts: 3.35 us -> none  [dense_experts(): weighted = (activated * gate_local[:, :, None]).astype(jnp.bfloat16)]
    unnamed x35 -> x43, local copies, waits for them, and re-layouts: 12.7 us -> 15.5 us
  transfers between devices with their start and end apart: 29 -> 32, of which waited for: 19 -> 23; matrix products, arithmetic and copies ran while one was open for 20% -> 19% of each run, Pallas kernels for 6% -> 3%
where the time goes in v17:
time: 290 us; the launch traced here: 289 us
  waiting for transfers between devices  139 us (48%)
  local copies, waits for them, and re-layouts  35.7 us (12%)
  matrix products  33 us (11%)
  starting transfers between devices  26.4 us (9%)
  other arithmetic  18 us (6%)
  between operations  14.3 us (5%)
  blocking collectives  14.2 us (5%)
  Pallas kernels  9 us (3%)
    all_gather x3, waiting for transfers between devices, dense_experts(): rows = lax.all_gather(rows_q, 'tp', axis=0, tiled=False)  37.4 us
    ppermute x3, waiting for transfers between devices, pair_gather(): far = lax.ppermute(block, 'tp', [(i, i ^ 2) for i in range(4)])  31.5 us
    ppermute x7, waiting for transfers between devices, ring_reduce_scatter(): lax.ppermute(acc.astype(jnp.bfloat16), 'seq', pairs).astype(jnp.float32)  18.6 us
    ppermute x4, waiting for transfers between devices, ring_all_gather(): ahead = lax.ppermute(ahead, 'seq', forward)  17.8 us
    dot_general x3, matrix products, dense_experts(): jnp.einsum('qtd,eqdf->etf', rows, gate_up_split, preferred_element_type=j...  17 us
    unnamed x43, local copies, waits for them, and re-layouts  15.5 us
    ppermute x3, waiting for transfers between devices, body(): pieces.append(lax.ppermute(piece, 'tp', pairs))  12.1 us
    ppermute x3, waiting for transfers between devices, permute_reduce_scatter(): total = total + lax.ppermute(piece, 'tp', pairs).astype(jnp.float32)  9.29 us
  transfers between devices with their start and end apart: 32, of which 23 were waited for; matrix products, arithmetic and copies ran while one was open for 19% of the time, Pallas kernels for 3%

profile of v17, /device:TPU:0, one launch (start us, length us, event | category | flops | bytes accessed | tf_op | source)
XLA Modules:
  0.0 289.3 jit_solution(16819920312402058034)
XLA Ops:
  7.3 2.8 dynamic-slice_bitcast_fusion
  10.6 2.5 collective-permute-start.1
  15.2 9.0 %shard_map.192 = bf16[256,512]{1,0:T(8,128)(2,1)} custom-call(s32[1]{0:T(128)} %dynamic_slice.55.len_ref, bf16[256,512]{1,0:T(8,128)(2,1)} %q_ref.1, bf16[4096,512]{1,0:T(8,128)(2,1)} %bitcast.141, bf16[4096,512]{1,0:T(8,128)(2,1)} %bitcast.142, bf16[256,512]{1,0:T(8,128)(2,1)} %nk_ref.1, bf16[256,512]{1,0:T(8,128)(2,1)} %nv_ref.1), custom_call_target="tpu_custom_call" | custom-call | tf_op jit(solution)/shard_map/pallas_call | solution.py:94
  24.4 1.8 collective-permute-done.1
  26.2 10.2 %collective-permute-done.2 = bf16[2,256,512]{2,1,0:T(8,128)(2,1)} collective-permute-done((bf16[2,256,512]{2,1,0:T(8,128)(2,1)}, bf16[2,256,512]{2,1,0:T(8,128)(2,1)}, u32[]{:S(2)}, u32[]{:S(2)}) %collective-permute-start.2) | collective-permute-done | bytes 524320 | tf_op jit(solution)/shard_map/ppermute | solution.py:314
  36.4 2.8 pad_maximum_fusion.2
  39.2 3.6 %gather_fusion = bf16[4,2,256,512]{3,2,1,0:T(8,128)(2,1)} fusion(bf16[4,2,256,512]{3,2,1,0:T(8,128)(2,1)} %pad_maximum_fusion.2, s32[1024]{0:T(1024)S(1)} %pad_clamp_fusion), kind=kCustom, calls=%fused_computation | custom fusion | bytes 4194320 | tf_op jit(solution)/shard_map/jit(_take)/gather | solution.py:319
  42.8 3.2 %broadcast_select_fusion = bf16[4,2,256,512]{3,2,1,0:T(8,128)(2,1)} fusion(bf16[4,2,256,512]{3,2,1,0:T(8,128)(2,1)} %gather_fusion, pred[4]{0:T(512)(128)(4,1)S(1)} %compare_and_fusion), kind=kLoop, calls=%fused_computation.20 | loop fusion | flops 1048576 | bytes 4194308 | tf_op jit(solution)/shard_map/jit(_take)/select_n | solution.py:319
  48.3 2.3 collective-permute-start.4
  50.6 5.8 %collective-permute-done.3 = bf16[256,512]{1,0:T(8,128)(2,1)S(1)} collective-permute-done((bf16[256,512]{1,0:T(8,128)(2,1)S(1)}, bf16[256,512]{1,0:T(8,128)(2,1)S(1)}, u32[]{:S(2)}, u32[]{:S(2)}) %collective-permute-start.3) | collective-permute-done | bytes 262176 | tf_op jit(solution)/shard_map/ppermute | solution.py:160
  57.7 2.2 collective-permute-done.5
  61.2 8.2 %psum.28 = f32[256]{0:T(256)S(1)} all-reduce(f32[256]{0:T(256)S(1)} %get-tuple-element.33), channel_id=1, replica_groups=mesh['seq'=8,'tp'=4] {'tp'}, use_global_device_ids=true, to_apply=%region_1.2 | all-reduce | flops 256 | bytes 2048 | tf_op jit(solution)/shard_map/psum | solution.py:347
  69.6 1.7 collective-permute-start.7
  71.7 6.0 %collective-permute-done.7 = bf16[272,512]{1,0:T(8,128)(2,1)S(1)} collective-permute-done((bf16[272,512]{1,0:T(8,128)(2,1)S(1)}, bf16[272,512]{1,0:T(8,128)(2,1)S(1)}, u32[]{:S(2)}, u32[]{:S(2)}) %collective-permute-start.7) | collective-permute-done | bytes 278560 | tf_op jit(solution)/shard_map/ppermute | solution.py:211
  82.1 4.8 %collective-permute-done.12 = bf16[272,512]{1,0:T(8,128)(2,1)S(1)} collective-permute-done((bf16[272,512]{1,0:T(8,128)(2,1)S(1)}, bf16[272,512]{1,0:T(8,128)(2,1)S(1)}, u32[]{:S(2)}, u32[]{:S(2)}) %collective-permute-start.12) | collective-permute-done | bytes 278560 | tf_op jit(solution)/shard_map/ppermute | solution.py:207
  89.0 5.7 %collective-permute-done.13 = bf16[272,512]{1,0:T(8,128)(2,1)S(1)} collective-permute-done((bf16[272,512]{1,0:T(8,128)(2,1)S(1)}, bf16[272,512]{1,0:T(8,128)(2,1)S(1)}, u32[]{:S(2)}, u32[]{:S(2)}) %collective-permute-start.13) | collective-permute-done | bytes 278560 | tf_op jit(solution)/shard_map/ppermute | solution.py:207
  95.1 6.1 %collective-permute-done.14 = bf16[272,512]{1,0:T(8,128)(2,1)S(1)} collective-permute-done((bf16[272,512]{1,0:T(8,128)(2,1)S(1)}, bf16[272,512]{1,0:T(8,128)(2,1)S(1)}, u32[]{:S(2)}, u32[]{:S(2)}) %collective-permute-start.14) | collective-permute-done | bytes 278560 | tf_op jit(solution)/shard_map/ppermute | solution.py:207
  103.5 8.8 %copy.79 = bf16[2048,3,512]{0,2,1:T(8,128)(2,1)} copy(bf16[2048,3,512]{2,0,1:T(8,128)(2,1)} %param.31) | data formatting | bytes 12582912 | tf_op args[14]
  112.3 7.7 %reshape.139 = bf16[2,2048,512]{2,1,0:T(8,128)(2,1)} reshape(bf16[2,2048,2,256]{3,2,1,0:T(2,128)(2,1)} %param.28) | data formatting | bytes 8388608 | tf_op jit(solution)/shard_map/reshape | solution.py:320
  121.0 11.2 %all-gather.6.cloned.1.call-done = bf16[4,512,512]{2,1,0:T(8,128)(2,1)} async-done(((bf16[1,512,512]{2,1,0:T(8,128)(2,1)}), bf16[4,512,512]{2,1,0:T(8,128)(2,1)}) %all-gather.6.cloned.1.call-update) | async-done | bytes 2097168 | tf_op jit(solution)/shard_map/all_gather | solution.py:130
  132.3 5.4 %fusion.19 = f32[2,512,512]{1,2,0:T(8,128)S(1)} fusion(bf16[2,4,512,512]{3,2,1,0:T(8,128)(2,1)} %bitcast.143, bf16[4,512,512]{2,1,0:T(8,128)(2,1)} %all-gather.6.cloned.1.call-done), kind=kOutput, calls=%fused_computation.23 | convolution fusion | flops 2147483648 | bytes 8388608 | tf_op jit(solution)/shard_map/qtd,eqdf->etf/dot_general | solution.py:134
  140.1 5.2 %fusion.13 = f32[2,768,512]{1,2,0:T(8,128)} fusion(bf16[2,4,512,512]{3,2,1,0:T(8,128)(2,1)S(1)} %bitcast.145, bf16[4,768,512]{2,1,0:T(8,128)(2,1)S(1)} %copy-done.16), kind=kOutput, calls=%fused_computation.21 | convolution fusion | flops 3221225472 | bytes 10485760 | tf_op jit(solution)/shard_map/qtd,eqdf->etf/dot_general | solution.py:134
  145.3 26.2 %all-gather.8.cloned.1.call-done = bf16[4,768,512]{2,1,0:T(8,128)(2,1)} async-done(((bf16[1,768,512]{2,1,0:T(8,128)(2,1)}), bf16[4,768,512]{2,1,0:T(8,128)(2,1)}) %all-gather.8.cloned.1.call-update) | async-done | bytes 3145744 | tf_op jit(solution)/shard_map/all_gather | solution.py:130
  171.5 6.4 %fusion.16 = f32[2,768,512]{1,2,0:T(8,128)S(1)} fusion(bf16[2,4,512,512]{3,2,1,0:T(8,128)(2,1)} %bitcast.144, bf16[4,768,512]{2,1,0:T(8,128)(2,1)} %all-gather.8.cloned.1.call-done), kind=kOutput, calls=%fused_computation.22 | convolution fusion | flops 3221225472 | bytes 10485760 | tf_op jit(solution)/shard_map/qtd,eqdf->etf/dot_general | solution.py:134
  180.8 1.5 collective-permute-start.8
  182.8 16.0 %collective-permute-done.18 = bf16[2,768,256]{1,2,0:T(8,128)(2,1)S(1)} collective-permute-done((bf16[2,768,256]{1,2,0:T(8,128)(2,1)S(1)}, bf16[2,768,256]{1,2,0:T(8,128)(2,1)S(1)}, u32[]{:S(2)}, u32[]{:S(2)}) %collective-permute-start.18) | collective-permute-done | bytes 786464 | tf_op jit(solution)/shard_map/ppermute | solution.py:188
  199.6 15.4 %collective-permute-done.8 = bf16[2,768,256]{1,2,0:T(8,128)(2,1)S(1)} collective-permute-done((bf16[2,768,256]{1,2,0:T(8,128)(2,1)S(1)}, bf16[2,768,256]{1,2,0:T(8,128)(2,1)S(1)}, u32[]{:S(2)}, u32[]{:S(2)}) %collective-permute-start.8) | collective-permute-done | bytes 786464 | tf_op jit(solution)/shard_map/ppermute | solution.py:188
  216.6 2.3 fusion.46
  219.0 1.5 collective-permute-start.22
  221.2 1.8 bitcast_convert_fusion
  223.0 3.7 %collective-permute-done.22 = bf16[256,512]{1,0:T(8,128)(2,1)S(1)} collective-permute-done((bf16[256,512]{1,0:T(8,128)(2,1)S(1)}, bf16[256,512]{1,0:T(8,128)(2,1)S(1)}, u32[]{:S(2)}, u32[]{:S(2)}) %collective-permute-start.22) | collective-permute-done | bytes 262176 | tf_op jit(solution)/shard_map/ppermute | solution.py:231
  226.8 1.5 collective-permute-start.23
  228.4 5.1 %collective-permute-done.23 = bf16[256,512]{1,0:T(8,128)(2,1)S(1)} collective-permute-done((bf16[256,512]{1,0:T(8,128)(2,1)S(1)}, bf16[256,512]{1,0:T(8,128)(2,1)S(1)}, u32[]{:S(2)}, u32[]{:S(2)}) %collective-permute-start.23) | collective-permute-done | bytes 262176 | tf_op jit(solution)/shard_map/ppermute | solution.py:231
  233.7 1.5 collective-permute-start.20
  235.8 1.8 bitcast_convert_fusion.1
  237.6 2.5 collective-permute-done.20
  241.7 1.6 collective-permute-start.21
  243.8 4.3 %collective-permute-done.21 = bf16[256,512]{1,0:T(8,128)(2,1)S(1)} collective-permute-done((bf16[256,512]{1,0:T(8,128)(2,1)S(1)}, bf16[256,512]{1,0:T(8,128)(2,1)S(1)}, u32[]{:S(2)}, u32[]{:S(2)}) %collective-permute-start.21) | collective-permute-done | bytes 262176 | tf_op jit(solution)/shard_map/ppermute | solution.py:231
  250.6 1.7 collective-permute-start.28
  252.9 2.0 fusion.31
  254.9 3.5 %collective-permute-done.26 = bf16[256,512]{1,0:T(8,128)(2,1)S(1)} collective-permute-done((bf16[256,512]{1,0:T(8,128)(2,1)S(1)}, bf16[256,512]{1,0:T(8,128)(2,1)S(1)}, u32[]{:S(2)}, u32[]{:S(2)}) %collective-permute-start.26) | collective-permute-done | bytes 262176 | tf_op jit(solution)/shard_map/ppermute | solution.py:176
  258.4 2.0 convolution_add_fusion.1
  260.5 2.0 fusion.27
  262.5 2.4 collective-permute-done.27
  264.9 3.3 %fusion.8 = f32[256,1536]{1,0:T(8,128)} fusion(f32[256,1536]{1,0:T(8,128)S(1)} %fusion.27, f32[256,1536]{1,0:T(8,128)S(1)} %convolution_add_fusion.1, bf16[256,512]{1,0:T(8,128)(2,1)S(1)} %collective-permute-done.27, bf16[2048,1536]{0,1:T(8,128)(2,1)} %bitcast.138, s32[]{:T(128)S(6)} %select_n.122), kind=kOutput, calls=%fused_computation.12 | convolution fusion | flops 403439616 | bytes 6553604 | tf_op jit(solution)/shard_map/dot_general | solution.py:177
  268.1 3.1 %copy.96 = f32[256,1536]{0,1:T(8,128)} copy(f32[256,1536]{1,0:T(8,128)} %fusion.8) | data formatting | bytes 3145728 | tf_op jit(solution)/shard_map/add | solution.py:177
  272.7 5.9 %all-reduce = (f32[256]{0:T(256)S(1)}, f32[256]{0:T(256)S(1)}, f32[256]{0:T(256)S(1)}) all-reduce(f32[256]{0:T(256)S(1)} %get-tuple-element.27, f32[256]{0:T(256)S(1)} %get-tuple-element.31, f32[256]{0:T(256)S(1)} %get-tuple-element.26), channel_id=1, replica_groups=mesh['seq'=8,'tp'=4] {'tp'}, use_global_device_ids=true, to_apply=%region_6.7 | all-reduce | flops 768 | bytes 6144 | tf_op jit(solution)/shard_map/psum | solution.py:373
  278.6 1.6 fusion.54
  (130 shorter events, 37.0 us)
Async XLA Ops:
  7.2 38.9 %copy-start = (bf16[512,2048]{1,0:T(8,128)(2,1)S(1)}, bf16[512,2048]{1,0:T(8,128)(2,1)}, u32[]{:S(2)}) copy-start(bf16[512,2048]{1,0:T(8,128)(2,1)} %param.24) | copy-start | bytes 6291460
  7.2 113.8 %all-gather.4.cloned.1.call-start = ((), (), s32[]{:S(2)}) async-start(), calls=%async_computation | async-start | bytes 3932160 | tf_op jit(solution)/shard_map/all_gather | solution.py:130
  7.3 7.3 %copy-start.17 = (s32[8]{0:T(128)S(1)}, s32[8]{0:T(128)}, u32[]{:S(2)}) copy-start(s32[8]{0:T(128)} %param.23) | copy-start | bytes 100
  10.1 14.3 %collective-permute-start = (bf16[2,256,512]{2,1,0:T(8,128)(2,1)}, bf16[2,256,512]{2,1,0:T(8,128)(2,1)S(1)}, u32[]{:S(2)}, u32[]{:S(2)}) collective-permute-start(bf16[2,256,512]{2,1,0:T(8,128)(2,1)} %get-tuple-element.41), channel_id=1, source_target_pairs={{0,1},{1,2},{2,3},{3,0},{4,5},{5,6},{6,7},{7,4},{8,9},{9,10},{10,1... | collective-permute-start | bytes 1572872 | tf_op jit(solution)/shard_map/ppermute | solution.py:314
  10.6 15.6 %collective-permute-start.1 = (bf16[2,256,512]{2,1,0:T(8,128)(2,1)}, bf16[2,256,512]{2,1,0:T(8,128)(2,1)}, u32[]{:S(2)}, u32[]{:S(2)}) collective-permute-start(bf16[2,256,512]{2,1,0:T(8,128)(2,1)} %get-tuple-element.43), channel_id=1, source_target_pairs={{0,2},{1,3},{2,0},{3,1},{4,6},{5,7},{6,4},{7,5},{8,10},{9,11},{10,... | collective-permute-start | bytes 1572872 | tf_op jit(solution)/shard_map/ppermute | solution.py:314
  13.1 23.3 %collective-permute-start.2 = (bf16[2,256,512]{2,1,0:T(8,128)(2,1)}, bf16[2,256,512]{2,1,0:T(8,128)(2,1)}, u32[]{:S(2)}, u32[]{:S(2)}) collective-permute-start(bf16[2,256,512]{2,1,0:T(8,128)(2,1)} %get-tuple-element.42), channel_id=1, source_target_pairs={{0,3},{1,0},{2,1},{3,2},{4,7},{5,4},{6,5},{7,6},{8,11},{9,8},{10,9... | collective-permute-start | bytes 1572872 | tf_op jit(solution)/shard_map/ppermute | solution.py:314
  15.2 9.0 %copy-start.10 = (f32[256,8]{0,1:T(8,128)S(1)}, f32[256,8]{0,1:T(8,128)}, u32[]{:S(2)}) copy-start(f32[256,8]{0,1:T(8,128)} %param.27) | copy-start | bytes 24580
  15.2 9.1 %copy-start.11 = (s32[256,8]{0,1:T(8,128)S(1)}, s32[256,8]{0,1:T(8,128)}, u32[]{:S(2)}) copy-start(s32[256,8]{0,1:T(8,128)} %param.26) | copy-start | bytes 24580
  42.8 3.3 %copy-start.8 = (bf16[256,512]{1,0:T(8,128)(2,1)S(1)}, bf16[256,512]{1,0:T(8,128)(2,1)}, u32[]{:S(2)}) copy-start(bf16[256,512]{1,0:T(8,128)(2,1)} %shard_map.192) | copy-start | bytes 786436
  46.1 13.9 %copy-start.9 = (bf16[256,512]{1,0:T(8,128)(2,1)S(1)}, bf16[256,512]{1,0:T(8,128)(2,1)}, u32[]{:S(2)}) copy-start(bf16[256,512]{1,0:T(8,128)(2,1)} %param.17) | copy-start | bytes 786436
  46.8 1.3 copy-start.3
  48.1 21.3 %copy-start.12 = (f32[512]{0:T(512)S(1)}, f32[512]{0:T(512)}, u32[]{:S(2)}) copy-start(f32[512]{0:T(512)} %param.25) | copy-start | bytes 6148
  48.2 8.2 %collective-permute-start.3 = (bf16[256,512]{1,0:T(8,128)(2,1)S(1)}, bf16[256,512]{1,0:T(8,128)(2,1)S(1)}, u32[]{:S(2)}, u32[]{:S(2)}) collective-permute-start(bf16[256,512]{1,0:T(8,128)(2,1)S(1)} %get-tuple-element.37), channel_id=1, source_target_pairs={{0,1},{1,2},{2,3},{3,0},{4,5},{5,6},{6,7},{7,4},{8,9},{9,10},{10,1... | collective-permute-start | bytes 786440 | tf_op jit(solution)/shard_map/ppermute | solution.py:160
  48.3 9.4 %collective-permute-start.4 = (bf16[256,512]{1,0:T(8,128)(2,1)S(1)}, bf16[256,512]{1,0:T(8,128)(2,1)S(1)}, u32[]{:S(2)}, u32[]{:S(2)}) collective-permute-start(bf16[256,512]{1,0:T(8,128)(2,1)S(1)} %get-tuple-element.39), channel_id=1, source_target_pairs={{0,2},{1,3},{2,0},{3,1},{4,6},{5,7},{6,4},{7,5},{8,10},{9,11},{10,... | collective-permute-start | bytes 786440 | tf_op jit(solution)/shard_map/ppermute | solution.py:160
  50.6 9.3 %collective-permute-start.5 = (bf16[256,512]{1,0:T(8,128)(2,1)S(1)}, bf16[256,512]{1,0:T(8,128)(2,1)S(1)}, u32[]{:S(2)}, u32[]{:S(2)}) collective-permute-start(bf16[256,512]{1,0:T(8,128)(2,1)S(1)} %get-tuple-element.38), channel_id=1, source_target_pairs={{0,3},{1,0},{2,1},{3,2},{4,7},{5,4},{6,5},{7,6},{8,11},{9,8},{10,9... | collective-permute-start | bytes 786440 | tf_op jit(solution)/shard_map/ppermute | solution.py:160
  69.6 8.1 %collective-permute-start.7 = (bf16[272,512]{1,0:T(8,128)(2,1)S(1)}, bf16[272,512]{1,0:T(8,128)(2,1)S(1)}, u32[]{:S(2)}, u32[]{:S(2)}) collective-permute-start(bf16[272,512]{1,0:T(8,128)(2,1)S(1)} %get-tuple-element.62), channel_id=1, source_target_pairs={{0,4},{8,0},{16,8},{24,16},{28,24},{20,28},{12,20},{4,12},{1,5},{9... | collective-permute-start | bytes 835592 | tf_op jit(solution)/shard_map/ppermute | solution.py:211
  71.3 7.6 %collective-permute-start.6 = (bf16[272,512]{1,0:T(8,128)(2,1)S(1)}, bf16[272,512]{1,0:T(8,128)(2,1)S(1)}, u32[]{:S(2)}, u32[]{:S(2)}) collective-permute-start(bf16[272,512]{1,0:T(8,128)(2,1)S(1)} %get-tuple-element.62), channel_id=1, source_target_pairs={{0,8},{8,16},{16,24},{24,28},{28,20},{20,12},{12,4},{4,0},{1,9},{9... | collective-permute-start | bytes 835592 | tf_op jit(solution)/shard_map/ppermute | solution.py:207
  80.0 52.2 %all-gather.6.cloned.1.call-start = ((), (), s32[]{:S(2)}) async-start(), calls=%async_computation.1 | async-start | bytes 2621440 | tf_op jit(solution)/shard_map/all_gather | solution.py:130
  80.1 6.9 %collective-permute-start.12 = (bf16[272,512]{1,0:T(8,128)(2,1)S(1)}, bf16[272,512]{1,0:T(8,128)(2,1)S(1)}, u32[]{:S(2)}, u32[]{:S(2)}) collective-permute-start(bf16[272,512]{1,0:T(8,128)(2,1)S(1)} %collective-permute-done.6), channel_id=1, source_target_pairs={{0,8},{8,16},{16,24},{24,28},{28,20},{20,12},{12,4},{4,0},{1,9},{9... | collective-permute-start | bytes 835592 | tf_op jit(solution)/shard_map/ppermute | solution.py:207
  80.7 6.8 %collective-permute-start.10 = (bf16[272,512]{1,0:T(8,128)(2,1)S(1)}, bf16[272,512]{1,0:T(8,128)(2,1)S(1)}, u32[]{:S(2)}, u32[]{:S(2)}) collective-permute-start(bf16[272,512]{1,0:T(8,128)(2,1)S(1)} %collective-permute-done.7), channel_id=1, source_target_pairs={{0,4},{8,0},{16,8},{24,16},{28,24},{20,28},{12,20},{4,12},{1,5},{9... | collective-permute-start | bytes 835592 | tf_op jit(solution)/shard_map/ppermute | solution.py:211
  86.9 7.7 %collective-permute-start.13 = (bf16[272,512]{1,0:T(8,128)(2,1)S(1)}, bf16[272,512]{1,0:T(8,128)(2,1)S(1)}, u32[]{:S(2)}, u32[]{:S(2)}) collective-permute-start(bf16[272,512]{1,0:T(8,128)(2,1)S(1)} %collective-permute-done.12), channel_id=1, source_target_pairs={{0,8},{8,16},{16,24},{24,28},{28,20},{20,12},{12,4},{4,0},{1,9},{9... | collective-permute-start | bytes 835592 | tf_op jit(solution)/shard_map/ppermute | solution.py:207
  87.5 7.6 %collective-permute-start.11 = (bf16[272,512]{1,0:T(8,128)(2,1)S(1)}, bf16[272,512]{1,0:T(8,128)(2,1)S(1)}, u32[]{:S(2)}, u32[]{:S(2)}) collective-permute-start(bf16[272,512]{1,0:T(8,128)(2,1)S(1)} %collective-permute-done.10), channel_id=1, source_target_pairs={{0,4},{8,0},{16,8},{24,16},{28,24},{20,28},{12,20},{4,12},{1,5},{9... | collective-permute-start | bytes 835592 | tf_op jit(solution)/shard_map/ppermute | solution.py:211
  94.7 6.5 %collective-permute-start.14 = (bf16[272,512]{1,0:T(8,128)(2,1)S(1)}, bf16[272,512]{1,0:T(8,128)(2,1)S(1)}, u32[]{:S(2)}, u32[]{:S(2)}) collective-permute-start(bf16[272,512]{1,0:T(8,128)(2,1)S(1)} %collective-permute-done.13), channel_id=1, source_target_pairs={{0,8},{8,16},{16,24},{24,28},{28,20},{20,12},{12,4},{4,0},{1,9},{9... | collective-permute-start | bytes 835592 | tf_op jit(solution)/shard_map/ppermute | solution.py:207
  102.1 69.3 %all-gather.8.cloned.1.call-start = ((), (), s32[]{:S(2)}) async-start(), calls=%async_computation.2 | async-start | bytes 3932160 | tf_op jit(solution)/shard_map/all_gather | solution.py:130
  132.3 7.2 %copy-start.16 = (bf16[4,768,512]{2,1,0:T(8,128)(2,1)S(1)}, bf16[4,768,512]{2,1,0:T(8,128)(2,1)}, u32[]{:S(2)}) copy-start(bf16[4,768,512]{2,1,0:T(8,128)(2,1)} %all-gather.4.cloned.1.call-done) | copy-start | bytes 9437188
  137.6 2.5 copy-start.4
  138.8 40.0 %collective-permute-start.15 = (bf16[2,512,256]{1,2,0:T(8,128)(2,1)}, bf16[2,512,256]{1,2,0:T(8,128)(2,1)}, u32[]{:S(2)}, u32[]{:S(2)}) collective-permute-start(bf16[2,512,256]{1,2,0:T(8,128)(2,1)} %multiply_convert_fusion.2), channel_id=1, source_target_pairs={{0,2},{1,3},{2,0},{3,1},{4,6},{5,7},{6,4},{7,5},{8,10},{9,11},{10,... | collective-permute-start | bytes 1572872 | tf_op jit(solution)/shard_map/ppermute | solution.py:188
  177.9 2.4 copy-start.2
  178.4 20.4 %collective-permute-start.18 = (bf16[2,768,256]{1,2,0:T(8,128)(2,1)S(1)}, bf16[2,768,256]{1,2,0:T(8,128)(2,1)S(1)}, u32[]{:S(2)}, u32[]{:S(2)}) collective-permute-start(bf16[2,768,256]{1,2,0:T(8,128)(2,1)S(1)} %multiply_convert_fusion), channel_id=1, source_target_pairs={{0,2},{1,3},{2,0},{3,1},{4,6},{5,7},{6,4},{7,5},{8,10},{9,11},{10,... | collective-permute-start | bytes 2359304 | tf_op jit(solution)/shard_map/ppermute | solution.py:188
  180.0 35.3 %collective-permute-start.16 = (bf16[2,2,512,256]{2,3,1,0:T(8,128)(2,1)S(1)}, bf16[2,2,512,256]{2,3,1,0:T(8,128)(2,1)S(1)}, u32[]{:S(2)}, u32[]{:S(2)}) collective-permute-start(bf16[2,2,512,256]{2,3,1,0:T(8,128)(2,1)S(1)} %pad_maximum_fusion.6), channel_id=1, source_target_pairs={{0,1},{1,0},{2,3},{3,2},{4,5},{5,4},{6,7},{7,6},{8,9},{9,8},{10,11... | collective-permute-start | bytes 3145736 | tf_op jit(solution)/shard_map/ppermute | solution.py:189
  180.8 34.2 %collective-permute-start.8 = (bf16[2,768,256]{1,2,0:T(8,128)(2,1)S(1)}, bf16[2,768,256]{1,2,0:T(8,128)(2,1)S(1)}, u32[]{:S(2)}, u32[]{:S(2)}) collective-permute-start(bf16[2,768,256]{1,2,0:T(8,128)(2,1)S(1)} %multiply_convert_fusion.1), channel_id=1, source_target_pairs={{0,2},{1,3},{2,0},{3,1},{4,6},{5,7},{6,4},{7,5},{8,10},{9,11},{10,... | collective-permute-start | bytes 2359304 | tf_op jit(solution)/shard_map/ppermute | solution.py:188
  199.0 22.1 %collective-permute-start.19 = (bf16[2,2,768,256]{2,3,1,0:T(8,128)(2,1)S(1)}, bf16[2,2,768,256]{2,3,1,0:T(8,128)(2,1)S(1)}, u32[]{:S(2)}, u32[]{:S(2)}) collective-permute-start(bf16[2,2,768,256]{2,3,1,0:T(8,128)(2,1)S(1)} %pad_maximum_fusion.5), channel_id=1, source_target_pairs={{0,1},{1,0},{2,3},{3,2},{4,5},{5,4},{6,7},{7,6},{8,9},{9,8},{10,11... | collective-permute-start | bytes 4718600 | tf_op jit(solution)/shard_map/ppermute | solution.py:189
  215.0 1.6 copy-start.5
  215.2 13.1 %collective-permute-start.9 = (bf16[2,2,768,256]{2,3,1,0:T(8,128)(2,1)S(1)}, bf16[2,2,768,256]{2,3,1,0:T(8,128)(2,1)S(1)}, u32[]{:S(2)}, u32[]{:S(2)}) collective-permute-start(bf16[2,2,768,256]{2,3,1,0:T(8,128)(2,1)S(1)} %pad_maximum_fusion.4), channel_id=1, source_target_pairs={{0,1},{1,0},{2,3},{3,2},{4,5},{5,4},{6,7},{7,6},{8,9},{9,8},{10,11... | collective-permute-start | bytes 4718600 | tf_op jit(solution)/shard_map/ppermute | solution.py:189
  219.0 7.7 %collective-permute-start.22 = (bf16[256,512]{1,0:T(8,128)(2,1)S(1)}, bf16[256,512]{1,0:T(8,128)(2,1)S(1)}, u32[]{:S(2)}, u32[]{:S(2)}) collective-permute-start(bf16[256,512]{1,0:T(8,128)(2,1)S(1)} %get-tuple-element.60), channel_id=1, source_target_pairs={{0,4},{8,0},{16,8},{24,16},{28,24},{20,28},{12,20},{4,12},{1,5},{9... | collective-permute-start | bytes 786440 | tf_op jit(solution)/shard_map/ppermute | solution.py:231
  220.5 7.9 %collective-permute-start.17 = (bf16[256,512]{1,0:T(8,128)(2,1)S(1)}, bf16[256,512]{1,0:T(8,128)(2,1)S(1)}, u32[]{:S(2)}, u32[]{:S(2)}) collective-permute-start(bf16[256,512]{1,0:T(8,128)(2,1)S(1)} %get-tuple-element.59), channel_id=1, source_target_pairs={{0,8},{8,16},{16,24},{24,28},{28,20},{20,12},{12,4},{4,0},{1,9},{9... | collective-permute-start | bytes 786440 | tf_op jit(solution)/shard_map/ppermute | solution.py:231
  226.8 6.8 %collective-permute-start.23 = (bf16[256,512]{1,0:T(8,128)(2,1)S(1)}, bf16[256,512]{1,0:T(8,128)(2,1)S(1)}, u32[]{:S(2)}, u32[]{:S(2)}) collective-permute-start(bf16[256,512]{1,0:T(8,128)(2,1)S(1)} %add_convert_fusion.2), channel_id=1, source_target_pairs={{0,4},{8,0},{16,8},{24,16},{28,24},{20,28},{12,20},{4,12},{1,5},{9... | collective-permute-start | bytes 786440 | tf_op jit(solution)/shard_map/ppermute | solution.py:231
  233.7 6.4 %collective-permute-start.20 = (bf16[256,512]{1,0:T(8,128)(2,1)S(1)}, bf16[256,512]{1,0:T(8,128)(2,1)S(1)}, u32[]{:S(2)}, u32[]{:S(2)}) collective-permute-start(bf16[256,512]{1,0:T(8,128)(2,1)S(1)} %get-tuple-element.55), channel_id=1, source_target_pairs={{0,8},{8,16},{16,24},{24,28},{28,20},{20,12},{12,4},{4,0},{1,9},{9... | collective-permute-start | bytes 786440 | tf_op jit(solution)/shard_map/ppermute | solution.py:231
  235.2 6.4 %collective-permute-start.24 = (bf16[256,512]{1,0:T(8,128)(2,1)S(1)}, bf16[256,512]{1,0:T(8,128)(2,1)S(1)}, u32[]{:S(2)}, u32[]{:S(2)}) collective-permute-start(bf16[256,512]{1,0:T(8,128)(2,1)S(1)} %get-tuple-element.56), channel_id=1, source_target_pairs={{0,4},{8,0},{16,8},{24,16},{28,24},{20,28},{12,20},{4,12},{1,5},{9... | collective-permute-start | bytes 786440 | tf_op jit(solution)/shard_map/ppermute | solution.py:231
  237.6 12.3 %copy-start.13 = (f32[512]{0:T(512)S(1)}, f32[512]{0:T(512)}, u32[]{:S(2)}) copy-start(f32[512]{0:T(512)} %param.30) | copy-start | bytes 6148
  241.7 6.4 %collective-permute-start.21 = (bf16[256,512]{1,0:T(8,128)(2,1)S(1)}, bf16[256,512]{1,0:T(8,128)(2,1)S(1)}, u32[]{:S(2)}, u32[]{:S(2)}) collective-permute-start(bf16[256,512]{1,0:T(8,128)(2,1)S(1)} %get-tuple-element.53), channel_id=1, source_target_pairs={{0,8},{8,16},{16,24},{24,28},{28,20},{20,12},{12,4},{4,0},{1,9},{9... | collective-permute-start | bytes 786440 | tf_op jit(solution)/shard_map/ppermute | solution.py:231
  243.3 6.4 %collective-permute-start.25 = (bf16[256,512]{1,0:T(8,128)(2,1)S(1)}, bf16[256,512]{1,0:T(8,128)(2,1)S(1)}, u32[]{:S(2)}, u32[]{:S(2)}) collective-permute-start(bf16[256,512]{1,0:T(8,128)(2,1)S(1)} %get-tuple-element.54), channel_id=1, source_target_pairs={{0,4},{8,0},{16,8},{24,16},{28,24},{20,28},{12,20},{4,12},{1,5},{9... | collective-permute-start | bytes 786440 | tf_op jit(solution)/shard_map/ppermute | solution.py:231
  250.6 7.8 %collective-permute-start.26 = (bf16[256,512]{1,0:T(8,128)(2,1)S(1)}, bf16[256,512]{1,0:T(8,128)(2,1)S(1)}, u32[]{:S(2)}, u32[]{:S(2)}) collective-permute-start(bf16[256,512]{1,0:T(8,128)(2,1)S(1)} %get-tuple-element.57), channel_id=1, source_target_pairs={{0,1},{1,2},{2,3},{3,0},{4,5},{5,6},{6,7},{7,4},{8,9},{9,10},{10,1... | collective-permute-start | bytes 786440 | tf_op jit(solution)/shard_map/ppermute | solution.py:176
  250.6 9.8 %collective-permute-start.28 = (bf16[256,512]{1,0:T(8,128)(2,1)S(1)}, bf16[256,512]{1,0:T(8,128)(2,1)S(1)}, u32[]{:S(2)}, u32[]{:S(2)}) collective-permute-start(bf16[256,512]{1,0:T(8,128)(2,1)S(1)} %get-tuple-element.57), channel_id=1, source_target_pairs={{0,3},{1,0},{2,1},{3,2},{4,7},{5,4},{6,5},{7,6},{8,11},{9,8},{10,9... | collective-permute-start | bytes 786440 | tf_op jit(solution)/shard_map/ppermute | solution.py:176
  252.4 12.5 %collective-permute-start.27 = (bf16[256,512]{1,0:T(8,128)(2,1)S(1)}, bf16[256,512]{1,0:T(8,128)(2,1)S(1)}, u32[]{:S(2)}, u32[]{:S(2)}) collective-permute-start(bf16[256,512]{1,0:T(8,128)(2,1)S(1)} %get-tuple-element.57), channel_id=1, source_target_pairs={{0,2},{1,3},{2,0},{3,1},{4,6},{5,7},{6,4},{7,5},{8,10},{9,11},{10,... | collective-permute-start | bytes 786440 | tf_op jit(solution)/shard_map/ppermute | solution.py:176
  268.1 10.5 %copy-start.14 = (f32[512]{0:T(512)S(1)}, f32[512]{0:T(512)}, u32[]{:S(2)}) copy-start(f32[512]{0:T(512)} %param.33) | copy-start | bytes 6148
  268.1 10.5 %copy-start.15 = (f32[512]{0:T(512)S(1)}, f32[512]{0:T(512)}, u32[]{:S(2)}) copy-start(f32[512]{0:T(512)} %param.32) | copy-start | bytes 6148
  271.2 11.5 %copy-start.1 = (bf16[512,2048]{1,0:T(8,128)(2,1)S(1)}, bf16[512,2048]{1,0:T(8,128)(2,1)}, u32[]{:S(2)}) copy-start(bf16[512,2048]{1,0:T(8,128)(2,1)} %param.24) | copy-start | bytes 6291460
  (2 other events, 2.1 us)
Sparse Core Ops, SparseCore 0:
  80.1 27.8 all-gather.3
  109.6 22.5 all-gather.5
  133.8 37.6 all-gather.7

commit v18 on v17

--- a/solution.py
+++ b/solution.py
@@ -101,7 +101,7 @@
 
 def dense_experts(moe_in, expert_ids, route_weights, expert_gate_up, down_full, qkv_flat, here, experts_all):
     local_experts = expert_gate_up.shape[0]
-    hidden_quarter = expert_gate_up.shape[2] // 2
+    hidden_quarter = expert_gate_up.shape[-1] // 2
     tokens, quarter = moe_in.shape
     seq_count = experts_all // local_experts
     gate_w = jnp.sum(
@@ -127,7 +127,7 @@
         gate_all = info_all[:, 0] + info_all[:, 1]
         gate_local = lax.dynamic_slice_in_dim(gate_all, here * local_experts, local_experts, axis=1)
         gate_local = jnp.transpose(gate_local, (1, 0, 2)).reshape(local_experts, count * tokens)
-        rows = lax.all_gather(rows_q, "tp", axis=0, tiled=False)
+        rows = pair_gather(rows_q)
         if begin == 0:
             rows, expert_gate_up, qkv_flat = lax.optimization_barrier((rows, expert_gate_up, qkv_flat))
         gate_up_split = expert_gate_up.reshape(local_experts, rows.shape[0], quarter, -1)
@@ -317,7 +317,10 @@
         else:
             order = (tp_here - jnp.arange(tp_count, dtype=jnp.int32)) % tp_count
         down_full = jnp.take(jnp.stack(pieces), order, axis=0)
-        gate_up_flat = expert_gate_up.reshape(local_experts, D, -1)
+        gate_up_flat = expert_gate_up.reshape(local_experts, tp_count, quarter_width, -1)
+        if tp_count == 4:
+            source_order = tp_here ^ jnp.arange(tp_count, dtype=jnp.int32)
+            gate_up_flat = jnp.take(gate_up_flat, source_order, axis=1)
         qkv_flat = qkv_proj.reshape(D, -1)
     local_width = new_queries.shape[1]
     local_heads = local_width // HEAD_DIM

time: 290 us -> 269 us (0.928)
  waiting for transfers between devices: 139 us -> 113 us
  between operations: 14.3 us -> 1.25 us
  other arithmetic: 18 us -> 28.4 us
  local copies, waits for them, and re-layouts: 35.7 us -> 43.5 us
  matrix products: 33 us -> 26.7 us
  starting transfers between devices: 26.4 us -> 31.5 us
    all_gather x3 -> x0, waiting for transfers between devices: 37.4 us -> none  [dense_experts(): rows = lax.all_gather(rows_q, 'tp', axis=0, tiled=False)]
    ppermute x3 -> x6, waiting for transfers between devices: 31.5 us -> 51.4 us  [pair_gather(): far = lax.ppermute(block, 'tp', [(i, i ^ 2) for i in range(4)])]
    ppermute x4, waiting for transfers between devices: 17.8 us -> 7.23 us  [ring_all_gather(): ahead = lax.ppermute(ahead, 'seq', forward)]
    dot_general x3, matrix products: 17 us -> 11.7 us  [dense_experts(): jnp.einsum('qtd,eqdf->etf', rows, gate_up_split, preferred_element_type=j...]
    gather x0 -> x1, local copies, waits for them, and re-layouts: none -> 5.13 us  [body(): gate_up_flat = jnp.take(gate_up_flat, source_order, axis=1)]
    select_n x0 -> x2, other arithmetic: none -> 4.74 us  [body(): gate_up_flat = jnp.take(gate_up_flat, source_order, axis=1)]
    ppermute x3 -> x6, starting transfers between devices: 2.23 us -> 6.38 us  [pair_gather(): far = lax.ppermute(block, 'tp', [(i, i ^ 2) for i in range(4)])]
    ppermute x3, waiting for transfers between devices: 6.01 us -> 9.49 us  [ring_all_gather(): behind = lax.ppermute(behind, 'seq', backward)]
  transfers between devices with their start and end apart: 32 -> 35, of which waited for: 23 -> 24; matrix products, arithmetic and copies ran while one was open for 19% -> 24% of each run, Pallas kernels for 3% -> 3%
where the time goes in v18:
time: 269 us; the launch traced here: 267 us
  waiting for transfers between devices  113 us (42%)
  local copies, waits for them, and re-layouts  43.5 us (16%)
  starting transfers between devices  31.5 us (12%)
  other arithmetic  28.4 us (11%)
  matrix products  26.7 us (10%)
  blocking collectives  14.4 us (5%)
  Pallas kernels  8.99 us (3%)
    ppermute x6, waiting for transfers between devices, pair_gather(): far = lax.ppermute(block, 'tp', [(i, i ^ 2) for i in range(4)])  51.4 us
    ppermute x7, waiting for transfers between devices, ring_reduce_scatter(): lax.ppermute(acc.astype(jnp.bfloat16), 'seq', pairs).astype(jnp.float32)  18.2 us
    unnamed x53, local copies, waits for them, and re-layouts  17.3 us
    ppermute x3, waiting for transfers between devices, body(): pieces.append(lax.ppermute(piece, 'tp', pairs))  12.1 us
    dot_general x3, matrix products, dense_experts(): jnp.einsum('qtd,eqdf->etf', rows, gate_up_split, preferred_element_type=j...  11.7 us
    ppermute x3, waiting for transfers between devices, ring_all_gather(): behind = lax.ppermute(behind, 'seq', backward)  9.49 us
    ppermute x3, waiting for transfers between devices, permute_reduce_scatter(): total = total + lax.ppermute(piece, 'tp', pairs).astype(jnp.float32)  9.29 us
    pallas_call x1, Pallas kernels, flash_attention(): pl.pallas_call(kernel, grid_spec=grid_spec, out_shape=jax.ShapeDtypeStruc...  8.99 us
  transfers between devices with their start and end apart: 35, of which 24 were waited for; matrix products, arithmetic and copies ran while one was open for 24% of the time, Pallas kernels for 3%

profile of v18, /device:TPU:0, one launch (start us, length us, event | category | flops | bytes accessed | tf_op | source)
XLA Modules:
  0.0 267.3 jit_solution(3690928809063326971)
XLA Ops:
  0.7 2.9 %dynamic-slice_bitcast_fusion = (bf16[1,2,256,512]{3,2,1,0:T(8,128)(2,1)S(1)}, bf16[2,256,512]{2,1,0:T(8,128)(2,1)}, bf16[2,256,512]{2,1,0:T(8,128)(2,1)}, bf16[2,256,512]{2,1,0:T(8,128)(2,1)}) fusion(bf16[2,256,2048]{2,1,0:T(8,128)(2,1)} %param.29, s32[]{:T(128)S(6)} %select_n.127, s32[]{:T(128)S(6)} %select_n.129, s32[]{:T(128)S(6)} %select_n.133, ...), kind=kLoop, calls=%fused_computation.95 | loop fusion | bytes 4194320 | tf_op jit(solution)/shard_map/stack | solution.py:319
  4.0 2.5 collective-permute-start.1
  8.6 9.0 %shard_map.192 = bf16[256,512]{1,0:T(8,128)(2,1)} custom-call(s32[1]{0:T(128)} %dynamic_slice.55.len_ref, bf16[256,512]{1,0:T(8,128)(2,1)} %q_ref.1, bf16[4096,512]{1,0:T(8,128)(2,1)} %bitcast.156, bf16[4096,512]{1,0:T(8,128)(2,1)} %bitcast.157, bf16[256,512]{1,0:T(8,128)(2,1)} %nk_ref.1, bf16[256,512]{1,0:T(8,128)(2,1)} %nv_ref.1), custom_call_target="tpu_custom_call" | custom-call | tf_op jit(solution)/shard_map/pallas_call | solution.py:94
  17.9 1.8 collective-permute-done.1
  19.6 10.2 %collective-permute-done.2 = bf16[2,256,512]{2,1,0:T(8,128)(2,1)} collective-permute-done((bf16[2,256,512]{2,1,0:T(8,128)(2,1)}, bf16[2,256,512]{2,1,0:T(8,128)(2,1)}, u32[]{:S(2)}, u32[]{:S(2)}) %collective-permute-start.2) | collective-permute-done | bytes 524320 | tf_op jit(solution)/shard_map/ppermute | solution.py:314
  29.9 2.8 %pad_maximum_fusion.3 = bf16[4,2,256,512]{3,2,1,0:T(8,128)(2,1)} fusion(bf16[1,2,256,512]{3,2,1,0:T(8,128)(2,1)} %bitcast.5, bf16[1,2,256,512]{3,2,1,0:T(8,128)(2,1)} %bitcast.4, bf16[1,2,256,512]{3,2,1,0:T(8,128)(2,1)S(1)} %bitcast.179, bf16[1,2,256,512]{3,2,1,0:T(8,128)(2,1)S(1)} %get-tuple-element.36), kind=kLoop, calls=%fused_computation.23 | loop fusion | flops 3145728 | bytes 4194304 | tf_op jit(solution)/shard_map/stack | solution.py:319
  32.7 3.7 %gather_fusion = bf16[4,2,256,512]{3,2,1,0:T(8,128)(2,1)} fusion(bf16[4,2,256,512]{3,2,1,0:T(8,128)(2,1)} %pad_maximum_fusion.3, s32[1024]{0:T(1024)S(1)} %pad_clamp_fusion.1), kind=kCustom, calls=%fused_computation | custom fusion | bytes 4194320 | tf_op jit(solution)/shard_map/jit(_take)/gather | solution.py:319
  36.4 3.3 %broadcast_select_fusion = bf16[4,2,256,512]{3,2,1,0:T(8,128)(2,1)} fusion(bf16[4,2,256,512]{3,2,1,0:T(8,128)(2,1)} %gather_fusion, pred[4]{0:T(512)(128)(4,1)S(1)} %compare_and_fusion.1), kind=kLoop, calls=%fused_computation.35 | loop fusion | flops 1048576 | bytes 4194308 | tf_op jit(solution)/shard_map/jit(_take)/select_n | solution.py:319
  41.9 2.3 collective-permute-start.4
  44.2 5.8 %collective-permute-done.3 = bf16[256,512]{1,0:T(8,128)(2,1)S(1)} collective-permute-done((bf16[256,512]{1,0:T(8,128)(2,1)S(1)}, bf16[256,512]{1,0:T(8,128)(2,1)S(1)}, u32[]{:S(2)}, u32[]{:S(2)}) %collective-permute-start.3) | collective-permute-done | bytes 262176 | tf_op jit(solution)/shard_map/ppermute | solution.py:160
  51.3 2.2 collective-permute-done.5
  54.8 8.2 %psum.28 = f32[256]{0:T(256)S(1)} all-reduce(f32[256]{0:T(256)S(1)} %get-tuple-element.29), channel_id=1, replica_groups=mesh['seq'=8,'tp'=4] {'tp'}, use_global_device_ids=true, to_apply=%region_1.2 | all-reduce | flops 256 | bytes 2048 | tf_op jit(solution)/shard_map/psum | solution.py:350
  63.2 1.7 collective-permute-start.7
  65.3 6.0 %collective-permute-done.7 = bf16[272,512]{1,0:T(8,128)(2,1)S(1)} collective-permute-done((bf16[272,512]{1,0:T(8,128)(2,1)S(1)}, bf16[272,512]{1,0:T(8,128)(2,1)S(1)}, u32[]{:S(2)}, u32[]{:S(2)}) %collective-permute-start.7) | collective-permute-done | bytes 278560 | tf_op jit(solution)/shard_map/ppermute | solution.py:211
  74.0 7.6 %reshape.159 = bf16[2,4,512,512]{3,2,1,0:T(8,128)(2,1)} reshape(bf16[2,2048,2,256]{3,2,1,0:T(2,128)(2,1)} %param.28) | data formatting | bytes 8388608 | tf_op jit(solution)/shard_map/reshape | solution.py:320
  81.6 5.1 %gather_fusion.1 = bf16[4,2,512,512]{3,2,1,0:T(8,128)(2,1)} fusion(bf16[2,4,512,512]{3,2,1,0:T(8,128)(2,1)} %reshape.159, s32[1024]{0:T(1024)S(1)} %pad_clamp_fusion), kind=kCustom, calls=%fused_computation.1 | custom fusion | bytes 8388624 | tf_op jit(solution)/shard_map/jit(_take)/gather | solution.py:323
  87.3 4.7 %select_bitcast_fusion = bf16[2,4,512,512]{3,2,0,1:T(8,128)(2,1)} fusion(bf16[4,2,512,512]{3,2,1,0:T(8,128)(2,1)} %gather_fusion.1, pred[4]{0:T(512)(128)(4,1)S(1)} %compare_and_fusion), kind=kLoop, calls=%fused_computation.2 | loop fusion | flops 2097152 | bytes 8388612 | tf_op jit(solution)/shard_map/jit(_take)/select_n | solution.py:323
  92.0 8.9 %copy.56 = bf16[2048,3,512]{0,2,1:T(8,128)(2,1)} copy(bf16[2048,3,512]{2,0,1:T(8,128)(2,1)} %param.31) | data formatting | bytes 12582912 | tf_op args[14]
  100.9 1.6 collective-permute-start.12
  104.3 3.3 %collective-permute-done.12 = bf16[272,512]{1,0:T(8,128)(2,1)} collective-permute-done((bf16[272,512]{1,0:T(8,128)(2,1)S(1)}, bf16[272,512]{1,0:T(8,128)(2,1)}, u32[]{:S(2)}, u32[]{:S(2)}) %collective-permute-start.12) | collective-permute-done | bytes 278560 | tf_op jit(solution)/shard_map/ppermute | solution.py:211
  114.5 6.0 %collective-permute-done.16 = bf16[272,512]{1,0:T(8,128)(2,1)S(1)} collective-permute-done((bf16[272,512]{1,0:T(8,128)(2,1)}, bf16[272,512]{1,0:T(8,128)(2,1)S(1)}, u32[]{:S(2)}, u32[]{:S(2)}) %collective-permute-start.16) | collective-permute-done | bytes 278560 | tf_op jit(solution)/shard_map/ppermute | solution.py:207
  122.9 9.4 %collective-permute-done.22 = bf16[768,512]{1,0:T(8,128)(2,1)} collective-permute-done((bf16[768,512]{1,0:T(8,128)(2,1)}, bf16[768,512]{1,0:T(8,128)(2,1)}, u32[]{:S(2)}, u32[]{:S(2)}) %collective-permute-start.22) | collective-permute-done | bytes 786464 | tf_op jit(solution)/shard_map/ppermute | solution.py:188
  133.8 5.6 %collective-permute-done.17 = bf16[512,512]{1,0:T(8,128)(2,1)} collective-permute-done((bf16[512,512]{1,0:T(8,128)(2,1)S(1)}, bf16[512,512]{1,0:T(8,128)(2,1)}, u32[]{:S(2)}, u32[]{:S(2)}) %collective-permute-start.17) | collective-permute-done | bytes 524320 | tf_op jit(solution)/shard_map/ppermute | solution.py:188
  144.3 3.5 %fusion.23 = f32[2,768,512]{1,2,0:T(8,128)S(1)} fusion(bf16[2,4,512,512]{3,2,0,1:T(8,128)(2,1)S(1)} %copy-done.3, bf16[4,768,512]{2,1,0:T(8,128)(2,1)S(1)} %pad_maximum_fusion), kind=kOutput, calls=%fused_computation.36 | convolution fusion | flops 3221225472 | bytes 10485760 | tf_op jit(solution)/shard_map/qtd,eqdf->etf/dot_general | solution.py:134
  148.8 3.4 %fusion.27 = f32[2,512,512]{1,2,0:T(8,128)S(1)} fusion(bf16[2,4,512,512]{3,2,0,1:T(8,128)(2,1)S(1)} %copy-done.3, bf16[1,512,512]{2,1,0:T(8,128)(2,1)S(1)} %get-tuple-element.54, bf16[1,512,512]{2,1,0:T(8,128)(2,1)} %bitcast.32, bf16[1,512,512]{2,1,0:T(8,128)(2,1)S(1)} %get-tuple-element.53, bf16[1,512,512]{2,1,0:T(8,128)(2,1)S(1)} %bitcast.162), kind=kOutput, calls=%fused_computation.38 | convolution fusion | flops 2150629376 | bytes 8388608 | tf_op jit(solution)/shard_map/qtd,eqdf->etf/dot_general | solution.py:134
  152.6 1.6 collective-permute-start.19
  154.6 4.8 %fusion.26 = f32[2,768,512]{1,2,0:T(8,128)S(1)} fusion(bf16[2,4,512,512]{3,2,0,1:T(8,128)(2,1)S(1)} %copy-done.3, bf16[1,768,512]{2,1,0:T(8,128)(2,1)S(1)} %get-tuple-element.48, bf16[1,768,512]{2,1,0:T(8,128)(2,1)} %bitcast.50, bf16[1,768,512]{2,1,0:T(8,128)(2,1)S(1)} %get-tuple-element.47, bf16[1,768,512]{2,1,0:T(8,128)(2,1)} %bitcast.48), kind=kOutput, calls=%fused_computation.37 | convolution fusion | flops 3225944064 | bytes 10485760 | tf_op jit(solution)/shard_map/qtd,eqdf->etf/dot_general | solution.py:134
  160.5 6.9 %collective-permute-done.19 = bf16[2,512,256]{1,2,0:T(8,128)(2,1)S(1)} collective-permute-done((bf16[2,512,256]{1,2,0:T(8,128)(2,1)S(1)}, bf16[2,512,256]{1,2,0:T(8,128)(2,1)S(1)}, u32[]{:S(2)}, u32[]{:S(2)}) %collective-permute-start.19) | collective-permute-done | bytes 524320 | tf_op jit(solution)/shard_map/ppermute | solution.py:188
  170.3 13.9 %collective-permute-done.24 = bf16[2,768,256]{1,2,0:T(8,128)(2,1)S(1)} collective-permute-done((bf16[2,768,256]{1,2,0:T(8,128)(2,1)S(1)}, bf16[2,768,256]{1,2,0:T(8,128)(2,1)S(1)}, u32[]{:S(2)}, u32[]{:S(2)}) %collective-permute-start.24) | collective-permute-done | bytes 786464 | tf_op jit(solution)/shard_map/ppermute | solution.py:188
  184.9 15.7 %collective-permute-done.10 = bf16[2,768,256]{1,2,0:T(8,128)(2,1)S(1)} collective-permute-done((bf16[2,768,256]{1,2,0:T(8,128)(2,1)S(1)}, bf16[2,768,256]{1,2,0:T(8,128)(2,1)S(1)}, u32[]{:S(2)}, u32[]{:S(2)}) %collective-permute-start.10) | collective-permute-done | bytes 786464 | tf_op jit(solution)/shard_map/ppermute | solution.py:188
  203.6 1.6 collective-permute-start.28
  205.8 1.8 bitcast_convert_fusion
  207.6 4.0 %collective-permute-done.28 = bf16[256,512]{1,0:T(8,128)(2,1)S(1)} collective-permute-done((bf16[256,512]{1,0:T(8,128)(2,1)S(1)}, bf16[256,512]{1,0:T(8,128)(2,1)S(1)}, u32[]{:S(2)}, u32[]{:S(2)}) %collective-permute-start.28) | collective-permute-done | bytes 262176 | tf_op jit(solution)/shard_map/ppermute | solution.py:231
  211.6 1.6 collective-permute-start.29
  213.4 5.3 %collective-permute-done.29 = bf16[256,512]{1,0:T(8,128)(2,1)S(1)} collective-permute-done((bf16[256,512]{1,0:T(8,128)(2,1)S(1)}, bf16[256,512]{1,0:T(8,128)(2,1)S(1)}, u32[]{:S(2)}, u32[]{:S(2)}) %collective-permute-start.29) | collective-permute-done | bytes 262176 | tf_op jit(solution)/shard_map/ppermute | solution.py:231
  220.9 1.8 bitcast_convert_fusion.1
  222.7 2.7 %collective-permute-done.26 = bf16[256,512]{1,0:T(8,128)(2,1)S(1)} collective-permute-done((bf16[256,512]{1,0:T(8,128)(2,1)S(1)}, bf16[256,512]{1,0:T(8,128)(2,1)S(1)}, u32[]{:S(2)}, u32[]{:S(2)}) %collective-permute-start.26) | collective-permute-done | bytes 262176 | tf_op jit(solution)/shard_map/ppermute | solution.py:231
  225.9 1.7 collective-permute-start.27
  227.9 4.3 %collective-permute-done.27 = bf16[256,512]{1,0:T(8,128)(2,1)S(1)} collective-permute-done((bf16[256,512]{1,0:T(8,128)(2,1)S(1)}, bf16[256,512]{1,0:T(8,128)(2,1)S(1)}, u32[]{:S(2)}, u32[]{:S(2)}) %collective-permute-start.27) | collective-permute-done | bytes 262176 | tf_op jit(solution)/shard_map/ppermute | solution.py:231
  232.3 1.6 collective-permute-done.31
  234.9 1.7 collective-permute-start.34
  238.2 2.0 fusion.37
  241.6 2.0 convolution_add_fusion.1
  243.7 2.0 fusion.33
  245.7 3.4 %collective-permute-done.33 = bf16[256,512]{1,0:T(8,128)(2,1)S(1)} collective-permute-done((bf16[256,512]{1,0:T(8,128)(2,1)S(1)}, bf16[256,512]{1,0:T(8,128)(2,1)S(1)}, u32[]{:S(2)}, u32[]{:S(2)}) %collective-permute-start.33) | collective-permute-done | bytes 262176 | tf_op jit(solution)/shard_map/ppermute | solution.py:176
  249.1 3.3 %fusion.13 = f32[256,1536]{1,0:T(8,128)} fusion(f32[256,1536]{1,0:T(8,128)S(1)} %fusion.33, f32[256,1536]{1,0:T(8,128)S(1)} %convolution_add_fusion.1, bf16[256,512]{1,0:T(8,128)(2,1)S(1)} %collective-permute-done.33, bf16[2048,1536]{0,1:T(8,128)(2,1)} %bitcast.150, s32[]{:T(128)S(6)} %select_n.144), kind=kOutput, calls=%fused_computation.21 | convolution fusion | flops 403439616 | bytes 6553604 | tf_op jit(solution)/shard_map/dot_general | solution.py:177
  252.4 3.1 %copy.73 = f32[256,1536]{0,1:T(8,128)} copy(f32[256,1536]{1,0:T(8,128)} %fusion.13) | data formatting | bytes 3145728 | tf_op jit(solution)/shard_map/add | solution.py:177
  257.0 6.2 %all-reduce = (f32[256]{0:T(256)S(1)}, f32[256]{0:T(256)S(1)}, f32[256]{0:T(256)S(1)}) all-reduce(f32[256]{0:T(256)S(1)} %get-tuple-element.23, f32[256]{0:T(256)S(1)} %get-tuple-element.27, f32[256]{0:T(256)S(1)} %get-tuple-element.22), channel_id=1, replica_groups=mesh['seq'=8,'tp'=4] {'tp'}, use_global_device_ids=true, to_apply=%region_6.7 | all-reduce | flops 768 | bytes 6144 | tf_op jit(solution)/shard_map/psum | solution.py:376
  (155 shorter events, 51.4 us)
Async XLA Ops:
  0.6 39.0 %copy-start = (bf16[512,2048]{1,0:T(8,128)(2,1)S(1)}, bf16[512,2048]{1,0:T(8,128)(2,1)}, u32[]{:S(2)}) copy-start(bf16[512,2048]{1,0:T(8,128)(2,1)} %param.24) | copy-start | bytes 6291460
  0.7 7.3 %copy-start.22 = (s32[8]{0:T(128)S(1)}, s32[8]{0:T(128)}, u32[]{:S(2)}) copy-start(s32[8]{0:T(128)} %param.23) | copy-start | bytes 100
  3.6 14.3 %collective-permute-start = (bf16[2,256,512]{2,1,0:T(8,128)(2,1)}, bf16[2,256,512]{2,1,0:T(8,128)(2,1)S(1)}, u32[]{:S(2)}, u32[]{:S(2)}) collective-permute-start(bf16[2,256,512]{2,1,0:T(8,128)(2,1)} %get-tuple-element.37), channel_id=1, source_target_pairs={{0,1},{1,2},{2,3},{3,0},{4,5},{5,6},{6,7},{7,4},{8,9},{9,10},{10,1... | collective-permute-start | bytes 1572872 | tf_op jit(solution)/shard_map/ppermute | solution.py:314
  4.0 15.6 %collective-permute-start.1 = (bf16[2,256,512]{2,1,0:T(8,128)(2,1)}, bf16[2,256,512]{2,1,0:T(8,128)(2,1)}, u32[]{:S(2)}, u32[]{:S(2)}) collective-permute-start(bf16[2,256,512]{2,1,0:T(8,128)(2,1)} %get-tuple-element.39), channel_id=1, source_target_pairs={{0,2},{1,3},{2,0},{3,1},{4,6},{5,7},{6,4},{7,5},{8,10},{9,11},{10,... | collective-permute-start | bytes 1572872 | tf_op jit(solution)/shard_map/ppermute | solution.py:314
  6.6 23.3 %collective-permute-start.2 = (bf16[2,256,512]{2,1,0:T(8,128)(2,1)}, bf16[2,256,512]{2,1,0:T(8,128)(2,1)}, u32[]{:S(2)}, u32[]{:S(2)}) collective-permute-start(bf16[2,256,512]{2,1,0:T(8,128)(2,1)} %get-tuple-element.38), channel_id=1, source_target_pairs={{0,3},{1,0},{2,1},{3,2},{4,7},{5,4},{6,5},{7,6},{8,11},{9,8},{10,9... | collective-permute-start | bytes 1572872 | tf_op jit(solution)/shard_map/ppermute | solution.py:314
  8.6 9.0 %copy-start.16 = (f32[256,8]{0,1:T(8,128)S(1)}, f32[256,8]{0,1:T(8,128)}, u32[]{:S(2)}) copy-start(f32[256,8]{0,1:T(8,128)} %param.27) | copy-start | bytes 24580
  8.6 9.1 %copy-start.17 = (s32[256,8]{0,1:T(8,128)S(1)}, s32[256,8]{0,1:T(8,128)}, u32[]{:S(2)}) copy-start(s32[256,8]{0,1:T(8,128)} %param.26) | copy-start | bytes 24580
  39.7 13.9 %copy-start.15 = (bf16[256,512]{1,0:T(8,128)(2,1)S(1)}, bf16[256,512]{1,0:T(8,128)(2,1)}, u32[]{:S(2)}) copy-start(bf16[256,512]{1,0:T(8,128)(2,1)} %param.17) | copy-start | bytes 786436
  41.7 21.3 %copy-start.18 = (f32[512]{0:T(512)S(1)}, f32[512]{0:T(512)}, u32[]{:S(2)}) copy-start(f32[512]{0:T(512)} %param.25) | copy-start | bytes 6148
  41.8 8.2 %collective-permute-start.3 = (bf16[256,512]{1,0:T(8,128)(2,1)S(1)}, bf16[256,512]{1,0:T(8,128)(2,1)S(1)}, u32[]{:S(2)}, u32[]{:S(2)}) collective-permute-start(bf16[256,512]{1,0:T(8,128)(2,1)S(1)} %get-tuple-element.33), channel_id=1, source_target_pairs={{0,1},{1,2},{2,3},{3,0},{4,5},{5,6},{6,7},{7,4},{8,9},{9,10},{10,1... | collective-permute-start | bytes 786440 | tf_op jit(solution)/shard_map/ppermute | solution.py:160
  41.9 9.4 %collective-permute-start.4 = (bf16[256,512]{1,0:T(8,128)(2,1)S(1)}, bf16[256,512]{1,0:T(8,128)(2,1)S(1)}, u32[]{:S(2)}, u32[]{:S(2)}) collective-permute-start(bf16[256,512]{1,0:T(8,128)(2,1)S(1)} %get-tuple-element.35), channel_id=1, source_target_pairs={{0,2},{1,3},{2,0},{3,1},{4,6},{5,7},{6,4},{7,5},{8,10},{9,11},{10,... | collective-permute-start | bytes 786440 | tf_op jit(solution)/shard_map/ppermute | solution.py:160
  44.2 9.3 %collective-permute-start.5 = (bf16[256,512]{1,0:T(8,128)(2,1)S(1)}, bf16[256,512]{1,0:T(8,128)(2,1)S(1)}, u32[]{:S(2)}, u32[]{:S(2)}) collective-permute-start(bf16[256,512]{1,0:T(8,128)(2,1)S(1)} %get-tuple-element.34), channel_id=1, source_target_pairs={{0,3},{1,0},{2,1},{3,2},{4,7},{5,4},{6,5},{7,6},{8,11},{9,8},{10,9... | collective-permute-start | bytes 786440 | tf_op jit(solution)/shard_map/ppermute | solution.py:160
  63.2 8.1 %collective-permute-start.7 = (bf16[272,512]{1,0:T(8,128)(2,1)S(1)}, bf16[272,512]{1,0:T(8,128)(2,1)S(1)}, u32[]{:S(2)}, u32[]{:S(2)}) collective-permute-start(bf16[272,512]{1,0:T(8,128)(2,1)S(1)} %get-tuple-element.64), channel_id=1, source_target_pairs={{0,4},{8,0},{16,8},{24,16},{28,24},{20,28},{12,20},{4,12},{1,5},{9... | collective-permute-start | bytes 835592 | tf_op jit(solution)/shard_map/ppermute | solution.py:211
  64.9 7.6 %collective-permute-start.6 = (bf16[272,512]{1,0:T(8,128)(2,1)S(1)}, bf16[272,512]{1,0:T(8,128)(2,1)S(1)}, u32[]{:S(2)}, u32[]{:S(2)}) collective-permute-start(bf16[272,512]{1,0:T(8,128)(2,1)S(1)} %get-tuple-element.64), channel_id=1, source_target_pairs={{0,8},{8,16},{16,24},{24,28},{28,20},{20,12},{12,4},{4,0},{1,9},{9... | collective-permute-start | bytes 835592 | tf_op jit(solution)/shard_map/ppermute | solution.py:207
  73.4 29.6 %collective-permute-start.8 = (bf16[768,512]{1,0:T(8,128)(2,1)S(1)}, bf16[768,512]{1,0:T(8,128)(2,1)S(1)}, u32[]{:S(2)}, u32[]{:S(2)}) collective-permute-start(bf16[768,512]{1,0:T(8,128)(2,1)S(1)} %bitcast.153), channel_id=1, source_target_pairs={{0,2},{1,3},{2,0},{3,1},{4,6},{5,7},{6,4},{7,5},{8,10},{9,11},{10,... | collective-permute-start | bytes 2359304 | tf_op jit(solution)/shard_map/ppermute | solution.py:188
  86.8 15.8 %collective-permute-start.14 = (bf16[272,512]{1,0:T(8,128)(2,1)S(1)}, bf16[272,512]{1,0:T(8,128)(2,1)S(1)}, u32[]{:S(2)}, u32[]{:S(2)}) collective-permute-start(bf16[272,512]{1,0:T(8,128)(2,1)S(1)} %copy-done.13), channel_id=1, source_target_pairs={{0,8},{8,16},{16,24},{24,28},{28,20},{20,12},{12,4},{4,0},{1,9},{9... | collective-permute-start | bytes 835592 | tf_op jit(solution)/shard_map/ppermute | solution.py:207
  92.0 8.9 %copy-start.8 = (bf16[272,512]{1,0:T(8,128)(2,1)S(1)}, bf16[272,512]{1,0:T(8,128)(2,1)}, u32[]{:S(2)}) copy-start(bf16[272,512]{1,0:T(8,128)(2,1)} %copy-done.7) | copy-start | bytes 835588
  100.9 6.7 %collective-permute-start.12 = (bf16[272,512]{1,0:T(8,128)(2,1)S(1)}, bf16[272,512]{1,0:T(8,128)(2,1)}, u32[]{:S(2)}, u32[]{:S(2)}) collective-permute-start(bf16[272,512]{1,0:T(8,128)(2,1)S(1)} %copy-done.8), channel_id=1, source_target_pairs={{0,4},{8,0},{16,8},{24,16},{28,24},{20,28},{12,20},{4,12},{1,5},{9... | collective-permute-start | bytes 835592 | tf_op jit(solution)/shard_map/ppermute | solution.py:211
  102.6 6.7 %copy-start.9 = (bf16[272,512]{1,0:T(8,128)(2,1)}, bf16[272,512]{1,0:T(8,128)(2,1)S(1)}, u32[]{:S(2)}) copy-start(bf16[272,512]{1,0:T(8,128)(2,1)S(1)} %collective-permute-done.14) | copy-start | bytes 835588
  102.6 6.7 %collective-permute-start.15 = (bf16[272,512]{1,0:T(8,128)(2,1)S(1)}, bf16[272,512]{1,0:T(8,128)(2,1)S(1)}, u32[]{:S(2)}, u32[]{:S(2)}) collective-permute-start(bf16[272,512]{1,0:T(8,128)(2,1)S(1)} %collective-permute-done.14), channel_id=1, source_target_pairs={{0,8},{8,16},{16,24},{24,28},{28,20},{20,12},{12,4},{4,0},{1,9},{9... | collective-permute-start | bytes 835592 | tf_op jit(solution)/shard_map/ppermute | solution.py:207
  104.3 36.4 %collective-permute-start.9 = (bf16[2,768,512]{2,1,0:T(8,128)(2,1)}, bf16[2,768,512]{2,1,0:T(8,128)(2,1)}, u32[]{:S(2)}, u32[]{:S(2)}) collective-permute-start(bf16[2,768,512]{2,1,0:T(8,128)(2,1)} %pad_maximum_fusion.5), channel_id=1, source_target_pairs={{0,1},{1,0},{2,3},{3,2},{4,5},{5,4},{6,7},{7,6},{8,9},{9,8},{10,11... | collective-permute-start | bytes 4718600 | tf_op jit(solution)/shard_map/ppermute | solution.py:189
  107.6 6.9 %collective-permute-start.13 = (bf16[272,512]{1,0:T(8,128)(2,1)}, bf16[272,512]{1,0:T(8,128)(2,1)}, u32[]{:S(2)}, u32[]{:S(2)}) collective-permute-start(bf16[272,512]{1,0:T(8,128)(2,1)} %collective-permute-done.12), channel_id=1, source_target_pairs={{0,4},{8,0},{16,8},{24,16},{28,24},{20,28},{12,20},{4,12},{1,5},{9... | collective-permute-start | bytes 835592 | tf_op jit(solution)/shard_map/ppermute | solution.py:211
  111.4 20.8 %collective-permute-start.22 = (bf16[768,512]{1,0:T(8,128)(2,1)}, bf16[768,512]{1,0:T(8,128)(2,1)}, u32[]{:S(2)}, u32[]{:S(2)}) collective-permute-start(bf16[768,512]{1,0:T(8,128)(2,1)} %bitcast.49), channel_id=1, source_target_pairs={{0,2},{1,3},{2,0},{3,1},{4,6},{5,7},{6,4},{7,5},{8,10},{9,11},{10,... | collective-permute-start | bytes 2359304 | tf_op jit(solution)/shard_map/ppermute | solution.py:188
  113.7 6.8 %collective-permute-start.16 = (bf16[272,512]{1,0:T(8,128)(2,1)}, bf16[272,512]{1,0:T(8,128)(2,1)S(1)}, u32[]{:S(2)}, u32[]{:S(2)}) collective-permute-start(bf16[272,512]{1,0:T(8,128)(2,1)} %copy-done.11), channel_id=1, source_target_pairs={{0,8},{8,16},{16,24},{24,28},{28,20},{20,12},{12,4},{4,0},{1,9},{9... | collective-permute-start | bytes 835592 | tf_op jit(solution)/shard_map/ppermute | solution.py:207
  121.5 19.0 %copy-start.5 = (bf16[2,256,512]{2,1,0:T(8,128)(2,1)}, bf16[2,256,512]{2,1,0:T(8,128)(2,1)S(1)}, u32[]{:S(2)}) copy-start(bf16[2,256,512]{2,1,0:T(8,128)(2,1)S(1)} %fusion.58) | copy-start | bytes 1572868
  121.5 17.9 %collective-permute-start.17 = (bf16[512,512]{1,0:T(8,128)(2,1)S(1)}, bf16[512,512]{1,0:T(8,128)(2,1)}, u32[]{:S(2)}, u32[]{:S(2)}) collective-permute-start(bf16[512,512]{1,0:T(8,128)(2,1)S(1)} %bitcast.160), channel_id=1, source_target_pairs={{0,2},{1,3},{2,0},{3,1},{4,6},{5,7},{6,4},{7,5},{8,10},{9,11},{10,... | collective-permute-start | bytes 1572872 | tf_op jit(solution)/shard_map/ppermute | solution.py:188
  133.8 20.7 %collective-permute-start.23 = (bf16[2,768,512]{2,1,0:T(8,128)(2,1)S(1)}, bf16[2,768,512]{2,1,0:T(8,128)(2,1)S(1)}, u32[]{:S(2)}, u32[]{:S(2)}) collective-permute-start(bf16[2,768,512]{2,1,0:T(8,128)(2,1)S(1)} %pad_maximum_fusion.7), channel_id=1, source_target_pairs={{0,1},{1,0},{2,3},{3,2},{4,5},{5,4},{6,7},{7,6},{8,9},{9,8},{10,11... | collective-permute-start | bytes 4718600 | tf_op jit(solution)/shard_map/ppermute | solution.py:189
  140.6 7.2 %collective-permute-start.18 = (bf16[2,512,512]{2,1,0:T(8,128)(2,1)S(1)}, bf16[2,512,512]{2,1,0:T(8,128)(2,1)S(1)}, u32[]{:S(2)}, u32[]{:S(2)}) collective-permute-start(bf16[2,512,512]{2,1,0:T(8,128)(2,1)S(1)} %pad_maximum_fusion.9), channel_id=1, source_target_pairs={{0,1},{1,0},{2,3},{3,2},{4,5},{5,4},{6,7},{7,6},{8,9},{9,8},{10,11... | collective-permute-start | bytes 3145736 | tf_op jit(solution)/shard_map/ppermute | solution.py:189
  152.6 14.8 %collective-permute-start.19 = (bf16[2,512,256]{1,2,0:T(8,128)(2,1)S(1)}, bf16[2,512,256]{1,2,0:T(8,128)(2,1)S(1)}, u32[]{:S(2)}, u32[]{:S(2)}) collective-permute-start(bf16[2,512,256]{1,2,0:T(8,128)(2,1)S(1)} %multiply_convert_fusion.2), channel_id=1, source_target_pairs={{0,2},{1,3},{2,0},{3,1},{4,6},{5,7},{6,4},{7,5},{8,10},{9,11},{10,... | collective-permute-start | bytes 1572872 | tf_op jit(solution)/shard_map/ppermute | solution.py:188
  159.9 24.3 %collective-permute-start.24 = (bf16[2,768,256]{1,2,0:T(8,128)(2,1)S(1)}, bf16[2,768,256]{1,2,0:T(8,128)(2,1)S(1)}, u32[]{:S(2)}, u32[]{:S(2)}) collective-permute-start(bf16[2,768,256]{1,2,0:T(8,128)(2,1)S(1)} %multiply_convert_fusion), channel_id=1, source_target_pairs={{0,2},{1,3},{2,0},{3,1},{4,6},{5,7},{6,4},{7,5},{8,10},{9,11},{10,... | collective-permute-start | bytes 2359304 | tf_op jit(solution)/shard_map/ppermute | solution.py:188
  167.5 33.4 %collective-permute-start.20 = (bf16[2,2,512,256]{2,3,1,0:T(8,128)(2,1)S(1)}, bf16[2,2,512,256]{2,3,1,0:T(8,128)(2,1)S(1)}, u32[]{:S(2)}, u32[]{:S(2)}) collective-permute-start(bf16[2,2,512,256]{2,3,1,0:T(8,128)(2,1)S(1)} %pad_maximum_fusion.10), channel_id=1, source_target_pairs={{0,1},{1,0},{2,3},{3,2},{4,5},{5,4},{6,7},{7,6},{8,9},{9,8},{10,11... | collective-permute-start | bytes 3145736 | tf_op jit(solution)/shard_map/ppermute | solution.py:189
  168.0 32.6 %collective-permute-start.10 = (bf16[2,768,256]{1,2,0:T(8,128)(2,1)S(1)}, bf16[2,768,256]{1,2,0:T(8,128)(2,1)S(1)}, u32[]{:S(2)}, u32[]{:S(2)}) collective-permute-start(bf16[2,768,256]{1,2,0:T(8,128)(2,1)S(1)} %multiply_convert_fusion.1), channel_id=1, source_target_pairs={{0,2},{1,3},{2,0},{3,1},{4,6},{5,7},{6,4},{7,5},{8,10},{9,11},{10,... | collective-permute-start | bytes 2359304 | tf_op jit(solution)/shard_map/ppermute | solution.py:188
  184.4 21.3 %collective-permute-start.25 = (bf16[2,2,768,256]{2,3,1,0:T(8,128)(2,1)S(1)}, bf16[2,2,768,256]{2,3,1,0:T(8,128)(2,1)S(1)}, u32[]{:S(2)}, u32[]{:S(2)}) collective-permute-start(bf16[2,2,768,256]{2,3,1,0:T(8,128)(2,1)S(1)} %pad_maximum_fusion.8), channel_id=1, source_target_pairs={{0,1},{1,0},{2,3},{3,2},{4,5},{5,4},{6,7},{7,6},{8,9},{9,8},{10,11... | collective-permute-start | bytes 4718600 | tf_op jit(solution)/shard_map/ppermute | solution.py:189
  200.8 12.4 %collective-permute-start.11 = (bf16[2,2,768,256]{2,3,1,0:T(8,128)(2,1)S(1)}, bf16[2,2,768,256]{2,3,1,0:T(8,128)(2,1)S(1)}, u32[]{:S(2)}, u32[]{:S(2)}) collective-permute-start(bf16[2,2,768,256]{2,3,1,0:T(8,128)(2,1)S(1)} %pad_maximum_fusion.6), channel_id=1, source_target_pairs={{0,1},{1,0},{2,3},{3,2},{4,5},{5,4},{6,7},{7,6},{8,9},{9,8},{10,11... | collective-permute-start | bytes 4718600 | tf_op jit(solution)/shard_map/ppermute | solution.py:189
  203.6 8.0 %collective-permute-start.28 = (bf16[256,512]{1,0:T(8,128)(2,1)S(1)}, bf16[256,512]{1,0:T(8,128)(2,1)S(1)}, u32[]{:S(2)}, u32[]{:S(2)}) collective-permute-start(bf16[256,512]{1,0:T(8,128)(2,1)S(1)} %get-tuple-element.62), channel_id=1, source_target_pairs={{0,4},{8,0},{16,8},{24,16},{28,24},{20,28},{12,20},{4,12},{1,5},{9... | collective-permute-start | bytes 786440 | tf_op jit(solution)/shard_map/ppermute | solution.py:231
  205.2 8.2 %collective-permute-start.21 = (bf16[256,512]{1,0:T(8,128)(2,1)S(1)}, bf16[256,512]{1,0:T(8,128)(2,1)S(1)}, u32[]{:S(2)}, u32[]{:S(2)}) collective-permute-start(bf16[256,512]{1,0:T(8,128)(2,1)S(1)} %get-tuple-element.61), channel_id=1, source_target_pairs={{0,8},{8,16},{16,24},{24,28},{28,20},{20,12},{12,4},{4,0},{1,9},{9... | collective-permute-start | bytes 786440 | tf_op jit(solution)/shard_map/ppermute | solution.py:231
  211.6 7.1 %collective-permute-start.29 = (bf16[256,512]{1,0:T(8,128)(2,1)S(1)}, bf16[256,512]{1,0:T(8,128)(2,1)S(1)}, u32[]{:S(2)}, u32[]{:S(2)}) collective-permute-start(bf16[256,512]{1,0:T(8,128)(2,1)S(1)} %add_convert_fusion.2), channel_id=1, source_target_pairs={{0,4},{8,0},{16,8},{24,16},{28,24},{20,28},{12,20},{4,12},{1,5},{9... | collective-permute-start | bytes 786440 | tf_op jit(solution)/shard_map/ppermute | solution.py:231
  218.8 6.6 %collective-permute-start.26 = (bf16[256,512]{1,0:T(8,128)(2,1)S(1)}, bf16[256,512]{1,0:T(8,128)(2,1)S(1)}, u32[]{:S(2)}, u32[]{:S(2)}) collective-permute-start(bf16[256,512]{1,0:T(8,128)(2,1)S(1)} %get-tuple-element.57), channel_id=1, source_target_pairs={{0,8},{8,16},{16,24},{24,28},{28,20},{20,12},{12,4},{4,0},{1,9},{9... | collective-permute-start | bytes 786440 | tf_op jit(solution)/shard_map/ppermute | solution.py:231
  219.4 6.4 %collective-permute-start.30 = (bf16[256,512]{1,0:T(8,128)(2,1)S(1)}, bf16[256,512]{1,0:T(8,128)(2,1)S(1)}, u32[]{:S(2)}, u32[]{:S(2)}) collective-permute-start(bf16[256,512]{1,0:T(8,128)(2,1)S(1)} %get-tuple-element.58), channel_id=1, source_target_pairs={{0,4},{8,0},{16,8},{24,16},{28,24},{20,28},{12,20},{4,12},{1,5},{9... | collective-permute-start | bytes 786440 | tf_op jit(solution)/shard_map/ppermute | solution.py:231
  222.7 11.4 %copy-start.19 = (f32[512]{0:T(512)S(1)}, f32[512]{0:T(512)}, u32[]{:S(2)}) copy-start(f32[512]{0:T(512)} %param.30) | copy-start | bytes 6148
  225.9 6.4 %collective-permute-start.27 = (bf16[256,512]{1,0:T(8,128)(2,1)S(1)}, bf16[256,512]{1,0:T(8,128)(2,1)S(1)}, u32[]{:S(2)}, u32[]{:S(2)}) collective-permute-start(bf16[256,512]{1,0:T(8,128)(2,1)S(1)} %get-tuple-element.55), channel_id=1, source_target_pairs={{0,8},{8,16},{16,24},{24,28},{28,20},{20,12},{12,4},{4,0},{1,9},{9... | collective-permute-start | bytes 786440 | tf_op jit(solution)/shard_map/ppermute | solution.py:231
  227.5 6.4 %collective-permute-start.31 = (bf16[256,512]{1,0:T(8,128)(2,1)S(1)}, bf16[256,512]{1,0:T(8,128)(2,1)S(1)}, u32[]{:S(2)}, u32[]{:S(2)}) collective-permute-start(bf16[256,512]{1,0:T(8,128)(2,1)S(1)} %get-tuple-element.56), channel_id=1, source_target_pairs={{0,4},{8,0},{16,8},{24,16},{28,24},{20,28},{12,20},{4,12},{1,5},{9... | collective-permute-start | bytes 786440 | tf_op jit(solution)/shard_map/ppermute | solution.py:231
  234.9 6.7 %collective-permute-start.32 = (bf16[256,512]{1,0:T(8,128)(2,1)S(1)}, bf16[256,512]{1,0:T(8,128)(2,1)S(1)}, u32[]{:S(2)}, u32[]{:S(2)}) collective-permute-start(bf16[256,512]{1,0:T(8,128)(2,1)S(1)} %get-tuple-element.59), channel_id=1, source_target_pairs={{0,1},{1,2},{2,3},{3,0},{4,5},{5,6},{6,7},{7,4},{8,9},{9,10},{10,1... | collective-permute-start | bytes 786440 | tf_op jit(solution)/shard_map/ppermute | solution.py:176
  234.9 8.7 %collective-permute-start.34 = (bf16[256,512]{1,0:T(8,128)(2,1)S(1)}, bf16[256,512]{1,0:T(8,128)(2,1)S(1)}, u32[]{:S(2)}, u32[]{:S(2)}) collective-permute-start(bf16[256,512]{1,0:T(8,128)(2,1)S(1)} %get-tuple-element.59), channel_id=1, source_target_pairs={{0,3},{1,0},{2,1},{3,2},{4,7},{5,4},{6,5},{7,6},{8,11},{9,8},{10,9... | collective-permute-start | bytes 786440 | tf_op jit(solution)/shard_map/ppermute | solution.py:176
  236.6 12.5 %collective-permute-start.33 = (bf16[256,512]{1,0:T(8,128)(2,1)S(1)}, bf16[256,512]{1,0:T(8,128)(2,1)S(1)}, u32[]{:S(2)}, u32[]{:S(2)}) collective-permute-start(bf16[256,512]{1,0:T(8,128)(2,1)S(1)} %get-tuple-element.59), channel_id=1, source_target_pairs={{0,2},{1,3},{2,0},{3,1},{4,6},{5,7},{6,4},{7,5},{8,10},{9,11},{10,... | collective-permute-start | bytes 786440 | tf_op jit(solution)/shard_map/ppermute | solution.py:176
  252.4 10.7 %copy-start.20 = (f32[512]{0:T(512)S(1)}, f32[512]{0:T(512)}, u32[]{:S(2)}) copy-start(f32[512]{0:T(512)} %param.33) | copy-start | bytes 6148
  252.4 10.8 %copy-start.21 = (f32[512]{0:T(512)S(1)}, f32[512]{0:T(512)}, u32[]{:S(2)}) copy-start(f32[512]{0:T(512)} %param.32) | copy-start | bytes 6148
  255.5 11.8 %copy-start.1 = (bf16[512,2048]{1,0:T(8,128)(2,1)S(1)}, bf16[512,2048]{1,0:T(8,128)(2,1)}, u32[]{:S(2)}) copy-start(bf16[512,2048]{1,0:T(8,128)(2,1)} %param.24) | copy-start | bytes 6291460
  (10 other events, 24.1 us)

commit v19 on v18

--- a/solution.py
+++ b/solution.py
@@ -128,8 +128,12 @@
         gate_local = lax.dynamic_slice_in_dim(gate_all, here * local_experts, local_experts, axis=1)
         gate_local = jnp.transpose(gate_local, (1, 0, 2)).reshape(local_experts, count * tokens)
         rows = pair_gather(rows_q)
+        if lax.axis_size("tp") == 4:
+            rows = jnp.take(rows, lax.axis_index("tp") ^ jnp.arange(4, dtype=jnp.int32), axis=0)
         if begin == 0:
-            rows, expert_gate_up, qkv_flat = lax.optimization_barrier((rows, expert_gate_up, qkv_flat))
+            rows, expert_gate_up = lax.optimization_barrier((rows, expert_gate_up))
+        if end == len(blocks):
+            rows, qkv_flat = lax.optimization_barrier((rows, qkv_flat))
         gate_up_split = expert_gate_up.reshape(local_experts, rows.shape[0], quarter, -1)
         projected = jnp.einsum("qtd,eqdf->etf", rows, gate_up_split, preferred_element_type=jnp.float32)
         activated = jax.nn.silu(projected[..., :hidden_quarter]) * projected[..., hidden_quarter:]
@@ -318,9 +322,6 @@
             order = (tp_here - jnp.arange(tp_count, dtype=jnp.int32)) % tp_count
         down_full = jnp.take(jnp.stack(pieces), order, axis=0)
         gate_up_flat = expert_gate_up.reshape(local_experts, tp_count, quarter_width, -1)
-        if tp_count == 4:
-            source_order = tp_here ^ jnp.arange(tp_count, dtype=jnp.int32)
-            gate_up_flat = jnp.take(gate_up_flat, source_order, axis=1)
         qkv_flat = qkv_proj.reshape(D, -1)
     local_width = new_queries.shape[1]
     local_heads = local_width // HEAD_DIM

time: 269 us -> 293 us (1.089)
  other arithmetic: 28.4 us -> 39.3 us
  Pallas kernels: 8.99 us -> 16.8 us
  local copies, waits for them, and re-layouts: 43.5 us -> 50.2 us
  waiting for transfers between devices: 113 us -> 108 us
  matrix products: 26.7 us -> 30.2 us
    ppermute x3, waiting for transfers between devices: 12.1 us -> 3.75 us  [body(): pieces.append(lax.ppermute(piece, 'tp', pairs))]
    pallas_call x1, Pallas kernels: 8.99 us -> 16.8 us  [flash_attention(): pl.pallas_call(kernel, grid_spec=grid_spec, out_shape=jax.ShapeDtypeStruc...]
    gather x1 -> x3, local copies, waits for them, and re-layouts: 5.13 us -> 10.9 us  [dense_experts(): jnp.take(rows, lax.axis_index('tp') ^ jnp.arange(4, dtype=jnp.int32), axi...]
    ppermute x3, waiting for transfers between devices: 4.83 us -> 10.5 us  [permute_gather_dot(): piece = lax.ppermute(rows, 'tp', pairs)]
    another operation x4 -> x6, other arithmetic: 2.14 us -> 7.22 us  [pair_gather(): return jnp.stack([block, near[0], far, near[1]])]
    ppermute x6, waiting for transfers between devices: 51.4 us -> 47 us  [pair_gather(): far = lax.ppermute(block, 'tp', [(i, i ^ 2) for i in range(4)])]
    ppermute x4, starting transfers between devices: 1.98 us -> 5.92 us  [ring_all_gather(): ahead = lax.ppermute(ahead, 'seq', forward)]
    ppermute x7, waiting for transfers between devices: 18.2 us -> 21.3 us  [ring_reduce_scatter(): lax.ppermute(acc.astype(jnp.bfloat16), 'seq', pairs).astype(jnp.float32)]
  transfers between devices with their start and end apart: 35 -> 35, of which waited for: 24 -> 20; matrix products, arithmetic and copies ran while one was open for 24% -> 29% of each run, Pallas kernels for 3% -> 6%
where the time goes in v19:
time: 293 us; the launch traced here: 291 us
  waiting for transfers between devices  108 us (37%)
  local copies, waits for them, and re-layouts  50.2 us (17%)
  other arithmetic  39.3 us (13%)
  starting transfers between devices  32.5 us (11%)
  matrix products  30.2 us (10%)
  Pallas kernels  16.8 us (6%)
  blocking collectives  13 us (4%)
    ppermute x6, waiting for transfers between devices, pair_gather(): far = lax.ppermute(block, 'tp', [(i, i ^ 2) for i in range(4)])  47 us
    ppermute x7, waiting for transfers between devices, ring_reduce_scatter(): lax.ppermute(acc.astype(jnp.bfloat16), 'seq', pairs).astype(jnp.float32)  21.3 us
    pallas_call x1, Pallas kernels, flash_attention(): pl.pallas_call(kernel, grid_spec=grid_spec, out_shape=jax.ShapeDtypeStruc...  16.8 us
    unnamed x63, local copies, waits for them, and re-layouts  16.5 us
    dot_general x3, matrix products, dense_experts(): jnp.einsum('qtd,eqdf->etf', rows, gate_up_split, preferred_element_type=j...  14.2 us
    gather x3, local copies, waits for them, and re-layouts, dense_experts(): jnp.take(rows, lax.axis_index('tp') ^ jnp.arange(4, dtype=jnp.int32), axi...  10.9 us
    ppermute x3, waiting for transfers between devices, permute_gather_dot(): piece = lax.ppermute(rows, 'tp', pairs)  10.5 us
    ppermute x3, waiting for transfers between devices, permute_reduce_scatter(): total = total + lax.ppermute(piece, 'tp', pairs).astype(jnp.float32)  10.4 us
  transfers between devices with their start and end apart: 35, of which 20 were waited for; matrix products, arithmetic and copies ran while one was open for 29% of the time, Pallas kernels for 6%

profile of v19, /device:TPU:0, one launch (start us, length us, event | category | flops | bytes accessed | tf_op | source)
XLA Modules:
  0.0 291.1 jit_solution(1397617868066296393)
XLA Ops:
  0.7 2.9 dynamic-slice_bitcast_fusion
  4.1 2.0 collective-permute-start.2
  6.0 2.3 collective-permute-start.1
  8.9 16.8 %shard_map.192 = bf16[256,512]{1,0:T(8,128)(2,1)} custom-call(s32[1]{0:T(128)} %dynamic_slice.55.len_ref, bf16[256,512]{1,0:T(8,128)(2,1)} %q_ref.1, bf16[4096,512]{1,0:T(8,128)(2,1)} %bitcast.157, bf16[4096,512]{1,0:T(8,128)(2,1)} %bitcast.158, bf16[256,512]{1,0:T(8,128)(2,1)} %nk_ref.1, bf16[256,512]{1,0:T(8,128)(2,1)} %nv_ref.1), custom_call_target="tpu_custom_call" | custom-call | tf_op jit(solution)/shard_map/pallas_call | solution.py:94
  26.3 3.7 %collective-permute-done.1 = bf16[2,256,512]{2,1,0:T(8,128)(2,1)} collective-permute-done((bf16[2,256,512]{2,1,0:T(8,128)(2,1)}, bf16[2,256,512]{2,1,0:T(8,128)(2,1)}, u32[]{:S(2)}, u32[]{:S(2)}) %collective-permute-start.1) | collective-permute-done | bytes 524320 | tf_op jit(solution)/shard_map/ppermute | solution.py:318
  30.0 2.8 pad_maximum_fusion.4
  32.8 3.6 %gather_fusion = bf16[4,2,256,512]{3,2,1,0:T(8,128)(2,1)} fusion(bf16[4,2,256,512]{3,2,1,0:T(8,128)(2,1)} %pad_maximum_fusion.4, s32[1024]{0:T(1024)S(1)} %pad_clamp_fusion.2), kind=kCustom, calls=%fused_computation.2 | custom fusion | bytes 4194320 | tf_op jit(solution)/shard_map/jit(_take)/gather | solution.py:323
  36.4 3.2 %broadcast_select_fusion.2 = bf16[4,2,256,512]{3,2,1,0:T(8,128)(2,1)} fusion(bf16[4,2,256,512]{3,2,1,0:T(8,128)(2,1)} %gather_fusion, pred[4]{0:T(512)(128)(4,1)S(1)} %get-tuple-element.78), kind=kLoop, calls=%fused_computation.30 | loop fusion | flops 1048576 | bytes 4194308 | tf_op jit(solution)/shard_map/jit(_take)/select_n | solution.py:323
  41.9 2.1 collective-permute-start.5
  43.9 2.0 collective-permute-start.4
  45.9 2.4 collective-permute-done.3
  48.3 2.3 collective-permute-done.5
  50.6 5.7 %collective-permute-done.4 = bf16[256,512]{1,0:T(8,128)(2,1)S(1)} collective-permute-done((bf16[256,512]{1,0:T(8,128)(2,1)S(1)}, bf16[256,512]{1,0:T(8,128)(2,1)S(1)}, u32[]{:S(2)}, u32[]{:S(2)}) %collective-permute-start.4) | collective-permute-done | bytes 262176 | tf_op jit(solution)/shard_map/ppermute | solution.py:164
  57.6 7.1 %psum.28 = f32[256]{0:T(256)S(1)} all-reduce(f32[256]{0:T(256)S(1)} %get-tuple-element.32), channel_id=1, replica_groups=mesh['seq'=8,'tp'=4] {'tp'}, use_global_device_ids=true, to_apply=%region_1.2 | all-reduce | flops 256 | bytes 2048 | tf_op jit(solution)/shard_map/psum | solution.py:351
  67.0 5.5 %collective-permute-done.6 = bf16[272,512]{1,0:T(8,128)(2,1)} collective-permute-done((bf16[272,512]{1,0:T(8,128)(2,1)S(1)}, bf16[272,512]{1,0:T(8,128)(2,1)}, u32[]{:S(2)}, u32[]{:S(2)}) %collective-permute-start.6) | collective-permute-done | bytes 278560 | tf_op jit(solution)/shard_map/ppermute | solution.py:211
  79.4 7.6 %reshape.164 = bf16[2,4,512,512]{3,2,1,0:T(8,128)(2,1)} reshape(bf16[2,2048,2,256]{3,2,1,0:T(2,128)(2,1)} %param.30) | data formatting | bytes 8388608 | tf_op jit(solution)/shard_map/reshape | solution.py:324
  87.0 8.9 %copy.65 = bf16[2048,3,512]{0,2,1:T(8,128)(2,1)} copy(bf16[2048,3,512]{2,0,1:T(8,128)(2,1)} %param.33) | data formatting | bytes 12582912 | tf_op args[14]
  100.8 3.1 %collective-permute-done.12 = bf16[272,512]{1,0:T(8,128)(2,1)} collective-permute-done((bf16[272,512]{1,0:T(8,128)(2,1)S(1)}, bf16[272,512]{1,0:T(8,128)(2,1)}, u32[]{:S(2)}, u32[]{:S(2)}) %collective-permute-start.12) | collective-permute-done | bytes 278560 | tf_op jit(solution)/shard_map/ppermute | solution.py:215
  108.6 2.2 collective-permute-done.13
  110.8 2.9 collective-permute-done.16
  117.1 9.8 %collective-permute-done.22 = bf16[768,512]{1,0:T(8,128)(2,1)S(1)} collective-permute-done((bf16[768,512]{1,0:T(8,128)(2,1)S(1)}, bf16[768,512]{1,0:T(8,128)(2,1)S(1)}, u32[]{:S(2)}, u32[]{:S(2)}) %collective-permute-start.22) | collective-permute-done | bytes 786464 | tf_op jit(solution)/shard_map/ppermute | solution.py:192
  128.4 6.0 %collective-permute-done.17 = bf16[512,512]{1,0:T(8,128)(2,1)} collective-permute-done((bf16[512,512]{1,0:T(8,128)(2,1)S(1)}, bf16[512,512]{1,0:T(8,128)(2,1)}, u32[]{:S(2)}, u32[]{:S(2)}) %collective-permute-start.17) | collective-permute-done | bytes 524320 | tf_op jit(solution)/shard_map/ppermute | solution.py:192
  134.4 2.1 pad_maximum_fusion.11
  138.1 1.9 pad_maximum_fusion
  140.1 4.4 %gather_fusion.2 = bf16[4,768,512]{2,1,0:T(8,128)(2,1)} fusion(bf16[4,768,512]{2,1,0:T(8,128)(2,1)} %pad_maximum_fusion, s32[1024]{0:T(1024)} %pad_clamp_fusion.1), kind=kCustom, calls=%fused_computation.clone | custom fusion | bytes 6291472 | tf_op jit(solution)/shard_map/jit(_take)/gather | solution.py:132
  144.5 2.4 broadcast_select_fusion
  147.6 5.2 %fusion.15 = f32[2,768,512]{1,2,0:T(8,128)} fusion(bf16[2,4,512,512]{3,2,1,0:T(8,128)(2,1)S(1)} %copy-done.6, bf16[4,768,512]{2,1,0:T(8,128)(2,1)S(1)} %broadcast_select_fusion), kind=kOutput, calls=%fused_computation.31 | convolution fusion | flops 3221225472 | bytes 10485760 | tf_op jit(solution)/shard_map/qtd,eqdf->etf/dot_general | solution.py:138
  155.5 2.1 gather_fusion.1
  157.6 2.0 broadcast_select_fusion.1
  160.4 2.4 fusion.21
  169.0 4.4 %gather_fusion.3 = bf16[4,768,512]{2,1,0:T(8,128)(2,1)} fusion(bf16[4,768,512]{2,1,0:T(8,128)(2,1)} %pad_maximum_fusion.2, s32[1024]{0:T(1024)} %pad_clamp_fusion.1), kind=kCustom, calls=%fused_computation.1.clone | custom fusion | bytes 6291472 | tf_op jit(solution)/shard_map/jit(_take)/gather | solution.py:132
  173.4 6.6 %fusion.18 = f32[2,768,512]{1,2,0:T(8,128)S(1)} fusion(bf16[2,4,512,512]{3,2,1,0:T(8,128)(2,1)} %reshape.164, bf16[4,768,512]{2,1,0:T(8,128)(2,1)} %gather_fusion.3, pred[4]{0:T(512)(128)(4,1)S(1)} %copy-done.26), kind=kOutput, calls=%fused_computation.32 | convolution fusion | flops 3222798336 | bytes 10485764 | tf_op jit(solution)/shard_map/qtd,eqdf->etf/dot_general | solution.py:138
  185.1 15.9 %collective-permute-done.24 = bf16[2,768,256]{1,2,0:T(8,128)(2,1)S(1)} collective-permute-done((bf16[2,768,256]{1,2,0:T(8,128)(2,1)S(1)}, bf16[2,768,256]{1,2,0:T(8,128)(2,1)S(1)}, u32[]{:S(2)}, u32[]{:S(2)}) %collective-permute-start.24) | collective-permute-done | bytes 786464 | tf_op jit(solution)/shard_map/ppermute | solution.py:192
  201.7 15.3 %collective-permute-done.10 = bf16[2,768,256]{1,2,0:T(8,128)(2,1)S(1)} collective-permute-done((bf16[2,768,256]{1,2,0:T(8,128)(2,1)S(1)}, bf16[2,768,256]{1,2,0:T(8,128)(2,1)S(1)}, u32[]{:S(2)}, u32[]{:S(2)}) %collective-permute-start.10) | collective-permute-done | bytes 786464 | tf_op jit(solution)/shard_map/ppermute | solution.py:192
  218.6 2.3 fusion.49
  225.0 4.9 %collective-permute-done.28 = bf16[256,512]{1,0:T(8,128)(2,1)S(1)} collective-permute-done((bf16[256,512]{1,0:T(8,128)(2,1)S(1)}, bf16[256,512]{1,0:T(8,128)(2,1)S(1)}, u32[]{:S(2)}, u32[]{:S(2)}) %collective-permute-start.28) | collective-permute-done | bytes 262176 | tf_op jit(solution)/shard_map/ppermute | solution.py:235
  230.6 5.8 %collective-permute-done.29 = bf16[256,512]{1,0:T(8,128)(2,1)S(1)} collective-permute-done((bf16[256,512]{1,0:T(8,128)(2,1)S(1)}, bf16[256,512]{1,0:T(8,128)(2,1)S(1)}, u32[]{:S(2)}, u32[]{:S(2)}) %collective-permute-start.29) | collective-permute-done | bytes 262176 | tf_op jit(solution)/shard_map/ppermute | solution.py:235
  240.4 2.5 collective-permute-done.26
  244.8 2.7 collective-permute-start.27
  247.5 3.9 %collective-permute-done.27 = bf16[256,512]{1,0:T(8,128)(2,1)S(1)} collective-permute-done((bf16[256,512]{1,0:T(8,128)(2,1)S(1)}, bf16[256,512]{1,0:T(8,128)(2,1)S(1)}, u32[]{:S(2)}, u32[]{:S(2)}) %collective-permute-start.27) | collective-permute-done | bytes 262176 | tf_op jit(solution)/shard_map/ppermute | solution.py:235
  251.4 2.5 collective-permute-done.31
  256.6 2.0 fusion.34
  258.6 10.5 %collective-permute-done.32 = bf16[256,512]{1,0:T(8,128)(2,1)S(1)} collective-permute-done((bf16[256,512]{1,0:T(8,128)(2,1)S(1)}, bf16[256,512]{1,0:T(8,128)(2,1)S(1)}, u32[]{:S(2)}, u32[]{:S(2)}) %collective-permute-start.32) | collective-permute-done | bytes 262176 | tf_op jit(solution)/shard_map/ppermute | solution.py:180
  269.1 2.0 convolution_add_fusion.1
  271.2 2.0 fusion.30
  273.2 3.3 %fusion.10 = f32[256,1536]{1,0:T(8,128)} fusion(f32[256,1536]{1,0:T(8,128)S(1)} %fusion.30, f32[256,1536]{1,0:T(8,128)S(1)} %convolution_add_fusion.1, bf16[256,512]{1,0:T(8,128)(2,1)S(1)} %collective-permute-done.33, bf16[2048,1536]{0,1:T(8,128)(2,1)} %bitcast.145, s32[]{:T(128)S(6)} %select_n.150), kind=kOutput, calls=%fused_computation.20 | convolution fusion | flops 403439616 | bytes 6553604 | tf_op jit(solution)/shard_map/dot_general | solution.py:181
  276.5 3.1 %copy.76 = f32[256,1536]{0,1:T(8,128)} copy(f32[256,1536]{1,0:T(8,128)} %fusion.10) | data formatting | bytes 3145728 | tf_op jit(solution)/shard_map/add | solution.py:181
  281.1 5.9 %all-reduce = (f32[256]{0:T(256)S(1)}, f32[256]{0:T(256)S(1)}, f32[256]{0:T(256)S(1)}) all-reduce(f32[256]{0:T(256)S(1)} %get-tuple-element.26, f32[256]{0:T(256)S(1)} %get-tuple-element.30, f32[256]{0:T(256)S(1)} %get-tuple-element.25), channel_id=1, replica_groups=mesh['seq'=8,'tp'=4] {'tp'}, use_global_device_ids=true, to_apply=%region_6.8 | all-reduce | flops 768 | bytes 6144 | tf_op jit(solution)/shard_map/psum | solution.py:377
  (171 shorter events, 66.8 us)
Async XLA Ops:
  0.6 39.0 %copy-start = (bf16[512,2048]{1,0:T(8,128)(2,1)S(1)}, bf16[512,2048]{1,0:T(8,128)(2,1)}, u32[]{:S(2)}) copy-start(bf16[512,2048]{1,0:T(8,128)(2,1)} %param.26) | copy-start | bytes 6291460
  0.7 7.6 %copy-start.27 = (s32[8]{0:T(128)S(1)}, s32[8]{0:T(128)}, u32[]{:S(2)}) copy-start(s32[8]{0:T(128)} %param.25) | copy-start | bytes 100
  3.6 22.7 %collective-permute-start = (bf16[2,256,512]{2,1,0:T(8,128)(2,1)}, bf16[2,256,512]{2,1,0:T(8,128)(2,1)S(1)}, u32[]{:S(2)}, u32[]{:S(2)}) collective-permute-start(bf16[2,256,512]{2,1,0:T(8,128)(2,1)} %get-tuple-element.40), channel_id=1, source_target_pairs={{0,1},{1,2},{2,3},{3,0},{4,5},{5,6},{6,7},{7,4},{8,9},{9,10},{10,1... | collective-permute-start | bytes 1572872 | tf_op jit(solution)/shard_map/ppermute | solution.py:318
  4.1 22.2 %collective-permute-start.2 = (bf16[2,256,512]{2,1,0:T(8,128)(2,1)}, bf16[2,256,512]{2,1,0:T(8,128)(2,1)}, u32[]{:S(2)}, u32[]{:S(2)}) collective-permute-start(bf16[2,256,512]{2,1,0:T(8,128)(2,1)} %get-tuple-element.41), channel_id=1, source_target_pairs={{0,3},{1,0},{2,1},{3,2},{4,7},{5,4},{6,5},{7,6},{8,11},{9,8},{10,9... | collective-permute-start | bytes 1572872 | tf_op jit(solution)/shard_map/ppermute | solution.py:318
  6.0 24.0 %collective-permute-start.1 = (bf16[2,256,512]{2,1,0:T(8,128)(2,1)}, bf16[2,256,512]{2,1,0:T(8,128)(2,1)}, u32[]{:S(2)}, u32[]{:S(2)}) collective-permute-start(bf16[2,256,512]{2,1,0:T(8,128)(2,1)} %get-tuple-element.42), channel_id=1, source_target_pairs={{0,2},{1,3},{2,0},{3,1},{4,6},{5,7},{6,4},{7,5},{8,10},{9,11},{10,... | collective-permute-start | bytes 1572872 | tf_op jit(solution)/shard_map/ppermute | solution.py:318
  8.9 17.3 %copy-start.20 = (f32[256,8]{0,1:T(8,128)S(1)}, f32[256,8]{0,1:T(8,128)}, u32[]{:S(2)}) copy-start(f32[256,8]{0,1:T(8,128)} %param.29) | copy-start | bytes 24580
  8.9 17.3 %copy-start.21 = (s32[256,8]{0,1:T(8,128)S(1)}, s32[256,8]{0,1:T(8,128)}, u32[]{:S(2)}) copy-start(s32[256,8]{0,1:T(8,128)} %param.28) | copy-start | bytes 24580
  39.6 16.7 %copy-start.19 = (bf16[256,512]{1,0:T(8,128)(2,1)S(1)}, bf16[256,512]{1,0:T(8,128)(2,1)}, u32[]{:S(2)}) copy-start(bf16[256,512]{1,0:T(8,128)(2,1)} %param.19) | copy-start | bytes 786436
  41.7 23.0 %copy-start.22 = (f32[512]{0:T(512)S(1)}, f32[512]{0:T(512)}, u32[]{:S(2)}) copy-start(f32[512]{0:T(512)} %param.27) | copy-start | bytes 6148
  41.8 6.5 %collective-permute-start.3 = (bf16[256,512]{1,0:T(8,128)(2,1)S(1)}, bf16[256,512]{1,0:T(8,128)(2,1)S(1)}, u32[]{:S(2)}, u32[]{:S(2)}) collective-permute-start(bf16[256,512]{1,0:T(8,128)(2,1)S(1)} %get-tuple-element.36), channel_id=1, source_target_pairs={{0,1},{1,2},{2,3},{3,0},{4,5},{5,6},{6,7},{7,4},{8,9},{9,10},{10,1... | collective-permute-start | bytes 786440 | tf_op jit(solution)/shard_map/ppermute | solution.py:164
  41.9 8.8 %collective-permute-start.5 = (bf16[256,512]{1,0:T(8,128)(2,1)S(1)}, bf16[256,512]{1,0:T(8,128)(2,1)S(1)}, u32[]{:S(2)}, u32[]{:S(2)}) collective-permute-start(bf16[256,512]{1,0:T(8,128)(2,1)S(1)} %get-tuple-element.37), channel_id=1, source_target_pairs={{0,3},{1,0},{2,1},{3,2},{4,7},{5,4},{6,5},{7,6},{8,11},{9,8},{10,9... | collective-permute-start | bytes 786440 | tf_op jit(solution)/shard_map/ppermute | solution.py:164
  43.9 12.4 %collective-permute-start.4 = (bf16[256,512]{1,0:T(8,128)(2,1)S(1)}, bf16[256,512]{1,0:T(8,128)(2,1)S(1)}, u32[]{:S(2)}, u32[]{:S(2)}) collective-permute-start(bf16[256,512]{1,0:T(8,128)(2,1)S(1)} %get-tuple-element.38), channel_id=1, source_target_pairs={{0,2},{1,3},{2,0},{3,1},{4,6},{5,7},{6,4},{7,5},{8,10},{9,11},{10,... | collective-permute-start | bytes 786440 | tf_op jit(solution)/shard_map/ppermute | solution.py:164
  64.9 7.6 %collective-permute-start.6 = (bf16[272,512]{1,0:T(8,128)(2,1)S(1)}, bf16[272,512]{1,0:T(8,128)(2,1)}, u32[]{:S(2)}, u32[]{:S(2)}) collective-permute-start(bf16[272,512]{1,0:T(8,128)(2,1)S(1)} %get-tuple-element.67), channel_id=1, source_target_pairs={{0,8},{8,16},{16,24},{24,28},{28,20},{20,12},{12,4},{4,0},{1,9},{9... | collective-permute-start | bytes 835592 | tf_op jit(solution)/shard_map/ppermute | solution.py:211
  66.1 7.7 %collective-permute-start.7 = (bf16[272,512]{1,0:T(8,128)(2,1)S(1)}, bf16[272,512]{1,0:T(8,128)(2,1)S(1)}, u32[]{:S(2)}, u32[]{:S(2)}) collective-permute-start(bf16[272,512]{1,0:T(8,128)(2,1)S(1)} %get-tuple-element.67), channel_id=1, source_target_pairs={{0,4},{8,0},{16,8},{24,16},{28,24},{20,28},{12,20},{4,12},{1,5},{9... | collective-permute-start | bytes 835592 | tf_op jit(solution)/shard_map/ppermute | solution.py:215
  75.6 23.7 %collective-permute-start.8 = (bf16[768,512]{1,0:T(8,128)(2,1)S(1)}, bf16[768,512]{1,0:T(8,128)(2,1)S(1)}, u32[]{:S(2)}, u32[]{:S(2)}) collective-permute-start(bf16[768,512]{1,0:T(8,128)(2,1)S(1)} %bitcast.148), channel_id=1, source_target_pairs={{0,2},{1,3},{2,0},{3,1},{4,6},{5,7},{6,4},{7,5},{8,10},{9,11},{10,... | collective-permute-start | bytes 2359304 | tf_op jit(solution)/shard_map/ppermute | solution.py:192
  77.8 19.9 %collective-permute-start.14 = (bf16[272,512]{1,0:T(8,128)(2,1)}, bf16[272,512]{1,0:T(8,128)(2,1)S(1)}, u32[]{:S(2)}, u32[]{:S(2)}) collective-permute-start(bf16[272,512]{1,0:T(8,128)(2,1)} %collective-permute-done.6), channel_id=1, source_target_pairs={{0,8},{8,16},{16,24},{24,28},{28,20},{20,12},{12,4},{4,0},{1,9},{9... | collective-permute-start | bytes 835592 | tf_op jit(solution)/shard_map/ppermute | solution.py:211
  87.0 9.5 %copy-start.15 = (bf16[272,512]{1,0:T(8,128)(2,1)S(1)}, bf16[272,512]{1,0:T(8,128)(2,1)}, u32[]{:S(2)}) copy-start(bf16[272,512]{1,0:T(8,128)(2,1)} %copy-done.14) | copy-start | bytes 835588
  97.2 6.7 %collective-permute-start.12 = (bf16[272,512]{1,0:T(8,128)(2,1)S(1)}, bf16[272,512]{1,0:T(8,128)(2,1)}, u32[]{:S(2)}, u32[]{:S(2)}) collective-permute-start(bf16[272,512]{1,0:T(8,128)(2,1)S(1)} %copy-done.15), channel_id=1, source_target_pairs={{0,4},{8,0},{16,8},{24,16},{28,24},{20,28},{12,20},{4,12},{1,5},{9... | collective-permute-start | bytes 835592 | tf_op jit(solution)/shard_map/ppermute | solution.py:215
  97.7 6.7 %collective-permute-start.15 = (bf16[272,512]{1,0:T(8,128)(2,1)S(1)}, bf16[272,512]{1,0:T(8,128)(2,1)S(1)}, u32[]{:S(2)}, u32[]{:S(2)}) collective-permute-start(bf16[272,512]{1,0:T(8,128)(2,1)S(1)} %collective-permute-done.14), channel_id=1, source_target_pairs={{0,8},{8,16},{16,24},{24,28},{28,20},{20,12},{12,4},{4,0},{1,9},{9... | collective-permute-start | bytes 835592 | tf_op jit(solution)/shard_map/ppermute | solution.py:211
  100.8 35.8 %collective-permute-start.9 = (bf16[2,768,512]{2,1,0:T(8,128)(2,1)}, bf16[2,768,512]{2,1,0:T(8,128)(2,1)}, u32[]{:S(2)}, u32[]{:S(2)}) collective-permute-start(bf16[2,768,512]{2,1,0:T(8,128)(2,1)} %pad_maximum_fusion.7), channel_id=1, source_target_pairs={{0,1},{1,0},{2,3},{3,2},{4,5},{5,4},{6,7},{7,6},{8,9},{9,8},{10,11... | collective-permute-start | bytes 4718600 | tf_op jit(solution)/shard_map/ppermute | solution.py:193
  103.9 6.9 %collective-permute-start.13 = (bf16[272,512]{1,0:T(8,128)(2,1)}, bf16[272,512]{1,0:T(8,128)(2,1)}, u32[]{:S(2)}, u32[]{:S(2)}) collective-permute-start(bf16[272,512]{1,0:T(8,128)(2,1)} %collective-permute-done.12), channel_id=1, source_target_pairs={{0,4},{8,0},{16,8},{24,16},{28,24},{20,28},{12,20},{4,12},{1,5},{9... | collective-permute-start | bytes 835592 | tf_op jit(solution)/shard_map/ppermute | solution.py:215
  106.4 20.5 %collective-permute-start.22 = (bf16[768,512]{1,0:T(8,128)(2,1)S(1)}, bf16[768,512]{1,0:T(8,128)(2,1)S(1)}, u32[]{:S(2)}, u32[]{:S(2)}) collective-permute-start(bf16[768,512]{1,0:T(8,128)(2,1)S(1)} %bitcast.151), channel_id=1, source_target_pairs={{0,2},{1,3},{2,0},{3,1},{4,6},{5,7},{6,4},{7,5},{8,10},{9,11},{10,... | collective-permute-start | bytes 2359304 | tf_op jit(solution)/shard_map/ppermute | solution.py:192
  106.9 6.8 %collective-permute-start.16 = (bf16[272,512]{1,0:T(8,128)(2,1)}, bf16[272,512]{1,0:T(8,128)(2,1)S(1)}, u32[]{:S(2)}, u32[]{:S(2)}) collective-permute-start(bf16[272,512]{1,0:T(8,128)(2,1)} %copy-done.17), channel_id=1, source_target_pairs={{0,8},{8,16},{16,24},{24,28},{28,20},{20,12},{12,4},{4,0},{1,9},{9... | collective-permute-start | bytes 835592 | tf_op jit(solution)/shard_map/ppermute | solution.py:211
  114.7 21.8 %copy-start.4 = (bf16[2,256,512]{2,1,0:T(8,128)(2,1)}, bf16[2,256,512]{2,1,0:T(8,128)(2,1)S(1)}, u32[]{:S(2)}) copy-start(bf16[2,256,512]{2,1,0:T(8,128)(2,1)S(1)} %fusion.55) | copy-start | bytes 1572868
  114.7 19.7 %collective-permute-start.17 = (bf16[512,512]{1,0:T(8,128)(2,1)S(1)}, bf16[512,512]{1,0:T(8,128)(2,1)}, u32[]{:S(2)}, u32[]{:S(2)}) collective-permute-start(bf16[512,512]{1,0:T(8,128)(2,1)S(1)} %bitcast.154), channel_id=1, source_target_pairs={{0,2},{1,3},{2,0},{3,1},{4,6},{5,7},{6,4},{7,5},{8,10},{9,11},{10,... | collective-permute-start | bytes 1572872 | tf_op jit(solution)/shard_map/ppermute | solution.py:192
  126.9 7.4 %copy-start.10 = (bf16[768,512]{1,0:T(8,128)(2,1)}, bf16[768,512]{1,0:T(8,128)(2,1)S(1)}, u32[]{:S(2)}) copy-start(bf16[768,512]{1,0:T(8,128)(2,1)S(1)} %collective-permute-done.22) | copy-start | bytes 2359300
  128.4 37.1 %collective-permute-start.23 = (bf16[2,768,512]{2,1,0:T(8,128)(2,1)}, bf16[2,768,512]{2,1,0:T(8,128)(2,1)}, u32[]{:S(2)}, u32[]{:S(2)}) collective-permute-start(bf16[2,768,512]{2,1,0:T(8,128)(2,1)} %pad_maximum_fusion.9), channel_id=1, source_target_pairs={{0,1},{1,0},{2,3},{3,2},{4,5},{5,4},{6,7},{7,6},{8,9},{9,8},{10,11... | collective-permute-start | bytes 4718600 | tf_op jit(solution)/shard_map/ppermute | solution.py:193
  136.5 16.3 %collective-permute-start.18 = (bf16[2,512,512]{2,1,0:T(8,128)(2,1)}, bf16[2,512,512]{2,1,0:T(8,128)(2,1)}, u32[]{:S(2)}, u32[]{:S(2)}) collective-permute-start(bf16[2,512,512]{2,1,0:T(8,128)(2,1)} %pad_maximum_fusion.11), channel_id=1, source_target_pairs={{0,1},{1,0},{2,3},{3,2},{4,5},{5,4},{6,7},{7,6},{8,9},{9,8},{10,11... | collective-permute-start | bytes 3145736 | tf_op jit(solution)/shard_map/ppermute | solution.py:193
  163.9 18.2 %collective-permute-start.19 = (bf16[2,512,256]{1,2,0:T(8,128)(2,1)}, bf16[2,512,256]{1,2,0:T(8,128)(2,1)}, u32[]{:S(2)}, u32[]{:S(2)}) collective-permute-start(bf16[2,512,256]{1,2,0:T(8,128)(2,1)} %multiply_convert_fusion.2), channel_id=1, source_target_pairs={{0,2},{1,3},{2,0},{3,1},{4,6},{5,7},{6,4},{7,5},{8,10},{9,11},{10,... | collective-permute-start | bytes 1572872 | tf_op jit(solution)/shard_map/ppermute | solution.py:192
  180.5 20.5 %collective-permute-start.24 = (bf16[2,768,256]{1,2,0:T(8,128)(2,1)S(1)}, bf16[2,768,256]{1,2,0:T(8,128)(2,1)S(1)}, u32[]{:S(2)}, u32[]{:S(2)}) collective-permute-start(bf16[2,768,256]{1,2,0:T(8,128)(2,1)S(1)} %multiply_convert_fusion), channel_id=1, source_target_pairs={{0,2},{1,3},{2,0},{3,1},{4,6},{5,7},{6,4},{7,5},{8,10},{9,11},{10,... | collective-permute-start | bytes 2359304 | tf_op jit(solution)/shard_map/ppermute | solution.py:192
  183.3 34.0 %collective-permute-start.20 = (bf16[2,2,512,256]{2,3,1,0:T(8,128)(2,1)S(1)}, bf16[2,2,512,256]{2,3,1,0:T(8,128)(2,1)S(1)}, u32[]{:S(2)}, u32[]{:S(2)}) collective-permute-start(bf16[2,2,512,256]{2,3,1,0:T(8,128)(2,1)S(1)} %pad_maximum_fusion.12), channel_id=1, source_target_pairs={{0,1},{1,0},{2,3},{3,2},{4,5},{5,4},{6,7},{7,6},{8,9},{9,8},{10,11... | collective-permute-start | bytes 3145736 | tf_op jit(solution)/shard_map/ppermute | solution.py:193
  183.9 33.2 %collective-permute-start.10 = (bf16[2,768,256]{1,2,0:T(8,128)(2,1)S(1)}, bf16[2,768,256]{1,2,0:T(8,128)(2,1)S(1)}, u32[]{:S(2)}, u32[]{:S(2)}) collective-permute-start(bf16[2,768,256]{1,2,0:T(8,128)(2,1)S(1)} %multiply_convert_fusion.1), channel_id=1, source_target_pairs={{0,2},{1,3},{2,0},{3,1},{4,6},{5,7},{6,4},{7,5},{8,10},{9,11},{10,... | collective-permute-start | bytes 2359304 | tf_op jit(solution)/shard_map/ppermute | solution.py:192
  201.1 22.0 %collective-permute-start.25 = (bf16[2,2,768,256]{2,3,1,0:T(8,128)(2,1)S(1)}, bf16[2,2,768,256]{2,3,1,0:T(8,128)(2,1)S(1)}, u32[]{:S(2)}, u32[]{:S(2)}) collective-permute-start(bf16[2,2,768,256]{2,3,1,0:T(8,128)(2,1)S(1)} %pad_maximum_fusion.10), channel_id=1, source_target_pairs={{0,1},{1,0},{2,3},{3,2},{4,5},{5,4},{6,7},{7,6},{8,9},{9,8},{10,11... | collective-permute-start | bytes 4718600 | tf_op jit(solution)/shard_map/ppermute | solution.py:193
  217.2 13.3 %collective-permute-start.11 = (bf16[2,2,768,256]{2,3,1,0:T(8,128)(2,1)S(1)}, bf16[2,2,768,256]{2,3,1,0:T(8,128)(2,1)S(1)}, u32[]{:S(2)}, u32[]{:S(2)}) collective-permute-start(bf16[2,2,768,256]{2,3,1,0:T(8,128)(2,1)S(1)} %pad_maximum_fusion.8), channel_id=1, source_target_pairs={{0,1},{1,0},{2,3},{3,2},{4,5},{5,4},{6,7},{7,6},{8,9},{9,8},{10,11... | collective-permute-start | bytes 4718600 | tf_op jit(solution)/shard_map/ppermute | solution.py:193
  221.0 9.6 %collective-permute-start.21 = (bf16[256,512]{1,0:T(8,128)(2,1)S(1)}, bf16[256,512]{1,0:T(8,128)(2,1)S(1)}, u32[]{:S(2)}, u32[]{:S(2)}) collective-permute-start(bf16[256,512]{1,0:T(8,128)(2,1)S(1)} %get-tuple-element.64), channel_id=1, source_target_pairs={{0,8},{8,16},{16,24},{24,28},{28,20},{20,12},{12,4},{4,0},{1,9},{9... | collective-permute-start | bytes 786440 | tf_op jit(solution)/shard_map/ppermute | solution.py:235
  222.6 7.3 %collective-permute-start.28 = (bf16[256,512]{1,0:T(8,128)(2,1)S(1)}, bf16[256,512]{1,0:T(8,128)(2,1)S(1)}, u32[]{:S(2)}, u32[]{:S(2)}) collective-permute-start(bf16[256,512]{1,0:T(8,128)(2,1)S(1)} %get-tuple-element.65), channel_id=1, source_target_pairs={{0,4},{8,0},{16,8},{24,16},{28,24},{20,28},{12,20},{4,12},{1,5},{9... | collective-permute-start | bytes 786440 | tf_op jit(solution)/shard_map/ppermute | solution.py:235
  230.0 6.4 %collective-permute-start.29 = (bf16[256,512]{1,0:T(8,128)(2,1)S(1)}, bf16[256,512]{1,0:T(8,128)(2,1)S(1)}, u32[]{:S(2)}, u32[]{:S(2)}) collective-permute-start(bf16[256,512]{1,0:T(8,128)(2,1)S(1)} %add_convert_fusion.2), channel_id=1, source_target_pairs={{0,4},{8,0},{16,8},{24,16},{28,24},{20,28},{12,20},{4,12},{1,5},{9... | collective-permute-start | bytes 786440 | tf_op jit(solution)/shard_map/ppermute | solution.py:235
  236.5 6.4 %collective-permute-start.26 = (bf16[256,512]{1,0:T(8,128)(2,1)S(1)}, bf16[256,512]{1,0:T(8,128)(2,1)S(1)}, u32[]{:S(2)}, u32[]{:S(2)}) collective-permute-start(bf16[256,512]{1,0:T(8,128)(2,1)S(1)} %get-tuple-element.60), channel_id=1, source_target_pairs={{0,8},{8,16},{16,24},{24,28},{28,20},{20,12},{12,4},{4,0},{1,9},{9... | collective-permute-start | bytes 786440 | tf_op jit(solution)/shard_map/ppermute | solution.py:235
  238.2 6.5 %collective-permute-start.30 = (bf16[256,512]{1,0:T(8,128)(2,1)S(1)}, bf16[256,512]{1,0:T(8,128)(2,1)S(1)}, u32[]{:S(2)}, u32[]{:S(2)}) collective-permute-start(bf16[256,512]{1,0:T(8,128)(2,1)S(1)} %get-tuple-element.61), channel_id=1, source_target_pairs={{0,4},{8,0},{16,8},{24,16},{28,24},{20,28},{12,20},{4,12},{1,5},{9... | collective-permute-start | bytes 786440 | tf_op jit(solution)/shard_map/ppermute | solution.py:235
  240.4 13.6 %copy-start.23 = (f32[512]{0:T(512)S(1)}, f32[512]{0:T(512)}, u32[]{:S(2)}) copy-start(f32[512]{0:T(512)} %param.32) | copy-start | bytes 6148
  244.8 6.6 %collective-permute-start.27 = (bf16[256,512]{1,0:T(8,128)(2,1)S(1)}, bf16[256,512]{1,0:T(8,128)(2,1)S(1)}, u32[]{:S(2)}, u32[]{:S(2)}) collective-permute-start(bf16[256,512]{1,0:T(8,128)(2,1)S(1)} %get-tuple-element.58), channel_id=1, source_target_pairs={{0,8},{8,16},{16,24},{24,28},{28,20},{20,12},{12,4},{4,0},{1,9},{9... | collective-permute-start | bytes 786440 | tf_op jit(solution)/shard_map/ppermute | solution.py:235
  247.5 6.4 %collective-permute-start.31 = (bf16[256,512]{1,0:T(8,128)(2,1)S(1)}, bf16[256,512]{1,0:T(8,128)(2,1)S(1)}, u32[]{:S(2)}, u32[]{:S(2)}) collective-permute-start(bf16[256,512]{1,0:T(8,128)(2,1)S(1)} %get-tuple-element.59), channel_id=1, source_target_pairs={{0,4},{8,0},{16,8},{24,16},{28,24},{20,28},{12,20},{4,12},{1,5},{9... | collective-permute-start | bytes 786440 | tf_op jit(solution)/shard_map/ppermute | solution.py:235
  254.8 16.4 %collective-permute-start.34 = (bf16[256,512]{1,0:T(8,128)(2,1)S(1)}, bf16[256,512]{1,0:T(8,128)(2,1)S(1)}, u32[]{:S(2)}, u32[]{:S(2)}) collective-permute-start(bf16[256,512]{1,0:T(8,128)(2,1)S(1)} %get-tuple-element.62), channel_id=1, source_target_pairs={{0,3},{1,0},{2,1},{3,2},{4,7},{5,4},{6,5},{7,6},{8,11},{9,8},{10,9... | collective-permute-start | bytes 786440 | tf_op jit(solution)/shard_map/ppermute | solution.py:180
  254.8 18.4 %collective-permute-start.33 = (bf16[256,512]{1,0:T(8,128)(2,1)S(1)}, bf16[256,512]{1,0:T(8,128)(2,1)S(1)}, u32[]{:S(2)}, u32[]{:S(2)}) collective-permute-start(bf16[256,512]{1,0:T(8,128)(2,1)S(1)} %get-tuple-element.62), channel_id=1, source_target_pairs={{0,2},{1,3},{2,0},{3,1},{4,6},{5,7},{6,4},{7,5},{8,10},{9,11},{10,... | collective-permute-start | bytes 786440 | tf_op jit(solution)/shard_map/ppermute | solution.py:180
  256.4 12.8 %collective-permute-start.32 = (bf16[256,512]{1,0:T(8,128)(2,1)S(1)}, bf16[256,512]{1,0:T(8,128)(2,1)S(1)}, u32[]{:S(2)}, u32[]{:S(2)}) collective-permute-start(bf16[256,512]{1,0:T(8,128)(2,1)S(1)} %get-tuple-element.62), channel_id=1, source_target_pairs={{0,1},{1,2},{2,3},{3,0},{4,5},{5,6},{6,7},{7,4},{8,9},{9,10},{10,1... | collective-permute-start | bytes 786440 | tf_op jit(solution)/shard_map/ppermute | solution.py:180
  276.5 10.4 %copy-start.24 = (f32[512]{0:T(512)S(1)}, f32[512]{0:T(512)}, u32[]{:S(2)}) copy-start(f32[512]{0:T(512)} %param.35) | copy-start | bytes 6148
  276.5 10.4 %copy-start.25 = (f32[512]{0:T(512)S(1)}, f32[512]{0:T(512)}, u32[]{:S(2)}) copy-start(f32[512]{0:T(512)} %param.34) | copy-start | bytes 6148
  279.6 11.5 %copy-start.1 = (bf16[512,2048]{1,0:T(8,128)(2,1)S(1)}, bf16[512,2048]{1,0:T(8,128)(2,1)}, u32[]{:S(2)}) copy-start(bf16[512,2048]{1,0:T(8,128)(2,1)} %param.26) | copy-start | bytes 6291460
  (15 other events, 42.5 us)

commit v20 on v19

--- a/solution.py
+++ b/solution.py
@@ -131,9 +131,7 @@
         if lax.axis_size("tp") == 4:
             rows = jnp.take(rows, lax.axis_index("tp") ^ jnp.arange(4, dtype=jnp.int32), axis=0)
         if begin == 0:
-            rows, expert_gate_up = lax.optimization_barrier((rows, expert_gate_up))
-        if end == len(blocks):
-            rows, qkv_flat = lax.optimization_barrier((rows, qkv_flat))
+            rows, expert_gate_up, qkv_flat = lax.optimization_barrier((rows, expert_gate_up, qkv_flat))
         gate_up_split = expert_gate_up.reshape(local_experts, rows.shape[0], quarter, -1)
         projected = jnp.einsum("qtd,eqdf->etf", rows, gate_up_split, preferred_element_type=jnp.float32)
         activated = jax.nn.silu(projected[..., :hidden_quarter]) * projected[..., hidden_quarter:]

time: 293 us -> 283 us (0.966)
  waiting for transfers between devices: 108 us -> 99.3 us
    ppermute x3, waiting for transfers between devices: 10.5 us -> 5.87 us  [permute_gather_dot(): piece = lax.ppermute(rows, 'tp', pairs)]
    ppermute x7, waiting for transfers between devices: 21.3 us -> 17.9 us  [ring_reduce_scatter(): lax.ppermute(acc.astype(jnp.bfloat16), 'seq', pairs).astype(jnp.float32)]
    ppermute x3, waiting for transfers between devices: 6.68 us -> 10 us  [ring_all_gather(): behind = lax.ppermute(behind, 'seq', backward)]
    dot_general x3, matrix products: 14.2 us -> 17.1 us  [dense_experts(): jnp.einsum('qtd,eqdf->etf', rows, gate_up_split, preferred_element_type=j...]
  transfers between devices with their start and end apart: 35 -> 35, of which waited for: 20 -> 21; matrix products, arithmetic and copies ran while one was open for 29% -> 31% of each run, Pallas kernels for 6% -> 6%
where the time goes in v20:
time: 283 us; the launch traced here: 281 us
  waiting for transfers between devices  99.3 us (35%)
  local copies, waits for them, and re-layouts  48.7 us (17%)
  other arithmetic  37.4 us (13%)
  matrix products  33.1 us (12%)
  starting transfers between devices  30.9 us (11%)
  Pallas kernels  16.8 us (6%)
  blocking collectives  14.1 us (5%)
    ppermute x6, waiting for transfers between devices, pair_gather(): far = lax.ppermute(block, 'tp', [(i, i ^ 2) for i in range(4)])  46.2 us
    ppermute x7, waiting for transfers between devices, ring_reduce_scatter(): lax.ppermute(acc.astype(jnp.bfloat16), 'seq', pairs).astype(jnp.float32)  17.9 us
    dot_general x3, matrix products, dense_experts(): jnp.einsum('qtd,eqdf->etf', rows, gate_up_split, preferred_element_type=j...  17.1 us
    pallas_call x1, Pallas kernels, flash_attention(): pl.pallas_call(kernel, grid_spec=grid_spec, out_shape=jax.ShapeDtypeStruc...  16.8 us
    unnamed x63, local copies, waits for them, and re-layouts  14.9 us
    gather x3, local copies, waits for them, and re-layouts, dense_experts(): jnp.take(rows, lax.axis_index('tp') ^ jnp.arange(4, dtype=jnp.int32), axi...  10.9 us
    ppermute x3, waiting for transfers between devices, ring_all_gather(): behind = lax.ppermute(behind, 'seq', backward)  10 us
    ppermute x3, waiting for transfers between devices, permute_reduce_scatter(): total = total + lax.ppermute(piece, 'tp', pairs).astype(jnp.float32)  9.29 us
  transfers between devices with their start and end apart: 35, of which 21 were waited for; matrix products, arithmetic and copies ran while one was open for 31% of the time, Pallas kernels for 6%

profile of v20, /device:TPU:0, one launch (start us, length us, event | category | flops | bytes accessed | tf_op | source)
XLA Modules:
  0.0 281.5 jit_solution(9150655041107833013)
XLA Ops:
  0.7 2.9 %dynamic-slice_bitcast_fusion = (bf16[1,2,256,512]{3,2,1,0:T(8,128)(2,1)S(1)}, bf16[2,256,512]{2,1,0:T(8,128)(2,1)}, bf16[2,256,512]{2,1,0:T(8,128)(2,1)}, bf16[2,256,512]{2,1,0:T(8,128)(2,1)}) fusion(bf16[2,256,2048]{2,1,0:T(8,128)(2,1)} %param.31, s32[]{:T(128)S(6)} %select_n.133, s32[]{:T(128)S(6)} %select_n.135, s32[]{:T(128)S(6)} %select_n.139, ...), kind=kLoop, calls=%fused_computation.93 | loop fusion | bytes 4194320 | tf_op jit(solution)/shard_map/stack | solution.py:321
  4.1 2.5 collective-permute-start.1
  8.6 16.8 %shard_map.192 = bf16[256,512]{1,0:T(8,128)(2,1)} custom-call(s32[1]{0:T(128)} %dynamic_slice.55.len_ref, bf16[256,512]{1,0:T(8,128)(2,1)} %q_ref.1, bf16[4096,512]{1,0:T(8,128)(2,1)} %bitcast.157, bf16[4096,512]{1,0:T(8,128)(2,1)} %bitcast.158, bf16[256,512]{1,0:T(8,128)(2,1)} %nk_ref.1, bf16[256,512]{1,0:T(8,128)(2,1)} %nv_ref.1), custom_call_target="tpu_custom_call" | custom-call | tf_op jit(solution)/shard_map/pallas_call | solution.py:94
  26.0 3.8 %collective-permute-done.2 = bf16[2,256,512]{2,1,0:T(8,128)(2,1)} collective-permute-done((bf16[2,256,512]{2,1,0:T(8,128)(2,1)}, bf16[2,256,512]{2,1,0:T(8,128)(2,1)}, u32[]{:S(2)}, u32[]{:S(2)}) %collective-permute-start.2) | collective-permute-done | bytes 524320 | tf_op jit(solution)/shard_map/ppermute | solution.py:316
  29.9 2.8 pad_maximum_fusion.4
  32.7 3.6 %gather_fusion = bf16[4,2,256,512]{3,2,1,0:T(8,128)(2,1)} fusion(bf16[4,2,256,512]{3,2,1,0:T(8,128)(2,1)} %pad_maximum_fusion.4, s32[1024]{0:T(1024)S(1)} %pad_clamp_fusion.2), kind=kCustom, calls=%fused_computation.2 | custom fusion | bytes 4194320 | tf_op jit(solution)/shard_map/jit(_take)/gather | solution.py:321
  36.2 3.2 %broadcast_select_fusion.1 = bf16[4,2,256,512]{3,2,1,0:T(8,128)(2,1)} fusion(bf16[4,2,256,512]{3,2,1,0:T(8,128)(2,1)} %gather_fusion, pred[4]{0:T(512)(128)(4,1)S(1)} %get-tuple-element.76), kind=kLoop, calls=%fused_computation.31 | loop fusion | flops 1048576 | bytes 4194308 | tf_op jit(solution)/shard_map/jit(_take)/select_n | solution.py:321
  41.7 2.3 collective-permute-start.4
  44.0 5.8 %collective-permute-done.3 = bf16[256,512]{1,0:T(8,128)(2,1)S(1)} collective-permute-done((bf16[256,512]{1,0:T(8,128)(2,1)S(1)}, bf16[256,512]{1,0:T(8,128)(2,1)S(1)}, u32[]{:S(2)}, u32[]{:S(2)}) %collective-permute-start.3) | collective-permute-done | bytes 262176 | tf_op jit(solution)/shard_map/ppermute | solution.py:162
  51.1 2.2 collective-permute-done.5
  54.6 8.2 %psum.28 = f32[256]{0:T(256)S(1)} all-reduce(f32[256]{0:T(256)S(1)} %get-tuple-element.30), channel_id=1, replica_groups=mesh['seq'=8,'tp'=4] {'tp'}, use_global_device_ids=true, to_apply=%region_1.2 | all-reduce | flops 256 | bytes 2048 | tf_op jit(solution)/shard_map/psum | solution.py:349
  63.0 1.7 collective-permute-start.7
  65.1 6.0 %collective-permute-done.7 = bf16[272,512]{1,0:T(8,128)(2,1)S(1)} collective-permute-done((bf16[272,512]{1,0:T(8,128)(2,1)S(1)}, bf16[272,512]{1,0:T(8,128)(2,1)S(1)}, u32[]{:S(2)}, u32[]{:S(2)}) %collective-permute-start.7) | collective-permute-done | bytes 278560 | tf_op jit(solution)/shard_map/ppermute | solution.py:213
  75.7 8.8 %copy.59 = bf16[2048,3,512]{0,2,1:T(8,128)(2,1)} copy(bf16[2048,3,512]{2,0,1:T(8,128)(2,1)} %param.33) | data formatting | bytes 12582912 | tf_op args[14]
  84.5 7.7 %reshape.164 = bf16[2,4,512,512]{3,2,1,0:T(8,128)(2,1)} reshape(bf16[2,2048,2,256]{3,2,1,0:T(2,128)(2,1)} %param.30) | data formatting | bytes 8388608 | tf_op jit(solution)/shard_map/reshape | solution.py:322
  97.1 3.1 %collective-permute-done.12 = bf16[272,512]{1,0:T(8,128)(2,1)} collective-permute-done((bf16[272,512]{1,0:T(8,128)(2,1)S(1)}, bf16[272,512]{1,0:T(8,128)(2,1)}, u32[]{:S(2)}, u32[]{:S(2)}) %collective-permute-start.12) | collective-permute-done | bytes 278560 | tf_op jit(solution)/shard_map/ppermute | solution.py:213
  107.1 4.9 %collective-permute-done.16 = bf16[272,512]{1,0:T(8,128)(2,1)S(1)} collective-permute-done((bf16[272,512]{1,0:T(8,128)(2,1)}, bf16[272,512]{1,0:T(8,128)(2,1)S(1)}, u32[]{:S(2)}, u32[]{:S(2)}) %collective-permute-start.16) | collective-permute-done | bytes 278560 | tf_op jit(solution)/shard_map/ppermute | solution.py:209
  114.3 8.9 %collective-permute-done.22 = bf16[768,512]{1,0:T(8,128)(2,1)S(1)} collective-permute-done((bf16[768,512]{1,0:T(8,128)(2,1)S(1)}, bf16[768,512]{1,0:T(8,128)(2,1)S(1)}, u32[]{:S(2)}, u32[]{:S(2)}) %collective-permute-start.22) | collective-permute-done | bytes 786464 | tf_op jit(solution)/shard_map/ppermute | solution.py:190
  124.7 6.0 %collective-permute-done.17 = bf16[512,512]{1,0:T(8,128)(2,1)} collective-permute-done((bf16[512,512]{1,0:T(8,128)(2,1)S(1)}, bf16[512,512]{1,0:T(8,128)(2,1)}, u32[]{:S(2)}, u32[]{:S(2)}) %collective-permute-start.17) | collective-permute-done | bytes 524320 | tf_op jit(solution)/shard_map/ppermute | solution.py:190
  130.6 2.1 pad_maximum_fusion.11
  134.4 1.9 pad_maximum_fusion
  136.3 4.4 %gather_fusion.2 = bf16[4,768,512]{2,1,0:T(8,128)(2,1)} fusion(bf16[4,768,512]{2,1,0:T(8,128)(2,1)} %pad_maximum_fusion, s32[1024]{0:T(1024)} %pad_clamp_fusion.1), kind=kCustom, calls=%fused_computation.clone | custom fusion | bytes 6291472 | tf_op jit(solution)/shard_map/jit(_take)/gather | solution.py:132
  140.7 2.4 broadcast_select_fusion
  143.9 5.2 %fusion.17 = f32[2,768,512]{1,2,0:T(8,128)} fusion(bf16[2,4,512,512]{3,2,1,0:T(8,128)(2,1)S(1)} %copy-done.6, bf16[4,768,512]{2,1,0:T(8,128)(2,1)S(1)} %broadcast_select_fusion), kind=kOutput, calls=%fused_computation.32 | convolution fusion | flops 3221225472 | bytes 10485760 | tf_op jit(solution)/shard_map/qtd,eqdf->etf/dot_general | solution.py:136
  151.7 2.1 gather_fusion.1
  153.8 5.3 %fusion.23 = f32[2,512,512]{1,2,0:T(8,128)S(1)} fusion(bf16[2,4,512,512]{3,2,1,0:T(8,128)(2,1)} %reshape.164, bf16[4,512,512]{2,1,0:T(8,128)(2,1)} %gather_fusion.1, pred[4]{0:T(512)(128)(4,1)S(1)} %copy-done.26), kind=kOutput, calls=%fused_computation.34 | convolution fusion | flops 2148532224 | bytes 8388612 | tf_op jit(solution)/shard_map/qtd,eqdf->etf/dot_general | solution.py:136
  164.5 1.9 pad_maximum_fusion.2
  166.4 4.4 %gather_fusion.3 = bf16[4,768,512]{2,1,0:T(8,128)(2,1)} fusion(bf16[4,768,512]{2,1,0:T(8,128)(2,1)} %pad_maximum_fusion.2, s32[1024]{0:T(1024)} %pad_clamp_fusion.1), kind=kCustom, calls=%fused_computation.1.clone | custom fusion | bytes 6291472 | tf_op jit(solution)/shard_map/jit(_take)/gather | solution.py:132
  170.8 6.6 %fusion.20 = f32[2,768,512]{1,2,0:T(8,128)S(1)} fusion(bf16[2,4,512,512]{3,2,1,0:T(8,128)(2,1)} %reshape.164, bf16[4,768,512]{2,1,0:T(8,128)(2,1)} %gather_fusion.3, pred[4]{0:T(512)(128)(4,1)S(1)} %copy-done.26), kind=kOutput, calls=%fused_computation.33 | convolution fusion | flops 3222798336 | bytes 10485764 | tf_op jit(solution)/shard_map/qtd,eqdf->etf/dot_general | solution.py:136
  182.3 16.1 %collective-permute-done.24 = bf16[2,768,256]{1,2,0:T(8,128)(2,1)S(1)} collective-permute-done((bf16[2,768,256]{1,2,0:T(8,128)(2,1)S(1)}, bf16[2,768,256]{1,2,0:T(8,128)(2,1)S(1)}, u32[]{:S(2)}, u32[]{:S(2)}) %collective-permute-start.24) | collective-permute-done | bytes 786464 | tf_op jit(solution)/shard_map/ppermute | solution.py:190
  199.1 15.3 %collective-permute-done.10 = bf16[2,768,256]{1,2,0:T(8,128)(2,1)S(1)} collective-permute-done((bf16[2,768,256]{1,2,0:T(8,128)(2,1)S(1)}, bf16[2,768,256]{1,2,0:T(8,128)(2,1)S(1)}, u32[]{:S(2)}, u32[]{:S(2)}) %collective-permute-start.10) | collective-permute-done | bytes 786464 | tf_op jit(solution)/shard_map/ppermute | solution.py:190
  216.0 2.3 fusion.51
  220.6 1.8 bitcast_convert_fusion
  222.4 3.6 %collective-permute-done.28 = bf16[256,512]{1,0:T(8,128)(2,1)S(1)} collective-permute-done((bf16[256,512]{1,0:T(8,128)(2,1)S(1)}, bf16[256,512]{1,0:T(8,128)(2,1)S(1)}, u32[]{:S(2)}, u32[]{:S(2)}) %collective-permute-start.28) | collective-permute-done | bytes 262176 | tf_op jit(solution)/shard_map/ppermute | solution.py:233
  226.0 1.6 collective-permute-start.29
  227.8 4.9 %collective-permute-done.29 = bf16[256,512]{1,0:T(8,128)(2,1)S(1)} collective-permute-done((bf16[256,512]{1,0:T(8,128)(2,1)S(1)}, bf16[256,512]{1,0:T(8,128)(2,1)S(1)}, u32[]{:S(2)}, u32[]{:S(2)}) %collective-permute-start.29) | collective-permute-done | bytes 262176 | tf_op jit(solution)/shard_map/ppermute | solution.py:233
  234.9 1.8 bitcast_convert_fusion.1
  236.8 2.5 collective-permute-done.26
  242.5 4.3 %collective-permute-done.27 = bf16[256,512]{1,0:T(8,128)(2,1)S(1)} collective-permute-done((bf16[256,512]{1,0:T(8,128)(2,1)S(1)}, bf16[256,512]{1,0:T(8,128)(2,1)S(1)}, u32[]{:S(2)}, u32[]{:S(2)}) %collective-permute-start.27) | collective-permute-done | bytes 262176 | tf_op jit(solution)/shard_map/ppermute | solution.py:233
  249.4 1.7 collective-permute-start.34
  251.6 2.0 fusion.36
  253.6 3.5 %collective-permute-done.32 = bf16[256,512]{1,0:T(8,128)(2,1)S(1)} collective-permute-done((bf16[256,512]{1,0:T(8,128)(2,1)S(1)}, bf16[256,512]{1,0:T(8,128)(2,1)S(1)}, u32[]{:S(2)}, u32[]{:S(2)}) %collective-permute-start.32) | collective-permute-done | bytes 262176 | tf_op jit(solution)/shard_map/ppermute | solution.py:178
  257.2 2.0 convolution_add_fusion.1
  259.2 2.0 fusion.32
  261.3 2.3 collective-permute-done.33
  263.6 3.3 %fusion.10 = f32[256,1536]{1,0:T(8,128)} fusion(f32[256,1536]{1,0:T(8,128)S(1)} %fusion.32, f32[256,1536]{1,0:T(8,128)S(1)} %convolution_add_fusion.1, bf16[256,512]{1,0:T(8,128)(2,1)S(1)} %collective-permute-done.33, bf16[2048,1536]{0,1:T(8,128)(2,1)} %bitcast.145, s32[]{:T(128)S(6)} %select_n.150), kind=kOutput, calls=%fused_computation.20 | convolution fusion | flops 403439616 | bytes 6553604 | tf_op jit(solution)/shard_map/dot_general | solution.py:179
  266.9 3.1 %copy.76 = f32[256,1536]{0,1:T(8,128)} copy(f32[256,1536]{1,0:T(8,128)} %fusion.10) | data formatting | bytes 3145728 | tf_op jit(solution)/shard_map/add | solution.py:179
  271.4 5.9 %all-reduce = (f32[256]{0:T(256)S(1)}, f32[256]{0:T(256)S(1)}, f32[256]{0:T(256)S(1)}) all-reduce(f32[256]{0:T(256)S(1)} %get-tuple-element.24, f32[256]{0:T(256)S(1)} %get-tuple-element.28, f32[256]{0:T(256)S(1)} %get-tuple-element.23), channel_id=1, replica_groups=mesh['seq'=8,'tp'=4] {'tp'}, use_global_device_ids=true, to_apply=%region_6.8 | all-reduce | flops 768 | bytes 6144 | tf_op jit(solution)/shard_map/psum | solution.py:375
  (170 shorter events, 62.5 us)
Async XLA Ops:
  0.6 38.8 %copy-start = (bf16[512,2048]{1,0:T(8,128)(2,1)S(1)}, bf16[512,2048]{1,0:T(8,128)(2,1)}, u32[]{:S(2)}) copy-start(bf16[512,2048]{1,0:T(8,128)(2,1)} %param.26) | copy-start | bytes 6291460
  0.7 7.3 %copy-start.27 = (s32[8]{0:T(128)S(1)}, s32[8]{0:T(128)}, u32[]{:S(2)}) copy-start(s32[8]{0:T(128)} %param.25) | copy-start | bytes 100
  3.6 22.4 %collective-permute-start = (bf16[2,256,512]{2,1,0:T(8,128)(2,1)}, bf16[2,256,512]{2,1,0:T(8,128)(2,1)S(1)}, u32[]{:S(2)}, u32[]{:S(2)}) collective-permute-start(bf16[2,256,512]{2,1,0:T(8,128)(2,1)} %get-tuple-element.38), channel_id=1, source_target_pairs={{0,1},{1,2},{2,3},{3,0},{4,5},{5,6},{6,7},{7,4},{8,9},{9,10},{10,1... | collective-permute-start | bytes 1572872 | tf_op jit(solution)/shard_map/ppermute | solution.py:316
  4.1 22.0 %collective-permute-start.1 = (bf16[2,256,512]{2,1,0:T(8,128)(2,1)}, bf16[2,256,512]{2,1,0:T(8,128)(2,1)}, u32[]{:S(2)}, u32[]{:S(2)}) collective-permute-start(bf16[2,256,512]{2,1,0:T(8,128)(2,1)} %get-tuple-element.40), channel_id=1, source_target_pairs={{0,2},{1,3},{2,0},{3,1},{4,6},{5,7},{6,4},{7,5},{8,10},{9,11},{10,... | collective-permute-start | bytes 1572872 | tf_op jit(solution)/shard_map/ppermute | solution.py:316
  6.6 23.3 %collective-permute-start.2 = (bf16[2,256,512]{2,1,0:T(8,128)(2,1)}, bf16[2,256,512]{2,1,0:T(8,128)(2,1)}, u32[]{:S(2)}, u32[]{:S(2)}) collective-permute-start(bf16[2,256,512]{2,1,0:T(8,128)(2,1)} %get-tuple-element.39), channel_id=1, source_target_pairs={{0,3},{1,0},{2,1},{3,2},{4,7},{5,4},{6,5},{7,6},{8,11},{9,8},{10,9... | collective-permute-start | bytes 1572872 | tf_op jit(solution)/shard_map/ppermute | solution.py:316
  8.6 17.3 %copy-start.20 = (f32[256,8]{0,1:T(8,128)S(1)}, f32[256,8]{0,1:T(8,128)}, u32[]{:S(2)}) copy-start(f32[256,8]{0,1:T(8,128)} %param.29) | copy-start | bytes 24580
  8.6 17.3 %copy-start.21 = (s32[256,8]{0,1:T(8,128)S(1)}, s32[256,8]{0,1:T(8,128)}, u32[]{:S(2)}) copy-start(s32[256,8]{0,1:T(8,128)} %param.28) | copy-start | bytes 24580
  39.5 13.8 %copy-start.19 = (bf16[256,512]{1,0:T(8,128)(2,1)S(1)}, bf16[256,512]{1,0:T(8,128)(2,1)}, u32[]{:S(2)}) copy-start(bf16[256,512]{1,0:T(8,128)(2,1)} %param.19) | copy-start | bytes 786436
  41.5 21.3 %copy-start.22 = (f32[512]{0:T(512)S(1)}, f32[512]{0:T(512)}, u32[]{:S(2)}) copy-start(f32[512]{0:T(512)} %param.27) | copy-start | bytes 6148
  41.6 8.2 %collective-permute-start.3 = (bf16[256,512]{1,0:T(8,128)(2,1)S(1)}, bf16[256,512]{1,0:T(8,128)(2,1)S(1)}, u32[]{:S(2)}, u32[]{:S(2)}) collective-permute-start(bf16[256,512]{1,0:T(8,128)(2,1)S(1)} %get-tuple-element.34), channel_id=1, source_target_pairs={{0,1},{1,2},{2,3},{3,0},{4,5},{5,6},{6,7},{7,4},{8,9},{9,10},{10,1... | collective-permute-start | bytes 786440 | tf_op jit(solution)/shard_map/ppermute | solution.py:162
  41.7 9.4 %collective-permute-start.4 = (bf16[256,512]{1,0:T(8,128)(2,1)S(1)}, bf16[256,512]{1,0:T(8,128)(2,1)S(1)}, u32[]{:S(2)}, u32[]{:S(2)}) collective-permute-start(bf16[256,512]{1,0:T(8,128)(2,1)S(1)} %get-tuple-element.36), channel_id=1, source_target_pairs={{0,2},{1,3},{2,0},{3,1},{4,6},{5,7},{6,4},{7,5},{8,10},{9,11},{10,... | collective-permute-start | bytes 786440 | tf_op jit(solution)/shard_map/ppermute | solution.py:162
  44.0 9.3 %collective-permute-start.5 = (bf16[256,512]{1,0:T(8,128)(2,1)S(1)}, bf16[256,512]{1,0:T(8,128)(2,1)S(1)}, u32[]{:S(2)}, u32[]{:S(2)}) collective-permute-start(bf16[256,512]{1,0:T(8,128)(2,1)S(1)} %get-tuple-element.35), channel_id=1, source_target_pairs={{0,3},{1,0},{2,1},{3,2},{4,7},{5,4},{6,5},{7,6},{8,11},{9,8},{10,9... | collective-permute-start | bytes 786440 | tf_op jit(solution)/shard_map/ppermute | solution.py:162
  63.0 8.1 %collective-permute-start.7 = (bf16[272,512]{1,0:T(8,128)(2,1)S(1)}, bf16[272,512]{1,0:T(8,128)(2,1)S(1)}, u32[]{:S(2)}, u32[]{:S(2)}) collective-permute-start(bf16[272,512]{1,0:T(8,128)(2,1)S(1)} %get-tuple-element.65), channel_id=1, source_target_pairs={{0,4},{8,0},{16,8},{24,16},{28,24},{20,28},{12,20},{4,12},{1,5},{9... | collective-permute-start | bytes 835592 | tf_op jit(solution)/shard_map/ppermute | solution.py:213
  64.7 7.7 %collective-permute-start.6 = (bf16[272,512]{1,0:T(8,128)(2,1)S(1)}, bf16[272,512]{1,0:T(8,128)(2,1)}, u32[]{:S(2)}, u32[]{:S(2)}) collective-permute-start(bf16[272,512]{1,0:T(8,128)(2,1)S(1)} %get-tuple-element.65), channel_id=1, source_target_pairs={{0,8},{8,16},{16,24},{24,28},{28,20},{20,12},{12,4},{4,0},{1,9},{9... | collective-permute-start | bytes 835592 | tf_op jit(solution)/shard_map/ppermute | solution.py:209
  73.5 22.1 %collective-permute-start.8 = (bf16[768,512]{1,0:T(8,128)(2,1)S(1)}, bf16[768,512]{1,0:T(8,128)(2,1)S(1)}, u32[]{:S(2)}, u32[]{:S(2)}) collective-permute-start(bf16[768,512]{1,0:T(8,128)(2,1)S(1)} %bitcast.148), channel_id=1, source_target_pairs={{0,2},{1,3},{2,0},{3,1},{4,6},{5,7},{6,4},{7,5},{8,10},{9,11},{10,... | collective-permute-start | bytes 2359304 | tf_op jit(solution)/shard_map/ppermute | solution.py:190
  74.7 19.9 %collective-permute-start.14 = (bf16[272,512]{1,0:T(8,128)(2,1)}, bf16[272,512]{1,0:T(8,128)(2,1)S(1)}, u32[]{:S(2)}, u32[]{:S(2)}) collective-permute-start(bf16[272,512]{1,0:T(8,128)(2,1)} %collective-permute-done.6), channel_id=1, source_target_pairs={{0,8},{8,16},{16,24},{24,28},{28,20},{20,12},{12,4},{4,0},{1,9},{9... | collective-permute-start | bytes 835592 | tf_op jit(solution)/shard_map/ppermute | solution.py:209
  84.5 8.3 %copy-start.14 = (bf16[272,512]{1,0:T(8,128)(2,1)S(1)}, bf16[272,512]{1,0:T(8,128)(2,1)}, u32[]{:S(2)}) copy-start(bf16[272,512]{1,0:T(8,128)(2,1)} %copy-done.13) | copy-start | bytes 835588
  93.5 6.7 %collective-permute-start.12 = (bf16[272,512]{1,0:T(8,128)(2,1)S(1)}, bf16[272,512]{1,0:T(8,128)(2,1)}, u32[]{:S(2)}, u32[]{:S(2)}) collective-permute-start(bf16[272,512]{1,0:T(8,128)(2,1)S(1)} %copy-done.14), channel_id=1, source_target_pairs={{0,4},{8,0},{16,8},{24,16},{28,24},{20,28},{12,20},{4,12},{1,5},{9... | collective-permute-start | bytes 835592 | tf_op jit(solution)/shard_map/ppermute | solution.py:213
  94.6 6.7 %collective-permute-start.15 = (bf16[272,512]{1,0:T(8,128)(2,1)S(1)}, bf16[272,512]{1,0:T(8,128)(2,1)S(1)}, u32[]{:S(2)}, u32[]{:S(2)}) collective-permute-start(bf16[272,512]{1,0:T(8,128)(2,1)S(1)} %collective-permute-done.14), channel_id=1, source_target_pairs={{0,8},{8,16},{16,24},{24,28},{28,20},{20,12},{12,4},{4,0},{1,9},{9... | collective-permute-start | bytes 835592 | tf_op jit(solution)/shard_map/ppermute | solution.py:209
  97.1 35.7 %collective-permute-start.9 = (bf16[2,768,512]{2,1,0:T(8,128)(2,1)}, bf16[2,768,512]{2,1,0:T(8,128)(2,1)}, u32[]{:S(2)}, u32[]{:S(2)}) collective-permute-start(bf16[2,768,512]{2,1,0:T(8,128)(2,1)} %pad_maximum_fusion.7), channel_id=1, source_target_pairs={{0,1},{1,0},{2,3},{3,2},{4,5},{5,4},{6,7},{7,6},{8,9},{9,8},{10,11... | collective-permute-start | bytes 4718600 | tf_op jit(solution)/shard_map/ppermute | solution.py:191
  100.2 6.9 %collective-permute-start.13 = (bf16[272,512]{1,0:T(8,128)(2,1)}, bf16[272,512]{1,0:T(8,128)(2,1)}, u32[]{:S(2)}, u32[]{:S(2)}) collective-permute-start(bf16[272,512]{1,0:T(8,128)(2,1)} %collective-permute-done.12), channel_id=1, source_target_pairs={{0,4},{8,0},{16,8},{24,16},{28,24},{20,28},{12,20},{4,12},{1,5},{9... | collective-permute-start | bytes 835592 | tf_op jit(solution)/shard_map/ppermute | solution.py:213
  102.6 20.5 %collective-permute-start.22 = (bf16[768,512]{1,0:T(8,128)(2,1)S(1)}, bf16[768,512]{1,0:T(8,128)(2,1)S(1)}, u32[]{:S(2)}, u32[]{:S(2)}) collective-permute-start(bf16[768,512]{1,0:T(8,128)(2,1)S(1)} %bitcast.151), channel_id=1, source_target_pairs={{0,2},{1,3},{2,0},{3,1},{4,6},{5,7},{6,4},{7,5},{8,10},{9,11},{10,... | collective-permute-start | bytes 2359304 | tf_op jit(solution)/shard_map/ppermute | solution.py:190
  105.0 7.0 %collective-permute-start.16 = (bf16[272,512]{1,0:T(8,128)(2,1)}, bf16[272,512]{1,0:T(8,128)(2,1)S(1)}, u32[]{:S(2)}, u32[]{:S(2)}) collective-permute-start(bf16[272,512]{1,0:T(8,128)(2,1)} %copy-done.17), channel_id=1, source_target_pairs={{0,8},{8,16},{16,24},{24,28},{28,20},{20,12},{12,4},{4,0},{1,9},{9... | collective-permute-start | bytes 835592 | tf_op jit(solution)/shard_map/ppermute | solution.py:209
  113.0 19.8 %copy-start.4 = (bf16[2,256,512]{2,1,0:T(8,128)(2,1)}, bf16[2,256,512]{2,1,0:T(8,128)(2,1)S(1)}, u32[]{:S(2)}) copy-start(bf16[2,256,512]{2,1,0:T(8,128)(2,1)S(1)} %fusion.58) | copy-start | bytes 1572868
  113.0 17.7 %collective-permute-start.17 = (bf16[512,512]{1,0:T(8,128)(2,1)S(1)}, bf16[512,512]{1,0:T(8,128)(2,1)}, u32[]{:S(2)}, u32[]{:S(2)}) collective-permute-start(bf16[512,512]{1,0:T(8,128)(2,1)S(1)} %bitcast.154), channel_id=1, source_target_pairs={{0,2},{1,3},{2,0},{3,1},{4,6},{5,7},{6,4},{7,5},{8,10},{9,11},{10,... | collective-permute-start | bytes 1572872 | tf_op jit(solution)/shard_map/ppermute | solution.py:190
  123.2 7.5 %copy-start.9 = (bf16[768,512]{1,0:T(8,128)(2,1)}, bf16[768,512]{1,0:T(8,128)(2,1)S(1)}, u32[]{:S(2)}) copy-start(bf16[768,512]{1,0:T(8,128)(2,1)S(1)} %collective-permute-done.22) | copy-start | bytes 2359300
  124.7 38.3 %collective-permute-start.23 = (bf16[2,768,512]{2,1,0:T(8,128)(2,1)}, bf16[2,768,512]{2,1,0:T(8,128)(2,1)}, u32[]{:S(2)}, u32[]{:S(2)}) collective-permute-start(bf16[2,768,512]{2,1,0:T(8,128)(2,1)} %pad_maximum_fusion.9), channel_id=1, source_target_pairs={{0,1},{1,0},{2,3},{3,2},{4,5},{5,4},{6,7},{7,6},{8,9},{9,8},{10,11... | collective-permute-start | bytes 4718600 | tf_op jit(solution)/shard_map/ppermute | solution.py:191
  132.8 16.3 %collective-permute-start.18 = (bf16[2,512,512]{2,1,0:T(8,128)(2,1)}, bf16[2,512,512]{2,1,0:T(8,128)(2,1)}, u32[]{:S(2)}, u32[]{:S(2)}) collective-permute-start(bf16[2,512,512]{2,1,0:T(8,128)(2,1)} %pad_maximum_fusion.11), channel_id=1, source_target_pairs={{0,1},{1,0},{2,3},{3,2},{4,5},{5,4},{6,7},{7,6},{8,9},{9,8},{10,11... | collective-permute-start | bytes 3145736 | tf_op jit(solution)/shard_map/ppermute | solution.py:191
  160.3 18.2 %collective-permute-start.19 = (bf16[2,512,256]{1,2,0:T(8,128)(2,1)}, bf16[2,512,256]{1,2,0:T(8,128)(2,1)}, u32[]{:S(2)}, u32[]{:S(2)}) collective-permute-start(bf16[2,512,256]{1,2,0:T(8,128)(2,1)} %multiply_convert_fusion.2), channel_id=1, source_target_pairs={{0,2},{1,3},{2,0},{3,1},{4,6},{5,7},{6,4},{7,5},{8,10},{9,11},{10,... | collective-permute-start | bytes 1572872 | tf_op jit(solution)/shard_map/ppermute | solution.py:190
  177.9 20.5 %collective-permute-start.24 = (bf16[2,768,256]{1,2,0:T(8,128)(2,1)S(1)}, bf16[2,768,256]{1,2,0:T(8,128)(2,1)S(1)}, u32[]{:S(2)}, u32[]{:S(2)}) collective-permute-start(bf16[2,768,256]{1,2,0:T(8,128)(2,1)S(1)} %multiply_convert_fusion), channel_id=1, source_target_pairs={{0,2},{1,3},{2,0},{3,1},{4,6},{5,7},{6,4},{7,5},{8,10},{9,11},{10,... | collective-permute-start | bytes 2359304 | tf_op jit(solution)/shard_map/ppermute | solution.py:190
  179.7 35.0 %collective-permute-start.20 = (bf16[2,2,512,256]{2,3,1,0:T(8,128)(2,1)S(1)}, bf16[2,2,512,256]{2,3,1,0:T(8,128)(2,1)S(1)}, u32[]{:S(2)}, u32[]{:S(2)}) collective-permute-start(bf16[2,2,512,256]{2,3,1,0:T(8,128)(2,1)S(1)} %pad_maximum_fusion.12), channel_id=1, source_target_pairs={{0,1},{1,0},{2,3},{3,2},{4,5},{5,4},{6,7},{7,6},{8,9},{9,8},{10,11... | collective-permute-start | bytes 3145736 | tf_op jit(solution)/shard_map/ppermute | solution.py:191
  180.4 34.1 %collective-permute-start.10 = (bf16[2,768,256]{1,2,0:T(8,128)(2,1)S(1)}, bf16[2,768,256]{1,2,0:T(8,128)(2,1)S(1)}, u32[]{:S(2)}, u32[]{:S(2)}) collective-permute-start(bf16[2,768,256]{1,2,0:T(8,128)(2,1)S(1)} %multiply_convert_fusion.1), channel_id=1, source_target_pairs={{0,2},{1,3},{2,0},{3,1},{4,6},{5,7},{6,4},{7,5},{8,10},{9,11},{10,... | collective-permute-start | bytes 2359304 | tf_op jit(solution)/shard_map/ppermute | solution.py:190
  198.5 22.0 %collective-permute-start.25 = (bf16[2,2,768,256]{2,3,1,0:T(8,128)(2,1)S(1)}, bf16[2,2,768,256]{2,3,1,0:T(8,128)(2,1)S(1)}, u32[]{:S(2)}, u32[]{:S(2)}) collective-permute-start(bf16[2,2,768,256]{2,3,1,0:T(8,128)(2,1)S(1)} %pad_maximum_fusion.10), channel_id=1, source_target_pairs={{0,1},{1,0},{2,3},{3,2},{4,5},{5,4},{6,7},{7,6},{8,9},{9,8},{10,11... | collective-permute-start | bytes 4718600 | tf_op jit(solution)/shard_map/ppermute | solution.py:191
  214.6 13.1 %collective-permute-start.11 = (bf16[2,2,768,256]{2,3,1,0:T(8,128)(2,1)S(1)}, bf16[2,2,768,256]{2,3,1,0:T(8,128)(2,1)S(1)}, u32[]{:S(2)}, u32[]{:S(2)}) collective-permute-start(bf16[2,2,768,256]{2,3,1,0:T(8,128)(2,1)S(1)} %pad_maximum_fusion.8), channel_id=1, source_target_pairs={{0,1},{1,0},{2,3},{3,2},{4,5},{5,4},{6,7},{7,6},{8,9},{9,8},{10,11... | collective-permute-start | bytes 4718600 | tf_op jit(solution)/shard_map/ppermute | solution.py:191
  218.4 7.6 %collective-permute-start.28 = (bf16[256,512]{1,0:T(8,128)(2,1)S(1)}, bf16[256,512]{1,0:T(8,128)(2,1)S(1)}, u32[]{:S(2)}, u32[]{:S(2)}) collective-permute-start(bf16[256,512]{1,0:T(8,128)(2,1)S(1)} %get-tuple-element.63), channel_id=1, source_target_pairs={{0,4},{8,0},{16,8},{24,16},{28,24},{20,28},{12,20},{4,12},{1,5},{9... | collective-permute-start | bytes 786440 | tf_op jit(solution)/shard_map/ppermute | solution.py:233
  220.0 7.8 %collective-permute-start.21 = (bf16[256,512]{1,0:T(8,128)(2,1)S(1)}, bf16[256,512]{1,0:T(8,128)(2,1)S(1)}, u32[]{:S(2)}, u32[]{:S(2)}) collective-permute-start(bf16[256,512]{1,0:T(8,128)(2,1)S(1)} %get-tuple-element.62), channel_id=1, source_target_pairs={{0,8},{8,16},{16,24},{24,28},{28,20},{20,12},{12,4},{4,0},{1,9},{9... | collective-permute-start | bytes 786440 | tf_op jit(solution)/shard_map/ppermute | solution.py:233
  226.0 6.7 %collective-permute-start.29 = (bf16[256,512]{1,0:T(8,128)(2,1)S(1)}, bf16[256,512]{1,0:T(8,128)(2,1)S(1)}, u32[]{:S(2)}, u32[]{:S(2)}) collective-permute-start(bf16[256,512]{1,0:T(8,128)(2,1)S(1)} %add_convert_fusion.2), channel_id=1, source_target_pairs={{0,4},{8,0},{16,8},{24,16},{28,24},{20,28},{12,20},{4,12},{1,5},{9... | collective-permute-start | bytes 786440 | tf_op jit(solution)/shard_map/ppermute | solution.py:233
  232.9 6.4 %collective-permute-start.26 = (bf16[256,512]{1,0:T(8,128)(2,1)S(1)}, bf16[256,512]{1,0:T(8,128)(2,1)S(1)}, u32[]{:S(2)}, u32[]{:S(2)}) collective-permute-start(bf16[256,512]{1,0:T(8,128)(2,1)S(1)} %get-tuple-element.58), channel_id=1, source_target_pairs={{0,8},{8,16},{16,24},{24,28},{28,20},{20,12},{12,4},{4,0},{1,9},{9... | collective-permute-start | bytes 786440 | tf_op jit(solution)/shard_map/ppermute | solution.py:233
  233.9 6.4 %collective-permute-start.30 = (bf16[256,512]{1,0:T(8,128)(2,1)S(1)}, bf16[256,512]{1,0:T(8,128)(2,1)S(1)}, u32[]{:S(2)}, u32[]{:S(2)}) collective-permute-start(bf16[256,512]{1,0:T(8,128)(2,1)S(1)} %get-tuple-element.59), channel_id=1, source_target_pairs={{0,4},{8,0},{16,8},{24,16},{28,24},{20,28},{12,20},{4,12},{1,5},{9... | collective-permute-start | bytes 786440 | tf_op jit(solution)/shard_map/ppermute | solution.py:233
  236.7 11.8 %copy-start.23 = (f32[512]{0:T(512)S(1)}, f32[512]{0:T(512)}, u32[]{:S(2)}) copy-start(f32[512]{0:T(512)} %param.32) | copy-start | bytes 6148
  240.4 6.4 %collective-permute-start.27 = (bf16[256,512]{1,0:T(8,128)(2,1)S(1)}, bf16[256,512]{1,0:T(8,128)(2,1)S(1)}, u32[]{:S(2)}, u32[]{:S(2)}) collective-permute-start(bf16[256,512]{1,0:T(8,128)(2,1)S(1)} %get-tuple-element.56), channel_id=1, source_target_pairs={{0,8},{8,16},{16,24},{24,28},{28,20},{20,12},{12,4},{4,0},{1,9},{9... | collective-permute-start | bytes 786440 | tf_op jit(solution)/shard_map/ppermute | solution.py:233
  242.0 6.4 %collective-permute-start.31 = (bf16[256,512]{1,0:T(8,128)(2,1)S(1)}, bf16[256,512]{1,0:T(8,128)(2,1)S(1)}, u32[]{:S(2)}, u32[]{:S(2)}) collective-permute-start(bf16[256,512]{1,0:T(8,128)(2,1)S(1)} %get-tuple-element.57), channel_id=1, source_target_pairs={{0,4},{8,0},{16,8},{24,16},{28,24},{20,28},{12,20},{4,12},{1,5},{9... | collective-permute-start | bytes 786440 | tf_op jit(solution)/shard_map/ppermute | solution.py:233
  249.4 7.8 %collective-permute-start.32 = (bf16[256,512]{1,0:T(8,128)(2,1)S(1)}, bf16[256,512]{1,0:T(8,128)(2,1)S(1)}, u32[]{:S(2)}, u32[]{:S(2)}) collective-permute-start(bf16[256,512]{1,0:T(8,128)(2,1)S(1)} %get-tuple-element.60), channel_id=1, source_target_pairs={{0,1},{1,2},{2,3},{3,0},{4,5},{5,6},{6,7},{7,4},{8,9},{9,10},{10,1... | collective-permute-start | bytes 786440 | tf_op jit(solution)/shard_map/ppermute | solution.py:178
  249.4 9.9 %collective-permute-start.34 = (bf16[256,512]{1,0:T(8,128)(2,1)S(1)}, bf16[256,512]{1,0:T(8,128)(2,1)S(1)}, u32[]{:S(2)}, u32[]{:S(2)}) collective-permute-start(bf16[256,512]{1,0:T(8,128)(2,1)S(1)} %get-tuple-element.60), channel_id=1, source_target_pairs={{0,3},{1,0},{2,1},{3,2},{4,7},{5,4},{6,5},{7,6},{8,11},{9,8},{10,9... | collective-permute-start | bytes 786440 | tf_op jit(solution)/shard_map/ppermute | solution.py:178
  251.1 12.5 %collective-permute-start.33 = (bf16[256,512]{1,0:T(8,128)(2,1)S(1)}, bf16[256,512]{1,0:T(8,128)(2,1)S(1)}, u32[]{:S(2)}, u32[]{:S(2)}) collective-permute-start(bf16[256,512]{1,0:T(8,128)(2,1)S(1)} %get-tuple-element.60), channel_id=1, source_target_pairs={{0,2},{1,3},{2,0},{3,1},{4,6},{5,7},{6,4},{7,5},{8,10},{9,11},{10,... | collective-permute-start | bytes 786440 | tf_op jit(solution)/shard_map/ppermute | solution.py:178
  266.9 10.5 %copy-start.24 = (f32[512]{0:T(512)S(1)}, f32[512]{0:T(512)}, u32[]{:S(2)}) copy-start(f32[512]{0:T(512)} %param.35) | copy-start | bytes 6148
  266.9 10.5 %copy-start.25 = (f32[512]{0:T(512)S(1)}, f32[512]{0:T(512)}, u32[]{:S(2)}) copy-start(f32[512]{0:T(512)} %param.34) | copy-start | bytes 6148
  270.0 11.5 %copy-start.1 = (bf16[512,2048]{1,0:T(8,128)(2,1)S(1)}, bf16[512,2048]{1,0:T(8,128)(2,1)}, u32[]{:S(2)}) copy-start(bf16[512,2048]{1,0:T(8,128)(2,1)} %param.26) | copy-start | bytes 6291460
  (15 other events, 41.3 us)

commit v21 on v18

--- a/solution.py
+++ b/solution.py
@@ -170,6 +170,16 @@
         lax.dynamic_slice_in_dim(weight, tp_here * width, width, axis=0),
         preferred_element_type=jnp.float32,
     )
+    if tp_count == 4:
+        far = lax.ppermute(rows, "tp", [(i, i ^ 2) for i in range(4)])
+        near = lax.ppermute(jnp.stack([rows, far]), "tp", [(i, i ^ 1) for i in range(4)])
+        for piece, source in ((far, tp_here ^ 2), (near[0], tp_here ^ 1), (near[1], tp_here ^ 3)):
+            total = total + jnp.dot(
+                piece,
+                lax.dynamic_slice_in_dim(weight, source * width, width, axis=0),
+                preferred_element_type=jnp.float32,
+            )
+        return total
     for shift in range(1, tp_count):
         source = (tp_here - shift) % tp_count
         pairs = [(i, (i + shift) % tp_count) for i in range(tp_count)]

time: 269 us -> 268 us (level)
  waiting for transfers between devices: 113 us -> 105 us
  Pallas kernels: 8.99 us -> 16.8 us
    ppermute x3, waiting for transfers between devices: 12.1 us -> 4.34 us  [body(): pieces.append(lax.ppermute(piece, 'tp', pairs))]
    pallas_call x1, Pallas kernels: 8.99 us -> 16.8 us  [flash_attention(): pl.pallas_call(kernel, grid_spec=grid_spec, out_shape=jax.ShapeDtypeStruc...]
  transfers between devices with their start and end apart: 35 -> 34, of which waited for: 24 -> 21; matrix products, arithmetic and copies ran while one was open for 24% -> 23% of each run, Pallas kernels for 3% -> 6%
where the time goes in v21:
time: 268 us; the launch traced here: 267 us
  waiting for transfers between devices  105 us (39%)
  local copies, waits for them, and re-layouts  43.4 us (16%)
  starting transfers between devices  29.8 us (11%)
  other arithmetic  28.4 us (11%)
  matrix products  26.6 us (10%)
  Pallas kernels  16.8 us (6%)
  blocking collectives  15.5 us (6%)
    ppermute x6, waiting for transfers between devices, pair_gather(): far = lax.ppermute(block, 'tp', [(i, i ^ 2) for i in range(4)])  51.4 us
    ppermute x7, waiting for transfers between devices, ring_reduce_scatter(): lax.ppermute(acc.astype(jnp.bfloat16), 'seq', pairs).astype(jnp.float32)  18.3 us
    unnamed x53, local copies, waits for them, and re-layouts  17.3 us
    pallas_call x1, Pallas kernels, flash_attention(): pl.pallas_call(kernel, grid_spec=grid_spec, out_shape=jax.ShapeDtypeStruc...  16.8 us
    dot_general x3, matrix products, dense_experts(): jnp.einsum('qtd,eqdf->etf', rows, gate_up_split, preferred_element_type=j...  11.7 us
    ppermute x3, waiting for transfers between devices, ring_all_gather(): behind = lax.ppermute(behind, 'seq', backward)  9.5 us
    ppermute x3, waiting for transfers between devices, permute_reduce_scatter(): total = total + lax.ppermute(piece, 'tp', pairs).astype(jnp.float32)  9.29 us
    psum x1, blocking collectives, body(): square_total = lax.psum(jnp.sum(residual * residual, axis=1), 'tp')  8.23 us
  transfers between devices with their start and end apart: 34, of which 21 were waited for; matrix products, arithmetic and copies ran while one was open for 23% of the time, Pallas kernels for 6%

profile of v21, /device:TPU:0, one launch (start us, length us, event | category | flops | bytes accessed | tf_op | source)
XLA Modules:
  0.0 266.7 jit_solution(320832479857090921)
XLA Ops:
  0.7 2.9 %dynamic-slice_bitcast_fusion = (bf16[1,2,256,512]{3,2,1,0:T(8,128)(2,1)S(1)}, bf16[2,256,512]{2,1,0:T(8,128)(2,1)}, bf16[2,256,512]{2,1,0:T(8,128)(2,1)}, bf16[2,256,512]{2,1,0:T(8,128)(2,1)}) fusion(bf16[2,256,2048]{2,1,0:T(8,128)(2,1)} %param.29, s32[]{:T(128)S(6)} %select_n.115, s32[]{:T(128)S(6)} %select_n.117, s32[]{:T(128)S(6)} %select_n.121, ...), kind=kLoop, calls=%fused_computation.96 | loop fusion | bytes 4194320 | tf_op jit(solution)/shard_map/stack | solution.py:329
  4.0 2.5 collective-permute-start.1
  8.6 16.8 %shard_map.192 = bf16[256,512]{1,0:T(8,128)(2,1)} custom-call(s32[1]{0:T(128)} %dynamic_slice.55.len_ref, bf16[256,512]{1,0:T(8,128)(2,1)} %q_ref.1, bf16[4096,512]{1,0:T(8,128)(2,1)} %bitcast.162, bf16[4096,512]{1,0:T(8,128)(2,1)} %bitcast.163, bf16[256,512]{1,0:T(8,128)(2,1)} %nk_ref.1, bf16[256,512]{1,0:T(8,128)(2,1)} %nv_ref.1), custom_call_target="tpu_custom_call" | custom-call | tf_op jit(solution)/shard_map/pallas_call | solution.py:94
  25.5 4.3 %collective-permute-done.2 = bf16[2,256,512]{2,1,0:T(8,128)(2,1)} collective-permute-done((bf16[2,256,512]{2,1,0:T(8,128)(2,1)}, bf16[2,256,512]{2,1,0:T(8,128)(2,1)}, u32[]{:S(2)}, u32[]{:S(2)}) %collective-permute-start.2) | collective-permute-done | bytes 524320 | tf_op jit(solution)/shard_map/ppermute | solution.py:324
  29.8 2.8 %pad_maximum_fusion.3 = bf16[4,2,256,512]{3,2,1,0:T(8,128)(2,1)} fusion(bf16[1,2,256,512]{3,2,1,0:T(8,128)(2,1)} %bitcast.5, bf16[1,2,256,512]{3,2,1,0:T(8,128)(2,1)} %bitcast.4, bf16[1,2,256,512]{3,2,1,0:T(8,128)(2,1)S(1)} %bitcast.187, bf16[1,2,256,512]{3,2,1,0:T(8,128)(2,1)S(1)} %get-tuple-element.36), kind=kLoop, calls=%fused_computation.23 | loop fusion | flops 3145728 | bytes 4194304 | tf_op jit(solution)/shard_map/stack | solution.py:329
  32.7 3.7 %gather_fusion = bf16[4,2,256,512]{3,2,1,0:T(8,128)(2,1)} fusion(bf16[4,2,256,512]{3,2,1,0:T(8,128)(2,1)} %pad_maximum_fusion.3, s32[1024]{0:T(1024)S(1)} %pad_clamp_fusion.1), kind=kCustom, calls=%fused_computation | custom fusion | bytes 4194320 | tf_op jit(solution)/shard_map/jit(_take)/gather | solution.py:329
  36.3 3.3 %broadcast_select_fusion = bf16[4,2,256,512]{3,2,1,0:T(8,128)(2,1)} fusion(bf16[4,2,256,512]{3,2,1,0:T(8,128)(2,1)} %gather_fusion, pred[4]{0:T(512)(128)(4,1)S(1)} %compare_and_fusion.1), kind=kLoop, calls=%fused_computation.35 | loop fusion | flops 1048576 | bytes 4194308 | tf_op jit(solution)/shard_map/jit(_take)/select_n | solution.py:329
  41.9 2.3 collective-permute-start.4
  44.2 5.8 %collective-permute-done.3 = bf16[256,512]{1,0:T(8,128)(2,1)S(1)} collective-permute-done((bf16[256,512]{1,0:T(8,128)(2,1)S(1)}, bf16[256,512]{1,0:T(8,128)(2,1)S(1)}, u32[]{:S(2)}, u32[]{:S(2)}) %collective-permute-start.3) | collective-permute-done | bytes 262176 | tf_op jit(solution)/shard_map/ppermute | solution.py:160
  51.3 2.2 collective-permute-done.5
  54.8 8.2 %psum.28 = f32[256]{0:T(256)S(1)} all-reduce(f32[256]{0:T(256)S(1)} %get-tuple-element.29), channel_id=1, replica_groups=mesh['seq'=8,'tp'=4] {'tp'}, use_global_device_ids=true, to_apply=%region_1.2 | all-reduce | flops 256 | bytes 2048 | tf_op jit(solution)/shard_map/psum | solution.py:360
  63.2 1.7 collective-permute-start.7
  65.3 6.0 %collective-permute-done.7 = bf16[272,512]{1,0:T(8,128)(2,1)S(1)} collective-permute-done((bf16[272,512]{1,0:T(8,128)(2,1)S(1)}, bf16[272,512]{1,0:T(8,128)(2,1)S(1)}, u32[]{:S(2)}, u32[]{:S(2)}) %collective-permute-start.7) | collective-permute-done | bytes 278560 | tf_op jit(solution)/shard_map/ppermute | solution.py:221
  73.9 7.6 %reshape.159 = bf16[2,4,512,512]{3,2,1,0:T(8,128)(2,1)} reshape(bf16[2,2048,2,256]{3,2,1,0:T(2,128)(2,1)} %param.28) | data formatting | bytes 8388608 | tf_op jit(solution)/shard_map/reshape | solution.py:330
  81.6 5.1 %gather_fusion.1 = bf16[4,2,512,512]{3,2,1,0:T(8,128)(2,1)} fusion(bf16[2,4,512,512]{3,2,1,0:T(8,128)(2,1)} %reshape.159, s32[1024]{0:T(1024)S(1)} %pad_clamp_fusion), kind=kCustom, calls=%fused_computation.1 | custom fusion | bytes 8388624 | tf_op jit(solution)/shard_map/jit(_take)/gather | solution.py:333
  87.2 4.7 %select_bitcast_fusion = bf16[2,4,512,512]{3,2,0,1:T(8,128)(2,1)} fusion(bf16[4,2,512,512]{3,2,1,0:T(8,128)(2,1)} %gather_fusion.1, pred[4]{0:T(512)(128)(4,1)S(1)} %compare_and_fusion), kind=kLoop, calls=%fused_computation.2 | loop fusion | flops 2097152 | bytes 8388612 | tf_op jit(solution)/shard_map/jit(_take)/select_n | solution.py:333
  91.9 8.9 %copy.56 = bf16[2048,3,512]{0,2,1:T(8,128)(2,1)} copy(bf16[2048,3,512]{2,0,1:T(8,128)(2,1)} %param.31) | data formatting | bytes 12582912 | tf_op args[14]
  100.9 1.6 collective-permute-start.12
  104.2 3.3 %collective-permute-done.12 = bf16[272,512]{1,0:T(8,128)(2,1)} collective-permute-done((bf16[272,512]{1,0:T(8,128)(2,1)S(1)}, bf16[272,512]{1,0:T(8,128)(2,1)}, u32[]{:S(2)}, u32[]{:S(2)}) %collective-permute-start.12) | collective-permute-done | bytes 278560 | tf_op jit(solution)/shard_map/ppermute | solution.py:221
  114.4 6.0 %collective-permute-done.16 = bf16[272,512]{1,0:T(8,128)(2,1)S(1)} collective-permute-done((bf16[272,512]{1,0:T(8,128)(2,1)}, bf16[272,512]{1,0:T(8,128)(2,1)S(1)}, u32[]{:S(2)}, u32[]{:S(2)}) %collective-permute-start.16) | collective-permute-done | bytes 278560 | tf_op jit(solution)/shard_map/ppermute | solution.py:217
  122.8 9.4 %collective-permute-done.22 = bf16[768,512]{1,0:T(8,128)(2,1)} collective-permute-done((bf16[768,512]{1,0:T(8,128)(2,1)}, bf16[768,512]{1,0:T(8,128)(2,1)}, u32[]{:S(2)}, u32[]{:S(2)}) %collective-permute-start.22) | collective-permute-done | bytes 786464 | tf_op jit(solution)/shard_map/ppermute | solution.py:198
  133.7 5.6 %collective-permute-done.17 = bf16[512,512]{1,0:T(8,128)(2,1)} collective-permute-done((bf16[512,512]{1,0:T(8,128)(2,1)S(1)}, bf16[512,512]{1,0:T(8,128)(2,1)}, u32[]{:S(2)}, u32[]{:S(2)}) %collective-permute-start.17) | collective-permute-done | bytes 524320 | tf_op jit(solution)/shard_map/ppermute | solution.py:198
  144.2 3.5 %fusion.23 = f32[2,768,512]{1,2,0:T(8,128)S(1)} fusion(bf16[2,4,512,512]{3,2,0,1:T(8,128)(2,1)S(1)} %copy-done.3, bf16[4,768,512]{2,1,0:T(8,128)(2,1)S(1)} %pad_maximum_fusion), kind=kOutput, calls=%fused_computation.36 | convolution fusion | flops 3221225472 | bytes 10485760 | tf_op jit(solution)/shard_map/qtd,eqdf->etf/dot_general | solution.py:134
  148.7 3.4 %fusion.27 = f32[2,512,512]{1,2,0:T(8,128)S(1)} fusion(bf16[2,4,512,512]{3,2,0,1:T(8,128)(2,1)S(1)} %copy-done.3, bf16[1,512,512]{2,1,0:T(8,128)(2,1)S(1)} %get-tuple-element.54, bf16[1,512,512]{2,1,0:T(8,128)(2,1)} %bitcast.32, bf16[1,512,512]{2,1,0:T(8,128)(2,1)S(1)} %get-tuple-element.53, bf16[1,512,512]{2,1,0:T(8,128)(2,1)S(1)} %bitcast.169), kind=kOutput, calls=%fused_computation.38 | convolution fusion | flops 2150629376 | bytes 8388608 | tf_op jit(solution)/shard_map/qtd,eqdf->etf/dot_general | solution.py:134
  152.5 1.6 collective-permute-start.19
  154.5 4.8 %fusion.26 = f32[2,768,512]{1,2,0:T(8,128)S(1)} fusion(bf16[2,4,512,512]{3,2,0,1:T(8,128)(2,1)S(1)} %copy-done.3, bf16[1,768,512]{2,1,0:T(8,128)(2,1)S(1)} %get-tuple-element.48, bf16[1,768,512]{2,1,0:T(8,128)(2,1)} %bitcast.50, bf16[1,768,512]{2,1,0:T(8,128)(2,1)S(1)} %get-tuple-element.47, bf16[1,768,512]{2,1,0:T(8,128)(2,1)} %bitcast.48), kind=kOutput, calls=%fused_computation.37 | convolution fusion | flops 3225944064 | bytes 10485760 | tf_op jit(solution)/shard_map/qtd,eqdf->etf/dot_general | solution.py:134
  160.4 6.8 %collective-permute-done.19 = bf16[2,512,256]{1,2,0:T(8,128)(2,1)S(1)} collective-permute-done((bf16[2,512,256]{1,2,0:T(8,128)(2,1)S(1)}, bf16[2,512,256]{1,2,0:T(8,128)(2,1)S(1)}, u32[]{:S(2)}, u32[]{:S(2)}) %collective-permute-start.19) | collective-permute-done | bytes 524320 | tf_op jit(solution)/shard_map/ppermute | solution.py:198
  167.9 1.6 collective-permute-start.10
  170.2 13.9 %collective-permute-done.24 = bf16[2,768,256]{1,2,0:T(8,128)(2,1)S(1)} collective-permute-done((bf16[2,768,256]{1,2,0:T(8,128)(2,1)S(1)}, bf16[2,768,256]{1,2,0:T(8,128)(2,1)S(1)}, u32[]{:S(2)}, u32[]{:S(2)}) %collective-permute-start.24) | collective-permute-done | bytes 786464 | tf_op jit(solution)/shard_map/ppermute | solution.py:198
  184.8 15.7 %collective-permute-done.10 = bf16[2,768,256]{1,2,0:T(8,128)(2,1)S(1)} collective-permute-done((bf16[2,768,256]{1,2,0:T(8,128)(2,1)S(1)}, bf16[2,768,256]{1,2,0:T(8,128)(2,1)S(1)}, u32[]{:S(2)}, u32[]{:S(2)}) %collective-permute-start.10) | collective-permute-done | bytes 786464 | tf_op jit(solution)/shard_map/ppermute | solution.py:198
  203.5 1.6 collective-permute-start.28
  205.7 1.8 bitcast_convert_fusion
  207.5 4.0 %collective-permute-done.28 = bf16[256,512]{1,0:T(8,128)(2,1)S(1)} collective-permute-done((bf16[256,512]{1,0:T(8,128)(2,1)S(1)}, bf16[256,512]{1,0:T(8,128)(2,1)S(1)}, u32[]{:S(2)}, u32[]{:S(2)}) %collective-permute-start.28) | collective-permute-done | bytes 262176 | tf_op jit(solution)/shard_map/ppermute | solution.py:241
  211.5 1.6 collective-permute-start.29
  213.3 5.3 %collective-permute-done.29 = bf16[256,512]{1,0:T(8,128)(2,1)S(1)} collective-permute-done((bf16[256,512]{1,0:T(8,128)(2,1)S(1)}, bf16[256,512]{1,0:T(8,128)(2,1)S(1)}, u32[]{:S(2)}, u32[]{:S(2)}) %collective-permute-start.29) | collective-permute-done | bytes 262176 | tf_op jit(solution)/shard_map/ppermute | solution.py:241
  220.8 1.8 bitcast_convert_fusion.1
  222.7 2.7 %collective-permute-done.26 = bf16[256,512]{1,0:T(8,128)(2,1)S(1)} collective-permute-done((bf16[256,512]{1,0:T(8,128)(2,1)S(1)}, bf16[256,512]{1,0:T(8,128)(2,1)S(1)}, u32[]{:S(2)}, u32[]{:S(2)}) %collective-permute-start.26) | collective-permute-done | bytes 262176 | tf_op jit(solution)/shard_map/ppermute | solution.py:241
  225.8 1.7 collective-permute-start.27
  227.8 4.3 %collective-permute-done.27 = bf16[256,512]{1,0:T(8,128)(2,1)S(1)} collective-permute-done((bf16[256,512]{1,0:T(8,128)(2,1)S(1)}, bf16[256,512]{1,0:T(8,128)(2,1)S(1)}, u32[]{:S(2)}, u32[]{:S(2)}) %collective-permute-start.27) | collective-permute-done | bytes 262176 | tf_op jit(solution)/shard_map/ppermute | solution.py:241
  232.2 1.7 collective-permute-done.31
  236.4 4.9 %collective-permute-done.32 = bf16[256,512]{1,0:T(8,128)(2,1)S(1)} collective-permute-done((bf16[256,512]{1,0:T(8,128)(2,1)S(1)}, bf16[256,512]{1,0:T(8,128)(2,1)S(1)}, u32[]{:S(2)}, u32[]{:S(2)}) %collective-permute-start.32) | collective-permute-done | bytes 262176 | tf_op jit(solution)/shard_map/ppermute | solution.py:174
  241.4 2.0 fusion.37
  243.4 2.0 convolution_add_fusion.1
  245.4 2.0 fusion.33
  247.4 3.3 %fusion.13 = f32[256,1536]{1,0:T(8,128)} fusion(f32[256,1536]{1,0:T(8,128)S(1)} %fusion.33, f32[256,1536]{1,0:T(8,128)S(1)} %convolution_add_fusion.1, bf16[2048,1536]{0,1:T(8,128)(2,1)} %bitcast.156, s32[]{:T(128)S(6)} %select_n.130, bf16[2,256,512]{2,1,0:T(8,128)(2,1)S(1)} %collective-permute-done.33), kind=kOutput, calls=%fused_computation.21 | convolution fusion | flops 403439616 | bytes 6553604 | tf_op jit(solution)/shard_map/dot_general | solution.py:177
  250.7 3.1 %copy.73 = f32[256,1536]{0,1:T(8,128)} copy(f32[256,1536]{1,0:T(8,128)} %fusion.13) | data formatting | bytes 3145728 | tf_op jit(solution)/shard_map/add | solution.py:177
  255.3 7.3 %all-reduce = (f32[256]{0:T(256)S(1)}, f32[256]{0:T(256)S(1)}, f32[256]{0:T(256)S(1)}) all-reduce(f32[256]{0:T(256)S(1)} %get-tuple-element.23, f32[256]{0:T(256)S(1)} %get-tuple-element.27, f32[256]{0:T(256)S(1)} %get-tuple-element.22), channel_id=1, replica_groups=mesh['seq'=8,'tp'=4] {'tp'}, use_global_device_ids=true, to_apply=%region_6.7 | all-reduce | flops 768 | bytes 6144 | tf_op jit(solution)/shard_map/psum | solution.py:386
  262.6 1.6 fusion.60
  (154 shorter events, 46.6 us)
Async XLA Ops:
  0.6 39.0 %copy-start = (bf16[512,2048]{1,0:T(8,128)(2,1)S(1)}, bf16[512,2048]{1,0:T(8,128)(2,1)}, u32[]{:S(2)}) copy-start(bf16[512,2048]{1,0:T(8,128)(2,1)} %param.24) | copy-start | bytes 6291460
  0.7 7.3 %copy-start.22 = (s32[8]{0:T(128)S(1)}, s32[8]{0:T(128)}, u32[]{:S(2)}) copy-start(s32[8]{0:T(128)} %param.23) | copy-start | bytes 100
  3.6 21.9 %collective-permute-start = (bf16[2,256,512]{2,1,0:T(8,128)(2,1)}, bf16[2,256,512]{2,1,0:T(8,128)(2,1)S(1)}, u32[]{:S(2)}, u32[]{:S(2)}) collective-permute-start(bf16[2,256,512]{2,1,0:T(8,128)(2,1)} %get-tuple-element.37), channel_id=1, source_target_pairs={{0,1},{1,2},{2,3},{3,0},{4,5},{5,6},{6,7},{7,4},{8,9},{9,10},{10,1... | collective-permute-start | bytes 1572872 | tf_op jit(solution)/shard_map/ppermute | solution.py:324
  4.0 21.5 %collective-permute-start.1 = (bf16[2,256,512]{2,1,0:T(8,128)(2,1)}, bf16[2,256,512]{2,1,0:T(8,128)(2,1)}, u32[]{:S(2)}, u32[]{:S(2)}) collective-permute-start(bf16[2,256,512]{2,1,0:T(8,128)(2,1)} %get-tuple-element.39), channel_id=1, source_target_pairs={{0,2},{1,3},{2,0},{3,1},{4,6},{5,7},{6,4},{7,5},{8,10},{9,11},{10,... | collective-permute-start | bytes 1572872 | tf_op jit(solution)/shard_map/ppermute | solution.py:324
  6.6 23.3 %collective-permute-start.2 = (bf16[2,256,512]{2,1,0:T(8,128)(2,1)}, bf16[2,256,512]{2,1,0:T(8,128)(2,1)}, u32[]{:S(2)}, u32[]{:S(2)}) collective-permute-start(bf16[2,256,512]{2,1,0:T(8,128)(2,1)} %get-tuple-element.38), channel_id=1, source_target_pairs={{0,3},{1,0},{2,1},{3,2},{4,7},{5,4},{6,5},{7,6},{8,11},{9,8},{10,9... | collective-permute-start | bytes 1572872 | tf_op jit(solution)/shard_map/ppermute | solution.py:324
  8.6 16.8 %copy-start.16 = (f32[256,8]{0,1:T(8,128)S(1)}, f32[256,8]{0,1:T(8,128)}, u32[]{:S(2)}) copy-start(f32[256,8]{0,1:T(8,128)} %param.27) | copy-start | bytes 24580
  8.6 16.9 %copy-start.17 = (s32[256,8]{0,1:T(8,128)S(1)}, s32[256,8]{0,1:T(8,128)}, u32[]{:S(2)}) copy-start(s32[256,8]{0,1:T(8,128)} %param.26) | copy-start | bytes 24580
  39.6 13.9 %copy-start.15 = (bf16[256,512]{1,0:T(8,128)(2,1)S(1)}, bf16[256,512]{1,0:T(8,128)(2,1)}, u32[]{:S(2)}) copy-start(bf16[256,512]{1,0:T(8,128)(2,1)} %param.17) | copy-start | bytes 786436
  41.7 21.3 %copy-start.18 = (f32[512]{0:T(512)S(1)}, f32[512]{0:T(512)}, u32[]{:S(2)}) copy-start(f32[512]{0:T(512)} %param.25) | copy-start | bytes 6148
  41.8 8.2 %collective-permute-start.3 = (bf16[256,512]{1,0:T(8,128)(2,1)S(1)}, bf16[256,512]{1,0:T(8,128)(2,1)S(1)}, u32[]{:S(2)}, u32[]{:S(2)}) collective-permute-start(bf16[256,512]{1,0:T(8,128)(2,1)S(1)} %get-tuple-element.33), channel_id=1, source_target_pairs={{0,1},{1,2},{2,3},{3,0},{4,5},{5,6},{6,7},{7,4},{8,9},{9,10},{10,1... | collective-permute-start | bytes 786440 | tf_op jit(solution)/shard_map/ppermute | solution.py:160
  41.9 9.4 %collective-permute-start.4 = (bf16[256,512]{1,0:T(8,128)(2,1)S(1)}, bf16[256,512]{1,0:T(8,128)(2,1)S(1)}, u32[]{:S(2)}, u32[]{:S(2)}) collective-permute-start(bf16[256,512]{1,0:T(8,128)(2,1)S(1)} %get-tuple-element.35), channel_id=1, source_target_pairs={{0,2},{1,3},{2,0},{3,1},{4,6},{5,7},{6,4},{7,5},{8,10},{9,11},{10,... | collective-permute-start | bytes 786440 | tf_op jit(solution)/shard_map/ppermute | solution.py:160
  44.2 9.3 %collective-permute-start.5 = (bf16[256,512]{1,0:T(8,128)(2,1)S(1)}, bf16[256,512]{1,0:T(8,128)(2,1)S(1)}, u32[]{:S(2)}, u32[]{:S(2)}) collective-permute-start(bf16[256,512]{1,0:T(8,128)(2,1)S(1)} %get-tuple-element.34), channel_id=1, source_target_pairs={{0,3},{1,0},{2,1},{3,2},{4,7},{5,4},{6,5},{7,6},{8,11},{9,8},{10,9... | collective-permute-start | bytes 786440 | tf_op jit(solution)/shard_map/ppermute | solution.py:160
  63.2 8.1 %collective-permute-start.7 = (bf16[272,512]{1,0:T(8,128)(2,1)S(1)}, bf16[272,512]{1,0:T(8,128)(2,1)S(1)}, u32[]{:S(2)}, u32[]{:S(2)}) collective-permute-start(bf16[272,512]{1,0:T(8,128)(2,1)S(1)} %get-tuple-element.64), channel_id=1, source_target_pairs={{0,4},{8,0},{16,8},{24,16},{28,24},{20,28},{12,20},{4,12},{1,5},{9... | collective-permute-start | bytes 835592 | tf_op jit(solution)/shard_map/ppermute | solution.py:221
  64.9 7.6 %collective-permute-start.6 = (bf16[272,512]{1,0:T(8,128)(2,1)S(1)}, bf16[272,512]{1,0:T(8,128)(2,1)S(1)}, u32[]{:S(2)}, u32[]{:S(2)}) collective-permute-start(bf16[272,512]{1,0:T(8,128)(2,1)S(1)} %get-tuple-element.64), channel_id=1, source_target_pairs={{0,8},{8,16},{16,24},{24,28},{28,20},{20,12},{12,4},{4,0},{1,9},{9... | collective-permute-start | bytes 835592 | tf_op jit(solution)/shard_map/ppermute | solution.py:217
  73.4 29.6 %collective-permute-start.8 = (bf16[768,512]{1,0:T(8,128)(2,1)S(1)}, bf16[768,512]{1,0:T(8,128)(2,1)S(1)}, u32[]{:S(2)}, u32[]{:S(2)}) collective-permute-start(bf16[768,512]{1,0:T(8,128)(2,1)S(1)} %bitcast.159), channel_id=1, source_target_pairs={{0,2},{1,3},{2,0},{3,1},{4,6},{5,7},{6,4},{7,5},{8,10},{9,11},{10,... | collective-permute-start | bytes 2359304 | tf_op jit(solution)/shard_map/ppermute | solution.py:198
  81.5 5.2 %copy-start.13 = (bf16[272,512]{1,0:T(8,128)(2,1)S(1)}, bf16[272,512]{1,0:T(8,128)(2,1)}, u32[]{:S(2)}) copy-start(bf16[272,512]{1,0:T(8,128)(2,1)} %copy-done.12) | copy-start | bytes 835588
  86.7 15.8 %collective-permute-start.14 = (bf16[272,512]{1,0:T(8,128)(2,1)S(1)}, bf16[272,512]{1,0:T(8,128)(2,1)S(1)}, u32[]{:S(2)}, u32[]{:S(2)}) collective-permute-start(bf16[272,512]{1,0:T(8,128)(2,1)S(1)} %copy-done.13), channel_id=1, source_target_pairs={{0,8},{8,16},{16,24},{24,28},{28,20},{20,12},{12,4},{4,0},{1,9},{9... | collective-permute-start | bytes 835592 | tf_op jit(solution)/shard_map/ppermute | solution.py:217
  91.9 8.9 %copy-start.8 = (bf16[272,512]{1,0:T(8,128)(2,1)S(1)}, bf16[272,512]{1,0:T(8,128)(2,1)}, u32[]{:S(2)}) copy-start(bf16[272,512]{1,0:T(8,128)(2,1)} %copy-done.7) | copy-start | bytes 835588
  100.9 6.7 %collective-permute-start.12 = (bf16[272,512]{1,0:T(8,128)(2,1)S(1)}, bf16[272,512]{1,0:T(8,128)(2,1)}, u32[]{:S(2)}, u32[]{:S(2)}) collective-permute-start(bf16[272,512]{1,0:T(8,128)(2,1)S(1)} %copy-done.8), channel_id=1, source_target_pairs={{0,4},{8,0},{16,8},{24,16},{28,24},{20,28},{12,20},{4,12},{1,5},{9... | collective-permute-start | bytes 835592 | tf_op jit(solution)/shard_map/ppermute | solution.py:221
  102.5 6.7 %copy-start.9 = (bf16[272,512]{1,0:T(8,128)(2,1)}, bf16[272,512]{1,0:T(8,128)(2,1)S(1)}, u32[]{:S(2)}) copy-start(bf16[272,512]{1,0:T(8,128)(2,1)S(1)} %collective-permute-done.14) | copy-start | bytes 835588
  102.5 6.7 %collective-permute-start.15 = (bf16[272,512]{1,0:T(8,128)(2,1)S(1)}, bf16[272,512]{1,0:T(8,128)(2,1)S(1)}, u32[]{:S(2)}, u32[]{:S(2)}) collective-permute-start(bf16[272,512]{1,0:T(8,128)(2,1)S(1)} %collective-permute-done.14), channel_id=1, source_target_pairs={{0,8},{8,16},{16,24},{24,28},{28,20},{20,12},{12,4},{4,0},{1,9},{9... | collective-permute-start | bytes 835592 | tf_op jit(solution)/shard_map/ppermute | solution.py:217
  104.2 36.3 %collective-permute-start.9 = (bf16[2,768,512]{2,1,0:T(8,128)(2,1)}, bf16[2,768,512]{2,1,0:T(8,128)(2,1)}, u32[]{:S(2)}, u32[]{:S(2)}) collective-permute-start(bf16[2,768,512]{2,1,0:T(8,128)(2,1)} %pad_maximum_fusion.5), channel_id=1, source_target_pairs={{0,1},{1,0},{2,3},{3,2},{4,5},{5,4},{6,7},{7,6},{8,9},{9,8},{10,11... | collective-permute-start | bytes 4718600 | tf_op jit(solution)/shard_map/ppermute | solution.py:199
  107.6 6.9 %collective-permute-start.13 = (bf16[272,512]{1,0:T(8,128)(2,1)}, bf16[272,512]{1,0:T(8,128)(2,1)}, u32[]{:S(2)}, u32[]{:S(2)}) collective-permute-start(bf16[272,512]{1,0:T(8,128)(2,1)} %collective-permute-done.12), channel_id=1, source_target_pairs={{0,4},{8,0},{16,8},{24,16},{28,24},{20,28},{12,20},{4,12},{1,5},{9... | collective-permute-start | bytes 835592 | tf_op jit(solution)/shard_map/ppermute | solution.py:221
  111.3 20.8 %collective-permute-start.22 = (bf16[768,512]{1,0:T(8,128)(2,1)}, bf16[768,512]{1,0:T(8,128)(2,1)}, u32[]{:S(2)}, u32[]{:S(2)}) collective-permute-start(bf16[768,512]{1,0:T(8,128)(2,1)} %bitcast.49), channel_id=1, source_target_pairs={{0,2},{1,3},{2,0},{3,1},{4,6},{5,7},{6,4},{7,5},{8,10},{9,11},{10,... | collective-permute-start | bytes 2359304 | tf_op jit(solution)/shard_map/ppermute | solution.py:198
  113.6 6.8 %collective-permute-start.16 = (bf16[272,512]{1,0:T(8,128)(2,1)}, bf16[272,512]{1,0:T(8,128)(2,1)S(1)}, u32[]{:S(2)}, u32[]{:S(2)}) collective-permute-start(bf16[272,512]{1,0:T(8,128)(2,1)} %copy-done.11), channel_id=1, source_target_pairs={{0,8},{8,16},{16,24},{24,28},{28,20},{20,12},{12,4},{4,0},{1,9},{9... | collective-permute-start | bytes 835592 | tf_op jit(solution)/shard_map/ppermute | solution.py:217
  121.4 19.0 %copy-start.5 = (bf16[2,256,512]{2,1,0:T(8,128)(2,1)}, bf16[2,256,512]{2,1,0:T(8,128)(2,1)S(1)}, u32[]{:S(2)}) copy-start(bf16[2,256,512]{2,1,0:T(8,128)(2,1)S(1)} %fusion.58) | copy-start | bytes 1572868
  121.4 17.9 %collective-permute-start.17 = (bf16[512,512]{1,0:T(8,128)(2,1)S(1)}, bf16[512,512]{1,0:T(8,128)(2,1)}, u32[]{:S(2)}, u32[]{:S(2)}) collective-permute-start(bf16[512,512]{1,0:T(8,128)(2,1)S(1)} %bitcast.167), channel_id=1, source_target_pairs={{0,2},{1,3},{2,0},{3,1},{4,6},{5,7},{6,4},{7,5},{8,10},{9,11},{10,... | collective-permute-start | bytes 1572872 | tf_op jit(solution)/shard_map/ppermute | solution.py:198
  133.7 20.7 %collective-permute-start.23 = (bf16[2,768,512]{2,1,0:T(8,128)(2,1)S(1)}, bf16[2,768,512]{2,1,0:T(8,128)(2,1)S(1)}, u32[]{:S(2)}, u32[]{:S(2)}) collective-permute-start(bf16[2,768,512]{2,1,0:T(8,128)(2,1)S(1)} %pad_maximum_fusion.7), channel_id=1, source_target_pairs={{0,1},{1,0},{2,3},{3,2},{4,5},{5,4},{6,7},{7,6},{8,9},{9,8},{10,11... | collective-permute-start | bytes 4718600 | tf_op jit(solution)/shard_map/ppermute | solution.py:199
  140.5 7.2 %collective-permute-start.18 = (bf16[2,512,512]{2,1,0:T(8,128)(2,1)S(1)}, bf16[2,512,512]{2,1,0:T(8,128)(2,1)S(1)}, u32[]{:S(2)}, u32[]{:S(2)}) collective-permute-start(bf16[2,512,512]{2,1,0:T(8,128)(2,1)S(1)} %pad_maximum_fusion.9), channel_id=1, source_target_pairs={{0,1},{1,0},{2,3},{3,2},{4,5},{5,4},{6,7},{7,6},{8,9},{9,8},{10,11... | collective-permute-start | bytes 3145736 | tf_op jit(solution)/shard_map/ppermute | solution.py:199
  152.5 14.8 %collective-permute-start.19 = (bf16[2,512,256]{1,2,0:T(8,128)(2,1)S(1)}, bf16[2,512,256]{1,2,0:T(8,128)(2,1)S(1)}, u32[]{:S(2)}, u32[]{:S(2)}) collective-permute-start(bf16[2,512,256]{1,2,0:T(8,128)(2,1)S(1)} %multiply_convert_fusion.2), channel_id=1, source_target_pairs={{0,2},{1,3},{2,0},{3,1},{4,6},{5,7},{6,4},{7,5},{8,10},{9,11},{10,... | collective-permute-start | bytes 1572872 | tf_op jit(solution)/shard_map/ppermute | solution.py:198
  159.8 24.3 %collective-permute-start.24 = (bf16[2,768,256]{1,2,0:T(8,128)(2,1)S(1)}, bf16[2,768,256]{1,2,0:T(8,128)(2,1)S(1)}, u32[]{:S(2)}, u32[]{:S(2)}) collective-permute-start(bf16[2,768,256]{1,2,0:T(8,128)(2,1)S(1)} %multiply_convert_fusion), channel_id=1, source_target_pairs={{0,2},{1,3},{2,0},{3,1},{4,6},{5,7},{6,4},{7,5},{8,10},{9,11},{10,... | collective-permute-start | bytes 2359304 | tf_op jit(solution)/shard_map/ppermute | solution.py:198
  167.4 33.4 %collective-permute-start.20 = (bf16[2,2,512,256]{2,3,1,0:T(8,128)(2,1)S(1)}, bf16[2,2,512,256]{2,3,1,0:T(8,128)(2,1)S(1)}, u32[]{:S(2)}, u32[]{:S(2)}) collective-permute-start(bf16[2,2,512,256]{2,3,1,0:T(8,128)(2,1)S(1)} %pad_maximum_fusion.10), channel_id=1, source_target_pairs={{0,1},{1,0},{2,3},{3,2},{4,5},{5,4},{6,7},{7,6},{8,9},{9,8},{10,11... | collective-permute-start | bytes 3145736 | tf_op jit(solution)/shard_map/ppermute | solution.py:199
  167.9 32.6 %collective-permute-start.10 = (bf16[2,768,256]{1,2,0:T(8,128)(2,1)S(1)}, bf16[2,768,256]{1,2,0:T(8,128)(2,1)S(1)}, u32[]{:S(2)}, u32[]{:S(2)}) collective-permute-start(bf16[2,768,256]{1,2,0:T(8,128)(2,1)S(1)} %multiply_convert_fusion.1), channel_id=1, source_target_pairs={{0,2},{1,3},{2,0},{3,1},{4,6},{5,7},{6,4},{7,5},{8,10},{9,11},{10,... | collective-permute-start | bytes 2359304 | tf_op jit(solution)/shard_map/ppermute | solution.py:198
  184.3 21.3 %collective-permute-start.25 = (bf16[2,2,768,256]{2,3,1,0:T(8,128)(2,1)S(1)}, bf16[2,2,768,256]{2,3,1,0:T(8,128)(2,1)S(1)}, u32[]{:S(2)}, u32[]{:S(2)}) collective-permute-start(bf16[2,2,768,256]{2,3,1,0:T(8,128)(2,1)S(1)} %pad_maximum_fusion.8), channel_id=1, source_target_pairs={{0,1},{1,0},{2,3},{3,2},{4,5},{5,4},{6,7},{7,6},{8,9},{9,8},{10,11... | collective-permute-start | bytes 4718600 | tf_op jit(solution)/shard_map/ppermute | solution.py:199
  200.7 12.4 %collective-permute-start.11 = (bf16[2,2,768,256]{2,3,1,0:T(8,128)(2,1)S(1)}, bf16[2,2,768,256]{2,3,1,0:T(8,128)(2,1)S(1)}, u32[]{:S(2)}, u32[]{:S(2)}) collective-permute-start(bf16[2,2,768,256]{2,3,1,0:T(8,128)(2,1)S(1)} %pad_maximum_fusion.6), channel_id=1, source_target_pairs={{0,1},{1,0},{2,3},{3,2},{4,5},{5,4},{6,7},{7,6},{8,9},{9,8},{10,11... | collective-permute-start | bytes 4718600 | tf_op jit(solution)/shard_map/ppermute | solution.py:199
  203.5 8.0 %collective-permute-start.28 = (bf16[256,512]{1,0:T(8,128)(2,1)S(1)}, bf16[256,512]{1,0:T(8,128)(2,1)S(1)}, u32[]{:S(2)}, u32[]{:S(2)}) collective-permute-start(bf16[256,512]{1,0:T(8,128)(2,1)S(1)} %get-tuple-element.62), channel_id=1, source_target_pairs={{0,4},{8,0},{16,8},{24,16},{28,24},{20,28},{12,20},{4,12},{1,5},{9... | collective-permute-start | bytes 786440 | tf_op jit(solution)/shard_map/ppermute | solution.py:241
  205.1 8.2 %collective-permute-start.21 = (bf16[256,512]{1,0:T(8,128)(2,1)S(1)}, bf16[256,512]{1,0:T(8,128)(2,1)S(1)}, u32[]{:S(2)}, u32[]{:S(2)}) collective-permute-start(bf16[256,512]{1,0:T(8,128)(2,1)S(1)} %get-tuple-element.61), channel_id=1, source_target_pairs={{0,8},{8,16},{16,24},{24,28},{28,20},{20,12},{12,4},{4,0},{1,9},{9... | collective-permute-start | bytes 786440 | tf_op jit(solution)/shard_map/ppermute | solution.py:241
  211.5 7.1 %collective-permute-start.29 = (bf16[256,512]{1,0:T(8,128)(2,1)S(1)}, bf16[256,512]{1,0:T(8,128)(2,1)S(1)}, u32[]{:S(2)}, u32[]{:S(2)}) collective-permute-start(bf16[256,512]{1,0:T(8,128)(2,1)S(1)} %add_convert_fusion.2), channel_id=1, source_target_pairs={{0,4},{8,0},{16,8},{24,16},{28,24},{20,28},{12,20},{4,12},{1,5},{9... | collective-permute-start | bytes 786440 | tf_op jit(solution)/shard_map/ppermute | solution.py:241
  218.8 6.6 %collective-permute-start.26 = (bf16[256,512]{1,0:T(8,128)(2,1)S(1)}, bf16[256,512]{1,0:T(8,128)(2,1)S(1)}, u32[]{:S(2)}, u32[]{:S(2)}) collective-permute-start(bf16[256,512]{1,0:T(8,128)(2,1)S(1)} %get-tuple-element.57), channel_id=1, source_target_pairs={{0,8},{8,16},{16,24},{24,28},{28,20},{20,12},{12,4},{4,0},{1,9},{9... | collective-permute-start | bytes 786440 | tf_op jit(solution)/shard_map/ppermute | solution.py:241
  219.3 6.4 %collective-permute-start.30 = (bf16[256,512]{1,0:T(8,128)(2,1)S(1)}, bf16[256,512]{1,0:T(8,128)(2,1)S(1)}, u32[]{:S(2)}, u32[]{:S(2)}) collective-permute-start(bf16[256,512]{1,0:T(8,128)(2,1)S(1)} %get-tuple-element.58), channel_id=1, source_target_pairs={{0,4},{8,0},{16,8},{24,16},{28,24},{20,28},{12,20},{4,12},{1,5},{9... | collective-permute-start | bytes 786440 | tf_op jit(solution)/shard_map/ppermute | solution.py:241
  222.6 11.4 %copy-start.19 = (f32[512]{0:T(512)S(1)}, f32[512]{0:T(512)}, u32[]{:S(2)}) copy-start(f32[512]{0:T(512)} %param.30) | copy-start | bytes 6148
  225.8 6.4 %collective-permute-start.27 = (bf16[256,512]{1,0:T(8,128)(2,1)S(1)}, bf16[256,512]{1,0:T(8,128)(2,1)S(1)}, u32[]{:S(2)}, u32[]{:S(2)}) collective-permute-start(bf16[256,512]{1,0:T(8,128)(2,1)S(1)} %get-tuple-element.55), channel_id=1, source_target_pairs={{0,8},{8,16},{16,24},{24,28},{28,20},{20,12},{12,4},{4,0},{1,9},{9... | collective-permute-start | bytes 786440 | tf_op jit(solution)/shard_map/ppermute | solution.py:241
  227.5 6.4 %collective-permute-start.31 = (bf16[256,512]{1,0:T(8,128)(2,1)S(1)}, bf16[256,512]{1,0:T(8,128)(2,1)S(1)}, u32[]{:S(2)}, u32[]{:S(2)}) collective-permute-start(bf16[256,512]{1,0:T(8,128)(2,1)S(1)} %get-tuple-element.56), channel_id=1, source_target_pairs={{0,4},{8,0},{16,8},{24,16},{28,24},{20,28},{12,20},{4,12},{1,5},{9... | collective-permute-start | bytes 786440 | tf_op jit(solution)/shard_map/ppermute | solution.py:241
  234.9 6.4 %collective-permute-start.32 = (bf16[256,512]{1,0:T(8,128)(2,1)S(1)}, bf16[256,512]{1,0:T(8,128)(2,1)S(1)}, u32[]{:S(2)}, u32[]{:S(2)}) collective-permute-start(bf16[256,512]{1,0:T(8,128)(2,1)S(1)} %get-tuple-element.59), channel_id=1, source_target_pairs={{0,2},{1,3},{2,0},{3,1},{4,6},{5,7},{6,4},{7,5},{8,10},{9,11},{10,... | collective-permute-start | bytes 786440 | tf_op jit(solution)/shard_map/ppermute | solution.py:174
  241.3 4.1 %collective-permute-start.33 = (bf16[2,256,512]{2,1,0:T(8,128)(2,1)S(1)}, bf16[2,256,512]{2,1,0:T(8,128)(2,1)S(1)}, u32[]{:S(2)}, u32[]{:S(2)}) collective-permute-start(bf16[2,256,512]{2,1,0:T(8,128)(2,1)S(1)} %pad_maximum_fusion.13), channel_id=1, source_target_pairs={{0,1},{1,0},{2,3},{3,2},{4,5},{5,4},{6,7},{7,6},{8,9},{9,8},{10,11... | collective-permute-start | bytes 1572872 | tf_op jit(solution)/shard_map/ppermute | solution.py:175
  250.7 11.8 %copy-start.20 = (f32[512]{0:T(512)S(1)}, f32[512]{0:T(512)}, u32[]{:S(2)}) copy-start(f32[512]{0:T(512)} %param.33) | copy-start | bytes 6148
  250.7 11.8 %copy-start.21 = (f32[512]{0:T(512)S(1)}, f32[512]{0:T(512)}, u32[]{:S(2)}) copy-start(f32[512]{0:T(512)} %param.32) | copy-start | bytes 6148
  253.8 12.9 %copy-start.1 = (bf16[512,2048]{1,0:T(8,128)(2,1)S(1)}, bf16[512,2048]{1,0:T(8,128)(2,1)}, u32[]{:S(2)}) copy-start(bf16[512,2048]{1,0:T(8,128)(2,1)} %param.24) | copy-start | bytes 6291460
  (9 other events, 18.9 us)

commit v22 on v21

--- a/solution.py
+++ b/solution.py
@@ -61,7 +61,7 @@
             o_ref[:, cols] = (acc_sc[:, cols] / l_sc[h]).astype(o_ref.dtype)
 
 
-def flash_attention(length, queries, cache_k, cache_v, new_k, new_v, block=1024):
+def flash_attention(length, queries, cache_k, cache_v, new_k, new_v, block=2048):
     tokens, width = queries.shape
     span = cache_k.shape[0]
     block = min(block, span)

time: 268 us -> 268 us (level)
  waiting for transfers between devices: 105 us -> 111 us
  Pallas kernels: 16.8 us -> 11.1 us
    pallas_call x1, Pallas kernels: 16.8 us -> 11.1 us  [flash_attention(): pl.pallas_call(kernel, grid_spec=grid_spec, out_shape=jax.ShapeDtypeStruc...]
    ppermute x3, waiting for transfers between devices: 4.34 us -> 10 us  [body(): pieces.append(lax.ppermute(piece, 'tp', pairs))]
  transfers between devices with their start and end apart: 34 -> 34, of which waited for: 21 -> 21; matrix products, arithmetic and copies ran while one was open for 23% -> 23% of each run, Pallas kernels for 6% -> 4%
where the time goes in v22:
time: 268 us; the launch traced here: 267 us
  waiting for transfers between devices  111 us (41%)
  local copies, waits for them, and re-layouts  43.4 us (16%)
  starting transfers between devices  29.8 us (11%)
  other arithmetic  28.4 us (11%)
  matrix products  26.6 us (10%)
  blocking collectives  15.5 us (6%)
  Pallas kernels  11.1 us (4%)
    ppermute x6, waiting for transfers between devices, pair_gather(): far = lax.ppermute(block, 'tp', [(i, i ^ 2) for i in range(4)])  51.4 us
    ppermute x7, waiting for transfers between devices, ring_reduce_scatter(): lax.ppermute(acc.astype(jnp.bfloat16), 'seq', pairs).astype(jnp.float32)  18.3 us
    unnamed x53, local copies, waits for them, and re-layouts  17.3 us
    dot_general x3, matrix products, dense_experts(): jnp.einsum('qtd,eqdf->etf', rows, gate_up_split, preferred_element_type=j...  11.7 us
    pallas_call x1, Pallas kernels, flash_attention(): pl.pallas_call(kernel, grid_spec=grid_spec, out_shape=jax.ShapeDtypeStruc...  11.1 us
    ppermute x3, waiting for transfers between devices, body(): pieces.append(lax.ppermute(piece, 'tp', pairs))  10 us
    ppermute x3, waiting for transfers between devices, ring_all_gather(): behind = lax.ppermute(behind, 'seq', backward)  9.5 us
    ppermute x3, waiting for transfers between devices, permute_reduce_scatter(): total = total + lax.ppermute(piece, 'tp', pairs).astype(jnp.float32)  9.29 us
  transfers between devices with their start and end apart: 34, of which 21 were waited for; matrix products, arithmetic and copies ran while one was open for 23% of the time, Pallas kernels for 4%

profile of v22, /device:TPU:0, one launch (start us, length us, event | category | flops | bytes accessed | tf_op | source)
XLA Modules:
  0.0 266.7 jit_solution(10204457243017631887)
XLA Ops:
  0.7 2.9 %dynamic-slice_bitcast_fusion = (bf16[1,2,256,512]{3,2,1,0:T(8,128)(2,1)S(1)}, bf16[2,256,512]{2,1,0:T(8,128)(2,1)}, bf16[2,256,512]{2,1,0:T(8,128)(2,1)}, bf16[2,256,512]{2,1,0:T(8,128)(2,1)}) fusion(bf16[2,256,2048]{2,1,0:T(8,128)(2,1)} %param.29, s32[]{:T(128)S(6)} %select_n.115, s32[]{:T(128)S(6)} %select_n.117, s32[]{:T(128)S(6)} %select_n.121, ...), kind=kLoop, calls=%fused_computation.96 | loop fusion | bytes 4194320 | tf_op jit(solution)/shard_map/stack | solution.py:329
  4.0 2.5 collective-permute-start.1
  8.6 11.1 %shard_map.192 = bf16[256,512]{1,0:T(8,128)(2,1)} custom-call(s32[1]{0:T(128)} %dynamic_slice.55.len_ref, bf16[256,512]{1,0:T(8,128)(2,1)} %q_ref.1, bf16[4096,512]{1,0:T(8,128)(2,1)} %bitcast.162, bf16[4096,512]{1,0:T(8,128)(2,1)} %bitcast.163, bf16[256,512]{1,0:T(8,128)(2,1)} %nk_ref.1, bf16[256,512]{1,0:T(8,128)(2,1)} %nv_ref.1), custom_call_target="tpu_custom_call" | custom-call | tf_op jit(solution)/shard_map/pallas_call | solution.py:94
  19.8 10.0 %collective-permute-done.2 = bf16[2,256,512]{2,1,0:T(8,128)(2,1)} collective-permute-done((bf16[2,256,512]{2,1,0:T(8,128)(2,1)}, bf16[2,256,512]{2,1,0:T(8,128)(2,1)}, u32[]{:S(2)}, u32[]{:S(2)}) %collective-permute-start.2) | collective-permute-done | bytes 524320 | tf_op jit(solution)/shard_map/ppermute | solution.py:324
  29.8 2.8 %pad_maximum_fusion.3 = bf16[4,2,256,512]{3,2,1,0:T(8,128)(2,1)} fusion(bf16[1,2,256,512]{3,2,1,0:T(8,128)(2,1)} %bitcast.5, bf16[1,2,256,512]{3,2,1,0:T(8,128)(2,1)} %bitcast.4, bf16[1,2,256,512]{3,2,1,0:T(8,128)(2,1)S(1)} %bitcast.187, bf16[1,2,256,512]{3,2,1,0:T(8,128)(2,1)S(1)} %get-tuple-element.36), kind=kLoop, calls=%fused_computation.23 | loop fusion | flops 3145728 | bytes 4194304 | tf_op jit(solution)/shard_map/stack | solution.py:329
  32.7 3.7 %gather_fusion = bf16[4,2,256,512]{3,2,1,0:T(8,128)(2,1)} fusion(bf16[4,2,256,512]{3,2,1,0:T(8,128)(2,1)} %pad_maximum_fusion.3, s32[1024]{0:T(1024)S(1)} %pad_clamp_fusion.1), kind=kCustom, calls=%fused_computation | custom fusion | bytes 4194320 | tf_op jit(solution)/shard_map/jit(_take)/gather | solution.py:329
  36.3 3.3 %broadcast_select_fusion = bf16[4,2,256,512]{3,2,1,0:T(8,128)(2,1)} fusion(bf16[4,2,256,512]{3,2,1,0:T(8,128)(2,1)} %gather_fusion, pred[4]{0:T(512)(128)(4,1)S(1)} %compare_and_fusion.1), kind=kLoop, calls=%fused_computation.35 | loop fusion | flops 1048576 | bytes 4194308 | tf_op jit(solution)/shard_map/jit(_take)/select_n | solution.py:329
  41.9 2.3 collective-permute-start.4
  44.2 5.8 %collective-permute-done.3 = bf16[256,512]{1,0:T(8,128)(2,1)S(1)} collective-permute-done((bf16[256,512]{1,0:T(8,128)(2,1)S(1)}, bf16[256,512]{1,0:T(8,128)(2,1)S(1)}, u32[]{:S(2)}, u32[]{:S(2)}) %collective-permute-start.3) | collective-permute-done | bytes 262176 | tf_op jit(solution)/shard_map/ppermute | solution.py:160
  51.3 2.2 collective-permute-done.5
  54.8 8.2 %psum.28 = f32[256]{0:T(256)S(1)} all-reduce(f32[256]{0:T(256)S(1)} %get-tuple-element.29), channel_id=1, replica_groups=mesh['seq'=8,'tp'=4] {'tp'}, use_global_device_ids=true, to_apply=%region_1.2 | all-reduce | flops 256 | bytes 2048 | tf_op jit(solution)/shard_map/psum | solution.py:360
  63.2 1.7 collective-permute-start.7
  65.3 6.0 %collective-permute-done.7 = bf16[272,512]{1,0:T(8,128)(2,1)S(1)} collective-permute-done((bf16[272,512]{1,0:T(8,128)(2,1)S(1)}, bf16[272,512]{1,0:T(8,128)(2,1)S(1)}, u32[]{:S(2)}, u32[]{:S(2)}) %collective-permute-start.7) | collective-permute-done | bytes 278560 | tf_op jit(solution)/shard_map/ppermute | solution.py:221
  73.9 7.6 %reshape.159 = bf16[2,4,512,512]{3,2,1,0:T(8,128)(2,1)} reshape(bf16[2,2048,2,256]{3,2,1,0:T(2,128)(2,1)} %param.28) | data formatting | bytes 8388608 | tf_op jit(solution)/shard_map/reshape | solution.py:330
  81.6 5.1 %gather_fusion.1 = bf16[4,2,512,512]{3,2,1,0:T(8,128)(2,1)} fusion(bf16[2,4,512,512]{3,2,1,0:T(8,128)(2,1)} %reshape.159, s32[1024]{0:T(1024)S(1)} %pad_clamp_fusion), kind=kCustom, calls=%fused_computation.1 | custom fusion | bytes 8388624 | tf_op jit(solution)/shard_map/jit(_take)/gather | solution.py:333
  87.2 4.7 %select_bitcast_fusion = bf16[2,4,512,512]{3,2,0,1:T(8,128)(2,1)} fusion(bf16[4,2,512,512]{3,2,1,0:T(8,128)(2,1)} %gather_fusion.1, pred[4]{0:T(512)(128)(4,1)S(1)} %compare_and_fusion), kind=kLoop, calls=%fused_computation.2 | loop fusion | flops 2097152 | bytes 8388612 | tf_op jit(solution)/shard_map/jit(_take)/select_n | solution.py:333
  91.9 8.9 %copy.56 = bf16[2048,3,512]{0,2,1:T(8,128)(2,1)} copy(bf16[2048,3,512]{2,0,1:T(8,128)(2,1)} %param.31) | data formatting | bytes 12582912 | tf_op args[14]
  100.9 1.6 collective-permute-start.12
  104.2 3.3 %collective-permute-done.12 = bf16[272,512]{1,0:T(8,128)(2,1)} collective-permute-done((bf16[272,512]{1,0:T(8,128)(2,1)S(1)}, bf16[272,512]{1,0:T(8,128)(2,1)}, u32[]{:S(2)}, u32[]{:S(2)}) %collective-permute-start.12) | collective-permute-done | bytes 278560 | tf_op jit(solution)/shard_map/ppermute | solution.py:221
  114.4 6.0 %collective-permute-done.16 = bf16[272,512]{1,0:T(8,128)(2,1)S(1)} collective-permute-done((bf16[272,512]{1,0:T(8,128)(2,1)}, bf16[272,512]{1,0:T(8,128)(2,1)S(1)}, u32[]{:S(2)}, u32[]{:S(2)}) %collective-permute-start.16) | collective-permute-done | bytes 278560 | tf_op jit(solution)/shard_map/ppermute | solution.py:217
  122.8 9.4 %collective-permute-done.22 = bf16[768,512]{1,0:T(8,128)(2,1)} collective-permute-done((bf16[768,512]{1,0:T(8,128)(2,1)}, bf16[768,512]{1,0:T(8,128)(2,1)}, u32[]{:S(2)}, u32[]{:S(2)}) %collective-permute-start.22) | collective-permute-done | bytes 786464 | tf_op jit(solution)/shard_map/ppermute | solution.py:198
  133.7 5.6 %collective-permute-done.17 = bf16[512,512]{1,0:T(8,128)(2,1)} collective-permute-done((bf16[512,512]{1,0:T(8,128)(2,1)S(1)}, bf16[512,512]{1,0:T(8,128)(2,1)}, u32[]{:S(2)}, u32[]{:S(2)}) %collective-permute-start.17) | collective-permute-done | bytes 524320 | tf_op jit(solution)/shard_map/ppermute | solution.py:198
  144.2 3.5 %fusion.23 = f32[2,768,512]{1,2,0:T(8,128)S(1)} fusion(bf16[2,4,512,512]{3,2,0,1:T(8,128)(2,1)S(1)} %copy-done.3, bf16[4,768,512]{2,1,0:T(8,128)(2,1)S(1)} %pad_maximum_fusion), kind=kOutput, calls=%fused_computation.36 | convolution fusion | flops 3221225472 | bytes 10485760 | tf_op jit(solution)/shard_map/qtd,eqdf->etf/dot_general | solution.py:134
  148.7 3.4 %fusion.27 = f32[2,512,512]{1,2,0:T(8,128)S(1)} fusion(bf16[2,4,512,512]{3,2,0,1:T(8,128)(2,1)S(1)} %copy-done.3, bf16[1,512,512]{2,1,0:T(8,128)(2,1)S(1)} %get-tuple-element.54, bf16[1,512,512]{2,1,0:T(8,128)(2,1)} %bitcast.32, bf16[1,512,512]{2,1,0:T(8,128)(2,1)S(1)} %get-tuple-element.53, bf16[1,512,512]{2,1,0:T(8,128)(2,1)S(1)} %bitcast.169), kind=kOutput, calls=%fused_computation.38 | convolution fusion | flops 2150629376 | bytes 8388608 | tf_op jit(solution)/shard_map/qtd,eqdf->etf/dot_general | solution.py:134
  152.5 1.6 collective-permute-start.19
  154.5 4.8 %fusion.26 = f32[2,768,512]{1,2,0:T(8,128)S(1)} fusion(bf16[2,4,512,512]{3,2,0,1:T(8,128)(2,1)S(1)} %copy-done.3, bf16[1,768,512]{2,1,0:T(8,128)(2,1)S(1)} %get-tuple-element.48, bf16[1,768,512]{2,1,0:T(8,128)(2,1)} %bitcast.50, bf16[1,768,512]{2,1,0:T(8,128)(2,1)S(1)} %get-tuple-element.47, bf16[1,768,512]{2,1,0:T(8,128)(2,1)} %bitcast.48), kind=kOutput, calls=%fused_computation.37 | convolution fusion | flops 3225944064 | bytes 10485760 | tf_op jit(solution)/shard_map/qtd,eqdf->etf/dot_general | solution.py:134
  160.4 6.8 %collective-permute-done.19 = bf16[2,512,256]{1,2,0:T(8,128)(2,1)S(1)} collective-permute-done((bf16[2,512,256]{1,2,0:T(8,128)(2,1)S(1)}, bf16[2,512,256]{1,2,0:T(8,128)(2,1)S(1)}, u32[]{:S(2)}, u32[]{:S(2)}) %collective-permute-start.19) | collective-permute-done | bytes 524320 | tf_op jit(solution)/shard_map/ppermute | solution.py:198
  167.9 1.6 collective-permute-start.10
  170.2 13.9 %collective-permute-done.24 = bf16[2,768,256]{1,2,0:T(8,128)(2,1)S(1)} collective-permute-done((bf16[2,768,256]{1,2,0:T(8,128)(2,1)S(1)}, bf16[2,768,256]{1,2,0:T(8,128)(2,1)S(1)}, u32[]{:S(2)}, u32[]{:S(2)}) %collective-permute-start.24) | collective-permute-done | bytes 786464 | tf_op jit(solution)/shard_map/ppermute | solution.py:198
  184.8 15.7 %collective-permute-done.10 = bf16[2,768,256]{1,2,0:T(8,128)(2,1)S(1)} collective-permute-done((bf16[2,768,256]{1,2,0:T(8,128)(2,1)S(1)}, bf16[2,768,256]{1,2,0:T(8,128)(2,1)S(1)}, u32[]{:S(2)}, u32[]{:S(2)}) %collective-permute-start.10) | collective-permute-done | bytes 786464 | tf_op jit(solution)/shard_map/ppermute | solution.py:198
  203.5 1.6 collective-permute-start.28
  205.7 1.8 bitcast_convert_fusion
  207.5 4.0 %collective-permute-done.28 = bf16[256,512]{1,0:T(8,128)(2,1)S(1)} collective-permute-done((bf16[256,512]{1,0:T(8,128)(2,1)S(1)}, bf16[256,512]{1,0:T(8,128)(2,1)S(1)}, u32[]{:S(2)}, u32[]{:S(2)}) %collective-permute-start.28) | collective-permute-done | bytes 262176 | tf_op jit(solution)/shard_map/ppermute | solution.py:241
  211.5 1.6 collective-permute-start.29
  213.3 5.3 %collective-permute-done.29 = bf16[256,512]{1,0:T(8,128)(2,1)S(1)} collective-permute-done((bf16[256,512]{1,0:T(8,128)(2,1)S(1)}, bf16[256,512]{1,0:T(8,128)(2,1)S(1)}, u32[]{:S(2)}, u32[]{:S(2)}) %collective-permute-start.29) | collective-permute-done | bytes 262176 | tf_op jit(solution)/shard_map/ppermute | solution.py:241
  220.8 1.8 bitcast_convert_fusion.1
  222.7 2.7 %collective-permute-done.26 = bf16[256,512]{1,0:T(8,128)(2,1)S(1)} collective-permute-done((bf16[256,512]{1,0:T(8,128)(2,1)S(1)}, bf16[256,512]{1,0:T(8,128)(2,1)S(1)}, u32[]{:S(2)}, u32[]{:S(2)}) %collective-permute-start.26) | collective-permute-done | bytes 262176 | tf_op jit(solution)/shard_map/ppermute | solution.py:241
  225.8 1.7 collective-permute-start.27
  227.8 4.3 %collective-permute-done.27 = bf16[256,512]{1,0:T(8,128)(2,1)S(1)} collective-permute-done((bf16[256,512]{1,0:T(8,128)(2,1)S(1)}, bf16[256,512]{1,0:T(8,128)(2,1)S(1)}, u32[]{:S(2)}, u32[]{:S(2)}) %collective-permute-start.27) | collective-permute-done | bytes 262176 | tf_op jit(solution)/shard_map/ppermute | solution.py:241
  232.2 1.7 collective-permute-done.31
  236.4 4.9 %collective-permute-done.32 = bf16[256,512]{1,0:T(8,128)(2,1)S(1)} collective-permute-done((bf16[256,512]{1,0:T(8,128)(2,1)S(1)}, bf16[256,512]{1,0:T(8,128)(2,1)S(1)}, u32[]{:S(2)}, u32[]{:S(2)}) %collective-permute-start.32) | collective-permute-done | bytes 262176 | tf_op jit(solution)/shard_map/ppermute | solution.py:174
  241.4 2.0 fusion.37
  243.4 2.0 convolution_add_fusion.1
  245.4 2.0 fusion.33
  247.4 3.3 %fusion.13 = f32[256,1536]{1,0:T(8,128)} fusion(f32[256,1536]{1,0:T(8,128)S(1)} %fusion.33, f32[256,1536]{1,0:T(8,128)S(1)} %convolution_add_fusion.1, bf16[2048,1536]{0,1:T(8,128)(2,1)} %bitcast.156, s32[]{:T(128)S(6)} %select_n.130, bf16[2,256,512]{2,1,0:T(8,128)(2,1)S(1)} %collective-permute-done.33), kind=kOutput, calls=%fused_computation.21 | convolution fusion | flops 403439616 | bytes 6553604 | tf_op jit(solution)/shard_map/dot_general | solution.py:177
  250.7 3.1 %copy.73 = f32[256,1536]{0,1:T(8,128)} copy(f32[256,1536]{1,0:T(8,128)} %fusion.13) | data formatting | bytes 3145728 | tf_op jit(solution)/shard_map/add | solution.py:177
  255.3 7.3 %all-reduce = (f32[256]{0:T(256)S(1)}, f32[256]{0:T(256)S(1)}, f32[256]{0:T(256)S(1)}) all-reduce(f32[256]{0:T(256)S(1)} %get-tuple-element.23, f32[256]{0:T(256)S(1)} %get-tuple-element.27, f32[256]{0:T(256)S(1)} %get-tuple-element.22), channel_id=1, replica_groups=mesh['seq'=8,'tp'=4] {'tp'}, use_global_device_ids=true, to_apply=%region_6.7 | all-reduce | flops 768 | bytes 6144 | tf_op jit(solution)/shard_map/psum | solution.py:386
  262.6 1.6 fusion.60
  (154 shorter events, 46.6 us)
Async XLA Ops:
  0.6 39.0 %copy-start = (bf16[512,2048]{1,0:T(8,128)(2,1)S(1)}, bf16[512,2048]{1,0:T(8,128)(2,1)}, u32[]{:S(2)}) copy-start(bf16[512,2048]{1,0:T(8,128)(2,1)} %param.24) | copy-start | bytes 6291460
  0.7 7.3 %copy-start.22 = (s32[8]{0:T(128)S(1)}, s32[8]{0:T(128)}, u32[]{:S(2)}) copy-start(s32[8]{0:T(128)} %param.23) | copy-start | bytes 100
  3.6 16.2 %collective-permute-start = (bf16[2,256,512]{2,1,0:T(8,128)(2,1)}, bf16[2,256,512]{2,1,0:T(8,128)(2,1)S(1)}, u32[]{:S(2)}, u32[]{:S(2)}) collective-permute-start(bf16[2,256,512]{2,1,0:T(8,128)(2,1)} %get-tuple-element.37), channel_id=1, source_target_pairs={{0,1},{1,2},{2,3},{3,0},{4,5},{5,6},{6,7},{7,4},{8,9},{9,10},{10,1... | collective-permute-start | bytes 1572872 | tf_op jit(solution)/shard_map/ppermute | solution.py:324
  4.0 15.8 %collective-permute-start.1 = (bf16[2,256,512]{2,1,0:T(8,128)(2,1)}, bf16[2,256,512]{2,1,0:T(8,128)(2,1)}, u32[]{:S(2)}, u32[]{:S(2)}) collective-permute-start(bf16[2,256,512]{2,1,0:T(8,128)(2,1)} %get-tuple-element.39), channel_id=1, source_target_pairs={{0,2},{1,3},{2,0},{3,1},{4,6},{5,7},{6,4},{7,5},{8,10},{9,11},{10,... | collective-permute-start | bytes 1572872 | tf_op jit(solution)/shard_map/ppermute | solution.py:324
  6.6 23.3 %collective-permute-start.2 = (bf16[2,256,512]{2,1,0:T(8,128)(2,1)}, bf16[2,256,512]{2,1,0:T(8,128)(2,1)}, u32[]{:S(2)}, u32[]{:S(2)}) collective-permute-start(bf16[2,256,512]{2,1,0:T(8,128)(2,1)} %get-tuple-element.38), channel_id=1, source_target_pairs={{0,3},{1,0},{2,1},{3,2},{4,7},{5,4},{6,5},{7,6},{8,11},{9,8},{10,9... | collective-permute-start | bytes 1572872 | tf_op jit(solution)/shard_map/ppermute | solution.py:324
  8.6 11.2 %copy-start.16 = (f32[256,8]{0,1:T(8,128)S(1)}, f32[256,8]{0,1:T(8,128)}, u32[]{:S(2)}) copy-start(f32[256,8]{0,1:T(8,128)} %param.27) | copy-start | bytes 24580
  8.6 11.2 %copy-start.17 = (s32[256,8]{0,1:T(8,128)S(1)}, s32[256,8]{0,1:T(8,128)}, u32[]{:S(2)}) copy-start(s32[256,8]{0,1:T(8,128)} %param.26) | copy-start | bytes 24580
  39.6 13.9 %copy-start.15 = (bf16[256,512]{1,0:T(8,128)(2,1)S(1)}, bf16[256,512]{1,0:T(8,128)(2,1)}, u32[]{:S(2)}) copy-start(bf16[256,512]{1,0:T(8,128)(2,1)} %param.17) | copy-start | bytes 786436
  41.7 21.3 %copy-start.18 = (f32[512]{0:T(512)S(1)}, f32[512]{0:T(512)}, u32[]{:S(2)}) copy-start(f32[512]{0:T(512)} %param.25) | copy-start | bytes 6148
  41.8 8.2 %collective-permute-start.3 = (bf16[256,512]{1,0:T(8,128)(2,1)S(1)}, bf16[256,512]{1,0:T(8,128)(2,1)S(1)}, u32[]{:S(2)}, u32[]{:S(2)}) collective-permute-start(bf16[256,512]{1,0:T(8,128)(2,1)S(1)} %get-tuple-element.33), channel_id=1, source_target_pairs={{0,1},{1,2},{2,3},{3,0},{4,5},{5,6},{6,7},{7,4},{8,9},{9,10},{10,1... | collective-permute-start | bytes 786440 | tf_op jit(solution)/shard_map/ppermute | solution.py:160
  41.9 9.4 %collective-permute-start.4 = (bf16[256,512]{1,0:T(8,128)(2,1)S(1)}, bf16[256,512]{1,0:T(8,128)(2,1)S(1)}, u32[]{:S(2)}, u32[]{:S(2)}) collective-permute-start(bf16[256,512]{1,0:T(8,128)(2,1)S(1)} %get-tuple-element.35), channel_id=1, source_target_pairs={{0,2},{1,3},{2,0},{3,1},{4,6},{5,7},{6,4},{7,5},{8,10},{9,11},{10,... | collective-permute-start | bytes 786440 | tf_op jit(solution)/shard_map/ppermute | solution.py:160
  44.2 9.3 %collective-permute-start.5 = (bf16[256,512]{1,0:T(8,128)(2,1)S(1)}, bf16[256,512]{1,0:T(8,128)(2,1)S(1)}, u32[]{:S(2)}, u32[]{:S(2)}) collective-permute-start(bf16[256,512]{1,0:T(8,128)(2,1)S(1)} %get-tuple-element.34), channel_id=1, source_target_pairs={{0,3},{1,0},{2,1},{3,2},{4,7},{5,4},{6,5},{7,6},{8,11},{9,8},{10,9... | collective-permute-start | bytes 786440 | tf_op jit(solution)/shard_map/ppermute | solution.py:160
  63.2 8.1 %collective-permute-start.7 = (bf16[272,512]{1,0:T(8,128)(2,1)S(1)}, bf16[272,512]{1,0:T(8,128)(2,1)S(1)}, u32[]{:S(2)}, u32[]{:S(2)}) collective-permute-start(bf16[272,512]{1,0:T(8,128)(2,1)S(1)} %get-tuple-element.64), channel_id=1, source_target_pairs={{0,4},{8,0},{16,8},{24,16},{28,24},{20,28},{12,20},{4,12},{1,5},{9... | collective-permute-start | bytes 835592 | tf_op jit(solution)/shard_map/ppermute | solution.py:221
  64.9 7.6 %collective-permute-start.6 = (bf16[272,512]{1,0:T(8,128)(2,1)S(1)}, bf16[272,512]{1,0:T(8,128)(2,1)S(1)}, u32[]{:S(2)}, u32[]{:S(2)}) collective-permute-start(bf16[272,512]{1,0:T(8,128)(2,1)S(1)} %get-tuple-element.64), channel_id=1, source_target_pairs={{0,8},{8,16},{16,24},{24,28},{28,20},{20,12},{12,4},{4,0},{1,9},{9... | collective-permute-start | bytes 835592 | tf_op jit(solution)/shard_map/ppermute | solution.py:217
  73.4 29.6 %collective-permute-start.8 = (bf16[768,512]{1,0:T(8,128)(2,1)S(1)}, bf16[768,512]{1,0:T(8,128)(2,1)S(1)}, u32[]{:S(2)}, u32[]{:S(2)}) collective-permute-start(bf16[768,512]{1,0:T(8,128)(2,1)S(1)} %bitcast.159), channel_id=1, source_target_pairs={{0,2},{1,3},{2,0},{3,1},{4,6},{5,7},{6,4},{7,5},{8,10},{9,11},{10,... | collective-permute-start | bytes 2359304 | tf_op jit(solution)/shard_map/ppermute | solution.py:198
  81.5 5.2 %copy-start.13 = (bf16[272,512]{1,0:T(8,128)(2,1)S(1)}, bf16[272,512]{1,0:T(8,128)(2,1)}, u32[]{:S(2)}) copy-start(bf16[272,512]{1,0:T(8,128)(2,1)} %copy-done.12) | copy-start | bytes 835588
  86.7 15.8 %collective-permute-start.14 = (bf16[272,512]{1,0:T(8,128)(2,1)S(1)}, bf16[272,512]{1,0:T(8,128)(2,1)S(1)}, u32[]{:S(2)}, u32[]{:S(2)}) collective-permute-start(bf16[272,512]{1,0:T(8,128)(2,1)S(1)} %copy-done.13), channel_id=1, source_target_pairs={{0,8},{8,16},{16,24},{24,28},{28,20},{20,12},{12,4},{4,0},{1,9},{9... | collective-permute-start | bytes 835592 | tf_op jit(solution)/shard_map/ppermute | solution.py:217
  91.9 8.9 %copy-start.8 = (bf16[272,512]{1,0:T(8,128)(2,1)S(1)}, bf16[272,512]{1,0:T(8,128)(2,1)}, u32[]{:S(2)}) copy-start(bf16[272,512]{1,0:T(8,128)(2,1)} %copy-done.7) | copy-start | bytes 835588
  100.9 6.7 %collective-permute-start.12 = (bf16[272,512]{1,0:T(8,128)(2,1)S(1)}, bf16[272,512]{1,0:T(8,128)(2,1)}, u32[]{:S(2)}, u32[]{:S(2)}) collective-permute-start(bf16[272,512]{1,0:T(8,128)(2,1)S(1)} %copy-done.8), channel_id=1, source_target_pairs={{0,4},{8,0},{16,8},{24,16},{28,24},{20,28},{12,20},{4,12},{1,5},{9... | collective-permute-start | bytes 835592 | tf_op jit(solution)/shard_map/ppermute | solution.py:221
  102.5 6.7 %copy-start.9 = (bf16[272,512]{1,0:T(8,128)(2,1)}, bf16[272,512]{1,0:T(8,128)(2,1)S(1)}, u32[]{:S(2)}) copy-start(bf16[272,512]{1,0:T(8,128)(2,1)S(1)} %collective-permute-done.14) | copy-start | bytes 835588
  102.5 6.7 %collective-permute-start.15 = (bf16[272,512]{1,0:T(8,128)(2,1)S(1)}, bf16[272,512]{1,0:T(8,128)(2,1)S(1)}, u32[]{:S(2)}, u32[]{:S(2)}) collective-permute-start(bf16[272,512]{1,0:T(8,128)(2,1)S(1)} %collective-permute-done.14), channel_id=1, source_target_pairs={{0,8},{8,16},{16,24},{24,28},{28,20},{20,12},{12,4},{4,0},{1,9},{9... | collective-permute-start | bytes 835592 | tf_op jit(solution)/shard_map/ppermute | solution.py:217
  104.2 36.3 %collective-permute-start.9 = (bf16[2,768,512]{2,1,0:T(8,128)(2,1)}, bf16[2,768,512]{2,1,0:T(8,128)(2,1)}, u32[]{:S(2)}, u32[]{:S(2)}) collective-permute-start(bf16[2,768,512]{2,1,0:T(8,128)(2,1)} %pad_maximum_fusion.5), channel_id=1, source_target_pairs={{0,1},{1,0},{2,3},{3,2},{4,5},{5,4},{6,7},{7,6},{8,9},{9,8},{10,11... | collective-permute-start | bytes 4718600 | tf_op jit(solution)/shard_map/ppermute | solution.py:199
  107.6 6.9 %collective-permute-start.13 = (bf16[272,512]{1,0:T(8,128)(2,1)}, bf16[272,512]{1,0:T(8,128)(2,1)}, u32[]{:S(2)}, u32[]{:S(2)}) collective-permute-start(bf16[272,512]{1,0:T(8,128)(2,1)} %collective-permute-done.12), channel_id=1, source_target_pairs={{0,4},{8,0},{16,8},{24,16},{28,24},{20,28},{12,20},{4,12},{1,5},{9... | collective-permute-start | bytes 835592 | tf_op jit(solution)/shard_map/ppermute | solution.py:221
  111.3 20.8 %collective-permute-start.22 = (bf16[768,512]{1,0:T(8,128)(2,1)}, bf16[768,512]{1,0:T(8,128)(2,1)}, u32[]{:S(2)}, u32[]{:S(2)}) collective-permute-start(bf16[768,512]{1,0:T(8,128)(2,1)} %bitcast.49), channel_id=1, source_target_pairs={{0,2},{1,3},{2,0},{3,1},{4,6},{5,7},{6,4},{7,5},{8,10},{9,11},{10,... | collective-permute-start | bytes 2359304 | tf_op jit(solution)/shard_map/ppermute | solution.py:198
  113.6 6.8 %collective-permute-start.16 = (bf16[272,512]{1,0:T(8,128)(2,1)}, bf16[272,512]{1,0:T(8,128)(2,1)S(1)}, u32[]{:S(2)}, u32[]{:S(2)}) collective-permute-start(bf16[272,512]{1,0:T(8,128)(2,1)} %copy-done.11), channel_id=1, source_target_pairs={{0,8},{8,16},{16,24},{24,28},{28,20},{20,12},{12,4},{4,0},{1,9},{9... | collective-permute-start | bytes 835592 | tf_op jit(solution)/shard_map/ppermute | solution.py:217
  121.4 19.0 %copy-start.5 = (bf16[2,256,512]{2,1,0:T(8,128)(2,1)}, bf16[2,256,512]{2,1,0:T(8,128)(2,1)S(1)}, u32[]{:S(2)}) copy-start(bf16[2,256,512]{2,1,0:T(8,128)(2,1)S(1)} %fusion.58) | copy-start | bytes 1572868
  121.4 17.9 %collective-permute-start.17 = (bf16[512,512]{1,0:T(8,128)(2,1)S(1)}, bf16[512,512]{1,0:T(8,128)(2,1)}, u32[]{:S(2)}, u32[]{:S(2)}) collective-permute-start(bf16[512,512]{1,0:T(8,128)(2,1)S(1)} %bitcast.167), channel_id=1, source_target_pairs={{0,2},{1,3},{2,0},{3,1},{4,6},{5,7},{6,4},{7,5},{8,10},{9,11},{10,... | collective-permute-start | bytes 1572872 | tf_op jit(solution)/shard_map/ppermute | solution.py:198
  133.7 20.7 %collective-permute-start.23 = (bf16[2,768,512]{2,1,0:T(8,128)(2,1)S(1)}, bf16[2,768,512]{2,1,0:T(8,128)(2,1)S(1)}, u32[]{:S(2)}, u32[]{:S(2)}) collective-permute-start(bf16[2,768,512]{2,1,0:T(8,128)(2,1)S(1)} %pad_maximum_fusion.7), channel_id=1, source_target_pairs={{0,1},{1,0},{2,3},{3,2},{4,5},{5,4},{6,7},{7,6},{8,9},{9,8},{10,11... | collective-permute-start | bytes 4718600 | tf_op jit(solution)/shard_map/ppermute | solution.py:199
  140.5 7.2 %collective-permute-start.18 = (bf16[2,512,512]{2,1,0:T(8,128)(2,1)S(1)}, bf16[2,512,512]{2,1,0:T(8,128)(2,1)S(1)}, u32[]{:S(2)}, u32[]{:S(2)}) collective-permute-start(bf16[2,512,512]{2,1,0:T(8,128)(2,1)S(1)} %pad_maximum_fusion.9), channel_id=1, source_target_pairs={{0,1},{1,0},{2,3},{3,2},{4,5},{5,4},{6,7},{7,6},{8,9},{9,8},{10,11... | collective-permute-start | bytes 3145736 | tf_op jit(solution)/shard_map/ppermute | solution.py:199
  152.5 14.8 %collective-permute-start.19 = (bf16[2,512,256]{1,2,0:T(8,128)(2,1)S(1)}, bf16[2,512,256]{1,2,0:T(8,128)(2,1)S(1)}, u32[]{:S(2)}, u32[]{:S(2)}) collective-permute-start(bf16[2,512,256]{1,2,0:T(8,128)(2,1)S(1)} %multiply_convert_fusion.2), channel_id=1, source_target_pairs={{0,2},{1,3},{2,0},{3,1},{4,6},{5,7},{6,4},{7,5},{8,10},{9,11},{10,... | collective-permute-start | bytes 1572872 | tf_op jit(solution)/shard_map/ppermute | solution.py:198
  159.8 24.3 %collective-permute-start.24 = (bf16[2,768,256]{1,2,0:T(8,128)(2,1)S(1)}, bf16[2,768,256]{1,2,0:T(8,128)(2,1)S(1)}, u32[]{:S(2)}, u32[]{:S(2)}) collective-permute-start(bf16[2,768,256]{1,2,0:T(8,128)(2,1)S(1)} %multiply_convert_fusion), channel_id=1, source_target_pairs={{0,2},{1,3},{2,0},{3,1},{4,6},{5,7},{6,4},{7,5},{8,10},{9,11},{10,... | collective-permute-start | bytes 2359304 | tf_op jit(solution)/shard_map/ppermute | solution.py:198
  167.4 33.4 %collective-permute-start.20 = (bf16[2,2,512,256]{2,3,1,0:T(8,128)(2,1)S(1)}, bf16[2,2,512,256]{2,3,1,0:T(8,128)(2,1)S(1)}, u32[]{:S(2)}, u32[]{:S(2)}) collective-permute-start(bf16[2,2,512,256]{2,3,1,0:T(8,128)(2,1)S(1)} %pad_maximum_fusion.10), channel_id=1, source_target_pairs={{0,1},{1,0},{2,3},{3,2},{4,5},{5,4},{6,7},{7,6},{8,9},{9,8},{10,11... | collective-permute-start | bytes 3145736 | tf_op jit(solution)/shard_map/ppermute | solution.py:199
  167.9 32.6 %collective-permute-start.10 = (bf16[2,768,256]{1,2,0:T(8,128)(2,1)S(1)}, bf16[2,768,256]{1,2,0:T(8,128)(2,1)S(1)}, u32[]{:S(2)}, u32[]{:S(2)}) collective-permute-start(bf16[2,768,256]{1,2,0:T(8,128)(2,1)S(1)} %multiply_convert_fusion.1), channel_id=1, source_target_pairs={{0,2},{1,3},{2,0},{3,1},{4,6},{5,7},{6,4},{7,5},{8,10},{9,11},{10,... | collective-permute-start | bytes 2359304 | tf_op jit(solution)/shard_map/ppermute | solution.py:198
  184.3 21.3 %collective-permute-start.25 = (bf16[2,2,768,256]{2,3,1,0:T(8,128)(2,1)S(1)}, bf16[2,2,768,256]{2,3,1,0:T(8,128)(2,1)S(1)}, u32[]{:S(2)}, u32[]{:S(2)}) collective-permute-start(bf16[2,2,768,256]{2,3,1,0:T(8,128)(2,1)S(1)} %pad_maximum_fusion.8), channel_id=1, source_target_pairs={{0,1},{1,0},{2,3},{3,2},{4,5},{5,4},{6,7},{7,6},{8,9},{9,8},{10,11... | collective-permute-start | bytes 4718600 | tf_op jit(solution)/shard_map/ppermute | solution.py:199
  200.7 12.4 %collective-permute-start.11 = (bf16[2,2,768,256]{2,3,1,0:T(8,128)(2,1)S(1)}, bf16[2,2,768,256]{2,3,1,0:T(8,128)(2,1)S(1)}, u32[]{:S(2)}, u32[]{:S(2)}) collective-permute-start(bf16[2,2,768,256]{2,3,1,0:T(8,128)(2,1)S(1)} %pad_maximum_fusion.6), channel_id=1, source_target_pairs={{0,1},{1,0},{2,3},{3,2},{4,5},{5,4},{6,7},{7,6},{8,9},{9,8},{10,11... | collective-permute-start | bytes 4718600 | tf_op jit(solution)/shard_map/ppermute | solution.py:199
  203.5 8.0 %collective-permute-start.28 = (bf16[256,512]{1,0:T(8,128)(2,1)S(1)}, bf16[256,512]{1,0:T(8,128)(2,1)S(1)}, u32[]{:S(2)}, u32[]{:S(2)}) collective-permute-start(bf16[256,512]{1,0:T(8,128)(2,1)S(1)} %get-tuple-element.62), channel_id=1, source_target_pairs={{0,4},{8,0},{16,8},{24,16},{28,24},{20,28},{12,20},{4,12},{1,5},{9... | collective-permute-start | bytes 786440 | tf_op jit(solution)/shard_map/ppermute | solution.py:241
  205.1 8.2 %collective-permute-start.21 = (bf16[256,512]{1,0:T(8,128)(2,1)S(1)}, bf16[256,512]{1,0:T(8,128)(2,1)S(1)}, u32[]{:S(2)}, u32[]{:S(2)}) collective-permute-start(bf16[256,512]{1,0:T(8,128)(2,1)S(1)} %get-tuple-element.61), channel_id=1, source_target_pairs={{0,8},{8,16},{16,24},{24,28},{28,20},{20,12},{12,4},{4,0},{1,9},{9... | collective-permute-start | bytes 786440 | tf_op jit(solution)/shard_map/ppermute | solution.py:241
  211.5 7.1 %collective-permute-start.29 = (bf16[256,512]{1,0:T(8,128)(2,1)S(1)}, bf16[256,512]{1,0:T(8,128)(2,1)S(1)}, u32[]{:S(2)}, u32[]{:S(2)}) collective-permute-start(bf16[256,512]{1,0:T(8,128)(2,1)S(1)} %add_convert_fusion.2), channel_id=1, source_target_pairs={{0,4},{8,0},{16,8},{24,16},{28,24},{20,28},{12,20},{4,12},{1,5},{9... | collective-permute-start | bytes 786440 | tf_op jit(solution)/shard_map/ppermute | solution.py:241
  218.8 6.6 %collective-permute-start.26 = (bf16[256,512]{1,0:T(8,128)(2,1)S(1)}, bf16[256,512]{1,0:T(8,128)(2,1)S(1)}, u32[]{:S(2)}, u32[]{:S(2)}) collective-permute-start(bf16[256,512]{1,0:T(8,128)(2,1)S(1)} %get-tuple-element.57), channel_id=1, source_target_pairs={{0,8},{8,16},{16,24},{24,28},{28,20},{20,12},{12,4},{4,0},{1,9},{9... | collective-permute-start | bytes 786440 | tf_op jit(solution)/shard_map/ppermute | solution.py:241
  219.3 6.4 %collective-permute-start.30 = (bf16[256,512]{1,0:T(8,128)(2,1)S(1)}, bf16[256,512]{1,0:T(8,128)(2,1)S(1)}, u32[]{:S(2)}, u32[]{:S(2)}) collective-permute-start(bf16[256,512]{1,0:T(8,128)(2,1)S(1)} %get-tuple-element.58), channel_id=1, source_target_pairs={{0,4},{8,0},{16,8},{24,16},{28,24},{20,28},{12,20},{4,12},{1,5},{9... | collective-permute-start | bytes 786440 | tf_op jit(solution)/shard_map/ppermute | solution.py:241
  222.6 11.4 %copy-start.19 = (f32[512]{0:T(512)S(1)}, f32[512]{0:T(512)}, u32[]{:S(2)}) copy-start(f32[512]{0:T(512)} %param.30) | copy-start | bytes 6148
  225.8 6.4 %collective-permute-start.27 = (bf16[256,512]{1,0:T(8,128)(2,1)S(1)}, bf16[256,512]{1,0:T(8,128)(2,1)S(1)}, u32[]{:S(2)}, u32[]{:S(2)}) collective-permute-start(bf16[256,512]{1,0:T(8,128)(2,1)S(1)} %get-tuple-element.55), channel_id=1, source_target_pairs={{0,8},{8,16},{16,24},{24,28},{28,20},{20,12},{12,4},{4,0},{1,9},{9... | collective-permute-start | bytes 786440 | tf_op jit(solution)/shard_map/ppermute | solution.py:241
  227.5 6.4 %collective-permute-start.31 = (bf16[256,512]{1,0:T(8,128)(2,1)S(1)}, bf16[256,512]{1,0:T(8,128)(2,1)S(1)}, u32[]{:S(2)}, u32[]{:S(2)}) collective-permute-start(bf16[256,512]{1,0:T(8,128)(2,1)S(1)} %get-tuple-element.56), channel_id=1, source_target_pairs={{0,4},{8,0},{16,8},{24,16},{28,24},{20,28},{12,20},{4,12},{1,5},{9... | collective-permute-start | bytes 786440 | tf_op jit(solution)/shard_map/ppermute | solution.py:241
  234.9 6.4 %collective-permute-start.32 = (bf16[256,512]{1,0:T(8,128)(2,1)S(1)}, bf16[256,512]{1,0:T(8,128)(2,1)S(1)}, u32[]{:S(2)}, u32[]{:S(2)}) collective-permute-start(bf16[256,512]{1,0:T(8,128)(2,1)S(1)} %get-tuple-element.59), channel_id=1, source_target_pairs={{0,2},{1,3},{2,0},{3,1},{4,6},{5,7},{6,4},{7,5},{8,10},{9,11},{10,... | collective-permute-start | bytes 786440 | tf_op jit(solution)/shard_map/ppermute | solution.py:174
  241.3 4.1 %collective-permute-start.33 = (bf16[2,256,512]{2,1,0:T(8,128)(2,1)S(1)}, bf16[2,256,512]{2,1,0:T(8,128)(2,1)S(1)}, u32[]{:S(2)}, u32[]{:S(2)}) collective-permute-start(bf16[2,256,512]{2,1,0:T(8,128)(2,1)S(1)} %pad_maximum_fusion.13), channel_id=1, source_target_pairs={{0,1},{1,0},{2,3},{3,2},{4,5},{5,4},{6,7},{7,6},{8,9},{9,8},{10,11... | collective-permute-start | bytes 1572872 | tf_op jit(solution)/shard_map/ppermute | solution.py:175
  250.7 11.8 %copy-start.20 = (f32[512]{0:T(512)S(1)}, f32[512]{0:T(512)}, u32[]{:S(2)}) copy-start(f32[512]{0:T(512)} %param.33) | copy-start | bytes 6148
  250.7 11.8 %copy-start.21 = (f32[512]{0:T(512)S(1)}, f32[512]{0:T(512)}, u32[]{:S(2)}) copy-start(f32[512]{0:T(512)} %param.32) | copy-start | bytes 6148
  253.8 12.9 %copy-start.1 = (bf16[512,2048]{1,0:T(8,128)(2,1)S(1)}, bf16[512,2048]{1,0:T(8,128)(2,1)}, u32[]{:S(2)}) copy-start(bf16[512,2048]{1,0:T(8,128)(2,1)} %param.24) | copy-start | bytes 6291460
  (9 other events, 18.9 us)
